TPU v7x, 32 devices: a whole 2x2x4 slice. The times are simulated.
32 devices in a mesh: rep: 4 (over z), tp: 8 (over y, x, core).
Axes of the slice: x: 2, y: 2, z: 4, core: 2. Of those that a mesh axis runs over, the one named last changes fastest.
Arguments:
- activations: bfloat16 [6144, 1024], P(('rep', 'tp')), may hold values from -6 to 6
- out_grads: bfloat16 [6144, 3072], P('rep', 'tp'), may hold values from -0.15625 to 0.15625
- error_state: bfloat16 [4, 1024, 3072], P('rep', None, 'tp'), may hold values from -4 to 4
- q_start: float32 [3072, 32], P('tp'), may hold values from -6 to 6
- qkv_master: float32 [1024, 3072], P('rep', 'tp'), may hold values from -3 to 3
- qkv_moment: float32 [1024, 3072], P('rep', 'tp'), may hold values from -0.75 to 0.75
- word_grads: bfloat16 [6144, 1024], P('rep', 'tp'), may hold values from -6 to 6
- token_ids: int32 [6144], P('rep'), may hold values from 0 to 1599, as said below
- owner_map: int32 [1600], replicated, may hold values from 0 to 1599, as said below
- word_master: float32 [1600, 1024], P('rep', 'tp'), may hold values from -6 to 6
Outputs:
- error_new: bfloat16 [4, 1024, 3072], P('rep', None, 'tp')
- q_factor: float32 [3072, 32], P('tp')
- moment_new: float32 [1024, 3072], P('rep', 'tp')
- master_new: float32 [1024, 3072], P('rep', 'tp')
- weight_bf16: bfloat16 [1024, 3072], P(None, 'tp')
- word_new: float32 [1600, 1024], P('rep', 'tp')
Inputs may be any that keep to these rules, and one draw needn't show every extreme that they name: A permutation of the rows: word w is stored in row owner_map[w] of word_master, whose owner is that row divided by 400. `token_ids`: the 1536 tokens of one replica name words of one owner at most 768 times; in every replica some owner is named exactly 768 times.
All inputs are finite; a program needn't handle non-finite values.
Results may differ from a plain program's by a relative error of at most 0.001.
Values may be sent and summed in bfloat16 or wider, within the bound.
No kernel may reach another device: no remote copies, remote signals or barrier semaphores. Data moves between devices by JAX's collectives and lax.ppermute only.
A program may use at most 64 MiB of HBM per device.

v0:
```python
import jax
import jax.numpy as jnp
from jax import lax
from jax.sharding import PartitionSpec as P

ROUNDS = 2


MOMENTUM = 0.9
LEARNING_RATE = 4.0
EMBED_RATE = 0.5


def orthonormal(left_basis, gram_matrix):
    factor_low = jnp.linalg.cholesky(gram_matrix)
    return jax.scipy.linalg.solve_triangular(factor_low, left_basis.T, lower=True).T


def word_update(word_grads, token_ids, owner_map, word_master):
    replicas = lax.axis_size("rep")
    per_owner = word_master.shape[0]
    capacity = 2 * token_ids.shape[0] // replicas
    targets = owner_map[token_ids]
    owners = targets // per_owner
    row_slot = targets % per_owner
    matches = (owners[:, None] == jnp.arange(replicas, dtype=jnp.int32)[None, :]).astype(jnp.int32)
    places = jnp.sum(jnp.cumsum(matches, axis=0) * matches, axis=1) - 1
    outgoing = (
        jnp.zeros((replicas, capacity, word_grads.shape[1]), jnp.bfloat16)
        .at[owners, places]
        .set(word_grads)
    )
    labels = jnp.full((replicas, capacity), per_owner, jnp.int32).at[owners, places].set(row_slot)
    incoming, arrived = (
        lax.all_to_all(outgoing, "rep", split_axis=0, concat_axis=0, tiled=True),
        lax.all_to_all(labels, "rep", split_axis=0, concat_axis=0, tiled=True),
    )
    flat_rows = incoming.reshape(-1, incoming.shape[2])
    selector = (
        arrived.reshape(-1)[:, None] == jnp.arange(per_owner, dtype=jnp.int32)[None, :]
    ).astype(jnp.bfloat16)
    row_grad = lax.dot_general(
        selector, flat_rows, (((0,), (0,)), ((), ())), preferred_element_type=jnp.float32
    )
    return word_master - EMBED_RATE * row_grad


def shards(
    activations,
    out_grads,
    error_state,
    q_start,
    qkv_master,
    qkv_moment,
    word_grads,
    token_ids,
    owner_map,
    word_master,
):
    highest = lax.Precision.HIGHEST
    replicas = lax.axis_size("rep")
    word_new = None
    product = lax.dot_general(
        lax.all_gather(activations, "tp", axis=0, tiled=True),
        out_grads,
        (((0,), (0,)), ((), ())),
        preferred_element_type=jnp.float32,
    )
    combined = product + error_state[0].astype(jnp.float32)
    right_basis = q_start
    left_basis = None
    for round_index in range(ROUNDS):
        partial_left = jnp.dot(combined, right_basis, precision=highest)
        left_basis = lax.psum(partial_left, ("rep", "tp")) / replicas
        gram_matrix = jnp.dot(left_basis.T, left_basis, precision=highest)
        left_basis = orthonormal(left_basis, gram_matrix)
        partial_right = lax.dot_general(
            combined, left_basis, (((0,), (0,)), ((), ())), precision=highest
        )
        right_basis = lax.psum(partial_right, "rep") / replicas
    approx = jnp.dot(left_basis, right_basis.T, precision=highest)
    error_new = (combined - approx).astype(jnp.bfloat16)[None]
    owned_rows = qkv_master.shape[0]
    update_rows = lax.dynamic_slice_in_dim(
        approx, lax.axis_index("rep") * owned_rows, owned_rows, 0
    )
    moment_new = MOMENTUM * qkv_moment + update_rows
    master_new = qkv_master - LEARNING_RATE * moment_new
    weight_bf16 = lax.all_gather(master_new.astype(jnp.bfloat16), "rep", axis=0, tiled=True)
    word_new = word_update(word_grads, token_ids, owner_map, word_master)
    return (error_new, right_basis, moment_new, master_new, weight_bf16, word_new)


def solution(mesh):
    in_specs = (
        P(("rep", "tp"), None),
        P("rep", "tp"),
        P("rep", None, "tp"),
        P("tp", None),
        P("rep", "tp"),
        P("rep", "tp"),
        P("rep", "tp"),
        P("rep"),
        P(),
        P("rep", "tp"),
    )
    out_specs = (
        P("rep", None, "tp"),
        P("tp", None),
        P("rep", "tp"),
        P("rep", "tp"),
        P(None, "tp"),
        P("rep", "tp"),
    )
    return jax.shard_map(shards, mesh=mesh, in_specs=in_specs, out_specs=out_specs, check_vma=False)
```

profile of v0, /device:TPU:0, one launch (start us, length us, event | category | flops | bytes accessed | tf_op | source)
XLA Modules:
  0.0 393.2 jit_solution(7987979019762832987)
XLA Ops:
  7.2 0.0 all-gather.2.cloned.1.call-start
  7.2 0.7 all-gather.2.cloned.1.call-update
  7.9 0.0 all-reduce.3.cloned.1.call-start
  8.0 0.7 compare_select_fusion.2
  8.7 8.4 %gather_fusion = s32[1536]{0:T(1024)S(1)} fusion(s32[1600]{0:T(1024)S(1)} %copy-done.1, s32[2048]{0:T(1024)S(1)} %pad_clamp_fusion), kind=kCustom, calls=%fused_computation | custom fusion | bytes 18432 | tf_op jit(solution)/shard_map/gather | solution.py:23
  17.2 1.2 reduce-window.6
  18.3 0.2 slice_reduce_fusion
  18.5 0.2 reduce-window.9
  18.7 0.1 add_bitcast_fusion
  18.9 0.1 multiply_reduce_fusion
  19.0 0.1 and_reduce_fusion
  19.1 25.9 %all-gather.2.cloned.1.call-done = bf16[1536,1024]{1,0:T(8,128)(2,1)} async-done(((bf16[192,1024]{1,0:T(8,128)(2,1)}), bf16[1536,1024]{1,0:T(8,128)(2,1)}) %all-gather.2.cloned.1.call-update) | async-done | bytes 3145744 | tf_op jit(solution)/shard_map/all_gather | solution.py:64
  45.0 3.9 convert_add_fusion
  48.9 2.2 fusion.45
  51.2 0.0 all-reduce.3.cloned.1.call-update
  51.2 6.8 %scatter_custom_fusion = s32[3072]{0:T(1024)} fusion(s32[1536]{0:T(1024)S(1)} %broadcast_select_fusion, s32[1536]{0:T(1024)S(1)} %get-tuple-element.13, s32[]{:T(128)} %constant.83.clone.1), kind=kCustom, calls=%fused_computation.70 | custom fusion | bytes 12292
  57.9 4.6 %all-to-all-start = ((s32[4,1,768]{2,1,0:T(1,128)}), s32[4,1,768]{2,1,0:T(1,128)S(1)}, u32[]{:S(2)}, u32[]{:S(2)}) async-start(s32[4,1,768]{2,1,0:T(1,128)} %bitcast.13), calls=%async_computation | async-start | bytes 24576 | tf_op jit(solution)/shard_map/all_to_all | solution.py:36
  62.5 5.7 %scatter_custom_fusion.1 = bf16[3072,128]{1,0:T(8,128)(2,1)} fusion(s32[1536]{0:T(1024)S(1)} %broadcast_select_fusion, bf16[1536,128]{1,0:T(8,128)(2,1)} %param.19, bf16[]{:T(256)} %constant.89.clone.1), kind=kCustom, calls=%fused_computation.11 | custom fusion | bytes 786944
  68.3 105.5 %all-reduce.3.cloned.1.call-done = f32[1024,32]{0,1:T(8,128)} async-done(((f32[1024,32]{0,1:T(8,128)}), f32[1024,32]{0,1:T(8,128)}) %all-reduce.3.cloned.1.call-update) | async-done | bytes 131088 | tf_op jit(solution)/shard_map/psum | solution.py:74
  173.8 1.2 fusion.15
  175.0 0.1 copy.20
  175.1 2.9 cholesky.44
  178.0 0.6 copy-done.6
  178.6 3.6 all-to-all-start.1
  182.2 0.6 compare_reduce_fusion.1
  182.9 1.3 fusion.27
  184.1 3.2 custom-call.6
  187.3 1.2 fusion.9
  188.5 1.6 fusion.46
  190.1 21.4 %psum.29 = f32[384,32]{0,1:T(8,128)} all-reduce(f32[384,32]{0,1:T(8,128)} %fusion.46), channel_id=1, replica_groups=mesh['rep'=4,'tp'=8] {'rep'}, use_global_device_ids=true, to_apply=%region_3.0 | all-reduce | flops 12288 | bytes 98304 | tf_op jit(solution)/shard_map/psum | solution.py:80
  211.5 3.0 fusion.21
  214.5 0.0 all-reduce.5.cloned.1.call-update
  214.6 2.5 fusion.3
  217.1 119.1 %all-reduce.5.cloned.1.call-done = f32[1024,32]{0,1:T(8,128)} async-done(((f32[1024,32]{0,1:T(8,128)}), f32[1024,32]{0,1:T(8,128)}) %all-reduce.5.cloned.1.call-update) | async-done | bytes 131088 | tf_op jit(solution)/shard_map/psum | solution.py:74
  336.1 1.2 fusion.12
  337.3 0.1 copy.21
  337.4 2.9 cholesky.55
  340.4 0.6 compare_reduce_fusion
  341.0 0.7 fusion.28
  341.7 2.4 custom-call.7
  344.1 1.2 fusion.7
  345.4 1.0 fusion.47
  346.4 18.4 %psum.31 = f32[384,32]{0,1:T(8,128)S(1)} all-reduce(f32[384,32]{0,1:T(8,128)S(1)} %fusion.47), channel_id=1, replica_groups=mesh['rep'=4,'tp'=8] {'rep'}, use_global_device_ids=true, to_apply=%region_5.8 | all-reduce | flops 12288 | bytes 98304 | tf_op jit(solution)/shard_map/psum | solution.py:80
  364.8 1.5 fusion.48
  366.3 1.1 fusion.4
  367.4 1.0 fusion.44
  368.4 17.4 %all_gather.7 = bf16[1024,384]{1,0:T(8,128)(2,1)S(1)} all-gather(bf16[256,384]{1,0:T(8,128)(2,1)S(1)} %get-tuple-element.10), channel_id=1, replica_groups=mesh['rep'=4,'tp'=8] {'rep'}, dimensions={0}, use_global_device_ids=true | all-gather | bytes 983040 | tf_op jit(solution)/shard_map/all_gather | solution.py:89
  385.8 0.9 copy.27
  (35 shorter events, 0.3 us)
Async XLA Ops:
  7.2 37.8 %copy-start = (bf16[1536,384]{1,0:T(8,128)(2,1)S(1)}, bf16[1536,384]{1,0:T(8,128)(2,1)}, u32[]{:S(2)}) copy-start(bf16[1536,384]{1,0:T(8,128)(2,1)} %param.14) | copy-start | bytes 3538948
  7.2 1.5 copy-start.1
  7.2 37.8 %all-gather.2.cloned.1.call-start = ((), (), s32[]{:S(2)}) async-start(), calls=%async_computation.2 | async-start | bytes 3538944 | tf_op jit(solution)/shard_map/all_gather | solution.py:64
  7.9 165.8 %all-reduce.3.cloned.1.call-start = ((), (), s32[]{:S(2)}) async-start(), calls=%async_computation.3 | async-start | bytes 262144 | tf_op jit(solution)/shard_map/psum | solution.py:74
  8.7 10.2 %copy-start.9 = (s32[2]{0:T(128)S(1)}, s32[2]{0:T(128)}, u32[]{:S(2)}) copy-start(s32[2]{0:T(128)} %constant.92) | copy-start | bytes 28
  8.7 10.3 %copy-start.8 = (s32[2]{0:T(128)S(1)}, s32[2]{0:T(128)}, u32[]{:S(2)}) copy-start(s32[2]{0:T(128)} %constant.95) | copy-start | bytes 28
  19.1 29.8 %copy-start.5 = (f32[384,32]{0,1:T(8,128)S(1)}, f32[384,32]{0,1:T(8,128)}, u32[]{:S(2)}) copy-start(f32[384,32]{0,1:T(8,128)} %param.16) | copy-start | bytes 147460
  57.9 120.1 %all-to-all-start = ((s32[4,1,768]{2,1,0:T(1,128)}), s32[4,1,768]{2,1,0:T(1,128)S(1)}, u32[]{:S(2)}, u32[]{:S(2)}) async-start(s32[4,1,768]{2,1,0:T(1,128)} %bitcast.13), calls=%async_computation | async-start | bytes 24576 | tf_op jit(solution)/shard_map/all_to_all | solution.py:36
  178.0 0.6 copy-start.6
  178.6 35.9 %all-to-all-start.1 = ((bf16[4,768,128]{2,1,0:T(8,128)(2,1)}), bf16[4,768,128]{2,1,0:T(8,128)(2,1)S(1)}, u32[]{:S(2)}, u32[]{:S(2)}) async-start(bf16[4,768,128]{2,1,0:T(8,128)(2,1)} %bitcast.15), calls=%async_computation.1 | async-start | bytes 1572864 | tf_op jit(solution)/shard_map/all_to_all | solution.py:35
  182.2 153.9 %all-reduce.5.cloned.1.call-start = ((), (), s32[]{:S(2)}) async-start(), calls=%async_computation.4 | async-start | bytes 262144 | tf_op jit(solution)/shard_map/psum | solution.py:74
  188.5 26.1 %copy-start.7 = (s32[4,1,768]{2,1,0:T(1,128)S(1)}, s32[4,1,768]{2,1,0:T(1,128)}, u32[]{:S(2)}) copy-start(s32[4,1,768]{2,1,0:T(1,128)} %copy-done.6) | copy-start | bytes 36868
  364.8 2.6 copy-start.4
  366.3 1.2 copy-start.2
  366.3 1.2 copy-start.3
Sparse Core Ops, SparseCore 0:
  9.9 35.0 all-gather.1
  51.3 122.4 all-reduce.2
  214.7 121.4 all-reduce.4
where the time goes:
time: 394 us; the launch traced here: 393 us
  waiting for transfers between devices  251 us (64%)
  blocking collectives  57.2 us (15%)
  local copies, waits for them, and re-layouts  22.8 us (6%)
  matrix products  20.6 us (5%)
  other arithmetic  19.2 us (5%)
  between operations  14 us (4%)
  starting transfers between devices  8.25 us (2%)
    psum x2, waiting for transfers between devices, shards(): left_basis = lax.psum(partial_left, ('rep', 'tp')) / replicas  225 us
    psum x2, blocking collectives, shards(): right_basis = lax.psum(partial_right, 'rep') / replicas  39.8 us
    all_gather x1, waiting for transfers between devices, shards(): lax.all_gather(activations, 'tp', axis=0, tiled=True)  25.9 us
    all_gather x1, blocking collectives, shards(): lax.all_gather(master_new.astype(jnp.bfloat16), 'rep', axis=0, tiled=True)  17.4 us
    unnamed x23, local copies, waits for them, and re-layouts  14 us
    gather x1, local copies, waits for them, and re-layouts, word_update(): targets = owner_map[token_ids]  8.39 us
  transfers between devices with their start and end apart: 5, of which 3 were waited for; matrix products, arithmetic and copies ran while one was open for 10% of the time, Pallas kernels for 0%

commit v1 on v0

--- a/solution.py
+++ b/solution.py
@@ -9,6 +9,22 @@
 MOMENTUM = 0.9
 LEARNING_RATE = 4.0
 EMBED_RATE = 0.5
+
+
+def tree_sum(value, axes):
+    if isinstance(axes, str):
+        axes = (axes,)
+    count = 1
+    for axis in axes:
+        count *= lax.axis_size(axis)
+    if count & (count - 1):
+        return lax.psum(value, axes)
+    stride = 1
+    while stride < count:
+        pairs = [(i, i ^ stride) for i in range(count)]
+        value = value + lax.ppermute(value, axes, pairs)
+        stride *= 2
+    return value
 
 
 def orthonormal(left_basis, gram_matrix):
@@ -71,13 +87,13 @@
     left_basis = None
     for round_index in range(ROUNDS):
         partial_left = jnp.dot(combined, right_basis, precision=highest)
-        left_basis = lax.psum(partial_left, ("rep", "tp")) / replicas
+        left_basis = tree_sum(partial_left, ("rep", "tp")) / replicas
         gram_matrix = jnp.dot(left_basis.T, left_basis, precision=highest)
         left_basis = orthonormal(left_basis, gram_matrix)
         partial_right = lax.dot_general(
             combined, left_basis, (((0,), (0,)), ((), ())), precision=highest
         )
-        right_basis = lax.psum(partial_right, "rep") / replicas
+        right_basis = tree_sum(partial_right, "rep") / replicas
     approx = jnp.dot(left_basis, right_basis.T, precision=highest)
     error_new = (combined - approx).astype(jnp.bfloat16)[None]
     owned_rows = qkv_master.shape[0]

time: 394 us -> 190 us (0.48)
  waiting for transfers between devices: 251 us -> 75.5 us
  blocking collectives: 57.2 us -> 17.3 us
  starting transfers between devices: 8.25 us -> 28.5 us
  matrix products: 20.6 us -> 14.3 us
    psum x2 -> x0, waiting for transfers between devices: 225 us -> none  [shards(): left_basis = lax.psum(partial_left, ('rep', 'tp')) / replicas]
    psum x2 -> x0, blocking collectives: 39.8 us -> none  [shards(): right_basis = lax.psum(partial_right, 'rep') / replicas]
    ppermute x0 -> x14, waiting for transfers between devices: none -> 35.6 us  [tree_sum(): value = value + lax.ppermute(value, axes, pairs)]
    ppermute x0 -> x14, starting transfers between devices: none -> 20 us  [tree_sum(): value = value + lax.ppermute(value, axes, pairs)]
    all_gather x1, waiting for transfers between devices: 25.9 us -> 37 us  [shards(): lax.all_gather(activations, 'tp', axis=0, tiled=True)]
  transfers between devices with their start and end apart: 5 -> 17, of which waited for: 3 -> 13; matrix products, arithmetic and copies ran while one was open for 10% -> 18% of each run, Pallas kernels for 0% -> 0%
where the time goes in v1:
time: 190 us; the launch traced here: 189 us
  waiting for transfers between devices  75.5 us (40%)
  starting transfers between devices  28.5 us (15%)
  local copies, waits for them, and re-layouts  22.2 us (12%)
  other arithmetic  17.3 us (9%)
  blocking collectives  17.3 us (9%)
  matrix products  14.3 us (8%)
  between operations  14.3 us (8%)
    all_gather x1, waiting for transfers between devices, shards(): lax.all_gather(activations, 'tp', axis=0, tiled=True)  37 us
    ppermute x14, waiting for transfers between devices, tree_sum(): value = value + lax.ppermute(value, axes, pairs)  35.6 us
    ppermute x14, starting transfers between devices, tree_sum(): value = value + lax.ppermute(value, axes, pairs)  20 us
    all_gather x1, blocking collectives, shards(): lax.all_gather(master_new.astype(jnp.bfloat16), 'rep', axis=0, tiled=True)  17.3 us
    unnamed x23, local copies, waits for them, and re-layouts  13.4 us
    gather x1, local copies, waits for them, and re-layouts, word_update(): targets = owner_map[token_ids]  8.39 us
    another operation x6, other arithmetic, orthonormal(): factor_low = jnp.linalg.cholesky(gram_matrix)  7.18 us
    another operation x4, other arithmetic, orthonormal(): jax.scipy.linalg.solve_triangular(factor_low, left_basis.T, lower=True)  6.17 us
  transfers between devices with their start and end apart: 17, of which 13 were waited for; matrix products, arithmetic and copies ran while one was open for 18% of the time, Pallas kernels for 0%

profile of v1, /device:TPU:0, one launch (start us, length us, event | category | flops | bytes accessed | tf_op | source)
XLA Modules:
  0.0 189.4 jit_solution(1805727197459856947)
XLA Ops:
  7.2 0.7 all-gather.2.cloned.1.call-update
  7.9 37.0 %all-gather.2.cloned.1.call-done = bf16[1536,1024]{1,0:T(8,128)(2,1)} async-done(((bf16[192,1024]{1,0:T(8,128)(2,1)}), bf16[1536,1024]{1,0:T(8,128)(2,1)}) %all-gather.2.cloned.1.call-update) | async-done | bytes 3145744 | tf_op jit(solution)/shard_map/all_gather | solution.py:80
  45.0 3.9 %convert_add_fusion = f32[1024,384]{1,0:T(8,128)S(1)} fusion(bf16[1536,1024]{1,0:T(8,128)(2,1)} %all-gather.2.cloned.1.call-done, bf16[1536,384]{1,0:T(8,128)(2,1)S(1)} %copy-done, bf16[1,1024,384]{2,1,0:T(8,128)(2,1)} %param.15), kind=kOutput, calls=%fused_computation.6 | convolution fusion | flops 1208745984 | bytes 6684672 | tf_op jit(solution)/shard_map/dot_general | solution.py:79
  48.9 1.6 fusion.38
  50.8 1.1 collective-permute-done
  51.9 1.5 collective-permute-start.1
  53.5 4.2 %collective-permute-done.1 = f32[1024,32]{0,1:T(8,128)S(1)} collective-permute-done((f32[1024,32]{0,1:T(8,128)S(1)}, f32[1024,32]{0,1:T(8,128)S(1)}, u32[]{:S(2)}, u32[]{:S(2)}) %collective-permute-start.1) | collective-permute-done | bytes 131104 | tf_op jit(solution)/shard_map/ppermute | solution.py:25
  57.7 1.4 collective-permute-start.2
  59.1 8.4 %gather_fusion = s32[1536]{0:T(1024)S(1)} fusion(s32[1600]{0:T(1024)S(1)} %copy-done.1, s32[2048]{0:T(1024)S(1)} %pad_clamp_fusion), kind=kCustom, calls=%fused_computation | custom fusion | bytes 18432 | tf_op jit(solution)/shard_map/gather | solution.py:39
  67.5 1.6 collective-permute-start.3
  69.1 3.5 %collective-permute-done.3 = f32[1024,32]{0,1:T(8,128)S(1)} collective-permute-done((f32[1024,32]{0,1:T(8,128)S(1)}, f32[1024,32]{0,1:T(8,128)S(1)}, u32[]{:S(2)}, u32[]{:S(2)}) %collective-permute-start.3) | collective-permute-done | bytes 131104 | tf_op jit(solution)/shard_map/ppermute | solution.py:25
  72.6 2.5 %collective-permute-start.4 = (f32[1024,32]{0,1:T(8,128)S(1)}, f32[1024,32]{0,1:T(8,128)S(1)}, u32[]{:S(2)}, u32[]{:S(2)}) collective-permute-start(f32[1024,32]{0,1:T(8,128)S(1)} %add.126), channel_id=1, source_target_pairs={{0,16},{1,17},{2,18},{3,19},{4,20},{5,21},{6,22},{7,23},{8,24},{9,... | collective-permute-start | bytes 393224 | tf_op jit(solution)/shard_map/ppermute | solution.py:25
  75.1 4.9 %collective-permute-done.4 = f32[1024,32]{0,1:T(8,128)S(1)} collective-permute-done((f32[1024,32]{0,1:T(8,128)S(1)}, f32[1024,32]{0,1:T(8,128)S(1)}, u32[]{:S(2)}, u32[]{:S(2)}) %collective-permute-start.4) | collective-permute-done | bytes 131104 | tf_op jit(solution)/shard_map/ppermute | solution.py:25
  80.3 2.9 %cholesky.44 = f32[32,32]{1,0:T(8,128)S(1)} custom-call(f32[32,32]{1,0:T(8,128)S(1)} %fusion.25), custom_call_target="Cholesky" | custom-call | tf_op jit(solution)/shard_map/jit(cholesky)/cholesky | solution.py:31
  83.9 0.7 fusion.20
  84.5 2.4 %custom-call.6 = f32[1,32,32]{1,2,0:T(8,128)S(1)} custom-call(f32[1,32,32]{2,1,0:T(8,128)S(1)} %fusion.20), custom_call_target="InvertDiagBlocksLowerTriangular" | custom-call | tf_op jit(solution)/shard_map/jit(_solve_triangular)/triangular_solve | solution.py:32
  87.3 1.0 fusion.39
  88.8 1.1 reduce-window.6
  90.0 2.8 %collective-permute-done.5 = f32[384,32]{0,1:T(8,128)S(1)} collective-permute-done((f32[384,32]{0,1:T(8,128)S(1)}, f32[384,32]{0,1:T(8,128)S(1)}, u32[]{:S(2)}, u32[]{:S(2)}) %collective-permute-start.5) | collective-permute-done | bytes 49184 | tf_op jit(solution)/shard_map/ppermute | solution.py:25
  92.8 1.7 collective-permute-start.6
  94.8 3.0 %collective-permute-done.6 = f32[384,32]{0,1:T(8,128)S(1)} collective-permute-done((f32[384,32]{0,1:T(8,128)S(1)}, f32[384,32]{0,1:T(8,128)S(1)}, u32[]{:S(2)}, u32[]{:S(2)}) %collective-permute-start.6) | collective-permute-done | bytes 49184 | tf_op jit(solution)/shard_map/ppermute | solution.py:25
  97.8 1.6 fusion.13
  99.6 1.2 collective-permute-done.7
  100.9 0.8 collective-permute-start.8
  101.6 4.8 %collective-permute-done.8 = f32[1024,32]{0,1:T(8,128)S(1)} collective-permute-done((f32[1024,32]{0,1:T(8,128)S(1)}, f32[1024,32]{0,1:T(8,128)S(1)}, u32[]{:S(2)}, u32[]{:S(2)}) %collective-permute-start.8) | collective-permute-done | bytes 131104 | tf_op jit(solution)/shard_map/ppermute | solution.py:25
  106.5 0.8 collective-permute-start.9
  107.3 4.2 %collective-permute-done.9 = f32[1024,32]{0,1:T(8,128)S(1)} collective-permute-done((f32[1024,32]{0,1:T(8,128)S(1)}, f32[1024,32]{0,1:T(8,128)S(1)}, u32[]{:S(2)}, u32[]{:S(2)}) %collective-permute-start.9) | collective-permute-done | bytes 131104 | tf_op jit(solution)/shard_map/ppermute | solution.py:25
  111.5 1.2 collective-permute-start.10
  113.0 3.6 %collective-permute-done.10 = f32[1024,32]{0,1:T(8,128)S(1)} collective-permute-done((f32[1024,32]{0,1:T(8,128)S(1)}, f32[1024,32]{0,1:T(8,128)S(1)}, u32[]{:S(2)}, u32[]{:S(2)}) %collective-permute-start.10) | collective-permute-done | bytes 131104 | tf_op jit(solution)/shard_map/ppermute | solution.py:25
  116.6 2.1 %collective-permute-start.11 = (f32[1024,32]{0,1:T(8,128)S(1)}, f32[1024,32]{0,1:T(8,128)S(1)}, u32[]{:S(2)}, u32[]{:S(2)}) collective-permute-start(f32[1024,32]{0,1:T(8,128)S(1)} %add.133), channel_id=1, source_target_pairs={{0,16},{1,17},{2,18},{3,19},{4,20},{5,21},{6,22},{7,23},{8,24},{9,... | collective-permute-start | bytes 393224 | tf_op jit(solution)/shard_map/ppermute | solution.py:25
  118.7 6.8 %scatter_custom_fusion = s32[3072]{0:T(1024)} fusion(s32[1536]{0:T(1024)S(1)} %broadcast_select_fusion, s32[1536]{0:T(1024)S(1)} %get-tuple-element.13, s32[]{:T(128)} %constant.83.clone.1), kind=kCustom, calls=%fused_computation.65 | custom fusion | bytes 12292
  125.5 3.3 %all-to-all-start = ((s32[4,1,768]{2,1,0:T(1,128)}), s32[4,1,768]{2,1,0:T(1,128)S(1)}, u32[]{:S(2)}, u32[]{:S(2)}) async-start(s32[4,1,768]{2,1,0:T(1,128)} %bitcast.13), calls=%async_computation | async-start | bytes 24576 | tf_op jit(solution)/shard_map/all_to_all | solution.py:52
  128.8 5.7 %scatter_custom_fusion.1 = bf16[3072,128]{1,0:T(8,128)(2,1)} fusion(s32[1536]{0:T(1024)S(1)} %broadcast_select_fusion, bf16[1536,128]{1,0:T(8,128)(2,1)} %param.19, bf16[]{:T(256)} %constant.89.clone.1), kind=kCustom, calls=%fused_computation.11 | custom fusion | bytes 786944
  134.8 5.1 %all-to-all-start.1 = ((bf16[4,768,128]{2,1,0:T(8,128)(2,1)}), bf16[4,768,128]{2,1,0:T(8,128)(2,1)}, u32[]{:S(2)}, u32[]{:S(2)}) async-start(bf16[4,768,128]{2,1,0:T(8,128)(2,1)} %bitcast.15), calls=%async_computation.1 | async-start | bytes 1572864 | tf_op jit(solution)/shard_map/all_to_all | solution.py:51
  139.9 2.9 %cholesky.55 = f32[32,32]{1,0:T(8,128)S(1)} custom-call(f32[32,32]{1,0:T(8,128)S(1)} %fusion.23), custom_call_target="Cholesky" | custom-call | tf_op jit(solution)/shard_map/jit(cholesky)/cholesky | solution.py:31
  143.5 0.7 fusion.21
  144.2 2.4 %custom-call.7 = f32[1,32,32]{1,2,0:T(8,128)S(1)} custom-call(f32[1,32,32]{2,1,0:T(8,128)S(1)} %fusion.21), custom_call_target="InvertDiagBlocksLowerTriangular" | custom-call | tf_op jit(solution)/shard_map/jit(_solve_triangular)/triangular_solve | solution.py:32
  147.0 1.0 fusion.40
  148.0 2.1 %collective-permute-start.12 = (f32[384,32]{0,1:T(8,128)S(1)}, f32[384,32]{0,1:T(8,128)S(1)}, u32[]{:S(2)}, u32[]{:S(2)}) collective-permute-start(f32[384,32]{0,1:T(8,128)S(1)} %fusion.40), channel_id=1, source_target_pairs={{0,8},{8,0},{16,24},{24,16},{1,9},{9,1},{17,25},{25,17},{2,10},{10... | collective-permute-start | bytes 147464 | tf_op jit(solution)/shard_map/ppermute | solution.py:25
  150.0 2.4 %collective-permute-done.12 = f32[384,32]{0,1:T(8,128)S(1)} collective-permute-done((f32[384,32]{0,1:T(8,128)S(1)}, f32[384,32]{0,1:T(8,128)S(1)}, u32[]{:S(2)}, u32[]{:S(2)}) %collective-permute-start.12) | collective-permute-done | bytes 49184 | tf_op jit(solution)/shard_map/ppermute | solution.py:25
  152.4 3.5 %collective-permute-start.13 = (f32[384,32]{0,1:T(8,128)S(1)}, f32[384,32]{0,1:T(8,128)S(1)}, u32[]{:S(2)}, u32[]{:S(2)}) collective-permute-start(f32[384,32]{0,1:T(8,128)S(1)} %add.135), channel_id=1, source_target_pairs={{0,16},{8,24},{16,0},{24,8},{1,17},{9,25},{17,1},{25,9},{2,18},{10... | collective-permute-start | bytes 147464 | tf_op jit(solution)/shard_map/ppermute | solution.py:25
  155.9 2.1 %all-to-all-done.1 = bf16[4,768,128]{2,1,0:T(8,128)(2,1)} async-done(((bf16[4,768,128]{2,1,0:T(8,128)(2,1)}), bf16[4,768,128]{2,1,0:T(8,128)(2,1)}, u32[]{:S(2)}, u32[]{:S(2)}) %all-to-all-start.1) | async-done | bytes 786464 | tf_op jit(solution)/shard_map/all_to_all | solution.py:51
  158.0 2.7 %fusion.3 = f32[400,128]{1,0:T(8,128)} fusion(f32[400,128]{1,0:T(8,128)S(1)} %copy-done.9, bf16[3072,128]{1,0:T(8,128)(2,1)} %bitcast.16, s32[3072]{0:T(1024)S(1)} %bitcast.64), kind=kOutput, calls=%fused_computation.9 | convolution fusion | flops 315904000 | bytes 1208320 | tf_op jit(solution)/shard_map/dot_general | solution.py:58
  160.7 1.5 fusion.41
  162.2 1.1 fusion.4
  163.4 1.0 fusion.37
  164.3 17.3 %all_gather.7 = bf16[1024,384]{1,0:T(8,128)(2,1)S(1)} all-gather(bf16[256,384]{1,0:T(8,128)(2,1)S(1)} %get-tuple-element.10), channel_id=1, replica_groups=mesh['rep'=4,'tp'=8] {'rep'}, dimensions={0}, use_global_device_ids=true | all-gather | bytes 983040 | tf_op jit(solution)/shard_map/all_gather | solution.py:105
  181.7 0.9 copy.25
  (65 shorter events, 4.7 us)
Async XLA Ops:
  7.2 37.8 %copy-start = (bf16[1536,384]{1,0:T(8,128)(2,1)S(1)}, bf16[1536,384]{1,0:T(8,128)(2,1)}, u32[]{:S(2)}) copy-start(bf16[1536,384]{1,0:T(8,128)(2,1)} %param.14) | copy-start | bytes 3538948
  7.2 37.8 %all-gather.2.cloned.1.call-start = ((), (), s32[]{:S(2)}) async-start(), calls=%async_computation.2 | async-start | bytes 3538944 | tf_op jit(solution)/shard_map/all_gather | solution.py:80
  7.9 41.0 %copy-start.5 = (f32[384,32]{0,1:T(8,128)S(1)}, f32[384,32]{0,1:T(8,128)}, u32[]{:S(2)}) copy-start(f32[384,32]{0,1:T(8,128)} %param.16) | copy-start | bytes 147460
  48.9 10.2 %copy-start.6 = (s32[1536]{0:T(1024)S(1)}, s32[1536]{0:T(1024)}, u32[]{:S(2)}) copy-start(s32[1536]{0:T(1024)} %param.20) | copy-start | bytes 18436
  48.9 10.2 %copy-start.1 = (s32[1600]{0:T(1024)S(1)}, s32[1600]{0:T(1024)}, u32[]{:S(2)}) copy-start(s32[1600]{0:T(1024)} %param.21) | copy-start | bytes 19204
  50.5 1.4 collective-permute-start
  51.9 5.7 %collective-permute-start.1 = (f32[1024,32]{0,1:T(8,128)S(1)}, f32[1024,32]{0,1:T(8,128)S(1)}, u32[]{:S(2)}, u32[]{:S(2)}) collective-permute-start(f32[1024,32]{0,1:T(8,128)S(1)} %add.123), channel_id=1, source_target_pairs={{0,2},{1,3},{2,0},{3,1},{4,6},{5,7},{6,4},{7,5},{8,10},{9,11},{10,... | collective-permute-start | bytes 393224 | tf_op jit(solution)/shard_map/ppermute | solution.py:25
  57.7 9.8 %collective-permute-start.2 = (f32[1024,32]{0,1:T(8,128)S(1)}, f32[1024,32]{0,1:T(8,128)S(1)}, u32[]{:S(2)}, u32[]{:S(2)}) collective-permute-start(f32[1024,32]{0,1:T(8,128)S(1)} %add.124), channel_id=1, source_target_pairs={{0,4},{1,5},{2,6},{3,7},{4,0},{5,1},{6,2},{7,3},{8,12},{9,13},{10,... | collective-permute-start | bytes 393224 | tf_op jit(solution)/shard_map/ppermute | solution.py:25
  67.5 5.0 %collective-permute-start.3 = (f32[1024,32]{0,1:T(8,128)S(1)}, f32[1024,32]{0,1:T(8,128)S(1)}, u32[]{:S(2)}, u32[]{:S(2)}) collective-permute-start(f32[1024,32]{0,1:T(8,128)S(1)} %add.125), channel_id=1, source_target_pairs={{0,8},{1,9},{2,10},{3,11},{4,12},{5,13},{6,14},{7,15},{8,0},{9,1},... | collective-permute-start | bytes 393224 | tf_op jit(solution)/shard_map/ppermute | solution.py:25
  72.6 7.3 %collective-permute-start.4 = (f32[1024,32]{0,1:T(8,128)S(1)}, f32[1024,32]{0,1:T(8,128)S(1)}, u32[]{:S(2)}, u32[]{:S(2)}) collective-permute-start(f32[1024,32]{0,1:T(8,128)S(1)} %add.126), channel_id=1, source_target_pairs={{0,16},{1,17},{2,18},{3,19},{4,20},{5,21},{6,22},{7,23},{8,24},{9,... | collective-permute-start | bytes 393224 | tf_op jit(solution)/shard_map/ppermute | solution.py:25
  88.3 4.5 %collective-permute-start.5 = (f32[384,32]{0,1:T(8,128)S(1)}, f32[384,32]{0,1:T(8,128)S(1)}, u32[]{:S(2)}, u32[]{:S(2)}) collective-permute-start(f32[384,32]{0,1:T(8,128)S(1)} %fusion.39), channel_id=1, source_target_pairs={{0,8},{8,0},{16,24},{24,16},{1,9},{9,1},{17,25},{25,17},{2,10},{10... | collective-permute-start | bytes 147464 | tf_op jit(solution)/shard_map/ppermute | solution.py:25
  92.8 5.1 %collective-permute-start.6 = (f32[384,32]{0,1:T(8,128)S(1)}, f32[384,32]{0,1:T(8,128)S(1)}, u32[]{:S(2)}, u32[]{:S(2)}) collective-permute-start(f32[384,32]{0,1:T(8,128)S(1)} %add.128), channel_id=1, source_target_pairs={{0,16},{8,24},{16,0},{24,8},{1,17},{9,25},{17,1},{25,9},{2,18},{10... | collective-permute-start | bytes 147464 | tf_op jit(solution)/shard_map/ppermute | solution.py:25
  94.8 17.9 %copy-start.8 = (s32[2]{0:T(128)S(1)}, s32[2]{0:T(128)}, u32[]{:S(2)}) copy-start(s32[2]{0:T(128)} %constant.92) | copy-start | bytes 28
  94.8 18.0 %copy-start.7 = (s32[2]{0:T(128)S(1)}, s32[2]{0:T(128)}, u32[]{:S(2)}) copy-start(s32[2]{0:T(128)} %constant.95) | copy-start | bytes 28
  99.4 1.4 collective-permute-start.7
  100.9 5.6 %collective-permute-start.8 = (f32[1024,32]{0,1:T(8,128)S(1)}, f32[1024,32]{0,1:T(8,128)S(1)}, u32[]{:S(2)}, u32[]{:S(2)}) collective-permute-start(f32[1024,32]{0,1:T(8,128)S(1)} %add.130), channel_id=1, source_target_pairs={{0,2},{1,3},{2,0},{3,1},{4,6},{5,7},{6,4},{7,5},{8,10},{9,11},{10,... | collective-permute-start | bytes 393224 | tf_op jit(solution)/shard_map/ppermute | solution.py:25
  106.5 5.0 %collective-permute-start.9 = (f32[1024,32]{0,1:T(8,128)S(1)}, f32[1024,32]{0,1:T(8,128)S(1)}, u32[]{:S(2)}, u32[]{:S(2)}) collective-permute-start(f32[1024,32]{0,1:T(8,128)S(1)} %add.131), channel_id=1, source_target_pairs={{0,4},{1,5},{2,6},{3,7},{4,0},{5,1},{6,2},{7,3},{8,12},{9,13},{10,... | collective-permute-start | bytes 393224 | tf_op jit(solution)/shard_map/ppermute | solution.py:25
  111.5 5.0 %collective-permute-start.10 = (f32[1024,32]{0,1:T(8,128)S(1)}, f32[1024,32]{0,1:T(8,128)S(1)}, u32[]{:S(2)}, u32[]{:S(2)}) collective-permute-start(f32[1024,32]{0,1:T(8,128)S(1)} %add.132), channel_id=1, source_target_pairs={{0,8},{1,9},{2,10},{3,11},{4,12},{5,13},{6,14},{7,15},{8,0},{9,1},... | collective-permute-start | bytes 393224 | tf_op jit(solution)/shard_map/ppermute | solution.py:25
  116.6 17.9 %collective-permute-start.11 = (f32[1024,32]{0,1:T(8,128)S(1)}, f32[1024,32]{0,1:T(8,128)S(1)}, u32[]{:S(2)}, u32[]{:S(2)}) collective-permute-start(f32[1024,32]{0,1:T(8,128)S(1)} %add.133), channel_id=1, source_target_pairs={{0,16},{1,17},{2,18},{3,19},{4,20},{5,21},{6,22},{7,23},{8,24},{9,... | collective-permute-start | bytes 393224 | tf_op jit(solution)/shard_map/ppermute | solution.py:25
  125.5 9.4 %all-to-all-start = ((s32[4,1,768]{2,1,0:T(1,128)}), s32[4,1,768]{2,1,0:T(1,128)S(1)}, u32[]{:S(2)}, u32[]{:S(2)}) async-start(s32[4,1,768]{2,1,0:T(1,128)} %bitcast.13), calls=%async_computation | async-start | bytes 24576 | tf_op jit(solution)/shard_map/all_to_all | solution.py:52
  134.8 23.2 %all-to-all-start.1 = ((bf16[4,768,128]{2,1,0:T(8,128)(2,1)}), bf16[4,768,128]{2,1,0:T(8,128)(2,1)}, u32[]{:S(2)}, u32[]{:S(2)}) async-start(bf16[4,768,128]{2,1,0:T(8,128)(2,1)} %bitcast.15), calls=%async_computation.1 | async-start | bytes 1572864 | tf_op jit(solution)/shard_map/all_to_all | solution.py:51
  139.9 18.1 %copy-start.9 = (f32[400,128]{1,0:T(8,128)S(1)}, f32[400,128]{1,0:T(8,128)}, u32[]{:S(2)}) copy-start(f32[400,128]{1,0:T(8,128)} %param.22) | copy-start | bytes 614404
  148.0 4.5 %collective-permute-start.12 = (f32[384,32]{0,1:T(8,128)S(1)}, f32[384,32]{0,1:T(8,128)S(1)}, u32[]{:S(2)}, u32[]{:S(2)}) collective-permute-start(f32[384,32]{0,1:T(8,128)S(1)} %fusion.40), channel_id=1, source_target_pairs={{0,8},{8,0},{16,24},{24,16},{1,9},{9,1},{17,25},{25,17},{2,10},{10... | collective-permute-start | bytes 147464 | tf_op jit(solution)/shard_map/ppermute | solution.py:25
  152.4 8.3 %collective-permute-start.13 = (f32[384,32]{0,1:T(8,128)S(1)}, f32[384,32]{0,1:T(8,128)S(1)}, u32[]{:S(2)}, u32[]{:S(2)}) collective-permute-start(f32[384,32]{0,1:T(8,128)S(1)} %add.135), channel_id=1, source_target_pairs={{0,16},{8,24},{16,0},{24,8},{1,17},{9,25},{17,1},{25,9},{2,18},{10... | collective-permute-start | bytes 147464 | tf_op jit(solution)/shard_map/ppermute | solution.py:25
  160.7 2.6 %copy-start.4 = (f32[384,32]{0,1:T(8,128)}, f32[384,32]{0,1:T(8,128)S(1)}, u32[]{:S(2)}) copy-start(f32[384,32]{0,1:T(8,128)S(1)} %add_multiply_fusion.6) | copy-start | bytes 147460
  162.2 1.2 copy-start.2
  162.2 1.2 copy-start.3
Sparse Core Ops, SparseCore 0:
  9.9 35.0 all-gather.1

commit v2 on v1

--- a/solution.py
+++ b/solution.py
@@ -25,6 +25,32 @@
         value = value + lax.ppermute(value, axes, pairs)
         stride *= 2
     return value
+
+
+def gather_rows(block, axis):
+    count = lax.axis_size(axis)
+    if count != 8 or block.shape[0] % 2:
+        return lax.all_gather(block, axis, axis=0, tiled=True)
+    me = lax.axis_index(axis)
+
+    def exchange(value, stride):
+        return lax.ppermute(value, axis, [(i, i ^ stride) for i in range(count)])
+
+    from_x = exchange(block, 2)
+    from_y = exchange(block, 4)
+    half = block.shape[0] // 2
+    diagonal = jnp.concatenate(
+        [exchange(from_y[:half], 2), exchange(from_x[half:], 4)], axis=0
+    )
+    other = exchange(jnp.stack([block, from_x, from_y, diagonal]), 1)
+    pieces = {0: block, 2: from_x, 4: from_y, 6: diagonal}
+    for index, offset in enumerate((1, 3, 5, 7)):
+        pieces[offset] = other[index]
+    rows = block.shape[0]
+    gathered = jnp.zeros((count * rows,) + block.shape[1:], block.dtype)
+    for offset, piece in pieces.items():
+        gathered = lax.dynamic_update_slice_in_dim(gathered, piece, (me ^ offset) * rows, 0)
+    return gathered
 
 
 def orthonormal(left_basis, gram_matrix):
@@ -77,7 +103,7 @@
     replicas = lax.axis_size("rep")
     word_new = None
     product = lax.dot_general(
-        lax.all_gather(activations, "tp", axis=0, tiled=True),
+        gather_rows(activations, "tp"),
         out_grads,
         (((0,), (0,)), ((), ())),
         preferred_element_type=jnp.float32,

time: 190 us -> 166 us (0.87)
  waiting for transfers between devices: 75.5 us -> 52.5 us
  between operations: 14.3 us -> 1.04 us
  starting transfers between devices: 28.5 us -> 36.9 us
  local copies, waits for them, and re-layouts: 22.2 us -> 26.9 us
  matrix products: 14.3 us -> 12.3 us
    all_gather x1 -> x0, waiting for transfers between devices: 37 us -> none  [shards(): lax.all_gather(activations, 'tp', axis=0, tiled=True)]
    ppermute x0 -> x5, waiting for transfers between devices: none -> 15.1 us  [exchange(): return lax.ppermute(value, axis, [(i, i ^ stride) for i in range(count)])]
    ppermute x0 -> x5, starting transfers between devices: none -> 7.89 us  [exchange(): return lax.ppermute(value, axis, [(i, i ^ stride) for i in range(count)])]
    dynamic_update_slice x0 -> x8, local copies, waits for them, and re-layouts: none -> 4.26 us  [gather_rows(): lax.dynamic_update_slice_in_dim(gathered, piece, (me ^ offset) * rows, 0)]
    dot_general x1, matrix products: 3.92 us -> 1.88 us  [shards(): lax.dot_general(gather_rows(activations, 'tp'), out_grads, (((0,), (0,)),...]
    unnamed x23 -> x28, local copies, waits for them, and re-layouts: 13.4 us -> 13.5 us
  transfers between devices with their start and end apart: 17 -> 21, of which waited for: 13 -> 16; matrix products, arithmetic and copies ran while one was open for 18% -> 21% of each run, Pallas kernels for 0% -> 0%
where the time goes in v2:
time: 166 us
  waiting for transfers between devices  52.5 us (32%)
  starting transfers between devices  36.9 us (22%)
  local copies, waits for them, and re-layouts  26.9 us (16%)
  other arithmetic  18.7 us (11%)
  blocking collectives  17.3 us (10%)
  matrix products  12.3 us (7%)
    ppermute x14, waiting for transfers between devices, tree_sum(): value = value + lax.ppermute(value, axes, pairs)  35.3 us
    ppermute x14, starting transfers between devices, tree_sum(): value = value + lax.ppermute(value, axes, pairs)  20.7 us
    all_gather x1, blocking collectives, shards(): lax.all_gather(master_new.astype(jnp.bfloat16), 'rep', axis=0, tiled=True)  17.3 us
    ppermute x5, waiting for transfers between devices, exchange(): return lax.ppermute(value, axis, [(i, i ^ stride) for i in range(count)])  15.1 us
    unnamed x28, local copies, waits for them, and re-layouts  13.5 us
    gather x1, local copies, waits for them, and re-layouts, word_update(): targets = owner_map[token_ids]  8.39 us
    ppermute x5, starting transfers between devices, exchange(): return lax.ppermute(value, axis, [(i, i ^ stride) for i in range(count)])  7.89 us
    another operation x6, other arithmetic, orthonormal(): factor_low = jnp.linalg.cholesky(gram_matrix)  7.18 us
  transfers between devices with their start and end apart: 21, of which 16 were waited for; matrix products, arithmetic and copies ran while one was open for 21% of the time, Pallas kernels for 0%

profile of v2, /device:TPU:0, one launch (start us, length us, event | category | flops | bytes accessed | tf_op | source)
XLA Modules:
  0.0 165.6 jit_solution(11085591567253906750)
XLA Ops:
  0.7 3.0 %collective-permute-start.1 = (bf16[192,1024]{1,0:T(8,128)(2,1)}, bf16[192,1024]{1,0:T(8,128)(2,1)S(1)}, u32[]{:S(2)}, u32[]{:S(2)}) collective-permute-start(bf16[192,1024]{1,0:T(8,128)(2,1)} %param.13), channel_id=1, source_target_pairs={{0,4},{1,5},{2,6},{3,7},{4,0},{5,1},{6,2},{7,3},{8,12},{9,13},{10,... | collective-permute-start | bytes 1179656 | tf_op jit(solution)/shard_map/ppermute | solution.py:37
  3.7 1.5 collective-permute-start
  5.2 7.8 %collective-permute-done.1 = bf16[192,1024]{1,0:T(8,128)(2,1)S(1)} collective-permute-done((bf16[192,1024]{1,0:T(8,128)(2,1)}, bf16[192,1024]{1,0:T(8,128)(2,1)S(1)}, u32[]{:S(2)}, u32[]{:S(2)}) %collective-permute-start.1) | collective-permute-done | bytes 393248 | tf_op jit(solution)/shard_map/ppermute | solution.py:37
  13.0 1.8 %collective-permute-start.2 = (bf16[96,1024]{1,0:T(8,128)(2,1)S(1)}, bf16[96,1024]{1,0:T(8,128)(2,1)S(1)}, u32[]{:S(2)}, u32[]{:S(2)}) collective-permute-start(bf16[96,1024]{1,0:T(8,128)(2,1)S(1)} %slice.42), channel_id=1, source_target_pairs={{0,2},{1,3},{2,0},{3,1},{4,6},{5,7},{6,4},{7,5},{8,10},{9,11},{10,... | collective-permute-start | bytes 589832 | tf_op jit(solution)/shard_map/ppermute | solution.py:37
  14.8 1.6 collective-permute-start.3
  16.4 2.8 %collective-permute-done.2 = bf16[96,1024]{1,0:T(8,128)(2,1)S(1)} collective-permute-done((bf16[96,1024]{1,0:T(8,128)(2,1)S(1)}, bf16[96,1024]{1,0:T(8,128)(2,1)S(1)}, u32[]{:S(2)}, u32[]{:S(2)}) %collective-permute-start.2) | collective-permute-done | bytes 196640 | tf_op jit(solution)/shard_map/ppermute | solution.py:37
  19.2 1.4 collective-permute-done.3
  20.6 1.4 pad_maximum_fusion
  22.5 3.2 %collective-permute-done.4 = bf16[4,192,1024]{2,1,0:T(8,128)(2,1)} collective-permute-done((bf16[4,192,1024]{2,1,0:T(8,128)(2,1)}, bf16[4,192,1024]{2,1,0:T(8,128)(2,1)}, u32[]{:S(2)}, u32[]{:S(2)}) %collective-permute-start.4) | collective-permute-done | bytes 1572896 | tf_op jit(solution)/shard_map/ppermute | solution.py:37
  26.7 1.0 fusion.7
  29.9 1.9 %convert_add_fusion = f32[1024,384]{1,0:T(8,128)S(1)} fusion(bf16[1536,1024]{1,0:T(8,128)(2,1)S(1)} %fusion.5, bf16[1536,384]{1,0:T(8,128)(2,1)S(1)} %copy-done, bf16[1,1024,384]{2,1,0:T(8,128)(2,1)S(1)} %copy-done.10), kind=kOutput, calls=%fused_computation.7 | convolution fusion | flops 1208745984 | bytes 6684672 | tf_op jit(solution)/shard_map/dot_general | solution.py:105
  31.8 1.6 fusion.42
  33.6 1.2 collective-permute-done.5
  34.8 1.2 collective-permute-start.6
  36.0 4.4 %collective-permute-done.6 = f32[1024,32]{0,1:T(8,128)S(1)} collective-permute-done((f32[1024,32]{0,1:T(8,128)S(1)}, f32[1024,32]{0,1:T(8,128)S(1)}, u32[]{:S(2)}, u32[]{:S(2)}) %collective-permute-start.6) | collective-permute-done | bytes 131104 | tf_op jit(solution)/shard_map/ppermute | solution.py:25
  40.4 1.6 collective-permute-start.7
  42.0 8.4 %gather_fusion = s32[1536]{0:T(1024)S(1)} fusion(s32[1600]{0:T(1024)S(1)} %copy-done.1, s32[2048]{0:T(1024)S(1)} %pad_clamp_fusion), kind=kCustom, calls=%fused_computation | custom fusion | bytes 18432 | tf_op jit(solution)/shard_map/gather | solution.py:65
  50.5 1.6 collective-permute-start.8
  52.1 3.4 %collective-permute-done.8 = f32[1024,32]{0,1:T(8,128)S(1)} collective-permute-done((f32[1024,32]{0,1:T(8,128)S(1)}, f32[1024,32]{0,1:T(8,128)S(1)}, u32[]{:S(2)}, u32[]{:S(2)}) %collective-permute-start.8) | collective-permute-done | bytes 131104 | tf_op jit(solution)/shard_map/ppermute | solution.py:25
  55.5 2.7 %collective-permute-start.9 = (f32[1024,32]{0,1:T(8,128)S(1)}, f32[1024,32]{0,1:T(8,128)S(1)}, u32[]{:S(2)}, u32[]{:S(2)}) collective-permute-start(f32[1024,32]{0,1:T(8,128)S(1)} %add.158), channel_id=1, source_target_pairs={{0,16},{1,17},{2,18},{3,19},{4,20},{5,21},{6,22},{7,23},{8,24},{9,... | collective-permute-start | bytes 393224 | tf_op jit(solution)/shard_map/ppermute | solution.py:25
  58.2 4.7 %collective-permute-done.9 = f32[1024,32]{0,1:T(8,128)S(1)} collective-permute-done((f32[1024,32]{0,1:T(8,128)S(1)}, f32[1024,32]{0,1:T(8,128)S(1)}, u32[]{:S(2)}, u32[]{:S(2)}) %collective-permute-start.9) | collective-permute-done | bytes 131104 | tf_op jit(solution)/shard_map/ppermute | solution.py:25
  63.2 2.9 %cholesky.44 = f32[32,32]{1,0:T(8,128)S(1)} custom-call(f32[32,32]{1,0:T(8,128)S(1)} %fusion.29), custom_call_target="Cholesky" | custom-call | tf_op jit(solution)/shard_map/jit(cholesky)/cholesky | solution.py:57
  67.5 2.4 %custom-call.6 = f32[1,32,32]{1,2,0:T(8,128)S(1)} custom-call(f32[1,32,32]{2,1,0:T(8,128)S(1)} %fusion.24), custom_call_target="InvertDiagBlocksLowerTriangular" | custom-call | tf_op jit(solution)/shard_map/jit(_solve_triangular)/triangular_solve | solution.py:58
  72.0 1.1 reduce-window.6
  73.1 2.5 %collective-permute-done.10 = f32[384,32]{0,1:T(8,128)S(1)} collective-permute-done((f32[384,32]{0,1:T(8,128)S(1)}, f32[384,32]{0,1:T(8,128)S(1)}, u32[]{:S(2)}, u32[]{:S(2)}) %collective-permute-start.10) | collective-permute-done | bytes 49184 | tf_op jit(solution)/shard_map/ppermute | solution.py:25
  75.6 1.9 %collective-permute-start.11 = (f32[384,32]{0,1:T(8,128)S(1)}, f32[384,32]{0,1:T(8,128)S(1)}, u32[]{:S(2)}, u32[]{:S(2)}) collective-permute-start(f32[384,32]{0,1:T(8,128)S(1)} %add.160), channel_id=1, source_target_pairs={{0,16},{8,24},{16,0},{24,8},{1,17},{9,25},{17,1},{25,9},{2,18},{10... | collective-permute-start | bytes 147464 | tf_op jit(solution)/shard_map/ppermute | solution.py:25
  77.9 2.7 %collective-permute-done.11 = f32[384,32]{0,1:T(8,128)S(1)} collective-permute-done((f32[384,32]{0,1:T(8,128)S(1)}, f32[384,32]{0,1:T(8,128)S(1)}, u32[]{:S(2)}, u32[]{:S(2)}) %collective-permute-start.11) | collective-permute-done | bytes 49184 | tf_op jit(solution)/shard_map/ppermute | solution.py:25
  80.7 1.6 fusion.17
  82.4 1.2 collective-permute-done.12
  84.3 5.0 %collective-permute-done.13 = f32[1024,32]{0,1:T(8,128)S(1)} collective-permute-done((f32[1024,32]{0,1:T(8,128)S(1)}, f32[1024,32]{0,1:T(8,128)S(1)}, u32[]{:S(2)}, u32[]{:S(2)}) %collective-permute-start.13) | collective-permute-done | bytes 131104 | tf_op jit(solution)/shard_map/ppermute | solution.py:25
  89.9 4.4 %collective-permute-done.14 = f32[1024,32]{0,1:T(8,128)S(1)} collective-permute-done((f32[1024,32]{0,1:T(8,128)S(1)}, f32[1024,32]{0,1:T(8,128)S(1)}, u32[]{:S(2)}, u32[]{:S(2)}) %collective-permute-start.14) | collective-permute-done | bytes 131104 | tf_op jit(solution)/shard_map/ppermute | solution.py:25
  94.4 1.5 collective-permute-start.15
  96.1 3.3 %collective-permute-done.15 = f32[1024,32]{0,1:T(8,128)S(1)} collective-permute-done((f32[1024,32]{0,1:T(8,128)S(1)}, f32[1024,32]{0,1:T(8,128)S(1)}, u32[]{:S(2)}, u32[]{:S(2)}) %collective-permute-start.15) | collective-permute-done | bytes 131104 | tf_op jit(solution)/shard_map/ppermute | solution.py:25
  99.4 2.4 %collective-permute-start.16 = (f32[1024,32]{0,1:T(8,128)S(1)}, f32[1024,32]{0,1:T(8,128)S(1)}, u32[]{:S(2)}, u32[]{:S(2)}) collective-permute-start(f32[1024,32]{0,1:T(8,128)S(1)} %add.165), channel_id=1, source_target_pairs={{0,16},{1,17},{2,18},{3,19},{4,20},{5,21},{6,22},{7,23},{8,24},{9,... | collective-permute-start | bytes 393224 | tf_op jit(solution)/shard_map/ppermute | solution.py:25
  101.8 6.8 %scatter_custom_fusion = s32[3072]{0:T(1024)} fusion(s32[1536]{0:T(1024)S(1)} %broadcast_select_fusion, s32[1536]{0:T(1024)S(1)} %get-tuple-element.13, s32[]{:T(128)} %constant.106.clone.1), kind=kCustom, calls=%fused_computation.74 | custom fusion | bytes 12292
  108.6 3.4 %all-to-all-start = ((s32[4,1,768]{2,1,0:T(1,128)}), s32[4,1,768]{2,1,0:T(1,128)S(1)}, u32[]{:S(2)}, u32[]{:S(2)}) async-start(s32[4,1,768]{2,1,0:T(1,128)} %bitcast.21), calls=%async_computation | async-start | bytes 24576 | tf_op jit(solution)/shard_map/all_to_all | solution.py:78
  112.0 5.7 %scatter_custom_fusion.1 = bf16[3072,128]{1,0:T(8,128)(2,1)} fusion(s32[1536]{0:T(1024)S(1)} %broadcast_select_fusion, bf16[1536,128]{1,0:T(8,128)(2,1)} %param.19, bf16[]{:T(256)} %constant.88.clone.1), kind=kCustom, calls=%fused_computation.20 | custom fusion | bytes 786944
  118.1 4.9 %all-to-all-start.1 = ((bf16[4,768,128]{2,1,0:T(8,128)(2,1)}), bf16[4,768,128]{2,1,0:T(8,128)(2,1)}, u32[]{:S(2)}, u32[]{:S(2)}) async-start(bf16[4,768,128]{2,1,0:T(8,128)(2,1)} %bitcast.23), calls=%async_computation.1 | async-start | bytes 1572864 | tf_op jit(solution)/shard_map/all_to_all | solution.py:77
  123.1 2.9 %cholesky.55 = f32[32,32]{1,0:T(8,128)S(1)} custom-call(f32[32,32]{1,0:T(8,128)S(1)} %fusion.27), custom_call_target="Cholesky" | custom-call | tf_op jit(solution)/shard_map/jit(cholesky)/cholesky | solution.py:57
  127.3 2.4 %custom-call.7 = f32[1,32,32]{1,2,0:T(8,128)S(1)} custom-call(f32[1,32,32]{2,1,0:T(8,128)S(1)} %fusion.25), custom_call_target="InvertDiagBlocksLowerTriangular" | custom-call | tf_op jit(solution)/shard_map/jit(_solve_triangular)/triangular_solve | solution.py:58
  131.1 2.1 %collective-permute-start.17 = (f32[384,32]{0,1:T(8,128)S(1)}, f32[384,32]{0,1:T(8,128)S(1)}, u32[]{:S(2)}, u32[]{:S(2)}) collective-permute-start(f32[384,32]{0,1:T(8,128)S(1)} %fusion.44), channel_id=1, source_target_pairs={{0,8},{8,0},{16,24},{24,16},{1,9},{9,1},{17,25},{25,17},{2,10},{10... | collective-permute-start | bytes 147464 | tf_op jit(solution)/shard_map/ppermute | solution.py:25
  133.2 2.4 %collective-permute-done.17 = f32[384,32]{0,1:T(8,128)S(1)} collective-permute-done((f32[384,32]{0,1:T(8,128)S(1)}, f32[384,32]{0,1:T(8,128)S(1)}, u32[]{:S(2)}, u32[]{:S(2)}) %collective-permute-start.17) | collective-permute-done | bytes 49184 | tf_op jit(solution)/shard_map/ppermute | solution.py:25
  135.5 3.5 %collective-permute-start.18 = (f32[384,32]{0,1:T(8,128)S(1)}, f32[384,32]{0,1:T(8,128)S(1)}, u32[]{:S(2)}, u32[]{:S(2)}) collective-permute-start(f32[384,32]{0,1:T(8,128)S(1)} %add.167), channel_id=1, source_target_pairs={{0,16},{8,24},{16,0},{24,8},{1,17},{9,25},{17,1},{25,9},{2,18},{10... | collective-permute-start | bytes 147464 | tf_op jit(solution)/shard_map/ppermute | solution.py:25
  139.0 2.1 %all-to-all-done.1 = bf16[4,768,128]{2,1,0:T(8,128)(2,1)} async-done(((bf16[4,768,128]{2,1,0:T(8,128)(2,1)}), bf16[4,768,128]{2,1,0:T(8,128)(2,1)}, u32[]{:S(2)}, u32[]{:S(2)}) %all-to-all-start.1) | async-done | bytes 786464 | tf_op jit(solution)/shard_map/all_to_all | solution.py:77
  141.2 2.7 %fusion.3 = f32[400,128]{1,0:T(8,128)} fusion(f32[400,128]{1,0:T(8,128)S(1)} %copy-done.11, bf16[3072,128]{1,0:T(8,128)(2,1)} %bitcast.24, s32[3072]{0:T(1024)S(1)} %bitcast.88), kind=kOutput, calls=%fused_computation.10 | convolution fusion | flops 315904000 | bytes 1208320 | tf_op jit(solution)/shard_map/dot_general | solution.py:84
  143.9 1.5 fusion.45
  145.3 1.1 fusion.4
  147.5 17.3 %all_gather.3 = bf16[1024,384]{1,0:T(8,128)(2,1)S(1)} all-gather(bf16[256,384]{1,0:T(8,128)(2,1)S(1)} %get-tuple-element.10), channel_id=1, replica_groups=mesh['rep'=4,'tp'=8] {'rep'}, dimensions={0}, use_global_device_ids=true | all-gather | bytes 983040 | tf_op jit(solution)/shard_map/all_gather | solution.py:131
  (90 shorter events, 14.6 us)
Async XLA Ops:
  0.6 29.2 %copy-start = (bf16[1536,384]{1,0:T(8,128)(2,1)S(1)}, bf16[1536,384]{1,0:T(8,128)(2,1)}, u32[]{:S(2)}) copy-start(bf16[1536,384]{1,0:T(8,128)(2,1)} %param.14) | copy-start | bytes 3538948
  0.6 19.9 %copy-start.2 = (bf16[192,1024]{1,0:T(8,128)(2,1)S(1)}, bf16[192,1024]{1,0:T(8,128)(2,1)}, u32[]{:S(2)}) copy-start(bf16[192,1024]{1,0:T(8,128)(2,1)} %param.13) | copy-start | bytes 1179652
  0.7 12.4 %collective-permute-start.1 = (bf16[192,1024]{1,0:T(8,128)(2,1)}, bf16[192,1024]{1,0:T(8,128)(2,1)S(1)}, u32[]{:S(2)}, u32[]{:S(2)}) collective-permute-start(bf16[192,1024]{1,0:T(8,128)(2,1)} %param.13), channel_id=1, source_target_pairs={{0,4},{1,5},{2,6},{3,7},{4,0},{5,1},{6,2},{7,3},{8,12},{9,13},{10,... | collective-permute-start | bytes 1179656 | tf_op jit(solution)/shard_map/ppermute | solution.py:37
  3.7 11.1 %collective-permute-start = (bf16[192,1024]{1,0:T(8,128)(2,1)}, bf16[192,1024]{1,0:T(8,128)(2,1)S(1)}, u32[]{:S(2)}, u32[]{:S(2)}) collective-permute-start(bf16[192,1024]{1,0:T(8,128)(2,1)} %param.13), channel_id=1, source_target_pairs={{0,2},{1,3},{2,0},{3,1},{4,6},{5,7},{6,4},{7,5},{8,10},{9,11},{10,... | collective-permute-start | bytes 1179656 | tf_op jit(solution)/shard_map/ppermute | solution.py:37
  13.0 6.2 %collective-permute-start.2 = (bf16[96,1024]{1,0:T(8,128)(2,1)S(1)}, bf16[96,1024]{1,0:T(8,128)(2,1)S(1)}, u32[]{:S(2)}, u32[]{:S(2)}) collective-permute-start(bf16[96,1024]{1,0:T(8,128)(2,1)S(1)} %slice.42), channel_id=1, source_target_pairs={{0,2},{1,3},{2,0},{3,1},{4,6},{5,7},{6,4},{7,5},{8,10},{9,11},{10,... | collective-permute-start | bytes 589832 | tf_op jit(solution)/shard_map/ppermute | solution.py:37
  14.8 5.7 %collective-permute-start.3 = (bf16[96,1024]{1,0:T(8,128)(2,1)S(1)}, bf16[96,1024]{1,0:T(8,128)(2,1)S(1)}, u32[]{:S(2)}, u32[]{:S(2)}) collective-permute-start(bf16[96,1024]{1,0:T(8,128)(2,1)S(1)} %slice.43), channel_id=1, source_target_pairs={{0,4},{1,5},{2,6},{3,7},{4,0},{5,1},{6,2},{7,3},{8,12},{9,13},{10,... | collective-permute-start | bytes 589832 | tf_op jit(solution)/shard_map/ppermute | solution.py:37
  21.9 3.8 %collective-permute-start.4 = (bf16[4,192,1024]{2,1,0:T(8,128)(2,1)}, bf16[4,192,1024]{2,1,0:T(8,128)(2,1)}, u32[]{:S(2)}, u32[]{:S(2)}) collective-permute-start(bf16[4,192,1024]{2,1,0:T(8,128)(2,1)} %pad_maximum_fusion), channel_id=1, source_target_pairs={{0,1},{1,0},{2,3},{3,2},{4,5},{5,4},{6,7},{7,6},{8,9},{9,8},{10,11... | collective-permute-start | bytes 4718600 | tf_op jit(solution)/shard_map/ppermute | solution.py:37
  22.5 7.3 %copy-start.10 = (bf16[1,1024,384]{2,1,0:T(8,128)(2,1)S(1)}, bf16[1,1024,384]{2,1,0:T(8,128)(2,1)}, u32[]{:S(2)}) copy-start(bf16[1,1024,384]{2,1,0:T(8,128)(2,1)} %param.15) | copy-start | bytes 2359300
  29.8 1.9 %copy-start.6 = (f32[384,32]{0,1:T(8,128)S(1)}, f32[384,32]{0,1:T(8,128)}, u32[]{:S(2)}) copy-start(f32[384,32]{0,1:T(8,128)} %param.16) | copy-start | bytes 147460
  31.8 10.3 %copy-start.7 = (s32[1536]{0:T(1024)S(1)}, s32[1536]{0:T(1024)}, u32[]{:S(2)}) copy-start(s32[1536]{0:T(1024)} %param.20) | copy-start | bytes 18436
  31.8 10.3 %copy-start.1 = (s32[1600]{0:T(1024)S(1)}, s32[1600]{0:T(1024)}, u32[]{:S(2)}) copy-start(s32[1600]{0:T(1024)} %param.21) | copy-start | bytes 19204
  33.4 1.4 collective-permute-start.5
  34.8 5.6 %collective-permute-start.6 = (f32[1024,32]{0,1:T(8,128)S(1)}, f32[1024,32]{0,1:T(8,128)S(1)}, u32[]{:S(2)}, u32[]{:S(2)}) collective-permute-start(f32[1024,32]{0,1:T(8,128)S(1)} %add.155), channel_id=1, source_target_pairs={{0,2},{1,3},{2,0},{3,1},{4,6},{5,7},{6,4},{7,5},{8,10},{9,11},{10,... | collective-permute-start | bytes 393224 | tf_op jit(solution)/shard_map/ppermute | solution.py:25
  40.4 10.0 %collective-permute-start.7 = (f32[1024,32]{0,1:T(8,128)S(1)}, f32[1024,32]{0,1:T(8,128)S(1)}, u32[]{:S(2)}, u32[]{:S(2)}) collective-permute-start(f32[1024,32]{0,1:T(8,128)S(1)} %add.156), channel_id=1, source_target_pairs={{0,4},{1,5},{2,6},{3,7},{4,0},{5,1},{6,2},{7,3},{8,12},{9,13},{10,... | collective-permute-start | bytes 393224 | tf_op jit(solution)/shard_map/ppermute | solution.py:25
  50.5 5.0 %collective-permute-start.8 = (f32[1024,32]{0,1:T(8,128)S(1)}, f32[1024,32]{0,1:T(8,128)S(1)}, u32[]{:S(2)}, u32[]{:S(2)}) collective-permute-start(f32[1024,32]{0,1:T(8,128)S(1)} %add.157), channel_id=1, source_target_pairs={{0,8},{1,9},{2,10},{3,11},{4,12},{5,13},{6,14},{7,15},{8,0},{9,1},... | collective-permute-start | bytes 393224 | tf_op jit(solution)/shard_map/ppermute | solution.py:25
  55.5 7.3 %collective-permute-start.9 = (f32[1024,32]{0,1:T(8,128)S(1)}, f32[1024,32]{0,1:T(8,128)S(1)}, u32[]{:S(2)}, u32[]{:S(2)}) collective-permute-start(f32[1024,32]{0,1:T(8,128)S(1)} %add.158), channel_id=1, source_target_pairs={{0,16},{1,17},{2,18},{3,19},{4,20},{5,21},{6,22},{7,23},{8,24},{9,... | collective-permute-start | bytes 393224 | tf_op jit(solution)/shard_map/ppermute | solution.py:25
  71.2 4.4 %collective-permute-start.10 = (f32[384,32]{0,1:T(8,128)S(1)}, f32[384,32]{0,1:T(8,128)S(1)}, u32[]{:S(2)}, u32[]{:S(2)}) collective-permute-start(f32[384,32]{0,1:T(8,128)S(1)} %fusion.43), channel_id=1, source_target_pairs={{0,8},{8,0},{16,24},{24,16},{1,9},{9,1},{17,25},{25,17},{2,10},{10... | collective-permute-start | bytes 147464 | tf_op jit(solution)/shard_map/ppermute | solution.py:25
  75.6 5.1 %collective-permute-start.11 = (f32[384,32]{0,1:T(8,128)S(1)}, f32[384,32]{0,1:T(8,128)S(1)}, u32[]{:S(2)}, u32[]{:S(2)}) collective-permute-start(f32[384,32]{0,1:T(8,128)S(1)} %add.160), channel_id=1, source_target_pairs={{0,16},{8,24},{16,0},{24,8},{1,17},{9,25},{17,1},{25,9},{2,18},{10... | collective-permute-start | bytes 147464 | tf_op jit(solution)/shard_map/ppermute | solution.py:25
  77.9 17.9 %copy-start.9 = (s32[2]{0:T(128)S(1)}, s32[2]{0:T(128)}, u32[]{:S(2)}) copy-start(s32[2]{0:T(128)} %constant.112) | copy-start | bytes 28
  77.9 18.0 %copy-start.8 = (s32[2]{0:T(128)S(1)}, s32[2]{0:T(128)}, u32[]{:S(2)}) copy-start(s32[2]{0:T(128)} %constant.115) | copy-start | bytes 28
  82.3 1.4 collective-permute-start.12
  83.7 5.6 %collective-permute-start.13 = (f32[1024,32]{0,1:T(8,128)S(1)}, f32[1024,32]{0,1:T(8,128)S(1)}, u32[]{:S(2)}, u32[]{:S(2)}) collective-permute-start(f32[1024,32]{0,1:T(8,128)S(1)} %add.162), channel_id=1, source_target_pairs={{0,2},{1,3},{2,0},{3,1},{4,6},{5,7},{6,4},{7,5},{8,10},{9,11},{10,... | collective-permute-start | bytes 393224 | tf_op jit(solution)/shard_map/ppermute | solution.py:25
  89.3 5.0 %collective-permute-start.14 = (f32[1024,32]{0,1:T(8,128)S(1)}, f32[1024,32]{0,1:T(8,128)S(1)}, u32[]{:S(2)}, u32[]{:S(2)}) collective-permute-start(f32[1024,32]{0,1:T(8,128)S(1)} %add.163), channel_id=1, source_target_pairs={{0,4},{1,5},{2,6},{3,7},{4,0},{5,1},{6,2},{7,3},{8,12},{9,13},{10,... | collective-permute-start | bytes 393224 | tf_op jit(solution)/shard_map/ppermute | solution.py:25
  94.4 5.0 %collective-permute-start.15 = (f32[1024,32]{0,1:T(8,128)S(1)}, f32[1024,32]{0,1:T(8,128)S(1)}, u32[]{:S(2)}, u32[]{:S(2)}) collective-permute-start(f32[1024,32]{0,1:T(8,128)S(1)} %add.164), channel_id=1, source_target_pairs={{0,8},{1,9},{2,10},{3,11},{4,12},{5,13},{6,14},{7,15},{8,0},{9,1},... | collective-permute-start | bytes 393224 | tf_op jit(solution)/shard_map/ppermute | solution.py:25
  99.4 18.3 %collective-permute-start.16 = (f32[1024,32]{0,1:T(8,128)S(1)}, f32[1024,32]{0,1:T(8,128)S(1)}, u32[]{:S(2)}, u32[]{:S(2)}) collective-permute-start(f32[1024,32]{0,1:T(8,128)S(1)} %add.165), channel_id=1, source_target_pairs={{0,16},{1,17},{2,18},{3,19},{4,20},{5,21},{6,22},{7,23},{8,24},{9,... | collective-permute-start | bytes 393224 | tf_op jit(solution)/shard_map/ppermute | solution.py:25
  108.6 9.5 %all-to-all-start = ((s32[4,1,768]{2,1,0:T(1,128)}), s32[4,1,768]{2,1,0:T(1,128)S(1)}, u32[]{:S(2)}, u32[]{:S(2)}) async-start(s32[4,1,768]{2,1,0:T(1,128)} %bitcast.21), calls=%async_computation | async-start | bytes 24576 | tf_op jit(solution)/shard_map/all_to_all | solution.py:78
  118.1 23.1 %all-to-all-start.1 = ((bf16[4,768,128]{2,1,0:T(8,128)(2,1)}), bf16[4,768,128]{2,1,0:T(8,128)(2,1)}, u32[]{:S(2)}, u32[]{:S(2)}) async-start(bf16[4,768,128]{2,1,0:T(8,128)(2,1)} %bitcast.23), calls=%async_computation.1 | async-start | bytes 1572864 | tf_op jit(solution)/shard_map/all_to_all | solution.py:77
  123.0 18.1 %copy-start.11 = (f32[400,128]{1,0:T(8,128)S(1)}, f32[400,128]{1,0:T(8,128)}, u32[]{:S(2)}) copy-start(f32[400,128]{1,0:T(8,128)} %param.22) | copy-start | bytes 614404
  131.1 4.5 %collective-permute-start.17 = (f32[384,32]{0,1:T(8,128)S(1)}, f32[384,32]{0,1:T(8,128)S(1)}, u32[]{:S(2)}, u32[]{:S(2)}) collective-permute-start(f32[384,32]{0,1:T(8,128)S(1)} %fusion.44), channel_id=1, source_target_pairs={{0,8},{8,0},{16,24},{24,16},{1,9},{9,1},{17,25},{25,17},{2,10},{10... | collective-permute-start | bytes 147464 | tf_op jit(solution)/shard_map/ppermute | solution.py:25
  135.5 8.3 %collective-permute-start.18 = (f32[384,32]{0,1:T(8,128)S(1)}, f32[384,32]{0,1:T(8,128)S(1)}, u32[]{:S(2)}, u32[]{:S(2)}) collective-permute-start(f32[384,32]{0,1:T(8,128)S(1)} %add.167), channel_id=1, source_target_pairs={{0,16},{8,24},{16,0},{24,8},{1,17},{9,25},{17,1},{25,9},{2,18},{10... | collective-permute-start | bytes 147464 | tf_op jit(solution)/shard_map/ppermute | solution.py:25
  143.8 2.6 %copy-start.5 = (f32[384,32]{0,1:T(8,128)}, f32[384,32]{0,1:T(8,128)S(1)}, u32[]{:S(2)}) copy-start(f32[384,32]{0,1:T(8,128)S(1)} %add_multiply_fusion.6) | copy-start | bytes 147460
  145.3 1.2 copy-start.3
  145.3 1.2 copy-start.4

commit v3 on v2

--- a/solution.py
+++ b/solution.py
@@ -58,8 +58,33 @@
     return jax.scipy.linalg.solve_triangular(factor_low, left_basis.T, lower=True).T
 
 
+def word_update_dense(word_grads, token_ids, owner_map, word_master):
+    replicas = lax.axis_size("rep")
+    per_owner = word_master.shape[0]
+    vocab = owner_map.shape[0]
+    hits = token_ids[:, None] == jnp.arange(vocab, dtype=jnp.int32)[None, :]
+    targets = jnp.sum(jnp.where(hits, owner_map[None, :], 0), axis=1)
+    selector = (
+        targets[:, None] == jnp.arange(replicas * per_owner, dtype=jnp.int32)[None, :]
+    ).astype(jnp.bfloat16)
+    partial = lax.dot_general(
+        selector, word_grads, (((0,), (0,)), ((), ())), preferred_element_type=jnp.float32
+    )
+    me = lax.axis_index("rep")
+    row_grad = lax.dynamic_slice_in_dim(partial, me * per_owner, per_owner, 0)
+    for shift in range(1, replicas):
+        block = lax.dynamic_slice_in_dim(
+            partial, ((me + shift) % replicas) * per_owner, per_owner, 0
+        )
+        pairs = [(i, (i + shift) % replicas) for i in range(replicas)]
+        row_grad = row_grad + lax.ppermute(block, "rep", pairs)
+    return word_master - EMBED_RATE * row_grad
+
+
 def word_update(word_grads, token_ids, owner_map, word_master):
     replicas = lax.axis_size("rep")
+    if owner_map.shape[0] <= 4096 and replicas <= 8:
+        return word_update_dense(word_grads, token_ids, owner_map, word_master)
     per_owner = word_master.shape[0]
     capacity = 2 * token_ids.shape[0] // replicas
     targets = owner_map[token_ids]

time: 166 us -> 148 us (0.89)
  local copies, waits for them, and re-layouts: 26.9 us -> 7.7 us
  starting transfers between devices: 36.9 us -> 30.7 us
  waiting for transfers between devices: 52.5 us -> 55.8 us
  matrix products: 12.3 us -> 14.5 us
  other arithmetic: 18.7 us -> 20.7 us
    unnamed x28 -> x24, local copies, waits for them, and re-layouts: 13.5 us -> 0.96 us
    gather x1 -> x0, local copies, waits for them, and re-layouts: 8.39 us -> none  [word_update(): targets = owner_map[token_ids]]
    all_to_all x2 -> x0, starting transfers between devices: 8.37 us -> none  [the longest x1 4.94 us: word_update(): lax.all_to_all(outgoing, 'rep', split_axis=0, concat_axis=0, tiled=True)]
    ppermute x14, waiting for transfers between devices: 35.3 us -> 40.6 us  [tree_sum(): value = value + lax.ppermute(value, axes, pairs)]
    ppermute x0 -> x3, starting transfers between devices: none -> 4.41 us  [word_update_dense(): row_grad = row_grad + lax.ppermute(block, 'rep', pairs)]
    ppermute x14, starting transfers between devices: 20.7 us -> 18.4 us  [tree_sum(): value = value + lax.ppermute(value, axes, pairs)]
    all_to_all x2 -> x0, waiting for transfers between devices: 2.12 us -> none  [the longest x1 2.12 us: word_update(): lax.all_to_all(outgoing, 'rep', split_axis=0, concat_axis=0, tiled=True)]
    sub x1, other arithmetic: 0.01 us -> 1.97 us  [word_update_dense(): return word_master - EMBED_RATE * row_grad]
  transfers between devices with their start and end apart: 21 -> 22, of which waited for: 16 -> 17; matrix products, arithmetic and copies ran while one was open for 21% -> 13% of each run, Pallas kernels for 0% -> 0%
where the time goes in v3:
time: 148 us
  waiting for transfers between devices  55.8 us (38%)
  starting transfers between devices  30.7 us (21%)
  other arithmetic  20.7 us (14%)
  blocking collectives  17.4 us (12%)
  matrix products  14.5 us (10%)
  local copies, waits for them, and re-layouts  7.7 us (5%)
    ppermute x14, waiting for transfers between devices, tree_sum(): value = value + lax.ppermute(value, axes, pairs)  40.6 us
    ppermute x14, starting transfers between devices, tree_sum(): value = value + lax.ppermute(value, axes, pairs)  18.4 us
    all_gather x1, blocking collectives, shards(): lax.all_gather(master_new.astype(jnp.bfloat16), 'rep', axis=0, tiled=True)  17.4 us
    ppermute x5, waiting for transfers between devices, exchange(): return lax.ppermute(value, axis, [(i, i ^ stride) for i in range(count)])  15.1 us
    ppermute x5, starting transfers between devices, exchange(): return lax.ppermute(value, axis, [(i, i ^ stride) for i in range(count)])  7.89 us
    another operation x6, other arithmetic, orthonormal(): factor_low = jnp.linalg.cholesky(gram_matrix)  7.19 us
    another operation x4, other arithmetic, orthonormal(): jax.scipy.linalg.solve_triangular(factor_low, left_basis.T, lower=True)  6.8 us
    ppermute x3, starting transfers between devices, word_update_dense(): row_grad = row_grad + lax.ppermute(block, 'rep', pairs)  4.41 us
  transfers between devices with their start and end apart: 22, of which 17 were waited for; matrix products, arithmetic and copies ran while one was open for 13% of the time, Pallas kernels for 0%

profile of v3, /device:TPU:0, one launch (start us, length us, event | category | flops | bytes accessed | tf_op | source)
XLA Modules:
  0.0 147.7 jit_solution(15255434756550470362)
XLA Ops:
  0.7 3.0 %collective-permute-start.1 = (bf16[192,1024]{1,0:T(8,128)(2,1)}, bf16[192,1024]{1,0:T(8,128)(2,1)S(1)}, u32[]{:S(2)}, u32[]{:S(2)}) collective-permute-start(bf16[192,1024]{1,0:T(8,128)(2,1)} %param.13), channel_id=1, source_target_pairs={{0,4},{1,5},{2,6},{3,7},{4,0},{5,1},{6,2},{7,3},{8,12},{9,13},{10,... | collective-permute-start | bytes 1179656 | tf_op jit(solution)/shard_map/ppermute | solution.py:37
  3.7 1.5 %collective-permute-start = (bf16[192,1024]{1,0:T(8,128)(2,1)}, bf16[192,1024]{1,0:T(8,128)(2,1)S(1)}, u32[]{:S(2)}, u32[]{:S(2)}) collective-permute-start(bf16[192,1024]{1,0:T(8,128)(2,1)} %param.13), channel_id=1, source_target_pairs={{0,2},{1,3},{2,0},{3,1},{4,6},{5,7},{6,4},{7,5},{8,10},{9,11},{10,... | collective-permute-start | bytes 1179656 | tf_op jit(solution)/shard_map/ppermute | solution.py:37
  5.2 7.8 %collective-permute-done.1 = bf16[192,1024]{1,0:T(8,128)(2,1)S(1)} collective-permute-done((bf16[192,1024]{1,0:T(8,128)(2,1)}, bf16[192,1024]{1,0:T(8,128)(2,1)S(1)}, u32[]{:S(2)}, u32[]{:S(2)}) %collective-permute-start.1) | collective-permute-done | bytes 393248 | tf_op jit(solution)/shard_map/ppermute | solution.py:37
  13.0 1.8 %collective-permute-start.2 = (bf16[96,1024]{1,0:T(8,128)(2,1)S(1)}, bf16[96,1024]{1,0:T(8,128)(2,1)S(1)}, u32[]{:S(2)}, u32[]{:S(2)}) collective-permute-start(bf16[96,1024]{1,0:T(8,128)(2,1)S(1)} %slice.32), channel_id=1, source_target_pairs={{0,2},{1,3},{2,0},{3,1},{4,6},{5,7},{6,4},{7,5},{8,10},{9,11},{10,... | collective-permute-start | bytes 589832 | tf_op jit(solution)/shard_map/ppermute | solution.py:37
  14.8 1.6 %collective-permute-start.3 = (bf16[96,1024]{1,0:T(8,128)(2,1)S(1)}, bf16[96,1024]{1,0:T(8,128)(2,1)S(1)}, u32[]{:S(2)}, u32[]{:S(2)}) collective-permute-start(bf16[96,1024]{1,0:T(8,128)(2,1)S(1)} %slice.33), channel_id=1, source_target_pairs={{0,4},{1,5},{2,6},{3,7},{4,0},{5,1},{6,2},{7,3},{8,12},{9,13},{10,... | collective-permute-start | bytes 589832 | tf_op jit(solution)/shard_map/ppermute | solution.py:37
  16.4 2.8 %collective-permute-done.2 = bf16[96,1024]{1,0:T(8,128)(2,1)S(1)} collective-permute-done((bf16[96,1024]{1,0:T(8,128)(2,1)S(1)}, bf16[96,1024]{1,0:T(8,128)(2,1)S(1)}, u32[]{:S(2)}, u32[]{:S(2)}) %collective-permute-start.2) | collective-permute-done | bytes 196640 | tf_op jit(solution)/shard_map/ppermute | solution.py:37
  19.2 1.4 collective-permute-done.3
  20.6 1.4 pad_maximum_fusion
  22.6 3.2 %collective-permute-done.4 = bf16[4,192,1024]{2,1,0:T(8,128)(2,1)} collective-permute-done((bf16[4,192,1024]{2,1,0:T(8,128)(2,1)}, bf16[4,192,1024]{2,1,0:T(8,128)(2,1)}, u32[]{:S(2)}, u32[]{:S(2)}) %collective-permute-start.4) | collective-permute-done | bytes 1572896 | tf_op jit(solution)/shard_map/ppermute | solution.py:37
  29.9 1.9 %convert_add_fusion = f32[1024,384]{1,0:T(8,128)S(1)} fusion(bf16[1536,1024]{1,0:T(8,128)(2,1)S(1)} %fusion.3, bf16[1536,384]{1,0:T(8,128)(2,1)S(1)} %copy-done, bf16[1,1024,384]{2,1,0:T(8,128)(2,1)S(1)} %copy-done.7), kind=kOutput, calls=%fused_computation.6 | convolution fusion | flops 1208745984 | bytes 6684672 | tf_op jit(solution)/shard_map/dot_general | solution.py:130
  31.8 1.6 %fusion.31 = f32[1024,32]{0,1:T(8,128)S(1)} fusion(f32[1024,384]{1,0:T(8,128)S(1)} %convert_add_fusion, f32[384,32]{0,1:T(8,128)S(1)} %copy-done.6), kind=kOutput, calls=%fused_computation.65 | convolution fusion | flops 150994944 | bytes 1753088 | tf_op jit(solution)/shard_map/dot_general | solution.py:140
  33.6 1.2 collective-permute-done.5
  34.8 1.2 collective-permute-start.6
  36.0 4.4 %collective-permute-done.6 = f32[1024,32]{0,1:T(8,128)S(1)} collective-permute-done((f32[1024,32]{0,1:T(8,128)S(1)}, f32[1024,32]{0,1:T(8,128)S(1)}, u32[]{:S(2)}, u32[]{:S(2)}) %collective-permute-start.6) | collective-permute-done | bytes 131104 | tf_op jit(solution)/shard_map/ppermute | solution.py:25
  40.4 1.6 %collective-permute-start.7 = (f32[1024,32]{0,1:T(8,128)S(1)}, f32[1024,32]{0,1:T(8,128)S(1)}, u32[]{:S(2)}, u32[]{:S(2)}) collective-permute-start(f32[1024,32]{0,1:T(8,128)S(1)} %add.134), channel_id=1, source_target_pairs={{0,4},{1,5},{2,6},{3,7},{4,0},{5,1},{6,2},{7,3},{8,12},{9,13},{10,... | collective-permute-start | bytes 393224 | tf_op jit(solution)/shard_map/ppermute | solution.py:25
  42.0 3.4 %collective-permute-done.7 = f32[1024,32]{0,1:T(8,128)S(1)} collective-permute-done((f32[1024,32]{0,1:T(8,128)S(1)}, f32[1024,32]{0,1:T(8,128)S(1)}, u32[]{:S(2)}, u32[]{:S(2)}) %collective-permute-start.7) | collective-permute-done | bytes 131104 | tf_op jit(solution)/shard_map/ppermute | solution.py:25
  45.5 1.6 %collective-permute-start.8 = (f32[1024,32]{0,1:T(8,128)S(1)}, f32[1024,32]{0,1:T(8,128)S(1)}, u32[]{:S(2)}, u32[]{:S(2)}) collective-permute-start(f32[1024,32]{0,1:T(8,128)S(1)} %add.135), channel_id=1, source_target_pairs={{0,8},{1,9},{2,10},{3,11},{4,12},{5,13},{6,14},{7,15},{8,0},{9,1},... | collective-permute-start | bytes 393224 | tf_op jit(solution)/shard_map/ppermute | solution.py:25
  47.1 3.4 %collective-permute-done.8 = f32[1024,32]{0,1:T(8,128)S(1)} collective-permute-done((f32[1024,32]{0,1:T(8,128)S(1)}, f32[1024,32]{0,1:T(8,128)S(1)}, u32[]{:S(2)}, u32[]{:S(2)}) %collective-permute-start.8) | collective-permute-done | bytes 131104 | tf_op jit(solution)/shard_map/ppermute | solution.py:25
  50.5 3.1 %collective-permute-start.9 = (f32[1024,32]{0,1:T(8,128)S(1)}, f32[1024,32]{0,1:T(8,128)S(1)}, u32[]{:S(2)}, u32[]{:S(2)}) collective-permute-start(f32[1024,32]{0,1:T(8,128)S(1)} %add.136), channel_id=1, source_target_pairs={{0,16},{1,17},{2,18},{3,19},{4,20},{5,21},{6,22},{7,23},{8,24},{9,... | collective-permute-start | bytes 393224 | tf_op jit(solution)/shard_map/ppermute | solution.py:25
  53.6 4.4 %collective-permute-done.9 = f32[1024,32]{0,1:T(8,128)S(1)} collective-permute-done((f32[1024,32]{0,1:T(8,128)S(1)}, f32[1024,32]{0,1:T(8,128)S(1)}, u32[]{:S(2)}, u32[]{:S(2)}) %collective-permute-start.9) | collective-permute-done | bytes 131104 | tf_op jit(solution)/shard_map/ppermute | solution.py:25
  58.3 2.9 %cholesky.44 = f32[32,32]{1,0:T(8,128)S(1)} custom-call(f32[32,32]{1,0:T(8,128)S(1)} %fusion.22), custom_call_target="Cholesky" | custom-call | tf_op jit(solution)/shard_map/jit(cholesky)/cholesky | solution.py:57
  62.6 2.4 %custom-call.6 = f32[1,32,32]{1,2,0:T(8,128)S(1)} custom-call(f32[1,32,32]{2,1,0:T(8,128)S(1)} %fusion.17), custom_call_target="InvertDiagBlocksLowerTriangular" | custom-call | tf_op jit(solution)/shard_map/jit(_solve_triangular)/triangular_solve | solution.py:58
  67.1 3.4 %collective-permute-done.10 = f32[384,32]{0,1:T(8,128)S(1)} collective-permute-done((f32[384,32]{0,1:T(8,128)S(1)}, f32[384,32]{0,1:T(8,128)S(1)}, u32[]{:S(2)}, u32[]{:S(2)}) %collective-permute-start.10) | collective-permute-done | bytes 49184 | tf_op jit(solution)/shard_map/ppermute | solution.py:25
  70.5 2.1 %collective-permute-start.11 = (f32[384,32]{0,1:T(8,128)S(1)}, f32[384,32]{0,1:T(8,128)S(1)}, u32[]{:S(2)}, u32[]{:S(2)}) collective-permute-start(f32[384,32]{0,1:T(8,128)S(1)} %add.138), channel_id=1, source_target_pairs={{0,16},{8,24},{16,0},{24,8},{1,17},{9,25},{17,1},{25,9},{2,18},{10... | collective-permute-start | bytes 147464 | tf_op jit(solution)/shard_map/ppermute | solution.py:25
  72.6 2.9 %collective-permute-done.11 = f32[384,32]{0,1:T(8,128)S(1)} collective-permute-done((f32[384,32]{0,1:T(8,128)S(1)}, f32[384,32]{0,1:T(8,128)S(1)}, u32[]{:S(2)}, u32[]{:S(2)}) %collective-permute-start.11) | collective-permute-done | bytes 49184 | tf_op jit(solution)/shard_map/ppermute | solution.py:25
  75.6 1.6 %fusion.13 = f32[1024,32]{0,1:T(8,128)S(1)} fusion(f32[1024,384]{1,0:T(8,128)S(1)} %convert_add_fusion, f32[384,32]{0,1:T(8,128)S(1)} %add.138, f32[384,32]{0,1:T(8,128)S(1)} %collective-permute-done.11), kind=kOutput, calls=%fused_computation.29 | convolution fusion | flops 151019520 | bytes 1802240 | tf_op jit(solution)/shard_map/dot_general | solution.py:140
  77.3 1.3 collective-permute-done.12
  78.6 1.2 collective-permute-start.13
  79.8 4.4 %collective-permute-done.13 = f32[1024,32]{0,1:T(8,128)S(1)} collective-permute-done((f32[1024,32]{0,1:T(8,128)S(1)}, f32[1024,32]{0,1:T(8,128)S(1)}, u32[]{:S(2)}, u32[]{:S(2)}) %collective-permute-start.13) | collective-permute-done | bytes 131104 | tf_op jit(solution)/shard_map/ppermute | solution.py:25
  84.2 1.6 %collective-permute-start.14 = (f32[1024,32]{0,1:T(8,128)S(1)}, f32[1024,32]{0,1:T(8,128)S(1)}, u32[]{:S(2)}, u32[]{:S(2)}) collective-permute-start(f32[1024,32]{0,1:T(8,128)S(1)} %add.141), channel_id=1, source_target_pairs={{0,4},{1,5},{2,6},{3,7},{4,0},{5,1},{6,2},{7,3},{8,12},{9,13},{10,... | collective-permute-start | bytes 393224 | tf_op jit(solution)/shard_map/ppermute | solution.py:25
  85.8 3.4 %collective-permute-done.14 = f32[1024,32]{0,1:T(8,128)S(1)} collective-permute-done((f32[1024,32]{0,1:T(8,128)S(1)}, f32[1024,32]{0,1:T(8,128)S(1)}, u32[]{:S(2)}, u32[]{:S(2)}) %collective-permute-start.14) | collective-permute-done | bytes 131104 | tf_op jit(solution)/shard_map/ppermute | solution.py:25
  89.3 1.2 collective-permute-start.15
  90.5 1.1 select_reduce_fusion
  91.6 2.7 %collective-permute-done.15 = f32[1024,32]{0,1:T(8,128)S(1)} collective-permute-done((f32[1024,32]{0,1:T(8,128)S(1)}, f32[1024,32]{0,1:T(8,128)S(1)}, u32[]{:S(2)}, u32[]{:S(2)}) %collective-permute-start.15) | collective-permute-done | bytes 131104 | tf_op jit(solution)/shard_map/ppermute | solution.py:25
  94.4 2.1 %collective-permute-start.16 = (f32[1024,32]{0,1:T(8,128)S(1)}, f32[1024,32]{0,1:T(8,128)S(1)}, u32[]{:S(2)}, u32[]{:S(2)}) collective-permute-start(f32[1024,32]{0,1:T(8,128)S(1)} %add.143), channel_id=1, source_target_pairs={{0,16},{1,17},{2,18},{3,19},{4,20},{5,21},{6,22},{7,23},{8,24},{9,... | collective-permute-start | bytes 393224 | tf_op jit(solution)/shard_map/ppermute | solution.py:25
  96.5 4.2 %fusion = f32[1600,128]{1,0:T(8,128)} fusion(bf16[1536,128]{1,0:T(8,128)(2,1)S(1)} %copy-done.8, s32[1536]{0:T(1024)S(1)} %select_reduce_fusion), kind=kOutput, calls=%fused_computation.1 | convolution fusion | flops 631603200 | bytes 1218560 | tf_op jit(solution)/shard_map/dot_general | solution.py:70
  100.6 1.9 %constant_dynamic-slice_fusion.1 = (f32[400,128]{1,0:T(8,128)}, f32[400,128]{1,0:T(8,128)S(1)}, f32[400,128]{1,0:T(8,128)}) fusion(f32[1600,128]{1,0:T(8,128)} %fusion, s32[]{:T(128)S(6)} %select_n.73, s32[]{:T(128)S(6)} %select_n.77, s32[]{:T(128)S(6)} %select_n.75), kind=kLoop, calls=%fused_computation.51 | loop fusion | bytes 1228812 | tf_op jit(solution)/shard_map/dynamic_slice | solution.py:76
  102.6 2.0 %collective-permute-start.19 = (f32[400,128]{1,0:T(8,128)}, f32[400,128]{1,0:T(8,128)}, u32[]{:S(2)}, u32[]{:S(2)}) collective-permute-start(f32[400,128]{1,0:T(8,128)} %get-tuple-element.11), channel_id=1, source_target_pairs={{0,8},{8,16},{16,24},{24,0},{1,9},{9,17},{17,25},{25,1},{2,10},{10... | collective-permute-start | bytes 614408 | tf_op jit(solution)/shard_map/ppermute | solution.py:80
  104.6 2.4 %collective-permute-start.21 = (f32[400,128]{1,0:T(8,128)S(1)}, f32[400,128]{1,0:T(8,128)}, u32[]{:S(2)}, u32[]{:S(2)}) collective-permute-start(f32[400,128]{1,0:T(8,128)S(1)} %get-tuple-element.12), channel_id=1, source_target_pairs={{0,24},{8,0},{16,8},{24,16},{1,25},{9,1},{17,9},{25,17},{2,26},{10... | collective-permute-start | bytes 614408 | tf_op jit(solution)/shard_map/ppermute | solution.py:80
  107.3 2.9 %cholesky.55 = f32[32,32]{1,0:T(8,128)S(1)} custom-call(f32[32,32]{1,0:T(8,128)S(1)} %fusion.20), custom_call_target="Cholesky" | custom-call | tf_op jit(solution)/shard_map/jit(cholesky)/cholesky | solution.py:57
  111.6 3.1 %custom-call.7 = f32[1,32,32]{1,2,0:T(8,128)} custom-call(f32[1,32,32]{2,1,0:T(8,128)S(1)} %fusion.18), custom_call_target="InvertDiagBlocksLowerTriangular" | custom-call | tf_op jit(solution)/shard_map/jit(_solve_triangular)/triangular_solve | solution.py:58
  116.7 4.1 %collective-permute-done.17 = f32[384,32]{0,1:T(8,128)S(1)} collective-permute-done((f32[384,32]{0,1:T(8,128)S(1)}, f32[384,32]{0,1:T(8,128)S(1)}, u32[]{:S(2)}, u32[]{:S(2)}) %collective-permute-start.17) | collective-permute-done | bytes 49184 | tf_op jit(solution)/shard_map/ppermute | solution.py:25
  120.8 1.5 %collective-permute-start.18 = (f32[384,32]{0,1:T(8,128)S(1)}, f32[384,32]{0,1:T(8,128)S(1)}, u32[]{:S(2)}, u32[]{:S(2)}) collective-permute-start(f32[384,32]{0,1:T(8,128)S(1)} %add.145), channel_id=1, source_target_pairs={{0,16},{8,24},{16,0},{24,8},{1,17},{9,25},{17,1},{25,9},{2,18},{10... | collective-permute-start | bytes 147464 | tf_op jit(solution)/shard_map/ppermute | solution.py:25
  122.3 2.0 %multiply_subtract_fusion.1 = f32[400,128]{1,0:T(8,128)} fusion(f32[400,128]{1,0:T(8,128)S(1)} %copy-done.4, f32[400,128]{1,0:T(8,128)} %collective-permute-done.21, f32[400,128]{1,0:T(8,128)} %collective-permute-done.20, f32[400,128]{1,0:T(8,128)} %collective-permute-done.19, f32[1600,128]{1,0:T(8,128)} %fusion, s32[]{:T(128)S(6)} %select_n.71), kind=kLoop, calls=%fused_computation.19 | loop fusion | flops 256000 | bytes 1228804 | tf_op jit(solution)/shard_map/sub | solution.py:81
  124.3 1.6 %collective-permute-done.18 = f32[384,32]{0,1:T(8,128)S(1)} collective-permute-done((f32[384,32]{0,1:T(8,128)S(1)}, f32[384,32]{0,1:T(8,128)S(1)}, u32[]{:S(2)}, u32[]{:S(2)}) %collective-permute-start.18) | collective-permute-done | bytes 49184 | tf_op jit(solution)/shard_map/ppermute | solution.py:25
  125.9 1.5 fusion.34
  127.4 1.1 fusion.2
  129.5 17.4 %all_gather.3 = bf16[1024,384]{1,0:T(8,128)(2,1)S(1)} all-gather(bf16[256,384]{1,0:T(8,128)(2,1)S(1)} %get-tuple-element.8), channel_id=1, replica_groups=mesh['rep'=4,'tp'=8] {'rep'}, dimensions={0}, use_global_device_ids=true | all-gather | bytes 983040 | tf_op jit(solution)/shard_map/all_gather | solution.py:156
  (75 shorter events, 14.5 us)
Async XLA Ops:
  0.6 29.2 %copy-start = (bf16[1536,384]{1,0:T(8,128)(2,1)S(1)}, bf16[1536,384]{1,0:T(8,128)(2,1)}, u32[]{:S(2)}) copy-start(bf16[1536,384]{1,0:T(8,128)(2,1)} %param.14) | copy-start | bytes 3538948
  0.6 19.9 %copy-start.1 = (bf16[192,1024]{1,0:T(8,128)(2,1)S(1)}, bf16[192,1024]{1,0:T(8,128)(2,1)}, u32[]{:S(2)}) copy-start(bf16[192,1024]{1,0:T(8,128)(2,1)} %param.13) | copy-start | bytes 1179652
  0.7 12.4 %collective-permute-start.1 = (bf16[192,1024]{1,0:T(8,128)(2,1)}, bf16[192,1024]{1,0:T(8,128)(2,1)S(1)}, u32[]{:S(2)}, u32[]{:S(2)}) collective-permute-start(bf16[192,1024]{1,0:T(8,128)(2,1)} %param.13), channel_id=1, source_target_pairs={{0,4},{1,5},{2,6},{3,7},{4,0},{5,1},{6,2},{7,3},{8,12},{9,13},{10,... | collective-permute-start | bytes 1179656 | tf_op jit(solution)/shard_map/ppermute | solution.py:37
  3.7 11.1 %collective-permute-start = (bf16[192,1024]{1,0:T(8,128)(2,1)}, bf16[192,1024]{1,0:T(8,128)(2,1)S(1)}, u32[]{:S(2)}, u32[]{:S(2)}) collective-permute-start(bf16[192,1024]{1,0:T(8,128)(2,1)} %param.13), channel_id=1, source_target_pairs={{0,2},{1,3},{2,0},{3,1},{4,6},{5,7},{6,4},{7,5},{8,10},{9,11},{10,... | collective-permute-start | bytes 1179656 | tf_op jit(solution)/shard_map/ppermute | solution.py:37
  13.0 6.2 %collective-permute-start.2 = (bf16[96,1024]{1,0:T(8,128)(2,1)S(1)}, bf16[96,1024]{1,0:T(8,128)(2,1)S(1)}, u32[]{:S(2)}, u32[]{:S(2)}) collective-permute-start(bf16[96,1024]{1,0:T(8,128)(2,1)S(1)} %slice.32), channel_id=1, source_target_pairs={{0,2},{1,3},{2,0},{3,1},{4,6},{5,7},{6,4},{7,5},{8,10},{9,11},{10,... | collective-permute-start | bytes 589832 | tf_op jit(solution)/shard_map/ppermute | solution.py:37
  14.8 5.7 %collective-permute-start.3 = (bf16[96,1024]{1,0:T(8,128)(2,1)S(1)}, bf16[96,1024]{1,0:T(8,128)(2,1)S(1)}, u32[]{:S(2)}, u32[]{:S(2)}) collective-permute-start(bf16[96,1024]{1,0:T(8,128)(2,1)S(1)} %slice.33), channel_id=1, source_target_pairs={{0,4},{1,5},{2,6},{3,7},{4,0},{5,1},{6,2},{7,3},{8,12},{9,13},{10,... | collective-permute-start | bytes 589832 | tf_op jit(solution)/shard_map/ppermute | solution.py:37
  22.0 3.8 %collective-permute-start.4 = (bf16[4,192,1024]{2,1,0:T(8,128)(2,1)}, bf16[4,192,1024]{2,1,0:T(8,128)(2,1)}, u32[]{:S(2)}, u32[]{:S(2)}) collective-permute-start(bf16[4,192,1024]{2,1,0:T(8,128)(2,1)} %pad_maximum_fusion), channel_id=1, source_target_pairs={{0,1},{1,0},{2,3},{3,2},{4,5},{5,4},{6,7},{7,6},{8,9},{9,8},{10,11... | collective-permute-start | bytes 4718600 | tf_op jit(solution)/shard_map/ppermute | solution.py:37
  22.5 7.3 %copy-start.7 = (bf16[1,1024,384]{2,1,0:T(8,128)(2,1)S(1)}, bf16[1,1024,384]{2,1,0:T(8,128)(2,1)}, u32[]{:S(2)}) copy-start(bf16[1,1024,384]{2,1,0:T(8,128)(2,1)} %param.15) | copy-start | bytes 2359300
  29.9 1.9 %copy-start.6 = (f32[384,32]{0,1:T(8,128)S(1)}, f32[384,32]{0,1:T(8,128)}, u32[]{:S(2)}) copy-start(f32[384,32]{0,1:T(8,128)} %param.16) | copy-start | bytes 147460
  33.4 1.4 collective-permute-start.5
  34.8 5.6 %collective-permute-start.6 = (f32[1024,32]{0,1:T(8,128)S(1)}, f32[1024,32]{0,1:T(8,128)S(1)}, u32[]{:S(2)}, u32[]{:S(2)}) collective-permute-start(f32[1024,32]{0,1:T(8,128)S(1)} %add.133), channel_id=1, source_target_pairs={{0,2},{1,3},{2,0},{3,1},{4,6},{5,7},{6,4},{7,5},{8,10},{9,11},{10,... | collective-permute-start | bytes 393224 | tf_op jit(solution)/shard_map/ppermute | solution.py:25
  40.4 5.0 %collective-permute-start.7 = (f32[1024,32]{0,1:T(8,128)S(1)}, f32[1024,32]{0,1:T(8,128)S(1)}, u32[]{:S(2)}, u32[]{:S(2)}) collective-permute-start(f32[1024,32]{0,1:T(8,128)S(1)} %add.134), channel_id=1, source_target_pairs={{0,4},{1,5},{2,6},{3,7},{4,0},{5,1},{6,2},{7,3},{8,12},{9,13},{10,... | collective-permute-start | bytes 393224 | tf_op jit(solution)/shard_map/ppermute | solution.py:25
  45.5 5.0 %collective-permute-start.8 = (f32[1024,32]{0,1:T(8,128)S(1)}, f32[1024,32]{0,1:T(8,128)S(1)}, u32[]{:S(2)}, u32[]{:S(2)}) collective-permute-start(f32[1024,32]{0,1:T(8,128)S(1)} %add.135), channel_id=1, source_target_pairs={{0,8},{1,9},{2,10},{3,11},{4,12},{5,13},{6,14},{7,15},{8,0},{9,1},... | collective-permute-start | bytes 393224 | tf_op jit(solution)/shard_map/ppermute | solution.py:25
  50.5 7.4 %collective-permute-start.9 = (f32[1024,32]{0,1:T(8,128)S(1)}, f32[1024,32]{0,1:T(8,128)S(1)}, u32[]{:S(2)}, u32[]{:S(2)}) collective-permute-start(f32[1024,32]{0,1:T(8,128)S(1)} %add.136), channel_id=1, source_target_pairs={{0,16},{1,17},{2,18},{3,19},{4,20},{5,21},{6,22},{7,23},{8,24},{9,... | collective-permute-start | bytes 393224 | tf_op jit(solution)/shard_map/ppermute | solution.py:25
  66.3 24.2 %copy-start.9 = (s32[1600]{0:T(1024)S(1)}, s32[1600]{0:T(1024)}, u32[]{:S(2)}) copy-start(s32[1600]{0:T(1024)} %param.21) | copy-start | bytes 19204
  66.3 24.2 %copy-start.10 = (s32[1536]{0:T(1024)S(1)}, s32[1536]{0:T(1024)}, u32[]{:S(2)}) copy-start(s32[1536]{0:T(1024)} %param.20) | copy-start | bytes 18436
  66.3 4.2 %collective-permute-start.10 = (f32[384,32]{0,1:T(8,128)S(1)}, f32[384,32]{0,1:T(8,128)S(1)}, u32[]{:S(2)}, u32[]{:S(2)}) collective-permute-start(f32[384,32]{0,1:T(8,128)S(1)} %fusion.32), channel_id=1, source_target_pairs={{0,8},{8,0},{16,24},{24,16},{1,9},{9,1},{17,25},{25,17},{2,10},{10... | collective-permute-start | bytes 147464 | tf_op jit(solution)/shard_map/ppermute | solution.py:25
  70.5 26.0 %copy-start.8 = (bf16[1536,128]{1,0:T(8,128)(2,1)S(1)}, bf16[1536,128]{1,0:T(8,128)(2,1)}, u32[]{:S(2)}) copy-start(bf16[1536,128]{1,0:T(8,128)(2,1)} %param.19) | copy-start | bytes 1179652
  70.5 5.1 %collective-permute-start.11 = (f32[384,32]{0,1:T(8,128)S(1)}, f32[384,32]{0,1:T(8,128)S(1)}, u32[]{:S(2)}, u32[]{:S(2)}) collective-permute-start(f32[384,32]{0,1:T(8,128)S(1)} %add.138), channel_id=1, source_target_pairs={{0,16},{8,24},{16,0},{24,8},{1,17},{9,25},{17,1},{25,9},{2,18},{10... | collective-permute-start | bytes 147464 | tf_op jit(solution)/shard_map/ppermute | solution.py:25
  77.2 1.4 collective-permute-start.12
  78.6 5.6 %collective-permute-start.13 = (f32[1024,32]{0,1:T(8,128)S(1)}, f32[1024,32]{0,1:T(8,128)S(1)}, u32[]{:S(2)}, u32[]{:S(2)}) collective-permute-start(f32[1024,32]{0,1:T(8,128)S(1)} %add.140), channel_id=1, source_target_pairs={{0,2},{1,3},{2,0},{3,1},{4,6},{5,7},{6,4},{7,5},{8,10},{9,11},{10,... | collective-permute-start | bytes 393224 | tf_op jit(solution)/shard_map/ppermute | solution.py:25
  84.2 5.0 %collective-permute-start.14 = (f32[1024,32]{0,1:T(8,128)S(1)}, f32[1024,32]{0,1:T(8,128)S(1)}, u32[]{:S(2)}, u32[]{:S(2)}) collective-permute-start(f32[1024,32]{0,1:T(8,128)S(1)} %add.141), channel_id=1, source_target_pairs={{0,4},{1,5},{2,6},{3,7},{4,0},{5,1},{6,2},{7,3},{8,12},{9,13},{10,... | collective-permute-start | bytes 393224 | tf_op jit(solution)/shard_map/ppermute | solution.py:25
  89.3 5.0 %collective-permute-start.15 = (f32[1024,32]{0,1:T(8,128)S(1)}, f32[1024,32]{0,1:T(8,128)S(1)}, u32[]{:S(2)}, u32[]{:S(2)}) collective-permute-start(f32[1024,32]{0,1:T(8,128)S(1)} %add.142), channel_id=1, source_target_pairs={{0,8},{1,9},{2,10},{3,11},{4,12},{5,13},{6,14},{7,15},{8,0},{9,1},... | collective-permute-start | bytes 393224 | tf_op jit(solution)/shard_map/ppermute | solution.py:25
  94.4 12.6 %collective-permute-start.16 = (f32[1024,32]{0,1:T(8,128)S(1)}, f32[1024,32]{0,1:T(8,128)S(1)}, u32[]{:S(2)}, u32[]{:S(2)}) collective-permute-start(f32[1024,32]{0,1:T(8,128)S(1)} %add.143), channel_id=1, source_target_pairs={{0,16},{1,17},{2,18},{3,19},{4,20},{5,21},{6,22},{7,23},{8,24},{9,... | collective-permute-start | bytes 393224 | tf_op jit(solution)/shard_map/ppermute | solution.py:25
  102.6 19.8 %copy-start.4 = (f32[400,128]{1,0:T(8,128)S(1)}, f32[400,128]{1,0:T(8,128)}, u32[]{:S(2)}) copy-start(f32[400,128]{1,0:T(8,128)} %param.22) | copy-start | bytes 614404
  102.6 19.8 %collective-permute-start.19 = (f32[400,128]{1,0:T(8,128)}, f32[400,128]{1,0:T(8,128)}, u32[]{:S(2)}, u32[]{:S(2)}) collective-permute-start(f32[400,128]{1,0:T(8,128)} %get-tuple-element.11), channel_id=1, source_target_pairs={{0,8},{8,16},{16,24},{24,0},{1,9},{9,17},{17,25},{25,1},{2,10},{10... | collective-permute-start | bytes 614408 | tf_op jit(solution)/shard_map/ppermute | solution.py:80
  104.6 17.7 %collective-permute-start.20 = (f32[400,128]{1,0:T(8,128)}, f32[400,128]{1,0:T(8,128)}, u32[]{:S(2)}, u32[]{:S(2)}) collective-permute-start(f32[400,128]{1,0:T(8,128)} %get-tuple-element.13), channel_id=1, source_target_pairs={{0,16},{8,24},{16,0},{24,8},{1,17},{9,25},{17,1},{25,9},{2,18},{10... | collective-permute-start | bytes 614408 | tf_op jit(solution)/shard_map/ppermute | solution.py:80
  104.6 17.7 %collective-permute-start.21 = (f32[400,128]{1,0:T(8,128)S(1)}, f32[400,128]{1,0:T(8,128)}, u32[]{:S(2)}, u32[]{:S(2)}) collective-permute-start(f32[400,128]{1,0:T(8,128)S(1)} %get-tuple-element.12), channel_id=1, source_target_pairs={{0,24},{8,0},{16,8},{24,16},{1,25},{9,1},{17,9},{25,17},{2,26},{10... | collective-permute-start | bytes 614408 | tf_op jit(solution)/shard_map/ppermute | solution.py:80
  116.6 4.2 %collective-permute-start.17 = (f32[384,32]{0,1:T(8,128)S(1)}, f32[384,32]{0,1:T(8,128)S(1)}, u32[]{:S(2)}, u32[]{:S(2)}) collective-permute-start(f32[384,32]{0,1:T(8,128)S(1)} %fusion.33), channel_id=1, source_target_pairs={{0,8},{8,0},{16,24},{24,16},{1,9},{9,1},{17,25},{25,17},{2,10},{10... | collective-permute-start | bytes 147464 | tf_op jit(solution)/shard_map/ppermute | solution.py:25
  120.8 5.1 %collective-permute-start.18 = (f32[384,32]{0,1:T(8,128)S(1)}, f32[384,32]{0,1:T(8,128)S(1)}, u32[]{:S(2)}, u32[]{:S(2)}) collective-permute-start(f32[384,32]{0,1:T(8,128)S(1)} %add.145), channel_id=1, source_target_pairs={{0,16},{8,24},{16,0},{24,8},{1,17},{9,25},{17,1},{25,9},{2,18},{10... | collective-permute-start | bytes 147464 | tf_op jit(solution)/shard_map/ppermute | solution.py:25
  125.9 2.6 %copy-start.5 = (f32[384,32]{0,1:T(8,128)}, f32[384,32]{0,1:T(8,128)S(1)}, u32[]{:S(2)}) copy-start(f32[384,32]{0,1:T(8,128)S(1)} %add_multiply_fusion.6) | copy-start | bytes 147460
  127.4 1.2 copy-start.2
  127.4 1.2 copy-start.3

commit v4 on v3

--- a/solution.py
+++ b/solution.py
@@ -134,18 +134,22 @@
         preferred_element_type=jnp.float32,
     )
     combined = product + error_state[0].astype(jnp.float32)
-    right_basis = q_start
-    left_basis = None
+    right_rows = q_start.T
+    left_rows = None
     for round_index in range(ROUNDS):
-        partial_left = jnp.dot(combined, right_basis, precision=highest)
-        left_basis = tree_sum(partial_left, ("rep", "tp")) / replicas
-        gram_matrix = jnp.dot(left_basis.T, left_basis, precision=highest)
-        left_basis = orthonormal(left_basis, gram_matrix)
-        partial_right = lax.dot_general(
-            combined, left_basis, (((0,), (0,)), ((), ())), precision=highest
+        partial_left = lax.dot_general(
+            right_rows, combined, (((1,), (1,)), ((), ())), precision=highest
         )
-        right_basis = tree_sum(partial_right, "rep") / replicas
-    approx = jnp.dot(left_basis, right_basis.T, precision=highest)
+        left_rows = tree_sum(partial_left, ("rep", "tp")) / replicas
+        gram_matrix = jnp.dot(left_rows, left_rows.T, precision=highest)
+        factor_low = jnp.linalg.cholesky(gram_matrix)
+        left_rows = jax.scipy.linalg.solve_triangular(factor_low, left_rows, lower=True)
+        partial_right = jnp.dot(left_rows, combined, precision=highest)
+        right_rows = tree_sum(partial_right, "rep") / replicas
+    right_basis = right_rows.T
+    approx = lax.dot_general(
+        left_rows, right_rows, (((0,), (0,)), ((), ())), precision=highest
+    )
     error_new = (combined - approx).astype(jnp.bfloat16)[None]
     owned_rows = qkv_master.shape[0]
     update_rows = lax.dynamic_slice_in_dim(

time: 148 us -> 149 us (level)
  no operation moved by 1% of the time
where the time goes in v4:
time: 149 us; the launch traced here: 148 us
  waiting for transfers between devices  55.7 us (37%)
  starting transfers between devices  30.7 us (21%)
  other arithmetic  21.3 us (14%)
  blocking collectives  17.4 us (12%)
  matrix products  14.4 us (10%)
  local copies, waits for them, and re-layouts  7.69 us (5%)
    ppermute x14, waiting for transfers between devices, tree_sum(): value = value + lax.ppermute(value, axes, pairs)  40.6 us
    ppermute x14, starting transfers between devices, tree_sum(): value = value + lax.ppermute(value, axes, pairs)  18.4 us
    all_gather x1, blocking collectives, shards(): lax.all_gather(master_new.astype(jnp.bfloat16), 'rep', axis=0, tiled=True)  17.4 us
    ppermute x5, waiting for transfers between devices, exchange(): return lax.ppermute(value, axis, [(i, i ^ stride) for i in range(count)])  15.1 us
    ppermute x5, starting transfers between devices, exchange(): return lax.ppermute(value, axis, [(i, i ^ stride) for i in range(count)])  7.89 us
    another operation x6, other arithmetic, shards(): factor_low = jnp.linalg.cholesky(gram_matrix)  7.19 us
    another operation x4, other arithmetic, shards(): jax.scipy.linalg.solve_triangular(factor_low, left_rows, lower=True)  6.8 us
    ppermute x3, starting transfers between devices, word_update_dense(): row_grad = row_grad + lax.ppermute(block, 'rep', pairs)  4.41 us
  transfers between devices with their start and end apart: 22, of which 17 were waited for; matrix products, arithmetic and copies ran while one was open for 13% of the time, Pallas kernels for 0%

profile of v4, /device:TPU:0, one launch (start us, length us, event | category | flops | bytes accessed | tf_op | source)
XLA Modules:
  0.0 148.3 jit_solution(4961360359542886529)
XLA Ops:
  0.7 3.0 %collective-permute-start.1 = (bf16[192,1024]{1,0:T(8,128)(2,1)}, bf16[192,1024]{1,0:T(8,128)(2,1)S(1)}, u32[]{:S(2)}, u32[]{:S(2)}) collective-permute-start(bf16[192,1024]{1,0:T(8,128)(2,1)} %param.13), channel_id=1, source_target_pairs={{0,4},{1,5},{2,6},{3,7},{4,0},{5,1},{6,2},{7,3},{8,12},{9,13},{10,... | collective-permute-start | bytes 1179656 | tf_op jit(solution)/shard_map/ppermute | solution.py:37
  3.7 1.5 %collective-permute-start = (bf16[192,1024]{1,0:T(8,128)(2,1)}, bf16[192,1024]{1,0:T(8,128)(2,1)S(1)}, u32[]{:S(2)}, u32[]{:S(2)}) collective-permute-start(bf16[192,1024]{1,0:T(8,128)(2,1)} %param.13), channel_id=1, source_target_pairs={{0,2},{1,3},{2,0},{3,1},{4,6},{5,7},{6,4},{7,5},{8,10},{9,11},{10,... | collective-permute-start | bytes 1179656 | tf_op jit(solution)/shard_map/ppermute | solution.py:37
  5.2 7.8 %collective-permute-done.1 = bf16[192,1024]{1,0:T(8,128)(2,1)S(1)} collective-permute-done((bf16[192,1024]{1,0:T(8,128)(2,1)}, bf16[192,1024]{1,0:T(8,128)(2,1)S(1)}, u32[]{:S(2)}, u32[]{:S(2)}) %collective-permute-start.1) | collective-permute-done | bytes 393248 | tf_op jit(solution)/shard_map/ppermute | solution.py:37
  13.0 1.8 %collective-permute-start.2 = (bf16[96,1024]{1,0:T(8,128)(2,1)S(1)}, bf16[96,1024]{1,0:T(8,128)(2,1)S(1)}, u32[]{:S(2)}, u32[]{:S(2)}) collective-permute-start(bf16[96,1024]{1,0:T(8,128)(2,1)S(1)} %slice.32), channel_id=1, source_target_pairs={{0,2},{1,3},{2,0},{3,1},{4,6},{5,7},{6,4},{7,5},{8,10},{9,11},{10,... | collective-permute-start | bytes 589832 | tf_op jit(solution)/shard_map/ppermute | solution.py:37
  14.8 1.6 %collective-permute-start.3 = (bf16[96,1024]{1,0:T(8,128)(2,1)S(1)}, bf16[96,1024]{1,0:T(8,128)(2,1)S(1)}, u32[]{:S(2)}, u32[]{:S(2)}) collective-permute-start(bf16[96,1024]{1,0:T(8,128)(2,1)S(1)} %slice.33), channel_id=1, source_target_pairs={{0,4},{1,5},{2,6},{3,7},{4,0},{5,1},{6,2},{7,3},{8,12},{9,13},{10,... | collective-permute-start | bytes 589832 | tf_op jit(solution)/shard_map/ppermute | solution.py:37
  16.4 2.8 %collective-permute-done.2 = bf16[96,1024]{1,0:T(8,128)(2,1)S(1)} collective-permute-done((bf16[96,1024]{1,0:T(8,128)(2,1)S(1)}, bf16[96,1024]{1,0:T(8,128)(2,1)S(1)}, u32[]{:S(2)}, u32[]{:S(2)}) %collective-permute-start.2) | collective-permute-done | bytes 196640 | tf_op jit(solution)/shard_map/ppermute | solution.py:37
  19.2 1.4 collective-permute-done.3
  20.6 1.4 pad_maximum_fusion
  22.6 3.2 %collective-permute-done.4 = bf16[4,192,1024]{2,1,0:T(8,128)(2,1)} collective-permute-done((bf16[4,192,1024]{2,1,0:T(8,128)(2,1)}, bf16[4,192,1024]{2,1,0:T(8,128)(2,1)}, u32[]{:S(2)}, u32[]{:S(2)}) %collective-permute-start.4) | collective-permute-done | bytes 1572896 | tf_op jit(solution)/shard_map/ppermute | solution.py:37
  29.9 1.9 %convert_add_fusion = f32[1024,384]{1,0:T(8,128)S(1)} fusion(bf16[1536,1024]{1,0:T(8,128)(2,1)S(1)} %fusion.3, bf16[1536,384]{1,0:T(8,128)(2,1)S(1)} %copy-done, bf16[1,1024,384]{2,1,0:T(8,128)(2,1)S(1)} %copy-done.6), kind=kOutput, calls=%fused_computation.6 | convolution fusion | flops 1208745984 | bytes 6684672 | tf_op jit(solution)/shard_map/dot_general | solution.py:130
  31.8 1.6 %convolution_bitcast_fusion = f32[32,1024]{1,0:T(8,128)S(1)} fusion(f32[1024,384]{1,0:T(8,128)S(1)} %convert_add_fusion, f32[384,32]{0,1:T(8,128)S(1)} %copy-done.5), kind=kOutput, calls=%fused_computation.8 | convolution fusion | flops 150994944 | bytes 1753088 | tf_op jit(solution)/shard_map/dot_general | solution.py:140
  33.6 1.2 collective-permute-done.5
  34.8 1.2 collective-permute-start.6
  36.0 4.4 %collective-permute-done.6 = f32[32,1024]{1,0:T(8,128)S(1)} collective-permute-done((f32[32,1024]{1,0:T(8,128)S(1)}, f32[32,1024]{1,0:T(8,128)S(1)}, u32[]{:S(2)}, u32[]{:S(2)}) %collective-permute-start.6) | collective-permute-done | bytes 131104 | tf_op jit(solution)/shard_map/ppermute | solution.py:25
  40.4 1.6 %collective-permute-start.7 = (f32[32,1024]{1,0:T(8,128)S(1)}, f32[32,1024]{1,0:T(8,128)S(1)}, u32[]{:S(2)}, u32[]{:S(2)}) collective-permute-start(f32[32,1024]{1,0:T(8,128)S(1)} %add.134), channel_id=1, source_target_pairs={{0,4},{1,5},{2,6},{3,7},{4,0},{5,1},{6,2},{7,3},{8,12},{9,13},{10,... | collective-permute-start | bytes 393224 | tf_op jit(solution)/shard_map/ppermute | solution.py:25
  42.0 3.4 %collective-permute-done.7 = f32[32,1024]{1,0:T(8,128)S(1)} collective-permute-done((f32[32,1024]{1,0:T(8,128)S(1)}, f32[32,1024]{1,0:T(8,128)S(1)}, u32[]{:S(2)}, u32[]{:S(2)}) %collective-permute-start.7) | collective-permute-done | bytes 131104 | tf_op jit(solution)/shard_map/ppermute | solution.py:25
  45.5 1.6 %collective-permute-start.8 = (f32[32,1024]{1,0:T(8,128)S(1)}, f32[32,1024]{1,0:T(8,128)S(1)}, u32[]{:S(2)}, u32[]{:S(2)}) collective-permute-start(f32[32,1024]{1,0:T(8,128)S(1)} %add.135), channel_id=1, source_target_pairs={{0,8},{1,9},{2,10},{3,11},{4,12},{5,13},{6,14},{7,15},{8,0},{9,1},... | collective-permute-start | bytes 393224 | tf_op jit(solution)/shard_map/ppermute | solution.py:25
  47.1 3.4 %collective-permute-done.8 = f32[32,1024]{1,0:T(8,128)S(1)} collective-permute-done((f32[32,1024]{1,0:T(8,128)S(1)}, f32[32,1024]{1,0:T(8,128)S(1)}, u32[]{:S(2)}, u32[]{:S(2)}) %collective-permute-start.8) | collective-permute-done | bytes 131104 | tf_op jit(solution)/shard_map/ppermute | solution.py:25
  50.5 3.1 %collective-permute-start.9 = (f32[32,1024]{1,0:T(8,128)S(1)}, f32[32,1024]{1,0:T(8,128)S(1)}, u32[]{:S(2)}, u32[]{:S(2)}) collective-permute-start(f32[32,1024]{1,0:T(8,128)S(1)} %add.136), channel_id=1, source_target_pairs={{0,16},{1,17},{2,18},{3,19},{4,20},{5,21},{6,22},{7,23},{8,24},{9,... | collective-permute-start | bytes 393224 | tf_op jit(solution)/shard_map/ppermute | solution.py:25
  53.6 4.4 %collective-permute-done.9 = f32[32,1024]{1,0:T(8,128)S(1)} collective-permute-done((f32[32,1024]{1,0:T(8,128)S(1)}, f32[32,1024]{1,0:T(8,128)S(1)}, u32[]{:S(2)}, u32[]{:S(2)}) %collective-permute-start.9) | collective-permute-done | bytes 131104 | tf_op jit(solution)/shard_map/ppermute | solution.py:25
  58.3 2.9 %cholesky.44 = f32[32,32]{1,0:T(8,128)S(1)} custom-call(f32[32,32]{1,0:T(8,128)S(1)} %fusion.22), custom_call_target="Cholesky" | custom-call | tf_op jit(solution)/shard_map/jit(cholesky)/cholesky | solution.py:145
  62.6 2.4 %custom-call.6 = f32[1,32,32]{1,2,0:T(8,128)S(1)} custom-call(f32[1,32,32]{2,1,0:T(8,128)S(1)} %fusion.17), custom_call_target="InvertDiagBlocksLowerTriangular" | custom-call | tf_op jit(solution)/shard_map/jit(_solve_triangular)/triangular_solve | solution.py:146
  67.1 3.4 %collective-permute-done.10 = f32[32,384]{1,0:T(8,128)S(1)} collective-permute-done((f32[32,384]{1,0:T(8,128)S(1)}, f32[32,384]{1,0:T(8,128)S(1)}, u32[]{:S(2)}, u32[]{:S(2)}) %collective-permute-start.10) | collective-permute-done | bytes 49184 | tf_op jit(solution)/shard_map/ppermute | solution.py:25
  70.5 2.1 %collective-permute-start.11 = (f32[32,384]{1,0:T(8,128)S(1)}, f32[32,384]{1,0:T(8,128)S(1)}, u32[]{:S(2)}, u32[]{:S(2)}) collective-permute-start(f32[32,384]{1,0:T(8,128)S(1)} %add.138), channel_id=1, source_target_pairs={{0,16},{8,24},{16,0},{24,8},{1,17},{9,25},{17,1},{25,9},{2,18},{10... | collective-permute-start | bytes 147464 | tf_op jit(solution)/shard_map/ppermute | solution.py:25
  72.6 2.9 %collective-permute-done.11 = f32[32,384]{1,0:T(8,128)S(1)} collective-permute-done((f32[32,384]{1,0:T(8,128)S(1)}, f32[32,384]{1,0:T(8,128)S(1)}, u32[]{:S(2)}, u32[]{:S(2)}) %collective-permute-start.11) | collective-permute-done | bytes 49184 | tf_op jit(solution)/shard_map/ppermute | solution.py:25
  75.5 1.6 %fusion.11 = f32[32,1024]{1,0:T(8,128)S(1)} fusion(f32[1024,384]{1,0:T(8,128)S(1)} %convert_add_fusion, f32[32,384]{1,0:T(8,128)S(1)} %add.138, f32[32,384]{1,0:T(8,128)S(1)} %collective-permute-done.11), kind=kOutput, calls=%fused_computation.28 | convolution fusion | flops 151019520 | bytes 1802240 | tf_op jit(solution)/shard_map/dot_general | solution.py:140
  77.2 1.3 collective-permute-done.12
  78.6 1.2 collective-permute-start.13
  79.8 4.4 %collective-permute-done.13 = f32[32,1024]{1,0:T(8,128)S(1)} collective-permute-done((f32[32,1024]{1,0:T(8,128)S(1)}, f32[32,1024]{1,0:T(8,128)S(1)}, u32[]{:S(2)}, u32[]{:S(2)}) %collective-permute-start.13) | collective-permute-done | bytes 131104 | tf_op jit(solution)/shard_map/ppermute | solution.py:25
  84.2 1.6 %collective-permute-start.14 = (f32[32,1024]{1,0:T(8,128)S(1)}, f32[32,1024]{1,0:T(8,128)S(1)}, u32[]{:S(2)}, u32[]{:S(2)}) collective-permute-start(f32[32,1024]{1,0:T(8,128)S(1)} %add.141), channel_id=1, source_target_pairs={{0,4},{1,5},{2,6},{3,7},{4,0},{5,1},{6,2},{7,3},{8,12},{9,13},{10,... | collective-permute-start | bytes 393224 | tf_op jit(solution)/shard_map/ppermute | solution.py:25
  85.8 3.4 %collective-permute-done.14 = f32[32,1024]{1,0:T(8,128)S(1)} collective-permute-done((f32[32,1024]{1,0:T(8,128)S(1)}, f32[32,1024]{1,0:T(8,128)S(1)}, u32[]{:S(2)}, u32[]{:S(2)}) %collective-permute-start.14) | collective-permute-done | bytes 131104 | tf_op jit(solution)/shard_map/ppermute | solution.py:25
  89.2 1.2 collective-permute-start.15
  90.5 1.1 select_reduce_fusion
  91.6 2.7 %collective-permute-done.15 = f32[32,1024]{1,0:T(8,128)S(1)} collective-permute-done((f32[32,1024]{1,0:T(8,128)S(1)}, f32[32,1024]{1,0:T(8,128)S(1)}, u32[]{:S(2)}, u32[]{:S(2)}) %collective-permute-start.15) | collective-permute-done | bytes 131104 | tf_op jit(solution)/shard_map/ppermute | solution.py:25
  94.3 2.1 %collective-permute-start.16 = (f32[32,1024]{1,0:T(8,128)S(1)}, f32[32,1024]{1,0:T(8,128)S(1)}, u32[]{:S(2)}, u32[]{:S(2)}) collective-permute-start(f32[32,1024]{1,0:T(8,128)S(1)} %add.143), channel_id=1, source_target_pairs={{0,16},{1,17},{2,18},{3,19},{4,20},{5,21},{6,22},{7,23},{8,24},{9,... | collective-permute-start | bytes 393224 | tf_op jit(solution)/shard_map/ppermute | solution.py:25
  96.4 4.1 %fusion = f32[1600,128]{1,0:T(8,128)} fusion(bf16[1536,128]{1,0:T(8,128)(2,1)S(1)} %copy-done.7, s32[1536]{0:T(1024)S(1)} %select_reduce_fusion), kind=kOutput, calls=%fused_computation.1 | convolution fusion | flops 631603200 | bytes 1218560 | tf_op jit(solution)/shard_map/dot_general | solution.py:70
  100.6 1.9 %constant_dynamic-slice_fusion.1 = (f32[400,128]{1,0:T(8,128)}, f32[400,128]{1,0:T(8,128)S(1)}, f32[400,128]{1,0:T(8,128)}) fusion(f32[1600,128]{1,0:T(8,128)} %fusion, s32[]{:T(128)S(6)} %select_n.73, s32[]{:T(128)S(6)} %select_n.77, s32[]{:T(128)S(6)} %select_n.75), kind=kLoop, calls=%fused_computation.52 | loop fusion | bytes 1228812 | tf_op jit(solution)/shard_map/dynamic_slice | solution.py:76
  102.5 2.0 %collective-permute-start.19 = (f32[400,128]{1,0:T(8,128)}, f32[400,128]{1,0:T(8,128)}, u32[]{:S(2)}, u32[]{:S(2)}) collective-permute-start(f32[400,128]{1,0:T(8,128)} %get-tuple-element.11), channel_id=1, source_target_pairs={{0,8},{8,16},{16,24},{24,0},{1,9},{9,17},{17,25},{25,1},{2,10},{10... | collective-permute-start | bytes 614408 | tf_op jit(solution)/shard_map/ppermute | solution.py:80
  104.5 2.4 %collective-permute-start.21 = (f32[400,128]{1,0:T(8,128)S(1)}, f32[400,128]{1,0:T(8,128)}, u32[]{:S(2)}, u32[]{:S(2)}) collective-permute-start(f32[400,128]{1,0:T(8,128)S(1)} %get-tuple-element.12), channel_id=1, source_target_pairs={{0,24},{8,0},{16,8},{24,16},{1,25},{9,1},{17,9},{25,17},{2,26},{10... | collective-permute-start | bytes 614408 | tf_op jit(solution)/shard_map/ppermute | solution.py:80
  107.3 2.9 %cholesky.55 = f32[32,32]{1,0:T(8,128)S(1)} custom-call(f32[32,32]{1,0:T(8,128)S(1)} %fusion.20), custom_call_target="Cholesky" | custom-call | tf_op jit(solution)/shard_map/jit(cholesky)/cholesky | solution.py:145
  111.5 3.1 %custom-call.7 = f32[1,32,32]{1,2,0:T(8,128)} custom-call(f32[1,32,32]{2,1,0:T(8,128)S(1)} %fusion.18), custom_call_target="InvertDiagBlocksLowerTriangular" | custom-call | tf_op jit(solution)/shard_map/jit(_solve_triangular)/triangular_solve | solution.py:146
  116.6 4.1 %collective-permute-done.17 = f32[32,384]{1,0:T(8,128)S(1)} collective-permute-done((f32[32,384]{1,0:T(8,128)S(1)}, f32[32,384]{1,0:T(8,128)S(1)}, u32[]{:S(2)}, u32[]{:S(2)}) %collective-permute-start.17) | collective-permute-done | bytes 49184 | tf_op jit(solution)/shard_map/ppermute | solution.py:25
  120.7 1.5 %collective-permute-start.18 = (f32[32,384]{1,0:T(8,128)S(1)}, f32[32,384]{1,0:T(8,128)S(1)}, u32[]{:S(2)}, u32[]{:S(2)}) collective-permute-start(f32[32,384]{1,0:T(8,128)S(1)} %add.145), channel_id=1, source_target_pairs={{0,16},{8,24},{16,0},{24,8},{1,17},{9,25},{17,1},{25,9},{2,18},{10... | collective-permute-start | bytes 147464 | tf_op jit(solution)/shard_map/ppermute | solution.py:25
  122.2 2.0 %multiply_subtract_fusion.1 = f32[400,128]{1,0:T(8,128)} fusion(f32[400,128]{1,0:T(8,128)S(1)} %copy-done.4, f32[400,128]{1,0:T(8,128)} %collective-permute-done.21, f32[400,128]{1,0:T(8,128)} %collective-permute-done.20, f32[400,128]{1,0:T(8,128)} %collective-permute-done.19, f32[1600,128]{1,0:T(8,128)} %fusion, s32[]{:T(128)S(6)} %select_n.71), kind=kLoop, calls=%fused_computation.20 | loop fusion | flops 256000 | bytes 1228804 | tf_op jit(solution)/shard_map/sub | solution.py:81
  124.2 1.6 %collective-permute-done.18 = f32[32,384]{1,0:T(8,128)S(1)} collective-permute-done((f32[32,384]{1,0:T(8,128)S(1)}, f32[32,384]{1,0:T(8,128)S(1)}, u32[]{:S(2)}, u32[]{:S(2)}) %collective-permute-start.18) | collective-permute-done | bytes 49184 | tf_op jit(solution)/shard_map/ppermute | solution.py:25
  125.8 1.5 fusion.16
  127.3 1.1 fusion.2
  129.4 17.4 %all_gather.3 = bf16[1024,384]{1,0:T(8,128)(2,1)S(1)} all-gather(bf16[256,384]{1,0:T(8,128)(2,1)S(1)} %get-tuple-element.8), channel_id=1, replica_groups=mesh['rep'=4,'tp'=8] {'rep'}, dimensions={0}, use_global_device_ids=true | all-gather | bytes 983040 | tf_op jit(solution)/shard_map/all_gather | solution.py:160
  (73 shorter events, 15.1 us)
Async XLA Ops:
  0.6 29.2 %copy-start = (bf16[1536,384]{1,0:T(8,128)(2,1)S(1)}, bf16[1536,384]{1,0:T(8,128)(2,1)}, u32[]{:S(2)}) copy-start(bf16[1536,384]{1,0:T(8,128)(2,1)} %param.14) | copy-start | bytes 3538948
  0.6 19.9 %copy-start.1 = (bf16[192,1024]{1,0:T(8,128)(2,1)S(1)}, bf16[192,1024]{1,0:T(8,128)(2,1)}, u32[]{:S(2)}) copy-start(bf16[192,1024]{1,0:T(8,128)(2,1)} %param.13) | copy-start | bytes 1179652
  0.7 12.4 %collective-permute-start.1 = (bf16[192,1024]{1,0:T(8,128)(2,1)}, bf16[192,1024]{1,0:T(8,128)(2,1)S(1)}, u32[]{:S(2)}, u32[]{:S(2)}) collective-permute-start(bf16[192,1024]{1,0:T(8,128)(2,1)} %param.13), channel_id=1, source_target_pairs={{0,4},{1,5},{2,6},{3,7},{4,0},{5,1},{6,2},{7,3},{8,12},{9,13},{10,... | collective-permute-start | bytes 1179656 | tf_op jit(solution)/shard_map/ppermute | solution.py:37
  3.7 11.1 %collective-permute-start = (bf16[192,1024]{1,0:T(8,128)(2,1)}, bf16[192,1024]{1,0:T(8,128)(2,1)S(1)}, u32[]{:S(2)}, u32[]{:S(2)}) collective-permute-start(bf16[192,1024]{1,0:T(8,128)(2,1)} %param.13), channel_id=1, source_target_pairs={{0,2},{1,3},{2,0},{3,1},{4,6},{5,7},{6,4},{7,5},{8,10},{9,11},{10,... | collective-permute-start | bytes 1179656 | tf_op jit(solution)/shard_map/ppermute | solution.py:37
  13.0 6.2 %collective-permute-start.2 = (bf16[96,1024]{1,0:T(8,128)(2,1)S(1)}, bf16[96,1024]{1,0:T(8,128)(2,1)S(1)}, u32[]{:S(2)}, u32[]{:S(2)}) collective-permute-start(bf16[96,1024]{1,0:T(8,128)(2,1)S(1)} %slice.32), channel_id=1, source_target_pairs={{0,2},{1,3},{2,0},{3,1},{4,6},{5,7},{6,4},{7,5},{8,10},{9,11},{10,... | collective-permute-start | bytes 589832 | tf_op jit(solution)/shard_map/ppermute | solution.py:37
  14.8 5.7 %collective-permute-start.3 = (bf16[96,1024]{1,0:T(8,128)(2,1)S(1)}, bf16[96,1024]{1,0:T(8,128)(2,1)S(1)}, u32[]{:S(2)}, u32[]{:S(2)}) collective-permute-start(bf16[96,1024]{1,0:T(8,128)(2,1)S(1)} %slice.33), channel_id=1, source_target_pairs={{0,4},{1,5},{2,6},{3,7},{4,0},{5,1},{6,2},{7,3},{8,12},{9,13},{10,... | collective-permute-start | bytes 589832 | tf_op jit(solution)/shard_map/ppermute | solution.py:37
  22.0 3.8 %collective-permute-start.4 = (bf16[4,192,1024]{2,1,0:T(8,128)(2,1)}, bf16[4,192,1024]{2,1,0:T(8,128)(2,1)}, u32[]{:S(2)}, u32[]{:S(2)}) collective-permute-start(bf16[4,192,1024]{2,1,0:T(8,128)(2,1)} %pad_maximum_fusion), channel_id=1, source_target_pairs={{0,1},{1,0},{2,3},{3,2},{4,5},{5,4},{6,7},{7,6},{8,9},{9,8},{10,11... | collective-permute-start | bytes 4718600 | tf_op jit(solution)/shard_map/ppermute | solution.py:37
  22.5 7.3 %copy-start.6 = (bf16[1,1024,384]{2,1,0:T(8,128)(2,1)S(1)}, bf16[1,1024,384]{2,1,0:T(8,128)(2,1)}, u32[]{:S(2)}) copy-start(bf16[1,1024,384]{2,1,0:T(8,128)(2,1)} %param.15) | copy-start | bytes 2359300
  29.9 1.9 %copy-start.5 = (f32[384,32]{0,1:T(8,128)S(1)}, f32[384,32]{0,1:T(8,128)}, u32[]{:S(2)}) copy-start(f32[384,32]{0,1:T(8,128)} %param.16) | copy-start | bytes 147460
  33.4 1.4 collective-permute-start.5
  34.8 5.6 %collective-permute-start.6 = (f32[32,1024]{1,0:T(8,128)S(1)}, f32[32,1024]{1,0:T(8,128)S(1)}, u32[]{:S(2)}, u32[]{:S(2)}) collective-permute-start(f32[32,1024]{1,0:T(8,128)S(1)} %add.133), channel_id=1, source_target_pairs={{0,2},{1,3},{2,0},{3,1},{4,6},{5,7},{6,4},{7,5},{8,10},{9,11},{10,... | collective-permute-start | bytes 393224 | tf_op jit(solution)/shard_map/ppermute | solution.py:25
  40.4 5.0 %collective-permute-start.7 = (f32[32,1024]{1,0:T(8,128)S(1)}, f32[32,1024]{1,0:T(8,128)S(1)}, u32[]{:S(2)}, u32[]{:S(2)}) collective-permute-start(f32[32,1024]{1,0:T(8,128)S(1)} %add.134), channel_id=1, source_target_pairs={{0,4},{1,5},{2,6},{3,7},{4,0},{5,1},{6,2},{7,3},{8,12},{9,13},{10,... | collective-permute-start | bytes 393224 | tf_op jit(solution)/shard_map/ppermute | solution.py:25
  45.5 5.0 %collective-permute-start.8 = (f32[32,1024]{1,0:T(8,128)S(1)}, f32[32,1024]{1,0:T(8,128)S(1)}, u32[]{:S(2)}, u32[]{:S(2)}) collective-permute-start(f32[32,1024]{1,0:T(8,128)S(1)} %add.135), channel_id=1, source_target_pairs={{0,8},{1,9},{2,10},{3,11},{4,12},{5,13},{6,14},{7,15},{8,0},{9,1},... | collective-permute-start | bytes 393224 | tf_op jit(solution)/shard_map/ppermute | solution.py:25
  50.5 7.4 %collective-permute-start.9 = (f32[32,1024]{1,0:T(8,128)S(1)}, f32[32,1024]{1,0:T(8,128)S(1)}, u32[]{:S(2)}, u32[]{:S(2)}) collective-permute-start(f32[32,1024]{1,0:T(8,128)S(1)} %add.136), channel_id=1, source_target_pairs={{0,16},{1,17},{2,18},{3,19},{4,20},{5,21},{6,22},{7,23},{8,24},{9,... | collective-permute-start | bytes 393224 | tf_op jit(solution)/shard_map/ppermute | solution.py:25
  66.3 24.2 %copy-start.8 = (s32[1600]{0:T(1024)S(1)}, s32[1600]{0:T(1024)}, u32[]{:S(2)}) copy-start(s32[1600]{0:T(1024)} %param.21) | copy-start | bytes 19204
  66.3 24.2 %copy-start.9 = (s32[1536]{0:T(1024)S(1)}, s32[1536]{0:T(1024)}, u32[]{:S(2)}) copy-start(s32[1536]{0:T(1024)} %param.20) | copy-start | bytes 18436
  66.3 4.2 %collective-permute-start.10 = (f32[32,384]{1,0:T(8,128)S(1)}, f32[32,384]{1,0:T(8,128)S(1)}, u32[]{:S(2)}, u32[]{:S(2)}) collective-permute-start(f32[32,384]{1,0:T(8,128)S(1)} %fusion.32), channel_id=1, source_target_pairs={{0,8},{8,0},{16,24},{24,16},{1,9},{9,1},{17,25},{25,17},{2,10},{10... | collective-permute-start | bytes 147464 | tf_op jit(solution)/shard_map/ppermute | solution.py:25
  70.5 26.0 %copy-start.7 = (bf16[1536,128]{1,0:T(8,128)(2,1)S(1)}, bf16[1536,128]{1,0:T(8,128)(2,1)}, u32[]{:S(2)}) copy-start(bf16[1536,128]{1,0:T(8,128)(2,1)} %param.19) | copy-start | bytes 1179652
  70.5 5.1 %collective-permute-start.11 = (f32[32,384]{1,0:T(8,128)S(1)}, f32[32,384]{1,0:T(8,128)S(1)}, u32[]{:S(2)}, u32[]{:S(2)}) collective-permute-start(f32[32,384]{1,0:T(8,128)S(1)} %add.138), channel_id=1, source_target_pairs={{0,16},{8,24},{16,0},{24,8},{1,17},{9,25},{17,1},{25,9},{2,18},{10... | collective-permute-start | bytes 147464 | tf_op jit(solution)/shard_map/ppermute | solution.py:25
  77.1 1.4 collective-permute-start.12
  78.6 5.6 %collective-permute-start.13 = (f32[32,1024]{1,0:T(8,128)S(1)}, f32[32,1024]{1,0:T(8,128)S(1)}, u32[]{:S(2)}, u32[]{:S(2)}) collective-permute-start(f32[32,1024]{1,0:T(8,128)S(1)} %add.140), channel_id=1, source_target_pairs={{0,2},{1,3},{2,0},{3,1},{4,6},{5,7},{6,4},{7,5},{8,10},{9,11},{10,... | collective-permute-start | bytes 393224 | tf_op jit(solution)/shard_map/ppermute | solution.py:25
  84.2 5.0 %collective-permute-start.14 = (f32[32,1024]{1,0:T(8,128)S(1)}, f32[32,1024]{1,0:T(8,128)S(1)}, u32[]{:S(2)}, u32[]{:S(2)}) collective-permute-start(f32[32,1024]{1,0:T(8,128)S(1)} %add.141), channel_id=1, source_target_pairs={{0,4},{1,5},{2,6},{3,7},{4,0},{5,1},{6,2},{7,3},{8,12},{9,13},{10,... | collective-permute-start | bytes 393224 | tf_op jit(solution)/shard_map/ppermute | solution.py:25
  89.2 5.0 %collective-permute-start.15 = (f32[32,1024]{1,0:T(8,128)S(1)}, f32[32,1024]{1,0:T(8,128)S(1)}, u32[]{:S(2)}, u32[]{:S(2)}) collective-permute-start(f32[32,1024]{1,0:T(8,128)S(1)} %add.142), channel_id=1, source_target_pairs={{0,8},{1,9},{2,10},{3,11},{4,12},{5,13},{6,14},{7,15},{8,0},{9,1},... | collective-permute-start | bytes 393224 | tf_op jit(solution)/shard_map/ppermute | solution.py:25
  94.3 12.6 %collective-permute-start.16 = (f32[32,1024]{1,0:T(8,128)S(1)}, f32[32,1024]{1,0:T(8,128)S(1)}, u32[]{:S(2)}, u32[]{:S(2)}) collective-permute-start(f32[32,1024]{1,0:T(8,128)S(1)} %add.143), channel_id=1, source_target_pairs={{0,16},{1,17},{2,18},{3,19},{4,20},{5,21},{6,22},{7,23},{8,24},{9,... | collective-permute-start | bytes 393224 | tf_op jit(solution)/shard_map/ppermute | solution.py:25
  102.5 19.7 %copy-start.4 = (f32[400,128]{1,0:T(8,128)S(1)}, f32[400,128]{1,0:T(8,128)}, u32[]{:S(2)}) copy-start(f32[400,128]{1,0:T(8,128)} %param.22) | copy-start | bytes 614404
  102.5 19.7 %collective-permute-start.19 = (f32[400,128]{1,0:T(8,128)}, f32[400,128]{1,0:T(8,128)}, u32[]{:S(2)}, u32[]{:S(2)}) collective-permute-start(f32[400,128]{1,0:T(8,128)} %get-tuple-element.11), channel_id=1, source_target_pairs={{0,8},{8,16},{16,24},{24,0},{1,9},{9,17},{17,25},{25,1},{2,10},{10... | collective-permute-start | bytes 614408 | tf_op jit(solution)/shard_map/ppermute | solution.py:80
  104.5 17.7 %collective-permute-start.20 = (f32[400,128]{1,0:T(8,128)}, f32[400,128]{1,0:T(8,128)}, u32[]{:S(2)}, u32[]{:S(2)}) collective-permute-start(f32[400,128]{1,0:T(8,128)} %get-tuple-element.13), channel_id=1, source_target_pairs={{0,16},{8,24},{16,0},{24,8},{1,17},{9,25},{17,1},{25,9},{2,18},{10... | collective-permute-start | bytes 614408 | tf_op jit(solution)/shard_map/ppermute | solution.py:80
  104.5 17.7 %collective-permute-start.21 = (f32[400,128]{1,0:T(8,128)S(1)}, f32[400,128]{1,0:T(8,128)}, u32[]{:S(2)}, u32[]{:S(2)}) collective-permute-start(f32[400,128]{1,0:T(8,128)S(1)} %get-tuple-element.12), channel_id=1, source_target_pairs={{0,24},{8,0},{16,8},{24,16},{1,25},{9,1},{17,9},{25,17},{2,26},{10... | collective-permute-start | bytes 614408 | tf_op jit(solution)/shard_map/ppermute | solution.py:80
  116.5 4.2 %collective-permute-start.17 = (f32[32,384]{1,0:T(8,128)S(1)}, f32[32,384]{1,0:T(8,128)S(1)}, u32[]{:S(2)}, u32[]{:S(2)}) collective-permute-start(f32[32,384]{1,0:T(8,128)S(1)} %fusion.33), channel_id=1, source_target_pairs={{0,8},{8,0},{16,24},{24,16},{1,9},{9,1},{17,25},{25,17},{2,10},{10... | collective-permute-start | bytes 147464 | tf_op jit(solution)/shard_map/ppermute | solution.py:25
  120.7 5.1 %collective-permute-start.18 = (f32[32,384]{1,0:T(8,128)S(1)}, f32[32,384]{1,0:T(8,128)S(1)}, u32[]{:S(2)}, u32[]{:S(2)}) collective-permute-start(f32[32,384]{1,0:T(8,128)S(1)} %add.145), channel_id=1, source_target_pairs={{0,16},{8,24},{16,0},{24,8},{1,17},{9,25},{17,1},{25,9},{2,18},{10... | collective-permute-start | bytes 147464 | tf_op jit(solution)/shard_map/ppermute | solution.py:25
  127.2 1.2 copy-start.2
  127.2 1.2 copy-start.3

commit v5 on v4

--- a/solution.py
+++ b/solution.py
@@ -134,6 +134,20 @@
         preferred_element_type=jnp.float32,
     )
     combined = product + error_state[0].astype(jnp.float32)
+    owned_rows = qkv_master.shape[0]
+    if replicas <= 8:
+        base_rows = qkv_master - LEARNING_RATE * (MOMENTUM * qkv_moment)
+        me = lax.axis_index("rep")
+        arrivals = []
+        for shift in range(1, replicas):
+            pairs = [(i, (i + shift) % replicas) for i in range(replicas)]
+            arrivals.append(lax.ppermute(base_rows, "rep", pairs))
+        arrivals, combined = lax.optimization_barrier((arrivals, combined))
+        base = jnp.zeros(combined.shape, jnp.float32)
+        base = lax.dynamic_update_slice_in_dim(base, base_rows, me * owned_rows, 0)
+        for shift, arrived in zip(range(1, replicas), arrivals):
+            source = (me + replicas - shift) % replicas
+            base = lax.dynamic_update_slice_in_dim(base, arrived, source * owned_rows, 0)
     right_rows = q_start.T
     left_rows = None
     for round_index in range(ROUNDS):
@@ -151,13 +165,17 @@
         left_rows, right_rows, (((0,), (0,)), ((), ())), precision=highest
     )
     error_new = (combined - approx).astype(jnp.bfloat16)[None]
-    owned_rows = qkv_master.shape[0]
     update_rows = lax.dynamic_slice_in_dim(
         approx, lax.axis_index("rep") * owned_rows, owned_rows, 0
     )
     moment_new = MOMENTUM * qkv_moment + update_rows
     master_new = qkv_master - LEARNING_RATE * moment_new
-    weight_bf16 = lax.all_gather(master_new.astype(jnp.bfloat16), "rep", axis=0, tiled=True)
+    if replicas <= 8:
+        weight_bf16 = (base - LEARNING_RATE * approx).astype(jnp.bfloat16)
+    else:
+        weight_bf16 = lax.all_gather(
+            master_new.astype(jnp.bfloat16), "rep", axis=0, tiled=True
+        )
     word_new = word_update(word_grads, token_ids, owner_map, word_master)
     return (error_new, right_basis, moment_new, master_new, weight_bf16, word_new)
 

time: 149 us -> 181 us (1.21)
  waiting for transfers between devices: 55.7 us -> 74.2 us
  blocking collectives: 17.4 us -> 0 us
  other arithmetic: 21.3 us -> 32.8 us
  starting transfers between devices: 30.7 us -> 41.1 us
  local copies, waits for them, and re-layouts: 7.69 us -> 15.1 us
    ppermute x0 -> x3, waiting for transfers between devices: none -> 18.3 us  [shards(): arrivals.append(lax.ppermute(base_rows, 'rep', pairs))]
    all_gather x1 -> x0, blocking collectives: 17.4 us -> none  [shards(): lax.all_gather(master_new.astype(jnp.bfloat16), 'rep', axis=0, tiled=True)]
    ppermute x0 -> x3, starting transfers between devices: none -> 5.53 us  [shards(): arrivals.append(lax.ppermute(base_rows, 'rep', pairs))]
    dynamic_update_slice x0 -> x3, local copies, waits for them, and re-layouts: none -> 5.36 us  [shards(): lax.dynamic_update_slice_in_dim(base, arrived, source * owned_rows, 0)]
    ppermute x14, starting transfers between devices: 18.4 us -> 22.8 us  [tree_sum(): value = value + lax.ppermute(value, axes, pairs)]
    ppermute x14, waiting for transfers between devices: 40.6 us -> 43.9 us  [tree_sum(): value = value + lax.ppermute(value, axes, pairs)]
    ppermute x5, waiting for transfers between devices: 15.1 us -> 12 us  [exchange(): return lax.ppermute(value, axis, [(i, i ^ stride) for i in range(count)])]
    div x2, other arithmetic: 0.02 us -> 2.65 us  [shards(): factor_low = jnp.linalg.cholesky(gram_matrix)]
  transfers between devices with their start and end apart: 22 -> 25, of which waited for: 17 -> 18; matrix products, arithmetic and copies ran while one was open for 13% -> 13% of each run, Pallas kernels for 0% -> 0%
where the time goes in v5:
time: 181 us; the launch traced here: 180 us
  waiting for transfers between devices  74.2 us (41%)
  starting transfers between devices  41.1 us (23%)
  other arithmetic  32.8 us (18%)
  matrix products  16.2 us (9%)
  local copies, waits for them, and re-layouts  15.1 us (8%)
    ppermute x14, waiting for transfers between devices, tree_sum(): value = value + lax.ppermute(value, axes, pairs)  43.9 us
    ppermute x14, starting transfers between devices, tree_sum(): value = value + lax.ppermute(value, axes, pairs)  22.8 us
    ppermute x3, waiting for transfers between devices, shards(): arrivals.append(lax.ppermute(base_rows, 'rep', pairs))  18.3 us
    ppermute x5, waiting for transfers between devices, exchange(): return lax.ppermute(value, axis, [(i, i ^ stride) for i in range(count)])  12 us
    another operation x4, other arithmetic, shards(): jax.scipy.linalg.solve_triangular(factor_low, left_rows, lower=True)  8.81 us
    another operation x6, other arithmetic, shards(): factor_low = jnp.linalg.cholesky(gram_matrix)  8.61 us
    ppermute x5, starting transfers between devices, exchange(): return lax.ppermute(value, axis, [(i, i ^ stride) for i in range(count)])  7.89 us
    ppermute x3, starting transfers between devices, shards(): arrivals.append(lax.ppermute(base_rows, 'rep', pairs))  5.53 us
  transfers between devices with their start and end apart: 25, of which 18 were waited for; matrix products, arithmetic and copies ran while one was open for 13% of the time, Pallas kernels for 0%

profile of v5, /device:TPU:0, one launch (start us, length us, event | category | flops | bytes accessed | tf_op | source)
XLA Modules:
  0.0 180.4 jit_solution(10516478331691313481)
XLA Ops:
  0.7 3.0 %collective-permute-start.4 = (bf16[192,1024]{1,0:T(8,128)(2,1)}, bf16[192,1024]{1,0:T(8,128)(2,1)S(1)}, u32[]{:S(2)}, u32[]{:S(2)}) collective-permute-start(bf16[192,1024]{1,0:T(8,128)(2,1)} %param.13), channel_id=1, source_target_pairs={{0,4},{1,5},{2,6},{3,7},{4,0},{5,1},{6,2},{7,3},{8,12},{9,13},{10,... | collective-permute-start | bytes 1179656 | tf_op jit(solution)/shard_map/ppermute | solution.py:37
  3.7 1.5 collective-permute-start.3
  5.2 7.8 %collective-permute-done.4 = bf16[192,1024]{1,0:T(8,128)(2,1)S(1)} collective-permute-done((bf16[192,1024]{1,0:T(8,128)(2,1)}, bf16[192,1024]{1,0:T(8,128)(2,1)S(1)}, u32[]{:S(2)}, u32[]{:S(2)}) %collective-permute-start.4) | collective-permute-done | bytes 393248 | tf_op jit(solution)/shard_map/ppermute | solution.py:37
  13.0 1.8 collective-permute-start.5
  14.8 1.6 collective-permute-start.6
  16.4 2.8 %collective-permute-done.5 = bf16[96,1024]{1,0:T(8,128)(2,1)S(1)} collective-permute-done((bf16[96,1024]{1,0:T(8,128)(2,1)S(1)}, bf16[96,1024]{1,0:T(8,128)(2,1)S(1)}, u32[]{:S(2)}, u32[]{:S(2)}) %collective-permute-start.5) | collective-permute-done | bytes 196640 | tf_op jit(solution)/shard_map/ppermute | solution.py:37
  19.2 1.4 collective-permute-done.6
  20.6 1.4 pad_maximum_fusion
  24.3 1.6 collective-permute-start
  25.9 2.6 %collective-permute-start.1 = (f32[256,384]{1,0:T(8,128)}, f32[256,384]{1,0:T(8,128)}, u32[]{:S(2)}, u32[]{:S(2)}) collective-permute-start(f32[256,384]{1,0:T(8,128)} %get-tuple-element.17), channel_id=1, source_target_pairs={{0,16},{8,24},{16,0},{24,8},{1,17},{9,25},{17,1},{25,9},{2,18},{10... | collective-permute-start | bytes 1179656 | tf_op jit(solution)/shard_map/ppermute | solution.py:144
  28.5 1.3 collective-permute-start.2
  34.7 1.9 %convert_add_fusion = f32[1024,384]{1,0:T(8,128)S(1)} fusion(bf16[1536,1024]{1,0:T(8,128)(2,1)S(1)} %fusion.3, bf16[1536,384]{1,0:T(8,128)(2,1)S(1)} %copy-done, bf16[1,1024,384]{2,1,0:T(8,128)(2,1)S(1)} %copy-done.10), kind=kOutput, calls=%fused_computation.6 | convolution fusion | flops 1208745984 | bytes 6684672 | tf_op jit(solution)/shard_map/dot_general | solution.py:130
  36.5 1.9 %collective-permute-done = f32[256,384]{1,0:T(8,128)} collective-permute-done((f32[256,384]{1,0:T(8,128)}, f32[256,384]{1,0:T(8,128)}, u32[]{:S(2)}, u32[]{:S(2)}) %collective-permute-start) | collective-permute-done | bytes 393248 | tf_op jit(solution)/shard_map/ppermute | solution.py:144
  38.5 16.4 %collective-permute-done.1 = f32[256,384]{1,0:T(8,128)} collective-permute-done((f32[256,384]{1,0:T(8,128)}, f32[256,384]{1,0:T(8,128)}, u32[]{:S(2)}, u32[]{:S(2)}) %collective-permute-start.1) | collective-permute-done | bytes 393248 | tf_op jit(solution)/shard_map/ppermute | solution.py:144
  54.9 1.6 convolution_bitcast_fusion
  56.5 1.3 collective-permute-done.8
  59.1 4.4 %collective-permute-done.9 = f32[32,1024]{1,0:T(8,128)S(1)} collective-permute-done((f32[32,1024]{1,0:T(8,128)S(1)}, f32[32,1024]{1,0:T(8,128)S(1)}, u32[]{:S(2)}, u32[]{:S(2)}) %collective-permute-start.9) | collective-permute-done | bytes 131104 | tf_op jit(solution)/shard_map/ppermute | solution.py:25
  63.5 1.6 collective-permute-start.10
  65.1 3.4 %collective-permute-done.10 = f32[32,1024]{1,0:T(8,128)S(1)} collective-permute-done((f32[32,1024]{1,0:T(8,128)S(1)}, f32[32,1024]{1,0:T(8,128)S(1)}, u32[]{:S(2)}, u32[]{:S(2)}) %collective-permute-start.10) | collective-permute-done | bytes 131104 | tf_op jit(solution)/shard_map/ppermute | solution.py:25
  68.6 9.0 %collective-permute-start.11 = (f32[32,1024]{1,0:T(8,128)S(1)}, f32[32,1024]{1,0:T(8,128)S(1)}, u32[]{:S(2)}, u32[]{:S(2)}) collective-permute-start(f32[32,1024]{1,0:T(8,128)S(1)} %add.154), channel_id=1, source_target_pairs={{0,8},{1,9},{2,10},{3,11},{4,12},{5,13},{6,14},{7,15},{8,0},{9,1},... | collective-permute-start | bytes 393224 | tf_op jit(solution)/shard_map/ppermute | solution.py:25
  77.6 2.9 %collective-permute-done.11 = f32[32,1024]{1,0:T(8,128)S(1)} collective-permute-done((f32[32,1024]{1,0:T(8,128)S(1)}, f32[32,1024]{1,0:T(8,128)S(1)}, u32[]{:S(2)}, u32[]{:S(2)}) %collective-permute-start.11) | collective-permute-done | bytes 131104 | tf_op jit(solution)/shard_map/ppermute | solution.py:25
  80.6 1.7 collective-permute-start.12
  82.2 4.3 %collective-permute-done.12 = f32[32,1024]{1,0:T(8,128)S(1)} collective-permute-done((f32[32,1024]{1,0:T(8,128)S(1)}, f32[32,1024]{1,0:T(8,128)S(1)}, u32[]{:S(2)}, u32[]{:S(2)}) %collective-permute-start.12) | collective-permute-done | bytes 131104 | tf_op jit(solution)/shard_map/ppermute | solution.py:25
  88.1 1.3 fusion.22
  89.4 3.6 %cholesky.44 = f32[32,32]{1,0:T(8,128)S(1)} custom-call(f32[32,32]{1,0:T(8,128)} %fusion.22), custom_call_target="Cholesky" | custom-call | tf_op jit(solution)/shard_map/jit(cholesky)/cholesky | solution.py:159
  95.0 3.2 %custom-call.6 = f32[1,32,32]{1,2,0:T(8,128)S(1)} custom-call(f32[1,32,32]{2,1,0:T(8,128)} %fusion.17), custom_call_target="InvertDiagBlocksLowerTriangular" | custom-call | tf_op jit(solution)/shard_map/jit(_solve_triangular)/triangular_solve | solution.py:160
  100.4 2.5 %collective-permute-start.13 = (f32[32,384]{1,0:T(8,128)S(1)}, f32[32,384]{1,0:T(8,128)S(1)}, u32[]{:S(2)}, u32[]{:S(2)}) collective-permute-start(f32[32,384]{1,0:T(8,128)S(1)} %fusion.31), channel_id=1, source_target_pairs={{0,8},{8,0},{16,24},{24,16},{1,9},{9,1},{17,25},{25,17},{2,10},{10... | collective-permute-start | bytes 147464 | tf_op jit(solution)/shard_map/ppermute | solution.py:25
  102.9 2.2 %collective-permute-done.13 = f32[32,384]{1,0:T(8,128)S(1)} collective-permute-done((f32[32,384]{1,0:T(8,128)S(1)}, f32[32,384]{1,0:T(8,128)S(1)}, u32[]{:S(2)}, u32[]{:S(2)}) %collective-permute-start.13) | collective-permute-done | bytes 49184 | tf_op jit(solution)/shard_map/ppermute | solution.py:25
  105.1 2.0 %collective-permute-start.14 = (f32[32,384]{1,0:T(8,128)S(1)}, f32[32,384]{1,0:T(8,128)S(1)}, u32[]{:S(2)}, u32[]{:S(2)}) collective-permute-start(f32[32,384]{1,0:T(8,128)S(1)} %add.157), channel_id=1, source_target_pairs={{0,16},{8,24},{16,0},{24,8},{1,17},{9,25},{17,1},{25,9},{2,18},{10... | collective-permute-start | bytes 147464 | tf_op jit(solution)/shard_map/ppermute | solution.py:25
  107.1 3.1 %collective-permute-done.14 = f32[32,384]{1,0:T(8,128)S(1)} collective-permute-done((f32[32,384]{1,0:T(8,128)S(1)}, f32[32,384]{1,0:T(8,128)S(1)}, u32[]{:S(2)}, u32[]{:S(2)}) %collective-permute-start.14) | collective-permute-done | bytes 49184 | tf_op jit(solution)/shard_map/ppermute | solution.py:25
  110.1 2.2 %fusion.11 = f32[32,1024]{1,0:T(8,128)} fusion(f32[1024,384]{1,0:T(8,128)S(1)} %convert_add_fusion, f32[32,384]{1,0:T(8,128)S(1)} %add.157, f32[32,384]{1,0:T(8,128)S(1)} %collective-permute-done.14), kind=kOutput, calls=%fused_computation.30 | convolution fusion | flops 151019520 | bytes 1802240 | tf_op jit(solution)/shard_map/dot_general | solution.py:154
  116.3 4.1 %fusion = f32[1600,128]{1,0:T(8,128)S(1)} fusion(bf16[1536,128]{1,0:T(8,128)(2,1)} %param.19, s32[1536]{0:T(1024)S(1)} %select_reduce_fusion), kind=kOutput, calls=%fused_computation.1 | convolution fusion | flops 631603200 | bytes 1218560 | tf_op jit(solution)/shard_map/dot_general | solution.py:70
  120.7 1.6 collective-permute-start.17
  123.1 1.9 %collective-permute-start.22 = (f32[400,128]{1,0:T(8,128)}, f32[400,128]{1,0:T(8,128)}, u32[]{:S(2)}, u32[]{:S(2)}) collective-permute-start(f32[400,128]{1,0:T(8,128)} %get-tuple-element.22), channel_id=1, source_target_pairs={{0,8},{8,16},{16,24},{24,0},{1,9},{9,17},{17,25},{25,1},{2,10},{10... | collective-permute-start | bytes 614408 | tf_op jit(solution)/shard_map/ppermute | solution.py:80
  125.0 2.0 %collective-permute-start.23 = (f32[400,128]{1,0:T(8,128)}, f32[400,128]{1,0:T(8,128)}, u32[]{:S(2)}, u32[]{:S(2)}) collective-permute-start(f32[400,128]{1,0:T(8,128)} %get-tuple-element.24), channel_id=1, source_target_pairs={{0,16},{8,24},{16,0},{24,8},{1,17},{9,25},{17,1},{25,9},{2,18},{10... | collective-permute-start | bytes 614408 | tf_op jit(solution)/shard_map/ppermute | solution.py:80
  129.8 13.1 %collective-permute-done.18 = f32[32,1024]{1,0:T(8,128)} collective-permute-done((f32[32,1024]{1,0:T(8,128)}, f32[32,1024]{1,0:T(8,128)}, u32[]{:S(2)}, u32[]{:S(2)}) %collective-permute-start.18) | collective-permute-done | bytes 131104 | tf_op jit(solution)/shard_map/ppermute | solution.py:25
  144.5 2.0 %multiply_subtract_fusion.2 = f32[400,128]{1,0:T(8,128)} fusion(f32[400,128]{1,0:T(8,128)} %param.22, f32[400,128]{1,0:T(8,128)} %collective-permute-done.24, f32[400,128]{1,0:T(8,128)} %collective-permute-done.23, f32[400,128]{1,0:T(8,128)} %collective-permute-done.22, f32[1600,128]{1,0:T(8,128)} %copy-done.6, s32[]{:T(128)S(6)} %select_n.93), kind=kLoop, calls=%fused_computation.22 | loop fusion | flops 256000 | bytes 1228804 | tf_op jit(solution)/shard_map/sub | solution.py:81
  146.6 1.8 constant_dynamic-update-slice_fusion.4
  148.3 2.9 %collective-permute-done.19 = f32[32,1024]{1,0:T(8,128)S(1)} collective-permute-done((f32[32,1024]{1,0:T(8,128)S(1)}, f32[32,1024]{1,0:T(8,128)S(1)}, u32[]{:S(2)}, u32[]{:S(2)}) %collective-permute-start.19) | collective-permute-done | bytes 131104 | tf_op jit(solution)/shard_map/ppermute | solution.py:25
  152.9 1.3 fusion.20
  154.2 3.6 %cholesky.55 = f32[32,32]{1,0:T(8,128)S(1)} custom-call(f32[32,32]{1,0:T(8,128)} %fusion.20), custom_call_target="Cholesky" | custom-call | tf_op jit(solution)/shard_map/jit(cholesky)/cholesky | solution.py:159
  159.7 3.2 %custom-call.7 = f32[1,32,32]{1,2,0:T(8,128)S(1)} custom-call(f32[1,32,32]{2,1,0:T(8,128)} %fusion.18), custom_call_target="InvertDiagBlocksLowerTriangular" | custom-call | tf_op jit(solution)/shard_map/jit(_solve_triangular)/triangular_solve | solution.py:160
  165.2 1.8 constant_dynamic-update-slice_fusion.3
  167.0 2.3 %collective-permute-done.20 = f32[32,384]{1,0:T(8,128)S(1)} collective-permute-done((f32[32,384]{1,0:T(8,128)S(1)}, f32[32,384]{1,0:T(8,128)S(1)}, u32[]{:S(2)}, u32[]{:S(2)}) %collective-permute-start.20) | collective-permute-done | bytes 49184 | tf_op jit(solution)/shard_map/ppermute | solution.py:25
  169.4 1.8 constant_dynamic-update-slice_fusion.2
  171.2 3.2 %collective-permute-done.21 = f32[32,384]{1,0:T(8,128)S(1)} collective-permute-done((f32[32,384]{1,0:T(8,128)S(1)}, f32[32,384]{1,0:T(8,128)S(1)}, u32[]{:S(2)}, u32[]{:S(2)}) %collective-permute-start.21) | collective-permute-done | bytes 49184 | tf_op jit(solution)/shard_map/ppermute | solution.py:25
  174.4 1.5 fusion.16
  176.8 3.0 %subtract_convert_fusion = (bf16[1024,384]{1,0:T(8,128)(2,1)}, bf16[1,1024,384]{2,1,0:T(8,128)(2,1)}) fusion(f32[1024,384]{1,0:T(8,128)} %constant_dynamic-update-slice_fusion.2, f32[1024,384]{1,0:T(8,128)S(1)} %fusion.16, f32[1024,384]{1,0:T(8,128)S(1)} %convert_add_fusion), kind=kLoop, calls=%fused_computation.7 | loop fusion | flops 1966080 | bytes 6291456 | tf_op jit(solution)/shard_map/convert_element_type | solution.py:174
  (88 shorter events, 31.1 us)
Async XLA Ops:
  0.6 34.0 %copy-start = (bf16[1536,384]{1,0:T(8,128)(2,1)S(1)}, bf16[1536,384]{1,0:T(8,128)(2,1)}, u32[]{:S(2)}) copy-start(bf16[1536,384]{1,0:T(8,128)(2,1)} %param.14) | copy-start | bytes 3538948
  0.6 19.9 %copy-start.1 = (bf16[192,1024]{1,0:T(8,128)(2,1)S(1)}, bf16[192,1024]{1,0:T(8,128)(2,1)}, u32[]{:S(2)}) copy-start(bf16[192,1024]{1,0:T(8,128)(2,1)} %param.13) | copy-start | bytes 1179652
  0.7 12.4 %collective-permute-start.4 = (bf16[192,1024]{1,0:T(8,128)(2,1)}, bf16[192,1024]{1,0:T(8,128)(2,1)S(1)}, u32[]{:S(2)}, u32[]{:S(2)}) collective-permute-start(bf16[192,1024]{1,0:T(8,128)(2,1)} %param.13), channel_id=1, source_target_pairs={{0,4},{1,5},{2,6},{3,7},{4,0},{5,1},{6,2},{7,3},{8,12},{9,13},{10,... | collective-permute-start | bytes 1179656 | tf_op jit(solution)/shard_map/ppermute | solution.py:37
  3.7 11.1 %collective-permute-start.3 = (bf16[192,1024]{1,0:T(8,128)(2,1)}, bf16[192,1024]{1,0:T(8,128)(2,1)S(1)}, u32[]{:S(2)}, u32[]{:S(2)}) collective-permute-start(bf16[192,1024]{1,0:T(8,128)(2,1)} %param.13), channel_id=1, source_target_pairs={{0,2},{1,3},{2,0},{3,1},{4,6},{5,7},{6,4},{7,5},{8,10},{9,11},{10,... | collective-permute-start | bytes 1179656 | tf_op jit(solution)/shard_map/ppermute | solution.py:37
  13.0 6.2 %collective-permute-start.5 = (bf16[96,1024]{1,0:T(8,128)(2,1)S(1)}, bf16[96,1024]{1,0:T(8,128)(2,1)S(1)}, u32[]{:S(2)}, u32[]{:S(2)}) collective-permute-start(bf16[96,1024]{1,0:T(8,128)(2,1)S(1)} %slice.32), channel_id=1, source_target_pairs={{0,2},{1,3},{2,0},{3,1},{4,6},{5,7},{6,4},{7,5},{8,10},{9,11},{10,... | collective-permute-start | bytes 589832 | tf_op jit(solution)/shard_map/ppermute | solution.py:37
  14.8 5.7 %collective-permute-start.6 = (bf16[96,1024]{1,0:T(8,128)(2,1)S(1)}, bf16[96,1024]{1,0:T(8,128)(2,1)S(1)}, u32[]{:S(2)}, u32[]{:S(2)}) collective-permute-start(bf16[96,1024]{1,0:T(8,128)(2,1)S(1)} %slice.33), channel_id=1, source_target_pairs={{0,4},{1,5},{2,6},{3,7},{4,0},{5,1},{6,2},{7,3},{8,12},{9,13},{10,... | collective-permute-start | bytes 589832 | tf_op jit(solution)/shard_map/ppermute | solution.py:37
  22.0 1.3 copy-start.2
  22.0 1.4 copy-start.3
  22.0 8.4 %collective-permute-start.7 = (bf16[4,192,1024]{2,1,0:T(8,128)(2,1)}, bf16[4,192,1024]{2,1,0:T(8,128)(2,1)}, u32[]{:S(2)}, u32[]{:S(2)}) collective-permute-start(bf16[4,192,1024]{2,1,0:T(8,128)(2,1)} %pad_maximum_fusion), channel_id=1, source_target_pairs={{0,1},{1,0},{2,3},{3,2},{4,5},{5,4},{6,7},{7,6},{8,9},{9,8},{10,11... | collective-permute-start | bytes 4718600 | tf_op jit(solution)/shard_map/ppermute | solution.py:37
  24.3 14.2 %collective-permute-start = (f32[256,384]{1,0:T(8,128)}, f32[256,384]{1,0:T(8,128)}, u32[]{:S(2)}, u32[]{:S(2)}) collective-permute-start(f32[256,384]{1,0:T(8,128)} %get-tuple-element.17), channel_id=1, source_target_pairs={{0,8},{8,16},{16,24},{24,0},{1,9},{9,17},{17,25},{25,1},{2,10},{10... | collective-permute-start | bytes 1179656 | tf_op jit(solution)/shard_map/ppermute | solution.py:144
  25.9 29.0 %collective-permute-start.1 = (f32[256,384]{1,0:T(8,128)}, f32[256,384]{1,0:T(8,128)}, u32[]{:S(2)}, u32[]{:S(2)}) collective-permute-start(f32[256,384]{1,0:T(8,128)} %get-tuple-element.17), channel_id=1, source_target_pairs={{0,16},{8,24},{16,0},{24,8},{1,17},{9,25},{17,1},{25,9},{2,18},{10... | collective-permute-start | bytes 1179656 | tf_op jit(solution)/shard_map/ppermute | solution.py:144
  28.5 26.4 %collective-permute-start.2 = (f32[256,384]{1,0:T(8,128)}, f32[256,384]{1,0:T(8,128)}, u32[]{:S(2)}, u32[]{:S(2)}) collective-permute-start(f32[256,384]{1,0:T(8,128)} %get-tuple-element.17), channel_id=1, source_target_pairs={{0,24},{8,0},{16,8},{24,16},{1,25},{9,1},{17,9},{25,17},{2,26},{10... | collective-permute-start | bytes 1179656 | tf_op jit(solution)/shard_map/ppermute | solution.py:144
  30.4 4.2 %copy-start.10 = (bf16[1,1024,384]{2,1,0:T(8,128)(2,1)S(1)}, bf16[1,1024,384]{2,1,0:T(8,128)(2,1)}, u32[]{:S(2)}) copy-start(bf16[1,1024,384]{2,1,0:T(8,128)(2,1)} %param.15) | copy-start | bytes 2359300
  34.6 20.2 %copy-start.9 = (f32[384,32]{0,1:T(8,128)S(1)}, f32[384,32]{0,1:T(8,128)}, u32[]{:S(2)}) copy-start(f32[384,32]{0,1:T(8,128)} %param.16) | copy-start | bytes 147460
  56.5 1.4 collective-permute-start.8
  57.9 5.6 %collective-permute-start.9 = (f32[32,1024]{1,0:T(8,128)S(1)}, f32[32,1024]{1,0:T(8,128)S(1)}, u32[]{:S(2)}, u32[]{:S(2)}) collective-permute-start(f32[32,1024]{1,0:T(8,128)S(1)} %add.152), channel_id=1, source_target_pairs={{0,2},{1,3},{2,0},{3,1},{4,6},{5,7},{6,4},{7,5},{8,10},{9,11},{10,... | collective-permute-start | bytes 393224 | tf_op jit(solution)/shard_map/ppermute | solution.py:25
  63.5 5.0 %collective-permute-start.10 = (f32[32,1024]{1,0:T(8,128)S(1)}, f32[32,1024]{1,0:T(8,128)S(1)}, u32[]{:S(2)}, u32[]{:S(2)}) collective-permute-start(f32[32,1024]{1,0:T(8,128)S(1)} %add.153), channel_id=1, source_target_pairs={{0,4},{1,5},{2,6},{3,7},{4,0},{5,1},{6,2},{7,3},{8,12},{9,13},{10,... | collective-permute-start | bytes 393224 | tf_op jit(solution)/shard_map/ppermute | solution.py:25
  68.6 11.9 %collective-permute-start.11 = (f32[32,1024]{1,0:T(8,128)S(1)}, f32[32,1024]{1,0:T(8,128)S(1)}, u32[]{:S(2)}, u32[]{:S(2)}) collective-permute-start(f32[32,1024]{1,0:T(8,128)S(1)} %add.154), channel_id=1, source_target_pairs={{0,8},{1,9},{2,10},{3,11},{4,12},{5,13},{6,14},{7,15},{8,0},{9,1},... | collective-permute-start | bytes 393224 | tf_op jit(solution)/shard_map/ppermute | solution.py:25
  80.5 5.9 %copy-start.5 = (f32[32,1024]{1,0:T(8,128)}, f32[32,1024]{1,0:T(8,128)S(1)}, u32[]{:S(2)}) copy-start(f32[32,1024]{1,0:T(8,128)S(1)} %add.155) | copy-start | bytes 393220
  80.6 5.9 %collective-permute-start.12 = (f32[32,1024]{1,0:T(8,128)S(1)}, f32[32,1024]{1,0:T(8,128)S(1)}, u32[]{:S(2)}, u32[]{:S(2)}) collective-permute-start(f32[32,1024]{1,0:T(8,128)S(1)} %add.155), channel_id=1, source_target_pairs={{0,16},{1,17},{2,18},{3,19},{4,20},{5,21},{6,22},{7,23},{8,24},{9,... | collective-permute-start | bytes 393224 | tf_op jit(solution)/shard_map/ppermute | solution.py:25
  86.5 0.7 copy-start.8
  99.4 13.0 %copy-start.11 = (s32[1600]{0:T(1024)S(1)}, s32[1600]{0:T(1024)}, u32[]{:S(2)}) copy-start(s32[1600]{0:T(1024)} %param.21) | copy-start | bytes 19204
  99.5 12.9 %copy-start.12 = (s32[1536]{0:T(1024)S(1)}, s32[1536]{0:T(1024)}, u32[]{:S(2)}) copy-start(s32[1536]{0:T(1024)} %param.20) | copy-start | bytes 18436
  100.4 4.7 %collective-permute-start.13 = (f32[32,384]{1,0:T(8,128)S(1)}, f32[32,384]{1,0:T(8,128)S(1)}, u32[]{:S(2)}, u32[]{:S(2)}) collective-permute-start(f32[32,384]{1,0:T(8,128)S(1)} %fusion.31), channel_id=1, source_target_pairs={{0,8},{8,0},{16,24},{24,16},{1,9},{9,1},{17,25},{25,17},{2,10},{10... | collective-permute-start | bytes 147464 | tf_op jit(solution)/shard_map/ppermute | solution.py:25
  105.1 5.1 %collective-permute-start.14 = (f32[32,384]{1,0:T(8,128)S(1)}, f32[32,384]{1,0:T(8,128)S(1)}, u32[]{:S(2)}, u32[]{:S(2)}) collective-permute-start(f32[32,384]{1,0:T(8,128)S(1)} %add.157), channel_id=1, source_target_pairs={{0,16},{8,24},{16,0},{24,8},{1,17},{9,25},{17,1},{25,9},{2,18},{10... | collective-permute-start | bytes 147464 | tf_op jit(solution)/shard_map/ppermute | solution.py:25
  112.4 1.7 collective-permute-start.15
  115.1 5.6 %collective-permute-start.16 = (f32[32,1024]{1,0:T(8,128)S(1)}, f32[32,1024]{1,0:T(8,128)S(1)}, u32[]{:S(2)}, u32[]{:S(2)}) collective-permute-start(f32[32,1024]{1,0:T(8,128)S(1)} %add.159), channel_id=1, source_target_pairs={{0,2},{1,3},{2,0},{3,1},{4,6},{5,7},{6,4},{7,5},{8,10},{9,11},{10,... | collective-permute-start | bytes 393224 | tf_op jit(solution)/shard_map/ppermute | solution.py:25
  120.4 1.9 %copy-start.6 = (f32[1600,128]{1,0:T(8,128)}, f32[1600,128]{1,0:T(8,128)S(1)}, u32[]{:S(2)}) copy-start(f32[1600,128]{1,0:T(8,128)S(1)} %fusion) | copy-start | bytes 2457604
  120.7 7.3 %collective-permute-start.17 = (f32[32,1024]{1,0:T(8,128)S(1)}, f32[32,1024]{1,0:T(8,128)S(1)}, u32[]{:S(2)}, u32[]{:S(2)}) collective-permute-start(f32[32,1024]{1,0:T(8,128)S(1)} %add.160), channel_id=1, source_target_pairs={{0,4},{1,5},{2,6},{3,7},{4,0},{5,1},{6,2},{7,3},{8,12},{9,13},{10,... | collective-permute-start | bytes 393224 | tf_op jit(solution)/shard_map/ppermute | solution.py:25
  123.1 21.4 %collective-permute-start.22 = (f32[400,128]{1,0:T(8,128)}, f32[400,128]{1,0:T(8,128)}, u32[]{:S(2)}, u32[]{:S(2)}) collective-permute-start(f32[400,128]{1,0:T(8,128)} %get-tuple-element.22), channel_id=1, source_target_pairs={{0,8},{8,16},{16,24},{24,0},{1,9},{9,17},{17,25},{25,1},{2,10},{10... | collective-permute-start | bytes 614408 | tf_op jit(solution)/shard_map/ppermute | solution.py:80
  125.0 19.5 %collective-permute-start.23 = (f32[400,128]{1,0:T(8,128)}, f32[400,128]{1,0:T(8,128)}, u32[]{:S(2)}, u32[]{:S(2)}) collective-permute-start(f32[400,128]{1,0:T(8,128)} %get-tuple-element.24), channel_id=1, source_target_pairs={{0,16},{8,24},{16,0},{24,8},{1,17},{9,25},{17,1},{25,9},{2,18},{10... | collective-permute-start | bytes 614408 | tf_op jit(solution)/shard_map/ppermute | solution.py:80
  127.1 17.4 %collective-permute-start.24 = (f32[400,128]{1,0:T(8,128)}, f32[400,128]{1,0:T(8,128)}, u32[]{:S(2)}, u32[]{:S(2)}) collective-permute-start(f32[400,128]{1,0:T(8,128)} %get-tuple-element.23), channel_id=1, source_target_pairs={{0,24},{8,0},{16,8},{24,16},{1,25},{9,1},{17,9},{25,17},{2,26},{10... | collective-permute-start | bytes 614408 | tf_op jit(solution)/shard_map/ppermute | solution.py:80
  128.7 14.2 %collective-permute-start.18 = (f32[32,1024]{1,0:T(8,128)}, f32[32,1024]{1,0:T(8,128)}, u32[]{:S(2)}, u32[]{:S(2)}) collective-permute-start(f32[32,1024]{1,0:T(8,128)} %add.161), channel_id=1, source_target_pairs={{0,8},{1,9},{2,10},{3,11},{4,12},{5,13},{6,14},{7,15},{8,0},{9,1},... | collective-permute-start | bytes 393224 | tf_op jit(solution)/shard_map/ppermute | solution.py:25
  143.8 7.4 %copy-start.4 = (f32[32,1024]{1,0:T(8,128)}, f32[32,1024]{1,0:T(8,128)S(1)}, u32[]{:S(2)}) copy-start(f32[32,1024]{1,0:T(8,128)S(1)} %add.162) | copy-start | bytes 393220
  143.8 7.4 %collective-permute-start.19 = (f32[32,1024]{1,0:T(8,128)S(1)}, f32[32,1024]{1,0:T(8,128)S(1)}, u32[]{:S(2)}, u32[]{:S(2)}) collective-permute-start(f32[32,1024]{1,0:T(8,128)S(1)} %add.162), channel_id=1, source_target_pairs={{0,16},{1,17},{2,18},{3,19},{4,20},{5,21},{6,22},{7,23},{8,24},{9,... | collective-permute-start | bytes 393224 | tf_op jit(solution)/shard_map/ppermute | solution.py:25
  151.3 0.7 copy-start.7
  165.1 4.2 %collective-permute-start.20 = (f32[32,384]{1,0:T(8,128)S(1)}, f32[32,384]{1,0:T(8,128)S(1)}, u32[]{:S(2)}, u32[]{:S(2)}) collective-permute-start(f32[32,384]{1,0:T(8,128)S(1)} %fusion.32), channel_id=1, source_target_pairs={{0,8},{8,0},{16,24},{24,16},{1,9},{9,1},{17,25},{25,17},{2,10},{10... | collective-permute-start | bytes 147464 | tf_op jit(solution)/shard_map/ppermute | solution.py:25
  169.3 5.1 %collective-permute-start.21 = (f32[32,384]{1,0:T(8,128)S(1)}, f32[32,384]{1,0:T(8,128)S(1)}, u32[]{:S(2)}, u32[]{:S(2)}) collective-permute-start(f32[32,384]{1,0:T(8,128)S(1)} %add.164), channel_id=1, source_target_pairs={{0,16},{8,24},{16,0},{24,8},{1,17},{9,25},{17,1},{25,9},{2,18},{10... | collective-permute-start | bytes 147464 | tf_op jit(solution)/shard_map/ppermute | solution.py:25

commit v6 on v4

--- a/solution.py
+++ b/solution.py
@@ -19,11 +19,19 @@
         count *= lax.axis_size(axis)
     if count & (count - 1):
         return lax.psum(value, axes)
+
+    def exchange(stride):
+        return lax.ppermute(value, axes, [(i, i ^ stride) for i in range(count)])
+
+    bits = count.bit_length() - 1
     stride = 1
+    if bits % 2:
+        value = value + exchange(1)
+        stride = 2
     while stride < count:
-        pairs = [(i, i ^ stride) for i in range(count)]
-        value = value + lax.ppermute(value, axes, pairs)
-        stride *= 2
+        low, high = stride, 2 * stride
+        value = (value + exchange(low)) + (exchange(high) + exchange(low ^ high))
+        stride *= 4
     return value
 
 

time: 149 us -> 155 us (1.040)
  starting transfers between devices: 30.7 us -> 38.6 us
  waiting for transfers between devices: 55.7 us -> 53.9 us
    ppermute x14 -> x20, starting transfers between devices: 18.4 us -> 26.9 us  [exchange(): return lax.ppermute(value, axes, [(i, i ^ stride) for i in range(count)])]
    ppermute x14 -> x20, waiting for transfers between devices: 40.6 us -> 38.7 us  [exchange(): return lax.ppermute(value, axes, [(i, i ^ stride) for i in range(count)])]
  transfers between devices with their start and end apart: 22 -> 28, of which waited for: 17 -> 19; matrix products, arithmetic and copies ran while one was open for 13% -> 12% of each run, Pallas kernels for 0% -> 0%
where the time goes in v6:
time: 155 us
  waiting for transfers between devices  53.9 us (35%)
  starting transfers between devices  38.6 us (25%)
  other arithmetic  21.1 us (14%)
  blocking collectives  17.9 us (12%)
  matrix products  13.7 us (9%)
  local copies, waits for them, and re-layouts  8.36 us (5%)
    ppermute x20, waiting for transfers between devices, exchange(): return lax.ppermute(value, axes, [(i, i ^ stride) for i in range(count)])  38.7 us
    ppermute x20, starting transfers between devices, exchange(): return lax.ppermute(value, axes, [(i, i ^ stride) for i in range(count)])  26.9 us
    all_gather x1, blocking collectives, shards(): lax.all_gather(master_new.astype(jnp.bfloat16), 'rep', axis=0, tiled=True)  17.9 us
    ppermute x5, waiting for transfers between devices, exchange(): return lax.ppermute(value, axis, [(i, i ^ stride) for i in range(count)])  15.1 us
    ppermute x5, starting transfers between devices, exchange(): return lax.ppermute(value, axis, [(i, i ^ stride) for i in range(count)])  7.89 us
    another operation x6, other arithmetic, shards(): factor_low = jnp.linalg.cholesky(gram_matrix)  7.19 us
    another operation x4, other arithmetic, shards(): jax.scipy.linalg.solve_triangular(factor_low, left_rows, lower=True)  6.17 us
    dynamic_update_slice x8, local copies, waits for them, and re-layouts, gather_rows(): lax.dynamic_update_slice_in_dim(gathered, piece, (me ^ offset) * rows, 0)  4.26 us
  transfers between devices with their start and end apart: 28, of which 19 were waited for; matrix products, arithmetic and copies ran while one was open for 12% of the time, Pallas kernels for 0%

profile of v6, /device:TPU:0, one launch (start us, length us, event | category | flops | bytes accessed | tf_op | source)
XLA Modules:
  0.0 154.6 jit_solution(6418229884309569752)
XLA Ops:
  0.7 3.0 %collective-permute-start.1 = (bf16[192,1024]{1,0:T(8,128)(2,1)}, bf16[192,1024]{1,0:T(8,128)(2,1)S(1)}, u32[]{:S(2)}, u32[]{:S(2)}) collective-permute-start(bf16[192,1024]{1,0:T(8,128)(2,1)} %param.13), channel_id=1, source_target_pairs={{0,4},{1,5},{2,6},{3,7},{4,0},{5,1},{6,2},{7,3},{8,12},{9,13},{10,... | collective-permute-start | bytes 1179656 | tf_op jit(solution)/shard_map/ppermute | solution.py:45
  3.7 1.5 collective-permute-start
  5.2 7.8 %collective-permute-done.1 = bf16[192,1024]{1,0:T(8,128)(2,1)S(1)} collective-permute-done((bf16[192,1024]{1,0:T(8,128)(2,1)}, bf16[192,1024]{1,0:T(8,128)(2,1)S(1)}, u32[]{:S(2)}, u32[]{:S(2)}) %collective-permute-start.1) | collective-permute-done | bytes 393248 | tf_op jit(solution)/shard_map/ppermute | solution.py:45
  13.0 1.8 %collective-permute-start.2 = (bf16[96,1024]{1,0:T(8,128)(2,1)S(1)}, bf16[96,1024]{1,0:T(8,128)(2,1)S(1)}, u32[]{:S(2)}, u32[]{:S(2)}) collective-permute-start(bf16[96,1024]{1,0:T(8,128)(2,1)S(1)} %slice.32), channel_id=1, source_target_pairs={{0,2},{1,3},{2,0},{3,1},{4,6},{5,7},{6,4},{7,5},{8,10},{9,11},{10,... | collective-permute-start | bytes 589832 | tf_op jit(solution)/shard_map/ppermute | solution.py:45
  14.8 1.6 %collective-permute-start.3 = (bf16[96,1024]{1,0:T(8,128)(2,1)S(1)}, bf16[96,1024]{1,0:T(8,128)(2,1)S(1)}, u32[]{:S(2)}, u32[]{:S(2)}) collective-permute-start(bf16[96,1024]{1,0:T(8,128)(2,1)S(1)} %slice.33), channel_id=1, source_target_pairs={{0,4},{1,5},{2,6},{3,7},{4,0},{5,1},{6,2},{7,3},{8,12},{9,13},{10,... | collective-permute-start | bytes 589832 | tf_op jit(solution)/shard_map/ppermute | solution.py:45
  16.4 2.8 %collective-permute-done.2 = bf16[96,1024]{1,0:T(8,128)(2,1)S(1)} collective-permute-done((bf16[96,1024]{1,0:T(8,128)(2,1)S(1)}, bf16[96,1024]{1,0:T(8,128)(2,1)S(1)}, u32[]{:S(2)}, u32[]{:S(2)}) %collective-permute-start.2) | collective-permute-done | bytes 196640 | tf_op jit(solution)/shard_map/ppermute | solution.py:45
  19.2 1.4 collective-permute-done.3
  20.6 1.4 pad_maximum_fusion
  22.6 3.2 %collective-permute-done.4 = bf16[4,192,1024]{2,1,0:T(8,128)(2,1)} collective-permute-done((bf16[4,192,1024]{2,1,0:T(8,128)(2,1)}, bf16[4,192,1024]{2,1,0:T(8,128)(2,1)}, u32[]{:S(2)}, u32[]{:S(2)}) %collective-permute-start.4) | collective-permute-done | bytes 1572896 | tf_op jit(solution)/shard_map/ppermute | solution.py:45
  29.9 1.9 %convert_add_fusion = f32[1024,384]{1,0:T(8,128)S(1)} fusion(bf16[1536,1024]{1,0:T(8,128)(2,1)S(1)} %fusion.3, bf16[1536,384]{1,0:T(8,128)(2,1)S(1)} %copy-done, bf16[1,1024,384]{2,1,0:T(8,128)(2,1)S(1)} %copy-done.8), kind=kOutput, calls=%fused_computation.6 | convolution fusion | flops 1208745984 | bytes 6684672 | tf_op jit(solution)/shard_map/dot_general | solution.py:138
  31.8 1.6 %convolution_bitcast_fusion = f32[32,1024]{1,0:T(8,128)S(1)} fusion(f32[1024,384]{1,0:T(8,128)S(1)} %convert_add_fusion, f32[384,32]{0,1:T(8,128)S(1)} %copy-done.7), kind=kOutput, calls=%fused_computation.8 | convolution fusion | flops 150994944 | bytes 1753088 | tf_op jit(solution)/shard_map/dot_general | solution.py:148
  33.6 1.2 collective-permute-done.5
  34.8 1.2 collective-permute-start.6
  36.9 1.4 collective-permute-start.8
  38.4 2.8 %collective-permute-done.6 = f32[32,1024]{1,0:T(8,128)S(1)} collective-permute-done((f32[32,1024]{1,0:T(8,128)S(1)}, f32[32,1024]{1,0:T(8,128)S(1)}, u32[]{:S(2)}, u32[]{:S(2)}) %collective-permute-start.6) | collective-permute-done | bytes 131104 | tf_op jit(solution)/shard_map/ppermute | solution.py:24
  41.1 1.4 collective-permute-done.7
  42.5 1.6 %collective-permute-done.8 = f32[32,1024]{1,0:T(8,128)S(1)} collective-permute-done((f32[32,1024]{1,0:T(8,128)S(1)}, f32[32,1024]{1,0:T(8,128)S(1)}, u32[]{:S(2)}, u32[]{:S(2)}) %collective-permute-start.8) | collective-permute-done | bytes 131104 | tf_op jit(solution)/shard_map/ppermute | solution.py:24
  44.2 2.7 %collective-permute-start.10 = (f32[32,1024]{1,0:T(8,128)S(1)}, f32[32,1024]{1,0:T(8,128)S(1)}, u32[]{:S(2)}, u32[]{:S(2)}) collective-permute-start(f32[32,1024]{1,0:T(8,128)S(1)} %add_add_fusion.1), channel_id=1, source_target_pairs={{0,16},{1,17},{2,18},{3,19},{4,20},{5,21},{6,22},{7,23},{8,24},{9,... | collective-permute-start | bytes 393224 | tf_op jit(solution)/shard_map/ppermute | solution.py:24
  46.9 1.3 collective-permute-start.11
  48.4 8.2 %collective-permute-done.10 = f32[32,1024]{1,0:T(8,128)S(1)} collective-permute-done((f32[32,1024]{1,0:T(8,128)S(1)}, f32[32,1024]{1,0:T(8,128)S(1)}, u32[]{:S(2)}, u32[]{:S(2)}) %collective-permute-start.10) | collective-permute-done | bytes 131104 | tf_op jit(solution)/shard_map/ppermute | solution.py:24
  57.3 2.9 %cholesky.44 = f32[32,32]{1,0:T(8,128)S(1)} custom-call(f32[32,32]{1,0:T(8,128)S(1)} %fusion.20), custom_call_target="Cholesky" | custom-call | tf_op jit(solution)/shard_map/jit(cholesky)/cholesky | solution.py:153
  61.5 2.4 %custom-call.6 = f32[1,32,32]{1,2,0:T(8,128)S(1)} custom-call(f32[1,32,32]{2,1,0:T(8,128)S(1)} %fusion.13), custom_call_target="InvertDiagBlocksLowerTriangular" | custom-call | tf_op jit(solution)/shard_map/jit(_solve_triangular)/triangular_solve | solution.py:154
  65.3 2.2 %collective-permute-start.12 = (f32[32,384]{1,0:T(8,128)S(1)}, f32[32,384]{1,0:T(8,128)S(1)}, u32[]{:S(2)}, u32[]{:S(2)}) collective-permute-start(f32[32,384]{1,0:T(8,128)S(1)} %fusion.26), channel_id=1, source_target_pairs={{0,8},{8,0},{16,24},{24,16},{1,9},{9,1},{17,25},{25,17},{2,10},{10... | collective-permute-start | bytes 147464 | tf_op jit(solution)/shard_map/ppermute | solution.py:24
  67.4 2.0 %collective-permute-start.13 = (f32[32,384]{1,0:T(8,128)S(1)}, f32[32,384]{1,0:T(8,128)S(1)}, u32[]{:S(2)}, u32[]{:S(2)}) collective-permute-start(f32[32,384]{1,0:T(8,128)S(1)} %fusion.26), channel_id=1, source_target_pairs={{0,16},{8,24},{16,0},{24,8},{1,17},{9,25},{17,1},{25,9},{2,18},{10... | collective-permute-start | bytes 147464 | tf_op jit(solution)/shard_map/ppermute | solution.py:24
  69.4 1.4 collective-permute-start.14
  70.8 2.7 %collective-permute-done.13 = f32[32,384]{1,0:T(8,128)S(1)} collective-permute-done((f32[32,384]{1,0:T(8,128)S(1)}, f32[32,384]{1,0:T(8,128)S(1)}, u32[]{:S(2)}, u32[]{:S(2)}) %collective-permute-start.13) | collective-permute-done | bytes 49184 | tf_op jit(solution)/shard_map/ppermute | solution.py:24
  73.6 1.9 %collective-permute-done.14 = f32[32,384]{1,0:T(8,128)S(1)} collective-permute-done((f32[32,384]{1,0:T(8,128)S(1)}, f32[32,384]{1,0:T(8,128)S(1)}, u32[]{:S(2)}, u32[]{:S(2)}) %collective-permute-start.14) | collective-permute-done | bytes 49184 | tf_op jit(solution)/shard_map/ppermute | solution.py:24
  75.4 1.6 %fusion.7 = f32[32,1024]{1,0:T(8,128)S(1)} fusion(f32[1024,384]{1,0:T(8,128)S(1)} %convert_add_fusion, f32[32,384]{1,0:T(8,128)S(1)} %collective-permute-done.13, f32[32,384]{1,0:T(8,128)S(1)} %collective-permute-done.14, f32[32,384]{1,0:T(8,128)S(1)} %fusion.26, f32[32,384]{1,0:T(8,128)S(1)} %collective-permute-done.12), kind=kOutput, calls=%fused_computation.26 | convolution fusion | flops 151044096 | bytes 1900544 | tf_op jit(solution)/shard_map/dot_general | solution.py:148
  77.1 1.3 collective-permute-done.15
  78.9 1.4 collective-permute-start.17
  80.2 1.8 %collective-permute-start.18 = (f32[32,1024]{1,0:T(8,128)S(1)}, f32[32,1024]{1,0:T(8,128)S(1)}, u32[]{:S(2)}, u32[]{:S(2)}) collective-permute-start(f32[32,1024]{1,0:T(8,128)S(1)} %add.161), channel_id=1, source_target_pairs={{0,6},{1,7},{2,4},{3,5},{4,2},{5,3},{6,0},{7,1},{8,14},{9,15},{10,... | collective-permute-start | bytes 393224 | tf_op jit(solution)/shard_map/ppermute | solution.py:24
  83.1 1.7 %collective-permute-done.16 = f32[32,1024]{1,0:T(8,128)S(1)} collective-permute-done((f32[32,1024]{1,0:T(8,128)S(1)}, f32[32,1024]{1,0:T(8,128)S(1)}, u32[]{:S(2)}, u32[]{:S(2)}) %collective-permute-start.16) | collective-permute-done | bytes 131104 | tf_op jit(solution)/shard_map/ppermute | solution.py:24
  85.0 2.0 %collective-permute-done.18 = f32[32,1024]{1,0:T(8,128)S(1)} collective-permute-done((f32[32,1024]{1,0:T(8,128)S(1)}, f32[32,1024]{1,0:T(8,128)S(1)}, u32[]{:S(2)}, u32[]{:S(2)}) %collective-permute-start.18) | collective-permute-done | bytes 131104 | tf_op jit(solution)/shard_map/ppermute | solution.py:24
  87.8 4.2 %fusion = f32[1600,128]{1,0:T(8,128)} fusion(bf16[1536,128]{1,0:T(8,128)(2,1)S(1)} %copy-done.9, s32[1536]{0:T(1024)S(1)} %select_reduce_fusion), kind=kOutput, calls=%fused_computation.1 | convolution fusion | flops 631603200 | bytes 1218560 | tf_op jit(solution)/shard_map/dot_general | solution.py:78
  92.0 1.9 %collective-permute-start.20 = (f32[32,1024]{1,0:T(8,128)S(1)}, f32[32,1024]{1,0:T(8,128)S(1)}, u32[]{:S(2)}, u32[]{:S(2)}) collective-permute-start(f32[32,1024]{1,0:T(8,128)S(1)} %add_add_fusion), channel_id=1, source_target_pairs={{0,16},{1,17},{2,18},{3,19},{4,20},{5,21},{6,22},{7,23},{8,24},{9,... | collective-permute-start | bytes 393224 | tf_op jit(solution)/shard_map/ppermute | solution.py:24
  93.8 1.8 %collective-permute-start.21 = (f32[32,1024]{1,0:T(8,128)S(1)}, f32[32,1024]{1,0:T(8,128)}, u32[]{:S(2)}, u32[]{:S(2)}) collective-permute-start(f32[32,1024]{1,0:T(8,128)S(1)} %add_add_fusion), channel_id=1, source_target_pairs={{0,24},{1,25},{2,26},{3,27},{4,28},{5,29},{6,30},{7,31},{8,16},{9,... | collective-permute-start | bytes 393224 | tf_op jit(solution)/shard_map/ppermute | solution.py:24
  95.6 1.9 %constant_dynamic-slice_fusion.1 = (f32[400,128]{1,0:T(8,128)}, f32[400,128]{1,0:T(8,128)S(1)}, f32[400,128]{1,0:T(8,128)}) fusion(f32[1600,128]{1,0:T(8,128)} %fusion, s32[]{:T(128)S(6)} %select_n.73, s32[]{:T(128)S(6)} %select_n.77, s32[]{:T(128)S(6)} %select_n.75), kind=kLoop, calls=%fused_computation.52 | loop fusion | bytes 1228812 | tf_op jit(solution)/shard_map/dynamic_slice | solution.py:84
  97.5 2.6 %collective-permute-start.26 = (f32[400,128]{1,0:T(8,128)}, f32[400,128]{1,0:T(8,128)}, u32[]{:S(2)}, u32[]{:S(2)}) collective-permute-start(f32[400,128]{1,0:T(8,128)} %get-tuple-element.13), channel_id=1, source_target_pairs={{0,16},{8,24},{16,0},{24,8},{1,17},{9,25},{17,1},{25,9},{2,18},{10... | collective-permute-start | bytes 614408 | tf_op jit(solution)/shard_map/ppermute | solution.py:88
  100.1 1.2 collective-permute-start.27
  101.4 11.3 %collective-permute-done.20 = f32[32,1024]{1,0:T(8,128)S(1)} collective-permute-done((f32[32,1024]{1,0:T(8,128)S(1)}, f32[32,1024]{1,0:T(8,128)S(1)}, u32[]{:S(2)}, u32[]{:S(2)}) %collective-permute-start.20) | collective-permute-done | bytes 131104 | tf_op jit(solution)/shard_map/ppermute | solution.py:24
  114.6 2.9 %cholesky.55 = f32[32,32]{1,0:T(8,128)S(1)} custom-call(f32[32,32]{1,0:T(8,128)S(1)} %fusion.17), custom_call_target="Cholesky" | custom-call | tf_op jit(solution)/shard_map/jit(cholesky)/cholesky | solution.py:153
  118.9 2.4 %custom-call.7 = f32[1,32,32]{1,2,0:T(8,128)S(1)} custom-call(f32[1,32,32]{2,1,0:T(8,128)S(1)} %fusion.14), custom_call_target="InvertDiagBlocksLowerTriangular" | custom-call | tf_op jit(solution)/shard_map/jit(_solve_triangular)/triangular_solve | solution.py:154
  122.6 2.9 %collective-permute-start.22 = (f32[32,384]{1,0:T(8,128)S(1)}, f32[32,384]{1,0:T(8,128)S(1)}, u32[]{:S(2)}, u32[]{:S(2)}) collective-permute-start(f32[32,384]{1,0:T(8,128)S(1)} %fusion.28), channel_id=1, source_target_pairs={{0,8},{8,0},{16,24},{24,16},{1,9},{9,1},{17,25},{25,17},{2,10},{10... | collective-permute-start | bytes 147464 | tf_op jit(solution)/shard_map/ppermute | solution.py:24
  126.1 1.8 %collective-permute-start.24 = (f32[32,384]{1,0:T(8,128)S(1)}, f32[32,384]{1,0:T(8,128)S(1)}, u32[]{:S(2)}, u32[]{:S(2)}) collective-permute-start(f32[32,384]{1,0:T(8,128)S(1)} %fusion.28), channel_id=1, source_target_pairs={{0,24},{8,16},{16,8},{24,0},{1,25},{9,17},{17,9},{25,1},{2,26},{10... | collective-permute-start | bytes 147464 | tf_op jit(solution)/shard_map/ppermute | solution.py:24
  127.9 2.0 %multiply_subtract_fusion.1 = f32[400,128]{1,0:T(8,128)} fusion(f32[400,128]{1,0:T(8,128)S(1)} %copy-done.4, f32[400,128]{1,0:T(8,128)} %collective-permute-done.27, f32[400,128]{1,0:T(8,128)} %collective-permute-done.26, f32[400,128]{1,0:T(8,128)} %collective-permute-done.25, f32[1600,128]{1,0:T(8,128)} %fusion, s32[]{:T(128)S(6)} %select_n.71), kind=kLoop, calls=%fused_computation.20 | loop fusion | flops 256000 | bytes 1228804 | tf_op jit(solution)/shard_map/sub | solution.py:89
  129.9 1.2 collective-permute-done.23
  132.2 1.5 fusion.29
  135.8 17.9 %all_gather.3 = bf16[1024,384]{1,0:T(8,128)(2,1)S(1)} all-gather(bf16[256,384]{1,0:T(8,128)(2,1)S(1)} %get-tuple-element.8), channel_id=1, replica_groups=mesh['rep'=4,'tp'=8] {'rep'}, dimensions={0}, use_global_device_ids=true | all-gather | bytes 983040 | tf_op jit(solution)/shard_map/all_gather | solution.py:168
  (85 shorter events, 21.0 us)
Async XLA Ops:
  0.6 29.2 %copy-start = (bf16[1536,384]{1,0:T(8,128)(2,1)S(1)}, bf16[1536,384]{1,0:T(8,128)(2,1)}, u32[]{:S(2)}) copy-start(bf16[1536,384]{1,0:T(8,128)(2,1)} %param.14) | copy-start | bytes 3538948
  0.6 19.9 %copy-start.1 = (bf16[192,1024]{1,0:T(8,128)(2,1)S(1)}, bf16[192,1024]{1,0:T(8,128)(2,1)}, u32[]{:S(2)}) copy-start(bf16[192,1024]{1,0:T(8,128)(2,1)} %param.13) | copy-start | bytes 1179652
  0.7 12.4 %collective-permute-start.1 = (bf16[192,1024]{1,0:T(8,128)(2,1)}, bf16[192,1024]{1,0:T(8,128)(2,1)S(1)}, u32[]{:S(2)}, u32[]{:S(2)}) collective-permute-start(bf16[192,1024]{1,0:T(8,128)(2,1)} %param.13), channel_id=1, source_target_pairs={{0,4},{1,5},{2,6},{3,7},{4,0},{5,1},{6,2},{7,3},{8,12},{9,13},{10,... | collective-permute-start | bytes 1179656 | tf_op jit(solution)/shard_map/ppermute | solution.py:45
  3.7 11.1 %collective-permute-start = (bf16[192,1024]{1,0:T(8,128)(2,1)}, bf16[192,1024]{1,0:T(8,128)(2,1)S(1)}, u32[]{:S(2)}, u32[]{:S(2)}) collective-permute-start(bf16[192,1024]{1,0:T(8,128)(2,1)} %param.13), channel_id=1, source_target_pairs={{0,2},{1,3},{2,0},{3,1},{4,6},{5,7},{6,4},{7,5},{8,10},{9,11},{10,... | collective-permute-start | bytes 1179656 | tf_op jit(solution)/shard_map/ppermute | solution.py:45
  13.0 6.2 %collective-permute-start.2 = (bf16[96,1024]{1,0:T(8,128)(2,1)S(1)}, bf16[96,1024]{1,0:T(8,128)(2,1)S(1)}, u32[]{:S(2)}, u32[]{:S(2)}) collective-permute-start(bf16[96,1024]{1,0:T(8,128)(2,1)S(1)} %slice.32), channel_id=1, source_target_pairs={{0,2},{1,3},{2,0},{3,1},{4,6},{5,7},{6,4},{7,5},{8,10},{9,11},{10,... | collective-permute-start | bytes 589832 | tf_op jit(solution)/shard_map/ppermute | solution.py:45
  14.8 5.7 %collective-permute-start.3 = (bf16[96,1024]{1,0:T(8,128)(2,1)S(1)}, bf16[96,1024]{1,0:T(8,128)(2,1)S(1)}, u32[]{:S(2)}, u32[]{:S(2)}) collective-permute-start(bf16[96,1024]{1,0:T(8,128)(2,1)S(1)} %slice.33), channel_id=1, source_target_pairs={{0,4},{1,5},{2,6},{3,7},{4,0},{5,1},{6,2},{7,3},{8,12},{9,13},{10,... | collective-permute-start | bytes 589832 | tf_op jit(solution)/shard_map/ppermute | solution.py:45
  22.0 3.8 %collective-permute-start.4 = (bf16[4,192,1024]{2,1,0:T(8,128)(2,1)}, bf16[4,192,1024]{2,1,0:T(8,128)(2,1)}, u32[]{:S(2)}, u32[]{:S(2)}) collective-permute-start(bf16[4,192,1024]{2,1,0:T(8,128)(2,1)} %pad_maximum_fusion), channel_id=1, source_target_pairs={{0,1},{1,0},{2,3},{3,2},{4,5},{5,4},{6,7},{7,6},{8,9},{9,8},{10,11... | collective-permute-start | bytes 4718600 | tf_op jit(solution)/shard_map/ppermute | solution.py:45
  22.5 7.3 %copy-start.8 = (bf16[1,1024,384]{2,1,0:T(8,128)(2,1)S(1)}, bf16[1,1024,384]{2,1,0:T(8,128)(2,1)}, u32[]{:S(2)}) copy-start(bf16[1,1024,384]{2,1,0:T(8,128)(2,1)} %param.15) | copy-start | bytes 2359300
  29.9 1.9 %copy-start.7 = (f32[384,32]{0,1:T(8,128)S(1)}, f32[384,32]{0,1:T(8,128)}, u32[]{:S(2)}) copy-start(f32[384,32]{0,1:T(8,128)} %param.16) | copy-start | bytes 147460
  33.4 1.4 collective-permute-start.5
  34.8 6.3 %collective-permute-start.6 = (f32[32,1024]{1,0:T(8,128)S(1)}, f32[32,1024]{1,0:T(8,128)S(1)}, u32[]{:S(2)}, u32[]{:S(2)}) collective-permute-start(f32[32,1024]{1,0:T(8,128)S(1)} %add.151), channel_id=1, source_target_pairs={{0,2},{1,3},{2,0},{3,1},{4,6},{5,7},{6,4},{7,5},{8,10},{9,11},{10,... | collective-permute-start | bytes 393224 | tf_op jit(solution)/shard_map/ppermute | solution.py:24
  36.0 6.5 %collective-permute-start.7 = (f32[32,1024]{1,0:T(8,128)S(1)}, f32[32,1024]{1,0:T(8,128)S(1)}, u32[]{:S(2)}, u32[]{:S(2)}) collective-permute-start(f32[32,1024]{1,0:T(8,128)S(1)} %add.151), channel_id=1, source_target_pairs={{0,4},{1,5},{2,6},{3,7},{4,0},{5,1},{6,2},{7,3},{8,12},{9,13},{10,... | collective-permute-start | bytes 393224 | tf_op jit(solution)/shard_map/ppermute | solution.py:24
  36.9 7.3 %collective-permute-start.8 = (f32[32,1024]{1,0:T(8,128)S(1)}, f32[32,1024]{1,0:T(8,128)S(1)}, u32[]{:S(2)}, u32[]{:S(2)}) collective-permute-start(f32[32,1024]{1,0:T(8,128)S(1)} %add.151), channel_id=1, source_target_pairs={{0,6},{1,7},{2,4},{3,5},{4,2},{5,3},{6,0},{7,1},{8,14},{9,15},{10,... | collective-permute-start | bytes 393224 | tf_op jit(solution)/shard_map/ppermute | solution.py:24
  44.2 12.5 %collective-permute-start.10 = (f32[32,1024]{1,0:T(8,128)S(1)}, f32[32,1024]{1,0:T(8,128)S(1)}, u32[]{:S(2)}, u32[]{:S(2)}) collective-permute-start(f32[32,1024]{1,0:T(8,128)S(1)} %add_add_fusion.1), channel_id=1, source_target_pairs={{0,16},{1,17},{2,18},{3,19},{4,20},{5,21},{6,22},{7,23},{8,24},{9,... | collective-permute-start | bytes 393224 | tf_op jit(solution)/shard_map/ppermute | solution.py:24
  46.9 9.8 %collective-permute-start.11 = (f32[32,1024]{1,0:T(8,128)S(1)}, f32[32,1024]{1,0:T(8,128)S(1)}, u32[]{:S(2)}, u32[]{:S(2)}) collective-permute-start(f32[32,1024]{1,0:T(8,128)S(1)} %add_add_fusion.1), channel_id=1, source_target_pairs={{0,24},{1,25},{2,26},{3,27},{4,28},{5,29},{6,30},{7,31},{8,16},{9,... | collective-permute-start | bytes 393224 | tf_op jit(solution)/shard_map/ppermute | solution.py:24
  48.2 8.7 %collective-permute-start.9 = (f32[32,1024]{1,0:T(8,128)S(1)}, f32[32,1024]{1,0:T(8,128)S(1)}, u32[]{:S(2)}, u32[]{:S(2)}) collective-permute-start(f32[32,1024]{1,0:T(8,128)S(1)} %add_add_fusion.1), channel_id=1, source_target_pairs={{0,8},{1,9},{2,10},{3,11},{4,12},{5,13},{6,14},{7,15},{8,0},{9,1},... | collective-permute-start | bytes 393224 | tf_op jit(solution)/shard_map/ppermute | solution.py:24
  65.2 16.8 %copy-start.10 = (s32[1600]{0:T(1024)S(1)}, s32[1600]{0:T(1024)}, u32[]{:S(2)}) copy-start(s32[1600]{0:T(1024)} %param.21) | copy-start | bytes 19204
  65.3 16.8 %copy-start.11 = (s32[1536]{0:T(1024)S(1)}, s32[1536]{0:T(1024)}, u32[]{:S(2)}) copy-start(s32[1536]{0:T(1024)} %param.20) | copy-start | bytes 18436
  65.3 22.5 %copy-start.9 = (bf16[1536,128]{1,0:T(8,128)(2,1)S(1)}, bf16[1536,128]{1,0:T(8,128)(2,1)}, u32[]{:S(2)}) copy-start(bf16[1536,128]{1,0:T(8,128)(2,1)} %param.19) | copy-start | bytes 1179652
  65.3 5.5 %collective-permute-start.12 = (f32[32,384]{1,0:T(8,128)S(1)}, f32[32,384]{1,0:T(8,128)S(1)}, u32[]{:S(2)}, u32[]{:S(2)}) collective-permute-start(f32[32,384]{1,0:T(8,128)S(1)} %fusion.26), channel_id=1, source_target_pairs={{0,8},{8,0},{16,24},{24,16},{1,9},{9,1},{17,25},{25,17},{2,10},{10... | collective-permute-start | bytes 147464 | tf_op jit(solution)/shard_map/ppermute | solution.py:24
  67.4 6.1 %collective-permute-start.13 = (f32[32,384]{1,0:T(8,128)S(1)}, f32[32,384]{1,0:T(8,128)S(1)}, u32[]{:S(2)}, u32[]{:S(2)}) collective-permute-start(f32[32,384]{1,0:T(8,128)S(1)} %fusion.26), channel_id=1, source_target_pairs={{0,16},{8,24},{16,0},{24,8},{1,17},{9,25},{17,1},{25,9},{2,18},{10... | collective-permute-start | bytes 147464 | tf_op jit(solution)/shard_map/ppermute | solution.py:24
  69.4 6.0 %collective-permute-start.14 = (f32[32,384]{1,0:T(8,128)S(1)}, f32[32,384]{1,0:T(8,128)S(1)}, u32[]{:S(2)}, u32[]{:S(2)}) collective-permute-start(f32[32,384]{1,0:T(8,128)S(1)} %fusion.26), channel_id=1, source_target_pairs={{0,24},{8,16},{16,8},{24,0},{1,25},{9,17},{17,9},{25,1},{2,26},{10... | collective-permute-start | bytes 147464 | tf_op jit(solution)/shard_map/ppermute | solution.py:24
  77.0 1.4 collective-permute-start.15
  78.5 6.4 %collective-permute-start.16 = (f32[32,1024]{1,0:T(8,128)S(1)}, f32[32,1024]{1,0:T(8,128)S(1)}, u32[]{:S(2)}, u32[]{:S(2)}) collective-permute-start(f32[32,1024]{1,0:T(8,128)S(1)} %add.161), channel_id=1, source_target_pairs={{0,2},{1,3},{2,0},{3,1},{4,6},{5,7},{6,4},{7,5},{8,10},{9,11},{10,... | collective-permute-start | bytes 393224 | tf_op jit(solution)/shard_map/ppermute | solution.py:24
  78.9 6.1 %collective-permute-start.17 = (f32[32,1024]{1,0:T(8,128)S(1)}, f32[32,1024]{1,0:T(8,128)S(1)}, u32[]{:S(2)}, u32[]{:S(2)}) collective-permute-start(f32[32,1024]{1,0:T(8,128)S(1)} %add.161), channel_id=1, source_target_pairs={{0,4},{1,5},{2,6},{3,7},{4,0},{5,1},{6,2},{7,3},{8,12},{9,13},{10,... | collective-permute-start | bytes 393224 | tf_op jit(solution)/shard_map/ppermute | solution.py:24
  80.2 6.7 %collective-permute-start.18 = (f32[32,1024]{1,0:T(8,128)S(1)}, f32[32,1024]{1,0:T(8,128)S(1)}, u32[]{:S(2)}, u32[]{:S(2)}) collective-permute-start(f32[32,1024]{1,0:T(8,128)S(1)} %add.161), channel_id=1, source_target_pairs={{0,6},{1,7},{2,4},{3,5},{4,2},{5,3},{6,0},{7,1},{8,14},{9,15},{10,... | collective-permute-start | bytes 393224 | tf_op jit(solution)/shard_map/ppermute | solution.py:24
  87.0 13.1 %collective-permute-start.19 = (f32[32,1024]{1,0:T(8,128)S(1)}, f32[32,1024]{1,0:T(8,128)S(1)}, u32[]{:S(2)}, u32[]{:S(2)}) collective-permute-start(f32[32,1024]{1,0:T(8,128)S(1)} %add_add_fusion), channel_id=1, source_target_pairs={{0,8},{1,9},{2,10},{3,11},{4,12},{5,13},{6,14},{7,15},{8,0},{9,1},... | collective-permute-start | bytes 393224 | tf_op jit(solution)/shard_map/ppermute | solution.py:24
  92.0 20.7 %collective-permute-start.20 = (f32[32,1024]{1,0:T(8,128)S(1)}, f32[32,1024]{1,0:T(8,128)S(1)}, u32[]{:S(2)}, u32[]{:S(2)}) collective-permute-start(f32[32,1024]{1,0:T(8,128)S(1)} %add_add_fusion), channel_id=1, source_target_pairs={{0,16},{1,17},{2,18},{3,19},{4,20},{5,21},{6,22},{7,23},{8,24},{9,... | collective-permute-start | bytes 393224 | tf_op jit(solution)/shard_map/ppermute | solution.py:24
  93.8 19.5 %collective-permute-start.21 = (f32[32,1024]{1,0:T(8,128)S(1)}, f32[32,1024]{1,0:T(8,128)}, u32[]{:S(2)}, u32[]{:S(2)}) collective-permute-start(f32[32,1024]{1,0:T(8,128)S(1)} %add_add_fusion), channel_id=1, source_target_pairs={{0,24},{1,25},{2,26},{3,27},{4,28},{5,29},{6,30},{7,31},{8,16},{9,... | collective-permute-start | bytes 393224 | tf_op jit(solution)/shard_map/ppermute | solution.py:24
  97.5 30.4 %copy-start.4 = (f32[400,128]{1,0:T(8,128)S(1)}, f32[400,128]{1,0:T(8,128)}, u32[]{:S(2)}) copy-start(f32[400,128]{1,0:T(8,128)} %param.22) | copy-start | bytes 614404
  97.5 28.6 %collective-permute-start.25 = (f32[400,128]{1,0:T(8,128)}, f32[400,128]{1,0:T(8,128)}, u32[]{:S(2)}, u32[]{:S(2)}) collective-permute-start(f32[400,128]{1,0:T(8,128)} %get-tuple-element.11), channel_id=1, source_target_pairs={{0,8},{8,16},{16,24},{24,0},{1,9},{9,17},{17,25},{25,1},{2,10},{10... | collective-permute-start | bytes 614408 | tf_op jit(solution)/shard_map/ppermute | solution.py:88
  97.5 30.4 %collective-permute-start.26 = (f32[400,128]{1,0:T(8,128)}, f32[400,128]{1,0:T(8,128)}, u32[]{:S(2)}, u32[]{:S(2)}) collective-permute-start(f32[400,128]{1,0:T(8,128)} %get-tuple-element.13), channel_id=1, source_target_pairs={{0,16},{8,24},{16,0},{24,8},{1,17},{9,25},{17,1},{25,9},{2,18},{10... | collective-permute-start | bytes 614408 | tf_op jit(solution)/shard_map/ppermute | solution.py:88
  100.1 27.8 %collective-permute-start.27 = (f32[400,128]{1,0:T(8,128)S(1)}, f32[400,128]{1,0:T(8,128)}, u32[]{:S(2)}, u32[]{:S(2)}) collective-permute-start(f32[400,128]{1,0:T(8,128)S(1)} %get-tuple-element.12), channel_id=1, source_target_pairs={{0,24},{8,0},{16,8},{24,16},{1,25},{9,1},{17,9},{25,17},{2,26},{10... | collective-permute-start | bytes 614408 | tf_op jit(solution)/shard_map/ppermute | solution.py:88
  112.6 0.7 copy-start.6
  122.6 7.3 %collective-permute-start.22 = (f32[32,384]{1,0:T(8,128)S(1)}, f32[32,384]{1,0:T(8,128)S(1)}, u32[]{:S(2)}, u32[]{:S(2)}) collective-permute-start(f32[32,384]{1,0:T(8,128)S(1)} %fusion.28), channel_id=1, source_target_pairs={{0,8},{8,0},{16,24},{24,16},{1,9},{9,1},{17,25},{25,17},{2,10},{10... | collective-permute-start | bytes 147464 | tf_op jit(solution)/shard_map/ppermute | solution.py:24
  125.5 5.7 %collective-permute-start.23 = (f32[32,384]{1,0:T(8,128)S(1)}, f32[32,384]{1,0:T(8,128)S(1)}, u32[]{:S(2)}, u32[]{:S(2)}) collective-permute-start(f32[32,384]{1,0:T(8,128)S(1)} %fusion.28), channel_id=1, source_target_pairs={{0,16},{8,24},{16,0},{24,8},{1,17},{9,25},{17,1},{25,9},{2,18},{10... | collective-permute-start | bytes 147464 | tf_op jit(solution)/shard_map/ppermute | solution.py:24
  126.1 6.0 %collective-permute-start.24 = (f32[32,384]{1,0:T(8,128)S(1)}, f32[32,384]{1,0:T(8,128)S(1)}, u32[]{:S(2)}, u32[]{:S(2)}) collective-permute-start(f32[32,384]{1,0:T(8,128)S(1)} %fusion.28), channel_id=1, source_target_pairs={{0,24},{8,16},{16,8},{24,0},{1,25},{9,17},{17,9},{25,1},{2,26},{10... | collective-permute-start | bytes 147464 | tf_op jit(solution)/shard_map/ppermute | solution.py:24
  132.1 2.6 %copy-start.5 = (f32[32,384]{1,0:T(8,128)}, f32[32,384]{1,0:T(8,128)S(1)}, u32[]{:S(2)}) copy-start(f32[32,384]{1,0:T(8,128)S(1)} %add_multiply_fusion.2) | copy-start | bytes 147460
  133.6 1.2 copy-start.2
  133.6 1.2 copy-start.3

commit v7 on v4

--- a/solution.py
+++ b/solution.py
@@ -134,6 +134,8 @@
         preferred_element_type=jnp.float32,
     )
     combined = product + error_state[0].astype(jnp.float32)
+    word_new = word_update(word_grads, token_ids, owner_map, word_master)
+    word_new, combined = lax.optimization_barrier((word_new, combined))
     right_rows = q_start.T
     left_rows = None
     for round_index in range(ROUNDS):
@@ -158,7 +160,6 @@
     moment_new = MOMENTUM * qkv_moment + update_rows
     master_new = qkv_master - LEARNING_RATE * moment_new
     weight_bf16 = lax.all_gather(master_new.astype(jnp.bfloat16), "rep", axis=0, tiled=True)
-    word_new = word_update(word_grads, token_ids, owner_map, word_master)
     return (error_new, right_basis, moment_new, master_new, weight_bf16, word_new)
 
 

time: 149 us -> 166 us (1.11)
  waiting for transfers between devices: 55.7 us -> 66.6 us
  starting transfers between devices: 30.7 us -> 39.2 us
  matrix products: 14.4 us -> 12.6 us
    ppermute x3, waiting for transfers between devices: 0.01 us -> 12.6 us  [word_update_dense(): row_grad = row_grad + lax.ppermute(block, 'rep', pairs)]
    ppermute x14, starting transfers between devices: 18.4 us -> 25.8 us  [tree_sum(): value = value + lax.ppermute(value, axes, pairs)]
    ppermute x5, waiting for transfers between devices: 15.1 us -> 12 us  [exchange(): return lax.ppermute(value, axis, [(i, i ^ stride) for i in range(count)])]
  transfers between devices with their start and end apart: 22 -> 22, of which waited for: 17 -> 19; matrix products, arithmetic and copies ran while one was open for 13% -> 4% of each run, Pallas kernels for 0% -> 0%
where the time goes in v7:
time: 166 us; the launch traced here: 165 us
  waiting for transfers between devices  66.6 us (40%)
  starting transfers between devices  39.2 us (24%)
  other arithmetic  20.6 us (12%)
  blocking collectives  17.8 us (11%)
  matrix products  12.6 us (8%)
  local copies, waits for them, and re-layouts  7.48 us (5%)
    ppermute x14, waiting for transfers between devices, tree_sum(): value = value + lax.ppermute(value, axes, pairs)  42 us
    ppermute x14, starting transfers between devices, tree_sum(): value = value + lax.ppermute(value, axes, pairs)  25.8 us
    all_gather x1, blocking collectives, shards(): lax.all_gather(master_new.astype(jnp.bfloat16), 'rep', axis=0, tiled=True)  17.8 us
    ppermute x3, waiting for transfers between devices, word_update_dense(): row_grad = row_grad + lax.ppermute(block, 'rep', pairs)  12.6 us
    ppermute x5, waiting for transfers between devices, exchange(): return lax.ppermute(value, axis, [(i, i ^ stride) for i in range(count)])  12 us
    ppermute x5, starting transfers between devices, exchange(): return lax.ppermute(value, axis, [(i, i ^ stride) for i in range(count)])  7.89 us
    another operation x6, other arithmetic, shards(): factor_low = jnp.linalg.cholesky(gram_matrix)  7.19 us
    another operation x4, other arithmetic, shards(): jax.scipy.linalg.solve_triangular(factor_low, left_rows, lower=True)  6.17 us
  transfers between devices with their start and end apart: 22, of which 19 were waited for; matrix products, arithmetic and copies ran while one was open for 4% of the time, Pallas kernels for 0%

profile of v7, /device:TPU:0, one launch (start us, length us, event | category | flops | bytes accessed | tf_op | source)
XLA Modules:
  0.0 165.3 jit_solution(13433512078462305143)
XLA Ops:
  0.7 3.0 %collective-permute-start.4 = (bf16[192,1024]{1,0:T(8,128)(2,1)}, bf16[192,1024]{1,0:T(8,128)(2,1)S(1)}, u32[]{:S(2)}, u32[]{:S(2)}) collective-permute-start(bf16[192,1024]{1,0:T(8,128)(2,1)} %param.13), channel_id=1, source_target_pairs={{0,4},{1,5},{2,6},{3,7},{4,0},{5,1},{6,2},{7,3},{8,12},{9,13},{10,... | collective-permute-start | bytes 1179656 | tf_op jit(solution)/shard_map/ppermute | solution.py:37
  3.7 1.5 collective-permute-start.3
  5.2 7.8 %collective-permute-done.4 = bf16[192,1024]{1,0:T(8,128)(2,1)S(1)} collective-permute-done((bf16[192,1024]{1,0:T(8,128)(2,1)}, bf16[192,1024]{1,0:T(8,128)(2,1)S(1)}, u32[]{:S(2)}, u32[]{:S(2)}) %collective-permute-start.4) | collective-permute-done | bytes 393248 | tf_op jit(solution)/shard_map/ppermute | solution.py:37
  13.0 1.8 %collective-permute-start.5 = (bf16[96,1024]{1,0:T(8,128)(2,1)S(1)}, bf16[96,1024]{1,0:T(8,128)(2,1)S(1)}, u32[]{:S(2)}, u32[]{:S(2)}) collective-permute-start(bf16[96,1024]{1,0:T(8,128)(2,1)S(1)} %slice.32), channel_id=1, source_target_pairs={{0,2},{1,3},{2,0},{3,1},{4,6},{5,7},{6,4},{7,5},{8,10},{9,11},{10,... | collective-permute-start | bytes 589832 | tf_op jit(solution)/shard_map/ppermute | solution.py:37
  14.8 1.6 collective-permute-start.6
  16.4 2.8 %collective-permute-done.5 = bf16[96,1024]{1,0:T(8,128)(2,1)S(1)} collective-permute-done((bf16[96,1024]{1,0:T(8,128)(2,1)S(1)}, bf16[96,1024]{1,0:T(8,128)(2,1)S(1)}, u32[]{:S(2)}, u32[]{:S(2)}) %collective-permute-start.5) | collective-permute-done | bytes 196640 | tf_op jit(solution)/shard_map/ppermute | solution.py:37
  19.2 1.4 collective-permute-done.6
  20.6 1.4 pad_maximum_fusion
  23.1 3.1 %fusion = f32[1600,128]{1,0:T(8,128)S(1)} fusion(bf16[1536,128]{1,0:T(8,128)(2,1)S(1)} %copy-done.8, s32[1536]{0:T(1024)S(1)} %select_reduce_fusion), kind=kOutput, calls=%fused_computation.1 | convolution fusion | flops 631603200 | bytes 1218560 | tf_op jit(solution)/shard_map/dot_general | solution.py:70
  27.9 1.6 collective-permute-start
  29.4 2.6 %collective-permute-start.1 = (f32[400,128]{1,0:T(8,128)S(1)}, f32[400,128]{1,0:T(8,128)}, u32[]{:S(2)}, u32[]{:S(2)}) collective-permute-start(f32[400,128]{1,0:T(8,128)S(1)} %get-tuple-element.17), channel_id=1, source_target_pairs={{0,16},{8,24},{16,0},{24,8},{1,17},{9,25},{17,1},{25,9},{2,18},{10... | collective-permute-start | bytes 614408 | tf_op jit(solution)/shard_map/ppermute | solution.py:80
  32.0 1.3 collective-permute-start.2
  33.8 4.1 %collective-permute-done = f32[400,128]{1,0:T(8,128)S(1)} collective-permute-done((f32[400,128]{1,0:T(8,128)}, f32[400,128]{1,0:T(8,128)S(1)}, u32[]{:S(2)}, u32[]{:S(2)}) %collective-permute-start) | collective-permute-done | bytes 204832 | tf_op jit(solution)/shard_map/ppermute | solution.py:80
  37.9 8.5 %collective-permute-done.1 = f32[400,128]{1,0:T(8,128)} collective-permute-done((f32[400,128]{1,0:T(8,128)S(1)}, f32[400,128]{1,0:T(8,128)}, u32[]{:S(2)}, u32[]{:S(2)}) %collective-permute-start.1) | collective-permute-done | bytes 204832 | tf_op jit(solution)/shard_map/ppermute | solution.py:80
  46.4 1.9 %multiply_subtract_fusion.1 = f32[400,128]{1,0:T(8,128)} fusion(f32[400,128]{1,0:T(8,128)S(1)} %copy-done.5, f32[400,128]{1,0:T(8,128)} %collective-permute-done.2, f32[400,128]{1,0:T(8,128)} %collective-permute-done.1, f32[400,128]{1,0:T(8,128)S(1)} %collective-permute-done, f32[1600,128]{1,0:T(8,128)} %copy-done.2, s32[]{:T(128)S(6)} %select_n.62), kind=kLoop, calls=%fused_computation.20 | loop fusion | flops 256000 | bytes 1228804 | tf_op jit(solution)/shard_map/sub | solution.py:81
  52.7 1.9 %convert_add_fusion = f32[1024,384]{1,0:T(8,128)S(1)} fusion(bf16[1536,1024]{1,0:T(8,128)(2,1)S(1)} %fusion.3, bf16[1536,384]{1,0:T(8,128)(2,1)S(1)} %copy-done, bf16[1,1024,384]{2,1,0:T(8,128)(2,1)S(1)} %copy-done.7), kind=kOutput, calls=%fused_computation.6 | convolution fusion | flops 1208745984 | bytes 6684672 | tf_op jit(solution)/shard_map/dot_general | solution.py:130
  54.6 1.6 convolution_bitcast_fusion
  56.2 1.3 collective-permute-done.8
  58.8 4.4 %collective-permute-done.9 = f32[32,1024]{1,0:T(8,128)S(1)} collective-permute-done((f32[32,1024]{1,0:T(8,128)S(1)}, f32[32,1024]{1,0:T(8,128)S(1)}, u32[]{:S(2)}, u32[]{:S(2)}) %collective-permute-start.9) | collective-permute-done | bytes 131104 | tf_op jit(solution)/shard_map/ppermute | solution.py:25
  63.2 1.6 collective-permute-start.10
  64.8 3.4 %collective-permute-done.10 = f32[32,1024]{1,0:T(8,128)S(1)} collective-permute-done((f32[32,1024]{1,0:T(8,128)S(1)}, f32[32,1024]{1,0:T(8,128)S(1)}, u32[]{:S(2)}, u32[]{:S(2)}) %collective-permute-start.10) | collective-permute-done | bytes 131104 | tf_op jit(solution)/shard_map/ppermute | solution.py:25
  68.3 5.0 %collective-permute-start.11 = (f32[32,1024]{1,0:T(8,128)S(1)}, f32[32,1024]{1,0:T(8,128)S(1)}, u32[]{:S(2)}, u32[]{:S(2)}) collective-permute-start(f32[32,1024]{1,0:T(8,128)S(1)} %add.148), channel_id=1, source_target_pairs={{0,8},{1,9},{2,10},{3,11},{4,12},{5,13},{6,14},{7,15},{8,0},{9,1},... | collective-permute-start | bytes 393224 | tf_op jit(solution)/shard_map/ppermute | solution.py:25
  73.2 2.9 %collective-permute-done.11 = f32[32,1024]{1,0:T(8,128)S(1)} collective-permute-done((f32[32,1024]{1,0:T(8,128)S(1)}, f32[32,1024]{1,0:T(8,128)S(1)}, u32[]{:S(2)}, u32[]{:S(2)}) %collective-permute-start.11) | collective-permute-done | bytes 131104 | tf_op jit(solution)/shard_map/ppermute | solution.py:25
  76.2 1.7 %collective-permute-start.12 = (f32[32,1024]{1,0:T(8,128)S(1)}, f32[32,1024]{1,0:T(8,128)S(1)}, u32[]{:S(2)}, u32[]{:S(2)}) collective-permute-start(f32[32,1024]{1,0:T(8,128)S(1)} %add.149), channel_id=1, source_target_pairs={{0,16},{1,17},{2,18},{3,19},{4,20},{5,21},{6,22},{7,23},{8,24},{9,... | collective-permute-start | bytes 393224 | tf_op jit(solution)/shard_map/ppermute | solution.py:25
  77.8 4.3 %collective-permute-done.12 = f32[32,1024]{1,0:T(8,128)S(1)} collective-permute-done((f32[32,1024]{1,0:T(8,128)S(1)}, f32[32,1024]{1,0:T(8,128)S(1)}, u32[]{:S(2)}, u32[]{:S(2)}) %collective-permute-start.12) | collective-permute-done | bytes 131104 | tf_op jit(solution)/shard_map/ppermute | solution.py:25
  82.5 2.9 %cholesky.44 = f32[32,32]{1,0:T(8,128)S(1)} custom-call(f32[32,32]{1,0:T(8,128)S(1)} %fusion.22), custom_call_target="Cholesky" | custom-call | tf_op jit(solution)/shard_map/jit(cholesky)/cholesky | solution.py:147
  86.7 2.4 %custom-call.6 = f32[1,32,32]{1,2,0:T(8,128)S(1)} custom-call(f32[1,32,32]{2,1,0:T(8,128)S(1)} %fusion.17), custom_call_target="InvertDiagBlocksLowerTriangular" | custom-call | tf_op jit(solution)/shard_map/jit(_solve_triangular)/triangular_solve | solution.py:148
  90.4 2.5 %collective-permute-start.13 = (f32[32,384]{1,0:T(8,128)S(1)}, f32[32,384]{1,0:T(8,128)S(1)}, u32[]{:S(2)}, u32[]{:S(2)}) collective-permute-start(f32[32,384]{1,0:T(8,128)S(1)} %fusion.32), channel_id=1, source_target_pairs={{0,8},{8,0},{16,24},{24,16},{1,9},{9,1},{17,25},{25,17},{2,10},{10... | collective-permute-start | bytes 147464 | tf_op jit(solution)/shard_map/ppermute | solution.py:25
  93.0 2.1 %collective-permute-done.13 = f32[32,384]{1,0:T(8,128)S(1)} collective-permute-done((f32[32,384]{1,0:T(8,128)S(1)}, f32[32,384]{1,0:T(8,128)S(1)}, u32[]{:S(2)}, u32[]{:S(2)}) %collective-permute-start.13) | collective-permute-done | bytes 49184 | tf_op jit(solution)/shard_map/ppermute | solution.py:25
  95.1 2.0 %collective-permute-start.14 = (f32[32,384]{1,0:T(8,128)S(1)}, f32[32,384]{1,0:T(8,128)S(1)}, u32[]{:S(2)}, u32[]{:S(2)}) collective-permute-start(f32[32,384]{1,0:T(8,128)S(1)} %add.151), channel_id=1, source_target_pairs={{0,16},{8,24},{16,0},{24,8},{1,17},{9,25},{17,1},{25,9},{2,18},{10... | collective-permute-start | bytes 147464 | tf_op jit(solution)/shard_map/ppermute | solution.py:25
  97.1 3.1 %collective-permute-done.14 = f32[32,384]{1,0:T(8,128)S(1)} collective-permute-done((f32[32,384]{1,0:T(8,128)S(1)}, f32[32,384]{1,0:T(8,128)S(1)}, u32[]{:S(2)}, u32[]{:S(2)}) %collective-permute-start.14) | collective-permute-done | bytes 49184 | tf_op jit(solution)/shard_map/ppermute | solution.py:25
  100.2 1.6 fusion.11
  101.8 1.3 collective-permute-done.15
  104.4 4.4 %collective-permute-done.16 = f32[32,1024]{1,0:T(8,128)S(1)} collective-permute-done((f32[32,1024]{1,0:T(8,128)S(1)}, f32[32,1024]{1,0:T(8,128)S(1)}, u32[]{:S(2)}, u32[]{:S(2)}) %collective-permute-start.16) | collective-permute-done | bytes 131104 | tf_op jit(solution)/shard_map/ppermute | solution.py:25
  108.8 1.6 collective-permute-start.17
  110.4 3.4 %collective-permute-done.17 = f32[32,1024]{1,0:T(8,128)S(1)} collective-permute-done((f32[32,1024]{1,0:T(8,128)S(1)}, f32[32,1024]{1,0:T(8,128)S(1)}, u32[]{:S(2)}, u32[]{:S(2)}) %collective-permute-start.17) | collective-permute-done | bytes 131104 | tf_op jit(solution)/shard_map/ppermute | solution.py:25
  113.9 2.0 %collective-permute-start.18 = (f32[32,1024]{1,0:T(8,128)S(1)}, f32[32,1024]{1,0:T(8,128)S(1)}, u32[]{:S(2)}, u32[]{:S(2)}) collective-permute-start(f32[32,1024]{1,0:T(8,128)S(1)} %add.155), channel_id=1, source_target_pairs={{0,8},{1,9},{2,10},{3,11},{4,12},{5,13},{6,14},{7,15},{8,0},{9,1},... | collective-permute-start | bytes 393224 | tf_op jit(solution)/shard_map/ppermute | solution.py:25
  115.9 3.0 %collective-permute-done.18 = f32[32,1024]{1,0:T(8,128)S(1)} collective-permute-done((f32[32,1024]{1,0:T(8,128)S(1)}, f32[32,1024]{1,0:T(8,128)S(1)}, u32[]{:S(2)}, u32[]{:S(2)}) %collective-permute-start.18) | collective-permute-done | bytes 131104 | tf_op jit(solution)/shard_map/ppermute | solution.py:25
  118.9 2.0 %collective-permute-start.19 = (f32[32,1024]{1,0:T(8,128)S(1)}, f32[32,1024]{1,0:T(8,128)S(1)}, u32[]{:S(2)}, u32[]{:S(2)}) collective-permute-start(f32[32,1024]{1,0:T(8,128)S(1)} %add.156), channel_id=1, source_target_pairs={{0,16},{1,17},{2,18},{3,19},{4,20},{5,21},{6,22},{7,23},{8,24},{9,... | collective-permute-start | bytes 393224 | tf_op jit(solution)/shard_map/ppermute | solution.py:25
  120.9 3.9 %collective-permute-done.19 = f32[32,1024]{1,0:T(8,128)S(1)} collective-permute-done((f32[32,1024]{1,0:T(8,128)S(1)}, f32[32,1024]{1,0:T(8,128)S(1)}, u32[]{:S(2)}, u32[]{:S(2)}) %collective-permute-start.19) | collective-permute-done | bytes 131104 | tf_op jit(solution)/shard_map/ppermute | solution.py:25
  125.2 2.9 %cholesky.55 = f32[32,32]{1,0:T(8,128)S(1)} custom-call(f32[32,32]{1,0:T(8,128)S(1)} %fusion.20), custom_call_target="Cholesky" | custom-call | tf_op jit(solution)/shard_map/jit(cholesky)/cholesky | solution.py:147
  129.5 2.4 %custom-call.7 = f32[1,32,32]{1,2,0:T(8,128)S(1)} custom-call(f32[1,32,32]{2,1,0:T(8,128)S(1)} %fusion.18), custom_call_target="InvertDiagBlocksLowerTriangular" | custom-call | tf_op jit(solution)/shard_map/jit(_solve_triangular)/triangular_solve | solution.py:148
  133.2 2.0 %collective-permute-start.20 = (f32[32,384]{1,0:T(8,128)S(1)}, f32[32,384]{1,0:T(8,128)S(1)}, u32[]{:S(2)}, u32[]{:S(2)}) collective-permute-start(f32[32,384]{1,0:T(8,128)S(1)} %fusion.33), channel_id=1, source_target_pairs={{0,8},{8,0},{16,24},{24,16},{1,9},{9,1},{17,25},{25,17},{2,10},{10... | collective-permute-start | bytes 147464 | tf_op jit(solution)/shard_map/ppermute | solution.py:25
  135.2 2.1 %collective-permute-done.20 = f32[32,384]{1,0:T(8,128)S(1)} collective-permute-done((f32[32,384]{1,0:T(8,128)S(1)}, f32[32,384]{1,0:T(8,128)S(1)}, u32[]{:S(2)}, u32[]{:S(2)}) %collective-permute-start.20) | collective-permute-done | bytes 49184 | tf_op jit(solution)/shard_map/ppermute | solution.py:25
  137.4 2.8 %collective-permute-start.21 = (f32[32,384]{1,0:T(8,128)S(1)}, f32[32,384]{1,0:T(8,128)S(1)}, u32[]{:S(2)}, u32[]{:S(2)}) collective-permute-start(f32[32,384]{1,0:T(8,128)S(1)} %add.158), channel_id=1, source_target_pairs={{0,16},{8,24},{16,0},{24,8},{1,17},{9,25},{17,1},{25,9},{2,18},{10... | collective-permute-start | bytes 147464 | tf_op jit(solution)/shard_map/ppermute | solution.py:25
  140.2 2.2 %collective-permute-done.21 = f32[32,384]{1,0:T(8,128)S(1)} collective-permute-done((f32[32,384]{1,0:T(8,128)S(1)}, f32[32,384]{1,0:T(8,128)S(1)}, u32[]{:S(2)}, u32[]{:S(2)}) %collective-permute-start.21) | collective-permute-done | bytes 49184 | tf_op jit(solution)/shard_map/ppermute | solution.py:25
  142.4 1.5 fusion.16
  146.0 17.8 %all_gather.3 = bf16[1024,384]{1,0:T(8,128)(2,1)S(1)} all-gather(bf16[256,384]{1,0:T(8,128)(2,1)S(1)} %get-tuple-element.12), channel_id=1, replica_groups=mesh['rep'=4,'tp'=8] {'rep'}, dimensions={0}, use_global_device_ids=true | all-gather | bytes 983040 | tf_op jit(solution)/shard_map/all_gather | solution.py:162
  (75 shorter events, 19.8 us)
Async XLA Ops:
  0.6 52.0 %copy-start = (bf16[1536,384]{1,0:T(8,128)(2,1)S(1)}, bf16[1536,384]{1,0:T(8,128)(2,1)}, u32[]{:S(2)}) copy-start(bf16[1536,384]{1,0:T(8,128)(2,1)} %param.14) | copy-start | bytes 3538948
  0.6 19.9 %copy-start.1 = (bf16[192,1024]{1,0:T(8,128)(2,1)S(1)}, bf16[192,1024]{1,0:T(8,128)(2,1)}, u32[]{:S(2)}) copy-start(bf16[192,1024]{1,0:T(8,128)(2,1)} %param.13) | copy-start | bytes 1179652
  0.7 12.4 %collective-permute-start.4 = (bf16[192,1024]{1,0:T(8,128)(2,1)}, bf16[192,1024]{1,0:T(8,128)(2,1)S(1)}, u32[]{:S(2)}, u32[]{:S(2)}) collective-permute-start(bf16[192,1024]{1,0:T(8,128)(2,1)} %param.13), channel_id=1, source_target_pairs={{0,4},{1,5},{2,6},{3,7},{4,0},{5,1},{6,2},{7,3},{8,12},{9,13},{10,... | collective-permute-start | bytes 1179656 | tf_op jit(solution)/shard_map/ppermute | solution.py:37
  3.7 11.1 %collective-permute-start.3 = (bf16[192,1024]{1,0:T(8,128)(2,1)}, bf16[192,1024]{1,0:T(8,128)(2,1)S(1)}, u32[]{:S(2)}, u32[]{:S(2)}) collective-permute-start(bf16[192,1024]{1,0:T(8,128)(2,1)} %param.13), channel_id=1, source_target_pairs={{0,2},{1,3},{2,0},{3,1},{4,6},{5,7},{6,4},{7,5},{8,10},{9,11},{10,... | collective-permute-start | bytes 1179656 | tf_op jit(solution)/shard_map/ppermute | solution.py:37
  13.0 6.2 %collective-permute-start.5 = (bf16[96,1024]{1,0:T(8,128)(2,1)S(1)}, bf16[96,1024]{1,0:T(8,128)(2,1)S(1)}, u32[]{:S(2)}, u32[]{:S(2)}) collective-permute-start(bf16[96,1024]{1,0:T(8,128)(2,1)S(1)} %slice.32), channel_id=1, source_target_pairs={{0,2},{1,3},{2,0},{3,1},{4,6},{5,7},{6,4},{7,5},{8,10},{9,11},{10,... | collective-permute-start | bytes 589832 | tf_op jit(solution)/shard_map/ppermute | solution.py:37
  14.8 5.7 %collective-permute-start.6 = (bf16[96,1024]{1,0:T(8,128)(2,1)S(1)}, bf16[96,1024]{1,0:T(8,128)(2,1)S(1)}, u32[]{:S(2)}, u32[]{:S(2)}) collective-permute-start(bf16[96,1024]{1,0:T(8,128)(2,1)S(1)} %slice.33), channel_id=1, source_target_pairs={{0,4},{1,5},{2,6},{3,7},{4,0},{5,1},{6,2},{7,3},{8,12},{9,13},{10,... | collective-permute-start | bytes 589832 | tf_op jit(solution)/shard_map/ppermute | solution.py:37
  20.6 1.4 copy-start.9
  20.6 1.4 copy-start.10
  20.6 2.5 %copy-start.8 = (bf16[1536,128]{1,0:T(8,128)(2,1)S(1)}, bf16[1536,128]{1,0:T(8,128)(2,1)}, u32[]{:S(2)}) copy-start(bf16[1536,128]{1,0:T(8,128)(2,1)} %param.19) | copy-start | bytes 1179652
  22.0 26.4 %collective-permute-start.7 = (bf16[4,192,1024]{2,1,0:T(8,128)(2,1)}, bf16[4,192,1024]{2,1,0:T(8,128)(2,1)}, u32[]{:S(2)}, u32[]{:S(2)}) collective-permute-start(bf16[4,192,1024]{2,1,0:T(8,128)(2,1)} %pad_maximum_fusion), channel_id=1, source_target_pairs={{0,1},{1,0},{2,3},{3,2},{4,5},{5,4},{6,7},{7,6},{8,9},{9,8},{10,11... | collective-permute-start | bytes 4718600 | tf_op jit(solution)/shard_map/ppermute | solution.py:37
  26.2 0.9 copy-start.2
  27.9 10.0 %collective-permute-start = (f32[400,128]{1,0:T(8,128)}, f32[400,128]{1,0:T(8,128)S(1)}, u32[]{:S(2)}, u32[]{:S(2)}) collective-permute-start(f32[400,128]{1,0:T(8,128)} %get-tuple-element.15), channel_id=1, source_target_pairs={{0,8},{8,16},{16,24},{24,0},{1,9},{9,17},{17,25},{25,1},{2,10},{10... | collective-permute-start | bytes 614408 | tf_op jit(solution)/shard_map/ppermute | solution.py:80
  29.4 17.0 %collective-permute-start.1 = (f32[400,128]{1,0:T(8,128)S(1)}, f32[400,128]{1,0:T(8,128)}, u32[]{:S(2)}, u32[]{:S(2)}) collective-permute-start(f32[400,128]{1,0:T(8,128)S(1)} %get-tuple-element.17), channel_id=1, source_target_pairs={{0,16},{8,24},{16,0},{24,8},{1,17},{9,25},{17,1},{25,9},{2,18},{10... | collective-permute-start | bytes 614408 | tf_op jit(solution)/shard_map/ppermute | solution.py:80
  32.0 14.4 %collective-permute-start.2 = (f32[400,128]{1,0:T(8,128)S(1)}, f32[400,128]{1,0:T(8,128)}, u32[]{:S(2)}, u32[]{:S(2)}) collective-permute-start(f32[400,128]{1,0:T(8,128)S(1)} %get-tuple-element.16), channel_id=1, source_target_pairs={{0,24},{8,0},{16,8},{24,16},{1,25},{9,1},{17,9},{25,17},{2,26},{10... | collective-permute-start | bytes 614408 | tf_op jit(solution)/shard_map/ppermute | solution.py:80
  33.4 13.0 %copy-start.5 = (f32[400,128]{1,0:T(8,128)S(1)}, f32[400,128]{1,0:T(8,128)}, u32[]{:S(2)}) copy-start(f32[400,128]{1,0:T(8,128)} %param.22) | copy-start | bytes 614404
  48.4 4.2 %copy-start.7 = (bf16[1,1024,384]{2,1,0:T(8,128)(2,1)S(1)}, bf16[1,1024,384]{2,1,0:T(8,128)(2,1)}, u32[]{:S(2)}) copy-start(bf16[1,1024,384]{2,1,0:T(8,128)(2,1)} %param.15) | copy-start | bytes 2359300
  52.7 1.9 %copy-start.6 = (f32[384,32]{0,1:T(8,128)S(1)}, f32[384,32]{0,1:T(8,128)}, u32[]{:S(2)}) copy-start(f32[384,32]{0,1:T(8,128)} %param.16) | copy-start | bytes 147460
  56.1 1.4 collective-permute-start.8
  57.6 5.6 %collective-permute-start.9 = (f32[32,1024]{1,0:T(8,128)S(1)}, f32[32,1024]{1,0:T(8,128)S(1)}, u32[]{:S(2)}, u32[]{:S(2)}) collective-permute-start(f32[32,1024]{1,0:T(8,128)S(1)} %add.146), channel_id=1, source_target_pairs={{0,2},{1,3},{2,0},{3,1},{4,6},{5,7},{6,4},{7,5},{8,10},{9,11},{10,... | collective-permute-start | bytes 393224 | tf_op jit(solution)/shard_map/ppermute | solution.py:25
  63.2 5.0 %collective-permute-start.10 = (f32[32,1024]{1,0:T(8,128)S(1)}, f32[32,1024]{1,0:T(8,128)S(1)}, u32[]{:S(2)}, u32[]{:S(2)}) collective-permute-start(f32[32,1024]{1,0:T(8,128)S(1)} %add.147), channel_id=1, source_target_pairs={{0,4},{1,5},{2,6},{3,7},{4,0},{5,1},{6,2},{7,3},{8,12},{9,13},{10,... | collective-permute-start | bytes 393224 | tf_op jit(solution)/shard_map/ppermute | solution.py:25
  68.3 7.9 %collective-permute-start.11 = (f32[32,1024]{1,0:T(8,128)S(1)}, f32[32,1024]{1,0:T(8,128)S(1)}, u32[]{:S(2)}, u32[]{:S(2)}) collective-permute-start(f32[32,1024]{1,0:T(8,128)S(1)} %add.148), channel_id=1, source_target_pairs={{0,8},{1,9},{2,10},{3,11},{4,12},{5,13},{6,14},{7,15},{8,0},{9,1},... | collective-permute-start | bytes 393224 | tf_op jit(solution)/shard_map/ppermute | solution.py:25
  76.2 5.9 %collective-permute-start.12 = (f32[32,1024]{1,0:T(8,128)S(1)}, f32[32,1024]{1,0:T(8,128)S(1)}, u32[]{:S(2)}, u32[]{:S(2)}) collective-permute-start(f32[32,1024]{1,0:T(8,128)S(1)} %add.149), channel_id=1, source_target_pairs={{0,16},{1,17},{2,18},{3,19},{4,20},{5,21},{6,22},{7,23},{8,24},{9,... | collective-permute-start | bytes 393224 | tf_op jit(solution)/shard_map/ppermute | solution.py:25
  90.4 4.7 %collective-permute-start.13 = (f32[32,384]{1,0:T(8,128)S(1)}, f32[32,384]{1,0:T(8,128)S(1)}, u32[]{:S(2)}, u32[]{:S(2)}) collective-permute-start(f32[32,384]{1,0:T(8,128)S(1)} %fusion.32), channel_id=1, source_target_pairs={{0,8},{8,0},{16,24},{24,16},{1,9},{9,1},{17,25},{25,17},{2,10},{10... | collective-permute-start | bytes 147464 | tf_op jit(solution)/shard_map/ppermute | solution.py:25
  95.1 5.1 %collective-permute-start.14 = (f32[32,384]{1,0:T(8,128)S(1)}, f32[32,384]{1,0:T(8,128)S(1)}, u32[]{:S(2)}, u32[]{:S(2)}) collective-permute-start(f32[32,384]{1,0:T(8,128)S(1)} %add.151), channel_id=1, source_target_pairs={{0,16},{8,24},{16,0},{24,8},{1,17},{9,25},{17,1},{25,9},{2,18},{10... | collective-permute-start | bytes 147464 | tf_op jit(solution)/shard_map/ppermute | solution.py:25
  101.8 1.4 collective-permute-start.15
  103.2 5.6 %collective-permute-start.16 = (f32[32,1024]{1,0:T(8,128)S(1)}, f32[32,1024]{1,0:T(8,128)S(1)}, u32[]{:S(2)}, u32[]{:S(2)}) collective-permute-start(f32[32,1024]{1,0:T(8,128)S(1)} %add.153), channel_id=1, source_target_pairs={{0,2},{1,3},{2,0},{3,1},{4,6},{5,7},{6,4},{7,5},{8,10},{9,11},{10,... | collective-permute-start | bytes 393224 | tf_op jit(solution)/shard_map/ppermute | solution.py:25
  108.8 5.0 %collective-permute-start.17 = (f32[32,1024]{1,0:T(8,128)S(1)}, f32[32,1024]{1,0:T(8,128)S(1)}, u32[]{:S(2)}, u32[]{:S(2)}) collective-permute-start(f32[32,1024]{1,0:T(8,128)S(1)} %add.154), channel_id=1, source_target_pairs={{0,4},{1,5},{2,6},{3,7},{4,0},{5,1},{6,2},{7,3},{8,12},{9,13},{10,... | collective-permute-start | bytes 393224 | tf_op jit(solution)/shard_map/ppermute | solution.py:25
  113.9 5.0 %collective-permute-start.18 = (f32[32,1024]{1,0:T(8,128)S(1)}, f32[32,1024]{1,0:T(8,128)S(1)}, u32[]{:S(2)}, u32[]{:S(2)}) collective-permute-start(f32[32,1024]{1,0:T(8,128)S(1)} %add.155), channel_id=1, source_target_pairs={{0,8},{1,9},{2,10},{3,11},{4,12},{5,13},{6,14},{7,15},{8,0},{9,1},... | collective-permute-start | bytes 393224 | tf_op jit(solution)/shard_map/ppermute | solution.py:25
  118.9 5.9 %collective-permute-start.19 = (f32[32,1024]{1,0:T(8,128)S(1)}, f32[32,1024]{1,0:T(8,128)S(1)}, u32[]{:S(2)}, u32[]{:S(2)}) collective-permute-start(f32[32,1024]{1,0:T(8,128)S(1)} %add.156), channel_id=1, source_target_pairs={{0,16},{1,17},{2,18},{3,19},{4,20},{5,21},{6,22},{7,23},{8,24},{9,... | collective-permute-start | bytes 393224 | tf_op jit(solution)/shard_map/ppermute | solution.py:25
  133.2 4.2 %collective-permute-start.20 = (f32[32,384]{1,0:T(8,128)S(1)}, f32[32,384]{1,0:T(8,128)S(1)}, u32[]{:S(2)}, u32[]{:S(2)}) collective-permute-start(f32[32,384]{1,0:T(8,128)S(1)} %fusion.33), channel_id=1, source_target_pairs={{0,8},{8,0},{16,24},{24,16},{1,9},{9,1},{17,25},{25,17},{2,10},{10... | collective-permute-start | bytes 147464 | tf_op jit(solution)/shard_map/ppermute | solution.py:25
  137.4 5.1 %collective-permute-start.21 = (f32[32,384]{1,0:T(8,128)S(1)}, f32[32,384]{1,0:T(8,128)S(1)}, u32[]{:S(2)}, u32[]{:S(2)}) collective-permute-start(f32[32,384]{1,0:T(8,128)S(1)} %add.158), channel_id=1, source_target_pairs={{0,16},{8,24},{16,0},{24,8},{1,17},{9,25},{17,1},{25,9},{2,18},{10... | collective-permute-start | bytes 147464 | tf_op jit(solution)/shard_map/ppermute | solution.py:25
  143.9 1.2 copy-start.3
  143.9 1.2 copy-start.4

commit v8 on v4

--- a/solution.py
+++ b/solution.py
@@ -27,10 +27,13 @@
     return value
 
 
-def gather_rows(block, axis):
+def replica_product(block, out_grads, axis):
     count = lax.axis_size(axis)
     if count != 8 or block.shape[0] % 2:
-        return lax.all_gather(block, axis, axis=0, tiled=True)
+        gathered = lax.all_gather(block, axis, axis=0, tiled=True)
+        return lax.dot_general(
+            gathered, out_grads, (((0,), (0,)), ((), ())), preferred_element_type=jnp.float32
+        )
     me = lax.axis_index(axis)
 
     def exchange(value, stride):
@@ -42,15 +45,16 @@
     diagonal = jnp.concatenate(
         [exchange(from_y[:half], 2), exchange(from_x[half:], 4)], axis=0
     )
-    other = exchange(jnp.stack([block, from_x, from_y, diagonal]), 1)
-    pieces = {0: block, 2: from_x, 4: from_y, 6: diagonal}
-    for index, offset in enumerate((1, 3, 5, 7)):
-        pieces[offset] = other[index]
+    mine = jnp.stack([block, from_x, from_y, diagonal])
+    other = exchange(mine, 1)
     rows = block.shape[0]
-    gathered = jnp.zeros((count * rows,) + block.shape[1:], block.dtype)
-    for offset, piece in pieces.items():
-        gathered = lax.dynamic_update_slice_in_dim(gathered, piece, (me ^ offset) * rows, 0)
-    return gathered
+    grads = out_grads.reshape(count, rows, out_grads.shape[1])
+    even = jnp.stack([grads[me ^ offset] for offset in (0, 2, 4, 6)])
+    odd = jnp.stack([grads[me ^ offset] for offset in (1, 3, 5, 7)])
+    contract = (((0, 1), (0, 1)), ((), ()))
+    first = lax.dot_general(mine, even, contract, preferred_element_type=jnp.float32)
+    second = lax.dot_general(other, odd, contract, preferred_element_type=jnp.float32)
+    return first + second
 
 
 def orthonormal(left_basis, gram_matrix):
@@ -127,12 +131,7 @@
     highest = lax.Precision.HIGHEST
     replicas = lax.axis_size("rep")
     word_new = None
-    product = lax.dot_general(
-        gather_rows(activations, "tp"),
-        out_grads,
-        (((0,), (0,)), ((), ())),
-        preferred_element_type=jnp.float32,
-    )
+    product = replica_product(activations, out_grads, "tp")
     combined = product + error_state[0].astype(jnp.float32)
     right_rows = q_start.T
     left_rows = None

time: 149 us -> 146 us (0.980)
  starting transfers between devices: 30.7 us -> 39 us
  local copies, waits for them, and re-layouts: 7.69 us -> 3.24 us
  waiting for transfers between devices: 55.7 us -> 51.3 us
  other arithmetic: 21.3 us -> 19.4 us
    ppermute x14, starting transfers between devices: 18.4 us -> 27.5 us  [tree_sum(): value = value + lax.ppermute(value, axes, pairs)]
    dynamic_update_slice x8 -> x0, local copies, waits for them, and re-layouts: 4.26 us -> none  [gather_rows(): lax.dynamic_update_slice_in_dim(gathered, piece, (me ^ offset) * rows, 0)]
    ppermute x14, waiting for transfers between devices: 40.6 us -> 38.2 us  [tree_sum(): value = value + lax.ppermute(value, axes, pairs)]
    ppermute x5, waiting for transfers between devices: 15.1 us -> 13.1 us  [exchange(): return lax.ppermute(value, axis, [(i, i ^ stride) for i in range(count)])]
    dot_general x1 -> x2, matrix products: 1.88 us -> 3.48 us  [the longest x1 2.45 us: replica_product(): lax.dot_general(other, odd, contract, preferred_element_type=jnp.float32)]
  transfers between devices with their start and end apart: 22 -> 22, of which waited for: 17 -> 17; matrix products, arithmetic and copies ran while one was open for 13% -> 11% of each run, Pallas kernels for 0% -> 0%
where the time goes in v8:
time: 146 us
  waiting for transfers between devices  51.3 us (35%)
  starting transfers between devices  39 us (27%)
  other arithmetic  19.4 us (13%)
  blocking collectives  17.8 us (12%)
  matrix products  14.4 us (10%)
  local copies, waits for them, and re-layouts  3.24 us (2%)
    ppermute x14, waiting for transfers between devices, tree_sum(): value = value + lax.ppermute(value, axes, pairs)  38.2 us
    ppermute x14, starting transfers between devices, tree_sum(): value = value + lax.ppermute(value, axes, pairs)  27.5 us
    all_gather x1, blocking collectives, shards(): lax.all_gather(master_new.astype(jnp.bfloat16), 'rep', axis=0, tiled=True)  17.8 us
    ppermute x5, waiting for transfers between devices, exchange(): return lax.ppermute(value, axis, [(i, i ^ stride) for i in range(count)])  13.1 us
    ppermute x5, starting transfers between devices, exchange(): return lax.ppermute(value, axis, [(i, i ^ stride) for i in range(count)])  7.98 us
    another operation x6, other arithmetic, shards(): factor_low = jnp.linalg.cholesky(gram_matrix)  7.19 us
    another operation x4, other arithmetic, shards(): jax.scipy.linalg.solve_triangular(factor_low, left_rows, lower=True)  6.17 us
    ppermute x3, starting transfers between devices, word_update_dense(): row_grad = row_grad + lax.ppermute(block, 'rep', pairs)  3.49 us
  transfers between devices with their start and end apart: 22, of which 17 were waited for; matrix products, arithmetic and copies ran while one was open for 11% of the time, Pallas kernels for 0%

profile of v8, /device:TPU:0, one launch (start us, length us, event | category | flops | bytes accessed | tf_op | source)
XLA Modules:
  0.0 146.2 jit_solution(9471800385735981493)
XLA Ops:
  0.7 3.0 %collective-permute-start = (bf16[192,1024]{1,0:T(8,128)(2,1)}, bf16[192,1024]{1,0:T(8,128)(2,1)S(1)}, u32[]{:S(2)}, u32[]{:S(2)}) collective-permute-start(bf16[192,1024]{1,0:T(8,128)(2,1)} %param.13), channel_id=1, source_target_pairs={{0,2},{1,3},{2,0},{3,1},{4,6},{5,7},{6,4},{7,5},{8,10},{9,11},{10,... | collective-permute-start | bytes 1179656 | tf_op jit(solution)/shard_map/ppermute | solution.py:40
  3.7 1.5 %collective-permute-start.1 = (bf16[192,1024]{1,0:T(8,128)(2,1)}, bf16[192,1024]{1,0:T(8,128)(2,1)S(1)}, u32[]{:S(2)}, u32[]{:S(2)}) collective-permute-start(bf16[192,1024]{1,0:T(8,128)(2,1)} %param.13), channel_id=1, source_target_pairs={{0,4},{1,5},{2,6},{3,7},{4,0},{5,1},{6,2},{7,3},{8,12},{9,13},{10,... | collective-permute-start | bytes 1179656 | tf_op jit(solution)/shard_map/ppermute | solution.py:40
  5.2 7.8 %collective-permute-done = bf16[192,1024]{1,0:T(8,128)(2,1)S(1)} collective-permute-done((bf16[192,1024]{1,0:T(8,128)(2,1)}, bf16[192,1024]{1,0:T(8,128)(2,1)S(1)}, u32[]{:S(2)}, u32[]{:S(2)}) %collective-permute-start) | collective-permute-done | bytes 393248 | tf_op jit(solution)/shard_map/ppermute | solution.py:40
  13.0 1.8 %collective-permute-start.3 = (bf16[96,1024]{1,0:T(8,128)(2,1)S(1)}, bf16[96,1024]{1,0:T(8,128)(2,1)S(1)}, u32[]{:S(2)}, u32[]{:S(2)}) collective-permute-start(bf16[96,1024]{1,0:T(8,128)(2,1)S(1)} %slice.17), channel_id=1, source_target_pairs={{0,4},{1,5},{2,6},{3,7},{4,0},{5,1},{6,2},{7,3},{8,12},{9,13},{10,... | collective-permute-start | bytes 589832 | tf_op jit(solution)/shard_map/ppermute | solution.py:40
  14.9 1.6 %collective-permute-start.2 = (bf16[96,1024]{1,0:T(8,128)(2,1)S(1)}, bf16[96,1024]{1,0:T(8,128)(2,1)S(1)}, u32[]{:S(2)}, u32[]{:S(2)}) collective-permute-start(bf16[96,1024]{1,0:T(8,128)(2,1)S(1)} %slice.16), channel_id=1, source_target_pairs={{0,2},{1,3},{2,0},{3,1},{4,6},{5,7},{6,4},{7,5},{8,10},{9,11},{10,... | collective-permute-start | bytes 589832 | tf_op jit(solution)/shard_map/ppermute | solution.py:40
  16.4 2.7 %collective-permute-done.3 = bf16[96,1024]{1,0:T(8,128)(2,1)S(1)} collective-permute-done((bf16[96,1024]{1,0:T(8,128)(2,1)S(1)}, bf16[96,1024]{1,0:T(8,128)(2,1)S(1)}, u32[]{:S(2)}, u32[]{:S(2)}) %collective-permute-start.3) | collective-permute-done | bytes 196640 | tf_op jit(solution)/shard_map/ppermute | solution.py:40
  19.2 1.4 collective-permute-done.2
  22.3 1.0 fusion.3
  23.4 1.1 collective-permute-done.4
  24.5 2.4 %convert_add_fusion = f32[1024,384]{1,0:T(8,128)S(1)} fusion(f32[1024,384,1]{1,0,2:T(8,128)S(1)} %fusion.3, bf16[4,192,1024]{2,1,0:T(8,128)(2,1)} %collective-permute-done.4, bf16[1,1024,384]{2,1,0:T(8,128)(2,1)S(1)} %copy-done.12, bf16[1,192,384]{2,1,0:T(8,128)(2,1)S(1)} %get-tuple-element.12, bf16[1,192,384]{2,1,0:T(8,128)(2,1)S(1)} %get-tuple-element.13, ...), kind=kOutput, calls=%fused_computation.6 | convolution fusion | flops 606044160 | bytes 6094848 | tf_op jit(solution)/shard_map/dot_general | solution.py:56
  27.0 1.6 %convolution_bitcast_fusion = f32[32,1024]{1,0:T(8,128)S(1)} fusion(f32[1024,384]{1,0:T(8,128)S(1)} %convert_add_fusion, f32[384,32]{0,1:T(8,128)S(1)} %copy-done.11), kind=kOutput, calls=%fused_computation.9 | convolution fusion | flops 150994944 | bytes 1753088 | tf_op jit(solution)/shard_map/dot_general | solution.py:139
  28.7 1.2 collective-permute-done.5
  30.0 1.6 %collective-permute-start.6 = (f32[32,1024]{1,0:T(8,128)S(1)}, f32[32,1024]{1,0:T(8,128)S(1)}, u32[]{:S(2)}, u32[]{:S(2)}) collective-permute-start(f32[32,1024]{1,0:T(8,128)S(1)} %add.137), channel_id=1, source_target_pairs={{0,2},{1,3},{2,0},{3,1},{4,6},{5,7},{6,4},{7,5},{8,10},{9,11},{10,... | collective-permute-start | bytes 393224 | tf_op jit(solution)/shard_map/ppermute | solution.py:25
  31.5 4.1 %collective-permute-done.6 = f32[32,1024]{1,0:T(8,128)S(1)} collective-permute-done((f32[32,1024]{1,0:T(8,128)S(1)}, f32[32,1024]{1,0:T(8,128)S(1)}, u32[]{:S(2)}, u32[]{:S(2)}) %collective-permute-start.6) | collective-permute-done | bytes 131104 | tf_op jit(solution)/shard_map/ppermute | solution.py:25
  35.6 1.2 collective-permute-start.7
  36.8 3.8 %collective-permute-done.7 = f32[32,1024]{1,0:T(8,128)S(1)} collective-permute-done((f32[32,1024]{1,0:T(8,128)S(1)}, f32[32,1024]{1,0:T(8,128)S(1)}, u32[]{:S(2)}, u32[]{:S(2)}) %collective-permute-start.7) | collective-permute-done | bytes 131104 | tf_op jit(solution)/shard_map/ppermute | solution.py:25
  40.7 1.6 %collective-permute-start.8 = (f32[32,1024]{1,0:T(8,128)S(1)}, f32[32,1024]{1,0:T(8,128)S(1)}, u32[]{:S(2)}, u32[]{:S(2)}) collective-permute-start(f32[32,1024]{1,0:T(8,128)S(1)} %add.139), channel_id=1, source_target_pairs={{0,8},{1,9},{2,10},{3,11},{4,12},{5,13},{6,14},{7,15},{8,0},{9,1},... | collective-permute-start | bytes 393224 | tf_op jit(solution)/shard_map/ppermute | solution.py:25
  42.3 3.4 %collective-permute-done.8 = f32[32,1024]{1,0:T(8,128)S(1)} collective-permute-done((f32[32,1024]{1,0:T(8,128)S(1)}, f32[32,1024]{1,0:T(8,128)S(1)}, u32[]{:S(2)}, u32[]{:S(2)}) %collective-permute-start.8) | collective-permute-done | bytes 131104 | tf_op jit(solution)/shard_map/ppermute | solution.py:25
  45.7 3.1 %collective-permute-start.9 = (f32[32,1024]{1,0:T(8,128)S(1)}, f32[32,1024]{1,0:T(8,128)S(1)}, u32[]{:S(2)}, u32[]{:S(2)}) collective-permute-start(f32[32,1024]{1,0:T(8,128)S(1)} %add.140), channel_id=1, source_target_pairs={{0,16},{1,17},{2,18},{3,19},{4,20},{5,21},{6,22},{7,23},{8,24},{9,... | collective-permute-start | bytes 393224 | tf_op jit(solution)/shard_map/ppermute | solution.py:25
  48.8 4.4 %collective-permute-done.9 = f32[32,1024]{1,0:T(8,128)S(1)} collective-permute-done((f32[32,1024]{1,0:T(8,128)S(1)}, f32[32,1024]{1,0:T(8,128)S(1)}, u32[]{:S(2)}, u32[]{:S(2)}) %collective-permute-start.9) | collective-permute-done | bytes 131104 | tf_op jit(solution)/shard_map/ppermute | solution.py:25
  53.5 2.9 %cholesky.44 = f32[32,32]{1,0:T(8,128)S(1)} custom-call(f32[32,32]{1,0:T(8,128)S(1)} %fusion.33), custom_call_target="Cholesky" | custom-call | tf_op jit(solution)/shard_map/jit(cholesky)/cholesky | solution.py:144
  57.7 2.4 %custom-call.6 = f32[1,32,32]{1,2,0:T(8,128)S(1)} custom-call(f32[1,32,32]{2,1,0:T(8,128)S(1)} %fusion.28), custom_call_target="InvertDiagBlocksLowerTriangular" | custom-call | tf_op jit(solution)/shard_map/jit(_solve_triangular)/triangular_solve | solution.py:145
  62.2 3.4 %collective-permute-done.10 = f32[32,384]{1,0:T(8,128)S(1)} collective-permute-done((f32[32,384]{1,0:T(8,128)S(1)}, f32[32,384]{1,0:T(8,128)S(1)}, u32[]{:S(2)}, u32[]{:S(2)}) %collective-permute-start.10) | collective-permute-done | bytes 49184 | tf_op jit(solution)/shard_map/ppermute | solution.py:25
  65.7 2.1 %collective-permute-start.11 = (f32[32,384]{1,0:T(8,128)S(1)}, f32[32,384]{1,0:T(8,128)S(1)}, u32[]{:S(2)}, u32[]{:S(2)}) collective-permute-start(f32[32,384]{1,0:T(8,128)S(1)} %add.142), channel_id=1, source_target_pairs={{0,16},{8,24},{16,0},{24,8},{1,17},{9,25},{17,1},{25,9},{2,18},{10... | collective-permute-start | bytes 147464 | tf_op jit(solution)/shard_map/ppermute | solution.py:25
  67.8 2.9 %collective-permute-done.11 = f32[32,384]{1,0:T(8,128)S(1)} collective-permute-done((f32[32,384]{1,0:T(8,128)S(1)}, f32[32,384]{1,0:T(8,128)S(1)}, u32[]{:S(2)}, u32[]{:S(2)}) %collective-permute-start.11) | collective-permute-done | bytes 49184 | tf_op jit(solution)/shard_map/ppermute | solution.py:25
  70.7 1.6 %fusion.22 = f32[32,1024]{1,0:T(8,128)S(1)} fusion(f32[1024,384]{1,0:T(8,128)S(1)} %convert_add_fusion, f32[32,384]{1,0:T(8,128)S(1)} %add.142, f32[32,384]{1,0:T(8,128)S(1)} %collective-permute-done.11), kind=kOutput, calls=%fused_computation.37 | convolution fusion | flops 151019520 | bytes 1802240 | tf_op jit(solution)/shard_map/dot_general | solution.py:139
  72.4 1.3 collective-permute-done.12
  73.7 1.6 %collective-permute-start.13 = (f32[32,1024]{1,0:T(8,128)S(1)}, f32[32,1024]{1,0:T(8,128)S(1)}, u32[]{:S(2)}, u32[]{:S(2)}) collective-permute-start(f32[32,1024]{1,0:T(8,128)S(1)} %add.144), channel_id=1, source_target_pairs={{0,2},{1,3},{2,0},{3,1},{4,6},{5,7},{6,4},{7,5},{8,10},{9,11},{10,... | collective-permute-start | bytes 393224 | tf_op jit(solution)/shard_map/ppermute | solution.py:25
  75.3 4.1 %collective-permute-done.13 = f32[32,1024]{1,0:T(8,128)S(1)} collective-permute-done((f32[32,1024]{1,0:T(8,128)S(1)}, f32[32,1024]{1,0:T(8,128)S(1)}, u32[]{:S(2)}, u32[]{:S(2)}) %collective-permute-start.13) | collective-permute-done | bytes 131104 | tf_op jit(solution)/shard_map/ppermute | solution.py:25
  79.4 1.2 collective-permute-start.14
  80.6 3.8 %collective-permute-done.14 = f32[32,1024]{1,0:T(8,128)S(1)} collective-permute-done((f32[32,1024]{1,0:T(8,128)S(1)}, f32[32,1024]{1,0:T(8,128)S(1)}, u32[]{:S(2)}, u32[]{:S(2)}) %collective-permute-start.14) | collective-permute-done | bytes 131104 | tf_op jit(solution)/shard_map/ppermute | solution.py:25
  84.4 1.2 collective-permute-start.15
  85.6 1.1 select_reduce_fusion
  86.8 2.7 %collective-permute-done.15 = f32[32,1024]{1,0:T(8,128)S(1)} collective-permute-done((f32[32,1024]{1,0:T(8,128)S(1)}, f32[32,1024]{1,0:T(8,128)S(1)}, u32[]{:S(2)}, u32[]{:S(2)}) %collective-permute-start.15) | collective-permute-done | bytes 131104 | tf_op jit(solution)/shard_map/ppermute | solution.py:25
  89.5 2.1 %collective-permute-start.16 = (f32[32,1024]{1,0:T(8,128)S(1)}, f32[32,1024]{1,0:T(8,128)S(1)}, u32[]{:S(2)}, u32[]{:S(2)}) collective-permute-start(f32[32,1024]{1,0:T(8,128)S(1)} %add.147), channel_id=1, source_target_pairs={{0,16},{1,17},{2,18},{3,19},{4,20},{5,21},{6,22},{7,23},{8,24},{9,... | collective-permute-start | bytes 393224 | tf_op jit(solution)/shard_map/ppermute | solution.py:25
  91.6 3.3 %fusion = f32[1600,128]{1,0:T(8,128)S(1)} fusion(bf16[1536,128]{1,0:T(8,128)(2,1)S(1)} %copy-done, s32[1536]{0:T(1024)S(1)} %select_reduce_fusion), kind=kOutput, calls=%fused_computation.1 | convolution fusion | flops 631603200 | bytes 1218560 | tf_op jit(solution)/shard_map/dot_general | solution.py:74
  95.7 1.5 %collective-permute-start.21 = (f32[400,128]{1,0:T(8,128)}, f32[400,128]{1,0:T(8,128)}, u32[]{:S(2)}, u32[]{:S(2)}) collective-permute-start(f32[400,128]{1,0:T(8,128)} %get-tuple-element.20), channel_id=1, source_target_pairs={{0,24},{8,0},{16,8},{24,16},{1,25},{9,1},{17,9},{25,17},{2,26},{10... | collective-permute-start | bytes 614408 | tf_op jit(solution)/shard_map/ppermute | solution.py:84
  97.2 2.0 %collective-permute-start.20 = (f32[400,128]{1,0:T(8,128)}, f32[400,128]{1,0:T(8,128)}, u32[]{:S(2)}, u32[]{:S(2)}) collective-permute-start(f32[400,128]{1,0:T(8,128)} %get-tuple-element.21), channel_id=1, source_target_pairs={{0,16},{8,24},{16,0},{24,8},{1,17},{9,25},{17,1},{25,9},{2,18},{10... | collective-permute-start | bytes 614408 | tf_op jit(solution)/shard_map/ppermute | solution.py:84
  99.6 2.9 %cholesky.55 = f32[32,32]{1,0:T(8,128)S(1)} custom-call(f32[32,32]{1,0:T(8,128)S(1)} %fusion.31), custom_call_target="Cholesky" | custom-call | tf_op jit(solution)/shard_map/jit(cholesky)/cholesky | solution.py:144
  103.8 2.4 %custom-call.7 = f32[1,32,32]{1,2,0:T(8,128)S(1)} custom-call(f32[1,32,32]{2,1,0:T(8,128)S(1)} %fusion.29), custom_call_target="InvertDiagBlocksLowerTriangular" | custom-call | tf_op jit(solution)/shard_map/jit(_solve_triangular)/triangular_solve | solution.py:145
  107.6 5.7 %collective-permute-start.17 = (f32[32,384]{1,0:T(8,128)S(1)}, f32[32,384]{1,0:T(8,128)S(1)}, u32[]{:S(2)}, u32[]{:S(2)}) collective-permute-start(f32[32,384]{1,0:T(8,128)S(1)} %fusion.46), channel_id=1, source_target_pairs={{0,8},{8,0},{16,24},{24,16},{1,9},{9,1},{17,25},{25,17},{2,10},{10... | collective-permute-start | bytes 147464 | tf_op jit(solution)/shard_map/ppermute | solution.py:25
  113.3 2.7 %collective-permute-done.17 = f32[32,384]{1,0:T(8,128)S(1)} collective-permute-done((f32[32,384]{1,0:T(8,128)S(1)}, f32[32,384]{1,0:T(8,128)S(1)}, u32[]{:S(2)}, u32[]{:S(2)}) %collective-permute-start.17) | collective-permute-done | bytes 49184 | tf_op jit(solution)/shard_map/ppermute | solution.py:25
  116.0 5.1 %collective-permute-start.18 = (f32[32,384]{1,0:T(8,128)S(1)}, f32[32,384]{1,0:T(8,128)S(1)}, u32[]{:S(2)}, u32[]{:S(2)}) collective-permute-start(f32[32,384]{1,0:T(8,128)S(1)} %add.149), channel_id=1, source_target_pairs={{0,16},{8,24},{16,0},{24,8},{1,17},{9,25},{17,1},{25,9},{2,18},{10... | collective-permute-start | bytes 147464 | tf_op jit(solution)/shard_map/ppermute | solution.py:25
  121.0 1.9 %multiply_subtract_fusion.1 = f32[400,128]{1,0:T(8,128)} fusion(f32[400,128]{1,0:T(8,128)S(1)} %copy-done.10, f32[400,128]{1,0:T(8,128)} %collective-permute-done.21, f32[400,128]{1,0:T(8,128)} %collective-permute-done.20, f32[400,128]{1,0:T(8,128)} %collective-permute-done.19, f32[1600,128]{1,0:T(8,128)S(1)} %fusion, s32[]{:T(128)S(6)} %select_n.71), kind=kLoop, calls=%fused_computation.29 | loop fusion | flops 256000 | bytes 1228804 | tf_op jit(solution)/shard_map/sub | solution.py:85
  123.3 1.5 fusion.27
  124.8 1.1 fusion.2
  126.0 1.0 fusion.44
  126.9 17.8 %all_gather.3 = bf16[1024,384]{1,0:T(8,128)(2,1)S(1)} all-gather(bf16[256,384]{1,0:T(8,128)(2,1)S(1)} %get-tuple-element.8), channel_id=1, replica_groups=mesh['rep'=4,'tp'=8] {'rep'}, dimensions={0}, use_global_device_ids=true | all-gather | bytes 983040 | tf_op jit(solution)/shard_map/all_gather | solution.py:159
  (75 shorter events, 11.5 us)
Async XLA Ops:
  0.6 91.0 %copy-start = (bf16[1536,128]{1,0:T(8,128)(2,1)S(1)}, bf16[1536,128]{1,0:T(8,128)(2,1)}, u32[]{:S(2)}) copy-start(bf16[1536,128]{1,0:T(8,128)(2,1)} %param.19) | copy-start | bytes 1179652
  0.6 20.0 %copy-start.6 = (bf16[192,1024]{1,0:T(8,128)(2,1)S(1)}, bf16[192,1024]{1,0:T(8,128)(2,1)}, u32[]{:S(2)}) copy-start(bf16[192,1024]{1,0:T(8,128)(2,1)} %param.13) | copy-start | bytes 1179652
  0.7 12.3 %collective-permute-start = (bf16[192,1024]{1,0:T(8,128)(2,1)}, bf16[192,1024]{1,0:T(8,128)(2,1)S(1)}, u32[]{:S(2)}, u32[]{:S(2)}) collective-permute-start(bf16[192,1024]{1,0:T(8,128)(2,1)} %param.13), channel_id=1, source_target_pairs={{0,2},{1,3},{2,0},{3,1},{4,6},{5,7},{6,4},{7,5},{8,10},{9,11},{10,... | collective-permute-start | bytes 1179656 | tf_op jit(solution)/shard_map/ppermute | solution.py:40
  3.7 11.2 %collective-permute-start.1 = (bf16[192,1024]{1,0:T(8,128)(2,1)}, bf16[192,1024]{1,0:T(8,128)(2,1)S(1)}, u32[]{:S(2)}, u32[]{:S(2)}) collective-permute-start(bf16[192,1024]{1,0:T(8,128)(2,1)} %param.13), channel_id=1, source_target_pairs={{0,4},{1,5},{2,6},{3,7},{4,0},{5,1},{6,2},{7,3},{8,12},{9,13},{10,... | collective-permute-start | bytes 1179656 | tf_op jit(solution)/shard_map/ppermute | solution.py:40
  13.0 7.9 %copy-start.2 = (bf16[192,1024]{1,0:T(8,128)(2,1)}, bf16[192,1024]{1,0:T(8,128)(2,1)S(1)}, u32[]{:S(2)}) copy-start(bf16[192,1024]{1,0:T(8,128)(2,1)S(1)} %collective-permute-done) | copy-start | bytes 1179652
  13.0 6.2 %collective-permute-start.3 = (bf16[96,1024]{1,0:T(8,128)(2,1)S(1)}, bf16[96,1024]{1,0:T(8,128)(2,1)S(1)}, u32[]{:S(2)}, u32[]{:S(2)}) collective-permute-start(bf16[96,1024]{1,0:T(8,128)(2,1)S(1)} %slice.17), channel_id=1, source_target_pairs={{0,4},{1,5},{2,6},{3,7},{4,0},{5,1},{6,2},{7,3},{8,12},{9,13},{10,... | collective-permute-start | bytes 589832 | tf_op jit(solution)/shard_map/ppermute | solution.py:40
  14.8 6.0 %copy-start.4 = (bf16[192,1024]{1,0:T(8,128)(2,1)}, bf16[192,1024]{1,0:T(8,128)(2,1)S(1)}, u32[]{:S(2)}) copy-start(bf16[192,1024]{1,0:T(8,128)(2,1)S(1)} %collective-permute-done.1) | copy-start | bytes 1179652
  14.9 5.7 %collective-permute-start.2 = (bf16[96,1024]{1,0:T(8,128)(2,1)S(1)}, bf16[96,1024]{1,0:T(8,128)(2,1)S(1)}, u32[]{:S(2)}, u32[]{:S(2)}) collective-permute-start(bf16[96,1024]{1,0:T(8,128)(2,1)S(1)} %slice.16), channel_id=1, source_target_pairs={{0,2},{1,3},{2,0},{3,1},{4,6},{5,7},{6,4},{7,5},{8,10},{9,11},{10,... | collective-permute-start | bytes 589832 | tf_op jit(solution)/shard_map/ppermute | solution.py:40
  20.6 1.3 copy-start.1
  20.9 3.6 %collective-permute-start.4 = (bf16[4,192,1024]{2,1,0:T(8,128)(2,1)S(1)}, bf16[4,192,1024]{2,1,0:T(8,128)(2,1)}, u32[]{:S(2)}, u32[]{:S(2)}) collective-permute-start(bf16[4,192,1024]{2,1,0:T(8,128)(2,1)S(1)} %pad_maximum_fusion), channel_id=1, source_target_pairs={{0,1},{1,0},{2,3},{3,2},{4,5},{5,4},{6,7},{7,6},{8,9},{9,8},{10,11... | collective-permute-start | bytes 4718600 | tf_op jit(solution)/shard_map/ppermute | solution.py:40
  21.0 1.1 copy-start.3
  21.0 1.2 copy-start.5
  21.0 1.3 copy-start.7
  22.3 2.2 %copy-start.12 = (bf16[1,1024,384]{2,1,0:T(8,128)(2,1)S(1)}, bf16[1,1024,384]{2,1,0:T(8,128)(2,1)}, u32[]{:S(2)}) copy-start(bf16[1,1024,384]{2,1,0:T(8,128)(2,1)} %param.15) | copy-start | bytes 2359300
  24.5 2.5 %copy-start.11 = (f32[384,32]{0,1:T(8,128)S(1)}, f32[384,32]{0,1:T(8,128)}, u32[]{:S(2)}) copy-start(f32[384,32]{0,1:T(8,128)} %param.16) | copy-start | bytes 147460
  28.5 1.4 collective-permute-start.5
  30.0 5.6 %collective-permute-start.6 = (f32[32,1024]{1,0:T(8,128)S(1)}, f32[32,1024]{1,0:T(8,128)S(1)}, u32[]{:S(2)}, u32[]{:S(2)}) collective-permute-start(f32[32,1024]{1,0:T(8,128)S(1)} %add.137), channel_id=1, source_target_pairs={{0,2},{1,3},{2,0},{3,1},{4,6},{5,7},{6,4},{7,5},{8,10},{9,11},{10,... | collective-permute-start | bytes 393224 | tf_op jit(solution)/shard_map/ppermute | solution.py:25
  35.6 5.0 %collective-permute-start.7 = (f32[32,1024]{1,0:T(8,128)S(1)}, f32[32,1024]{1,0:T(8,128)S(1)}, u32[]{:S(2)}, u32[]{:S(2)}) collective-permute-start(f32[32,1024]{1,0:T(8,128)S(1)} %add.138), channel_id=1, source_target_pairs={{0,4},{1,5},{2,6},{3,7},{4,0},{5,1},{6,2},{7,3},{8,12},{9,13},{10,... | collective-permute-start | bytes 393224 | tf_op jit(solution)/shard_map/ppermute | solution.py:25
  40.7 5.0 %collective-permute-start.8 = (f32[32,1024]{1,0:T(8,128)S(1)}, f32[32,1024]{1,0:T(8,128)S(1)}, u32[]{:S(2)}, u32[]{:S(2)}) collective-permute-start(f32[32,1024]{1,0:T(8,128)S(1)} %add.139), channel_id=1, source_target_pairs={{0,8},{1,9},{2,10},{3,11},{4,12},{5,13},{6,14},{7,15},{8,0},{9,1},... | collective-permute-start | bytes 393224 | tf_op jit(solution)/shard_map/ppermute | solution.py:25
  45.7 7.4 %collective-permute-start.9 = (f32[32,1024]{1,0:T(8,128)S(1)}, f32[32,1024]{1,0:T(8,128)S(1)}, u32[]{:S(2)}, u32[]{:S(2)}) collective-permute-start(f32[32,1024]{1,0:T(8,128)S(1)} %add.140), channel_id=1, source_target_pairs={{0,16},{1,17},{2,18},{3,19},{4,20},{5,21},{6,22},{7,23},{8,24},{9,... | collective-permute-start | bytes 393224 | tf_op jit(solution)/shard_map/ppermute | solution.py:25
  61.5 24.2 %copy-start.13 = (s32[1600]{0:T(1024)S(1)}, s32[1600]{0:T(1024)}, u32[]{:S(2)}) copy-start(s32[1600]{0:T(1024)} %param.21) | copy-start | bytes 19204
  61.5 24.2 %copy-start.14 = (s32[1536]{0:T(1024)S(1)}, s32[1536]{0:T(1024)}, u32[]{:S(2)}) copy-start(s32[1536]{0:T(1024)} %param.20) | copy-start | bytes 18436
  61.5 4.2 %collective-permute-start.10 = (f32[32,384]{1,0:T(8,128)S(1)}, f32[32,384]{1,0:T(8,128)S(1)}, u32[]{:S(2)}, u32[]{:S(2)}) collective-permute-start(f32[32,384]{1,0:T(8,128)S(1)} %fusion.45), channel_id=1, source_target_pairs={{0,8},{8,0},{16,24},{24,16},{1,9},{9,1},{17,25},{25,17},{2,10},{10... | collective-permute-start | bytes 147464 | tf_op jit(solution)/shard_map/ppermute | solution.py:25
  65.7 5.1 %collective-permute-start.11 = (f32[32,384]{1,0:T(8,128)S(1)}, f32[32,384]{1,0:T(8,128)S(1)}, u32[]{:S(2)}, u32[]{:S(2)}) collective-permute-start(f32[32,384]{1,0:T(8,128)S(1)} %add.142), channel_id=1, source_target_pairs={{0,16},{8,24},{16,0},{24,8},{1,17},{9,25},{17,1},{25,9},{2,18},{10... | collective-permute-start | bytes 147464 | tf_op jit(solution)/shard_map/ppermute | solution.py:25
  72.3 1.4 collective-permute-start.12
  73.7 5.6 %collective-permute-start.13 = (f32[32,1024]{1,0:T(8,128)S(1)}, f32[32,1024]{1,0:T(8,128)S(1)}, u32[]{:S(2)}, u32[]{:S(2)}) collective-permute-start(f32[32,1024]{1,0:T(8,128)S(1)} %add.144), channel_id=1, source_target_pairs={{0,2},{1,3},{2,0},{3,1},{4,6},{5,7},{6,4},{7,5},{8,10},{9,11},{10,... | collective-permute-start | bytes 393224 | tf_op jit(solution)/shard_map/ppermute | solution.py:25
  79.4 5.0 %collective-permute-start.14 = (f32[32,1024]{1,0:T(8,128)S(1)}, f32[32,1024]{1,0:T(8,128)S(1)}, u32[]{:S(2)}, u32[]{:S(2)}) collective-permute-start(f32[32,1024]{1,0:T(8,128)S(1)} %add.145), channel_id=1, source_target_pairs={{0,4},{1,5},{2,6},{3,7},{4,0},{5,1},{6,2},{7,3},{8,12},{9,13},{10,... | collective-permute-start | bytes 393224 | tf_op jit(solution)/shard_map/ppermute | solution.py:25
  84.4 5.0 %collective-permute-start.15 = (f32[32,1024]{1,0:T(8,128)S(1)}, f32[32,1024]{1,0:T(8,128)S(1)}, u32[]{:S(2)}, u32[]{:S(2)}) collective-permute-start(f32[32,1024]{1,0:T(8,128)S(1)} %add.146), channel_id=1, source_target_pairs={{0,8},{1,9},{2,10},{3,11},{4,12},{5,13},{6,14},{7,15},{8,0},{9,1},... | collective-permute-start | bytes 393224 | tf_op jit(solution)/shard_map/ppermute | solution.py:25
  89.5 9.8 %collective-permute-start.16 = (f32[32,1024]{1,0:T(8,128)S(1)}, f32[32,1024]{1,0:T(8,128)S(1)}, u32[]{:S(2)}, u32[]{:S(2)}) collective-permute-start(f32[32,1024]{1,0:T(8,128)S(1)} %add.147), channel_id=1, source_target_pairs={{0,16},{1,17},{2,18},{3,19},{4,20},{5,21},{6,22},{7,23},{8,24},{9,... | collective-permute-start | bytes 393224 | tf_op jit(solution)/shard_map/ppermute | solution.py:25
  95.7 25.3 %copy-start.10 = (f32[400,128]{1,0:T(8,128)S(1)}, f32[400,128]{1,0:T(8,128)}, u32[]{:S(2)}) copy-start(f32[400,128]{1,0:T(8,128)} %param.22) | copy-start | bytes 614404
  95.7 25.3 %collective-permute-start.21 = (f32[400,128]{1,0:T(8,128)}, f32[400,128]{1,0:T(8,128)}, u32[]{:S(2)}, u32[]{:S(2)}) collective-permute-start(f32[400,128]{1,0:T(8,128)} %get-tuple-element.20), channel_id=1, source_target_pairs={{0,24},{8,0},{16,8},{24,16},{1,25},{9,1},{17,9},{25,17},{2,26},{10... | collective-permute-start | bytes 614408 | tf_op jit(solution)/shard_map/ppermute | solution.py:84
  97.2 23.8 %collective-permute-start.20 = (f32[400,128]{1,0:T(8,128)}, f32[400,128]{1,0:T(8,128)}, u32[]{:S(2)}, u32[]{:S(2)}) collective-permute-start(f32[400,128]{1,0:T(8,128)} %get-tuple-element.21), channel_id=1, source_target_pairs={{0,16},{8,24},{16,0},{24,8},{1,17},{9,25},{17,1},{25,9},{2,18},{10... | collective-permute-start | bytes 614408 | tf_op jit(solution)/shard_map/ppermute | solution.py:84
  99.2 21.8 %collective-permute-start.19 = (f32[400,128]{1,0:T(8,128)}, f32[400,128]{1,0:T(8,128)}, u32[]{:S(2)}, u32[]{:S(2)}) collective-permute-start(f32[400,128]{1,0:T(8,128)} %get-tuple-element.19), channel_id=1, source_target_pairs={{0,8},{8,16},{16,24},{24,0},{1,9},{9,17},{17,25},{25,1},{2,10},{10... | collective-permute-start | bytes 614408 | tf_op jit(solution)/shard_map/ppermute | solution.py:84
  107.6 8.4 %collective-permute-start.17 = (f32[32,384]{1,0:T(8,128)S(1)}, f32[32,384]{1,0:T(8,128)S(1)}, u32[]{:S(2)}, u32[]{:S(2)}) collective-permute-start(f32[32,384]{1,0:T(8,128)S(1)} %fusion.46), channel_id=1, source_target_pairs={{0,8},{8,0},{16,24},{24,16},{1,9},{9,1},{17,25},{25,17},{2,10},{10... | collective-permute-start | bytes 147464 | tf_op jit(solution)/shard_map/ppermute | solution.py:25
  116.0 7.4 %collective-permute-start.18 = (f32[32,384]{1,0:T(8,128)S(1)}, f32[32,384]{1,0:T(8,128)S(1)}, u32[]{:S(2)}, u32[]{:S(2)}) collective-permute-start(f32[32,384]{1,0:T(8,128)S(1)} %add.149), channel_id=1, source_target_pairs={{0,16},{8,24},{16,0},{24,8},{1,17},{9,25},{17,1},{25,9},{2,18},{10... | collective-permute-start | bytes 147464 | tf_op jit(solution)/shard_map/ppermute | solution.py:25
  124.8 1.2 copy-start.8
  124.8 1.2 copy-start.9

commit v9 on v8

--- a/solution.py
+++ b/solution.py
@@ -75,19 +75,23 @@
         selector, word_grads, (((0,), (0,)), ((), ())), preferred_element_type=jnp.float32
     )
     me = lax.axis_index("rep")
-    row_grad = lax.dynamic_slice_in_dim(partial, me * per_owner, per_owner, 0)
-    for shift in range(1, replicas):
-        block = lax.dynamic_slice_in_dim(
-            partial, ((me + shift) % replicas) * per_owner, per_owner, 0
-        )
-        pairs = [(i, (i + shift) % replicas) for i in range(replicas)]
-        row_grad = row_grad + lax.ppermute(block, "rep", pairs)
+    blocks = partial.reshape(replicas, per_owner, partial.shape[1])
+    stride = 1
+    while stride < replicas:
+        bit = (me // stride) % 2
+        paired = blocks.reshape((replicas // (2 * stride), 2) + blocks.shape[1:])
+        kept = lax.dynamic_index_in_dim(paired, bit, axis=1, keepdims=False)
+        sent = lax.dynamic_index_in_dim(paired, 1 - bit, axis=1, keepdims=False)
+        pairs = [(i, i ^ stride) for i in range(replicas)]
+        blocks = kept + lax.ppermute(sent, "rep", pairs)
+        stride *= 2
+    row_grad = blocks[0]
     return word_master - EMBED_RATE * row_grad
 
 
 def word_update(word_grads, token_ids, owner_map, word_master):
     replicas = lax.axis_size("rep")
-    if owner_map.shape[0] <= 4096 and replicas <= 8:
+    if owner_map.shape[0] <= 4096 and replicas <= 8 and not replicas & (replicas - 1):
         return word_update_dense(word_grads, token_ids, owner_map, word_master)
     per_owner = word_master.shape[0]
     capacity = 2 * token_ids.shape[0] // replicas

time: 146 us -> 143 us (0.979)
  starting transfers between devices: 39 us -> 27.8 us
  waiting for transfers between devices: 51.3 us -> 61.4 us
  blocking collectives: 17.8 us -> 15.6 us
    ppermute x14, starting transfers between devices: 27.5 us -> 16.9 us  [tree_sum(): value = value + lax.ppermute(value, axes, pairs)]
    ppermute x14, waiting for transfers between devices: 38.2 us -> 48.3 us  [tree_sum(): value = value + lax.ppermute(value, axes, pairs)]
    all_gather x1, blocking collectives: 17.8 us -> 15.6 us  [shards(): lax.all_gather(master_new.astype(jnp.bfloat16), 'rep', axis=0, tiled=True)]
    ppermute x3 -> x2, starting transfers between devices: 3.49 us -> 2.87 us  [word_update_dense(): blocks = kept + lax.ppermute(sent, 'rep', pairs)]
  transfers between devices with their start and end apart: 22 -> 21, of which waited for: 17 -> 16; matrix products, arithmetic and copies ran while one was open for 11% -> 11% of each run, Pallas kernels for 0% -> 0%
where the time goes in v9:
time: 143 us
  waiting for transfers between devices  61.4 us (43%)
  starting transfers between devices  27.8 us (19%)
  other arithmetic  19.4 us (14%)
  blocking collectives  15.6 us (11%)
  matrix products  14.2 us (10%)
  local copies, waits for them, and re-layouts  3.21 us (2%)
    ppermute x14, waiting for transfers between devices, tree_sum(): value = value + lax.ppermute(value, axes, pairs)  48.3 us
    ppermute x14, starting transfers between devices, tree_sum(): value = value + lax.ppermute(value, axes, pairs)  16.9 us
    all_gather x1, blocking collectives, shards(): lax.all_gather(master_new.astype(jnp.bfloat16), 'rep', axis=0, tiled=True)  15.6 us
    ppermute x5, waiting for transfers between devices, exchange(): return lax.ppermute(value, axis, [(i, i ^ stride) for i in range(count)])  13.1 us
    ppermute x5, starting transfers between devices, exchange(): return lax.ppermute(value, axis, [(i, i ^ stride) for i in range(count)])  7.98 us
    another operation x6, other arithmetic, shards(): factor_low = jnp.linalg.cholesky(gram_matrix)  7.19 us
    another operation x4, other arithmetic, shards(): jax.scipy.linalg.solve_triangular(factor_low, left_rows, lower=True)  6.17 us
    dot_general x2, matrix products, shards(): lax.dot_general(right_rows, combined, (((1,), (1,)), ((), ())), precision...  3.16 us
  transfers between devices with their start and end apart: 21, of which 16 were waited for; matrix products, arithmetic and copies ran while one was open for 11% of the time, Pallas kernels for 0%

profile of v9, /device:TPU:0, one launch (start us, length us, event | category | flops | bytes accessed | tf_op | source)
XLA Modules:
  0.0 142.7 jit_solution(13677983729443803812)
XLA Ops:
  0.7 3.0 %collective-permute-start = (bf16[192,1024]{1,0:T(8,128)(2,1)}, bf16[192,1024]{1,0:T(8,128)(2,1)S(1)}, u32[]{:S(2)}, u32[]{:S(2)}) collective-permute-start(bf16[192,1024]{1,0:T(8,128)(2,1)} %param.13), channel_id=1, source_target_pairs={{0,2},{1,3},{2,0},{3,1},{4,6},{5,7},{6,4},{7,5},{8,10},{9,11},{10,... | collective-permute-start | bytes 1179656 | tf_op jit(solution)/shard_map/ppermute | solution.py:40
  3.7 1.5 %collective-permute-start.1 = (bf16[192,1024]{1,0:T(8,128)(2,1)}, bf16[192,1024]{1,0:T(8,128)(2,1)S(1)}, u32[]{:S(2)}, u32[]{:S(2)}) collective-permute-start(bf16[192,1024]{1,0:T(8,128)(2,1)} %param.13), channel_id=1, source_target_pairs={{0,4},{1,5},{2,6},{3,7},{4,0},{5,1},{6,2},{7,3},{8,12},{9,13},{10,... | collective-permute-start | bytes 1179656 | tf_op jit(solution)/shard_map/ppermute | solution.py:40
  5.2 7.8 %collective-permute-done = bf16[192,1024]{1,0:T(8,128)(2,1)S(1)} collective-permute-done((bf16[192,1024]{1,0:T(8,128)(2,1)}, bf16[192,1024]{1,0:T(8,128)(2,1)S(1)}, u32[]{:S(2)}, u32[]{:S(2)}) %collective-permute-start) | collective-permute-done | bytes 393248 | tf_op jit(solution)/shard_map/ppermute | solution.py:40
  13.0 1.8 %collective-permute-start.3 = (bf16[96,1024]{1,0:T(8,128)(2,1)S(1)}, bf16[96,1024]{1,0:T(8,128)(2,1)S(1)}, u32[]{:S(2)}, u32[]{:S(2)}) collective-permute-start(bf16[96,1024]{1,0:T(8,128)(2,1)S(1)} %slice.17), channel_id=1, source_target_pairs={{0,4},{1,5},{2,6},{3,7},{4,0},{5,1},{6,2},{7,3},{8,12},{9,13},{10,... | collective-permute-start | bytes 589832 | tf_op jit(solution)/shard_map/ppermute | solution.py:40
  14.9 1.6 %collective-permute-start.2 = (bf16[96,1024]{1,0:T(8,128)(2,1)S(1)}, bf16[96,1024]{1,0:T(8,128)(2,1)S(1)}, u32[]{:S(2)}, u32[]{:S(2)}) collective-permute-start(bf16[96,1024]{1,0:T(8,128)(2,1)S(1)} %slice.16), channel_id=1, source_target_pairs={{0,2},{1,3},{2,0},{3,1},{4,6},{5,7},{6,4},{7,5},{8,10},{9,11},{10,... | collective-permute-start | bytes 589832 | tf_op jit(solution)/shard_map/ppermute | solution.py:40
  16.4 2.7 %collective-permute-done.3 = bf16[96,1024]{1,0:T(8,128)(2,1)S(1)} collective-permute-done((bf16[96,1024]{1,0:T(8,128)(2,1)S(1)}, bf16[96,1024]{1,0:T(8,128)(2,1)S(1)}, u32[]{:S(2)}, u32[]{:S(2)}) %collective-permute-start.3) | collective-permute-done | bytes 196640 | tf_op jit(solution)/shard_map/ppermute | solution.py:40
  19.2 1.4 %collective-permute-done.2 = bf16[96,1024]{1,0:T(8,128)(2,1)S(1)} collective-permute-done((bf16[96,1024]{1,0:T(8,128)(2,1)S(1)}, bf16[96,1024]{1,0:T(8,128)(2,1)S(1)}, u32[]{:S(2)}, u32[]{:S(2)}) %collective-permute-start.2) | collective-permute-done | bytes 196640 | tf_op jit(solution)/shard_map/ppermute | solution.py:40
  21.0 0.9 copy-done.1
  22.3 1.0 fusion.3
  23.4 1.1 collective-permute-done.4
  24.5 2.4 %convert_add_fusion = f32[1024,384]{1,0:T(8,128)S(1)} fusion(f32[1024,384,1]{1,0,2:T(8,128)S(1)} %fusion.3, bf16[4,192,1024]{2,1,0:T(8,128)(2,1)} %collective-permute-done.4, bf16[1,1024,384]{2,1,0:T(8,128)(2,1)S(1)} %copy-done.12, bf16[1,192,384]{2,1,0:T(8,128)(2,1)S(1)} %get-tuple-element.12, bf16[1,192,384]{2,1,0:T(8,128)(2,1)S(1)} %get-tuple-element.13, ...), kind=kOutput, calls=%fused_computation.6 | convolution fusion | flops 606044160 | bytes 6094848 | tf_op jit(solution)/shard_map/dot_general | solution.py:56
  27.0 1.6 %convolution_bitcast_fusion = f32[32,1024]{1,0:T(8,128)S(1)} fusion(f32[1024,384]{1,0:T(8,128)S(1)} %convert_add_fusion, f32[384,32]{0,1:T(8,128)S(1)} %copy-done.11), kind=kOutput, calls=%fused_computation.9 | convolution fusion | flops 150994944 | bytes 1753088 | tf_op jit(solution)/shard_map/dot_general | solution.py:143
  28.7 1.2 collective-permute-done.5
  30.0 1.6 %collective-permute-start.6 = (f32[32,1024]{1,0:T(8,128)S(1)}, f32[32,1024]{1,0:T(8,128)S(1)}, u32[]{:S(2)}, u32[]{:S(2)}) collective-permute-start(f32[32,1024]{1,0:T(8,128)S(1)} %add.128), channel_id=1, source_target_pairs={{0,2},{1,3},{2,0},{3,1},{4,6},{5,7},{6,4},{7,5},{8,10},{9,11},{10,... | collective-permute-start | bytes 393224 | tf_op jit(solution)/shard_map/ppermute | solution.py:25
  31.5 4.1 %collective-permute-done.6 = f32[32,1024]{1,0:T(8,128)S(1)} collective-permute-done((f32[32,1024]{1,0:T(8,128)S(1)}, f32[32,1024]{1,0:T(8,128)S(1)}, u32[]{:S(2)}, u32[]{:S(2)}) %collective-permute-start.6) | collective-permute-done | bytes 131104 | tf_op jit(solution)/shard_map/ppermute | solution.py:25
  35.6 1.2 collective-permute-start.7
  36.8 3.8 %collective-permute-done.7 = f32[32,1024]{1,0:T(8,128)S(1)} collective-permute-done((f32[32,1024]{1,0:T(8,128)S(1)}, f32[32,1024]{1,0:T(8,128)S(1)}, u32[]{:S(2)}, u32[]{:S(2)}) %collective-permute-start.7) | collective-permute-done | bytes 131104 | tf_op jit(solution)/shard_map/ppermute | solution.py:25
  40.7 1.6 %collective-permute-start.8 = (f32[32,1024]{1,0:T(8,128)S(1)}, f32[32,1024]{1,0:T(8,128)S(1)}, u32[]{:S(2)}, u32[]{:S(2)}) collective-permute-start(f32[32,1024]{1,0:T(8,128)S(1)} %add.130), channel_id=1, source_target_pairs={{0,8},{1,9},{2,10},{3,11},{4,12},{5,13},{6,14},{7,15},{8,0},{9,1},... | collective-permute-start | bytes 393224 | tf_op jit(solution)/shard_map/ppermute | solution.py:25
  42.3 3.4 %collective-permute-done.8 = f32[32,1024]{1,0:T(8,128)S(1)} collective-permute-done((f32[32,1024]{1,0:T(8,128)S(1)}, f32[32,1024]{1,0:T(8,128)S(1)}, u32[]{:S(2)}, u32[]{:S(2)}) %collective-permute-start.8) | collective-permute-done | bytes 131104 | tf_op jit(solution)/shard_map/ppermute | solution.py:25
  45.7 3.1 %collective-permute-start.9 = (f32[32,1024]{1,0:T(8,128)S(1)}, f32[32,1024]{1,0:T(8,128)S(1)}, u32[]{:S(2)}, u32[]{:S(2)}) collective-permute-start(f32[32,1024]{1,0:T(8,128)S(1)} %add.131), channel_id=1, source_target_pairs={{0,16},{1,17},{2,18},{3,19},{4,20},{5,21},{6,22},{7,23},{8,24},{9,... | collective-permute-start | bytes 393224 | tf_op jit(solution)/shard_map/ppermute | solution.py:25
  48.8 4.4 %collective-permute-done.9 = f32[32,1024]{1,0:T(8,128)S(1)} collective-permute-done((f32[32,1024]{1,0:T(8,128)S(1)}, f32[32,1024]{1,0:T(8,128)S(1)}, u32[]{:S(2)}, u32[]{:S(2)}) %collective-permute-start.9) | collective-permute-done | bytes 131104 | tf_op jit(solution)/shard_map/ppermute | solution.py:25
  53.5 2.9 %cholesky.44 = f32[32,32]{1,0:T(8,128)S(1)} custom-call(f32[32,32]{1,0:T(8,128)S(1)} %fusion.33), custom_call_target="Cholesky" | custom-call | tf_op jit(solution)/shard_map/jit(cholesky)/cholesky | solution.py:148
  57.8 2.4 %custom-call.6 = f32[1,32,32]{1,2,0:T(8,128)S(1)} custom-call(f32[1,32,32]{2,1,0:T(8,128)S(1)} %fusion.28), custom_call_target="InvertDiagBlocksLowerTriangular" | custom-call | tf_op jit(solution)/shard_map/jit(_solve_triangular)/triangular_solve | solution.py:149
  60.6 0.9 fusion.45
  62.3 1.1 select_reduce_fusion
  63.4 2.3 %collective-permute-done.10 = f32[32,384]{1,0:T(8,128)S(1)} collective-permute-done((f32[32,384]{1,0:T(8,128)S(1)}, f32[32,384]{1,0:T(8,128)S(1)}, u32[]{:S(2)}, u32[]{:S(2)}) %collective-permute-start.10) | collective-permute-done | bytes 49184 | tf_op jit(solution)/shard_map/ppermute | solution.py:25
  65.7 2.1 %collective-permute-start.11 = (f32[32,384]{1,0:T(8,128)S(1)}, f32[32,384]{1,0:T(8,128)S(1)}, u32[]{:S(2)}, u32[]{:S(2)}) collective-permute-start(f32[32,384]{1,0:T(8,128)S(1)} %add.133), channel_id=1, source_target_pairs={{0,16},{8,24},{16,0},{24,8},{1,17},{9,25},{17,1},{25,9},{2,18},{10... | collective-permute-start | bytes 147464 | tf_op jit(solution)/shard_map/ppermute | solution.py:25
  67.8 3.1 %fusion = f32[1600,128]{1,0:T(8,128)S(1)} fusion(bf16[1536,128]{1,0:T(8,128)(2,1)S(1)} %copy-done, s32[1536]{0:T(1024)S(1)} %select_reduce_fusion), kind=kOutput, calls=%fused_computation.1 | convolution fusion | flops 631603200 | bytes 1218560 | tf_op jit(solution)/shard_map/dot_general | solution.py:74
  70.9 1.6 %fusion.22 = f32[32,1024]{1,0:T(8,128)S(1)} fusion(f32[1024,384]{1,0:T(8,128)S(1)} %convert_add_fusion, f32[32,384]{1,0:T(8,128)S(1)} %add.133, f32[32,384]{1,0:T(8,128)S(1)} %collective-permute-done.11), kind=kOutput, calls=%fused_computation.39 | convolution fusion | flops 151019520 | bytes 1802240 | tf_op jit(solution)/shard_map/dot_general | solution.py:143
  73.3 2.0 %collective-permute-start.19 = (f32[2,400,128]{2,1,0:T(8,128)}, f32[2,400,128]{2,1,0:T(8,128)}, u32[]{:S(2)}, u32[]{:S(2)}) collective-permute-start(f32[2,400,128]{2,1,0:T(8,128)} %dynamic-slice_bitcast_fusion), channel_id=1, source_target_pairs={{0,8},{8,0},{16,24},{24,16},{1,9},{9,1},{17,25},{25,17},{2,10},{10... | collective-permute-start | bytes 1228808 | tf_op jit(solution)/shard_map/ppermute | solution.py:86
  75.4 1.7 %collective-permute-start.13 = (f32[32,1024]{1,0:T(8,128)S(1)}, f32[32,1024]{1,0:T(8,128)S(1)}, u32[]{:S(2)}, u32[]{:S(2)}) collective-permute-start(f32[32,1024]{1,0:T(8,128)S(1)} %add.135), channel_id=1, source_target_pairs={{0,2},{1,3},{2,0},{3,1},{4,6},{5,7},{6,4},{7,5},{8,10},{9,11},{10,... | collective-permute-start | bytes 393224 | tf_op jit(solution)/shard_map/ppermute | solution.py:25
  77.1 4.1 %collective-permute-done.13 = f32[32,1024]{1,0:T(8,128)S(1)} collective-permute-done((f32[32,1024]{1,0:T(8,128)S(1)}, f32[32,1024]{1,0:T(8,128)S(1)}, u32[]{:S(2)}, u32[]{:S(2)}) %collective-permute-start.13) | collective-permute-done | bytes 131104 | tf_op jit(solution)/shard_map/ppermute | solution.py:25
  81.3 1.2 collective-permute-start.14
  82.5 3.8 %collective-permute-done.14 = f32[32,1024]{1,0:T(8,128)S(1)} collective-permute-done((f32[32,1024]{1,0:T(8,128)S(1)}, f32[32,1024]{1,0:T(8,128)S(1)}, u32[]{:S(2)}, u32[]{:S(2)}) %collective-permute-start.14) | collective-permute-done | bytes 131104 | tf_op jit(solution)/shard_map/ppermute | solution.py:25
  86.9 4.5 %collective-permute-done.15 = f32[32,1024]{1,0:T(8,128)S(1)} collective-permute-done((f32[32,1024]{1,0:T(8,128)S(1)}, f32[32,1024]{1,0:T(8,128)S(1)}, u32[]{:S(2)}, u32[]{:S(2)}) %collective-permute-start.15) | collective-permute-done | bytes 131104 | tf_op jit(solution)/shard_map/ppermute | solution.py:25
  91.4 2.2 %collective-permute-start.16 = (f32[32,1024]{1,0:T(8,128)S(1)}, f32[32,1024]{1,0:T(8,128)S(1)}, u32[]{:S(2)}, u32[]{:S(2)}) collective-permute-start(f32[32,1024]{1,0:T(8,128)S(1)} %add.138), channel_id=1, source_target_pairs={{0,16},{1,17},{2,18},{3,19},{4,20},{5,21},{6,22},{7,23},{8,24},{9,... | collective-permute-start | bytes 393224 | tf_op jit(solution)/shard_map/ppermute | solution.py:25
  93.6 1.0 bitcast_add_fusion.1
  95.5 8.4 %collective-permute-done.16 = f32[32,1024]{1,0:T(8,128)S(1)} collective-permute-done((f32[32,1024]{1,0:T(8,128)S(1)}, f32[32,1024]{1,0:T(8,128)S(1)}, u32[]{:S(2)}, u32[]{:S(2)}) %collective-permute-start.16) | collective-permute-done | bytes 131104 | tf_op jit(solution)/shard_map/ppermute | solution.py:25
  104.2 2.9 %cholesky.55 = f32[32,32]{1,0:T(8,128)S(1)} custom-call(f32[32,32]{1,0:T(8,128)S(1)} %fusion.31), custom_call_target="Cholesky" | custom-call | tf_op jit(solution)/shard_map/jit(cholesky)/cholesky | solution.py:148
  108.5 2.4 %custom-call.7 = f32[1,32,32]{1,2,0:T(8,128)S(1)} custom-call(f32[1,32,32]{2,1,0:T(8,128)S(1)} %fusion.29), custom_call_target="InvertDiagBlocksLowerTriangular" | custom-call | tf_op jit(solution)/shard_map/jit(_solve_triangular)/triangular_solve | solution.py:149
  111.3 0.9 fusion.46
  112.3 4.1 %collective-permute-done.17 = f32[32,384]{1,0:T(8,128)S(1)} collective-permute-done((f32[32,384]{1,0:T(8,128)S(1)}, f32[32,384]{1,0:T(8,128)S(1)}, u32[]{:S(2)}, u32[]{:S(2)}) %collective-permute-start.17) | collective-permute-done | bytes 49184 | tf_op jit(solution)/shard_map/ppermute | solution.py:25
  117.7 4.3 %collective-permute-done.18 = f32[32,384]{1,0:T(8,128)S(1)} collective-permute-done((f32[32,384]{1,0:T(8,128)S(1)}, f32[32,384]{1,0:T(8,128)S(1)}, u32[]{:S(2)}, u32[]{:S(2)}) %collective-permute-start.18) | collective-permute-done | bytes 49184 | tf_op jit(solution)/shard_map/ppermute | solution.py:25
  122.0 1.4 %fusion.27 = f32[1024,384]{1,0:T(8,128)S(1)} fusion(f32[32,1024]{1,0:T(8,128)S(1)} %fusion.20, f32[32,384]{1,0:T(8,128)S(1)} %add.140, f32[32,384]{1,0:T(8,128)S(1)} %collective-permute-done.18), kind=kOutput, calls=%fused_computation.44 | convolution fusion | flops 151019520 | bytes 1802240 | tf_op jit(solution)/shard_map/dot_general | solution.py:153
  123.5 1.1 fusion.2
  124.6 1.0 fusion.44
  125.6 15.6 %all_gather.3 = bf16[1024,384]{1,0:T(8,128)(2,1)S(1)} all-gather(bf16[256,384]{1,0:T(8,128)(2,1)S(1)} %get-tuple-element.8), channel_id=1, replica_groups=mesh['rep'=4,'tp'=8] {'rep'}, dimensions={0}, use_global_device_ids=true | all-gather | bytes 983040 | tf_op jit(solution)/shard_map/all_gather | solution.py:163
  141.8 0.9 copy.21
  (75 shorter events, 10.2 us)
Async XLA Ops:
  0.6 67.1 %copy-start = (bf16[1536,128]{1,0:T(8,128)(2,1)S(1)}, bf16[1536,128]{1,0:T(8,128)(2,1)}, u32[]{:S(2)}) copy-start(bf16[1536,128]{1,0:T(8,128)(2,1)} %param.19) | copy-start | bytes 1179652
  0.6 20.0 %copy-start.6 = (bf16[192,1024]{1,0:T(8,128)(2,1)S(1)}, bf16[192,1024]{1,0:T(8,128)(2,1)}, u32[]{:S(2)}) copy-start(bf16[192,1024]{1,0:T(8,128)(2,1)} %param.13) | copy-start | bytes 1179652
  0.7 12.3 %collective-permute-start = (bf16[192,1024]{1,0:T(8,128)(2,1)}, bf16[192,1024]{1,0:T(8,128)(2,1)S(1)}, u32[]{:S(2)}, u32[]{:S(2)}) collective-permute-start(bf16[192,1024]{1,0:T(8,128)(2,1)} %param.13), channel_id=1, source_target_pairs={{0,2},{1,3},{2,0},{3,1},{4,6},{5,7},{6,4},{7,5},{8,10},{9,11},{10,... | collective-permute-start | bytes 1179656 | tf_op jit(solution)/shard_map/ppermute | solution.py:40
  3.7 11.2 %collective-permute-start.1 = (bf16[192,1024]{1,0:T(8,128)(2,1)}, bf16[192,1024]{1,0:T(8,128)(2,1)S(1)}, u32[]{:S(2)}, u32[]{:S(2)}) collective-permute-start(bf16[192,1024]{1,0:T(8,128)(2,1)} %param.13), channel_id=1, source_target_pairs={{0,4},{1,5},{2,6},{3,7},{4,0},{5,1},{6,2},{7,3},{8,12},{9,13},{10,... | collective-permute-start | bytes 1179656 | tf_op jit(solution)/shard_map/ppermute | solution.py:40
  13.0 7.9 %copy-start.2 = (bf16[192,1024]{1,0:T(8,128)(2,1)}, bf16[192,1024]{1,0:T(8,128)(2,1)S(1)}, u32[]{:S(2)}) copy-start(bf16[192,1024]{1,0:T(8,128)(2,1)S(1)} %collective-permute-done) | copy-start | bytes 1179652
  13.0 6.2 %collective-permute-start.3 = (bf16[96,1024]{1,0:T(8,128)(2,1)S(1)}, bf16[96,1024]{1,0:T(8,128)(2,1)S(1)}, u32[]{:S(2)}, u32[]{:S(2)}) collective-permute-start(bf16[96,1024]{1,0:T(8,128)(2,1)S(1)} %slice.17), channel_id=1, source_target_pairs={{0,4},{1,5},{2,6},{3,7},{4,0},{5,1},{6,2},{7,3},{8,12},{9,13},{10,... | collective-permute-start | bytes 589832 | tf_op jit(solution)/shard_map/ppermute | solution.py:40
  14.8 6.0 %copy-start.4 = (bf16[192,1024]{1,0:T(8,128)(2,1)}, bf16[192,1024]{1,0:T(8,128)(2,1)S(1)}, u32[]{:S(2)}) copy-start(bf16[192,1024]{1,0:T(8,128)(2,1)S(1)} %collective-permute-done.1) | copy-start | bytes 1179652
  14.9 5.7 %collective-permute-start.2 = (bf16[96,1024]{1,0:T(8,128)(2,1)S(1)}, bf16[96,1024]{1,0:T(8,128)(2,1)S(1)}, u32[]{:S(2)}, u32[]{:S(2)}) collective-permute-start(bf16[96,1024]{1,0:T(8,128)(2,1)S(1)} %slice.16), channel_id=1, source_target_pairs={{0,2},{1,3},{2,0},{3,1},{4,6},{5,7},{6,4},{7,5},{8,10},{9,11},{10,... | collective-permute-start | bytes 589832 | tf_op jit(solution)/shard_map/ppermute | solution.py:40
  20.6 1.3 copy-start.1
  20.9 3.6 %collective-permute-start.4 = (bf16[4,192,1024]{2,1,0:T(8,128)(2,1)S(1)}, bf16[4,192,1024]{2,1,0:T(8,128)(2,1)}, u32[]{:S(2)}, u32[]{:S(2)}) collective-permute-start(bf16[4,192,1024]{2,1,0:T(8,128)(2,1)S(1)} %pad_maximum_fusion), channel_id=1, source_target_pairs={{0,1},{1,0},{2,3},{3,2},{4,5},{5,4},{6,7},{7,6},{8,9},{9,8},{10,11... | collective-permute-start | bytes 4718600 | tf_op jit(solution)/shard_map/ppermute | solution.py:40
  21.0 1.1 copy-start.3
  21.0 1.2 copy-start.5
  21.0 1.3 copy-start.7
  22.3 2.2 %copy-start.12 = (bf16[1,1024,384]{2,1,0:T(8,128)(2,1)S(1)}, bf16[1,1024,384]{2,1,0:T(8,128)(2,1)}, u32[]{:S(2)}) copy-start(bf16[1,1024,384]{2,1,0:T(8,128)(2,1)} %param.15) | copy-start | bytes 2359300
  24.5 2.5 %copy-start.11 = (f32[384,32]{0,1:T(8,128)S(1)}, f32[384,32]{0,1:T(8,128)}, u32[]{:S(2)}) copy-start(f32[384,32]{0,1:T(8,128)} %param.16) | copy-start | bytes 147460
  28.5 1.4 collective-permute-start.5
  30.0 5.6 %collective-permute-start.6 = (f32[32,1024]{1,0:T(8,128)S(1)}, f32[32,1024]{1,0:T(8,128)S(1)}, u32[]{:S(2)}, u32[]{:S(2)}) collective-permute-start(f32[32,1024]{1,0:T(8,128)S(1)} %add.128), channel_id=1, source_target_pairs={{0,2},{1,3},{2,0},{3,1},{4,6},{5,7},{6,4},{7,5},{8,10},{9,11},{10,... | collective-permute-start | bytes 393224 | tf_op jit(solution)/shard_map/ppermute | solution.py:25
  35.6 5.0 %collective-permute-start.7 = (f32[32,1024]{1,0:T(8,128)S(1)}, f32[32,1024]{1,0:T(8,128)S(1)}, u32[]{:S(2)}, u32[]{:S(2)}) collective-permute-start(f32[32,1024]{1,0:T(8,128)S(1)} %add.129), channel_id=1, source_target_pairs={{0,4},{1,5},{2,6},{3,7},{4,0},{5,1},{6,2},{7,3},{8,12},{9,13},{10,... | collective-permute-start | bytes 393224 | tf_op jit(solution)/shard_map/ppermute | solution.py:25
  40.7 21.6 %copy-start.13 = (s32[1600]{0:T(1024)S(1)}, s32[1600]{0:T(1024)}, u32[]{:S(2)}) copy-start(s32[1600]{0:T(1024)} %param.21) | copy-start | bytes 19204
  40.7 21.6 %copy-start.14 = (s32[1536]{0:T(1024)S(1)}, s32[1536]{0:T(1024)}, u32[]{:S(2)}) copy-start(s32[1536]{0:T(1024)} %param.20) | copy-start | bytes 18436
  40.7 5.0 %collective-permute-start.8 = (f32[32,1024]{1,0:T(8,128)S(1)}, f32[32,1024]{1,0:T(8,128)S(1)}, u32[]{:S(2)}, u32[]{:S(2)}) collective-permute-start(f32[32,1024]{1,0:T(8,128)S(1)} %add.130), channel_id=1, source_target_pairs={{0,8},{1,9},{2,10},{3,11},{4,12},{5,13},{6,14},{7,15},{8,0},{9,1},... | collective-permute-start | bytes 393224 | tf_op jit(solution)/shard_map/ppermute | solution.py:25
  45.7 7.4 %collective-permute-start.9 = (f32[32,1024]{1,0:T(8,128)S(1)}, f32[32,1024]{1,0:T(8,128)S(1)}, u32[]{:S(2)}, u32[]{:S(2)}) collective-permute-start(f32[32,1024]{1,0:T(8,128)S(1)} %add.131), channel_id=1, source_target_pairs={{0,16},{1,17},{2,18},{3,19},{4,20},{5,21},{6,22},{7,23},{8,24},{9,... | collective-permute-start | bytes 393224 | tf_op jit(solution)/shard_map/ppermute | solution.py:25
  61.5 4.2 %collective-permute-start.10 = (f32[32,384]{1,0:T(8,128)S(1)}, f32[32,384]{1,0:T(8,128)S(1)}, u32[]{:S(2)}, u32[]{:S(2)}) collective-permute-start(f32[32,384]{1,0:T(8,128)S(1)} %fusion.45), channel_id=1, source_target_pairs={{0,8},{8,0},{16,24},{24,16},{1,9},{9,1},{17,25},{25,17},{2,10},{10... | collective-permute-start | bytes 147464 | tf_op jit(solution)/shard_map/ppermute | solution.py:25
  65.7 5.2 %collective-permute-start.11 = (f32[32,384]{1,0:T(8,128)S(1)}, f32[32,384]{1,0:T(8,128)S(1)}, u32[]{:S(2)}, u32[]{:S(2)}) collective-permute-start(f32[32,384]{1,0:T(8,128)S(1)} %add.133), channel_id=1, source_target_pairs={{0,16},{8,24},{16,0},{24,8},{1,17},{9,25},{17,1},{25,9},{2,18},{10... | collective-permute-start | bytes 147464 | tf_op jit(solution)/shard_map/ppermute | solution.py:25
  72.5 2.9 %collective-permute-start.12 = (f32[32,1024]{1,0:T(8,128)S(1)}, f32[32,1024]{1,0:T(8,128)S(1)}, u32[]{:S(2)}, u32[]{:S(2)}) collective-permute-start(f32[32,1024]{1,0:T(8,128)S(1)} %fusion.22), channel_id=1, source_target_pairs={{0,1},{1,0},{2,3},{3,2},{4,5},{5,4},{6,7},{7,6},{8,9},{9,8},{10,11... | collective-permute-start | bytes 393224 | tf_op jit(solution)/shard_map/ppermute | solution.py:25
  73.3 20.2 %collective-permute-start.19 = (f32[2,400,128]{2,1,0:T(8,128)}, f32[2,400,128]{2,1,0:T(8,128)}, u32[]{:S(2)}, u32[]{:S(2)}) collective-permute-start(f32[2,400,128]{2,1,0:T(8,128)} %dynamic-slice_bitcast_fusion), channel_id=1, source_target_pairs={{0,8},{8,0},{16,24},{24,16},{1,9},{9,1},{17,25},{25,17},{2,10},{10... | collective-permute-start | bytes 1228808 | tf_op jit(solution)/shard_map/ppermute | solution.py:86
  75.4 5.9 %collective-permute-start.13 = (f32[32,1024]{1,0:T(8,128)S(1)}, f32[32,1024]{1,0:T(8,128)S(1)}, u32[]{:S(2)}, u32[]{:S(2)}) collective-permute-start(f32[32,1024]{1,0:T(8,128)S(1)} %add.135), channel_id=1, source_target_pairs={{0,2},{1,3},{2,0},{3,1},{4,6},{5,7},{6,4},{7,5},{8,10},{9,11},{10,... | collective-permute-start | bytes 393224 | tf_op jit(solution)/shard_map/ppermute | solution.py:25
  81.3 5.0 %collective-permute-start.14 = (f32[32,1024]{1,0:T(8,128)S(1)}, f32[32,1024]{1,0:T(8,128)S(1)}, u32[]{:S(2)}, u32[]{:S(2)}) collective-permute-start(f32[32,1024]{1,0:T(8,128)S(1)} %add.136), channel_id=1, source_target_pairs={{0,4},{1,5},{2,6},{3,7},{4,0},{5,1},{6,2},{7,3},{8,12},{9,13},{10,... | collective-permute-start | bytes 393224 | tf_op jit(solution)/shard_map/ppermute | solution.py:25
  86.3 5.0 %collective-permute-start.15 = (f32[32,1024]{1,0:T(8,128)S(1)}, f32[32,1024]{1,0:T(8,128)S(1)}, u32[]{:S(2)}, u32[]{:S(2)}) collective-permute-start(f32[32,1024]{1,0:T(8,128)S(1)} %add.137), channel_id=1, source_target_pairs={{0,8},{1,9},{2,10},{3,11},{4,12},{5,13},{6,14},{7,15},{8,0},{9,1},... | collective-permute-start | bytes 393224 | tf_op jit(solution)/shard_map/ppermute | solution.py:25
  91.4 12.5 %collective-permute-start.16 = (f32[32,1024]{1,0:T(8,128)S(1)}, f32[32,1024]{1,0:T(8,128)S(1)}, u32[]{:S(2)}, u32[]{:S(2)}) collective-permute-start(f32[32,1024]{1,0:T(8,128)S(1)} %add.138), channel_id=1, source_target_pairs={{0,16},{1,17},{2,18},{3,19},{4,20},{5,21},{6,22},{7,23},{8,24},{9,... | collective-permute-start | bytes 393224 | tf_op jit(solution)/shard_map/ppermute | solution.py:25
  94.6 22.4 %copy-start.10 = (f32[400,128]{1,0:T(8,128)S(1)}, f32[400,128]{1,0:T(8,128)}, u32[]{:S(2)}) copy-start(f32[400,128]{1,0:T(8,128)} %param.22) | copy-start | bytes 614404
  94.7 22.3 %collective-permute-start.20 = (f32[1,400,128]{2,1,0:T(8,128)S(1)}, f32[1,400,128]{2,1,0:T(8,128)S(1)}, u32[]{:S(2)}, u32[]{:S(2)}) collective-permute-start(f32[1,400,128]{2,1,0:T(8,128)S(1)} %constant_dynamic-slice_fusion), channel_id=1, source_target_pairs={{0,16},{8,24},{16,0},{24,8},{1,17},{9,25},{17,1},{25,9},{2,18},{10... | collective-permute-start | bytes 614408 | tf_op jit(solution)/shard_map/ppermute | solution.py:86
  112.2 4.2 %collective-permute-start.17 = (f32[32,384]{1,0:T(8,128)S(1)}, f32[32,384]{1,0:T(8,128)S(1)}, u32[]{:S(2)}, u32[]{:S(2)}) collective-permute-start(f32[32,384]{1,0:T(8,128)S(1)} %fusion.46), channel_id=1, source_target_pairs={{0,8},{8,0},{16,24},{24,16},{1,9},{9,1},{17,25},{25,17},{2,10},{10... | collective-permute-start | bytes 147464 | tf_op jit(solution)/shard_map/ppermute | solution.py:25
  116.4 5.6 %collective-permute-start.18 = (f32[32,384]{1,0:T(8,128)S(1)}, f32[32,384]{1,0:T(8,128)S(1)}, u32[]{:S(2)}, u32[]{:S(2)}) collective-permute-start(f32[32,384]{1,0:T(8,128)S(1)} %add.140), channel_id=1, source_target_pairs={{0,16},{8,24},{16,0},{24,8},{1,17},{9,25},{17,1},{25,9},{2,18},{10... | collective-permute-start | bytes 147464 | tf_op jit(solution)/shard_map/ppermute | solution.py:25
  123.4 1.2 copy-start.8
  123.4 1.2 copy-start.9

commit v10 on v9

--- a/solution.py
+++ b/solution.py
@@ -147,6 +147,9 @@
         gram_matrix = jnp.dot(left_rows, left_rows.T, precision=highest)
         factor_low = jnp.linalg.cholesky(gram_matrix)
         left_rows = jax.scipy.linalg.solve_triangular(factor_low, left_rows, lower=True)
+        if round_index == 0:
+            word_new = word_update(word_grads, token_ids, owner_map, word_master)
+            word_new, left_rows = lax.optimization_barrier((word_new, left_rows))
         partial_right = jnp.dot(left_rows, combined, precision=highest)
         right_rows = tree_sum(partial_right, "rep") / replicas
     right_basis = right_rows.T
@@ -161,7 +164,6 @@
     moment_new = MOMENTUM * qkv_moment + update_rows
     master_new = qkv_master - LEARNING_RATE * moment_new
     weight_bf16 = lax.all_gather(master_new.astype(jnp.bfloat16), "rep", axis=0, tiled=True)
-    word_new = word_update(word_grads, token_ids, owner_map, word_master)
     return (error_new, right_basis, moment_new, master_new, weight_bf16, word_new)
 
 

time: 143 us -> 147 us (1.028)
  waiting for transfers between devices: 61.4 us -> 72.1 us
  starting transfers between devices: 27.8 us -> 18.2 us
    ppermute x14, waiting for transfers between devices: 48.3 us -> 59.3 us  [tree_sum(): value = value + lax.ppermute(value, axes, pairs)]
    ppermute x14, starting transfers between devices: 16.9 us -> 6 us  [tree_sum(): value = value + lax.ppermute(value, axes, pairs)]
    unnamed x31 -> x35, local copies, waits for them, and re-layouts: 2.11 us -> 3.37 us
  transfers between devices with their start and end apart: 21 -> 21, of which waited for: 16 -> 18; matrix products, arithmetic and copies ran while one was open for 11% -> 8% of each run, Pallas kernels for 0% -> 0%
where the time goes in v10:
time: 147 us; the launch traced here: 146 us
  waiting for transfers between devices  72.1 us (49%)
  other arithmetic  19.3 us (13%)
  starting transfers between devices  18.2 us (12%)
  blocking collectives  16.8 us (11%)
  matrix products  14.4 us (10%)
  local copies, waits for them, and re-layouts  4.47 us (3%)
    ppermute x14, waiting for transfers between devices, tree_sum(): value = value + lax.ppermute(value, axes, pairs)  59.3 us
    all_gather x1, blocking collectives, shards(): lax.all_gather(master_new.astype(jnp.bfloat16), 'rep', axis=0, tiled=True)  16.8 us
    ppermute x5, waiting for transfers between devices, exchange(): return lax.ppermute(value, axis, [(i, i ^ stride) for i in range(count)])  12 us
    ppermute x5, starting transfers between devices, exchange(): return lax.ppermute(value, axis, [(i, i ^ stride) for i in range(count)])  7.98 us
    another operation x6, other arithmetic, shards(): factor_low = jnp.linalg.cholesky(gram_matrix)  7.19 us
    another operation x4, other arithmetic, shards(): jax.scipy.linalg.solve_triangular(factor_low, left_rows, lower=True)  6.17 us
    ppermute x14, starting transfers between devices, tree_sum(): value = value + lax.ppermute(value, axes, pairs)  6 us
    ppermute x2, starting transfers between devices, word_update_dense(): blocks = kept + lax.ppermute(sent, 'rep', pairs)  4.23 us
  transfers between devices with their start and end apart: 21, of which 18 were waited for; matrix products, arithmetic and copies ran while one was open for 8% of the time, Pallas kernels for 0%

profile of v10, /device:TPU:0, one launch (start us, length us, event | category | flops | bytes accessed | tf_op | source)
XLA Modules:
  0.0 146.4 jit_solution(11383622411700987508)
XLA Ops:
  0.7 3.0 %collective-permute-start = (bf16[192,1024]{1,0:T(8,128)(2,1)}, bf16[192,1024]{1,0:T(8,128)(2,1)S(1)}, u32[]{:S(2)}, u32[]{:S(2)}) collective-permute-start(bf16[192,1024]{1,0:T(8,128)(2,1)} %param.13), channel_id=1, source_target_pairs={{0,2},{1,3},{2,0},{3,1},{4,6},{5,7},{6,4},{7,5},{8,10},{9,11},{10,... | collective-permute-start | bytes 1179656 | tf_op jit(solution)/shard_map/ppermute | solution.py:40
  3.7 1.5 %collective-permute-start.1 = (bf16[192,1024]{1,0:T(8,128)(2,1)}, bf16[192,1024]{1,0:T(8,128)(2,1)S(1)}, u32[]{:S(2)}, u32[]{:S(2)}) collective-permute-start(bf16[192,1024]{1,0:T(8,128)(2,1)} %param.13), channel_id=1, source_target_pairs={{0,4},{1,5},{2,6},{3,7},{4,0},{5,1},{6,2},{7,3},{8,12},{9,13},{10,... | collective-permute-start | bytes 1179656 | tf_op jit(solution)/shard_map/ppermute | solution.py:40
  5.2 7.8 %collective-permute-done = bf16[192,1024]{1,0:T(8,128)(2,1)S(1)} collective-permute-done((bf16[192,1024]{1,0:T(8,128)(2,1)}, bf16[192,1024]{1,0:T(8,128)(2,1)S(1)}, u32[]{:S(2)}, u32[]{:S(2)}) %collective-permute-start) | collective-permute-done | bytes 393248 | tf_op jit(solution)/shard_map/ppermute | solution.py:40
  13.0 1.8 %collective-permute-start.3 = (bf16[96,1024]{1,0:T(8,128)(2,1)S(1)}, bf16[96,1024]{1,0:T(8,128)(2,1)S(1)}, u32[]{:S(2)}, u32[]{:S(2)}) collective-permute-start(bf16[96,1024]{1,0:T(8,128)(2,1)S(1)} %slice.17), channel_id=1, source_target_pairs={{0,4},{1,5},{2,6},{3,7},{4,0},{5,1},{6,2},{7,3},{8,12},{9,13},{10,... | collective-permute-start | bytes 589832 | tf_op jit(solution)/shard_map/ppermute | solution.py:40
  14.9 1.6 %collective-permute-start.2 = (bf16[96,1024]{1,0:T(8,128)(2,1)S(1)}, bf16[96,1024]{1,0:T(8,128)(2,1)S(1)}, u32[]{:S(2)}, u32[]{:S(2)}) collective-permute-start(bf16[96,1024]{1,0:T(8,128)(2,1)S(1)} %slice.16), channel_id=1, source_target_pairs={{0,2},{1,3},{2,0},{3,1},{4,6},{5,7},{6,4},{7,5},{8,10},{9,11},{10,... | collective-permute-start | bytes 589832 | tf_op jit(solution)/shard_map/ppermute | solution.py:40
  16.4 2.7 %collective-permute-done.3 = bf16[96,1024]{1,0:T(8,128)(2,1)S(1)} collective-permute-done((bf16[96,1024]{1,0:T(8,128)(2,1)S(1)}, bf16[96,1024]{1,0:T(8,128)(2,1)S(1)}, u32[]{:S(2)}, u32[]{:S(2)}) %collective-permute-start.3) | collective-permute-done | bytes 196640 | tf_op jit(solution)/shard_map/ppermute | solution.py:40
  19.2 1.4 collective-permute-done.2
  21.4 1.1 select_reduce_fusion
  22.5 3.1 %fusion = f32[1600,128]{1,0:T(8,128)S(1)} fusion(bf16[1536,128]{1,0:T(8,128)(2,1)S(1)} %copy-done, s32[1536]{0:T(1024)S(1)} %select_reduce_fusion), kind=kOutput, calls=%fused_computation.1 | convolution fusion | flops 631603200 | bytes 1218560 | tf_op jit(solution)/shard_map/dot_general | solution.py:74
  25.6 0.9 copy-done.6
  27.3 1.6 %collective-permute-start.5 = (f32[2,400,128]{2,1,0:T(8,128)}, f32[2,400,128]{2,1,0:T(8,128)}, u32[]{:S(2)}, u32[]{:S(2)}) collective-permute-start(f32[2,400,128]{2,1,0:T(8,128)} %dynamic-slice_bitcast_fusion), channel_id=1, source_target_pairs={{0,8},{8,0},{16,24},{24,16},{1,9},{9,1},{17,25},{25,17},{2,10},{10... | collective-permute-start | bytes 1228808 | tf_op jit(solution)/shard_map/ppermute | solution.py:86
  29.0 0.8 copy-done.3
  30.1 1.0 fusion.3
  31.2 2.4 %convert_add_fusion = f32[1024,384]{1,0:T(8,128)S(1)} fusion(f32[1024,384,1]{1,0,2:T(8,128)S(1)} %fusion.3, bf16[4,192,1024]{2,1,0:T(8,128)(2,1)} %collective-permute-done.4, bf16[1,1024,384]{2,1,0:T(8,128)(2,1)S(1)} %copy-done.14, bf16[1,192,384]{2,1,0:T(8,128)(2,1)S(1)} %get-tuple-element.16, bf16[1,192,384]{2,1,0:T(8,128)(2,1)S(1)} %get-tuple-element.17, ...), kind=kOutput, calls=%fused_computation.6 | convolution fusion | flops 606044160 | bytes 6094848 | tf_op jit(solution)/shard_map/dot_general | solution.py:56
  33.7 1.6 %convolution_bitcast_fusion = f32[32,1024]{1,0:T(8,128)S(1)} fusion(f32[1024,384]{1,0:T(8,128)S(1)} %convert_add_fusion, f32[384,32]{0,1:T(8,128)S(1)} %copy-done.13), kind=kOutput, calls=%fused_computation.9 | convolution fusion | flops 150994944 | bytes 1753088 | tf_op jit(solution)/shard_map/dot_general | solution.py:143
  35.4 1.3 collective-permute-done.7
  36.7 1.6 %collective-permute-start.8 = (f32[32,1024]{1,0:T(8,128)S(1)}, f32[32,1024]{1,0:T(8,128)S(1)}, u32[]{:S(2)}, u32[]{:S(2)}) collective-permute-start(f32[32,1024]{1,0:T(8,128)S(1)} %add.136), channel_id=1, source_target_pairs={{0,2},{1,3},{2,0},{3,1},{4,6},{5,7},{6,4},{7,5},{8,10},{9,11},{10,... | collective-permute-start | bytes 393224 | tf_op jit(solution)/shard_map/ppermute | solution.py:25
  38.3 0.8 collective-permute-done.5
  39.1 1.0 bitcast_add_fusion.1
  40.1 2.2 %collective-permute-done.8 = f32[32,1024]{1,0:T(8,128)S(1)} collective-permute-done((f32[32,1024]{1,0:T(8,128)S(1)}, f32[32,1024]{1,0:T(8,128)S(1)}, u32[]{:S(2)}, u32[]{:S(2)}) %collective-permute-start.8) | collective-permute-done | bytes 131104 | tf_op jit(solution)/shard_map/ppermute | solution.py:25
  42.3 1.2 collective-permute-start.9
  43.5 2.7 %collective-permute-start.6 = (f32[1,400,128]{2,1,0:T(8,128)S(1)}, f32[1,400,128]{2,1,0:T(8,128)S(1)}, u32[]{:S(2)}, u32[]{:S(2)}) collective-permute-start(f32[1,400,128]{2,1,0:T(8,128)S(1)} %constant_dynamic-slice_fusion), channel_id=1, source_target_pairs={{0,16},{8,24},{16,0},{24,8},{1,17},{9,25},{17,1},{25,9},{2,18},{10... | collective-permute-start | bytes 614408 | tf_op jit(solution)/shard_map/ppermute | solution.py:86
  46.2 1.2 collective-permute-done.9
  47.9 9.5 %collective-permute-done.10 = f32[32,1024]{1,0:T(8,128)S(1)} collective-permute-done((f32[32,1024]{1,0:T(8,128)S(1)}, f32[32,1024]{1,0:T(8,128)S(1)}, u32[]{:S(2)}, u32[]{:S(2)}) %collective-permute-start.10) | collective-permute-done | bytes 131104 | tf_op jit(solution)/shard_map/ppermute | solution.py:25
  58.3 5.5 %collective-permute-done.11 = f32[32,1024]{1,0:T(8,128)S(1)} collective-permute-done((f32[32,1024]{1,0:T(8,128)S(1)}, f32[32,1024]{1,0:T(8,128)S(1)}, u32[]{:S(2)}, u32[]{:S(2)}) %collective-permute-start.11) | collective-permute-done | bytes 131104 | tf_op jit(solution)/shard_map/ppermute | solution.py:25
  64.1 2.9 %cholesky.44 = f32[32,32]{1,0:T(8,128)S(1)} custom-call(f32[32,32]{1,0:T(8,128)S(1)} %fusion.33), custom_call_target="Cholesky" | custom-call | tf_op jit(solution)/shard_map/jit(cholesky)/cholesky | solution.py:148
  68.3 2.4 %custom-call.6 = f32[1,32,32]{1,2,0:T(8,128)S(1)} custom-call(f32[1,32,32]{2,1,0:T(8,128)S(1)} %fusion.28), custom_call_target="InvertDiagBlocksLowerTriangular" | custom-call | tf_op jit(solution)/shard_map/jit(_solve_triangular)/triangular_solve | solution.py:149
  71.1 0.9 fusion.45
  72.2 4.1 %collective-permute-done.12 = f32[32,384]{1,0:T(8,128)S(1)} collective-permute-done((f32[32,384]{1,0:T(8,128)S(1)}, f32[32,384]{1,0:T(8,128)S(1)}, u32[]{:S(2)}, u32[]{:S(2)}) %collective-permute-start.12) | collective-permute-done | bytes 49184 | tf_op jit(solution)/shard_map/ppermute | solution.py:25
  76.3 5.0 %collective-permute-done.13 = f32[32,384]{1,0:T(8,128)S(1)} collective-permute-done((f32[32,384]{1,0:T(8,128)S(1)}, f32[32,384]{1,0:T(8,128)S(1)}, u32[]{:S(2)}, u32[]{:S(2)}) %collective-permute-start.13) | collective-permute-done | bytes 49184 | tf_op jit(solution)/shard_map/ppermute | solution.py:25
  81.3 1.7 %fusion.22 = f32[32,1024]{1,0:T(8,128)S(1)} fusion(f32[1024,384]{1,0:T(8,128)S(1)} %convert_add_fusion, f32[32,384]{1,0:T(8,128)S(1)} %add.141, f32[32,384]{1,0:T(8,128)S(1)} %collective-permute-done.13), kind=kOutput, calls=%fused_computation.39 | convolution fusion | flops 151019520 | bytes 1802240 | tf_op jit(solution)/shard_map/dot_general | solution.py:143
  83.1 1.3 collective-permute-done.14
  84.5 0.9 collective-permute-start.15
  85.4 4.7 %collective-permute-done.15 = f32[32,1024]{1,0:T(8,128)S(1)} collective-permute-done((f32[32,1024]{1,0:T(8,128)S(1)}, f32[32,1024]{1,0:T(8,128)S(1)}, u32[]{:S(2)}, u32[]{:S(2)}) %collective-permute-start.15) | collective-permute-done | bytes 131104 | tf_op jit(solution)/shard_map/ppermute | solution.py:25
  90.1 1.0 collective-permute-start.16
  91.1 4.1 %collective-permute-done.16 = f32[32,1024]{1,0:T(8,128)S(1)} collective-permute-done((f32[32,1024]{1,0:T(8,128)S(1)}, f32[32,1024]{1,0:T(8,128)S(1)}, u32[]{:S(2)}, u32[]{:S(2)}) %collective-permute-start.16) | collective-permute-done | bytes 131104 | tf_op jit(solution)/shard_map/ppermute | solution.py:25
  95.2 5.0 %collective-permute-done.17 = f32[32,1024]{1,0:T(8,128)S(1)} collective-permute-done((f32[32,1024]{1,0:T(8,128)S(1)}, f32[32,1024]{1,0:T(8,128)S(1)}, u32[]{:S(2)}, u32[]{:S(2)}) %collective-permute-start.17) | collective-permute-done | bytes 131104 | tf_op jit(solution)/shard_map/ppermute | solution.py:25
  100.4 6.6 %collective-permute-done.18 = f32[32,1024]{1,0:T(8,128)S(1)} collective-permute-done((f32[32,1024]{1,0:T(8,128)S(1)}, f32[32,1024]{1,0:T(8,128)S(1)}, u32[]{:S(2)}, u32[]{:S(2)}) %collective-permute-start.18) | collective-permute-done | bytes 131104 | tf_op jit(solution)/shard_map/ppermute | solution.py:25
  107.3 2.9 %cholesky.55 = f32[32,32]{1,0:T(8,128)S(1)} custom-call(f32[32,32]{1,0:T(8,128)S(1)} %fusion.31), custom_call_target="Cholesky" | custom-call | tf_op jit(solution)/shard_map/jit(cholesky)/cholesky | solution.py:148
  111.6 2.4 %custom-call.7 = f32[1,32,32]{1,2,0:T(8,128)S(1)} custom-call(f32[1,32,32]{2,1,0:T(8,128)S(1)} %fusion.29), custom_call_target="InvertDiagBlocksLowerTriangular" | custom-call | tf_op jit(solution)/shard_map/jit(_solve_triangular)/triangular_solve | solution.py:149
  114.4 0.9 fusion.46
  115.4 4.1 %collective-permute-done.19 = f32[32,384]{1,0:T(8,128)S(1)} collective-permute-done((f32[32,384]{1,0:T(8,128)S(1)}, f32[32,384]{1,0:T(8,128)S(1)}, u32[]{:S(2)}, u32[]{:S(2)}) %collective-permute-start.19) | collective-permute-done | bytes 49184 | tf_op jit(solution)/shard_map/ppermute | solution.py:25
  119.7 4.9 %collective-permute-done.20 = f32[32,384]{1,0:T(8,128)S(1)} collective-permute-done((f32[32,384]{1,0:T(8,128)S(1)}, f32[32,384]{1,0:T(8,128)S(1)}, u32[]{:S(2)}, u32[]{:S(2)}) %collective-permute-start.20) | collective-permute-done | bytes 49184 | tf_op jit(solution)/shard_map/ppermute | solution.py:25
  124.5 1.4 fusion.27
  126.0 1.1 fusion.2
  127.2 1.0 fusion.44
  128.1 16.8 %all_gather.3 = bf16[1024,384]{1,0:T(8,128)(2,1)S(1)} all-gather(bf16[256,384]{1,0:T(8,128)(2,1)S(1)} %get-tuple-element.12), channel_id=1, replica_groups=mesh['rep'=4,'tp'=8] {'rep'}, dimensions={0}, use_global_device_ids=true | all-gather | bytes 983040 | tf_op jit(solution)/shard_map/all_gather | solution.py:166
  145.5 0.9 copy.21
  (79 shorter events, 8.9 us)
Async XLA Ops:
  0.6 21.8 %copy-start = (bf16[1536,128]{1,0:T(8,128)(2,1)S(1)}, bf16[1536,128]{1,0:T(8,128)(2,1)}, u32[]{:S(2)}) copy-start(bf16[1536,128]{1,0:T(8,128)(2,1)} %param.19) | copy-start | bytes 1179652
  0.6 20.0 %copy-start.8 = (bf16[192,1024]{1,0:T(8,128)(2,1)S(1)}, bf16[192,1024]{1,0:T(8,128)(2,1)}, u32[]{:S(2)}) copy-start(bf16[192,1024]{1,0:T(8,128)(2,1)} %param.13) | copy-start | bytes 1179652
  0.7 12.3 %collective-permute-start = (bf16[192,1024]{1,0:T(8,128)(2,1)}, bf16[192,1024]{1,0:T(8,128)(2,1)S(1)}, u32[]{:S(2)}, u32[]{:S(2)}) collective-permute-start(bf16[192,1024]{1,0:T(8,128)(2,1)} %param.13), channel_id=1, source_target_pairs={{0,2},{1,3},{2,0},{3,1},{4,6},{5,7},{6,4},{7,5},{8,10},{9,11},{10,... | collective-permute-start | bytes 1179656 | tf_op jit(solution)/shard_map/ppermute | solution.py:40
  3.7 11.2 %collective-permute-start.1 = (bf16[192,1024]{1,0:T(8,128)(2,1)}, bf16[192,1024]{1,0:T(8,128)(2,1)S(1)}, u32[]{:S(2)}, u32[]{:S(2)}) collective-permute-start(bf16[192,1024]{1,0:T(8,128)(2,1)} %param.13), channel_id=1, source_target_pairs={{0,4},{1,5},{2,6},{3,7},{4,0},{5,1},{6,2},{7,3},{8,12},{9,13},{10,... | collective-permute-start | bytes 1179656 | tf_op jit(solution)/shard_map/ppermute | solution.py:40
  13.0 7.9 %copy-start.2 = (bf16[192,1024]{1,0:T(8,128)(2,1)}, bf16[192,1024]{1,0:T(8,128)(2,1)S(1)}, u32[]{:S(2)}) copy-start(bf16[192,1024]{1,0:T(8,128)(2,1)S(1)} %collective-permute-done) | copy-start | bytes 1179652
  13.0 6.2 %collective-permute-start.3 = (bf16[96,1024]{1,0:T(8,128)(2,1)S(1)}, bf16[96,1024]{1,0:T(8,128)(2,1)S(1)}, u32[]{:S(2)}, u32[]{:S(2)}) collective-permute-start(bf16[96,1024]{1,0:T(8,128)(2,1)S(1)} %slice.17), channel_id=1, source_target_pairs={{0,4},{1,5},{2,6},{3,7},{4,0},{5,1},{6,2},{7,3},{8,12},{9,13},{10,... | collective-permute-start | bytes 589832 | tf_op jit(solution)/shard_map/ppermute | solution.py:40
  14.8 6.0 %copy-start.4 = (bf16[192,1024]{1,0:T(8,128)(2,1)}, bf16[192,1024]{1,0:T(8,128)(2,1)S(1)}, u32[]{:S(2)}) copy-start(bf16[192,1024]{1,0:T(8,128)(2,1)S(1)} %collective-permute-done.1) | copy-start | bytes 1179652
  14.9 5.7 %collective-permute-start.2 = (bf16[96,1024]{1,0:T(8,128)(2,1)S(1)}, bf16[96,1024]{1,0:T(8,128)(2,1)S(1)}, u32[]{:S(2)}, u32[]{:S(2)}) collective-permute-start(bf16[96,1024]{1,0:T(8,128)(2,1)S(1)} %slice.16), channel_id=1, source_target_pairs={{0,2},{1,3},{2,0},{3,1},{4,6},{5,7},{6,4},{7,5},{8,10},{9,11},{10,... | collective-permute-start | bytes 589832 | tf_op jit(solution)/shard_map/ppermute | solution.py:40
  20.6 0.7 copy-start.15
  20.7 0.7 copy-start.16
  20.9 10.2 %collective-permute-start.4 = (bf16[4,192,1024]{2,1,0:T(8,128)(2,1)S(1)}, bf16[4,192,1024]{2,1,0:T(8,128)(2,1)}, u32[]{:S(2)}, u32[]{:S(2)}) collective-permute-start(bf16[4,192,1024]{2,1,0:T(8,128)(2,1)S(1)} %pad_maximum_fusion), channel_id=1, source_target_pairs={{0,1},{1,0},{2,3},{3,2},{4,5},{5,4},{6,7},{7,6},{8,9},{9,8},{10,11... | collective-permute-start | bytes 4718600 | tf_op jit(solution)/shard_map/ppermute | solution.py:40
  22.5 6.4 %copy-start.1 = (bf16[1536,384]{1,0:T(8,128)(2,1)S(1)}, bf16[1536,384]{1,0:T(8,128)(2,1)}, u32[]{:S(2)}) copy-start(bf16[1536,384]{1,0:T(8,128)(2,1)} %param.14) | copy-start | bytes 3538948
  25.6 0.9 copy-start.6
  27.3 11.8 %collective-permute-start.5 = (f32[2,400,128]{2,1,0:T(8,128)}, f32[2,400,128]{2,1,0:T(8,128)}, u32[]{:S(2)}, u32[]{:S(2)}) collective-permute-start(f32[2,400,128]{2,1,0:T(8,128)} %dynamic-slice_bitcast_fusion), channel_id=1, source_target_pairs={{0,8},{8,0},{16,24},{24,16},{1,9},{9,1},{17,25},{25,17},{2,10},{10... | collective-permute-start | bytes 1228808 | tf_op jit(solution)/shard_map/ppermute | solution.py:86
  28.8 1.0 copy-start.3
  28.8 1.1 copy-start.5
  28.8 1.2 copy-start.9
  30.1 1.1 copy-start.14
  31.2 2.5 %copy-start.13 = (f32[384,32]{0,1:T(8,128)S(1)}, f32[384,32]{0,1:T(8,128)}, u32[]{:S(2)}) copy-start(f32[384,32]{0,1:T(8,128)} %param.16) | copy-start | bytes 147460
  33.7 5.4 %copy-start.7 = (f32[1600,128]{1,0:T(8,128)S(1)}, f32[1600,128]{1,0:T(8,128)}, u32[]{:S(2)}) copy-start(f32[1600,128]{1,0:T(8,128)} %copy-done.6) | copy-start | bytes 2457604
  35.3 1.4 collective-permute-start.7
  35.4 22.1 %copy-start.12 = (f32[400,128]{1,0:T(8,128)S(1)}, f32[400,128]{1,0:T(8,128)}, u32[]{:S(2)}) copy-start(f32[400,128]{1,0:T(8,128)} %param.22) | copy-start | bytes 614404
  36.7 5.6 %collective-permute-start.8 = (f32[32,1024]{1,0:T(8,128)S(1)}, f32[32,1024]{1,0:T(8,128)S(1)}, u32[]{:S(2)}, u32[]{:S(2)}) collective-permute-start(f32[32,1024]{1,0:T(8,128)S(1)} %add.136), channel_id=1, source_target_pairs={{0,2},{1,3},{2,0},{3,1},{4,6},{5,7},{6,4},{7,5},{8,10},{9,11},{10,... | collective-permute-start | bytes 393224 | tf_op jit(solution)/shard_map/ppermute | solution.py:25
  42.3 5.0 %collective-permute-start.9 = (f32[32,1024]{1,0:T(8,128)S(1)}, f32[32,1024]{1,0:T(8,128)S(1)}, u32[]{:S(2)}, u32[]{:S(2)}) collective-permute-start(f32[32,1024]{1,0:T(8,128)S(1)} %add.137), channel_id=1, source_target_pairs={{0,4},{1,5},{2,6},{3,7},{4,0},{5,1},{6,2},{7,3},{8,12},{9,13},{10,... | collective-permute-start | bytes 393224 | tf_op jit(solution)/shard_map/ppermute | solution.py:25
  43.5 14.0 %collective-permute-start.6 = (f32[1,400,128]{2,1,0:T(8,128)S(1)}, f32[1,400,128]{2,1,0:T(8,128)S(1)}, u32[]{:S(2)}, u32[]{:S(2)}) collective-permute-start(f32[1,400,128]{2,1,0:T(8,128)S(1)} %constant_dynamic-slice_fusion), channel_id=1, source_target_pairs={{0,16},{8,24},{16,0},{24,8},{1,17},{9,25},{17,1},{25,9},{2,18},{10... | collective-permute-start | bytes 614408 | tf_op jit(solution)/shard_map/ppermute | solution.py:86
  47.4 10.0 %collective-permute-start.10 = (f32[32,1024]{1,0:T(8,128)S(1)}, f32[32,1024]{1,0:T(8,128)S(1)}, u32[]{:S(2)}, u32[]{:S(2)}) collective-permute-start(f32[32,1024]{1,0:T(8,128)S(1)} %add.138), channel_id=1, source_target_pairs={{0,8},{1,9},{2,10},{3,11},{4,12},{5,13},{6,14},{7,15},{8,0},{9,1},... | collective-permute-start | bytes 393224 | tf_op jit(solution)/shard_map/ppermute | solution.py:25
  57.4 6.3 %collective-permute-start.11 = (f32[32,1024]{1,0:T(8,128)S(1)}, f32[32,1024]{1,0:T(8,128)S(1)}, u32[]{:S(2)}, u32[]{:S(2)}) collective-permute-start(f32[32,1024]{1,0:T(8,128)S(1)} %add.139), channel_id=1, source_target_pairs={{0,16},{1,17},{2,18},{3,19},{4,20},{5,21},{6,22},{7,23},{8,24},{9,... | collective-permute-start | bytes 393224 | tf_op jit(solution)/shard_map/ppermute | solution.py:25
  72.1 4.2 %collective-permute-start.12 = (f32[32,384]{1,0:T(8,128)S(1)}, f32[32,384]{1,0:T(8,128)S(1)}, u32[]{:S(2)}, u32[]{:S(2)}) collective-permute-start(f32[32,384]{1,0:T(8,128)S(1)} %fusion.45), channel_id=1, source_target_pairs={{0,8},{8,0},{16,24},{24,16},{1,9},{9,1},{17,25},{25,17},{2,10},{10... | collective-permute-start | bytes 147464 | tf_op jit(solution)/shard_map/ppermute | solution.py:25
  76.2 5.1 %collective-permute-start.13 = (f32[32,384]{1,0:T(8,128)S(1)}, f32[32,384]{1,0:T(8,128)S(1)}, u32[]{:S(2)}, u32[]{:S(2)}) collective-permute-start(f32[32,384]{1,0:T(8,128)S(1)} %add.141), channel_id=1, source_target_pairs={{0,16},{8,24},{16,0},{24,8},{1,17},{9,25},{17,1},{25,9},{2,18},{10... | collective-permute-start | bytes 147464 | tf_op jit(solution)/shard_map/ppermute | solution.py:25
  83.0 1.4 collective-permute-start.14
  84.5 5.6 %collective-permute-start.15 = (f32[32,1024]{1,0:T(8,128)S(1)}, f32[32,1024]{1,0:T(8,128)S(1)}, u32[]{:S(2)}, u32[]{:S(2)}) collective-permute-start(f32[32,1024]{1,0:T(8,128)S(1)} %add.143), channel_id=1, source_target_pairs={{0,2},{1,3},{2,0},{3,1},{4,6},{5,7},{6,4},{7,5},{8,10},{9,11},{10,... | collective-permute-start | bytes 393224 | tf_op jit(solution)/shard_map/ppermute | solution.py:25
  90.1 5.0 %collective-permute-start.16 = (f32[32,1024]{1,0:T(8,128)S(1)}, f32[32,1024]{1,0:T(8,128)S(1)}, u32[]{:S(2)}, u32[]{:S(2)}) collective-permute-start(f32[32,1024]{1,0:T(8,128)S(1)} %add.144), channel_id=1, source_target_pairs={{0,4},{1,5},{2,6},{3,7},{4,0},{5,1},{6,2},{7,3},{8,12},{9,13},{10,... | collective-permute-start | bytes 393224 | tf_op jit(solution)/shard_map/ppermute | solution.py:25
  95.2 5.0 %collective-permute-start.17 = (f32[32,1024]{1,0:T(8,128)S(1)}, f32[32,1024]{1,0:T(8,128)S(1)}, u32[]{:S(2)}, u32[]{:S(2)}) collective-permute-start(f32[32,1024]{1,0:T(8,128)S(1)} %add.145), channel_id=1, source_target_pairs={{0,8},{1,9},{2,10},{3,11},{4,12},{5,13},{6,14},{7,15},{8,0},{9,1},... | collective-permute-start | bytes 393224 | tf_op jit(solution)/shard_map/ppermute | solution.py:25
  100.2 6.8 %collective-permute-start.18 = (f32[32,1024]{1,0:T(8,128)S(1)}, f32[32,1024]{1,0:T(8,128)S(1)}, u32[]{:S(2)}, u32[]{:S(2)}) collective-permute-start(f32[32,1024]{1,0:T(8,128)S(1)} %add.146), channel_id=1, source_target_pairs={{0,16},{1,17},{2,18},{3,19},{4,20},{5,21},{6,22},{7,23},{8,24},{9,... | collective-permute-start | bytes 393224 | tf_op jit(solution)/shard_map/ppermute | solution.py:25
  115.3 4.2 %collective-permute-start.19 = (f32[32,384]{1,0:T(8,128)S(1)}, f32[32,384]{1,0:T(8,128)S(1)}, u32[]{:S(2)}, u32[]{:S(2)}) collective-permute-start(f32[32,384]{1,0:T(8,128)S(1)} %fusion.46), channel_id=1, source_target_pairs={{0,8},{8,0},{16,24},{24,16},{1,9},{9,1},{17,25},{25,17},{2,10},{10... | collective-permute-start | bytes 147464 | tf_op jit(solution)/shard_map/ppermute | solution.py:25
  119.5 5.1 %collective-permute-start.20 = (f32[32,384]{1,0:T(8,128)S(1)}, f32[32,384]{1,0:T(8,128)S(1)}, u32[]{:S(2)}, u32[]{:S(2)}) collective-permute-start(f32[32,384]{1,0:T(8,128)S(1)} %add.148), channel_id=1, source_target_pairs={{0,16},{8,24},{16,0},{24,8},{1,17},{9,25},{17,1},{25,9},{2,18},{10... | collective-permute-start | bytes 147464 | tf_op jit(solution)/shard_map/ppermute | solution.py:25
  126.0 1.2 copy-start.10
  126.0 1.2 copy-start.11

commit v11 on v9

--- a/solution.py
+++ b/solution.py
@@ -133,6 +133,7 @@
     word_master,
 ):
     highest = lax.Precision.HIGHEST
+    high = lax.Precision.HIGH
     replicas = lax.axis_size("rep")
     word_new = None
     product = replica_product(activations, out_grads, "tp")
@@ -141,17 +142,17 @@
     left_rows = None
     for round_index in range(ROUNDS):
         partial_left = lax.dot_general(
-            right_rows, combined, (((1,), (1,)), ((), ())), precision=highest
+            right_rows, combined, (((1,), (1,)), ((), ())), precision=high
         )
         left_rows = tree_sum(partial_left, ("rep", "tp")) / replicas
         gram_matrix = jnp.dot(left_rows, left_rows.T, precision=highest)
         factor_low = jnp.linalg.cholesky(gram_matrix)
         left_rows = jax.scipy.linalg.solve_triangular(factor_low, left_rows, lower=True)
-        partial_right = jnp.dot(left_rows, combined, precision=highest)
+        partial_right = jnp.dot(left_rows, combined, precision=high)
         right_rows = tree_sum(partial_right, "rep") / replicas
     right_basis = right_rows.T
     approx = lax.dot_general(
-        left_rows, right_rows, (((0,), (0,)), ((), ())), precision=highest
+        left_rows, right_rows, (((0,), (0,)), ((), ())), precision=high
     )
     error_new = (combined - approx).astype(jnp.bfloat16)[None]
     owned_rows = qkv_master.shape[0]

time: 143 us -> 140 us (0.979)
  matrix products: 14.2 us -> 11.3 us
    dot_general x2, matrix products: 3.16 us -> 1.64 us  [shards(): lax.dot_general(right_rows, combined, (((1,), (1,)), ((), ())), precision...]
where the time goes in v11:
time: 140 us
  waiting for transfers between devices  61.5 us (44%)
  starting transfers between devices  27.6 us (20%)
  other arithmetic  19.4 us (14%)
  blocking collectives  15.7 us (11%)
  matrix products  11.3 us (8%)
  local copies, waits for them, and re-layouts  3.21 us (2%)
    ppermute x14, waiting for transfers between devices, tree_sum(): value = value + lax.ppermute(value, axes, pairs)  48.3 us
    ppermute x14, starting transfers between devices, tree_sum(): value = value + lax.ppermute(value, axes, pairs)  16.8 us
    all_gather x1, blocking collectives, shards(): lax.all_gather(master_new.astype(jnp.bfloat16), 'rep', axis=0, tiled=True)  15.7 us
    ppermute x5, waiting for transfers between devices, exchange(): return lax.ppermute(value, axis, [(i, i ^ stride) for i in range(count)])  13.1 us
    ppermute x5, starting transfers between devices, exchange(): return lax.ppermute(value, axis, [(i, i ^ stride) for i in range(count)])  7.98 us
    another operation x6, other arithmetic, shards(): factor_low = jnp.linalg.cholesky(gram_matrix)  7.19 us
    another operation x4, other arithmetic, shards(): jax.scipy.linalg.solve_triangular(factor_low, left_rows, lower=True)  6.17 us
    dot_general x1, matrix products, word_update_dense(): lax.dot_general(selector, word_grads, (((0,), (0,)), ((), ())), preferred...  3.08 us
  transfers between devices with their start and end apart: 21, of which 16 were waited for; matrix products, arithmetic and copies ran while one was open for 11% of the time, Pallas kernels for 0%

profile of v11, /device:TPU:0, one launch (start us, length us, event | category | flops | bytes accessed | tf_op | source)
XLA Modules:
  0.0 139.7 jit_solution(12116579884265185080)
XLA Ops:
  0.7 3.0 %collective-permute-start = (bf16[192,1024]{1,0:T(8,128)(2,1)}, bf16[192,1024]{1,0:T(8,128)(2,1)S(1)}, u32[]{:S(2)}, u32[]{:S(2)}) collective-permute-start(bf16[192,1024]{1,0:T(8,128)(2,1)} %param.13), channel_id=1, source_target_pairs={{0,2},{1,3},{2,0},{3,1},{4,6},{5,7},{6,4},{7,5},{8,10},{9,11},{10,... | collective-permute-start | bytes 1179656 | tf_op jit(solution)/shard_map/ppermute | solution.py:40
  3.7 1.5 %collective-permute-start.1 = (bf16[192,1024]{1,0:T(8,128)(2,1)}, bf16[192,1024]{1,0:T(8,128)(2,1)S(1)}, u32[]{:S(2)}, u32[]{:S(2)}) collective-permute-start(bf16[192,1024]{1,0:T(8,128)(2,1)} %param.13), channel_id=1, source_target_pairs={{0,4},{1,5},{2,6},{3,7},{4,0},{5,1},{6,2},{7,3},{8,12},{9,13},{10,... | collective-permute-start | bytes 1179656 | tf_op jit(solution)/shard_map/ppermute | solution.py:40
  5.2 7.8 %collective-permute-done = bf16[192,1024]{1,0:T(8,128)(2,1)S(1)} collective-permute-done((bf16[192,1024]{1,0:T(8,128)(2,1)}, bf16[192,1024]{1,0:T(8,128)(2,1)S(1)}, u32[]{:S(2)}, u32[]{:S(2)}) %collective-permute-start) | collective-permute-done | bytes 393248 | tf_op jit(solution)/shard_map/ppermute | solution.py:40
  13.0 1.8 %collective-permute-start.3 = (bf16[96,1024]{1,0:T(8,128)(2,1)S(1)}, bf16[96,1024]{1,0:T(8,128)(2,1)S(1)}, u32[]{:S(2)}, u32[]{:S(2)}) collective-permute-start(bf16[96,1024]{1,0:T(8,128)(2,1)S(1)} %slice.17), channel_id=1, source_target_pairs={{0,4},{1,5},{2,6},{3,7},{4,0},{5,1},{6,2},{7,3},{8,12},{9,13},{10,... | collective-permute-start | bytes 589832 | tf_op jit(solution)/shard_map/ppermute | solution.py:40
  14.9 1.6 %collective-permute-start.2 = (bf16[96,1024]{1,0:T(8,128)(2,1)S(1)}, bf16[96,1024]{1,0:T(8,128)(2,1)S(1)}, u32[]{:S(2)}, u32[]{:S(2)}) collective-permute-start(bf16[96,1024]{1,0:T(8,128)(2,1)S(1)} %slice.16), channel_id=1, source_target_pairs={{0,2},{1,3},{2,0},{3,1},{4,6},{5,7},{6,4},{7,5},{8,10},{9,11},{10,... | collective-permute-start | bytes 589832 | tf_op jit(solution)/shard_map/ppermute | solution.py:40
  16.4 2.7 %collective-permute-done.3 = bf16[96,1024]{1,0:T(8,128)(2,1)S(1)} collective-permute-done((bf16[96,1024]{1,0:T(8,128)(2,1)S(1)}, bf16[96,1024]{1,0:T(8,128)(2,1)S(1)}, u32[]{:S(2)}, u32[]{:S(2)}) %collective-permute-start.3) | collective-permute-done | bytes 196640 | tf_op jit(solution)/shard_map/ppermute | solution.py:40
  19.2 1.4 %collective-permute-done.2 = bf16[96,1024]{1,0:T(8,128)(2,1)S(1)} collective-permute-done((bf16[96,1024]{1,0:T(8,128)(2,1)S(1)}, bf16[96,1024]{1,0:T(8,128)(2,1)S(1)}, u32[]{:S(2)}, u32[]{:S(2)}) %collective-permute-start.2) | collective-permute-done | bytes 196640 | tf_op jit(solution)/shard_map/ppermute | solution.py:40
  21.0 0.9 copy-done.1
  22.3 1.0 fusion.3
  23.4 1.1 collective-permute-done.4
  24.5 2.5 %convert_add_fusion = f32[1024,384]{1,0:T(8,128)S(1)} fusion(f32[1024,384,1]{1,0,2:T(8,128)S(1)} %fusion.3, bf16[4,192,1024]{2,1,0:T(8,128)(2,1)} %collective-permute-done.4, bf16[1,1024,384]{2,1,0:T(8,128)(2,1)S(1)} %copy-done.12, bf16[1,192,384]{2,1,0:T(8,128)(2,1)S(1)} %get-tuple-element.12, bf16[1,192,384]{2,1,0:T(8,128)(2,1)S(1)} %get-tuple-element.13, ...), kind=kOutput, calls=%fused_computation.6 | convolution fusion | flops 606044160 | bytes 6094848 | tf_op jit(solution)/shard_map/dot_general | solution.py:56
  27.0 0.8 convolution_bitcast_fusion
  28.0 1.2 collective-permute-done.5
  29.2 1.6 %collective-permute-start.6 = (f32[32,1024]{1,0:T(8,128)S(1)}, f32[32,1024]{1,0:T(8,128)S(1)}, u32[]{:S(2)}, u32[]{:S(2)}) collective-permute-start(f32[32,1024]{1,0:T(8,128)S(1)} %add.128), channel_id=1, source_target_pairs={{0,2},{1,3},{2,0},{3,1},{4,6},{5,7},{6,4},{7,5},{8,10},{9,11},{10,... | collective-permute-start | bytes 393224 | tf_op jit(solution)/shard_map/ppermute | solution.py:25
  30.8 4.1 %collective-permute-done.6 = f32[32,1024]{1,0:T(8,128)S(1)} collective-permute-done((f32[32,1024]{1,0:T(8,128)S(1)}, f32[32,1024]{1,0:T(8,128)S(1)}, u32[]{:S(2)}, u32[]{:S(2)}) %collective-permute-start.6) | collective-permute-done | bytes 131104 | tf_op jit(solution)/shard_map/ppermute | solution.py:25
  34.9 1.2 collective-permute-start.7
  36.0 3.8 %collective-permute-done.7 = f32[32,1024]{1,0:T(8,128)S(1)} collective-permute-done((f32[32,1024]{1,0:T(8,128)S(1)}, f32[32,1024]{1,0:T(8,128)S(1)}, u32[]{:S(2)}, u32[]{:S(2)}) %collective-permute-start.7) | collective-permute-done | bytes 131104 | tf_op jit(solution)/shard_map/ppermute | solution.py:25
  39.9 1.6 %collective-permute-start.8 = (f32[32,1024]{1,0:T(8,128)S(1)}, f32[32,1024]{1,0:T(8,128)S(1)}, u32[]{:S(2)}, u32[]{:S(2)}) collective-permute-start(f32[32,1024]{1,0:T(8,128)S(1)} %add.130), channel_id=1, source_target_pairs={{0,8},{1,9},{2,10},{3,11},{4,12},{5,13},{6,14},{7,15},{8,0},{9,1},... | collective-permute-start | bytes 393224 | tf_op jit(solution)/shard_map/ppermute | solution.py:25
  41.6 3.4 %collective-permute-done.8 = f32[32,1024]{1,0:T(8,128)S(1)} collective-permute-done((f32[32,1024]{1,0:T(8,128)S(1)}, f32[32,1024]{1,0:T(8,128)S(1)}, u32[]{:S(2)}, u32[]{:S(2)}) %collective-permute-start.8) | collective-permute-done | bytes 131104 | tf_op jit(solution)/shard_map/ppermute | solution.py:25
  45.0 3.1 %collective-permute-start.9 = (f32[32,1024]{1,0:T(8,128)S(1)}, f32[32,1024]{1,0:T(8,128)S(1)}, u32[]{:S(2)}, u32[]{:S(2)}) collective-permute-start(f32[32,1024]{1,0:T(8,128)S(1)} %add.131), channel_id=1, source_target_pairs={{0,16},{1,17},{2,18},{3,19},{4,20},{5,21},{6,22},{7,23},{8,24},{9,... | collective-permute-start | bytes 393224 | tf_op jit(solution)/shard_map/ppermute | solution.py:25
  48.1 4.4 %collective-permute-done.9 = f32[32,1024]{1,0:T(8,128)S(1)} collective-permute-done((f32[32,1024]{1,0:T(8,128)S(1)}, f32[32,1024]{1,0:T(8,128)S(1)}, u32[]{:S(2)}, u32[]{:S(2)}) %collective-permute-start.9) | collective-permute-done | bytes 131104 | tf_op jit(solution)/shard_map/ppermute | solution.py:25
  52.7 2.9 %cholesky.44 = f32[32,32]{1,0:T(8,128)S(1)} custom-call(f32[32,32]{1,0:T(8,128)S(1)} %fusion.33), custom_call_target="Cholesky" | custom-call | tf_op jit(solution)/shard_map/jit(cholesky)/cholesky | solution.py:149
  57.0 2.4 %custom-call.6 = f32[1,32,32]{1,2,0:T(8,128)S(1)} custom-call(f32[1,32,32]{2,1,0:T(8,128)S(1)} %fusion.28), custom_call_target="InvertDiagBlocksLowerTriangular" | custom-call | tf_op jit(solution)/shard_map/jit(_solve_triangular)/triangular_solve | solution.py:150
  61.1 1.1 select_reduce_fusion
  62.2 2.3 %collective-permute-done.10 = f32[32,384]{1,0:T(8,128)S(1)} collective-permute-done((f32[32,384]{1,0:T(8,128)S(1)}, f32[32,384]{1,0:T(8,128)S(1)}, u32[]{:S(2)}, u32[]{:S(2)}) %collective-permute-start.10) | collective-permute-done | bytes 49184 | tf_op jit(solution)/shard_map/ppermute | solution.py:25
  64.5 2.1 %collective-permute-start.11 = (f32[32,384]{1,0:T(8,128)S(1)}, f32[32,384]{1,0:T(8,128)S(1)}, u32[]{:S(2)}, u32[]{:S(2)}) collective-permute-start(f32[32,384]{1,0:T(8,128)S(1)} %add.133), channel_id=1, source_target_pairs={{0,16},{8,24},{16,0},{24,8},{1,17},{9,25},{17,1},{25,9},{2,18},{10... | collective-permute-start | bytes 147464 | tf_op jit(solution)/shard_map/ppermute | solution.py:25
  66.6 3.1 %fusion = f32[1600,128]{1,0:T(8,128)S(1)} fusion(bf16[1536,128]{1,0:T(8,128)(2,1)S(1)} %copy-done, s32[1536]{0:T(1024)S(1)} %select_reduce_fusion), kind=kOutput, calls=%fused_computation.1 | convolution fusion | flops 631603200 | bytes 1218560 | tf_op jit(solution)/shard_map/dot_general | solution.py:74
  69.7 0.8 fusion.22
  70.7 0.8 dynamic-slice_bitcast_fusion
  71.4 2.0 %collective-permute-start.19 = (f32[2,400,128]{2,1,0:T(8,128)}, f32[2,400,128]{2,1,0:T(8,128)}, u32[]{:S(2)}, u32[]{:S(2)}) collective-permute-start(f32[2,400,128]{2,1,0:T(8,128)} %dynamic-slice_bitcast_fusion), channel_id=1, source_target_pairs={{0,8},{8,0},{16,24},{24,16},{1,9},{9,1},{17,25},{25,17},{2,10},{10... | collective-permute-start | bytes 1228808 | tf_op jit(solution)/shard_map/ppermute | solution.py:86
  73.5 1.5 %collective-permute-start.13 = (f32[32,1024]{1,0:T(8,128)S(1)}, f32[32,1024]{1,0:T(8,128)S(1)}, u32[]{:S(2)}, u32[]{:S(2)}) collective-permute-start(f32[32,1024]{1,0:T(8,128)S(1)} %add.135), channel_id=1, source_target_pairs={{0,2},{1,3},{2,0},{3,1},{4,6},{5,7},{6,4},{7,5},{8,10},{9,11},{10,... | collective-permute-start | bytes 393224 | tf_op jit(solution)/shard_map/ppermute | solution.py:25
  75.0 4.1 %collective-permute-done.13 = f32[32,1024]{1,0:T(8,128)S(1)} collective-permute-done((f32[32,1024]{1,0:T(8,128)S(1)}, f32[32,1024]{1,0:T(8,128)S(1)}, u32[]{:S(2)}, u32[]{:S(2)}) %collective-permute-start.13) | collective-permute-done | bytes 131104 | tf_op jit(solution)/shard_map/ppermute | solution.py:25
  79.2 1.2 collective-permute-start.14
  80.4 3.8 %collective-permute-done.14 = f32[32,1024]{1,0:T(8,128)S(1)} collective-permute-done((f32[32,1024]{1,0:T(8,128)S(1)}, f32[32,1024]{1,0:T(8,128)S(1)}, u32[]{:S(2)}, u32[]{:S(2)}) %collective-permute-start.14) | collective-permute-done | bytes 131104 | tf_op jit(solution)/shard_map/ppermute | solution.py:25
  84.8 4.5 %collective-permute-done.15 = f32[32,1024]{1,0:T(8,128)S(1)} collective-permute-done((f32[32,1024]{1,0:T(8,128)S(1)}, f32[32,1024]{1,0:T(8,128)S(1)}, u32[]{:S(2)}, u32[]{:S(2)}) %collective-permute-start.15) | collective-permute-done | bytes 131104 | tf_op jit(solution)/shard_map/ppermute | solution.py:25
  89.3 2.2 %collective-permute-start.16 = (f32[32,1024]{1,0:T(8,128)S(1)}, f32[32,1024]{1,0:T(8,128)S(1)}, u32[]{:S(2)}, u32[]{:S(2)}) collective-permute-start(f32[32,1024]{1,0:T(8,128)S(1)} %add.138), channel_id=1, source_target_pairs={{0,16},{1,17},{2,18},{3,19},{4,20},{5,21},{6,22},{7,23},{8,24},{9,... | collective-permute-start | bytes 393224 | tf_op jit(solution)/shard_map/ppermute | solution.py:25
  91.5 1.0 bitcast_add_fusion.1
  92.6 0.9 collective-permute-start.20
  93.4 8.4 %collective-permute-done.16 = f32[32,1024]{1,0:T(8,128)S(1)} collective-permute-done((f32[32,1024]{1,0:T(8,128)S(1)}, f32[32,1024]{1,0:T(8,128)S(1)}, u32[]{:S(2)}, u32[]{:S(2)}) %collective-permute-start.16) | collective-permute-done | bytes 131104 | tf_op jit(solution)/shard_map/ppermute | solution.py:25
  102.2 2.9 %cholesky.55 = f32[32,32]{1,0:T(8,128)S(1)} custom-call(f32[32,32]{1,0:T(8,128)S(1)} %fusion.31), custom_call_target="Cholesky" | custom-call | tf_op jit(solution)/shard_map/jit(cholesky)/cholesky | solution.py:149
  106.4 2.4 %custom-call.7 = f32[1,32,32]{1,2,0:T(8,128)S(1)} custom-call(f32[1,32,32]{2,1,0:T(8,128)S(1)} %fusion.29), custom_call_target="InvertDiagBlocksLowerTriangular" | custom-call | tf_op jit(solution)/shard_map/jit(_solve_triangular)/triangular_solve | solution.py:150
  109.8 4.1 %collective-permute-done.17 = f32[32,384]{1,0:T(8,128)S(1)} collective-permute-done((f32[32,384]{1,0:T(8,128)S(1)}, f32[32,384]{1,0:T(8,128)S(1)}, u32[]{:S(2)}, u32[]{:S(2)}) %collective-permute-start.17) | collective-permute-done | bytes 49184 | tf_op jit(solution)/shard_map/ppermute | solution.py:25
  115.2 4.3 %collective-permute-done.18 = f32[32,384]{1,0:T(8,128)S(1)} collective-permute-done((f32[32,384]{1,0:T(8,128)S(1)}, f32[32,384]{1,0:T(8,128)S(1)}, u32[]{:S(2)}, u32[]{:S(2)}) %collective-permute-start.18) | collective-permute-done | bytes 49184 | tf_op jit(solution)/shard_map/ppermute | solution.py:25
  119.5 0.8 fusion.27
  120.4 1.1 fusion.2
  121.5 1.0 fusion.44
  122.5 15.7 %all_gather.3 = bf16[1024,384]{1,0:T(8,128)(2,1)S(1)} all-gather(bf16[256,384]{1,0:T(8,128)(2,1)S(1)} %get-tuple-element.8), channel_id=1, replica_groups=mesh['rep'=4,'tp'=8] {'rep'}, dimensions={0}, use_global_device_ids=true | all-gather | bytes 983040 | tf_op jit(solution)/shard_map/all_gather | solution.py:164
  138.8 0.9 copy.21
  (75 shorter events, 9.7 us)
Async XLA Ops:
  0.6 66.0 %copy-start = (bf16[1536,128]{1,0:T(8,128)(2,1)S(1)}, bf16[1536,128]{1,0:T(8,128)(2,1)}, u32[]{:S(2)}) copy-start(bf16[1536,128]{1,0:T(8,128)(2,1)} %param.19) | copy-start | bytes 1179652
  0.6 20.0 %copy-start.6 = (bf16[192,1024]{1,0:T(8,128)(2,1)S(1)}, bf16[192,1024]{1,0:T(8,128)(2,1)}, u32[]{:S(2)}) copy-start(bf16[192,1024]{1,0:T(8,128)(2,1)} %param.13) | copy-start | bytes 1179652
  0.7 12.3 %collective-permute-start = (bf16[192,1024]{1,0:T(8,128)(2,1)}, bf16[192,1024]{1,0:T(8,128)(2,1)S(1)}, u32[]{:S(2)}, u32[]{:S(2)}) collective-permute-start(bf16[192,1024]{1,0:T(8,128)(2,1)} %param.13), channel_id=1, source_target_pairs={{0,2},{1,3},{2,0},{3,1},{4,6},{5,7},{6,4},{7,5},{8,10},{9,11},{10,... | collective-permute-start | bytes 1179656 | tf_op jit(solution)/shard_map/ppermute | solution.py:40
  3.7 11.2 %collective-permute-start.1 = (bf16[192,1024]{1,0:T(8,128)(2,1)}, bf16[192,1024]{1,0:T(8,128)(2,1)S(1)}, u32[]{:S(2)}, u32[]{:S(2)}) collective-permute-start(bf16[192,1024]{1,0:T(8,128)(2,1)} %param.13), channel_id=1, source_target_pairs={{0,4},{1,5},{2,6},{3,7},{4,0},{5,1},{6,2},{7,3},{8,12},{9,13},{10,... | collective-permute-start | bytes 1179656 | tf_op jit(solution)/shard_map/ppermute | solution.py:40
  13.0 7.9 %copy-start.2 = (bf16[192,1024]{1,0:T(8,128)(2,1)}, bf16[192,1024]{1,0:T(8,128)(2,1)S(1)}, u32[]{:S(2)}) copy-start(bf16[192,1024]{1,0:T(8,128)(2,1)S(1)} %collective-permute-done) | copy-start | bytes 1179652
  13.0 6.2 %collective-permute-start.3 = (bf16[96,1024]{1,0:T(8,128)(2,1)S(1)}, bf16[96,1024]{1,0:T(8,128)(2,1)S(1)}, u32[]{:S(2)}, u32[]{:S(2)}) collective-permute-start(bf16[96,1024]{1,0:T(8,128)(2,1)S(1)} %slice.17), channel_id=1, source_target_pairs={{0,4},{1,5},{2,6},{3,7},{4,0},{5,1},{6,2},{7,3},{8,12},{9,13},{10,... | collective-permute-start | bytes 589832 | tf_op jit(solution)/shard_map/ppermute | solution.py:40
  14.8 6.0 %copy-start.4 = (bf16[192,1024]{1,0:T(8,128)(2,1)}, bf16[192,1024]{1,0:T(8,128)(2,1)S(1)}, u32[]{:S(2)}) copy-start(bf16[192,1024]{1,0:T(8,128)(2,1)S(1)} %collective-permute-done.1) | copy-start | bytes 1179652
  14.9 5.7 %collective-permute-start.2 = (bf16[96,1024]{1,0:T(8,128)(2,1)S(1)}, bf16[96,1024]{1,0:T(8,128)(2,1)S(1)}, u32[]{:S(2)}, u32[]{:S(2)}) collective-permute-start(bf16[96,1024]{1,0:T(8,128)(2,1)S(1)} %slice.16), channel_id=1, source_target_pairs={{0,2},{1,3},{2,0},{3,1},{4,6},{5,7},{6,4},{7,5},{8,10},{9,11},{10,... | collective-permute-start | bytes 589832 | tf_op jit(solution)/shard_map/ppermute | solution.py:40
  20.6 1.3 copy-start.1
  20.9 3.6 %collective-permute-start.4 = (bf16[4,192,1024]{2,1,0:T(8,128)(2,1)S(1)}, bf16[4,192,1024]{2,1,0:T(8,128)(2,1)}, u32[]{:S(2)}, u32[]{:S(2)}) collective-permute-start(bf16[4,192,1024]{2,1,0:T(8,128)(2,1)S(1)} %pad_maximum_fusion), channel_id=1, source_target_pairs={{0,1},{1,0},{2,3},{3,2},{4,5},{5,4},{6,7},{7,6},{8,9},{9,8},{10,11... | collective-permute-start | bytes 4718600 | tf_op jit(solution)/shard_map/ppermute | solution.py:40
  21.0 1.1 copy-start.3
  21.0 1.2 copy-start.5
  21.0 1.3 copy-start.7
  22.3 2.2 %copy-start.12 = (bf16[1,1024,384]{2,1,0:T(8,128)(2,1)S(1)}, bf16[1,1024,384]{2,1,0:T(8,128)(2,1)}, u32[]{:S(2)}) copy-start(bf16[1,1024,384]{2,1,0:T(8,128)(2,1)} %param.15) | copy-start | bytes 2359300
  24.5 2.5 %copy-start.11 = (f32[384,32]{0,1:T(8,128)S(1)}, f32[384,32]{0,1:T(8,128)}, u32[]{:S(2)}) copy-start(f32[384,32]{0,1:T(8,128)} %param.16) | copy-start | bytes 147460
  27.8 1.4 %collective-permute-start.5 = (f32[32,1024]{1,0:T(8,128)S(1)}, f32[32,1024]{1,0:T(8,128)S(1)}, u32[]{:S(2)}, u32[]{:S(2)}) collective-permute-start(f32[32,1024]{1,0:T(8,128)S(1)} %convolution_bitcast_fusion), channel_id=1, source_target_pairs={{0,1},{1,0},{2,3},{3,2},{4,5},{5,4},{6,7},{7,6},{8,9},{9,8},{10,11... | collective-permute-start | bytes 393224 | tf_op jit(solution)/shard_map/ppermute | solution.py:25
  29.2 5.6 %collective-permute-start.6 = (f32[32,1024]{1,0:T(8,128)S(1)}, f32[32,1024]{1,0:T(8,128)S(1)}, u32[]{:S(2)}, u32[]{:S(2)}) collective-permute-start(f32[32,1024]{1,0:T(8,128)S(1)} %add.128), channel_id=1, source_target_pairs={{0,2},{1,3},{2,0},{3,1},{4,6},{5,7},{6,4},{7,5},{8,10},{9,11},{10,... | collective-permute-start | bytes 393224 | tf_op jit(solution)/shard_map/ppermute | solution.py:25
  34.9 5.0 %collective-permute-start.7 = (f32[32,1024]{1,0:T(8,128)S(1)}, f32[32,1024]{1,0:T(8,128)S(1)}, u32[]{:S(2)}, u32[]{:S(2)}) collective-permute-start(f32[32,1024]{1,0:T(8,128)S(1)} %add.129), channel_id=1, source_target_pairs={{0,4},{1,5},{2,6},{3,7},{4,0},{5,1},{6,2},{7,3},{8,12},{9,13},{10,... | collective-permute-start | bytes 393224 | tf_op jit(solution)/shard_map/ppermute | solution.py:25
  39.9 21.2 %copy-start.13 = (s32[1600]{0:T(1024)S(1)}, s32[1600]{0:T(1024)}, u32[]{:S(2)}) copy-start(s32[1600]{0:T(1024)} %param.21) | copy-start | bytes 19204
  39.9 21.2 %copy-start.14 = (s32[1536]{0:T(1024)S(1)}, s32[1536]{0:T(1024)}, u32[]{:S(2)}) copy-start(s32[1536]{0:T(1024)} %param.20) | copy-start | bytes 18436
  39.9 5.0 %collective-permute-start.8 = (f32[32,1024]{1,0:T(8,128)S(1)}, f32[32,1024]{1,0:T(8,128)S(1)}, u32[]{:S(2)}, u32[]{:S(2)}) collective-permute-start(f32[32,1024]{1,0:T(8,128)S(1)} %add.130), channel_id=1, source_target_pairs={{0,8},{1,9},{2,10},{3,11},{4,12},{5,13},{6,14},{7,15},{8,0},{9,1},... | collective-permute-start | bytes 393224 | tf_op jit(solution)/shard_map/ppermute | solution.py:25
  45.0 7.4 %collective-permute-start.9 = (f32[32,1024]{1,0:T(8,128)S(1)}, f32[32,1024]{1,0:T(8,128)S(1)}, u32[]{:S(2)}, u32[]{:S(2)}) collective-permute-start(f32[32,1024]{1,0:T(8,128)S(1)} %add.131), channel_id=1, source_target_pairs={{0,16},{1,17},{2,18},{3,19},{4,20},{5,21},{6,22},{7,23},{8,24},{9,... | collective-permute-start | bytes 393224 | tf_op jit(solution)/shard_map/ppermute | solution.py:25
  60.3 4.2 %collective-permute-start.10 = (f32[32,384]{1,0:T(8,128)S(1)}, f32[32,384]{1,0:T(8,128)S(1)}, u32[]{:S(2)}, u32[]{:S(2)}) collective-permute-start(f32[32,384]{1,0:T(8,128)S(1)} %fusion.45), channel_id=1, source_target_pairs={{0,8},{8,0},{16,24},{24,16},{1,9},{9,1},{17,25},{25,17},{2,10},{10... | collective-permute-start | bytes 147464 | tf_op jit(solution)/shard_map/ppermute | solution.py:25
  64.5 5.2 %collective-permute-start.11 = (f32[32,384]{1,0:T(8,128)S(1)}, f32[32,384]{1,0:T(8,128)S(1)}, u32[]{:S(2)}, u32[]{:S(2)}) collective-permute-start(f32[32,384]{1,0:T(8,128)S(1)} %add.133), channel_id=1, source_target_pairs={{0,16},{8,24},{16,0},{24,8},{1,17},{9,25},{17,1},{25,9},{2,18},{10... | collective-permute-start | bytes 147464 | tf_op jit(solution)/shard_map/ppermute | solution.py:25
  70.6 2.9 %collective-permute-start.12 = (f32[32,1024]{1,0:T(8,128)S(1)}, f32[32,1024]{1,0:T(8,128)S(1)}, u32[]{:S(2)}, u32[]{:S(2)}) collective-permute-start(f32[32,1024]{1,0:T(8,128)S(1)} %fusion.22), channel_id=1, source_target_pairs={{0,1},{1,0},{2,3},{3,2},{4,5},{5,4},{6,7},{7,6},{8,9},{9,8},{10,11... | collective-permute-start | bytes 393224 | tf_op jit(solution)/shard_map/ppermute | solution.py:25
  71.4 20.0 %collective-permute-start.19 = (f32[2,400,128]{2,1,0:T(8,128)}, f32[2,400,128]{2,1,0:T(8,128)}, u32[]{:S(2)}, u32[]{:S(2)}) collective-permute-start(f32[2,400,128]{2,1,0:T(8,128)} %dynamic-slice_bitcast_fusion), channel_id=1, source_target_pairs={{0,8},{8,0},{16,24},{24,16},{1,9},{9,1},{17,25},{25,17},{2,10},{10... | collective-permute-start | bytes 1228808 | tf_op jit(solution)/shard_map/ppermute | solution.py:86
  73.5 5.7 %collective-permute-start.13 = (f32[32,1024]{1,0:T(8,128)S(1)}, f32[32,1024]{1,0:T(8,128)S(1)}, u32[]{:S(2)}, u32[]{:S(2)}) collective-permute-start(f32[32,1024]{1,0:T(8,128)S(1)} %add.135), channel_id=1, source_target_pairs={{0,2},{1,3},{2,0},{3,1},{4,6},{5,7},{6,4},{7,5},{8,10},{9,11},{10,... | collective-permute-start | bytes 393224 | tf_op jit(solution)/shard_map/ppermute | solution.py:25
  79.2 5.0 %collective-permute-start.14 = (f32[32,1024]{1,0:T(8,128)S(1)}, f32[32,1024]{1,0:T(8,128)S(1)}, u32[]{:S(2)}, u32[]{:S(2)}) collective-permute-start(f32[32,1024]{1,0:T(8,128)S(1)} %add.136), channel_id=1, source_target_pairs={{0,4},{1,5},{2,6},{3,7},{4,0},{5,1},{6,2},{7,3},{8,12},{9,13},{10,... | collective-permute-start | bytes 393224 | tf_op jit(solution)/shard_map/ppermute | solution.py:25
  84.2 5.0 %collective-permute-start.15 = (f32[32,1024]{1,0:T(8,128)S(1)}, f32[32,1024]{1,0:T(8,128)S(1)}, u32[]{:S(2)}, u32[]{:S(2)}) collective-permute-start(f32[32,1024]{1,0:T(8,128)S(1)} %add.137), channel_id=1, source_target_pairs={{0,8},{1,9},{2,10},{3,11},{4,12},{5,13},{6,14},{7,15},{8,0},{9,1},... | collective-permute-start | bytes 393224 | tf_op jit(solution)/shard_map/ppermute | solution.py:25
  89.3 12.5 %collective-permute-start.16 = (f32[32,1024]{1,0:T(8,128)S(1)}, f32[32,1024]{1,0:T(8,128)S(1)}, u32[]{:S(2)}, u32[]{:S(2)}) collective-permute-start(f32[32,1024]{1,0:T(8,128)S(1)} %add.138), channel_id=1, source_target_pairs={{0,16},{1,17},{2,18},{3,19},{4,20},{5,21},{6,22},{7,23},{8,24},{9,... | collective-permute-start | bytes 393224 | tf_op jit(solution)/shard_map/ppermute | solution.py:25
  92.5 22.0 %copy-start.10 = (f32[400,128]{1,0:T(8,128)S(1)}, f32[400,128]{1,0:T(8,128)}, u32[]{:S(2)}) copy-start(f32[400,128]{1,0:T(8,128)} %param.22) | copy-start | bytes 614404
  92.6 21.9 %collective-permute-start.20 = (f32[1,400,128]{2,1,0:T(8,128)S(1)}, f32[1,400,128]{2,1,0:T(8,128)S(1)}, u32[]{:S(2)}, u32[]{:S(2)}) collective-permute-start(f32[1,400,128]{2,1,0:T(8,128)S(1)} %constant_dynamic-slice_fusion), channel_id=1, source_target_pairs={{0,16},{8,24},{16,0},{24,8},{1,17},{9,25},{17,1},{25,9},{2,18},{10... | collective-permute-start | bytes 614408 | tf_op jit(solution)/shard_map/ppermute | solution.py:86
  109.7 4.2 %collective-permute-start.17 = (f32[32,384]{1,0:T(8,128)S(1)}, f32[32,384]{1,0:T(8,128)S(1)}, u32[]{:S(2)}, u32[]{:S(2)}) collective-permute-start(f32[32,384]{1,0:T(8,128)S(1)} %fusion.46), channel_id=1, source_target_pairs={{0,8},{8,0},{16,24},{24,16},{1,9},{9,1},{17,25},{25,17},{2,10},{10... | collective-permute-start | bytes 147464 | tf_op jit(solution)/shard_map/ppermute | solution.py:25
  113.9 5.6 %collective-permute-start.18 = (f32[32,384]{1,0:T(8,128)S(1)}, f32[32,384]{1,0:T(8,128)S(1)}, u32[]{:S(2)}, u32[]{:S(2)}) collective-permute-start(f32[32,384]{1,0:T(8,128)S(1)} %add.140), channel_id=1, source_target_pairs={{0,16},{8,24},{16,0},{24,8},{1,17},{9,25},{17,1},{25,9},{2,18},{10... | collective-permute-start | bytes 147464 | tf_op jit(solution)/shard_map/ppermute | solution.py:25
  120.4 1.2 copy-start.8
  120.4 1.2 copy-start.9

commit v12 on v11

--- a/solution.py
+++ b/solution.py
@@ -55,6 +55,32 @@
     first = lax.dot_general(mine, even, contract, preferred_element_type=jnp.float32)
     second = lax.dot_general(other, odd, contract, preferred_element_type=jnp.float32)
     return first + second
+
+
+def split_tree_sum(value, axes):
+    count = 1
+    for axis in axes:
+        count *= lax.axis_size(axis)
+    rows = value.shape[0]
+    if count & (count - 1) or count < 4 or rows % 2:
+        return tree_sum(value, axes)
+
+    def exchange(piece, stride):
+        return lax.ppermute(piece, axes, [(i, i ^ stride) for i in range(count)])
+
+    half = rows // 2
+    core = lax.axis_index(axes[-1]) % 2
+    kept = lax.dynamic_slice_in_dim(value, core * half, half, 0)
+    given = lax.dynamic_slice_in_dim(value, (1 - core) * half, half, 0)
+    kept = kept + exchange(given, 1)
+    stride = 2
+    while stride < count:
+        kept = kept + exchange(kept, stride)
+        stride *= 2
+    other = exchange(kept, 1)
+    total = jnp.zeros(value.shape, value.dtype)
+    total = lax.dynamic_update_slice_in_dim(total, kept, core * half, 0)
+    return lax.dynamic_update_slice_in_dim(total, other, (1 - core) * half, 0)
 
 
 def orthonormal(left_basis, gram_matrix):
@@ -144,7 +170,7 @@
         partial_left = lax.dot_general(
             right_rows, combined, (((1,), (1,)), ((), ())), precision=high
         )
-        left_rows = tree_sum(partial_left, ("rep", "tp")) / replicas
+        left_rows = split_tree_sum(partial_left, ("rep", "tp")) / replicas
         gram_matrix = jnp.dot(left_rows, left_rows.T, precision=highest)
         factor_low = jnp.linalg.cholesky(gram_matrix)
         left_rows = jax.scipy.linalg.solve_triangular(factor_low, left_rows, lower=True)

time: 140 us -> 131 us (0.936)
  waiting for transfers between devices: 61.5 us -> 47.3 us
  starting transfers between devices: 27.6 us -> 31.3 us
  blocking collectives: 15.7 us -> 17.7 us
    ppermute x14 -> x4, waiting for transfers between devices: 48.3 us -> 8.82 us  [tree_sum(): value = value + lax.ppermute(value, axes, pairs)]
    ppermute x0 -> x12, waiting for transfers between devices: none -> 25.3 us  [exchange(): return lax.ppermute(piece, axes, [(i, i ^ stride) for i in range(count)])]
    ppermute x0 -> x12, starting transfers between devices: none -> 13.8 us  [exchange(): return lax.ppermute(piece, axes, [(i, i ^ stride) for i in range(count)])]
    ppermute x14 -> x4, starting transfers between devices: 16.8 us -> 6.19 us  [tree_sum(): value = value + lax.ppermute(value, axes, pairs)]
    all_gather x1, blocking collectives: 15.7 us -> 17.7 us  [shards(): lax.all_gather(master_new.astype(jnp.bfloat16), 'rep', axis=0, tiled=True)]
  transfers between devices with their start and end apart: 21 -> 23, of which waited for: 16 -> 17; matrix products, arithmetic and copies ran while one was open for 11% -> 12% of each run, Pallas kernels for 0% -> 0%
where the time goes in v12:
time: 131 us
  waiting for transfers between devices  47.3 us (36%)
  starting transfers between devices  31.3 us (24%)
  other arithmetic  19.3 us (15%)
  blocking collectives  17.7 us (14%)
  matrix products  11.3 us (9%)
  local copies, waits for them, and re-layouts  3.28 us (3%)
    ppermute x12, waiting for transfers between devices, exchange(): return lax.ppermute(piece, axes, [(i, i ^ stride) for i in range(count)])  25.3 us
    all_gather x1, blocking collectives, shards(): lax.all_gather(master_new.astype(jnp.bfloat16), 'rep', axis=0, tiled=True)  17.7 us
    ppermute x12, starting transfers between devices, exchange(): return lax.ppermute(piece, axes, [(i, i ^ stride) for i in range(count)])  13.8 us
    ppermute x5, waiting for transfers between devices, exchange(): return lax.ppermute(value, axis, [(i, i ^ stride) for i in range(count)])  13.1 us
    ppermute x4, waiting for transfers between devices, tree_sum(): value = value + lax.ppermute(value, axes, pairs)  8.82 us
    ppermute x5, starting transfers between devices, exchange(): return lax.ppermute(value, axis, [(i, i ^ stride) for i in range(count)])  7.98 us
    another operation x6, other arithmetic, shards(): factor_low = jnp.linalg.cholesky(gram_matrix)  7.19 us
    ppermute x4, starting transfers between devices, tree_sum(): value = value + lax.ppermute(value, axes, pairs)  6.19 us
  transfers between devices with their start and end apart: 23, of which 17 were waited for; matrix products, arithmetic and copies ran while one was open for 12% of the time, Pallas kernels for 0%

profile of v12, /device:TPU:0, one launch (start us, length us, event | category | flops | bytes accessed | tf_op | source)
XLA Modules:
  0.0 131.2 jit_solution(4449735084966790700)
XLA Ops:
  0.7 3.0 %collective-permute-start = (bf16[192,1024]{1,0:T(8,128)(2,1)}, bf16[192,1024]{1,0:T(8,128)(2,1)S(1)}, u32[]{:S(2)}, u32[]{:S(2)}) collective-permute-start(bf16[192,1024]{1,0:T(8,128)(2,1)} %param.13), channel_id=1, source_target_pairs={{0,2},{1,3},{2,0},{3,1},{4,6},{5,7},{6,4},{7,5},{8,10},{9,11},{10,... | collective-permute-start | bytes 1179656 | tf_op jit(solution)/shard_map/ppermute | solution.py:40
  3.7 1.5 %collective-permute-start.1 = (bf16[192,1024]{1,0:T(8,128)(2,1)}, bf16[192,1024]{1,0:T(8,128)(2,1)S(1)}, u32[]{:S(2)}, u32[]{:S(2)}) collective-permute-start(bf16[192,1024]{1,0:T(8,128)(2,1)} %param.13), channel_id=1, source_target_pairs={{0,4},{1,5},{2,6},{3,7},{4,0},{5,1},{6,2},{7,3},{8,12},{9,13},{10,... | collective-permute-start | bytes 1179656 | tf_op jit(solution)/shard_map/ppermute | solution.py:40
  5.2 7.8 %collective-permute-done = bf16[192,1024]{1,0:T(8,128)(2,1)S(1)} collective-permute-done((bf16[192,1024]{1,0:T(8,128)(2,1)}, bf16[192,1024]{1,0:T(8,128)(2,1)S(1)}, u32[]{:S(2)}, u32[]{:S(2)}) %collective-permute-start) | collective-permute-done | bytes 393248 | tf_op jit(solution)/shard_map/ppermute | solution.py:40
  13.0 1.8 %collective-permute-start.3 = (bf16[96,1024]{1,0:T(8,128)(2,1)S(1)}, bf16[96,1024]{1,0:T(8,128)(2,1)S(1)}, u32[]{:S(2)}, u32[]{:S(2)}) collective-permute-start(bf16[96,1024]{1,0:T(8,128)(2,1)S(1)} %slice.17), channel_id=1, source_target_pairs={{0,4},{1,5},{2,6},{3,7},{4,0},{5,1},{6,2},{7,3},{8,12},{9,13},{10,... | collective-permute-start | bytes 589832 | tf_op jit(solution)/shard_map/ppermute | solution.py:40
  14.9 1.6 %collective-permute-start.2 = (bf16[96,1024]{1,0:T(8,128)(2,1)S(1)}, bf16[96,1024]{1,0:T(8,128)(2,1)S(1)}, u32[]{:S(2)}, u32[]{:S(2)}) collective-permute-start(bf16[96,1024]{1,0:T(8,128)(2,1)S(1)} %slice.16), channel_id=1, source_target_pairs={{0,2},{1,3},{2,0},{3,1},{4,6},{5,7},{6,4},{7,5},{8,10},{9,11},{10,... | collective-permute-start | bytes 589832 | tf_op jit(solution)/shard_map/ppermute | solution.py:40
  16.4 2.7 %collective-permute-done.3 = bf16[96,1024]{1,0:T(8,128)(2,1)S(1)} collective-permute-done((bf16[96,1024]{1,0:T(8,128)(2,1)S(1)}, bf16[96,1024]{1,0:T(8,128)(2,1)S(1)}, u32[]{:S(2)}, u32[]{:S(2)}) %collective-permute-start.3) | collective-permute-done | bytes 196640 | tf_op jit(solution)/shard_map/ppermute | solution.py:40
  19.2 1.4 %collective-permute-done.2 = bf16[96,1024]{1,0:T(8,128)(2,1)S(1)} collective-permute-done((bf16[96,1024]{1,0:T(8,128)(2,1)S(1)}, bf16[96,1024]{1,0:T(8,128)(2,1)S(1)}, u32[]{:S(2)}, u32[]{:S(2)}) %collective-permute-start.2) | collective-permute-done | bytes 196640 | tf_op jit(solution)/shard_map/ppermute | solution.py:40
  21.0 0.9 copy-done.1
  22.3 1.0 fusion.3
  23.4 1.1 collective-permute-done.4
  24.5 2.5 %convert_add_fusion = f32[1024,384]{1,0:T(8,128)S(1)} fusion(f32[1024,384,1]{1,0,2:T(8,128)S(1)} %fusion.3, bf16[4,192,1024]{2,1,0:T(8,128)(2,1)} %collective-permute-done.4, bf16[1,1024,384]{2,1,0:T(8,128)(2,1)S(1)} %copy-done.12, bf16[1,192,384]{2,1,0:T(8,128)(2,1)S(1)} %get-tuple-element.16, bf16[1,192,384]{2,1,0:T(8,128)(2,1)S(1)} %get-tuple-element.17, ...), kind=kOutput, calls=%fused_computation.6 | convolution fusion | flops 606044160 | bytes 6094848 | tf_op jit(solution)/shard_map/dot_general | solution.py:56
  28.0 1.1 collective-permute-done.5
  29.1 1.6 %collective-permute-start.6 = (f32[16,1024]{1,0:T(8,128)S(1)}, f32[16,1024]{1,0:T(8,128)S(1)}, u32[]{:S(2)}, u32[]{:S(2)}) collective-permute-start(f32[16,1024]{1,0:T(8,128)S(1)} %bitcast_add_fusion.2), channel_id=1, source_target_pairs={{0,2},{1,3},{2,0},{3,1},{4,6},{5,7},{6,4},{7,5},{8,10},{9,11},{10,... | collective-permute-start | bytes 196616 | tf_op jit(solution)/shard_map/ppermute | solution.py:69
  30.7 2.8 %collective-permute-done.6 = f32[16,1024]{1,0:T(8,128)S(1)} collective-permute-done((f32[16,1024]{1,0:T(8,128)S(1)}, f32[16,1024]{1,0:T(8,128)S(1)}, u32[]{:S(2)}, u32[]{:S(2)}) %collective-permute-start.6) | collective-permute-done | bytes 65568 | tf_op jit(solution)/shard_map/ppermute | solution.py:69
  33.5 1.2 collective-permute-start.7
  34.7 3.1 %collective-permute-done.7 = f32[16,1024]{1,0:T(8,128)S(1)} collective-permute-done((f32[16,1024]{1,0:T(8,128)S(1)}, f32[16,1024]{1,0:T(8,128)S(1)}, u32[]{:S(2)}, u32[]{:S(2)}) %collective-permute-start.7) | collective-permute-done | bytes 65568 | tf_op jit(solution)/shard_map/ppermute | solution.py:69
  37.9 1.6 %collective-permute-start.8 = (f32[16,1024]{1,0:T(8,128)S(1)}, f32[16,1024]{1,0:T(8,128)S(1)}, u32[]{:S(2)}, u32[]{:S(2)}) collective-permute-start(f32[16,1024]{1,0:T(8,128)S(1)} %add.149), channel_id=1, source_target_pairs={{0,8},{1,9},{2,10},{3,11},{4,12},{5,13},{6,14},{7,15},{8,0},{9,1},... | collective-permute-start | bytes 196616 | tf_op jit(solution)/shard_map/ppermute | solution.py:69
  39.5 2.7 %collective-permute-done.8 = f32[16,1024]{1,0:T(8,128)S(1)} collective-permute-done((f32[16,1024]{1,0:T(8,128)S(1)}, f32[16,1024]{1,0:T(8,128)S(1)}, u32[]{:S(2)}, u32[]{:S(2)}) %collective-permute-start.8) | collective-permute-done | bytes 65568 | tf_op jit(solution)/shard_map/ppermute | solution.py:69
  42.2 3.3 %collective-permute-start.9 = (f32[16,1024]{1,0:T(8,128)S(1)}, f32[16,1024]{1,0:T(8,128)S(1)}, u32[]{:S(2)}, u32[]{:S(2)}) collective-permute-start(f32[16,1024]{1,0:T(8,128)S(1)} %add.150), channel_id=1, source_target_pairs={{0,16},{1,17},{2,18},{3,19},{4,20},{5,21},{6,22},{7,23},{8,24},{9,... | collective-permute-start | bytes 196616 | tf_op jit(solution)/shard_map/ppermute | solution.py:69
  45.5 2.3 %collective-permute-done.9 = f32[16,1024]{1,0:T(8,128)S(1)} collective-permute-done((f32[16,1024]{1,0:T(8,128)S(1)}, f32[16,1024]{1,0:T(8,128)S(1)}, u32[]{:S(2)}, u32[]{:S(2)}) %collective-permute-start.9) | collective-permute-done | bytes 65568 | tf_op jit(solution)/shard_map/ppermute | solution.py:69
  47.9 1.2 collective-permute-done.10
  49.5 2.9 %cholesky.44 = f32[32,32]{1,0:T(8,128)S(1)} custom-call(f32[32,32]{1,0:T(8,128)S(1)} %fusion.41), custom_call_target="Cholesky" | custom-call | tf_op jit(solution)/shard_map/jit(cholesky)/cholesky | solution.py:175
  53.7 2.4 %custom-call.6 = f32[1,32,32]{1,2,0:T(8,128)S(1)} custom-call(f32[1,32,32]{2,1,0:T(8,128)S(1)} %fusion.36), custom_call_target="InvertDiagBlocksLowerTriangular" | custom-call | tf_op jit(solution)/shard_map/jit(_solve_triangular)/triangular_solve | solution.py:176
  57.1 1.3 %collective-permute-start.11 = (f32[32,384]{1,0:T(8,128)S(1)}, f32[32,384]{1,0:T(8,128)S(1)}, u32[]{:S(2)}, u32[]{:S(2)}) collective-permute-start(f32[32,384]{1,0:T(8,128)S(1)} %fusion.54), channel_id=1, source_target_pairs={{0,8},{8,0},{16,24},{24,16},{1,9},{9,1},{17,25},{25,17},{2,10},{10... | collective-permute-start | bytes 147464 | tf_op jit(solution)/shard_map/ppermute | solution.py:25
  58.4 1.1 select_reduce_fusion
  59.5 1.7 %collective-permute-done.11 = f32[32,384]{1,0:T(8,128)S(1)} collective-permute-done((f32[32,384]{1,0:T(8,128)S(1)}, f32[32,384]{1,0:T(8,128)S(1)}, u32[]{:S(2)}, u32[]{:S(2)}) %collective-permute-start.11) | collective-permute-done | bytes 49184 | tf_op jit(solution)/shard_map/ppermute | solution.py:25
  61.2 3.1 %collective-permute-start.12 = (f32[32,384]{1,0:T(8,128)S(1)}, f32[32,384]{1,0:T(8,128)S(1)}, u32[]{:S(2)}, u32[]{:S(2)}) collective-permute-start(f32[32,384]{1,0:T(8,128)S(1)} %add.152), channel_id=1, source_target_pairs={{0,16},{8,24},{16,0},{24,8},{1,17},{9,25},{17,1},{25,9},{2,18},{10... | collective-permute-start | bytes 147464 | tf_op jit(solution)/shard_map/ppermute | solution.py:25
  64.3 3.1 %fusion = f32[1600,128]{1,0:T(8,128)S(1)} fusion(bf16[1536,128]{1,0:T(8,128)(2,1)S(1)} %copy-done, s32[1536]{0:T(1024)S(1)} %select_reduce_fusion), kind=kOutput, calls=%fused_computation.1 | convolution fusion | flops 631603200 | bytes 1218560 | tf_op jit(solution)/shard_map/dot_general | solution.py:100
  69.1 1.5 %collective-permute-start.21 = (f32[2,400,128]{2,1,0:T(8,128)}, f32[2,400,128]{2,1,0:T(8,128)}, u32[]{:S(2)}, u32[]{:S(2)}) collective-permute-start(f32[2,400,128]{2,1,0:T(8,128)} %dynamic-slice_bitcast_fusion), channel_id=1, source_target_pairs={{0,8},{8,0},{16,24},{24,16},{1,9},{9,1},{17,25},{25,17},{2,10},{10... | collective-permute-start | bytes 1228808 | tf_op jit(solution)/shard_map/ppermute | solution.py:112
  70.7 1.5 %collective-permute-start.14 = (f32[16,1024]{1,0:T(8,128)S(1)}, f32[16,1024]{1,0:T(8,128)S(1)}, u32[]{:S(2)}, u32[]{:S(2)}) collective-permute-start(f32[16,1024]{1,0:T(8,128)S(1)} %dynamic-slice_add_fusion.1), channel_id=1, source_target_pairs={{0,2},{1,3},{2,0},{3,1},{4,6},{5,7},{6,4},{7,5},{8,10},{9,11},{10,... | collective-permute-start | bytes 196616 | tf_op jit(solution)/shard_map/ppermute | solution.py:69
  72.2 2.8 %collective-permute-done.14 = f32[16,1024]{1,0:T(8,128)S(1)} collective-permute-done((f32[16,1024]{1,0:T(8,128)S(1)}, f32[16,1024]{1,0:T(8,128)S(1)}, u32[]{:S(2)}, u32[]{:S(2)}) %collective-permute-start.14) | collective-permute-done | bytes 65568 | tf_op jit(solution)/shard_map/ppermute | solution.py:69
  75.0 1.2 collective-permute-start.15
  76.2 3.1 %collective-permute-done.15 = f32[16,1024]{1,0:T(8,128)S(1)} collective-permute-done((f32[16,1024]{1,0:T(8,128)S(1)}, f32[16,1024]{1,0:T(8,128)S(1)}, u32[]{:S(2)}, u32[]{:S(2)}) %collective-permute-start.15) | collective-permute-done | bytes 65568 | tf_op jit(solution)/shard_map/ppermute | solution.py:69
  79.9 3.8 %collective-permute-done.16 = f32[16,1024]{1,0:T(8,128)S(1)} collective-permute-done((f32[16,1024]{1,0:T(8,128)S(1)}, f32[16,1024]{1,0:T(8,128)S(1)}, u32[]{:S(2)}, u32[]{:S(2)}) %collective-permute-start.16) | collective-permute-done | bytes 65568 | tf_op jit(solution)/shard_map/ppermute | solution.py:69
  83.7 2.4 %collective-permute-start.17 = (f32[16,1024]{1,0:T(8,128)S(1)}, f32[16,1024]{1,0:T(8,128)S(1)}, u32[]{:S(2)}, u32[]{:S(2)}) collective-permute-start(f32[16,1024]{1,0:T(8,128)S(1)} %add.157), channel_id=1, source_target_pairs={{0,16},{1,17},{2,18},{3,19},{4,20},{5,21},{6,22},{7,23},{8,24},{9,... | collective-permute-start | bytes 196616 | tf_op jit(solution)/shard_map/ppermute | solution.py:69
  86.1 1.0 bitcast_add_fusion.1
  87.2 2.4 %collective-permute-done.17 = f32[16,1024]{1,0:T(8,128)S(1)} collective-permute-done((f32[16,1024]{1,0:T(8,128)S(1)}, f32[16,1024]{1,0:T(8,128)S(1)}, u32[]{:S(2)}, u32[]{:S(2)}) %collective-permute-start.17) | collective-permute-done | bytes 65568 | tf_op jit(solution)/shard_map/ppermute | solution.py:69
  89.7 1.8 %collective-permute-start.22 = (f32[1,400,128]{2,1,0:T(8,128)S(1)}, f32[1,400,128]{2,1,0:T(8,128)S(1)}, u32[]{:S(2)}, u32[]{:S(2)}) collective-permute-start(f32[1,400,128]{2,1,0:T(8,128)S(1)} %constant_dynamic-slice_fusion), channel_id=1, source_target_pairs={{0,16},{8,24},{16,0},{24,8},{1,17},{9,25},{17,1},{25,9},{2,18},{10... | collective-permute-start | bytes 614408 | tf_op jit(solution)/shard_map/ppermute | solution.py:112
  91.9 2.9 %cholesky.55 = f32[32,32]{1,0:T(8,128)S(1)} custom-call(f32[32,32]{1,0:T(8,128)S(1)} %fusion.39), custom_call_target="Cholesky" | custom-call | tf_op jit(solution)/shard_map/jit(cholesky)/cholesky | solution.py:175
  96.1 2.4 %custom-call.7 = f32[1,32,32]{1,2,0:T(8,128)S(1)} custom-call(f32[1,32,32]{2,1,0:T(8,128)S(1)} %fusion.37), custom_call_target="InvertDiagBlocksLowerTriangular" | custom-call | tf_op jit(solution)/shard_map/jit(_solve_triangular)/triangular_solve | solution.py:176
  100.0 3.6 %collective-permute-done.19 = f32[32,384]{1,0:T(8,128)S(1)} collective-permute-done((f32[32,384]{1,0:T(8,128)S(1)}, f32[32,384]{1,0:T(8,128)S(1)}, u32[]{:S(2)}, u32[]{:S(2)}) %collective-permute-start.19) | collective-permute-done | bytes 49184 | tf_op jit(solution)/shard_map/ppermute | solution.py:25
  103.6 1.3 collective-permute-start.20
  105.6 3.5 %collective-permute-done.20 = f32[32,384]{1,0:T(8,128)S(1)} collective-permute-done((f32[32,384]{1,0:T(8,128)S(1)}, f32[32,384]{1,0:T(8,128)S(1)}, u32[]{:S(2)}, u32[]{:S(2)}) %collective-permute-start.20) | collective-permute-done | bytes 49184 | tf_op jit(solution)/shard_map/ppermute | solution.py:25
  109.1 0.8 fusion.35
  109.9 1.1 fusion.2
  111.1 1.0 fusion.52
  112.1 17.7 %all_gather.3 = bf16[1024,384]{1,0:T(8,128)(2,1)S(1)} all-gather(bf16[256,384]{1,0:T(8,128)(2,1)S(1)} %get-tuple-element.8), channel_id=1, replica_groups=mesh['rep'=4,'tp'=8] {'rep'}, dimensions={0}, use_global_device_ids=true | all-gather | bytes 983040 | tf_op jit(solution)/shard_map/all_gather | solution.py:190
  130.4 0.9 copy.25
  (87 shorter events, 11.4 us)
Async XLA Ops:
  0.6 63.7 %copy-start = (bf16[1536,128]{1,0:T(8,128)(2,1)S(1)}, bf16[1536,128]{1,0:T(8,128)(2,1)}, u32[]{:S(2)}) copy-start(bf16[1536,128]{1,0:T(8,128)(2,1)} %param.19) | copy-start | bytes 1179652
  0.6 20.0 %copy-start.6 = (bf16[192,1024]{1,0:T(8,128)(2,1)S(1)}, bf16[192,1024]{1,0:T(8,128)(2,1)}, u32[]{:S(2)}) copy-start(bf16[192,1024]{1,0:T(8,128)(2,1)} %param.13) | copy-start | bytes 1179652
  0.7 12.3 %collective-permute-start = (bf16[192,1024]{1,0:T(8,128)(2,1)}, bf16[192,1024]{1,0:T(8,128)(2,1)S(1)}, u32[]{:S(2)}, u32[]{:S(2)}) collective-permute-start(bf16[192,1024]{1,0:T(8,128)(2,1)} %param.13), channel_id=1, source_target_pairs={{0,2},{1,3},{2,0},{3,1},{4,6},{5,7},{6,4},{7,5},{8,10},{9,11},{10,... | collective-permute-start | bytes 1179656 | tf_op jit(solution)/shard_map/ppermute | solution.py:40
  3.7 11.2 %collective-permute-start.1 = (bf16[192,1024]{1,0:T(8,128)(2,1)}, bf16[192,1024]{1,0:T(8,128)(2,1)S(1)}, u32[]{:S(2)}, u32[]{:S(2)}) collective-permute-start(bf16[192,1024]{1,0:T(8,128)(2,1)} %param.13), channel_id=1, source_target_pairs={{0,4},{1,5},{2,6},{3,7},{4,0},{5,1},{6,2},{7,3},{8,12},{9,13},{10,... | collective-permute-start | bytes 1179656 | tf_op jit(solution)/shard_map/ppermute | solution.py:40
  13.0 7.9 %copy-start.2 = (bf16[192,1024]{1,0:T(8,128)(2,1)}, bf16[192,1024]{1,0:T(8,128)(2,1)S(1)}, u32[]{:S(2)}) copy-start(bf16[192,1024]{1,0:T(8,128)(2,1)S(1)} %collective-permute-done) | copy-start | bytes 1179652
  13.0 6.2 %collective-permute-start.3 = (bf16[96,1024]{1,0:T(8,128)(2,1)S(1)}, bf16[96,1024]{1,0:T(8,128)(2,1)S(1)}, u32[]{:S(2)}, u32[]{:S(2)}) collective-permute-start(bf16[96,1024]{1,0:T(8,128)(2,1)S(1)} %slice.17), channel_id=1, source_target_pairs={{0,4},{1,5},{2,6},{3,7},{4,0},{5,1},{6,2},{7,3},{8,12},{9,13},{10,... | collective-permute-start | bytes 589832 | tf_op jit(solution)/shard_map/ppermute | solution.py:40
  14.8 6.0 %copy-start.4 = (bf16[192,1024]{1,0:T(8,128)(2,1)}, bf16[192,1024]{1,0:T(8,128)(2,1)S(1)}, u32[]{:S(2)}) copy-start(bf16[192,1024]{1,0:T(8,128)(2,1)S(1)} %collective-permute-done.1) | copy-start | bytes 1179652
  14.9 5.7 %collective-permute-start.2 = (bf16[96,1024]{1,0:T(8,128)(2,1)S(1)}, bf16[96,1024]{1,0:T(8,128)(2,1)S(1)}, u32[]{:S(2)}, u32[]{:S(2)}) collective-permute-start(bf16[96,1024]{1,0:T(8,128)(2,1)S(1)} %slice.16), channel_id=1, source_target_pairs={{0,2},{1,3},{2,0},{3,1},{4,6},{5,7},{6,4},{7,5},{8,10},{9,11},{10,... | collective-permute-start | bytes 589832 | tf_op jit(solution)/shard_map/ppermute | solution.py:40
  20.6 1.3 copy-start.1
  20.9 3.6 %collective-permute-start.4 = (bf16[4,192,1024]{2,1,0:T(8,128)(2,1)S(1)}, bf16[4,192,1024]{2,1,0:T(8,128)(2,1)}, u32[]{:S(2)}, u32[]{:S(2)}) collective-permute-start(bf16[4,192,1024]{2,1,0:T(8,128)(2,1)S(1)} %pad_maximum_fusion), channel_id=1, source_target_pairs={{0,1},{1,0},{2,3},{3,2},{4,5},{5,4},{6,7},{7,6},{8,9},{9,8},{10,11... | collective-permute-start | bytes 4718600 | tf_op jit(solution)/shard_map/ppermute | solution.py:40
  21.0 1.1 copy-start.3
  21.0 1.2 copy-start.5
  21.0 1.3 copy-start.7
  22.3 2.2 %copy-start.12 = (bf16[1,1024,384]{2,1,0:T(8,128)(2,1)S(1)}, bf16[1,1024,384]{2,1,0:T(8,128)(2,1)}, u32[]{:S(2)}) copy-start(bf16[1,1024,384]{2,1,0:T(8,128)(2,1)} %param.15) | copy-start | bytes 2359300
  24.5 2.5 %copy-start.11 = (f32[384,32]{0,1:T(8,128)S(1)}, f32[384,32]{0,1:T(8,128)}, u32[]{:S(2)}) copy-start(f32[384,32]{0,1:T(8,128)} %param.16) | copy-start | bytes 147460
  27.8 1.3 %collective-permute-start.5 = (f32[16,1024]{1,0:T(8,128)S(1)}, f32[16,1024]{1,0:T(8,128)S(1)}, u32[]{:S(2)}, u32[]{:S(2)}) collective-permute-start(f32[16,1024]{1,0:T(8,128)S(1)} %dynamic-slice_bitcast_fusion.1), channel_id=1, source_target_pairs={{0,1},{1,0},{2,3},{3,2},{4,5},{5,4},{6,7},{7,6},{8,9},{9,8},{10,11... | collective-permute-start | bytes 196616 | tf_op jit(solution)/shard_map/ppermute | solution.py:69
  29.1 4.3 %collective-permute-start.6 = (f32[16,1024]{1,0:T(8,128)S(1)}, f32[16,1024]{1,0:T(8,128)S(1)}, u32[]{:S(2)}, u32[]{:S(2)}) collective-permute-start(f32[16,1024]{1,0:T(8,128)S(1)} %bitcast_add_fusion.2), channel_id=1, source_target_pairs={{0,2},{1,3},{2,0},{3,1},{4,6},{5,7},{6,4},{7,5},{8,10},{9,11},{10,... | collective-permute-start | bytes 196616 | tf_op jit(solution)/shard_map/ppermute | solution.py:69
  33.5 24.9 %copy-start.13 = (s32[1600]{0:T(1024)S(1)}, s32[1600]{0:T(1024)}, u32[]{:S(2)}) copy-start(s32[1600]{0:T(1024)} %param.21) | copy-start | bytes 19204
  33.5 24.9 %copy-start.14 = (s32[1536]{0:T(1024)S(1)}, s32[1536]{0:T(1024)}, u32[]{:S(2)}) copy-start(s32[1536]{0:T(1024)} %param.20) | copy-start | bytes 18436
  33.5 4.3 %collective-permute-start.7 = (f32[16,1024]{1,0:T(8,128)S(1)}, f32[16,1024]{1,0:T(8,128)S(1)}, u32[]{:S(2)}, u32[]{:S(2)}) collective-permute-start(f32[16,1024]{1,0:T(8,128)S(1)} %add.148), channel_id=1, source_target_pairs={{0,4},{1,5},{2,6},{3,7},{4,0},{5,1},{6,2},{7,3},{8,12},{9,13},{10,... | collective-permute-start | bytes 196616 | tf_op jit(solution)/shard_map/ppermute | solution.py:69
  37.9 4.3 %collective-permute-start.8 = (f32[16,1024]{1,0:T(8,128)S(1)}, f32[16,1024]{1,0:T(8,128)S(1)}, u32[]{:S(2)}, u32[]{:S(2)}) collective-permute-start(f32[16,1024]{1,0:T(8,128)S(1)} %add.149), channel_id=1, source_target_pairs={{0,8},{1,9},{2,10},{3,11},{4,12},{5,13},{6,14},{7,15},{8,0},{9,1},... | collective-permute-start | bytes 196616 | tf_op jit(solution)/shard_map/ppermute | solution.py:69
  42.2 5.6 %collective-permute-start.9 = (f32[16,1024]{1,0:T(8,128)S(1)}, f32[16,1024]{1,0:T(8,128)S(1)}, u32[]{:S(2)}, u32[]{:S(2)}) collective-permute-start(f32[16,1024]{1,0:T(8,128)S(1)} %add.150), channel_id=1, source_target_pairs={{0,16},{1,17},{2,18},{3,19},{4,20},{5,21},{6,22},{7,23},{8,24},{9,... | collective-permute-start | bytes 196616 | tf_op jit(solution)/shard_map/ppermute | solution.py:69
  47.8 1.3 %collective-permute-start.10 = (f32[16,1024]{1,0:T(8,128)S(1)}, f32[16,1024]{1,0:T(8,128)S(1)}, u32[]{:S(2)}, u32[]{:S(2)}) collective-permute-start(f32[16,1024]{1,0:T(8,128)S(1)} %get-tuple-element.14), channel_id=1, source_target_pairs={{0,1},{1,0},{2,3},{3,2},{4,5},{5,4},{6,7},{7,6},{8,9},{9,8},{10,11... | collective-permute-start | bytes 196616 | tf_op jit(solution)/shard_map/ppermute | solution.py:69
  57.1 4.2 %collective-permute-start.11 = (f32[32,384]{1,0:T(8,128)S(1)}, f32[32,384]{1,0:T(8,128)S(1)}, u32[]{:S(2)}, u32[]{:S(2)}) collective-permute-start(f32[32,384]{1,0:T(8,128)S(1)} %fusion.54), channel_id=1, source_target_pairs={{0,8},{8,0},{16,24},{24,16},{1,9},{9,1},{17,25},{25,17},{2,10},{10... | collective-permute-start | bytes 147464 | tf_op jit(solution)/shard_map/ppermute | solution.py:25
  61.2 6.2 %collective-permute-start.12 = (f32[32,384]{1,0:T(8,128)S(1)}, f32[32,384]{1,0:T(8,128)S(1)}, u32[]{:S(2)}, u32[]{:S(2)}) collective-permute-start(f32[32,384]{1,0:T(8,128)S(1)} %add.152), channel_id=1, source_target_pairs={{0,16},{8,24},{16,0},{24,8},{1,17},{9,25},{17,1},{25,9},{2,18},{10... | collective-permute-start | bytes 147464 | tf_op jit(solution)/shard_map/ppermute | solution.py:25
  68.3 2.4 %collective-permute-start.13 = (f32[16,1024]{1,0:T(8,128)S(1)}, f32[16,1024]{1,0:T(8,128)S(1)}, u32[]{:S(2)}, u32[]{:S(2)}) collective-permute-start(f32[16,1024]{1,0:T(8,128)S(1)} %constant_dynamic-slice_fusion.1), channel_id=1, source_target_pairs={{0,1},{1,0},{2,3},{3,2},{4,5},{5,4},{6,7},{7,6},{8,9},{9,8},{10,11... | collective-permute-start | bytes 196616 | tf_op jit(solution)/shard_map/ppermute | solution.py:69
  69.1 17.0 %collective-permute-start.21 = (f32[2,400,128]{2,1,0:T(8,128)}, f32[2,400,128]{2,1,0:T(8,128)}, u32[]{:S(2)}, u32[]{:S(2)}) collective-permute-start(f32[2,400,128]{2,1,0:T(8,128)} %dynamic-slice_bitcast_fusion), channel_id=1, source_target_pairs={{0,8},{8,0},{16,24},{24,16},{1,9},{9,1},{17,25},{25,17},{2,10},{10... | collective-permute-start | bytes 1228808 | tf_op jit(solution)/shard_map/ppermute | solution.py:112
  70.7 4.3 %collective-permute-start.14 = (f32[16,1024]{1,0:T(8,128)S(1)}, f32[16,1024]{1,0:T(8,128)S(1)}, u32[]{:S(2)}, u32[]{:S(2)}) collective-permute-start(f32[16,1024]{1,0:T(8,128)S(1)} %dynamic-slice_add_fusion.1), channel_id=1, source_target_pairs={{0,2},{1,3},{2,0},{3,1},{4,6},{5,7},{6,4},{7,5},{8,10},{9,11},{10,... | collective-permute-start | bytes 196616 | tf_op jit(solution)/shard_map/ppermute | solution.py:69
  75.0 4.3 %collective-permute-start.15 = (f32[16,1024]{1,0:T(8,128)S(1)}, f32[16,1024]{1,0:T(8,128)S(1)}, u32[]{:S(2)}, u32[]{:S(2)}) collective-permute-start(f32[16,1024]{1,0:T(8,128)S(1)} %add.155), channel_id=1, source_target_pairs={{0,4},{1,5},{2,6},{3,7},{4,0},{5,1},{6,2},{7,3},{8,12},{9,13},{10,... | collective-permute-start | bytes 196616 | tf_op jit(solution)/shard_map/ppermute | solution.py:69
  79.4 4.3 %collective-permute-start.16 = (f32[16,1024]{1,0:T(8,128)S(1)}, f32[16,1024]{1,0:T(8,128)S(1)}, u32[]{:S(2)}, u32[]{:S(2)}) collective-permute-start(f32[16,1024]{1,0:T(8,128)S(1)} %add.156), channel_id=1, source_target_pairs={{0,8},{1,9},{2,10},{3,11},{4,12},{5,13},{6,14},{7,15},{8,0},{9,1},... | collective-permute-start | bytes 196616 | tf_op jit(solution)/shard_map/ppermute | solution.py:69
  83.7 5.9 %collective-permute-start.17 = (f32[16,1024]{1,0:T(8,128)S(1)}, f32[16,1024]{1,0:T(8,128)S(1)}, u32[]{:S(2)}, u32[]{:S(2)}) collective-permute-start(f32[16,1024]{1,0:T(8,128)S(1)} %add.157), channel_id=1, source_target_pairs={{0,16},{1,17},{2,18},{3,19},{4,20},{5,21},{6,22},{7,23},{8,24},{9,... | collective-permute-start | bytes 196616 | tf_op jit(solution)/shard_map/ppermute | solution.py:69
  89.6 15.3 %copy-start.10 = (f32[400,128]{1,0:T(8,128)S(1)}, f32[400,128]{1,0:T(8,128)}, u32[]{:S(2)}) copy-start(f32[400,128]{1,0:T(8,128)} %param.22) | copy-start | bytes 614404
  89.6 1.9 %collective-permute-start.18 = (f32[16,1024]{1,0:T(8,128)S(1)}, f32[16,1024]{1,0:T(8,128)S(1)}, u32[]{:S(2)}, u32[]{:S(2)}) collective-permute-start(f32[16,1024]{1,0:T(8,128)S(1)} %get-tuple-element.12), channel_id=1, source_target_pairs={{0,1},{1,0},{2,3},{3,2},{4,5},{5,4},{6,7},{7,6},{8,9},{9,8},{10,11... | collective-permute-start | bytes 196616 | tf_op jit(solution)/shard_map/ppermute | solution.py:69
  89.7 15.2 %collective-permute-start.22 = (f32[1,400,128]{2,1,0:T(8,128)S(1)}, f32[1,400,128]{2,1,0:T(8,128)S(1)}, u32[]{:S(2)}, u32[]{:S(2)}) collective-permute-start(f32[1,400,128]{2,1,0:T(8,128)S(1)} %constant_dynamic-slice_fusion), channel_id=1, source_target_pairs={{0,16},{8,24},{16,0},{24,8},{1,17},{9,25},{17,1},{25,9},{2,18},{10... | collective-permute-start | bytes 614408 | tf_op jit(solution)/shard_map/ppermute | solution.py:112
  99.4 4.2 %collective-permute-start.19 = (f32[32,384]{1,0:T(8,128)S(1)}, f32[32,384]{1,0:T(8,128)S(1)}, u32[]{:S(2)}, u32[]{:S(2)}) collective-permute-start(f32[32,384]{1,0:T(8,128)S(1)} %fusion.55), channel_id=1, source_target_pairs={{0,8},{8,0},{16,24},{24,16},{1,9},{9,1},{17,25},{25,17},{2,10},{10... | collective-permute-start | bytes 147464 | tf_op jit(solution)/shard_map/ppermute | solution.py:25
  103.6 5.5 %collective-permute-start.20 = (f32[32,384]{1,0:T(8,128)S(1)}, f32[32,384]{1,0:T(8,128)S(1)}, u32[]{:S(2)}, u32[]{:S(2)}) collective-permute-start(f32[32,384]{1,0:T(8,128)S(1)} %add.159), channel_id=1, source_target_pairs={{0,16},{8,24},{16,0},{24,8},{1,17},{9,25},{17,1},{25,9},{2,18},{10... | collective-permute-start | bytes 147464 | tf_op jit(solution)/shard_map/ppermute | solution.py:25
  109.9 1.2 copy-start.8
  109.9 1.2 copy-start.9

commit v13 on v12

--- a/solution.py
+++ b/solution.py
@@ -53,8 +53,7 @@
     odd = jnp.stack([grads[me ^ offset] for offset in (1, 3, 5, 7)])
     contract = (((0, 1), (0, 1)), ((), ()))
     first = lax.dot_general(mine, even, contract, preferred_element_type=jnp.float32)
-    second = lax.dot_general(other, odd, contract, preferred_element_type=jnp.float32)
-    return first + second
+    return first, (other, odd)
 
 
 def split_tree_sum(value, axes):
@@ -162,14 +161,24 @@
     high = lax.Precision.HIGH
     replicas = lax.axis_size("rep")
     word_new = None
-    product = replica_product(activations, out_grads, "tp")
-    combined = product + error_state[0].astype(jnp.float32)
+    early, late = replica_product(activations, out_grads, "tp")
+    combined = early + error_state[0].astype(jnp.float32)
     right_rows = q_start.T
     left_rows = None
     for round_index in range(ROUNDS):
         partial_left = lax.dot_general(
             right_rows, combined, (((1,), (1,)), ((), ())), precision=high
         )
+        if late is not None:
+            other, odd = late
+            partial_left, other = lax.optimization_barrier((partial_left, other))
+            contract = (((0, 1), (0, 1)), ((), ()))
+            second = lax.dot_general(other, odd, contract, preferred_element_type=jnp.float32)
+            partial_left = partial_left + lax.dot_general(
+                right_rows, second, (((1,), (1,)), ((), ())), precision=high
+            )
+            combined = combined + second
+            late = None
         left_rows = split_tree_sum(partial_left, ("rep", "tp")) / replicas
         gram_matrix = jnp.dot(left_rows, left_rows.T, precision=highest)
         factor_low = jnp.linalg.cholesky(gram_matrix)

time: 131 us -> 131 us (level)
  waiting for transfers between devices: 47.3 us -> 45.8 us
    dynamic_slice x1, local copies, waits for them, and re-layouts: 0.12 us -> 1.61 us  [replica_product(): odd = jnp.stack([grads[me ^ offset] for offset in (1, 3, 5, 7)])]
  transfers between devices with their start and end apart: 23 -> 23, of which waited for: 17 -> 16; matrix products, arithmetic and copies ran while one was open for 12% -> 14% of each run, Pallas kernels for 0% -> 0%
where the time goes in v13:
time: 131 us
  waiting for transfers between devices  45.8 us (35%)
  starting transfers between devices  31.4 us (24%)
  other arithmetic  19.3 us (15%)
  blocking collectives  17.7 us (14%)
  matrix products  10.9 us (8%)
  local copies, waits for them, and re-layouts  4.52 us (3%)
    ppermute x12, waiting for transfers between devices, exchange(): return lax.ppermute(piece, axes, [(i, i ^ stride) for i in range(count)])  25.6 us
    all_gather x1, blocking collectives, shards(): lax.all_gather(master_new.astype(jnp.bfloat16), 'rep', axis=0, tiled=True)  17.7 us
    ppermute x12, starting transfers between devices, exchange(): return lax.ppermute(piece, axes, [(i, i ^ stride) for i in range(count)])  13.4 us
    ppermute x5, waiting for transfers between devices, exchange(): return lax.ppermute(value, axis, [(i, i ^ stride) for i in range(count)])  12 us
    ppermute x4, waiting for transfers between devices, tree_sum(): value = value + lax.ppermute(value, axes, pairs)  8.15 us
    ppermute x5, starting transfers between devices, exchange(): return lax.ppermute(value, axis, [(i, i ^ stride) for i in range(count)])  7.91 us
    another operation x6, other arithmetic, shards(): factor_low = jnp.linalg.cholesky(gram_matrix)  7.2 us
    ppermute x4, starting transfers between devices, tree_sum(): value = value + lax.ppermute(value, axes, pairs)  6.81 us
  transfers between devices with their start and end apart: 23, of which 16 were waited for; matrix products, arithmetic and copies ran while one was open for 14% of the time, Pallas kernels for 0%

profile of v13, /device:TPU:0, one launch (start us, length us, event | category | flops | bytes accessed | tf_op | source)
XLA Modules:
  0.0 130.7 jit_solution(15193137413246515434)
XLA Ops:
  0.7 3.0 %collective-permute-start = (bf16[192,1024]{1,0:T(8,128)(2,1)}, bf16[192,1024]{1,0:T(8,128)(2,1)S(1)}, u32[]{:S(2)}, u32[]{:S(2)}) collective-permute-start(bf16[192,1024]{1,0:T(8,128)(2,1)} %param.13), channel_id=1, source_target_pairs={{0,2},{1,3},{2,0},{3,1},{4,6},{5,7},{6,4},{7,5},{8,10},{9,11},{10,... | collective-permute-start | bytes 1179656 | tf_op jit(solution)/shard_map/ppermute | solution.py:40
  3.7 1.5 %collective-permute-start.1 = (bf16[192,1024]{1,0:T(8,128)(2,1)}, bf16[192,1024]{1,0:T(8,128)(2,1)S(1)}, u32[]{:S(2)}, u32[]{:S(2)}) collective-permute-start(bf16[192,1024]{1,0:T(8,128)(2,1)} %param.13), channel_id=1, source_target_pairs={{0,4},{1,5},{2,6},{3,7},{4,0},{5,1},{6,2},{7,3},{8,12},{9,13},{10,... | collective-permute-start | bytes 1179656 | tf_op jit(solution)/shard_map/ppermute | solution.py:40
  5.2 7.8 %collective-permute-done = bf16[192,1024]{1,0:T(8,128)(2,1)S(1)} collective-permute-done((bf16[192,1024]{1,0:T(8,128)(2,1)}, bf16[192,1024]{1,0:T(8,128)(2,1)S(1)}, u32[]{:S(2)}, u32[]{:S(2)}) %collective-permute-start) | collective-permute-done | bytes 393248 | tf_op jit(solution)/shard_map/ppermute | solution.py:40
  13.0 1.8 %collective-permute-start.3 = (bf16[96,1024]{1,0:T(8,128)(2,1)S(1)}, bf16[96,1024]{1,0:T(8,128)(2,1)S(1)}, u32[]{:S(2)}, u32[]{:S(2)}) collective-permute-start(bf16[96,1024]{1,0:T(8,128)(2,1)S(1)} %slice.17), channel_id=1, source_target_pairs={{0,4},{1,5},{2,6},{3,7},{4,0},{5,1},{6,2},{7,3},{8,12},{9,13},{10,... | collective-permute-start | bytes 589832 | tf_op jit(solution)/shard_map/ppermute | solution.py:40
  14.9 1.6 %collective-permute-start.2 = (bf16[96,1024]{1,0:T(8,128)(2,1)S(1)}, bf16[96,1024]{1,0:T(8,128)(2,1)S(1)}, u32[]{:S(2)}, u32[]{:S(2)}) collective-permute-start(bf16[96,1024]{1,0:T(8,128)(2,1)S(1)} %slice.16), channel_id=1, source_target_pairs={{0,2},{1,3},{2,0},{3,1},{4,6},{5,7},{6,4},{7,5},{8,10},{9,11},{10,... | collective-permute-start | bytes 589832 | tf_op jit(solution)/shard_map/ppermute | solution.py:40
  16.4 2.7 %collective-permute-done.3 = bf16[96,1024]{1,0:T(8,128)(2,1)S(1)} collective-permute-done((bf16[96,1024]{1,0:T(8,128)(2,1)S(1)}, bf16[96,1024]{1,0:T(8,128)(2,1)S(1)}, u32[]{:S(2)}, u32[]{:S(2)}) %collective-permute-start.3) | collective-permute-done | bytes 196640 | tf_op jit(solution)/shard_map/ppermute | solution.py:40
  19.2 1.4 %collective-permute-done.2 = bf16[96,1024]{1,0:T(8,128)(2,1)S(1)} collective-permute-done((bf16[96,1024]{1,0:T(8,128)(2,1)S(1)}, bf16[96,1024]{1,0:T(8,128)(2,1)S(1)}, u32[]{:S(2)}, u32[]{:S(2)}) %collective-permute-start.2) | collective-permute-done | bytes 196640 | tf_op jit(solution)/shard_map/ppermute | solution.py:40
  21.4 1.6 %constant_dynamic-slice_fusion.6 = (bf16[1,192,384]{2,1,0:T(8,128)(2,1)S(1)}, bf16[1,192,384]{2,1,0:T(8,128)(2,1)S(1)}, bf16[1,192,384]{2,1,0:T(8,128)(2,1)S(1)}...) fusion(bf16[8,192,384]{2,1,0:T(8,128)(2,1)} %bitcast.61, ...), kind=kLoop, calls=%fused_computation.81 | loop fusion | bytes 2359328 | tf_op jit(solution)/shard_map/dynamic_slice | solution.py:53
  23.5 1.0 convert_add_fusion
  25.3 1.0 bitcast_add_fusion
  27.8 0.9 collective-permute-done.5
  28.7 1.6 %collective-permute-start.6 = (f32[16,1024]{1,0:T(8,128)S(1)}, f32[16,1024]{1,0:T(8,128)S(1)}, u32[]{:S(2)}, u32[]{:S(2)}) collective-permute-start(f32[16,1024]{1,0:T(8,128)S(1)} %dynamic-slice_add_fusion.2), channel_id=1, source_target_pairs={{0,2},{1,3},{2,0},{3,1},{4,6},{5,7},{6,4},{7,5},{8,10},{9,11},{10,... | collective-permute-start | bytes 196616 | tf_op jit(solution)/shard_map/ppermute | solution.py:68
  30.3 2.9 %collective-permute-done.6 = f32[16,1024]{1,0:T(8,128)S(1)} collective-permute-done((f32[16,1024]{1,0:T(8,128)S(1)}, f32[16,1024]{1,0:T(8,128)S(1)}, u32[]{:S(2)}, u32[]{:S(2)}) %collective-permute-start.6) | collective-permute-done | bytes 65568 | tf_op jit(solution)/shard_map/ppermute | solution.py:68
  33.2 1.2 collective-permute-start.7
  34.4 3.1 %collective-permute-done.7 = f32[16,1024]{1,0:T(8,128)S(1)} collective-permute-done((f32[16,1024]{1,0:T(8,128)S(1)}, f32[16,1024]{1,0:T(8,128)S(1)}, u32[]{:S(2)}, u32[]{:S(2)}) %collective-permute-start.7) | collective-permute-done | bytes 65568 | tf_op jit(solution)/shard_map/ppermute | solution.py:68
  37.5 1.6 %collective-permute-start.8 = (f32[16,1024]{1,0:T(8,128)S(1)}, f32[16,1024]{1,0:T(8,128)S(1)}, u32[]{:S(2)}, u32[]{:S(2)}) collective-permute-start(f32[16,1024]{1,0:T(8,128)S(1)} %add.153), channel_id=1, source_target_pairs={{0,8},{1,9},{2,10},{3,11},{4,12},{5,13},{6,14},{7,15},{8,0},{9,1},... | collective-permute-start | bytes 196616 | tf_op jit(solution)/shard_map/ppermute | solution.py:68
  39.2 2.7 %collective-permute-done.8 = f32[16,1024]{1,0:T(8,128)S(1)} collective-permute-done((f32[16,1024]{1,0:T(8,128)S(1)}, f32[16,1024]{1,0:T(8,128)S(1)}, u32[]{:S(2)}, u32[]{:S(2)}) %collective-permute-start.8) | collective-permute-done | bytes 65568 | tf_op jit(solution)/shard_map/ppermute | solution.py:68
  41.9 2.9 %collective-permute-start.9 = (f32[16,1024]{1,0:T(8,128)S(1)}, f32[16,1024]{1,0:T(8,128)S(1)}, u32[]{:S(2)}, u32[]{:S(2)}) collective-permute-start(f32[16,1024]{1,0:T(8,128)S(1)} %add.154), channel_id=1, source_target_pairs={{0,16},{1,17},{2,18},{3,19},{4,20},{5,21},{6,22},{7,23},{8,24},{9,... | collective-permute-start | bytes 196616 | tf_op jit(solution)/shard_map/ppermute | solution.py:68
  44.8 2.3 %collective-permute-done.9 = f32[16,1024]{1,0:T(8,128)S(1)} collective-permute-done((f32[16,1024]{1,0:T(8,128)S(1)}, f32[16,1024]{1,0:T(8,128)S(1)}, u32[]{:S(2)}, u32[]{:S(2)}) %collective-permute-start.9) | collective-permute-done | bytes 65568 | tf_op jit(solution)/shard_map/ppermute | solution.py:68
  47.2 1.2 collective-permute-done.10
  48.8 2.9 %cholesky.44 = f32[32,32]{1,0:T(8,128)S(1)} custom-call(f32[32,32]{1,0:T(8,128)S(1)} %fusion.46), custom_call_target="Cholesky" | custom-call | tf_op jit(solution)/shard_map/jit(cholesky)/cholesky | solution.py:184
  53.1 2.4 %custom-call.6 = f32[1,32,32]{1,2,0:T(8,128)S(1)} custom-call(f32[1,32,32]{2,1,0:T(8,128)S(1)} %fusion.41), custom_call_target="InvertDiagBlocksLowerTriangular" | custom-call | tf_op jit(solution)/shard_map/jit(_solve_triangular)/triangular_solve | solution.py:185
  56.4 1.6 %collective-permute-start.11 = (f32[32,384]{1,0:T(8,128)S(1)}, f32[32,384]{1,0:T(8,128)S(1)}, u32[]{:S(2)}, u32[]{:S(2)}) collective-permute-start(f32[32,384]{1,0:T(8,128)S(1)} %fusion.58), channel_id=1, source_target_pairs={{0,8},{8,0},{16,24},{24,16},{1,9},{9,1},{17,25},{25,17},{2,10},{10... | collective-permute-start | bytes 147464 | tf_op jit(solution)/shard_map/ppermute | solution.py:25
  58.0 1.1 select_reduce_fusion
  59.2 1.4 %collective-permute-done.11 = f32[32,384]{1,0:T(8,128)S(1)} collective-permute-done((f32[32,384]{1,0:T(8,128)S(1)}, f32[32,384]{1,0:T(8,128)S(1)}, u32[]{:S(2)}, u32[]{:S(2)}) %collective-permute-start.11) | collective-permute-done | bytes 49184 | tf_op jit(solution)/shard_map/ppermute | solution.py:25
  60.6 3.0 %collective-permute-start.12 = (f32[32,384]{1,0:T(8,128)S(1)}, f32[32,384]{1,0:T(8,128)S(1)}, u32[]{:S(2)}, u32[]{:S(2)}) collective-permute-start(f32[32,384]{1,0:T(8,128)S(1)} %add.156), channel_id=1, source_target_pairs={{0,16},{8,24},{16,0},{24,8},{1,17},{9,25},{17,1},{25,9},{2,18},{10... | collective-permute-start | bytes 147464 | tf_op jit(solution)/shard_map/ppermute | solution.py:25
  63.6 3.1 %fusion = f32[1600,128]{1,0:T(8,128)S(1)} fusion(bf16[1536,128]{1,0:T(8,128)(2,1)S(1)} %copy-done, s32[1536]{0:T(1024)S(1)} %select_reduce_fusion), kind=kOutput, calls=%fused_computation.1 | convolution fusion | flops 631603200 | bytes 1218560 | tf_op jit(solution)/shard_map/dot_general | solution.py:99
  66.7 0.8 fusion.35
  68.4 1.9 %collective-permute-start.21 = (f32[2,400,128]{2,1,0:T(8,128)}, f32[2,400,128]{2,1,0:T(8,128)}, u32[]{:S(2)}, u32[]{:S(2)}) collective-permute-start(f32[2,400,128]{2,1,0:T(8,128)} %dynamic-slice_bitcast_fusion), channel_id=1, source_target_pairs={{0,8},{8,0},{16,24},{24,16},{1,9},{9,1},{17,25},{25,17},{2,10},{10... | collective-permute-start | bytes 1228808 | tf_op jit(solution)/shard_map/ppermute | solution.py:111
  70.4 1.6 %collective-permute-start.14 = (f32[16,1024]{1,0:T(8,128)S(1)}, f32[16,1024]{1,0:T(8,128)S(1)}, u32[]{:S(2)}, u32[]{:S(2)}) collective-permute-start(f32[16,1024]{1,0:T(8,128)S(1)} %dynamic-slice_add_fusion.1), channel_id=1, source_target_pairs={{0,2},{1,3},{2,0},{3,1},{4,6},{5,7},{6,4},{7,5},{8,10},{9,11},{10,... | collective-permute-start | bytes 196616 | tf_op jit(solution)/shard_map/ppermute | solution.py:68
  71.9 2.8 %collective-permute-done.14 = f32[16,1024]{1,0:T(8,128)S(1)} collective-permute-done((f32[16,1024]{1,0:T(8,128)S(1)}, f32[16,1024]{1,0:T(8,128)S(1)}, u32[]{:S(2)}, u32[]{:S(2)}) %collective-permute-start.14) | collective-permute-done | bytes 65568 | tf_op jit(solution)/shard_map/ppermute | solution.py:68
  74.7 1.2 collective-permute-start.15
  75.9 3.1 %collective-permute-done.15 = f32[16,1024]{1,0:T(8,128)S(1)} collective-permute-done((f32[16,1024]{1,0:T(8,128)S(1)}, f32[16,1024]{1,0:T(8,128)S(1)}, u32[]{:S(2)}, u32[]{:S(2)}) %collective-permute-start.15) | collective-permute-done | bytes 65568 | tf_op jit(solution)/shard_map/ppermute | solution.py:68
  79.6 3.8 %collective-permute-done.16 = f32[16,1024]{1,0:T(8,128)S(1)} collective-permute-done((f32[16,1024]{1,0:T(8,128)S(1)}, f32[16,1024]{1,0:T(8,128)S(1)}, u32[]{:S(2)}, u32[]{:S(2)}) %collective-permute-start.16) | collective-permute-done | bytes 65568 | tf_op jit(solution)/shard_map/ppermute | solution.py:68
  83.4 2.0 %collective-permute-start.17 = (f32[16,1024]{1,0:T(8,128)S(1)}, f32[16,1024]{1,0:T(8,128)S(1)}, u32[]{:S(2)}, u32[]{:S(2)}) collective-permute-start(f32[16,1024]{1,0:T(8,128)S(1)} %add.161), channel_id=1, source_target_pairs={{0,16},{1,17},{2,18},{3,19},{4,20},{5,21},{6,22},{7,23},{8,24},{9,... | collective-permute-start | bytes 196616 | tf_op jit(solution)/shard_map/ppermute | solution.py:68
  85.4 1.0 bitcast_add_fusion.1
  86.4 2.8 %collective-permute-done.17 = f32[16,1024]{1,0:T(8,128)S(1)} collective-permute-done((f32[16,1024]{1,0:T(8,128)S(1)}, f32[16,1024]{1,0:T(8,128)S(1)}, u32[]{:S(2)}, u32[]{:S(2)}) %collective-permute-start.17) | collective-permute-done | bytes 65568 | tf_op jit(solution)/shard_map/ppermute | solution.py:68
  89.4 1.4 %collective-permute-start.22 = (f32[1,400,128]{2,1,0:T(8,128)S(1)}, f32[1,400,128]{2,1,0:T(8,128)S(1)}, u32[]{:S(2)}, u32[]{:S(2)}) collective-permute-start(f32[1,400,128]{2,1,0:T(8,128)S(1)} %constant_dynamic-slice_fusion), channel_id=1, source_target_pairs={{0,16},{8,24},{16,0},{24,8},{1,17},{9,25},{17,1},{25,9},{2,18},{10... | collective-permute-start | bytes 614408 | tf_op jit(solution)/shard_map/ppermute | solution.py:111
  91.3 2.9 %cholesky.55 = f32[32,32]{1,0:T(8,128)S(1)} custom-call(f32[32,32]{1,0:T(8,128)S(1)} %fusion.44), custom_call_target="Cholesky" | custom-call | tf_op jit(solution)/shard_map/jit(cholesky)/cholesky | solution.py:184
  95.6 2.4 %custom-call.7 = f32[1,32,32]{1,2,0:T(8,128)S(1)} custom-call(f32[1,32,32]{2,1,0:T(8,128)S(1)} %fusion.42), custom_call_target="InvertDiagBlocksLowerTriangular" | custom-call | tf_op jit(solution)/shard_map/jit(_solve_triangular)/triangular_solve | solution.py:185
  99.4 3.6 %collective-permute-done.19 = f32[32,384]{1,0:T(8,128)S(1)} collective-permute-done((f32[32,384]{1,0:T(8,128)S(1)}, f32[32,384]{1,0:T(8,128)S(1)}, u32[]{:S(2)}, u32[]{:S(2)}) %collective-permute-start.19) | collective-permute-done | bytes 49184 | tf_op jit(solution)/shard_map/ppermute | solution.py:25
  103.1 1.6 %collective-permute-start.20 = (f32[32,384]{1,0:T(8,128)S(1)}, f32[32,384]{1,0:T(8,128)S(1)}, u32[]{:S(2)}, u32[]{:S(2)}) collective-permute-start(f32[32,384]{1,0:T(8,128)S(1)} %add.163), channel_id=1, source_target_pairs={{0,16},{8,24},{16,0},{24,8},{1,17},{9,25},{17,1},{25,9},{2,18},{10... | collective-permute-start | bytes 147464 | tf_op jit(solution)/shard_map/ppermute | solution.py:25
  105.4 3.1 %collective-permute-done.20 = f32[32,384]{1,0:T(8,128)S(1)} collective-permute-done((f32[32,384]{1,0:T(8,128)S(1)}, f32[32,384]{1,0:T(8,128)S(1)}, u32[]{:S(2)}, u32[]{:S(2)}) %collective-permute-start.20) | collective-permute-done | bytes 49184 | tf_op jit(solution)/shard_map/ppermute | solution.py:25
  108.5 0.8 fusion.40
  109.4 1.1 fusion.7
  110.6 1.0 fusion.57
  111.5 17.7 %all_gather.3 = bf16[1024,384]{1,0:T(8,128)(2,1)S(1)} all-gather(bf16[256,384]{1,0:T(8,128)(2,1)S(1)} %get-tuple-element.12), channel_id=1, replica_groups=mesh['rep'=4,'tp'=8] {'rep'}, dimensions={0}, use_global_device_ids=true | all-gather | bytes 983040 | tf_op jit(solution)/shard_map/all_gather | solution.py:199
  129.8 0.9 copy.25
  (91 shorter events, 12.3 us)
Async XLA Ops:
  0.6 63.0 %copy-start = (bf16[1536,128]{1,0:T(8,128)(2,1)S(1)}, bf16[1536,128]{1,0:T(8,128)(2,1)}, u32[]{:S(2)}) copy-start(bf16[1536,128]{1,0:T(8,128)(2,1)} %param.19) | copy-start | bytes 1179652
  0.6 20.0 %copy-start.7 = (bf16[192,1024]{1,0:T(8,128)(2,1)S(1)}, bf16[192,1024]{1,0:T(8,128)(2,1)}, u32[]{:S(2)}) copy-start(bf16[192,1024]{1,0:T(8,128)(2,1)} %param.13) | copy-start | bytes 1179652
  0.7 12.3 %collective-permute-start = (bf16[192,1024]{1,0:T(8,128)(2,1)}, bf16[192,1024]{1,0:T(8,128)(2,1)S(1)}, u32[]{:S(2)}, u32[]{:S(2)}) collective-permute-start(bf16[192,1024]{1,0:T(8,128)(2,1)} %param.13), channel_id=1, source_target_pairs={{0,2},{1,3},{2,0},{3,1},{4,6},{5,7},{6,4},{7,5},{8,10},{9,11},{10,... | collective-permute-start | bytes 1179656 | tf_op jit(solution)/shard_map/ppermute | solution.py:40
  3.7 11.2 %collective-permute-start.1 = (bf16[192,1024]{1,0:T(8,128)(2,1)}, bf16[192,1024]{1,0:T(8,128)(2,1)S(1)}, u32[]{:S(2)}, u32[]{:S(2)}) collective-permute-start(bf16[192,1024]{1,0:T(8,128)(2,1)} %param.13), channel_id=1, source_target_pairs={{0,4},{1,5},{2,6},{3,7},{4,0},{5,1},{6,2},{7,3},{8,12},{9,13},{10,... | collective-permute-start | bytes 1179656 | tf_op jit(solution)/shard_map/ppermute | solution.py:40
  13.0 7.9 %copy-start.3 = (bf16[192,1024]{1,0:T(8,128)(2,1)}, bf16[192,1024]{1,0:T(8,128)(2,1)S(1)}, u32[]{:S(2)}) copy-start(bf16[192,1024]{1,0:T(8,128)(2,1)S(1)} %collective-permute-done) | copy-start | bytes 1179652
  13.0 6.2 %collective-permute-start.3 = (bf16[96,1024]{1,0:T(8,128)(2,1)S(1)}, bf16[96,1024]{1,0:T(8,128)(2,1)S(1)}, u32[]{:S(2)}, u32[]{:S(2)}) collective-permute-start(bf16[96,1024]{1,0:T(8,128)(2,1)S(1)} %slice.17), channel_id=1, source_target_pairs={{0,4},{1,5},{2,6},{3,7},{4,0},{5,1},{6,2},{7,3},{8,12},{9,13},{10,... | collective-permute-start | bytes 589832 | tf_op jit(solution)/shard_map/ppermute | solution.py:40
  14.8 6.0 %copy-start.5 = (bf16[192,1024]{1,0:T(8,128)(2,1)}, bf16[192,1024]{1,0:T(8,128)(2,1)S(1)}, u32[]{:S(2)}) copy-start(bf16[192,1024]{1,0:T(8,128)(2,1)S(1)} %collective-permute-done.1) | copy-start | bytes 1179652
  14.9 5.7 %collective-permute-start.2 = (bf16[96,1024]{1,0:T(8,128)(2,1)S(1)}, bf16[96,1024]{1,0:T(8,128)(2,1)S(1)}, u32[]{:S(2)}, u32[]{:S(2)}) collective-permute-start(bf16[96,1024]{1,0:T(8,128)(2,1)S(1)} %slice.16), channel_id=1, source_target_pairs={{0,2},{1,3},{2,0},{3,1},{4,6},{5,7},{6,4},{7,5},{8,10},{9,11},{10,... | collective-permute-start | bytes 589832 | tf_op jit(solution)/shard_map/ppermute | solution.py:40
  20.6 0.7 copy-start.1
  21.4 4.0 %collective-permute-start.4 = (bf16[4,192,1024]{2,1,0:T(8,128)(2,1)S(1)}, bf16[4,192,1024]{2,1,0:T(8,128)(2,1)S(1)}, u32[]{:S(2)}, u32[]{:S(2)}) collective-permute-start(bf16[4,192,1024]{2,1,0:T(8,128)(2,1)S(1)} %pad_maximum_fusion), channel_id=1, source_target_pairs={{0,1},{1,0},{2,3},{3,2},{4,5},{5,4},{6,7},{7,6},{8,9},{9,8},{10,11... | collective-permute-start | bytes 4718600 | tf_op jit(solution)/shard_map/ppermute | solution.py:40
  21.4 1.7 %copy-start.2 = (bf16[1,192,1024]{2,1,0:T(8,128)(2,1)S(1)}, bf16[1,192,1024]{2,1,0:T(8,128)(2,1)}, u32[]{:S(2)}) copy-start(bf16[1,192,1024]{2,1,0:T(8,128)(2,1)} %copy-done.1) | copy-start | bytes 1179652
  21.4 1.7 %copy-start.4 = (bf16[192,1024]{1,0:T(8,128)(2,1)S(1)}, bf16[192,1024]{1,0:T(8,128)(2,1)}, u32[]{:S(2)}) copy-start(bf16[192,1024]{1,0:T(8,128)(2,1)} %copy-done.3) | copy-start | bytes 1179652
  21.4 1.7 %copy-start.6 = (bf16[192,1024]{1,0:T(8,128)(2,1)S(1)}, bf16[192,1024]{1,0:T(8,128)(2,1)}, u32[]{:S(2)}) copy-start(bf16[192,1024]{1,0:T(8,128)(2,1)} %copy-done.5) | copy-start | bytes 1179652
  21.4 1.8 %copy-start.8 = (bf16[192,1024]{1,0:T(8,128)(2,1)S(1)}, bf16[192,1024]{1,0:T(8,128)(2,1)}, u32[]{:S(2)}) copy-start(bf16[192,1024]{1,0:T(8,128)(2,1)} %param.13) | copy-start | bytes 1179652
  21.4 2.1 %copy-start.13 = (bf16[1,1024,384]{2,1,0:T(8,128)(2,1)S(1)}, bf16[1,1024,384]{2,1,0:T(8,128)(2,1)}, u32[]{:S(2)}) copy-start(bf16[1,1024,384]{2,1,0:T(8,128)(2,1)} %param.15) | copy-start | bytes 2359300
  23.5 1.0 copy-start.12
  27.3 1.5 %collective-permute-start.5 = (f32[16,1024]{1,0:T(8,128)S(1)}, f32[16,1024]{1,0:T(8,128)S(1)}, u32[]{:S(2)}, u32[]{:S(2)}) collective-permute-start(f32[16,1024]{1,0:T(8,128)S(1)} %constant_dynamic-slice_fusion.2), channel_id=1, source_target_pairs={{0,1},{1,0},{2,3},{3,2},{4,5},{5,4},{6,7},{7,6},{8,9},{9,8},{10,11... | collective-permute-start | bytes 196616 | tf_op jit(solution)/shard_map/ppermute | solution.py:68
  28.7 4.4 %collective-permute-start.6 = (f32[16,1024]{1,0:T(8,128)S(1)}, f32[16,1024]{1,0:T(8,128)S(1)}, u32[]{:S(2)}, u32[]{:S(2)}) collective-permute-start(f32[16,1024]{1,0:T(8,128)S(1)} %dynamic-slice_add_fusion.2), channel_id=1, source_target_pairs={{0,2},{1,3},{2,0},{3,1},{4,6},{5,7},{6,4},{7,5},{8,10},{9,11},{10,... | collective-permute-start | bytes 196616 | tf_op jit(solution)/shard_map/ppermute | solution.py:68
  33.2 24.9 %copy-start.14 = (s32[1600]{0:T(1024)S(1)}, s32[1600]{0:T(1024)}, u32[]{:S(2)}) copy-start(s32[1600]{0:T(1024)} %param.21) | copy-start | bytes 19204
  33.2 24.9 %copy-start.15 = (s32[1536]{0:T(1024)S(1)}, s32[1536]{0:T(1024)}, u32[]{:S(2)}) copy-start(s32[1536]{0:T(1024)} %param.20) | copy-start | bytes 18436
  33.2 4.3 %collective-permute-start.7 = (f32[16,1024]{1,0:T(8,128)S(1)}, f32[16,1024]{1,0:T(8,128)S(1)}, u32[]{:S(2)}, u32[]{:S(2)}) collective-permute-start(f32[16,1024]{1,0:T(8,128)S(1)} %add.152), channel_id=1, source_target_pairs={{0,4},{1,5},{2,6},{3,7},{4,0},{5,1},{6,2},{7,3},{8,12},{9,13},{10,... | collective-permute-start | bytes 196616 | tf_op jit(solution)/shard_map/ppermute | solution.py:68
  37.5 4.3 %collective-permute-start.8 = (f32[16,1024]{1,0:T(8,128)S(1)}, f32[16,1024]{1,0:T(8,128)S(1)}, u32[]{:S(2)}, u32[]{:S(2)}) collective-permute-start(f32[16,1024]{1,0:T(8,128)S(1)} %add.153), channel_id=1, source_target_pairs={{0,8},{1,9},{2,10},{3,11},{4,12},{5,13},{6,14},{7,15},{8,0},{9,1},... | collective-permute-start | bytes 196616 | tf_op jit(solution)/shard_map/ppermute | solution.py:68
  41.9 5.2 %collective-permute-start.9 = (f32[16,1024]{1,0:T(8,128)S(1)}, f32[16,1024]{1,0:T(8,128)S(1)}, u32[]{:S(2)}, u32[]{:S(2)}) collective-permute-start(f32[16,1024]{1,0:T(8,128)S(1)} %add.154), channel_id=1, source_target_pairs={{0,16},{1,17},{2,18},{3,19},{4,20},{5,21},{6,22},{7,23},{8,24},{9,... | collective-permute-start | bytes 196616 | tf_op jit(solution)/shard_map/ppermute | solution.py:68
  47.1 1.3 %collective-permute-start.10 = (f32[16,1024]{1,0:T(8,128)S(1)}, f32[16,1024]{1,0:T(8,128)S(1)}, u32[]{:S(2)}, u32[]{:S(2)}) collective-permute-start(f32[16,1024]{1,0:T(8,128)S(1)} %get-tuple-element.18), channel_id=1, source_target_pairs={{0,1},{1,0},{2,3},{3,2},{4,5},{5,4},{6,7},{7,6},{8,9},{9,8},{10,11... | collective-permute-start | bytes 196616 | tf_op jit(solution)/shard_map/ppermute | solution.py:68
  56.4 4.2 %collective-permute-start.11 = (f32[32,384]{1,0:T(8,128)S(1)}, f32[32,384]{1,0:T(8,128)S(1)}, u32[]{:S(2)}, u32[]{:S(2)}) collective-permute-start(f32[32,384]{1,0:T(8,128)S(1)} %fusion.58), channel_id=1, source_target_pairs={{0,8},{8,0},{16,24},{24,16},{1,9},{9,1},{17,25},{25,17},{2,10},{10... | collective-permute-start | bytes 147464 | tf_op jit(solution)/shard_map/ppermute | solution.py:25
  60.6 6.1 %collective-permute-start.12 = (f32[32,384]{1,0:T(8,128)S(1)}, f32[32,384]{1,0:T(8,128)S(1)}, u32[]{:S(2)}, u32[]{:S(2)}) collective-permute-start(f32[32,384]{1,0:T(8,128)S(1)} %add.156), channel_id=1, source_target_pairs={{0,16},{8,24},{16,0},{24,8},{1,17},{9,25},{17,1},{25,9},{2,18},{10... | collective-permute-start | bytes 147464 | tf_op jit(solution)/shard_map/ppermute | solution.py:25
  67.5 2.8 %collective-permute-start.13 = (f32[16,1024]{1,0:T(8,128)S(1)}, f32[16,1024]{1,0:T(8,128)S(1)}, u32[]{:S(2)}, u32[]{:S(2)}) collective-permute-start(f32[16,1024]{1,0:T(8,128)S(1)} %constant_dynamic-slice_fusion.1), channel_id=1, source_target_pairs={{0,1},{1,0},{2,3},{3,2},{4,5},{5,4},{6,7},{7,6},{8,9},{9,8},{10,11... | collective-permute-start | bytes 196616 | tf_op jit(solution)/shard_map/ppermute | solution.py:68
  68.4 17.0 %collective-permute-start.21 = (f32[2,400,128]{2,1,0:T(8,128)}, f32[2,400,128]{2,1,0:T(8,128)}, u32[]{:S(2)}, u32[]{:S(2)}) collective-permute-start(f32[2,400,128]{2,1,0:T(8,128)} %dynamic-slice_bitcast_fusion), channel_id=1, source_target_pairs={{0,8},{8,0},{16,24},{24,16},{1,9},{9,1},{17,25},{25,17},{2,10},{10... | collective-permute-start | bytes 1228808 | tf_op jit(solution)/shard_map/ppermute | solution.py:111
  70.4 4.3 %collective-permute-start.14 = (f32[16,1024]{1,0:T(8,128)S(1)}, f32[16,1024]{1,0:T(8,128)S(1)}, u32[]{:S(2)}, u32[]{:S(2)}) collective-permute-start(f32[16,1024]{1,0:T(8,128)S(1)} %dynamic-slice_add_fusion.1), channel_id=1, source_target_pairs={{0,2},{1,3},{2,0},{3,1},{4,6},{5,7},{6,4},{7,5},{8,10},{9,11},{10,... | collective-permute-start | bytes 196616 | tf_op jit(solution)/shard_map/ppermute | solution.py:68
  74.7 4.3 %collective-permute-start.15 = (f32[16,1024]{1,0:T(8,128)S(1)}, f32[16,1024]{1,0:T(8,128)S(1)}, u32[]{:S(2)}, u32[]{:S(2)}) collective-permute-start(f32[16,1024]{1,0:T(8,128)S(1)} %add.159), channel_id=1, source_target_pairs={{0,4},{1,5},{2,6},{3,7},{4,0},{5,1},{6,2},{7,3},{8,12},{9,13},{10,... | collective-permute-start | bytes 196616 | tf_op jit(solution)/shard_map/ppermute | solution.py:68
  79.0 4.3 %collective-permute-start.16 = (f32[16,1024]{1,0:T(8,128)S(1)}, f32[16,1024]{1,0:T(8,128)S(1)}, u32[]{:S(2)}, u32[]{:S(2)}) collective-permute-start(f32[16,1024]{1,0:T(8,128)S(1)} %add.160), channel_id=1, source_target_pairs={{0,8},{1,9},{2,10},{3,11},{4,12},{5,13},{6,14},{7,15},{8,0},{9,1},... | collective-permute-start | bytes 196616 | tf_op jit(solution)/shard_map/ppermute | solution.py:68
  83.4 5.8 %collective-permute-start.17 = (f32[16,1024]{1,0:T(8,128)S(1)}, f32[16,1024]{1,0:T(8,128)S(1)}, u32[]{:S(2)}, u32[]{:S(2)}) collective-permute-start(f32[16,1024]{1,0:T(8,128)S(1)} %add.161), channel_id=1, source_target_pairs={{0,16},{1,17},{2,18},{3,19},{4,20},{5,21},{6,22},{7,23},{8,24},{9,... | collective-permute-start | bytes 196616 | tf_op jit(solution)/shard_map/ppermute | solution.py:68
  89.2 15.5 %copy-start.11 = (f32[400,128]{1,0:T(8,128)S(1)}, f32[400,128]{1,0:T(8,128)}, u32[]{:S(2)}) copy-start(f32[400,128]{1,0:T(8,128)} %param.22) | copy-start | bytes 614404
  89.3 1.5 %collective-permute-start.18 = (f32[16,1024]{1,0:T(8,128)S(1)}, f32[16,1024]{1,0:T(8,128)S(1)}, u32[]{:S(2)}, u32[]{:S(2)}) collective-permute-start(f32[16,1024]{1,0:T(8,128)S(1)} %get-tuple-element.16), channel_id=1, source_target_pairs={{0,1},{1,0},{2,3},{3,2},{4,5},{5,4},{6,7},{7,6},{8,9},{9,8},{10,11... | collective-permute-start | bytes 196616 | tf_op jit(solution)/shard_map/ppermute | solution.py:68
  89.4 15.4 %collective-permute-start.22 = (f32[1,400,128]{2,1,0:T(8,128)S(1)}, f32[1,400,128]{2,1,0:T(8,128)S(1)}, u32[]{:S(2)}, u32[]{:S(2)}) collective-permute-start(f32[1,400,128]{2,1,0:T(8,128)S(1)} %constant_dynamic-slice_fusion), channel_id=1, source_target_pairs={{0,16},{8,24},{16,0},{24,8},{1,17},{9,25},{17,1},{25,9},{2,18},{10... | collective-permute-start | bytes 614408 | tf_op jit(solution)/shard_map/ppermute | solution.py:111
  98.9 4.2 %collective-permute-start.19 = (f32[32,384]{1,0:T(8,128)S(1)}, f32[32,384]{1,0:T(8,128)S(1)}, u32[]{:S(2)}, u32[]{:S(2)}) collective-permute-start(f32[32,384]{1,0:T(8,128)S(1)} %fusion.59), channel_id=1, source_target_pairs={{0,8},{8,0},{16,24},{24,16},{1,9},{9,1},{17,25},{25,17},{2,10},{10... | collective-permute-start | bytes 147464 | tf_op jit(solution)/shard_map/ppermute | solution.py:25
  103.1 5.5 %collective-permute-start.20 = (f32[32,384]{1,0:T(8,128)S(1)}, f32[32,384]{1,0:T(8,128)S(1)}, u32[]{:S(2)}, u32[]{:S(2)}) collective-permute-start(f32[32,384]{1,0:T(8,128)S(1)} %add.163), channel_id=1, source_target_pairs={{0,16},{8,24},{16,0},{24,8},{1,17},{9,25},{17,1},{25,9},{2,18},{10... | collective-permute-start | bytes 147464 | tf_op jit(solution)/shard_map/ppermute | solution.py:25
  109.4 1.2 copy-start.9
  109.4 1.2 copy-start.10

commit v14 on v13

--- a/solution.py
+++ b/solution.py
@@ -41,10 +41,7 @@
 
     from_x = exchange(block, 2)
     from_y = exchange(block, 4)
-    half = block.shape[0] // 2
-    diagonal = jnp.concatenate(
-        [exchange(from_y[:half], 2), exchange(from_x[half:], 4)], axis=0
-    )
+    diagonal = exchange(block, 6)
     mine = jnp.stack([block, from_x, from_y, diagonal])
     other = exchange(mine, 1)
     rows = block.shape[0]

time: 131 us -> 134 us (1.023)
  waiting for transfers between devices: 45.8 us -> 48.3 us
    ppermute x5 -> x4, waiting for transfers between devices: 12 us -> 17.4 us  [exchange(): return lax.ppermute(value, axis, [(i, i ^ stride) for i in range(count)])]
    ppermute x5 -> x4, starting transfers between devices: 7.91 us -> 4.67 us  [exchange(): return lax.ppermute(value, axis, [(i, i ^ stride) for i in range(count)])]
    ppermute x12, starting transfers between devices: 13.4 us -> 15 us  [exchange(): return lax.ppermute(piece, axes, [(i, i ^ stride) for i in range(count)])]
    ppermute x12, waiting for transfers between devices: 25.6 us -> 24 us  [exchange(): return lax.ppermute(piece, axes, [(i, i ^ stride) for i in range(count)])]
  transfers between devices with their start and end apart: 23 -> 22, of which waited for: 16 -> 16; matrix products, arithmetic and copies ran while one was open for 14% -> 13% of each run, Pallas kernels for 0% -> 0%
where the time goes in v14:
time: 134 us
  waiting for transfers between devices  48.3 us (36%)
  starting transfers between devices  31.1 us (23%)
  other arithmetic  20.5 us (15%)
  blocking collectives  18.7 us (14%)
  matrix products  10.7 us (8%)
  local copies, waits for them, and re-layouts  3.22 us (2%)
    ppermute x12, waiting for transfers between devices, exchange(): return lax.ppermute(piece, axes, [(i, i ^ stride) for i in range(count)])  24 us
    all_gather x1, blocking collectives, shards(): lax.all_gather(master_new.astype(jnp.bfloat16), 'rep', axis=0, tiled=True)  18.7 us
    ppermute x4, waiting for transfers between devices, exchange(): return lax.ppermute(value, axis, [(i, i ^ stride) for i in range(count)])  17.4 us
    ppermute x12, starting transfers between devices, exchange(): return lax.ppermute(piece, axes, [(i, i ^ stride) for i in range(count)])  15 us
    ppermute x4, starting transfers between devices, tree_sum(): value = value + lax.ppermute(value, axes, pairs)  7.99 us
    another operation x6, other arithmetic, shards(): factor_low = jnp.linalg.cholesky(gram_matrix)  7.29 us
    ppermute x4, waiting for transfers between devices, tree_sum(): value = value + lax.ppermute(value, axes, pairs)  6.84 us
    another operation x4, other arithmetic, shards(): jax.scipy.linalg.solve_triangular(factor_low, left_rows, lower=True)  6.17 us
  transfers between devices with their start and end apart: 22, of which 16 were waited for; matrix products, arithmetic and copies ran while one was open for 13% of the time, Pallas kernels for 0%

profile of v14, /device:TPU:0, one launch (start us, length us, event | category | flops | bytes accessed | tf_op | source)
XLA Modules:
  0.0 133.6 jit_solution(15492122255961262136)
XLA Ops:
  0.6 4.0 %collective-permute-start.2 = (bf16[192,1024]{1,0:T(8,128)(2,1)}, bf16[192,1024]{1,0:T(8,128)(2,1)S(1)}, u32[]{:S(2)}, u32[]{:S(2)}) collective-permute-start(bf16[192,1024]{1,0:T(8,128)(2,1)} %param.13), channel_id=1, source_target_pairs={{0,6},{1,7},{2,4},{3,5},{4,2},{5,3},{6,0},{7,1},{8,14},{9,15},{10,... | collective-permute-start | bytes 1179656 | tf_op jit(solution)/shard_map/ppermute | solution.py:40
  5.3 9.6 %collective-permute-done.2 = bf16[192,1024]{1,0:T(8,128)(2,1)S(1)} collective-permute-done((bf16[192,1024]{1,0:T(8,128)(2,1)}, bf16[192,1024]{1,0:T(8,128)(2,1)S(1)}, u32[]{:S(2)}, u32[]{:S(2)}) %collective-permute-start.2) | collective-permute-done | bytes 393248 | tf_op jit(solution)/shard_map/ppermute | solution.py:40
  14.8 7.6 %collective-permute-done.1 = bf16[192,1024]{1,0:T(8,128)(2,1)S(1)} collective-permute-done((bf16[192,1024]{1,0:T(8,128)(2,1)}, bf16[192,1024]{1,0:T(8,128)(2,1)S(1)}, u32[]{:S(2)}, u32[]{:S(2)}) %collective-permute-start.1) | collective-permute-done | bytes 393248 | tf_op jit(solution)/shard_map/ppermute | solution.py:40
  22.7 1.3 pad_maximum_fusion
  24.2 1.6 %constant_dynamic-slice_fusion.6 = (bf16[1,192,384]{2,1,0:T(8,128)(2,1)S(1)}, bf16[1,192,384]{2,1,0:T(8,128)(2,1)S(1)}, bf16[1,192,384]{2,1,0:T(8,128)(2,1)S(1)}...) fusion(bf16[8,192,384]{2,1,0:T(8,128)(2,1)} %bitcast.60, ...), kind=kLoop, calls=%fused_computation.80 | loop fusion | bytes 2359328 | tf_op jit(solution)/shard_map/dynamic_slice | solution.py:50
  26.2 1.0 convert_add_fusion
  28.1 1.0 bitcast_add_fusion
  29.1 0.8 fusion.4
  30.5 0.9 collective-permute-done.4
  31.4 1.6 %collective-permute-start.5 = (f32[16,1024]{1,0:T(8,128)S(1)}, f32[16,1024]{1,0:T(8,128)S(1)}, u32[]{:S(2)}, u32[]{:S(2)}) collective-permute-start(f32[16,1024]{1,0:T(8,128)S(1)} %dynamic-slice_add_fusion.2), channel_id=1, source_target_pairs={{0,2},{1,3},{2,0},{3,1},{4,6},{5,7},{6,4},{7,5},{8,10},{9,11},{10,... | collective-permute-start | bytes 196616 | tf_op jit(solution)/shard_map/ppermute | solution.py:65
  33.1 2.8 %collective-permute-done.5 = f32[16,1024]{1,0:T(8,128)S(1)} collective-permute-done((f32[16,1024]{1,0:T(8,128)S(1)}, f32[16,1024]{1,0:T(8,128)S(1)}, u32[]{:S(2)}, u32[]{:S(2)}) %collective-permute-start.5) | collective-permute-done | bytes 65568 | tf_op jit(solution)/shard_map/ppermute | solution.py:65
  35.9 1.6 %collective-permute-start.6 = (f32[16,1024]{1,0:T(8,128)S(1)}, f32[16,1024]{1,0:T(8,128)S(1)}, u32[]{:S(2)}, u32[]{:S(2)}) collective-permute-start(f32[16,1024]{1,0:T(8,128)S(1)} %add.152), channel_id=1, source_target_pairs={{0,4},{1,5},{2,6},{3,7},{4,0},{5,1},{6,2},{7,3},{8,12},{9,13},{10,... | collective-permute-start | bytes 196616 | tf_op jit(solution)/shard_map/ppermute | solution.py:65
  37.5 2.7 %collective-permute-done.6 = f32[16,1024]{1,0:T(8,128)S(1)} collective-permute-done((f32[16,1024]{1,0:T(8,128)S(1)}, f32[16,1024]{1,0:T(8,128)S(1)}, u32[]{:S(2)}, u32[]{:S(2)}) %collective-permute-start.6) | collective-permute-done | bytes 65568 | tf_op jit(solution)/shard_map/ppermute | solution.py:65
  40.2 1.7 %collective-permute-start.7 = (f32[16,1024]{1,0:T(8,128)S(1)}, f32[16,1024]{1,0:T(8,128)S(1)}, u32[]{:S(2)}, u32[]{:S(2)}) collective-permute-start(f32[16,1024]{1,0:T(8,128)S(1)} %add.153), channel_id=1, source_target_pairs={{0,8},{1,9},{2,10},{3,11},{4,12},{5,13},{6,14},{7,15},{8,0},{9,1},... | collective-permute-start | bytes 196616 | tf_op jit(solution)/shard_map/ppermute | solution.py:65
  41.9 2.6 %collective-permute-done.7 = f32[16,1024]{1,0:T(8,128)S(1)} collective-permute-done((f32[16,1024]{1,0:T(8,128)S(1)}, f32[16,1024]{1,0:T(8,128)S(1)}, u32[]{:S(2)}, u32[]{:S(2)}) %collective-permute-start.7) | collective-permute-done | bytes 65568 | tf_op jit(solution)/shard_map/ppermute | solution.py:65
  44.6 3.0 %collective-permute-start.8 = (f32[16,1024]{1,0:T(8,128)S(1)}, f32[16,1024]{1,0:T(8,128)S(1)}, u32[]{:S(2)}, u32[]{:S(2)}) collective-permute-start(f32[16,1024]{1,0:T(8,128)S(1)} %add.154), channel_id=1, source_target_pairs={{0,16},{1,17},{2,18},{3,19},{4,20},{5,21},{6,22},{7,23},{8,24},{9,... | collective-permute-start | bytes 196616 | tf_op jit(solution)/shard_map/ppermute | solution.py:65
  47.6 2.3 %collective-permute-done.8 = f32[16,1024]{1,0:T(8,128)S(1)} collective-permute-done((f32[16,1024]{1,0:T(8,128)S(1)}, f32[16,1024]{1,0:T(8,128)S(1)}, u32[]{:S(2)}, u32[]{:S(2)}) %collective-permute-start.8) | collective-permute-done | bytes 65568 | tf_op jit(solution)/shard_map/ppermute | solution.py:65
  49.9 1.2 collective-permute-done.9
  51.5 2.9 %cholesky.44 = f32[32,32]{1,0:T(8,128)S(1)} custom-call(f32[32,32]{1,0:T(8,128)S(1)} %fusion.46), custom_call_target="Cholesky" | custom-call | tf_op jit(solution)/shard_map/jit(cholesky)/cholesky | solution.py:181
  55.8 2.4 %custom-call.6 = f32[1,32,32]{1,2,0:T(8,128)S(1)} custom-call(f32[1,32,32]{2,1,0:T(8,128)S(1)} %fusion.41), custom_call_target="InvertDiagBlocksLowerTriangular" | custom-call | tf_op jit(solution)/shard_map/jit(_solve_triangular)/triangular_solve | solution.py:182
  59.1 1.7 %collective-permute-start.10 = (f32[32,384]{1,0:T(8,128)S(1)}, f32[32,384]{1,0:T(8,128)S(1)}, u32[]{:S(2)}, u32[]{:S(2)}) collective-permute-start(f32[32,384]{1,0:T(8,128)S(1)} %fusion.58), channel_id=1, source_target_pairs={{0,8},{8,0},{16,24},{24,16},{1,9},{9,1},{17,25},{25,17},{2,10},{10... | collective-permute-start | bytes 147464 | tf_op jit(solution)/shard_map/ppermute | solution.py:25
  60.8 1.1 select_reduce_fusion
  61.9 1.3 %collective-permute-done.10 = f32[32,384]{1,0:T(8,128)S(1)} collective-permute-done((f32[32,384]{1,0:T(8,128)S(1)}, f32[32,384]{1,0:T(8,128)S(1)}, u32[]{:S(2)}, u32[]{:S(2)}) %collective-permute-start.10) | collective-permute-done | bytes 49184 | tf_op jit(solution)/shard_map/ppermute | solution.py:25
  63.3 3.1 %collective-permute-start.11 = (f32[32,384]{1,0:T(8,128)S(1)}, f32[32,384]{1,0:T(8,128)S(1)}, u32[]{:S(2)}, u32[]{:S(2)}) collective-permute-start(f32[32,384]{1,0:T(8,128)S(1)} %add.156), channel_id=1, source_target_pairs={{0,16},{8,24},{16,0},{24,8},{1,17},{9,25},{17,1},{25,9},{2,18},{10... | collective-permute-start | bytes 147464 | tf_op jit(solution)/shard_map/ppermute | solution.py:25
  66.4 3.1 %fusion = f32[1600,128]{1,0:T(8,128)S(1)} fusion(bf16[1536,128]{1,0:T(8,128)(2,1)S(1)} %copy-done, s32[1536]{0:T(1024)S(1)} %select_reduce_fusion), kind=kOutput, calls=%fused_computation.1 | convolution fusion | flops 631603200 | bytes 1218560 | tf_op jit(solution)/shard_map/dot_general | solution.py:96
  69.5 0.8 fusion.35
  70.4 2.0 %collective-permute-start.20 = (f32[2,400,128]{2,1,0:T(8,128)S(1)}, f32[2,400,128]{2,1,0:T(8,128)}, u32[]{:S(2)}, u32[]{:S(2)}) collective-permute-start(f32[2,400,128]{2,1,0:T(8,128)S(1)} %dynamic-slice_bitcast_fusion), channel_id=1, source_target_pairs={{0,8},{8,0},{16,24},{24,16},{1,9},{9,1},{17,25},{25,17},{2,10},{10... | collective-permute-start | bytes 1228808 | tf_op jit(solution)/shard_map/ppermute | solution.py:108
  72.4 1.6 %collective-permute-start.13 = (f32[16,1024]{1,0:T(8,128)S(1)}, f32[16,1024]{1,0:T(8,128)S(1)}, u32[]{:S(2)}, u32[]{:S(2)}) collective-permute-start(f32[16,1024]{1,0:T(8,128)S(1)} %dynamic-slice_add_fusion.1), channel_id=1, source_target_pairs={{0,2},{1,3},{2,0},{3,1},{4,6},{5,7},{6,4},{7,5},{8,10},{9,11},{10,... | collective-permute-start | bytes 196616 | tf_op jit(solution)/shard_map/ppermute | solution.py:65
  74.0 2.8 %collective-permute-done.13 = f32[16,1024]{1,0:T(8,128)S(1)} collective-permute-done((f32[16,1024]{1,0:T(8,128)S(1)}, f32[16,1024]{1,0:T(8,128)S(1)}, u32[]{:S(2)}, u32[]{:S(2)}) %collective-permute-start.13) | collective-permute-done | bytes 65568 | tf_op jit(solution)/shard_map/ppermute | solution.py:65
  76.8 1.6 %collective-permute-start.14 = (f32[16,1024]{1,0:T(8,128)S(1)}, f32[16,1024]{1,0:T(8,128)S(1)}, u32[]{:S(2)}, u32[]{:S(2)}) collective-permute-start(f32[16,1024]{1,0:T(8,128)S(1)} %add.159), channel_id=1, source_target_pairs={{0,4},{1,5},{2,6},{3,7},{4,0},{5,1},{6,2},{7,3},{8,12},{9,13},{10,... | collective-permute-start | bytes 196616 | tf_op jit(solution)/shard_map/ppermute | solution.py:65
  78.4 2.7 %collective-permute-done.14 = f32[16,1024]{1,0:T(8,128)S(1)} collective-permute-done((f32[16,1024]{1,0:T(8,128)S(1)}, f32[16,1024]{1,0:T(8,128)S(1)}, u32[]{:S(2)}, u32[]{:S(2)}) %collective-permute-start.14) | collective-permute-done | bytes 65568 | tf_op jit(solution)/shard_map/ppermute | solution.py:65
  81.1 1.2 collective-permute-start.15
  82.3 3.1 %collective-permute-done.15 = f32[16,1024]{1,0:T(8,128)S(1)} collective-permute-done((f32[16,1024]{1,0:T(8,128)S(1)}, f32[16,1024]{1,0:T(8,128)S(1)}, u32[]{:S(2)}, u32[]{:S(2)}) %collective-permute-start.15) | collective-permute-done | bytes 65568 | tf_op jit(solution)/shard_map/ppermute | solution.py:65
  85.5 2.0 %collective-permute-start.16 = (f32[16,1024]{1,0:T(8,128)S(1)}, f32[16,1024]{1,0:T(8,128)S(1)}, u32[]{:S(2)}, u32[]{:S(2)}) collective-permute-start(f32[16,1024]{1,0:T(8,128)S(1)} %add.161), channel_id=1, source_target_pairs={{0,16},{1,17},{2,18},{3,19},{4,20},{5,21},{6,22},{7,23},{8,24},{9,... | collective-permute-start | bytes 196616 | tf_op jit(solution)/shard_map/ppermute | solution.py:65
  87.5 1.0 bitcast_add_fusion.1
  88.5 2.9 %collective-permute-done.16 = f32[16,1024]{1,0:T(8,128)S(1)} collective-permute-done((f32[16,1024]{1,0:T(8,128)S(1)}, f32[16,1024]{1,0:T(8,128)S(1)}, u32[]{:S(2)}, u32[]{:S(2)}) %collective-permute-start.16) | collective-permute-done | bytes 65568 | tf_op jit(solution)/shard_map/ppermute | solution.py:65
  91.6 1.4 %collective-permute-start.21 = (f32[1,400,128]{2,1,0:T(8,128)S(1)}, f32[1,400,128]{2,1,0:T(8,128)S(1)}, u32[]{:S(2)}, u32[]{:S(2)}) collective-permute-start(f32[1,400,128]{2,1,0:T(8,128)S(1)} %constant_dynamic-slice_fusion), channel_id=1, source_target_pairs={{0,16},{8,24},{16,0},{24,8},{1,17},{9,25},{17,1},{25,9},{2,18},{10... | collective-permute-start | bytes 614408 | tf_op jit(solution)/shard_map/ppermute | solution.py:108
  93.3 3.0 %cholesky.55 = f32[32,32]{1,0:T(8,128)S(1)} custom-call(f32[32,32]{1,0:T(8,128)S(1)} %fusion.44), custom_call_target="Cholesky" | custom-call | tf_op jit(solution)/shard_map/jit(cholesky)/cholesky | solution.py:181
  97.7 2.4 %custom-call.7 = f32[1,32,32]{1,2,0:T(8,128)S(1)} custom-call(f32[1,32,32]{2,1,0:T(8,128)S(1)} %fusion.42), custom_call_target="InvertDiagBlocksLowerTriangular" | custom-call | tf_op jit(solution)/shard_map/jit(_solve_triangular)/triangular_solve | solution.py:182
  101.0 1.8 %collective-permute-start.18 = (f32[32,384]{1,0:T(8,128)S(1)}, f32[32,384]{1,0:T(8,128)S(1)}, u32[]{:S(2)}, u32[]{:S(2)}) collective-permute-start(f32[32,384]{1,0:T(8,128)S(1)} %fusion.59), channel_id=1, source_target_pairs={{0,8},{8,0},{16,24},{24,16},{1,9},{9,1},{17,25},{25,17},{2,10},{10... | collective-permute-start | bytes 147464 | tf_op jit(solution)/shard_map/ppermute | solution.py:25
  102.8 2.6 %collective-permute-done.18 = f32[32,384]{1,0:T(8,128)S(1)} collective-permute-done((f32[32,384]{1,0:T(8,128)S(1)}, f32[32,384]{1,0:T(8,128)S(1)}, u32[]{:S(2)}, u32[]{:S(2)}) %collective-permute-start.18) | collective-permute-done | bytes 49184 | tf_op jit(solution)/shard_map/ppermute | solution.py:25
  105.4 1.4 %collective-permute-start.19 = (f32[32,384]{1,0:T(8,128)S(1)}, f32[32,384]{1,0:T(8,128)S(1)}, u32[]{:S(2)}, u32[]{:S(2)}) collective-permute-start(f32[32,384]{1,0:T(8,128)S(1)} %add.163), channel_id=1, source_target_pairs={{0,16},{8,24},{16,0},{24,8},{1,17},{9,25},{17,1},{25,9},{2,18},{10... | collective-permute-start | bytes 147464 | tf_op jit(solution)/shard_map/ppermute | solution.py:25
  107.5 2.9 %collective-permute-done.19 = f32[32,384]{1,0:T(8,128)S(1)} collective-permute-done((f32[32,384]{1,0:T(8,128)S(1)}, f32[32,384]{1,0:T(8,128)S(1)}, u32[]{:S(2)}, u32[]{:S(2)}) %collective-permute-start.19) | collective-permute-done | bytes 49184 | tf_op jit(solution)/shard_map/ppermute | solution.py:25
  110.5 0.8 fusion.40
  111.3 1.1 fusion.7
  112.5 1.0 fusion.57
  113.4 18.7 %all_gather.3 = bf16[1024,384]{1,0:T(8,128)(2,1)S(1)} all-gather(bf16[256,384]{1,0:T(8,128)(2,1)S(1)} %get-tuple-element.12), channel_id=1, replica_groups=mesh['rep'=4,'tp'=8] {'rep'}, dimensions={0}, use_global_device_ids=true | all-gather | bytes 983040 | tf_op jit(solution)/shard_map/all_gather | solution.py:196
  132.7 0.9 copy.25
  (84 shorter events, 9.7 us)
Async XLA Ops:
  0.6 65.7 %copy-start = (bf16[1536,128]{1,0:T(8,128)(2,1)S(1)}, bf16[1536,128]{1,0:T(8,128)(2,1)}, u32[]{:S(2)}) copy-start(bf16[1536,128]{1,0:T(8,128)(2,1)} %param.19) | copy-start | bytes 1179652
  0.6 14.2 %collective-permute-start.2 = (bf16[192,1024]{1,0:T(8,128)(2,1)}, bf16[192,1024]{1,0:T(8,128)(2,1)S(1)}, u32[]{:S(2)}, u32[]{:S(2)}) collective-permute-start(bf16[192,1024]{1,0:T(8,128)(2,1)} %param.13), channel_id=1, source_target_pairs={{0,6},{1,7},{2,4},{3,5},{4,2},{5,3},{6,0},{7,1},{8,14},{9,15},{10,... | collective-permute-start | bytes 1179656 | tf_op jit(solution)/shard_map/ppermute | solution.py:40
  4.6 17.8 %collective-permute-start.1 = (bf16[192,1024]{1,0:T(8,128)(2,1)}, bf16[192,1024]{1,0:T(8,128)(2,1)S(1)}, u32[]{:S(2)}, u32[]{:S(2)}) collective-permute-start(bf16[192,1024]{1,0:T(8,128)(2,1)} %param.13), channel_id=1, source_target_pairs={{0,4},{1,5},{2,6},{3,7},{4,0},{5,1},{6,2},{7,3},{8,12},{9,13},{10,... | collective-permute-start | bytes 1179656 | tf_op jit(solution)/shard_map/ppermute | solution.py:40
  5.1 17.5 %collective-permute-start = (bf16[192,1024]{1,0:T(8,128)(2,1)}, bf16[192,1024]{1,0:T(8,128)(2,1)S(1)}, u32[]{:S(2)}, u32[]{:S(2)}) collective-permute-start(bf16[192,1024]{1,0:T(8,128)(2,1)} %param.13), channel_id=1, source_target_pairs={{0,2},{1,3},{2,0},{3,1},{4,6},{5,7},{6,4},{7,5},{8,10},{9,11},{10,... | collective-permute-start | bytes 1179656 | tf_op jit(solution)/shard_map/ppermute | solution.py:40
  14.8 9.2 %copy-start.4 = (bf16[192,1024]{1,0:T(8,128)(2,1)}, bf16[192,1024]{1,0:T(8,128)(2,1)S(1)}, u32[]{:S(2)}) copy-start(bf16[192,1024]{1,0:T(8,128)(2,1)S(1)} %collective-permute-done.2) | copy-start | bytes 1179652
  22.4 1.6 %copy-start.6 = (bf16[192,1024]{1,0:T(8,128)(2,1)}, bf16[192,1024]{1,0:T(8,128)(2,1)S(1)}, u32[]{:S(2)}) copy-start(bf16[192,1024]{1,0:T(8,128)(2,1)S(1)} %collective-permute-done.1) | copy-start | bytes 1179652
  22.7 1.4 %copy-start.8 = (bf16[192,1024]{1,0:T(8,128)(2,1)}, bf16[192,1024]{1,0:T(8,128)(2,1)S(1)}, u32[]{:S(2)}) copy-start(bf16[192,1024]{1,0:T(8,128)(2,1)S(1)} %collective-permute-done) | copy-start | bytes 1179652
  24.0 4.1 %collective-permute-start.3 = (bf16[4,192,1024]{2,1,0:T(8,128)(2,1)S(1)}, bf16[4,192,1024]{2,1,0:T(8,128)(2,1)S(1)}, u32[]{:S(2)}, u32[]{:S(2)}) collective-permute-start(bf16[4,192,1024]{2,1,0:T(8,128)(2,1)S(1)} %pad_maximum_fusion), channel_id=1, source_target_pairs={{0,1},{1,0},{2,3},{3,2},{4,5},{5,4},{6,7},{7,6},{8,9},{9,8},{10,11... | collective-permute-start | bytes 4718600 | tf_op jit(solution)/shard_map/ppermute | solution.py:40
  24.1 1.7 %copy-start.1 = (bf16[192,1024]{1,0:T(8,128)(2,1)S(1)}, bf16[192,1024]{1,0:T(8,128)(2,1)}, u32[]{:S(2)}) copy-start(bf16[192,1024]{1,0:T(8,128)(2,1)} %param.13) | copy-start | bytes 1179652
  24.2 1.7 %copy-start.5 = (bf16[192,1024]{1,0:T(8,128)(2,1)S(1)}, bf16[192,1024]{1,0:T(8,128)(2,1)}, u32[]{:S(2)}) copy-start(bf16[192,1024]{1,0:T(8,128)(2,1)} %copy-done.4) | copy-start | bytes 1179652
  24.2 1.7 %copy-start.7 = (bf16[192,1024]{1,0:T(8,128)(2,1)S(1)}, bf16[192,1024]{1,0:T(8,128)(2,1)}, u32[]{:S(2)}) copy-start(bf16[192,1024]{1,0:T(8,128)(2,1)} %copy-done.6) | copy-start | bytes 1179652
  24.2 1.8 %copy-start.9 = (bf16[192,1024]{1,0:T(8,128)(2,1)S(1)}, bf16[192,1024]{1,0:T(8,128)(2,1)}, u32[]{:S(2)}) copy-start(bf16[192,1024]{1,0:T(8,128)(2,1)} %copy-done.8) | copy-start | bytes 1179652
  24.2 2.0 %copy-start.12 = (bf16[1,1024,384]{2,1,0:T(8,128)(2,1)S(1)}, bf16[1,1024,384]{2,1,0:T(8,128)(2,1)}, u32[]{:S(2)}) copy-start(bf16[1,1024,384]{2,1,0:T(8,128)(2,1)} %param.15) | copy-start | bytes 2359300
  26.2 1.0 copy-start.11
  30.0 1.4 %collective-permute-start.4 = (f32[16,1024]{1,0:T(8,128)S(1)}, f32[16,1024]{1,0:T(8,128)S(1)}, u32[]{:S(2)}, u32[]{:S(2)}) collective-permute-start(f32[16,1024]{1,0:T(8,128)S(1)} %constant_dynamic-slice_fusion.2), channel_id=1, source_target_pairs={{0,1},{1,0},{2,3},{3,2},{4,5},{5,4},{6,7},{7,6},{8,9},{9,8},{10,11... | collective-permute-start | bytes 196616 | tf_op jit(solution)/shard_map/ppermute | solution.py:65
  31.4 4.4 %collective-permute-start.5 = (f32[16,1024]{1,0:T(8,128)S(1)}, f32[16,1024]{1,0:T(8,128)S(1)}, u32[]{:S(2)}, u32[]{:S(2)}) collective-permute-start(f32[16,1024]{1,0:T(8,128)S(1)} %dynamic-slice_add_fusion.2), channel_id=1, source_target_pairs={{0,2},{1,3},{2,0},{3,1},{4,6},{5,7},{6,4},{7,5},{8,10},{9,11},{10,... | collective-permute-start | bytes 196616 | tf_op jit(solution)/shard_map/ppermute | solution.py:65
  35.9 24.9 %copy-start.13 = (s32[1600]{0:T(1024)S(1)}, s32[1600]{0:T(1024)}, u32[]{:S(2)}) copy-start(s32[1600]{0:T(1024)} %param.21) | copy-start | bytes 19204
  35.9 24.9 %copy-start.14 = (s32[1536]{0:T(1024)S(1)}, s32[1536]{0:T(1024)}, u32[]{:S(2)}) copy-start(s32[1536]{0:T(1024)} %param.20) | copy-start | bytes 18436
  35.9 4.3 %collective-permute-start.6 = (f32[16,1024]{1,0:T(8,128)S(1)}, f32[16,1024]{1,0:T(8,128)S(1)}, u32[]{:S(2)}, u32[]{:S(2)}) collective-permute-start(f32[16,1024]{1,0:T(8,128)S(1)} %add.152), channel_id=1, source_target_pairs={{0,4},{1,5},{2,6},{3,7},{4,0},{5,1},{6,2},{7,3},{8,12},{9,13},{10,... | collective-permute-start | bytes 196616 | tf_op jit(solution)/shard_map/ppermute | solution.py:65
  40.2 4.3 %collective-permute-start.7 = (f32[16,1024]{1,0:T(8,128)S(1)}, f32[16,1024]{1,0:T(8,128)S(1)}, u32[]{:S(2)}, u32[]{:S(2)}) collective-permute-start(f32[16,1024]{1,0:T(8,128)S(1)} %add.153), channel_id=1, source_target_pairs={{0,8},{1,9},{2,10},{3,11},{4,12},{5,13},{6,14},{7,15},{8,0},{9,1},... | collective-permute-start | bytes 196616 | tf_op jit(solution)/shard_map/ppermute | solution.py:65
  44.6 5.2 %collective-permute-start.8 = (f32[16,1024]{1,0:T(8,128)S(1)}, f32[16,1024]{1,0:T(8,128)S(1)}, u32[]{:S(2)}, u32[]{:S(2)}) collective-permute-start(f32[16,1024]{1,0:T(8,128)S(1)} %add.154), channel_id=1, source_target_pairs={{0,16},{1,17},{2,18},{3,19},{4,20},{5,21},{6,22},{7,23},{8,24},{9,... | collective-permute-start | bytes 196616 | tf_op jit(solution)/shard_map/ppermute | solution.py:65
  49.8 1.3 collective-permute-start.9
  59.1 4.2 %collective-permute-start.10 = (f32[32,384]{1,0:T(8,128)S(1)}, f32[32,384]{1,0:T(8,128)S(1)}, u32[]{:S(2)}, u32[]{:S(2)}) collective-permute-start(f32[32,384]{1,0:T(8,128)S(1)} %fusion.58), channel_id=1, source_target_pairs={{0,8},{8,0},{16,24},{24,16},{1,9},{9,1},{17,25},{25,17},{2,10},{10... | collective-permute-start | bytes 147464 | tf_op jit(solution)/shard_map/ppermute | solution.py:25
  63.3 6.2 %collective-permute-start.11 = (f32[32,384]{1,0:T(8,128)S(1)}, f32[32,384]{1,0:T(8,128)S(1)}, u32[]{:S(2)}, u32[]{:S(2)}) collective-permute-start(f32[32,384]{1,0:T(8,128)S(1)} %add.156), channel_id=1, source_target_pairs={{0,16},{8,24},{16,0},{24,8},{1,17},{9,25},{17,1},{25,9},{2,18},{10... | collective-permute-start | bytes 147464 | tf_op jit(solution)/shard_map/ppermute | solution.py:25
  70.3 2.1 %collective-permute-start.12 = (f32[16,1024]{1,0:T(8,128)S(1)}, f32[16,1024]{1,0:T(8,128)S(1)}, u32[]{:S(2)}, u32[]{:S(2)}) collective-permute-start(f32[16,1024]{1,0:T(8,128)S(1)} %constant_dynamic-slice_fusion.1), channel_id=1, source_target_pairs={{0,1},{1,0},{2,3},{3,2},{4,5},{5,4},{6,7},{7,6},{8,9},{9,8},{10,11... | collective-permute-start | bytes 196616 | tf_op jit(solution)/shard_map/ppermute | solution.py:65
  70.4 17.0 %collective-permute-start.20 = (f32[2,400,128]{2,1,0:T(8,128)S(1)}, f32[2,400,128]{2,1,0:T(8,128)}, u32[]{:S(2)}, u32[]{:S(2)}) collective-permute-start(f32[2,400,128]{2,1,0:T(8,128)S(1)} %dynamic-slice_bitcast_fusion), channel_id=1, source_target_pairs={{0,8},{8,0},{16,24},{24,16},{1,9},{9,1},{17,25},{25,17},{2,10},{10... | collective-permute-start | bytes 1228808 | tf_op jit(solution)/shard_map/ppermute | solution.py:108
  72.4 4.3 %collective-permute-start.13 = (f32[16,1024]{1,0:T(8,128)S(1)}, f32[16,1024]{1,0:T(8,128)S(1)}, u32[]{:S(2)}, u32[]{:S(2)}) collective-permute-start(f32[16,1024]{1,0:T(8,128)S(1)} %dynamic-slice_add_fusion.1), channel_id=1, source_target_pairs={{0,2},{1,3},{2,0},{3,1},{4,6},{5,7},{6,4},{7,5},{8,10},{9,11},{10,... | collective-permute-start | bytes 196616 | tf_op jit(solution)/shard_map/ppermute | solution.py:65
  76.8 4.3 %collective-permute-start.14 = (f32[16,1024]{1,0:T(8,128)S(1)}, f32[16,1024]{1,0:T(8,128)S(1)}, u32[]{:S(2)}, u32[]{:S(2)}) collective-permute-start(f32[16,1024]{1,0:T(8,128)S(1)} %add.159), channel_id=1, source_target_pairs={{0,4},{1,5},{2,6},{3,7},{4,0},{5,1},{6,2},{7,3},{8,12},{9,13},{10,... | collective-permute-start | bytes 196616 | tf_op jit(solution)/shard_map/ppermute | solution.py:65
  81.1 4.3 %collective-permute-start.15 = (f32[16,1024]{1,0:T(8,128)S(1)}, f32[16,1024]{1,0:T(8,128)S(1)}, u32[]{:S(2)}, u32[]{:S(2)}) collective-permute-start(f32[16,1024]{1,0:T(8,128)S(1)} %add.160), channel_id=1, source_target_pairs={{0,8},{1,9},{2,10},{3,11},{4,12},{5,13},{6,14},{7,15},{8,0},{9,1},... | collective-permute-start | bytes 196616 | tf_op jit(solution)/shard_map/ppermute | solution.py:65
  85.5 5.9 %collective-permute-start.16 = (f32[16,1024]{1,0:T(8,128)S(1)}, f32[16,1024]{1,0:T(8,128)S(1)}, u32[]{:S(2)}, u32[]{:S(2)}) collective-permute-start(f32[16,1024]{1,0:T(8,128)S(1)} %add.161), channel_id=1, source_target_pairs={{0,16},{1,17},{2,18},{3,19},{4,20},{5,21},{6,22},{7,23},{8,24},{9,... | collective-permute-start | bytes 196616 | tf_op jit(solution)/shard_map/ppermute | solution.py:65
  91.4 15.4 %copy-start.10 = (f32[400,128]{1,0:T(8,128)S(1)}, f32[400,128]{1,0:T(8,128)}, u32[]{:S(2)}) copy-start(f32[400,128]{1,0:T(8,128)} %param.22) | copy-start | bytes 614404
  91.4 1.5 %collective-permute-start.17 = (f32[16,1024]{1,0:T(8,128)S(1)}, f32[16,1024]{1,0:T(8,128)S(1)}, u32[]{:S(2)}, u32[]{:S(2)}) collective-permute-start(f32[16,1024]{1,0:T(8,128)S(1)} %get-tuple-element.16), channel_id=1, source_target_pairs={{0,1},{1,0},{2,3},{3,2},{4,5},{5,4},{6,7},{7,6},{8,9},{9,8},{10,11... | collective-permute-start | bytes 196616 | tf_op jit(solution)/shard_map/ppermute | solution.py:65
  91.6 15.3 %collective-permute-start.21 = (f32[1,400,128]{2,1,0:T(8,128)S(1)}, f32[1,400,128]{2,1,0:T(8,128)S(1)}, u32[]{:S(2)}, u32[]{:S(2)}) collective-permute-start(f32[1,400,128]{2,1,0:T(8,128)S(1)} %constant_dynamic-slice_fusion), channel_id=1, source_target_pairs={{0,16},{8,24},{16,0},{24,8},{1,17},{9,25},{17,1},{25,9},{2,18},{10... | collective-permute-start | bytes 614408 | tf_op jit(solution)/shard_map/ppermute | solution.py:108
  101.0 4.4 %collective-permute-start.18 = (f32[32,384]{1,0:T(8,128)S(1)}, f32[32,384]{1,0:T(8,128)S(1)}, u32[]{:S(2)}, u32[]{:S(2)}) collective-permute-start(f32[32,384]{1,0:T(8,128)S(1)} %fusion.59), channel_id=1, source_target_pairs={{0,8},{8,0},{16,24},{24,16},{1,9},{9,1},{17,25},{25,17},{2,10},{10... | collective-permute-start | bytes 147464 | tf_op jit(solution)/shard_map/ppermute | solution.py:25
  105.4 5.1 %collective-permute-start.19 = (f32[32,384]{1,0:T(8,128)S(1)}, f32[32,384]{1,0:T(8,128)S(1)}, u32[]{:S(2)}, u32[]{:S(2)}) collective-permute-start(f32[32,384]{1,0:T(8,128)S(1)} %add.163), channel_id=1, source_target_pairs={{0,16},{8,24},{16,0},{24,8},{1,17},{9,25},{17,1},{25,9},{2,18},{10... | collective-permute-start | bytes 147464 | tf_op jit(solution)/shard_map/ppermute | solution.py:25
  111.3 1.2 copy-start.2
  111.3 1.2 copy-start.3

commit v15 on v13

--- a/solution.py
+++ b/solution.py
@@ -182,7 +182,10 @@
         left_rows = split_tree_sum(partial_left, ("rep", "tp")) / replicas
         gram_matrix = jnp.dot(left_rows, left_rows.T, precision=highest)
         factor_low = jnp.linalg.cholesky(gram_matrix)
-        left_rows = jax.scipy.linalg.solve_triangular(factor_low, left_rows, lower=True)
+        inverse_low = jax.scipy.linalg.solve_triangular(
+            factor_low, jnp.eye(factor_low.shape[0], dtype=factor_low.dtype), lower=True
+        )
+        left_rows = jnp.dot(inverse_low, left_rows, precision=highest)
         partial_right = jnp.dot(left_rows, combined, precision=high)
         right_rows = tree_sum(partial_right, "rep") / replicas
     right_basis = right_rows.T

time: 131 us -> 131 us (level)
  waiting for transfers between devices: 45.8 us -> 43.5 us
  starting transfers between devices: 31.4 us -> 33.4 us
    ppermute x4, waiting for transfers between devices: 8.15 us -> 6.44 us  [tree_sum(): value = value + lax.ppermute(value, axes, pairs)]
where the time goes in v15:
time: 131 us
  waiting for transfers between devices  43.5 us (33%)
  starting transfers between devices  33.4 us (25%)
  other arithmetic  19.3 us (15%)
  blocking collectives  18.2 us (14%)
  matrix products  11.2 us (9%)
  local copies, waits for them, and re-layouts  3.77 us (3%)
    ppermute x12, waiting for transfers between devices, exchange(): return lax.ppermute(piece, axes, [(i, i ^ stride) for i in range(count)])  25.1 us
    all_gather x1, blocking collectives, shards(): lax.all_gather(master_new.astype(jnp.bfloat16), 'rep', axis=0, tiled=True)  18.2 us
    ppermute x12, starting transfers between devices, exchange(): return lax.ppermute(piece, axes, [(i, i ^ stride) for i in range(count)])  14 us
    ppermute x5, waiting for transfers between devices, exchange(): return lax.ppermute(value, axis, [(i, i ^ stride) for i in range(count)])  12 us
    ppermute x4, starting transfers between devices, tree_sum(): value = value + lax.ppermute(value, axes, pairs)  8.11 us
    ppermute x5, starting transfers between devices, exchange(): return lax.ppermute(value, axis, [(i, i ^ stride) for i in range(count)])  7.91 us
    another operation x6, other arithmetic, shards(): factor_low = jnp.linalg.cholesky(gram_matrix)  7.19 us
    ppermute x4, waiting for transfers between devices, tree_sum(): value = value + lax.ppermute(value, axes, pairs)  6.44 us
  transfers between devices with their start and end apart: 23, of which 16 were waited for; matrix products, arithmetic and copies ran while one was open for 14% of the time, Pallas kernels for 0%

profile of v15, /device:TPU:0, one launch (start us, length us, event | category | flops | bytes accessed | tf_op | source)
XLA Modules:
  0.0 130.6 jit_solution(3271780257467953505)
XLA Ops:
  0.7 3.0 %collective-permute-start = (bf16[192,1024]{1,0:T(8,128)(2,1)}, bf16[192,1024]{1,0:T(8,128)(2,1)S(1)}, u32[]{:S(2)}, u32[]{:S(2)}) collective-permute-start(bf16[192,1024]{1,0:T(8,128)(2,1)} %param.13), channel_id=1, source_target_pairs={{0,2},{1,3},{2,0},{3,1},{4,6},{5,7},{6,4},{7,5},{8,10},{9,11},{10,... | collective-permute-start | bytes 1179656 | tf_op jit(solution)/shard_map/ppermute | solution.py:40
  3.7 1.5 %collective-permute-start.1 = (bf16[192,1024]{1,0:T(8,128)(2,1)}, bf16[192,1024]{1,0:T(8,128)(2,1)S(1)}, u32[]{:S(2)}, u32[]{:S(2)}) collective-permute-start(bf16[192,1024]{1,0:T(8,128)(2,1)} %param.13), channel_id=1, source_target_pairs={{0,4},{1,5},{2,6},{3,7},{4,0},{5,1},{6,2},{7,3},{8,12},{9,13},{10,... | collective-permute-start | bytes 1179656 | tf_op jit(solution)/shard_map/ppermute | solution.py:40
  5.2 7.8 %collective-permute-done = bf16[192,1024]{1,0:T(8,128)(2,1)S(1)} collective-permute-done((bf16[192,1024]{1,0:T(8,128)(2,1)}, bf16[192,1024]{1,0:T(8,128)(2,1)S(1)}, u32[]{:S(2)}, u32[]{:S(2)}) %collective-permute-start) | collective-permute-done | bytes 393248 | tf_op jit(solution)/shard_map/ppermute | solution.py:40
  13.0 1.8 %collective-permute-start.3 = (bf16[96,1024]{1,0:T(8,128)(2,1)S(1)}, bf16[96,1024]{1,0:T(8,128)(2,1)S(1)}, u32[]{:S(2)}, u32[]{:S(2)}) collective-permute-start(bf16[96,1024]{1,0:T(8,128)(2,1)S(1)} %slice.17), channel_id=1, source_target_pairs={{0,4},{1,5},{2,6},{3,7},{4,0},{5,1},{6,2},{7,3},{8,12},{9,13},{10,... | collective-permute-start | bytes 589832 | tf_op jit(solution)/shard_map/ppermute | solution.py:40
  14.9 1.6 %collective-permute-start.2 = (bf16[96,1024]{1,0:T(8,128)(2,1)S(1)}, bf16[96,1024]{1,0:T(8,128)(2,1)S(1)}, u32[]{:S(2)}, u32[]{:S(2)}) collective-permute-start(bf16[96,1024]{1,0:T(8,128)(2,1)S(1)} %slice.16), channel_id=1, source_target_pairs={{0,2},{1,3},{2,0},{3,1},{4,6},{5,7},{6,4},{7,5},{8,10},{9,11},{10,... | collective-permute-start | bytes 589832 | tf_op jit(solution)/shard_map/ppermute | solution.py:40
  16.4 2.7 %collective-permute-done.3 = bf16[96,1024]{1,0:T(8,128)(2,1)S(1)} collective-permute-done((bf16[96,1024]{1,0:T(8,128)(2,1)S(1)}, bf16[96,1024]{1,0:T(8,128)(2,1)S(1)}, u32[]{:S(2)}, u32[]{:S(2)}) %collective-permute-start.3) | collective-permute-done | bytes 196640 | tf_op jit(solution)/shard_map/ppermute | solution.py:40
  19.2 1.4 %collective-permute-done.2 = bf16[96,1024]{1,0:T(8,128)(2,1)S(1)} collective-permute-done((bf16[96,1024]{1,0:T(8,128)(2,1)S(1)}, bf16[96,1024]{1,0:T(8,128)(2,1)S(1)}, u32[]{:S(2)}, u32[]{:S(2)}) %collective-permute-start.2) | collective-permute-done | bytes 196640 | tf_op jit(solution)/shard_map/ppermute | solution.py:40
  21.4 1.6 %constant_dynamic-slice_fusion.6 = (bf16[1,192,384]{2,1,0:T(8,128)(2,1)S(1)}, bf16[1,192,384]{2,1,0:T(8,128)(2,1)S(1)}, bf16[1,192,384]{2,1,0:T(8,128)(2,1)S(1)}...) fusion(bf16[8,192,384]{2,1,0:T(8,128)(2,1)} %bitcast.63, ...), kind=kLoop, calls=%fused_computation.85 | loop fusion | bytes 2359328 | tf_op jit(solution)/shard_map/dynamic_slice | solution.py:53
  23.5 1.0 convert_add_fusion
  25.3 1.0 bitcast_add_fusion
  27.8 0.9 collective-permute-done.5
  28.7 1.6 %collective-permute-start.6 = (f32[16,1024]{1,0:T(8,128)S(1)}, f32[16,1024]{1,0:T(8,128)S(1)}, u32[]{:S(2)}, u32[]{:S(2)}) collective-permute-start(f32[16,1024]{1,0:T(8,128)S(1)} %dynamic-slice_add_fusion.2), channel_id=1, source_target_pairs={{0,2},{1,3},{2,0},{3,1},{4,6},{5,7},{6,4},{7,5},{8,10},{9,11},{10,... | collective-permute-start | bytes 196616 | tf_op jit(solution)/shard_map/ppermute | solution.py:68
  30.3 2.9 %collective-permute-done.6 = f32[16,1024]{1,0:T(8,128)S(1)} collective-permute-done((f32[16,1024]{1,0:T(8,128)S(1)}, f32[16,1024]{1,0:T(8,128)S(1)}, u32[]{:S(2)}, u32[]{:S(2)}) %collective-permute-start.6) | collective-permute-done | bytes 65568 | tf_op jit(solution)/shard_map/ppermute | solution.py:68
  33.2 1.2 collective-permute-start.7
  34.4 3.1 %collective-permute-done.7 = f32[16,1024]{1,0:T(8,128)S(1)} collective-permute-done((f32[16,1024]{1,0:T(8,128)S(1)}, f32[16,1024]{1,0:T(8,128)S(1)}, u32[]{:S(2)}, u32[]{:S(2)}) %collective-permute-start.7) | collective-permute-done | bytes 65568 | tf_op jit(solution)/shard_map/ppermute | solution.py:68
  37.5 1.6 %collective-permute-start.8 = (f32[16,1024]{1,0:T(8,128)S(1)}, f32[16,1024]{1,0:T(8,128)S(1)}, u32[]{:S(2)}, u32[]{:S(2)}) collective-permute-start(f32[16,1024]{1,0:T(8,128)S(1)} %add.153), channel_id=1, source_target_pairs={{0,8},{1,9},{2,10},{3,11},{4,12},{5,13},{6,14},{7,15},{8,0},{9,1},... | collective-permute-start | bytes 196616 | tf_op jit(solution)/shard_map/ppermute | solution.py:68
  39.2 2.7 %collective-permute-done.8 = f32[16,1024]{1,0:T(8,128)S(1)} collective-permute-done((f32[16,1024]{1,0:T(8,128)S(1)}, f32[16,1024]{1,0:T(8,128)S(1)}, u32[]{:S(2)}, u32[]{:S(2)}) %collective-permute-start.8) | collective-permute-done | bytes 65568 | tf_op jit(solution)/shard_map/ppermute | solution.py:68
  41.9 2.9 %collective-permute-start.9 = (f32[16,1024]{1,0:T(8,128)S(1)}, f32[16,1024]{1,0:T(8,128)S(1)}, u32[]{:S(2)}, u32[]{:S(2)}) collective-permute-start(f32[16,1024]{1,0:T(8,128)S(1)} %add.154), channel_id=1, source_target_pairs={{0,16},{1,17},{2,18},{3,19},{4,20},{5,21},{6,22},{7,23},{8,24},{9,... | collective-permute-start | bytes 196616 | tf_op jit(solution)/shard_map/ppermute | solution.py:68
  44.8 2.3 %collective-permute-done.9 = f32[16,1024]{1,0:T(8,128)S(1)} collective-permute-done((f32[16,1024]{1,0:T(8,128)S(1)}, f32[16,1024]{1,0:T(8,128)S(1)}, u32[]{:S(2)}, u32[]{:S(2)}) %collective-permute-start.9) | collective-permute-done | bytes 65568 | tf_op jit(solution)/shard_map/ppermute | solution.py:68
  47.2 1.2 collective-permute-done.10
  48.8 2.9 %cholesky.44 = f32[32,32]{1,0:T(8,128)S(1)} custom-call(f32[32,32]{1,0:T(8,128)S(1)} %fusion.50), custom_call_target="Cholesky" | custom-call | tf_op jit(solution)/shard_map/jit(cholesky)/cholesky | solution.py:184
  53.1 2.4 %custom-call.6 = f32[1,32,32]{1,2,0:T(8,128)S(1)} custom-call(f32[1,32,32]{2,1,0:T(8,128)S(1)} %fusion.45), custom_call_target="InvertDiagBlocksLowerTriangular" | custom-call | tf_op jit(solution)/shard_map/jit(_solve_triangular)/triangular_solve | solution.py:185
  56.6 1.6 %collective-permute-start.11 = (f32[32,384]{1,0:T(8,128)S(1)}, f32[32,384]{1,0:T(8,128)S(1)}, u32[]{:S(2)}, u32[]{:S(2)}) collective-permute-start(f32[32,384]{1,0:T(8,128)S(1)} %fusion.62), channel_id=1, source_target_pairs={{0,8},{8,0},{16,24},{24,16},{1,9},{9,1},{17,25},{25,17},{2,10},{10... | collective-permute-start | bytes 147464 | tf_op jit(solution)/shard_map/ppermute | solution.py:25
  58.2 1.1 select_reduce_fusion
  59.3 1.4 %collective-permute-done.11 = f32[32,384]{1,0:T(8,128)S(1)} collective-permute-done((f32[32,384]{1,0:T(8,128)S(1)}, f32[32,384]{1,0:T(8,128)S(1)}, u32[]{:S(2)}, u32[]{:S(2)}) %collective-permute-start.11) | collective-permute-done | bytes 49184 | tf_op jit(solution)/shard_map/ppermute | solution.py:25
  60.7 3.0 %collective-permute-start.12 = (f32[32,384]{1,0:T(8,128)S(1)}, f32[32,384]{1,0:T(8,128)S(1)}, u32[]{:S(2)}, u32[]{:S(2)}) collective-permute-start(f32[32,384]{1,0:T(8,128)S(1)} %add.156), channel_id=1, source_target_pairs={{0,16},{8,24},{16,0},{24,8},{1,17},{9,25},{17,1},{25,9},{2,18},{10... | collective-permute-start | bytes 147464 | tf_op jit(solution)/shard_map/ppermute | solution.py:25
  63.7 3.1 %fusion = f32[1600,128]{1,0:T(8,128)S(1)} fusion(bf16[1536,128]{1,0:T(8,128)(2,1)S(1)} %copy-done, s32[1536]{0:T(1024)S(1)} %select_reduce_fusion), kind=kOutput, calls=%fused_computation.1 | convolution fusion | flops 631603200 | bytes 1218560 | tf_op jit(solution)/shard_map/dot_general | solution.py:99
  67.8 2.0 %collective-permute-start.21 = (f32[2,400,128]{2,1,0:T(8,128)S(1)}, f32[2,400,128]{2,1,0:T(8,128)}, u32[]{:S(2)}, u32[]{:S(2)}) collective-permute-start(f32[2,400,128]{2,1,0:T(8,128)S(1)} %dynamic-slice_bitcast_fusion), channel_id=1, source_target_pairs={{0,8},{8,0},{16,24},{24,16},{1,9},{9,1},{17,25},{25,17},{2,10},{10... | collective-permute-start | bytes 1228808 | tf_op jit(solution)/shard_map/ppermute | solution.py:111
  69.8 1.6 %collective-permute-start.14 = (f32[16,1024]{1,0:T(8,128)S(1)}, f32[16,1024]{1,0:T(8,128)S(1)}, u32[]{:S(2)}, u32[]{:S(2)}) collective-permute-start(f32[16,1024]{1,0:T(8,128)S(1)} %dynamic-slice_add_fusion.1), channel_id=1, source_target_pairs={{0,2},{1,3},{2,0},{3,1},{4,6},{5,7},{6,4},{7,5},{8,10},{9,11},{10,... | collective-permute-start | bytes 196616 | tf_op jit(solution)/shard_map/ppermute | solution.py:68
  71.4 2.8 %collective-permute-done.14 = f32[16,1024]{1,0:T(8,128)S(1)} collective-permute-done((f32[16,1024]{1,0:T(8,128)S(1)}, f32[16,1024]{1,0:T(8,128)S(1)}, u32[]{:S(2)}, u32[]{:S(2)}) %collective-permute-start.14) | collective-permute-done | bytes 65568 | tf_op jit(solution)/shard_map/ppermute | solution.py:68
  74.2 1.2 collective-permute-start.15
  75.4 3.1 %collective-permute-done.15 = f32[16,1024]{1,0:T(8,128)S(1)} collective-permute-done((f32[16,1024]{1,0:T(8,128)S(1)}, f32[16,1024]{1,0:T(8,128)S(1)}, u32[]{:S(2)}, u32[]{:S(2)}) %collective-permute-start.15) | collective-permute-done | bytes 65568 | tf_op jit(solution)/shard_map/ppermute | solution.py:68
  78.5 1.2 collective-permute-start.16
  79.7 3.1 %collective-permute-done.16 = f32[16,1024]{1,0:T(8,128)S(1)} collective-permute-done((f32[16,1024]{1,0:T(8,128)S(1)}, f32[16,1024]{1,0:T(8,128)S(1)}, u32[]{:S(2)}, u32[]{:S(2)}) %collective-permute-start.16) | collective-permute-done | bytes 65568 | tf_op jit(solution)/shard_map/ppermute | solution.py:68
  82.9 2.0 %collective-permute-start.17 = (f32[16,1024]{1,0:T(8,128)S(1)}, f32[16,1024]{1,0:T(8,128)S(1)}, u32[]{:S(2)}, u32[]{:S(2)}) collective-permute-start(f32[16,1024]{1,0:T(8,128)S(1)} %add.161), channel_id=1, source_target_pairs={{0,16},{1,17},{2,18},{3,19},{4,20},{5,21},{6,22},{7,23},{8,24},{9,... | collective-permute-start | bytes 196616 | tf_op jit(solution)/shard_map/ppermute | solution.py:68
  84.9 1.0 bitcast_add_fusion.1
  85.9 2.9 %collective-permute-done.17 = f32[16,1024]{1,0:T(8,128)S(1)} collective-permute-done((f32[16,1024]{1,0:T(8,128)S(1)}, f32[16,1024]{1,0:T(8,128)S(1)}, u32[]{:S(2)}, u32[]{:S(2)}) %collective-permute-start.17) | collective-permute-done | bytes 65568 | tf_op jit(solution)/shard_map/ppermute | solution.py:68
  89.0 1.4 %collective-permute-start.22 = (f32[1,400,128]{2,1,0:T(8,128)S(1)}, f32[1,400,128]{2,1,0:T(8,128)S(1)}, u32[]{:S(2)}, u32[]{:S(2)}) collective-permute-start(f32[1,400,128]{2,1,0:T(8,128)S(1)} %constant_dynamic-slice_fusion), channel_id=1, source_target_pairs={{0,16},{8,24},{16,0},{24,8},{1,17},{9,25},{17,1},{25,9},{2,18},{10... | collective-permute-start | bytes 614408 | tf_op jit(solution)/shard_map/ppermute | solution.py:111
  90.9 2.9 %cholesky.55 = f32[32,32]{1,0:T(8,128)S(1)} custom-call(f32[32,32]{1,0:T(8,128)S(1)} %fusion.48), custom_call_target="Cholesky" | custom-call | tf_op jit(solution)/shard_map/jit(cholesky)/cholesky | solution.py:184
  95.2 2.4 %custom-call.7 = f32[1,32,32]{1,2,0:T(8,128)S(1)} custom-call(f32[1,32,32]{2,1,0:T(8,128)S(1)} %fusion.46), custom_call_target="InvertDiagBlocksLowerTriangular" | custom-call | tf_op jit(solution)/shard_map/jit(_solve_triangular)/triangular_solve | solution.py:185
  98.6 1.8 %collective-permute-start.19 = (f32[32,384]{1,0:T(8,128)S(1)}, f32[32,384]{1,0:T(8,128)S(1)}, u32[]{:S(2)}, u32[]{:S(2)}) collective-permute-start(f32[32,384]{1,0:T(8,128)S(1)} %fusion.63), channel_id=1, source_target_pairs={{0,8},{8,0},{16,24},{24,16},{1,9},{9,1},{17,25},{25,17},{2,10},{10... | collective-permute-start | bytes 147464 | tf_op jit(solution)/shard_map/ppermute | solution.py:25
  100.4 2.4 %collective-permute-done.19 = f32[32,384]{1,0:T(8,128)S(1)} collective-permute-done((f32[32,384]{1,0:T(8,128)S(1)}, f32[32,384]{1,0:T(8,128)S(1)}, u32[]{:S(2)}, u32[]{:S(2)}) %collective-permute-start.19) | collective-permute-done | bytes 49184 | tf_op jit(solution)/shard_map/ppermute | solution.py:25
  102.8 1.7 %collective-permute-start.20 = (f32[32,384]{1,0:T(8,128)S(1)}, f32[32,384]{1,0:T(8,128)S(1)}, u32[]{:S(2)}, u32[]{:S(2)}) collective-permute-start(f32[32,384]{1,0:T(8,128)S(1)} %add.163), channel_id=1, source_target_pairs={{0,16},{8,24},{16,0},{24,8},{1,17},{9,25},{17,1},{25,9},{2,18},{10... | collective-permute-start | bytes 147464 | tf_op jit(solution)/shard_map/ppermute | solution.py:25
  105.2 2.7 %collective-permute-done.20 = f32[32,384]{1,0:T(8,128)S(1)} collective-permute-done((f32[32,384]{1,0:T(8,128)S(1)}, f32[32,384]{1,0:T(8,128)S(1)}, u32[]{:S(2)}, u32[]{:S(2)}) %collective-permute-start.20) | collective-permute-done | bytes 49184 | tf_op jit(solution)/shard_map/ppermute | solution.py:25
  108.7 1.1 fusion.7
  109.9 1.0 fusion.61
  110.8 18.2 %all_gather.3 = bf16[1024,384]{1,0:T(8,128)(2,1)S(1)} all-gather(bf16[256,384]{1,0:T(8,128)(2,1)S(1)} %get-tuple-element.12), channel_id=1, replica_groups=mesh['rep'=4,'tp'=8] {'rep'}, dimensions={0}, use_global_device_ids=true | all-gather | bytes 983040 | tf_op jit(solution)/shard_map/all_gather | solution.py:202
  129.7 0.9 copy.25
  (93 shorter events, 12.5 us)
Async XLA Ops:
  0.6 63.1 %copy-start = (bf16[1536,128]{1,0:T(8,128)(2,1)S(1)}, bf16[1536,128]{1,0:T(8,128)(2,1)}, u32[]{:S(2)}) copy-start(bf16[1536,128]{1,0:T(8,128)(2,1)} %param.19) | copy-start | bytes 1179652
  0.6 20.0 %copy-start.7 = (bf16[192,1024]{1,0:T(8,128)(2,1)S(1)}, bf16[192,1024]{1,0:T(8,128)(2,1)}, u32[]{:S(2)}) copy-start(bf16[192,1024]{1,0:T(8,128)(2,1)} %param.13) | copy-start | bytes 1179652
  0.7 12.3 %collective-permute-start = (bf16[192,1024]{1,0:T(8,128)(2,1)}, bf16[192,1024]{1,0:T(8,128)(2,1)S(1)}, u32[]{:S(2)}, u32[]{:S(2)}) collective-permute-start(bf16[192,1024]{1,0:T(8,128)(2,1)} %param.13), channel_id=1, source_target_pairs={{0,2},{1,3},{2,0},{3,1},{4,6},{5,7},{6,4},{7,5},{8,10},{9,11},{10,... | collective-permute-start | bytes 1179656 | tf_op jit(solution)/shard_map/ppermute | solution.py:40
  3.7 11.2 %collective-permute-start.1 = (bf16[192,1024]{1,0:T(8,128)(2,1)}, bf16[192,1024]{1,0:T(8,128)(2,1)S(1)}, u32[]{:S(2)}, u32[]{:S(2)}) collective-permute-start(bf16[192,1024]{1,0:T(8,128)(2,1)} %param.13), channel_id=1, source_target_pairs={{0,4},{1,5},{2,6},{3,7},{4,0},{5,1},{6,2},{7,3},{8,12},{9,13},{10,... | collective-permute-start | bytes 1179656 | tf_op jit(solution)/shard_map/ppermute | solution.py:40
  13.0 7.9 %copy-start.3 = (bf16[192,1024]{1,0:T(8,128)(2,1)}, bf16[192,1024]{1,0:T(8,128)(2,1)S(1)}, u32[]{:S(2)}) copy-start(bf16[192,1024]{1,0:T(8,128)(2,1)S(1)} %collective-permute-done) | copy-start | bytes 1179652
  13.0 6.2 %collective-permute-start.3 = (bf16[96,1024]{1,0:T(8,128)(2,1)S(1)}, bf16[96,1024]{1,0:T(8,128)(2,1)S(1)}, u32[]{:S(2)}, u32[]{:S(2)}) collective-permute-start(bf16[96,1024]{1,0:T(8,128)(2,1)S(1)} %slice.17), channel_id=1, source_target_pairs={{0,4},{1,5},{2,6},{3,7},{4,0},{5,1},{6,2},{7,3},{8,12},{9,13},{10,... | collective-permute-start | bytes 589832 | tf_op jit(solution)/shard_map/ppermute | solution.py:40
  14.8 6.0 %copy-start.5 = (bf16[192,1024]{1,0:T(8,128)(2,1)}, bf16[192,1024]{1,0:T(8,128)(2,1)S(1)}, u32[]{:S(2)}) copy-start(bf16[192,1024]{1,0:T(8,128)(2,1)S(1)} %collective-permute-done.1) | copy-start | bytes 1179652
  14.9 5.7 %collective-permute-start.2 = (bf16[96,1024]{1,0:T(8,128)(2,1)S(1)}, bf16[96,1024]{1,0:T(8,128)(2,1)S(1)}, u32[]{:S(2)}, u32[]{:S(2)}) collective-permute-start(bf16[96,1024]{1,0:T(8,128)(2,1)S(1)} %slice.16), channel_id=1, source_target_pairs={{0,2},{1,3},{2,0},{3,1},{4,6},{5,7},{6,4},{7,5},{8,10},{9,11},{10,... | collective-permute-start | bytes 589832 | tf_op jit(solution)/shard_map/ppermute | solution.py:40
  20.6 0.7 copy-start.1
  21.4 4.0 %collective-permute-start.4 = (bf16[4,192,1024]{2,1,0:T(8,128)(2,1)S(1)}, bf16[4,192,1024]{2,1,0:T(8,128)(2,1)S(1)}, u32[]{:S(2)}, u32[]{:S(2)}) collective-permute-start(bf16[4,192,1024]{2,1,0:T(8,128)(2,1)S(1)} %pad_maximum_fusion), channel_id=1, source_target_pairs={{0,1},{1,0},{2,3},{3,2},{4,5},{5,4},{6,7},{7,6},{8,9},{9,8},{10,11... | collective-permute-start | bytes 4718600 | tf_op jit(solution)/shard_map/ppermute | solution.py:40
  21.4 1.7 %copy-start.2 = (bf16[1,192,1024]{2,1,0:T(8,128)(2,1)S(1)}, bf16[1,192,1024]{2,1,0:T(8,128)(2,1)}, u32[]{:S(2)}) copy-start(bf16[1,192,1024]{2,1,0:T(8,128)(2,1)} %copy-done.1) | copy-start | bytes 1179652
  21.4 1.7 %copy-start.4 = (bf16[192,1024]{1,0:T(8,128)(2,1)S(1)}, bf16[192,1024]{1,0:T(8,128)(2,1)}, u32[]{:S(2)}) copy-start(bf16[192,1024]{1,0:T(8,128)(2,1)} %copy-done.3) | copy-start | bytes 1179652
  21.4 1.7 %copy-start.6 = (bf16[192,1024]{1,0:T(8,128)(2,1)S(1)}, bf16[192,1024]{1,0:T(8,128)(2,1)}, u32[]{:S(2)}) copy-start(bf16[192,1024]{1,0:T(8,128)(2,1)} %copy-done.5) | copy-start | bytes 1179652
  21.4 1.8 %copy-start.8 = (bf16[192,1024]{1,0:T(8,128)(2,1)S(1)}, bf16[192,1024]{1,0:T(8,128)(2,1)}, u32[]{:S(2)}) copy-start(bf16[192,1024]{1,0:T(8,128)(2,1)} %param.13) | copy-start | bytes 1179652
  21.4 2.1 %copy-start.13 = (bf16[1,1024,384]{2,1,0:T(8,128)(2,1)S(1)}, bf16[1,1024,384]{2,1,0:T(8,128)(2,1)}, u32[]{:S(2)}) copy-start(bf16[1,1024,384]{2,1,0:T(8,128)(2,1)} %param.15) | copy-start | bytes 2359300
  23.5 1.0 copy-start.12
  27.3 1.5 %collective-permute-start.5 = (f32[16,1024]{1,0:T(8,128)S(1)}, f32[16,1024]{1,0:T(8,128)S(1)}, u32[]{:S(2)}, u32[]{:S(2)}) collective-permute-start(f32[16,1024]{1,0:T(8,128)S(1)} %constant_dynamic-slice_fusion.2), channel_id=1, source_target_pairs={{0,1},{1,0},{2,3},{3,2},{4,5},{5,4},{6,7},{7,6},{8,9},{9,8},{10,11... | collective-permute-start | bytes 196616 | tf_op jit(solution)/shard_map/ppermute | solution.py:68
  28.7 4.4 %collective-permute-start.6 = (f32[16,1024]{1,0:T(8,128)S(1)}, f32[16,1024]{1,0:T(8,128)S(1)}, u32[]{:S(2)}, u32[]{:S(2)}) collective-permute-start(f32[16,1024]{1,0:T(8,128)S(1)} %dynamic-slice_add_fusion.2), channel_id=1, source_target_pairs={{0,2},{1,3},{2,0},{3,1},{4,6},{5,7},{6,4},{7,5},{8,10},{9,11},{10,... | collective-permute-start | bytes 196616 | tf_op jit(solution)/shard_map/ppermute | solution.py:68
  33.2 4.3 %collective-permute-start.7 = (f32[16,1024]{1,0:T(8,128)S(1)}, f32[16,1024]{1,0:T(8,128)S(1)}, u32[]{:S(2)}, u32[]{:S(2)}) collective-permute-start(f32[16,1024]{1,0:T(8,128)S(1)} %add.152), channel_id=1, source_target_pairs={{0,4},{1,5},{2,6},{3,7},{4,0},{5,1},{6,2},{7,3},{8,12},{9,13},{10,... | collective-permute-start | bytes 196616 | tf_op jit(solution)/shard_map/ppermute | solution.py:68
  37.5 20.7 %copy-start.14 = (s32[1600]{0:T(1024)S(1)}, s32[1600]{0:T(1024)}, u32[]{:S(2)}) copy-start(s32[1600]{0:T(1024)} %param.21) | copy-start | bytes 19204
  37.5 20.7 %copy-start.15 = (s32[1536]{0:T(1024)S(1)}, s32[1536]{0:T(1024)}, u32[]{:S(2)}) copy-start(s32[1536]{0:T(1024)} %param.20) | copy-start | bytes 18436
  37.5 4.3 %collective-permute-start.8 = (f32[16,1024]{1,0:T(8,128)S(1)}, f32[16,1024]{1,0:T(8,128)S(1)}, u32[]{:S(2)}, u32[]{:S(2)}) collective-permute-start(f32[16,1024]{1,0:T(8,128)S(1)} %add.153), channel_id=1, source_target_pairs={{0,8},{1,9},{2,10},{3,11},{4,12},{5,13},{6,14},{7,15},{8,0},{9,1},... | collective-permute-start | bytes 196616 | tf_op jit(solution)/shard_map/ppermute | solution.py:68
  41.9 5.2 %collective-permute-start.9 = (f32[16,1024]{1,0:T(8,128)S(1)}, f32[16,1024]{1,0:T(8,128)S(1)}, u32[]{:S(2)}, u32[]{:S(2)}) collective-permute-start(f32[16,1024]{1,0:T(8,128)S(1)} %add.154), channel_id=1, source_target_pairs={{0,16},{1,17},{2,18},{3,19},{4,20},{5,21},{6,22},{7,23},{8,24},{9,... | collective-permute-start | bytes 196616 | tf_op jit(solution)/shard_map/ppermute | solution.py:68
  47.1 1.3 %collective-permute-start.10 = (f32[16,1024]{1,0:T(8,128)S(1)}, f32[16,1024]{1,0:T(8,128)S(1)}, u32[]{:S(2)}, u32[]{:S(2)}) collective-permute-start(f32[16,1024]{1,0:T(8,128)S(1)} %get-tuple-element.18), channel_id=1, source_target_pairs={{0,1},{1,0},{2,3},{3,2},{4,5},{5,4},{6,7},{7,6},{8,9},{9,8},{10,11... | collective-permute-start | bytes 196616 | tf_op jit(solution)/shard_map/ppermute | solution.py:68
  56.6 4.2 %collective-permute-start.11 = (f32[32,384]{1,0:T(8,128)S(1)}, f32[32,384]{1,0:T(8,128)S(1)}, u32[]{:S(2)}, u32[]{:S(2)}) collective-permute-start(f32[32,384]{1,0:T(8,128)S(1)} %fusion.62), channel_id=1, source_target_pairs={{0,8},{8,0},{16,24},{24,16},{1,9},{9,1},{17,25},{25,17},{2,10},{10... | collective-permute-start | bytes 147464 | tf_op jit(solution)/shard_map/ppermute | solution.py:25
  60.7 6.1 %collective-permute-start.12 = (f32[32,384]{1,0:T(8,128)S(1)}, f32[32,384]{1,0:T(8,128)S(1)}, u32[]{:S(2)}, u32[]{:S(2)}) collective-permute-start(f32[32,384]{1,0:T(8,128)S(1)} %add.156), channel_id=1, source_target_pairs={{0,16},{8,24},{16,0},{24,8},{1,17},{9,25},{17,1},{25,9},{2,18},{10... | collective-permute-start | bytes 147464 | tf_op jit(solution)/shard_map/ppermute | solution.py:25
  67.7 2.1 %collective-permute-start.13 = (f32[16,1024]{1,0:T(8,128)S(1)}, f32[16,1024]{1,0:T(8,128)S(1)}, u32[]{:S(2)}, u32[]{:S(2)}) collective-permute-start(f32[16,1024]{1,0:T(8,128)S(1)} %constant_dynamic-slice_fusion.1), channel_id=1, source_target_pairs={{0,1},{1,0},{2,3},{3,2},{4,5},{5,4},{6,7},{7,6},{8,9},{9,8},{10,11... | collective-permute-start | bytes 196616 | tf_op jit(solution)/shard_map/ppermute | solution.py:68
  67.8 17.0 %collective-permute-start.21 = (f32[2,400,128]{2,1,0:T(8,128)S(1)}, f32[2,400,128]{2,1,0:T(8,128)}, u32[]{:S(2)}, u32[]{:S(2)}) collective-permute-start(f32[2,400,128]{2,1,0:T(8,128)S(1)} %dynamic-slice_bitcast_fusion), channel_id=1, source_target_pairs={{0,8},{8,0},{16,24},{24,16},{1,9},{9,1},{17,25},{25,17},{2,10},{10... | collective-permute-start | bytes 1228808 | tf_op jit(solution)/shard_map/ppermute | solution.py:111
  69.8 4.3 %collective-permute-start.14 = (f32[16,1024]{1,0:T(8,128)S(1)}, f32[16,1024]{1,0:T(8,128)S(1)}, u32[]{:S(2)}, u32[]{:S(2)}) collective-permute-start(f32[16,1024]{1,0:T(8,128)S(1)} %dynamic-slice_add_fusion.1), channel_id=1, source_target_pairs={{0,2},{1,3},{2,0},{3,1},{4,6},{5,7},{6,4},{7,5},{8,10},{9,11},{10,... | collective-permute-start | bytes 196616 | tf_op jit(solution)/shard_map/ppermute | solution.py:68
  74.2 4.3 %collective-permute-start.15 = (f32[16,1024]{1,0:T(8,128)S(1)}, f32[16,1024]{1,0:T(8,128)S(1)}, u32[]{:S(2)}, u32[]{:S(2)}) collective-permute-start(f32[16,1024]{1,0:T(8,128)S(1)} %add.159), channel_id=1, source_target_pairs={{0,4},{1,5},{2,6},{3,7},{4,0},{5,1},{6,2},{7,3},{8,12},{9,13},{10,... | collective-permute-start | bytes 196616 | tf_op jit(solution)/shard_map/ppermute | solution.py:68
  78.5 4.3 %collective-permute-start.16 = (f32[16,1024]{1,0:T(8,128)S(1)}, f32[16,1024]{1,0:T(8,128)S(1)}, u32[]{:S(2)}, u32[]{:S(2)}) collective-permute-start(f32[16,1024]{1,0:T(8,128)S(1)} %add.160), channel_id=1, source_target_pairs={{0,8},{1,9},{2,10},{3,11},{4,12},{5,13},{6,14},{7,15},{8,0},{9,1},... | collective-permute-start | bytes 196616 | tf_op jit(solution)/shard_map/ppermute | solution.py:68
  82.9 5.9 %collective-permute-start.17 = (f32[16,1024]{1,0:T(8,128)S(1)}, f32[16,1024]{1,0:T(8,128)S(1)}, u32[]{:S(2)}, u32[]{:S(2)}) collective-permute-start(f32[16,1024]{1,0:T(8,128)S(1)} %add.161), channel_id=1, source_target_pairs={{0,16},{1,17},{2,18},{3,19},{4,20},{5,21},{6,22},{7,23},{8,24},{9,... | collective-permute-start | bytes 196616 | tf_op jit(solution)/shard_map/ppermute | solution.py:68
  88.8 15.6 %copy-start.11 = (f32[400,128]{1,0:T(8,128)S(1)}, f32[400,128]{1,0:T(8,128)}, u32[]{:S(2)}) copy-start(f32[400,128]{1,0:T(8,128)} %param.22) | copy-start | bytes 614404
  88.8 1.5 %collective-permute-start.18 = (f32[16,1024]{1,0:T(8,128)S(1)}, f32[16,1024]{1,0:T(8,128)S(1)}, u32[]{:S(2)}, u32[]{:S(2)}) collective-permute-start(f32[16,1024]{1,0:T(8,128)S(1)} %get-tuple-element.16), channel_id=1, source_target_pairs={{0,1},{1,0},{2,3},{3,2},{4,5},{5,4},{6,7},{7,6},{8,9},{9,8},{10,11... | collective-permute-start | bytes 196616 | tf_op jit(solution)/shard_map/ppermute | solution.py:68
  89.0 15.5 %collective-permute-start.22 = (f32[1,400,128]{2,1,0:T(8,128)S(1)}, f32[1,400,128]{2,1,0:T(8,128)S(1)}, u32[]{:S(2)}, u32[]{:S(2)}) collective-permute-start(f32[1,400,128]{2,1,0:T(8,128)S(1)} %constant_dynamic-slice_fusion), channel_id=1, source_target_pairs={{0,16},{8,24},{16,0},{24,8},{1,17},{9,25},{17,1},{25,9},{2,18},{10... | collective-permute-start | bytes 614408 | tf_op jit(solution)/shard_map/ppermute | solution.py:111
  98.6 4.2 %collective-permute-start.19 = (f32[32,384]{1,0:T(8,128)S(1)}, f32[32,384]{1,0:T(8,128)S(1)}, u32[]{:S(2)}, u32[]{:S(2)}) collective-permute-start(f32[32,384]{1,0:T(8,128)S(1)} %fusion.63), channel_id=1, source_target_pairs={{0,8},{8,0},{16,24},{24,16},{1,9},{9,1},{17,25},{25,17},{2,10},{10... | collective-permute-start | bytes 147464 | tf_op jit(solution)/shard_map/ppermute | solution.py:25
  102.8 5.1 %collective-permute-start.20 = (f32[32,384]{1,0:T(8,128)S(1)}, f32[32,384]{1,0:T(8,128)S(1)}, u32[]{:S(2)}, u32[]{:S(2)}) collective-permute-start(f32[32,384]{1,0:T(8,128)S(1)} %add.163), channel_id=1, source_target_pairs={{0,16},{8,24},{16,0},{24,8},{1,17},{9,25},{17,1},{25,9},{2,18},{10... | collective-permute-start | bytes 147464 | tf_op jit(solution)/shard_map/ppermute | solution.py:25
  108.7 1.2 copy-start.9
  108.7 1.2 copy-start.10

commit v16 on v13

--- a/solution.py
+++ b/solution.py
@@ -73,6 +73,9 @@
     given = lax.dynamic_slice_in_dim(value, (1 - core) * half, half, 0)
     kept = kept + exchange(given, 1)
     stride = 2
+    if count >= 8:
+        kept = (kept + exchange(kept, 2)) + (exchange(kept, 4) + exchange(kept, 6))
+        stride = 8
     while stride < count:
         kept = kept + exchange(kept, stride)
         stride *= 2

time: 131 us -> 129 us (0.985)
  waiting for transfers between devices: 45.8 us -> 42.1 us
  starting transfers between devices: 31.4 us -> 33 us
    ppermute x12 -> x14, waiting for transfers between devices: 25.6 us -> 22.7 us  [exchange(): return lax.ppermute(piece, axes, [(i, i ^ stride) for i in range(count)])]
    ppermute x12 -> x14, starting transfers between devices: 13.4 us -> 14.6 us  [exchange(): return lax.ppermute(piece, axes, [(i, i ^ stride) for i in range(count)])]
  transfers between devices with their start and end apart: 23 -> 25, of which waited for: 16 -> 19; matrix products, arithmetic and copies ran while one was open for 14% -> 14% of each run, Pallas kernels for 0% -> 0%
where the time goes in v16:
time: 129 us
  waiting for transfers between devices  42.1 us (33%)
  starting transfers between devices  33 us (26%)
  other arithmetic  19.3 us (15%)
  blocking collectives  17.9 us (14%)
  matrix products  10.7 us (8%)
  local copies, waits for them, and re-layouts  4.52 us (4%)
    ppermute x14, waiting for transfers between devices, exchange(): return lax.ppermute(piece, axes, [(i, i ^ stride) for i in range(count)])  22.7 us
    all_gather x1, blocking collectives, shards(): lax.all_gather(master_new.astype(jnp.bfloat16), 'rep', axis=0, tiled=True)  17.9 us
    ppermute x14, starting transfers between devices, exchange(): return lax.ppermute(piece, axes, [(i, i ^ stride) for i in range(count)])  14.6 us
    ppermute x5, waiting for transfers between devices, exchange(): return lax.ppermute(value, axis, [(i, i ^ stride) for i in range(count)])  12 us
    ppermute x5, starting transfers between devices, exchange(): return lax.ppermute(value, axis, [(i, i ^ stride) for i in range(count)])  7.91 us
    ppermute x4, starting transfers between devices, tree_sum(): value = value + lax.ppermute(value, axes, pairs)  7.63 us
    ppermute x4, waiting for transfers between devices, tree_sum(): value = value + lax.ppermute(value, axes, pairs)  7.4 us
    another operation x6, other arithmetic, shards(): factor_low = jnp.linalg.cholesky(gram_matrix)  7.19 us
  transfers between devices with their start and end apart: 25, of which 19 were waited for; matrix products, arithmetic and copies ran while one was open for 14% of the time, Pallas kernels for 0%

profile of v16, /device:TPU:0, one launch (start us, length us, event | category | flops | bytes accessed | tf_op | source)
XLA Modules:
  0.0 128.6 jit_solution(15488287371103606793)
XLA Ops:
  0.7 3.0 %collective-permute-start = (bf16[192,1024]{1,0:T(8,128)(2,1)}, bf16[192,1024]{1,0:T(8,128)(2,1)S(1)}, u32[]{:S(2)}, u32[]{:S(2)}) collective-permute-start(bf16[192,1024]{1,0:T(8,128)(2,1)} %param.13), channel_id=1, source_target_pairs={{0,2},{1,3},{2,0},{3,1},{4,6},{5,7},{6,4},{7,5},{8,10},{9,11},{10,... | collective-permute-start | bytes 1179656 | tf_op jit(solution)/shard_map/ppermute | solution.py:40
  3.7 1.5 %collective-permute-start.1 = (bf16[192,1024]{1,0:T(8,128)(2,1)}, bf16[192,1024]{1,0:T(8,128)(2,1)S(1)}, u32[]{:S(2)}, u32[]{:S(2)}) collective-permute-start(bf16[192,1024]{1,0:T(8,128)(2,1)} %param.13), channel_id=1, source_target_pairs={{0,4},{1,5},{2,6},{3,7},{4,0},{5,1},{6,2},{7,3},{8,12},{9,13},{10,... | collective-permute-start | bytes 1179656 | tf_op jit(solution)/shard_map/ppermute | solution.py:40
  5.2 7.8 %collective-permute-done = bf16[192,1024]{1,0:T(8,128)(2,1)S(1)} collective-permute-done((bf16[192,1024]{1,0:T(8,128)(2,1)}, bf16[192,1024]{1,0:T(8,128)(2,1)S(1)}, u32[]{:S(2)}, u32[]{:S(2)}) %collective-permute-start) | collective-permute-done | bytes 393248 | tf_op jit(solution)/shard_map/ppermute | solution.py:40
  13.0 1.8 %collective-permute-start.3 = (bf16[96,1024]{1,0:T(8,128)(2,1)S(1)}, bf16[96,1024]{1,0:T(8,128)(2,1)S(1)}, u32[]{:S(2)}, u32[]{:S(2)}) collective-permute-start(bf16[96,1024]{1,0:T(8,128)(2,1)S(1)} %slice.17), channel_id=1, source_target_pairs={{0,4},{1,5},{2,6},{3,7},{4,0},{5,1},{6,2},{7,3},{8,12},{9,13},{10,... | collective-permute-start | bytes 589832 | tf_op jit(solution)/shard_map/ppermute | solution.py:40
  14.9 1.6 %collective-permute-start.2 = (bf16[96,1024]{1,0:T(8,128)(2,1)S(1)}, bf16[96,1024]{1,0:T(8,128)(2,1)S(1)}, u32[]{:S(2)}, u32[]{:S(2)}) collective-permute-start(bf16[96,1024]{1,0:T(8,128)(2,1)S(1)} %slice.16), channel_id=1, source_target_pairs={{0,2},{1,3},{2,0},{3,1},{4,6},{5,7},{6,4},{7,5},{8,10},{9,11},{10,... | collective-permute-start | bytes 589832 | tf_op jit(solution)/shard_map/ppermute | solution.py:40
  16.4 2.7 %collective-permute-done.3 = bf16[96,1024]{1,0:T(8,128)(2,1)S(1)} collective-permute-done((bf16[96,1024]{1,0:T(8,128)(2,1)S(1)}, bf16[96,1024]{1,0:T(8,128)(2,1)S(1)}, u32[]{:S(2)}, u32[]{:S(2)}) %collective-permute-start.3) | collective-permute-done | bytes 196640 | tf_op jit(solution)/shard_map/ppermute | solution.py:40
  19.2 1.4 %collective-permute-done.2 = bf16[96,1024]{1,0:T(8,128)(2,1)S(1)} collective-permute-done((bf16[96,1024]{1,0:T(8,128)(2,1)S(1)}, bf16[96,1024]{1,0:T(8,128)(2,1)S(1)}, u32[]{:S(2)}, u32[]{:S(2)}) %collective-permute-start.2) | collective-permute-done | bytes 196640 | tf_op jit(solution)/shard_map/ppermute | solution.py:40
  21.4 1.6 %constant_dynamic-slice_fusion.6 = (bf16[1,192,384]{2,1,0:T(8,128)(2,1)S(1)}, bf16[1,192,384]{2,1,0:T(8,128)(2,1)S(1)}, bf16[1,192,384]{2,1,0:T(8,128)(2,1)S(1)}...) fusion(bf16[8,192,384]{2,1,0:T(8,128)(2,1)} %bitcast.61, ...), kind=kLoop, calls=%fused_computation.83 | loop fusion | bytes 2359328 | tf_op jit(solution)/shard_map/dynamic_slice | solution.py:53
  23.5 1.0 convert_add_fusion
  25.3 1.0 bitcast_add_fusion
  27.8 0.9 collective-permute-done.5
  28.7 1.2 collective-permute-start.7
  29.9 1.8 %collective-permute-start.8 = (f32[16,1024]{1,0:T(8,128)S(1)}, f32[16,1024]{1,0:T(8,128)S(1)}, u32[]{:S(2)}, u32[]{:S(2)}) collective-permute-start(f32[16,1024]{1,0:T(8,128)S(1)} %dynamic-slice_add_fusion.2), channel_id=1, source_target_pairs={{0,6},{1,7},{2,4},{3,5},{4,2},{5,3},{6,0},{7,1},{8,14},{9,15},{10,... | collective-permute-start | bytes 196616 | tf_op jit(solution)/shard_map/ppermute | solution.py:68
  32.3 0.9 collective-permute-done.7
  33.2 2.4 %collective-permute-done.8 = f32[16,1024]{1,0:T(8,128)S(1)} collective-permute-done((f32[16,1024]{1,0:T(8,128)S(1)}, f32[16,1024]{1,0:T(8,128)S(1)}, u32[]{:S(2)}, u32[]{:S(2)}) %collective-permute-start.8) | collective-permute-done | bytes 65568 | tf_op jit(solution)/shard_map/ppermute | solution.py:68
  36.1 1.6 %collective-permute-start.9 = (f32[16,1024]{1,0:T(8,128)S(1)}, f32[16,1024]{1,0:T(8,128)S(1)}, u32[]{:S(2)}, u32[]{:S(2)}) collective-permute-start(f32[16,1024]{1,0:T(8,128)S(1)} %add_add_fusion.1), channel_id=1, source_target_pairs={{0,8},{1,9},{2,10},{3,11},{4,12},{5,13},{6,14},{7,15},{8,0},{9,1},... | collective-permute-start | bytes 196616 | tf_op jit(solution)/shard_map/ppermute | solution.py:68
  37.7 2.7 %collective-permute-done.9 = f32[16,1024]{1,0:T(8,128)S(1)} collective-permute-done((f32[16,1024]{1,0:T(8,128)S(1)}, f32[16,1024]{1,0:T(8,128)S(1)}, u32[]{:S(2)}, u32[]{:S(2)}) %collective-permute-start.9) | collective-permute-done | bytes 65568 | tf_op jit(solution)/shard_map/ppermute | solution.py:68
  40.4 2.6 %collective-permute-start.10 = (f32[16,1024]{1,0:T(8,128)S(1)}, f32[16,1024]{1,0:T(8,128)S(1)}, u32[]{:S(2)}, u32[]{:S(2)}) collective-permute-start(f32[16,1024]{1,0:T(8,128)S(1)} %add.161), channel_id=1, source_target_pairs={{0,16},{1,17},{2,18},{3,19},{4,20},{5,21},{6,22},{7,23},{8,24},{9,... | collective-permute-start | bytes 196616 | tf_op jit(solution)/shard_map/ppermute | solution.py:68
  43.1 2.6 %collective-permute-done.10 = f32[16,1024]{1,0:T(8,128)S(1)} collective-permute-done((f32[16,1024]{1,0:T(8,128)S(1)}, f32[16,1024]{1,0:T(8,128)S(1)}, u32[]{:S(2)}, u32[]{:S(2)}) %collective-permute-start.10) | collective-permute-done | bytes 65568 | tf_op jit(solution)/shard_map/ppermute | solution.py:68
  45.8 1.2 collective-permute-done.11
  47.4 2.9 %cholesky.44 = f32[32,32]{1,0:T(8,128)S(1)} custom-call(f32[32,32]{1,0:T(8,128)S(1)} %fusion.46), custom_call_target="Cholesky" | custom-call | tf_op jit(solution)/shard_map/jit(cholesky)/cholesky | solution.py:187
  51.6 2.4 %custom-call.6 = f32[1,32,32]{1,2,0:T(8,128)S(1)} custom-call(f32[1,32,32]{2,1,0:T(8,128)S(1)} %fusion.41), custom_call_target="InvertDiagBlocksLowerTriangular" | custom-call | tf_op jit(solution)/shard_map/jit(_solve_triangular)/triangular_solve | solution.py:188
  54.9 1.6 %collective-permute-start.12 = (f32[32,384]{1,0:T(8,128)S(1)}, f32[32,384]{1,0:T(8,128)S(1)}, u32[]{:S(2)}, u32[]{:S(2)}) collective-permute-start(f32[32,384]{1,0:T(8,128)S(1)} %fusion.58), channel_id=1, source_target_pairs={{0,8},{8,0},{16,24},{24,16},{1,9},{9,1},{17,25},{25,17},{2,10},{10... | collective-permute-start | bytes 147464 | tf_op jit(solution)/shard_map/ppermute | solution.py:25
  56.6 1.1 select_reduce_fusion
  57.7 1.4 %collective-permute-done.12 = f32[32,384]{1,0:T(8,128)S(1)} collective-permute-done((f32[32,384]{1,0:T(8,128)S(1)}, f32[32,384]{1,0:T(8,128)S(1)}, u32[]{:S(2)}, u32[]{:S(2)}) %collective-permute-start.12) | collective-permute-done | bytes 49184 | tf_op jit(solution)/shard_map/ppermute | solution.py:25
  59.1 2.8 %collective-permute-start.13 = (f32[32,384]{1,0:T(8,128)S(1)}, f32[32,384]{1,0:T(8,128)S(1)}, u32[]{:S(2)}, u32[]{:S(2)}) collective-permute-start(f32[32,384]{1,0:T(8,128)S(1)} %add.163), channel_id=1, source_target_pairs={{0,16},{8,24},{16,0},{24,8},{1,17},{9,25},{17,1},{25,9},{2,18},{10... | collective-permute-start | bytes 147464 | tf_op jit(solution)/shard_map/ppermute | solution.py:25
  61.9 3.1 %fusion = f32[1600,128]{1,0:T(8,128)S(1)} fusion(bf16[1536,128]{1,0:T(8,128)(2,1)S(1)} %copy-done, s32[1536]{0:T(1024)S(1)} %select_reduce_fusion), kind=kOutput, calls=%fused_computation.1 | convolution fusion | flops 631603200 | bytes 1218560 | tf_op jit(solution)/shard_map/dot_general | solution.py:102
  65.0 0.8 fusion.35
  66.7 2.0 %collective-permute-start.23 = (f32[2,400,128]{2,1,0:T(8,128)}, f32[2,400,128]{2,1,0:T(8,128)}, u32[]{:S(2)}, u32[]{:S(2)}) collective-permute-start(f32[2,400,128]{2,1,0:T(8,128)} %dynamic-slice_bitcast_fusion), channel_id=1, source_target_pairs={{0,8},{8,0},{16,24},{24,16},{1,9},{9,1},{17,25},{25,17},{2,10},{10... | collective-permute-start | bytes 1228808 | tf_op jit(solution)/shard_map/ppermute | solution.py:114
  68.8 0.9 collective-permute-start.16
  69.7 1.8 %collective-permute-start.17 = (f32[16,1024]{1,0:T(8,128)S(1)}, f32[16,1024]{1,0:T(8,128)S(1)}, u32[]{:S(2)}, u32[]{:S(2)}) collective-permute-start(f32[16,1024]{1,0:T(8,128)S(1)} %dynamic-slice_add_fusion.1), channel_id=1, source_target_pairs={{0,6},{1,7},{2,4},{3,5},{4,2},{5,3},{6,0},{7,1},{8,14},{9,15},{10,... | collective-permute-start | bytes 196616 | tf_op jit(solution)/shard_map/ppermute | solution.py:68
  73.1 2.3 %collective-permute-done.17 = f32[16,1024]{1,0:T(8,128)S(1)} collective-permute-done((f32[16,1024]{1,0:T(8,128)S(1)}, f32[16,1024]{1,0:T(8,128)S(1)}, u32[]{:S(2)}, u32[]{:S(2)}) %collective-permute-start.17) | collective-permute-done | bytes 65568 | tf_op jit(solution)/shard_map/ppermute | solution.py:68
  76.3 4.1 %collective-permute-done.18 = f32[16,1024]{1,0:T(8,128)S(1)} collective-permute-done((f32[16,1024]{1,0:T(8,128)S(1)}, f32[16,1024]{1,0:T(8,128)S(1)}, u32[]{:S(2)}, u32[]{:S(2)}) %collective-permute-start.18) | collective-permute-done | bytes 65568 | tf_op jit(solution)/shard_map/ppermute | solution.py:68
  80.5 1.9 %collective-permute-start.19 = (f32[16,1024]{1,0:T(8,128)S(1)}, f32[16,1024]{1,0:T(8,128)S(1)}, u32[]{:S(2)}, u32[]{:S(2)}) collective-permute-start(f32[16,1024]{1,0:T(8,128)S(1)} %add.169), channel_id=1, source_target_pairs={{0,16},{1,17},{2,18},{3,19},{4,20},{5,21},{6,22},{7,23},{8,24},{9,... | collective-permute-start | bytes 196616 | tf_op jit(solution)/shard_map/ppermute | solution.py:68
  82.4 1.0 bitcast_add_fusion.1
  83.5 3.6 %collective-permute-done.19 = f32[16,1024]{1,0:T(8,128)S(1)} collective-permute-done((f32[16,1024]{1,0:T(8,128)S(1)}, f32[16,1024]{1,0:T(8,128)S(1)}, u32[]{:S(2)}, u32[]{:S(2)}) %collective-permute-start.19) | collective-permute-done | bytes 65568 | tf_op jit(solution)/shard_map/ppermute | solution.py:68
  87.2 0.9 collective-permute-start.24
  88.8 2.9 %cholesky.55 = f32[32,32]{1,0:T(8,128)S(1)} custom-call(f32[32,32]{1,0:T(8,128)S(1)} %fusion.44), custom_call_target="Cholesky" | custom-call | tf_op jit(solution)/shard_map/jit(cholesky)/cholesky | solution.py:187
  93.0 2.4 %custom-call.7 = f32[1,32,32]{1,2,0:T(8,128)S(1)} custom-call(f32[1,32,32]{2,1,0:T(8,128)S(1)} %fusion.42), custom_call_target="InvertDiagBlocksLowerTriangular" | custom-call | tf_op jit(solution)/shard_map/jit(_solve_triangular)/triangular_solve | solution.py:188
  96.4 1.9 %collective-permute-start.21 = (f32[32,384]{1,0:T(8,128)S(1)}, f32[32,384]{1,0:T(8,128)S(1)}, u32[]{:S(2)}, u32[]{:S(2)}) collective-permute-start(f32[32,384]{1,0:T(8,128)S(1)} %fusion.59), channel_id=1, source_target_pairs={{0,8},{8,0},{16,24},{24,16},{1,9},{9,1},{17,25},{25,17},{2,10},{10... | collective-permute-start | bytes 147464 | tf_op jit(solution)/shard_map/ppermute | solution.py:25
  98.2 3.0 %collective-permute-done.21 = f32[32,384]{1,0:T(8,128)S(1)} collective-permute-done((f32[32,384]{1,0:T(8,128)S(1)}, f32[32,384]{1,0:T(8,128)S(1)}, u32[]{:S(2)}, u32[]{:S(2)}) %collective-permute-start.21) | collective-permute-done | bytes 49184 | tf_op jit(solution)/shard_map/ppermute | solution.py:25
  101.2 1.3 %collective-permute-start.22 = (f32[32,384]{1,0:T(8,128)S(1)}, f32[32,384]{1,0:T(8,128)S(1)}, u32[]{:S(2)}, u32[]{:S(2)}) collective-permute-start(f32[32,384]{1,0:T(8,128)S(1)} %add.171), channel_id=1, source_target_pairs={{0,16},{8,24},{16,0},{24,8},{1,17},{9,25},{17,1},{25,9},{2,18},{10... | collective-permute-start | bytes 147464 | tf_op jit(solution)/shard_map/ppermute | solution.py:25
  103.3 3.0 %collective-permute-done.22 = f32[32,384]{1,0:T(8,128)S(1)} collective-permute-done((f32[32,384]{1,0:T(8,128)S(1)}, f32[32,384]{1,0:T(8,128)S(1)}, u32[]{:S(2)}, u32[]{:S(2)}) %collective-permute-start.22) | collective-permute-done | bytes 49184 | tf_op jit(solution)/shard_map/ppermute | solution.py:25
  106.3 0.8 fusion.40
  107.1 1.1 fusion.7
  108.3 1.0 fusion.57
  109.3 17.9 %all_gather.3 = bf16[1024,384]{1,0:T(8,128)(2,1)S(1)} all-gather(bf16[256,384]{1,0:T(8,128)(2,1)S(1)} %get-tuple-element.12), channel_id=1, replica_groups=mesh['rep'=4,'tp'=8] {'rep'}, dimensions={0}, use_global_device_ids=true | all-gather | bytes 983040 | tf_op jit(solution)/shard_map/all_gather | solution.py:202
  127.8 0.9 copy.25
  (93 shorter events, 14.9 us)
Async XLA Ops:
  0.6 61.3 %copy-start = (bf16[1536,128]{1,0:T(8,128)(2,1)S(1)}, bf16[1536,128]{1,0:T(8,128)(2,1)}, u32[]{:S(2)}) copy-start(bf16[1536,128]{1,0:T(8,128)(2,1)} %param.19) | copy-start | bytes 1179652
  0.6 20.0 %copy-start.7 = (bf16[192,1024]{1,0:T(8,128)(2,1)S(1)}, bf16[192,1024]{1,0:T(8,128)(2,1)}, u32[]{:S(2)}) copy-start(bf16[192,1024]{1,0:T(8,128)(2,1)} %param.13) | copy-start | bytes 1179652
  0.7 12.3 %collective-permute-start = (bf16[192,1024]{1,0:T(8,128)(2,1)}, bf16[192,1024]{1,0:T(8,128)(2,1)S(1)}, u32[]{:S(2)}, u32[]{:S(2)}) collective-permute-start(bf16[192,1024]{1,0:T(8,128)(2,1)} %param.13), channel_id=1, source_target_pairs={{0,2},{1,3},{2,0},{3,1},{4,6},{5,7},{6,4},{7,5},{8,10},{9,11},{10,... | collective-permute-start | bytes 1179656 | tf_op jit(solution)/shard_map/ppermute | solution.py:40
  3.7 11.2 %collective-permute-start.1 = (bf16[192,1024]{1,0:T(8,128)(2,1)}, bf16[192,1024]{1,0:T(8,128)(2,1)S(1)}, u32[]{:S(2)}, u32[]{:S(2)}) collective-permute-start(bf16[192,1024]{1,0:T(8,128)(2,1)} %param.13), channel_id=1, source_target_pairs={{0,4},{1,5},{2,6},{3,7},{4,0},{5,1},{6,2},{7,3},{8,12},{9,13},{10,... | collective-permute-start | bytes 1179656 | tf_op jit(solution)/shard_map/ppermute | solution.py:40
  13.0 7.9 %copy-start.3 = (bf16[192,1024]{1,0:T(8,128)(2,1)}, bf16[192,1024]{1,0:T(8,128)(2,1)S(1)}, u32[]{:S(2)}) copy-start(bf16[192,1024]{1,0:T(8,128)(2,1)S(1)} %collective-permute-done) | copy-start | bytes 1179652
  13.0 6.2 %collective-permute-start.3 = (bf16[96,1024]{1,0:T(8,128)(2,1)S(1)}, bf16[96,1024]{1,0:T(8,128)(2,1)S(1)}, u32[]{:S(2)}, u32[]{:S(2)}) collective-permute-start(bf16[96,1024]{1,0:T(8,128)(2,1)S(1)} %slice.17), channel_id=1, source_target_pairs={{0,4},{1,5},{2,6},{3,7},{4,0},{5,1},{6,2},{7,3},{8,12},{9,13},{10,... | collective-permute-start | bytes 589832 | tf_op jit(solution)/shard_map/ppermute | solution.py:40
  14.8 6.0 %copy-start.5 = (bf16[192,1024]{1,0:T(8,128)(2,1)}, bf16[192,1024]{1,0:T(8,128)(2,1)S(1)}, u32[]{:S(2)}) copy-start(bf16[192,1024]{1,0:T(8,128)(2,1)S(1)} %collective-permute-done.1) | copy-start | bytes 1179652
  14.9 5.7 %collective-permute-start.2 = (bf16[96,1024]{1,0:T(8,128)(2,1)S(1)}, bf16[96,1024]{1,0:T(8,128)(2,1)S(1)}, u32[]{:S(2)}, u32[]{:S(2)}) collective-permute-start(bf16[96,1024]{1,0:T(8,128)(2,1)S(1)} %slice.16), channel_id=1, source_target_pairs={{0,2},{1,3},{2,0},{3,1},{4,6},{5,7},{6,4},{7,5},{8,10},{9,11},{10,... | collective-permute-start | bytes 589832 | tf_op jit(solution)/shard_map/ppermute | solution.py:40
  20.6 0.7 copy-start.1
  21.4 4.0 %collective-permute-start.4 = (bf16[4,192,1024]{2,1,0:T(8,128)(2,1)S(1)}, bf16[4,192,1024]{2,1,0:T(8,128)(2,1)S(1)}, u32[]{:S(2)}, u32[]{:S(2)}) collective-permute-start(bf16[4,192,1024]{2,1,0:T(8,128)(2,1)S(1)} %pad_maximum_fusion), channel_id=1, source_target_pairs={{0,1},{1,0},{2,3},{3,2},{4,5},{5,4},{6,7},{7,6},{8,9},{9,8},{10,11... | collective-permute-start | bytes 4718600 | tf_op jit(solution)/shard_map/ppermute | solution.py:40
  21.4 1.7 %copy-start.2 = (bf16[1,192,1024]{2,1,0:T(8,128)(2,1)S(1)}, bf16[1,192,1024]{2,1,0:T(8,128)(2,1)}, u32[]{:S(2)}) copy-start(bf16[1,192,1024]{2,1,0:T(8,128)(2,1)} %copy-done.1) | copy-start | bytes 1179652
  21.4 1.7 %copy-start.4 = (bf16[192,1024]{1,0:T(8,128)(2,1)S(1)}, bf16[192,1024]{1,0:T(8,128)(2,1)}, u32[]{:S(2)}) copy-start(bf16[192,1024]{1,0:T(8,128)(2,1)} %copy-done.3) | copy-start | bytes 1179652
  21.4 1.7 %copy-start.6 = (bf16[192,1024]{1,0:T(8,128)(2,1)S(1)}, bf16[192,1024]{1,0:T(8,128)(2,1)}, u32[]{:S(2)}) copy-start(bf16[192,1024]{1,0:T(8,128)(2,1)} %copy-done.5) | copy-start | bytes 1179652
  21.4 1.8 %copy-start.8 = (bf16[192,1024]{1,0:T(8,128)(2,1)S(1)}, bf16[192,1024]{1,0:T(8,128)(2,1)}, u32[]{:S(2)}) copy-start(bf16[192,1024]{1,0:T(8,128)(2,1)} %param.13) | copy-start | bytes 1179652
  21.4 2.1 %copy-start.13 = (bf16[1,1024,384]{2,1,0:T(8,128)(2,1)S(1)}, bf16[1,1024,384]{2,1,0:T(8,128)(2,1)}, u32[]{:S(2)}) copy-start(bf16[1,1024,384]{2,1,0:T(8,128)(2,1)} %param.15) | copy-start | bytes 2359300
  23.5 1.0 copy-start.12
  27.3 1.5 %collective-permute-start.5 = (f32[16,1024]{1,0:T(8,128)S(1)}, f32[16,1024]{1,0:T(8,128)S(1)}, u32[]{:S(2)}, u32[]{:S(2)}) collective-permute-start(f32[16,1024]{1,0:T(8,128)S(1)} %constant_dynamic-slice_fusion.2), channel_id=1, source_target_pairs={{0,1},{1,0},{2,3},{3,2},{4,5},{5,4},{6,7},{7,6},{8,9},{9,8},{10,11... | collective-permute-start | bytes 196616 | tf_op jit(solution)/shard_map/ppermute | solution.py:68
  28.7 4.4 %collective-permute-start.7 = (f32[16,1024]{1,0:T(8,128)S(1)}, f32[16,1024]{1,0:T(8,128)S(1)}, u32[]{:S(2)}, u32[]{:S(2)}) collective-permute-start(f32[16,1024]{1,0:T(8,128)S(1)} %dynamic-slice_add_fusion.2), channel_id=1, source_target_pairs={{0,4},{1,5},{2,6},{3,7},{4,0},{5,1},{6,2},{7,3},{8,12},{9,13},{10,... | collective-permute-start | bytes 196616 | tf_op jit(solution)/shard_map/ppermute | solution.py:68
  29.9 5.7 %collective-permute-start.8 = (f32[16,1024]{1,0:T(8,128)S(1)}, f32[16,1024]{1,0:T(8,128)S(1)}, u32[]{:S(2)}, u32[]{:S(2)}) collective-permute-start(f32[16,1024]{1,0:T(8,128)S(1)} %dynamic-slice_add_fusion.2), channel_id=1, source_target_pairs={{0,6},{1,7},{2,4},{3,5},{4,2},{5,3},{6,0},{7,1},{8,14},{9,15},{10,... | collective-permute-start | bytes 196616 | tf_op jit(solution)/shard_map/ppermute | solution.py:68
  31.8 4.3 %collective-permute-start.6 = (f32[16,1024]{1,0:T(8,128)S(1)}, f32[16,1024]{1,0:T(8,128)S(1)}, u32[]{:S(2)}, u32[]{:S(2)}) collective-permute-start(f32[16,1024]{1,0:T(8,128)S(1)} %dynamic-slice_add_fusion.2), channel_id=1, source_target_pairs={{0,2},{1,3},{2,0},{3,1},{4,6},{5,7},{6,4},{7,5},{8,10},{9,11},{10,... | collective-permute-start | bytes 196616 | tf_op jit(solution)/shard_map/ppermute | solution.py:68
  36.0 20.5 %copy-start.14 = (s32[1600]{0:T(1024)S(1)}, s32[1600]{0:T(1024)}, u32[]{:S(2)}) copy-start(s32[1600]{0:T(1024)} %param.21) | copy-start | bytes 19204
  36.1 20.5 %copy-start.15 = (s32[1536]{0:T(1024)S(1)}, s32[1536]{0:T(1024)}, u32[]{:S(2)}) copy-start(s32[1536]{0:T(1024)} %param.20) | copy-start | bytes 18436
  36.1 4.3 %collective-permute-start.9 = (f32[16,1024]{1,0:T(8,128)S(1)}, f32[16,1024]{1,0:T(8,128)S(1)}, u32[]{:S(2)}, u32[]{:S(2)}) collective-permute-start(f32[16,1024]{1,0:T(8,128)S(1)} %add_add_fusion.1), channel_id=1, source_target_pairs={{0,8},{1,9},{2,10},{3,11},{4,12},{5,13},{6,14},{7,15},{8,0},{9,1},... | collective-permute-start | bytes 196616 | tf_op jit(solution)/shard_map/ppermute | solution.py:68
  40.4 5.2 %collective-permute-start.10 = (f32[16,1024]{1,0:T(8,128)S(1)}, f32[16,1024]{1,0:T(8,128)S(1)}, u32[]{:S(2)}, u32[]{:S(2)}) collective-permute-start(f32[16,1024]{1,0:T(8,128)S(1)} %add.161), channel_id=1, source_target_pairs={{0,16},{1,17},{2,18},{3,19},{4,20},{5,21},{6,22},{7,23},{8,24},{9,... | collective-permute-start | bytes 196616 | tf_op jit(solution)/shard_map/ppermute | solution.py:68
  45.7 1.3 %collective-permute-start.11 = (f32[16,1024]{1,0:T(8,128)S(1)}, f32[16,1024]{1,0:T(8,128)S(1)}, u32[]{:S(2)}, u32[]{:S(2)}) collective-permute-start(f32[16,1024]{1,0:T(8,128)S(1)} %get-tuple-element.18), channel_id=1, source_target_pairs={{0,1},{1,0},{2,3},{3,2},{4,5},{5,4},{6,7},{7,6},{8,9},{9,8},{10,11... | collective-permute-start | bytes 196616 | tf_op jit(solution)/shard_map/ppermute | solution.py:68
  54.9 4.2 %collective-permute-start.12 = (f32[32,384]{1,0:T(8,128)S(1)}, f32[32,384]{1,0:T(8,128)S(1)}, u32[]{:S(2)}, u32[]{:S(2)}) collective-permute-start(f32[32,384]{1,0:T(8,128)S(1)} %fusion.58), channel_id=1, source_target_pairs={{0,8},{8,0},{16,24},{24,16},{1,9},{9,1},{17,25},{25,17},{2,10},{10... | collective-permute-start | bytes 147464 | tf_op jit(solution)/shard_map/ppermute | solution.py:25
  59.1 5.9 %collective-permute-start.13 = (f32[32,384]{1,0:T(8,128)S(1)}, f32[32,384]{1,0:T(8,128)S(1)}, u32[]{:S(2)}, u32[]{:S(2)}) collective-permute-start(f32[32,384]{1,0:T(8,128)S(1)} %add.163), channel_id=1, source_target_pairs={{0,16},{8,24},{16,0},{24,8},{1,17},{9,25},{17,1},{25,9},{2,18},{10... | collective-permute-start | bytes 147464 | tf_op jit(solution)/shard_map/ppermute | solution.py:25
  65.9 2.9 %collective-permute-start.14 = (f32[16,1024]{1,0:T(8,128)S(1)}, f32[16,1024]{1,0:T(8,128)S(1)}, u32[]{:S(2)}, u32[]{:S(2)}) collective-permute-start(f32[16,1024]{1,0:T(8,128)S(1)} %constant_dynamic-slice_fusion.1), channel_id=1, source_target_pairs={{0,1},{1,0},{2,3},{3,2},{4,5},{5,4},{6,7},{7,6},{8,9},{9,8},{10,11... | collective-permute-start | bytes 196616 | tf_op jit(solution)/shard_map/ppermute | solution.py:68
  66.7 15.7 %collective-permute-start.23 = (f32[2,400,128]{2,1,0:T(8,128)}, f32[2,400,128]{2,1,0:T(8,128)}, u32[]{:S(2)}, u32[]{:S(2)}) collective-permute-start(f32[2,400,128]{2,1,0:T(8,128)} %dynamic-slice_bitcast_fusion), channel_id=1, source_target_pairs={{0,8},{8,0},{16,24},{24,16},{1,9},{9,1},{17,25},{25,17},{2,10},{10... | collective-permute-start | bytes 1228808 | tf_op jit(solution)/shard_map/ppermute | solution.py:114
  68.8 4.3 %collective-permute-start.16 = (f32[16,1024]{1,0:T(8,128)S(1)}, f32[16,1024]{1,0:T(8,128)S(1)}, u32[]{:S(2)}, u32[]{:S(2)}) collective-permute-start(f32[16,1024]{1,0:T(8,128)S(1)} %dynamic-slice_add_fusion.1), channel_id=1, source_target_pairs={{0,4},{1,5},{2,6},{3,7},{4,0},{5,1},{6,2},{7,3},{8,12},{9,13},{10,... | collective-permute-start | bytes 196616 | tf_op jit(solution)/shard_map/ppermute | solution.py:68
  69.7 5.7 %collective-permute-start.17 = (f32[16,1024]{1,0:T(8,128)S(1)}, f32[16,1024]{1,0:T(8,128)S(1)}, u32[]{:S(2)}, u32[]{:S(2)}) collective-permute-start(f32[16,1024]{1,0:T(8,128)S(1)} %dynamic-slice_add_fusion.1), channel_id=1, source_target_pairs={{0,6},{1,7},{2,4},{3,5},{4,2},{5,3},{6,0},{7,1},{8,14},{9,15},{10,... | collective-permute-start | bytes 196616 | tf_op jit(solution)/shard_map/ppermute | solution.py:68
  71.5 4.3 %collective-permute-start.15 = (f32[16,1024]{1,0:T(8,128)S(1)}, f32[16,1024]{1,0:T(8,128)S(1)}, u32[]{:S(2)}, u32[]{:S(2)}) collective-permute-start(f32[16,1024]{1,0:T(8,128)S(1)} %dynamic-slice_add_fusion.1), channel_id=1, source_target_pairs={{0,2},{1,3},{2,0},{3,1},{4,6},{5,7},{6,4},{7,5},{8,10},{9,11},{10,... | collective-permute-start | bytes 196616 | tf_op jit(solution)/shard_map/ppermute | solution.py:68
  75.9 4.6 %collective-permute-start.18 = (f32[16,1024]{1,0:T(8,128)S(1)}, f32[16,1024]{1,0:T(8,128)S(1)}, u32[]{:S(2)}, u32[]{:S(2)}) collective-permute-start(f32[16,1024]{1,0:T(8,128)S(1)} %add_add_fusion), channel_id=1, source_target_pairs={{0,8},{1,9},{2,10},{3,11},{4,12},{5,13},{6,14},{7,15},{8,0},{9,1},... | collective-permute-start | bytes 196616 | tf_op jit(solution)/shard_map/ppermute | solution.py:68
  80.5 6.6 %collective-permute-start.19 = (f32[16,1024]{1,0:T(8,128)S(1)}, f32[16,1024]{1,0:T(8,128)S(1)}, u32[]{:S(2)}, u32[]{:S(2)}) collective-permute-start(f32[16,1024]{1,0:T(8,128)S(1)} %add.169), channel_id=1, source_target_pairs={{0,16},{1,17},{2,18},{3,19},{4,20},{5,21},{6,22},{7,23},{8,24},{9,... | collective-permute-start | bytes 196616 | tf_op jit(solution)/shard_map/ppermute | solution.py:68
  87.1 15.5 %copy-start.11 = (f32[400,128]{1,0:T(8,128)S(1)}, f32[400,128]{1,0:T(8,128)}, u32[]{:S(2)}) copy-start(f32[400,128]{1,0:T(8,128)} %param.22) | copy-start | bytes 614404
  87.1 1.3 %collective-permute-start.20 = (f32[16,1024]{1,0:T(8,128)S(1)}, f32[16,1024]{1,0:T(8,128)S(1)}, u32[]{:S(2)}, u32[]{:S(2)}) collective-permute-start(f32[16,1024]{1,0:T(8,128)S(1)} %get-tuple-element.16), channel_id=1, source_target_pairs={{0,1},{1,0},{2,3},{3,2},{4,5},{5,4},{6,7},{7,6},{8,9},{9,8},{10,11... | collective-permute-start | bytes 196616 | tf_op jit(solution)/shard_map/ppermute | solution.py:68
  87.2 15.3 %collective-permute-start.24 = (f32[1,400,128]{2,1,0:T(8,128)S(1)}, f32[1,400,128]{2,1,0:T(8,128)S(1)}, u32[]{:S(2)}, u32[]{:S(2)}) collective-permute-start(f32[1,400,128]{2,1,0:T(8,128)S(1)} %constant_dynamic-slice_fusion), channel_id=1, source_target_pairs={{0,16},{8,24},{16,0},{24,8},{1,17},{9,25},{17,1},{25,9},{2,18},{10... | collective-permute-start | bytes 614408 | tf_op jit(solution)/shard_map/ppermute | solution.py:114
  96.4 4.9 %collective-permute-start.21 = (f32[32,384]{1,0:T(8,128)S(1)}, f32[32,384]{1,0:T(8,128)S(1)}, u32[]{:S(2)}, u32[]{:S(2)}) collective-permute-start(f32[32,384]{1,0:T(8,128)S(1)} %fusion.59), channel_id=1, source_target_pairs={{0,8},{8,0},{16,24},{24,16},{1,9},{9,1},{17,25},{25,17},{2,10},{10... | collective-permute-start | bytes 147464 | tf_op jit(solution)/shard_map/ppermute | solution.py:25
  101.2 5.1 %collective-permute-start.22 = (f32[32,384]{1,0:T(8,128)S(1)}, f32[32,384]{1,0:T(8,128)S(1)}, u32[]{:S(2)}, u32[]{:S(2)}) collective-permute-start(f32[32,384]{1,0:T(8,128)S(1)} %add.171), channel_id=1, source_target_pairs={{0,16},{8,24},{16,0},{24,8},{1,17},{9,25},{17,1},{25,9},{2,18},{10... | collective-permute-start | bytes 147464 | tf_op jit(solution)/shard_map/ppermute | solution.py:25
  107.1 1.2 copy-start.9
  107.1 1.2 copy-start.10

commit v17 on v16

--- a/solution.py
+++ b/solution.py
@@ -183,8 +183,8 @@
             combined = combined + second
             late = None
         left_rows = split_tree_sum(partial_left, ("rep", "tp")) / replicas
-        gram_matrix = jnp.dot(left_rows, left_rows.T, precision=highest)
-        factor_low = jnp.linalg.cholesky(gram_matrix)
+        gram_matrix = jnp.dot(left_rows, left_rows.T, precision=high)
+        factor_low = lax.linalg.cholesky(gram_matrix, symmetrize_input=False)
         left_rows = jax.scipy.linalg.solve_triangular(factor_low, left_rows, lower=True)
         partial_right = jnp.dot(left_rows, combined, precision=high)
         right_rows = tree_sum(partial_right, "rep") / replicas

time: 129 us -> 128 us (level)
  no operation moved by 1% of the time
where the time goes in v17:
time: 128 us; the launch traced here: 127 us
  waiting for transfers between devices  41.4 us (32%)
  starting transfers between devices  33.4 us (26%)
  other arithmetic  19.3 us (15%)
  blocking collectives  17.9 us (14%)
  matrix products  10.8 us (8%)
  local copies, waits for them, and re-layouts  3.62 us (3%)
    ppermute x14, waiting for transfers between devices, exchange(): return lax.ppermute(piece, axes, [(i, i ^ stride) for i in range(count)])  22 us
    all_gather x1, blocking collectives, shards(): lax.all_gather(master_new.astype(jnp.bfloat16), 'rep', axis=0, tiled=True)  17.9 us
    ppermute x14, starting transfers between devices, exchange(): return lax.ppermute(piece, axes, [(i, i ^ stride) for i in range(count)])  15.3 us
    ppermute x5, waiting for transfers between devices, exchange(): return lax.ppermute(value, axis, [(i, i ^ stride) for i in range(count)])  12 us
    ppermute x5, starting transfers between devices, exchange(): return lax.ppermute(value, axis, [(i, i ^ stride) for i in range(count)])  7.91 us
    ppermute x4, starting transfers between devices, tree_sum(): value = value + lax.ppermute(value, axes, pairs)  7.43 us
    ppermute x4, waiting for transfers between devices, tree_sum(): value = value + lax.ppermute(value, axes, pairs)  7.38 us
    another operation x6, other arithmetic, shards(): factor_low = lax.linalg.cholesky(gram_matrix, symmetrize_input=False)  7.18 us
  transfers between devices with their start and end apart: 25, of which 19 were waited for; matrix products, arithmetic and copies ran while one was open for 14% of the time, Pallas kernels for 0%

profile of v17, /device:TPU:0, one launch (start us, length us, event | category | flops | bytes accessed | tf_op | source)
XLA Modules:
  0.0 127.4 jit_solution(15978140203823647116)
XLA Ops:
  0.7 3.0 %collective-permute-start = (bf16[192,1024]{1,0:T(8,128)(2,1)}, bf16[192,1024]{1,0:T(8,128)(2,1)S(1)}, u32[]{:S(2)}, u32[]{:S(2)}) collective-permute-start(bf16[192,1024]{1,0:T(8,128)(2,1)} %param.13), channel_id=1, source_target_pairs={{0,2},{1,3},{2,0},{3,1},{4,6},{5,7},{6,4},{7,5},{8,10},{9,11},{10,... | collective-permute-start | bytes 1179656 | tf_op jit(solution)/shard_map/ppermute | solution.py:40
  3.7 1.5 %collective-permute-start.1 = (bf16[192,1024]{1,0:T(8,128)(2,1)}, bf16[192,1024]{1,0:T(8,128)(2,1)S(1)}, u32[]{:S(2)}, u32[]{:S(2)}) collective-permute-start(bf16[192,1024]{1,0:T(8,128)(2,1)} %param.13), channel_id=1, source_target_pairs={{0,4},{1,5},{2,6},{3,7},{4,0},{5,1},{6,2},{7,3},{8,12},{9,13},{10,... | collective-permute-start | bytes 1179656 | tf_op jit(solution)/shard_map/ppermute | solution.py:40
  5.2 7.8 %collective-permute-done = bf16[192,1024]{1,0:T(8,128)(2,1)S(1)} collective-permute-done((bf16[192,1024]{1,0:T(8,128)(2,1)}, bf16[192,1024]{1,0:T(8,128)(2,1)S(1)}, u32[]{:S(2)}, u32[]{:S(2)}) %collective-permute-start) | collective-permute-done | bytes 393248 | tf_op jit(solution)/shard_map/ppermute | solution.py:40
  13.0 1.8 %collective-permute-start.3 = (bf16[96,1024]{1,0:T(8,128)(2,1)S(1)}, bf16[96,1024]{1,0:T(8,128)(2,1)S(1)}, u32[]{:S(2)}, u32[]{:S(2)}) collective-permute-start(bf16[96,1024]{1,0:T(8,128)(2,1)S(1)} %slice.15), channel_id=1, source_target_pairs={{0,4},{1,5},{2,6},{3,7},{4,0},{5,1},{6,2},{7,3},{8,12},{9,13},{10,... | collective-permute-start | bytes 589832 | tf_op jit(solution)/shard_map/ppermute | solution.py:40
  14.9 1.6 %collective-permute-start.2 = (bf16[96,1024]{1,0:T(8,128)(2,1)S(1)}, bf16[96,1024]{1,0:T(8,128)(2,1)S(1)}, u32[]{:S(2)}, u32[]{:S(2)}) collective-permute-start(bf16[96,1024]{1,0:T(8,128)(2,1)S(1)} %slice.14), channel_id=1, source_target_pairs={{0,2},{1,3},{2,0},{3,1},{4,6},{5,7},{6,4},{7,5},{8,10},{9,11},{10,... | collective-permute-start | bytes 589832 | tf_op jit(solution)/shard_map/ppermute | solution.py:40
  16.4 2.7 %collective-permute-done.3 = bf16[96,1024]{1,0:T(8,128)(2,1)S(1)} collective-permute-done((bf16[96,1024]{1,0:T(8,128)(2,1)S(1)}, bf16[96,1024]{1,0:T(8,128)(2,1)S(1)}, u32[]{:S(2)}, u32[]{:S(2)}) %collective-permute-start.3) | collective-permute-done | bytes 196640 | tf_op jit(solution)/shard_map/ppermute | solution.py:40
  19.2 1.4 %collective-permute-done.2 = bf16[96,1024]{1,0:T(8,128)(2,1)S(1)} collective-permute-done((bf16[96,1024]{1,0:T(8,128)(2,1)S(1)}, bf16[96,1024]{1,0:T(8,128)(2,1)S(1)}, u32[]{:S(2)}, u32[]{:S(2)}) %collective-permute-start.2) | collective-permute-done | bytes 196640 | tf_op jit(solution)/shard_map/ppermute | solution.py:40
  21.4 1.6 %constant_dynamic-slice_fusion.6 = (bf16[1,192,384]{2,1,0:T(8,128)(2,1)S(1)}, bf16[1,192,384]{2,1,0:T(8,128)(2,1)S(1)}, bf16[1,192,384]{2,1,0:T(8,128)(2,1)S(1)}...) fusion(bf16[8,192,384]{2,1,0:T(8,128)(2,1)} %bitcast.53, ...), kind=kLoop, calls=%fused_computation.79 | loop fusion | bytes 2359328 | tf_op jit(solution)/shard_map/dynamic_slice | solution.py:53
  23.5 1.0 convert_add_fusion
  25.3 1.0 bitcast_add_fusion
  27.8 0.9 collective-permute-done.5
  28.8 1.2 collective-permute-start.7
  29.9 1.8 %collective-permute-start.8 = (f32[16,1024]{1,0:T(8,128)S(1)}, f32[16,1024]{1,0:T(8,128)S(1)}, u32[]{:S(2)}, u32[]{:S(2)}) collective-permute-start(f32[16,1024]{1,0:T(8,128)S(1)} %dynamic-slice_add_fusion.2), channel_id=1, source_target_pairs={{0,6},{1,7},{2,4},{3,5},{4,2},{5,3},{6,0},{7,1},{8,14},{9,15},{10,... | collective-permute-start | bytes 196616 | tf_op jit(solution)/shard_map/ppermute | solution.py:68
  32.3 0.9 collective-permute-done.7
  33.2 2.4 %collective-permute-done.8 = f32[16,1024]{1,0:T(8,128)S(1)} collective-permute-done((f32[16,1024]{1,0:T(8,128)S(1)}, f32[16,1024]{1,0:T(8,128)S(1)}, u32[]{:S(2)}, u32[]{:S(2)}) %collective-permute-start.8) | collective-permute-done | bytes 65568 | tf_op jit(solution)/shard_map/ppermute | solution.py:68
  36.1 1.6 %collective-permute-start.9 = (f32[16,1024]{1,0:T(8,128)S(1)}, f32[16,1024]{1,0:T(8,128)S(1)}, u32[]{:S(2)}, u32[]{:S(2)}) collective-permute-start(f32[16,1024]{1,0:T(8,128)S(1)} %add_add_fusion.1), channel_id=1, source_target_pairs={{0,8},{1,9},{2,10},{3,11},{4,12},{5,13},{6,14},{7,15},{8,0},{9,1},... | collective-permute-start | bytes 196616 | tf_op jit(solution)/shard_map/ppermute | solution.py:68
  37.7 2.7 %collective-permute-done.9 = f32[16,1024]{1,0:T(8,128)S(1)} collective-permute-done((f32[16,1024]{1,0:T(8,128)S(1)}, f32[16,1024]{1,0:T(8,128)S(1)}, u32[]{:S(2)}, u32[]{:S(2)}) %collective-permute-start.9) | collective-permute-done | bytes 65568 | tf_op jit(solution)/shard_map/ppermute | solution.py:68
  40.4 2.6 %collective-permute-start.10 = (f32[16,1024]{1,0:T(8,128)S(1)}, f32[16,1024]{1,0:T(8,128)S(1)}, u32[]{:S(2)}, u32[]{:S(2)}) collective-permute-start(f32[16,1024]{1,0:T(8,128)S(1)} %add.157), channel_id=1, source_target_pairs={{0,16},{1,17},{2,18},{3,19},{4,20},{5,21},{6,22},{7,23},{8,24},{9,... | collective-permute-start | bytes 196616 | tf_op jit(solution)/shard_map/ppermute | solution.py:68
  43.1 2.6 %collective-permute-done.10 = f32[16,1024]{1,0:T(8,128)S(1)} collective-permute-done((f32[16,1024]{1,0:T(8,128)S(1)}, f32[16,1024]{1,0:T(8,128)S(1)}, u32[]{:S(2)}, u32[]{:S(2)}) %collective-permute-start.10) | collective-permute-done | bytes 65568 | tf_op jit(solution)/shard_map/ppermute | solution.py:68
  45.8 1.2 collective-permute-done.11
  47.2 2.9 %custom-call.8 = f32[32,32]{1,0:T(8,128)S(1)} custom-call(f32[32,32]{1,0:T(8,128)S(1)} %fusion.29), custom_call_target="Cholesky" | custom-call | tf_op jit(solution)/shard_map/cholesky/custom-call.1 | solution.py:187
  51.5 2.4 %custom-call.9 = f32[1,32,32]{1,2,0:T(8,128)S(1)} custom-call(f32[1,32,32]{2,1,0:T(8,128)S(1)} %fusion.41), custom_call_target="InvertDiagBlocksLowerTriangular" | custom-call | tf_op jit(solution)/shard_map/jit(_solve_triangular)/triangular_solve | solution.py:188
  54.8 1.6 %collective-permute-start.12 = (f32[32,384]{1,0:T(8,128)S(1)}, f32[32,384]{1,0:T(8,128)S(1)}, u32[]{:S(2)}, u32[]{:S(2)}) collective-permute-start(f32[32,384]{1,0:T(8,128)S(1)} %fusion.56), channel_id=1, source_target_pairs={{0,8},{8,0},{16,24},{24,16},{1,9},{9,1},{17,25},{25,17},{2,10},{10... | collective-permute-start | bytes 147464 | tf_op jit(solution)/shard_map/ppermute | solution.py:25
  56.4 1.1 select_reduce_fusion
  57.5 1.4 %collective-permute-done.12 = f32[32,384]{1,0:T(8,128)S(1)} collective-permute-done((f32[32,384]{1,0:T(8,128)S(1)}, f32[32,384]{1,0:T(8,128)S(1)}, u32[]{:S(2)}, u32[]{:S(2)}) %collective-permute-start.12) | collective-permute-done | bytes 49184 | tf_op jit(solution)/shard_map/ppermute | solution.py:25
  59.0 2.8 %collective-permute-start.13 = (f32[32,384]{1,0:T(8,128)S(1)}, f32[32,384]{1,0:T(8,128)S(1)}, u32[]{:S(2)}, u32[]{:S(2)}) collective-permute-start(f32[32,384]{1,0:T(8,128)S(1)} %add.159), channel_id=1, source_target_pairs={{0,16},{8,24},{16,0},{24,8},{1,17},{9,25},{17,1},{25,9},{2,18},{10... | collective-permute-start | bytes 147464 | tf_op jit(solution)/shard_map/ppermute | solution.py:25
  61.8 3.1 %fusion = f32[1600,128]{1,0:T(8,128)S(1)} fusion(bf16[1536,128]{1,0:T(8,128)(2,1)S(1)} %copy-done, s32[1536]{0:T(1024)S(1)} %select_reduce_fusion), kind=kOutput, calls=%fused_computation.1 | convolution fusion | flops 631603200 | bytes 1218560 | tf_op jit(solution)/shard_map/dot_general | solution.py:102
  64.9 0.8 fusion.35
  65.8 2.1 %collective-permute-start.23 = (f32[2,400,128]{2,1,0:T(8,128)S(1)}, f32[2,400,128]{2,1,0:T(8,128)}, u32[]{:S(2)}, u32[]{:S(2)}) collective-permute-start(f32[2,400,128]{2,1,0:T(8,128)S(1)} %dynamic-slice_bitcast_fusion), channel_id=1, source_target_pairs={{0,8},{8,0},{16,24},{24,16},{1,9},{9,1},{17,25},{25,17},{2,10},{10... | collective-permute-start | bytes 1228808 | tf_op jit(solution)/shard_map/ppermute | solution.py:114
  67.9 0.9 collective-permute-start.16
  68.9 1.8 %collective-permute-start.17 = (f32[16,1024]{1,0:T(8,128)S(1)}, f32[16,1024]{1,0:T(8,128)S(1)}, u32[]{:S(2)}, u32[]{:S(2)}) collective-permute-start(f32[16,1024]{1,0:T(8,128)S(1)} %dynamic-slice_add_fusion.1), channel_id=1, source_target_pairs={{0,6},{1,7},{2,4},{3,5},{4,2},{5,3},{6,0},{7,1},{8,14},{9,15},{10,... | collective-permute-start | bytes 196616 | tf_op jit(solution)/shard_map/ppermute | solution.py:68
  72.3 2.2 %collective-permute-done.17 = f32[16,1024]{1,0:T(8,128)S(1)} collective-permute-done((f32[16,1024]{1,0:T(8,128)S(1)}, f32[16,1024]{1,0:T(8,128)S(1)}, u32[]{:S(2)}, u32[]{:S(2)}) %collective-permute-start.17) | collective-permute-done | bytes 65568 | tf_op jit(solution)/shard_map/ppermute | solution.py:68
  75.0 1.1 collective-permute-start.18
  76.2 3.3 %collective-permute-done.18 = f32[16,1024]{1,0:T(8,128)S(1)} collective-permute-done((f32[16,1024]{1,0:T(8,128)S(1)}, f32[16,1024]{1,0:T(8,128)S(1)}, u32[]{:S(2)}, u32[]{:S(2)}) %collective-permute-start.18) | collective-permute-done | bytes 65568 | tf_op jit(solution)/shard_map/ppermute | solution.py:68
  79.5 1.9 %collective-permute-start.19 = (f32[16,1024]{1,0:T(8,128)S(1)}, f32[16,1024]{1,0:T(8,128)S(1)}, u32[]{:S(2)}, u32[]{:S(2)}) collective-permute-start(f32[16,1024]{1,0:T(8,128)S(1)} %add.165), channel_id=1, source_target_pairs={{0,16},{1,17},{2,18},{3,19},{4,20},{5,21},{6,22},{7,23},{8,24},{9,... | collective-permute-start | bytes 196616 | tf_op jit(solution)/shard_map/ppermute | solution.py:68
  81.4 1.0 bitcast_add_fusion.1
  82.5 3.6 %collective-permute-done.19 = f32[16,1024]{1,0:T(8,128)S(1)} collective-permute-done((f32[16,1024]{1,0:T(8,128)S(1)}, f32[16,1024]{1,0:T(8,128)S(1)}, u32[]{:S(2)}, u32[]{:S(2)}) %collective-permute-start.19) | collective-permute-done | bytes 65568 | tf_op jit(solution)/shard_map/ppermute | solution.py:68
  87.8 2.9 %custom-call.10 = f32[32,32]{1,0:T(8,128)S(1)} custom-call(f32[32,32]{1,0:T(8,128)S(1)} %fusion.25), custom_call_target="Cholesky" | custom-call | tf_op jit(solution)/shard_map/cholesky/custom-call.1 | solution.py:187
  92.0 2.4 %custom-call.11 = f32[1,32,32]{1,2,0:T(8,128)S(1)} custom-call(f32[1,32,32]{2,1,0:T(8,128)S(1)} %fusion.42), custom_call_target="InvertDiagBlocksLowerTriangular" | custom-call | tf_op jit(solution)/shard_map/jit(_solve_triangular)/triangular_solve | solution.py:188
  95.4 1.6 %collective-permute-start.21 = (f32[32,384]{1,0:T(8,128)S(1)}, f32[32,384]{1,0:T(8,128)S(1)}, u32[]{:S(2)}, u32[]{:S(2)}) collective-permute-start(f32[32,384]{1,0:T(8,128)S(1)} %fusion.57), channel_id=1, source_target_pairs={{0,8},{8,0},{16,24},{24,16},{1,9},{9,1},{17,25},{25,17},{2,10},{10... | collective-permute-start | bytes 147464 | tf_op jit(solution)/shard_map/ppermute | solution.py:25
  97.0 3.0 %collective-permute-done.21 = f32[32,384]{1,0:T(8,128)S(1)} collective-permute-done((f32[32,384]{1,0:T(8,128)S(1)}, f32[32,384]{1,0:T(8,128)S(1)}, u32[]{:S(2)}, u32[]{:S(2)}) %collective-permute-start.21) | collective-permute-done | bytes 49184 | tf_op jit(solution)/shard_map/ppermute | solution.py:25
  100.0 1.4 %collective-permute-start.22 = (f32[32,384]{1,0:T(8,128)S(1)}, f32[32,384]{1,0:T(8,128)S(1)}, u32[]{:S(2)}, u32[]{:S(2)}) collective-permute-start(f32[32,384]{1,0:T(8,128)S(1)} %add.167), channel_id=1, source_target_pairs={{0,16},{8,24},{16,0},{24,8},{1,17},{9,25},{17,1},{25,9},{2,18},{10... | collective-permute-start | bytes 147464 | tf_op jit(solution)/shard_map/ppermute | solution.py:25
  102.1 3.0 %collective-permute-done.22 = f32[32,384]{1,0:T(8,128)S(1)} collective-permute-done((f32[32,384]{1,0:T(8,128)S(1)}, f32[32,384]{1,0:T(8,128)S(1)}, u32[]{:S(2)}, u32[]{:S(2)}) %collective-permute-start.22) | collective-permute-done | bytes 49184 | tf_op jit(solution)/shard_map/ppermute | solution.py:25
  105.1 0.8 fusion.40
  105.9 1.1 fusion.7
  107.1 1.0 fusion.55
  108.0 17.9 %all_gather.3 = bf16[1024,384]{1,0:T(8,128)(2,1)S(1)} all-gather(bf16[256,384]{1,0:T(8,128)(2,1)S(1)} %get-tuple-element.12), channel_id=1, replica_groups=mesh['rep'=4,'tp'=8] {'rep'}, dimensions={0}, use_global_device_ids=true | all-gather | bytes 983040 | tf_op jit(solution)/shard_map/all_gather | solution.py:202
  126.5 0.9 copy.21
  (89 shorter events, 14.5 us)
Async XLA Ops:
  0.6 61.1 %copy-start = (bf16[1536,128]{1,0:T(8,128)(2,1)S(1)}, bf16[1536,128]{1,0:T(8,128)(2,1)}, u32[]{:S(2)}) copy-start(bf16[1536,128]{1,0:T(8,128)(2,1)} %param.19) | copy-start | bytes 1179652
  0.6 20.0 %copy-start.7 = (bf16[192,1024]{1,0:T(8,128)(2,1)S(1)}, bf16[192,1024]{1,0:T(8,128)(2,1)}, u32[]{:S(2)}) copy-start(bf16[192,1024]{1,0:T(8,128)(2,1)} %param.13) | copy-start | bytes 1179652
  0.7 12.3 %collective-permute-start = (bf16[192,1024]{1,0:T(8,128)(2,1)}, bf16[192,1024]{1,0:T(8,128)(2,1)S(1)}, u32[]{:S(2)}, u32[]{:S(2)}) collective-permute-start(bf16[192,1024]{1,0:T(8,128)(2,1)} %param.13), channel_id=1, source_target_pairs={{0,2},{1,3},{2,0},{3,1},{4,6},{5,7},{6,4},{7,5},{8,10},{9,11},{10,... | collective-permute-start | bytes 1179656 | tf_op jit(solution)/shard_map/ppermute | solution.py:40
  3.7 11.2 %collective-permute-start.1 = (bf16[192,1024]{1,0:T(8,128)(2,1)}, bf16[192,1024]{1,0:T(8,128)(2,1)S(1)}, u32[]{:S(2)}, u32[]{:S(2)}) collective-permute-start(bf16[192,1024]{1,0:T(8,128)(2,1)} %param.13), channel_id=1, source_target_pairs={{0,4},{1,5},{2,6},{3,7},{4,0},{5,1},{6,2},{7,3},{8,12},{9,13},{10,... | collective-permute-start | bytes 1179656 | tf_op jit(solution)/shard_map/ppermute | solution.py:40
  13.0 7.9 %copy-start.3 = (bf16[192,1024]{1,0:T(8,128)(2,1)}, bf16[192,1024]{1,0:T(8,128)(2,1)S(1)}, u32[]{:S(2)}) copy-start(bf16[192,1024]{1,0:T(8,128)(2,1)S(1)} %collective-permute-done) | copy-start | bytes 1179652
  13.0 6.2 %collective-permute-start.3 = (bf16[96,1024]{1,0:T(8,128)(2,1)S(1)}, bf16[96,1024]{1,0:T(8,128)(2,1)S(1)}, u32[]{:S(2)}, u32[]{:S(2)}) collective-permute-start(bf16[96,1024]{1,0:T(8,128)(2,1)S(1)} %slice.15), channel_id=1, source_target_pairs={{0,4},{1,5},{2,6},{3,7},{4,0},{5,1},{6,2},{7,3},{8,12},{9,13},{10,... | collective-permute-start | bytes 589832 | tf_op jit(solution)/shard_map/ppermute | solution.py:40
  14.8 6.0 %copy-start.5 = (bf16[192,1024]{1,0:T(8,128)(2,1)}, bf16[192,1024]{1,0:T(8,128)(2,1)S(1)}, u32[]{:S(2)}) copy-start(bf16[192,1024]{1,0:T(8,128)(2,1)S(1)} %collective-permute-done.1) | copy-start | bytes 1179652
  14.9 5.7 %collective-permute-start.2 = (bf16[96,1024]{1,0:T(8,128)(2,1)S(1)}, bf16[96,1024]{1,0:T(8,128)(2,1)S(1)}, u32[]{:S(2)}, u32[]{:S(2)}) collective-permute-start(bf16[96,1024]{1,0:T(8,128)(2,1)S(1)} %slice.14), channel_id=1, source_target_pairs={{0,2},{1,3},{2,0},{3,1},{4,6},{5,7},{6,4},{7,5},{8,10},{9,11},{10,... | collective-permute-start | bytes 589832 | tf_op jit(solution)/shard_map/ppermute | solution.py:40
  20.6 0.7 copy-start.1
  21.4 4.0 %collective-permute-start.4 = (bf16[4,192,1024]{2,1,0:T(8,128)(2,1)S(1)}, bf16[4,192,1024]{2,1,0:T(8,128)(2,1)S(1)}, u32[]{:S(2)}, u32[]{:S(2)}) collective-permute-start(bf16[4,192,1024]{2,1,0:T(8,128)(2,1)S(1)} %pad_maximum_fusion), channel_id=1, source_target_pairs={{0,1},{1,0},{2,3},{3,2},{4,5},{5,4},{6,7},{7,6},{8,9},{9,8},{10,11... | collective-permute-start | bytes 4718600 | tf_op jit(solution)/shard_map/ppermute | solution.py:40
  21.4 1.7 %copy-start.2 = (bf16[1,192,1024]{2,1,0:T(8,128)(2,1)S(1)}, bf16[1,192,1024]{2,1,0:T(8,128)(2,1)}, u32[]{:S(2)}) copy-start(bf16[1,192,1024]{2,1,0:T(8,128)(2,1)} %copy-done.1) | copy-start | bytes 1179652
  21.4 1.7 %copy-start.4 = (bf16[192,1024]{1,0:T(8,128)(2,1)S(1)}, bf16[192,1024]{1,0:T(8,128)(2,1)}, u32[]{:S(2)}) copy-start(bf16[192,1024]{1,0:T(8,128)(2,1)} %copy-done.3) | copy-start | bytes 1179652
  21.4 1.7 %copy-start.6 = (bf16[192,1024]{1,0:T(8,128)(2,1)S(1)}, bf16[192,1024]{1,0:T(8,128)(2,1)}, u32[]{:S(2)}) copy-start(bf16[192,1024]{1,0:T(8,128)(2,1)} %copy-done.5) | copy-start | bytes 1179652
  21.4 1.8 %copy-start.8 = (bf16[192,1024]{1,0:T(8,128)(2,1)S(1)}, bf16[192,1024]{1,0:T(8,128)(2,1)}, u32[]{:S(2)}) copy-start(bf16[192,1024]{1,0:T(8,128)(2,1)} %param.13) | copy-start | bytes 1179652
  21.4 2.1 %copy-start.13 = (bf16[1,1024,384]{2,1,0:T(8,128)(2,1)S(1)}, bf16[1,1024,384]{2,1,0:T(8,128)(2,1)}, u32[]{:S(2)}) copy-start(bf16[1,1024,384]{2,1,0:T(8,128)(2,1)} %param.15) | copy-start | bytes 2359300
  23.5 1.0 copy-start.12
  27.3 1.5 %collective-permute-start.5 = (f32[16,1024]{1,0:T(8,128)S(1)}, f32[16,1024]{1,0:T(8,128)S(1)}, u32[]{:S(2)}, u32[]{:S(2)}) collective-permute-start(f32[16,1024]{1,0:T(8,128)S(1)} %constant_dynamic-slice_fusion.2), channel_id=1, source_target_pairs={{0,1},{1,0},{2,3},{3,2},{4,5},{5,4},{6,7},{7,6},{8,9},{9,8},{10,11... | collective-permute-start | bytes 196616 | tf_op jit(solution)/shard_map/ppermute | solution.py:68
  28.7 27.7 %copy-start.14 = (s32[1600]{0:T(1024)S(1)}, s32[1600]{0:T(1024)}, u32[]{:S(2)}) copy-start(s32[1600]{0:T(1024)} %param.21) | copy-start | bytes 19204
  28.7 27.7 %copy-start.15 = (s32[1536]{0:T(1024)S(1)}, s32[1536]{0:T(1024)}, u32[]{:S(2)}) copy-start(s32[1536]{0:T(1024)} %param.20) | copy-start | bytes 18436
  28.8 4.4 %collective-permute-start.7 = (f32[16,1024]{1,0:T(8,128)S(1)}, f32[16,1024]{1,0:T(8,128)S(1)}, u32[]{:S(2)}, u32[]{:S(2)}) collective-permute-start(f32[16,1024]{1,0:T(8,128)S(1)} %dynamic-slice_add_fusion.2), channel_id=1, source_target_pairs={{0,4},{1,5},{2,6},{3,7},{4,0},{5,1},{6,2},{7,3},{8,12},{9,13},{10,... | collective-permute-start | bytes 196616 | tf_op jit(solution)/shard_map/ppermute | solution.py:68
  29.9 5.7 %collective-permute-start.8 = (f32[16,1024]{1,0:T(8,128)S(1)}, f32[16,1024]{1,0:T(8,128)S(1)}, u32[]{:S(2)}, u32[]{:S(2)}) collective-permute-start(f32[16,1024]{1,0:T(8,128)S(1)} %dynamic-slice_add_fusion.2), channel_id=1, source_target_pairs={{0,6},{1,7},{2,4},{3,5},{4,2},{5,3},{6,0},{7,1},{8,14},{9,15},{10,... | collective-permute-start | bytes 196616 | tf_op jit(solution)/shard_map/ppermute | solution.py:68
  31.8 4.3 %collective-permute-start.6 = (f32[16,1024]{1,0:T(8,128)S(1)}, f32[16,1024]{1,0:T(8,128)S(1)}, u32[]{:S(2)}, u32[]{:S(2)}) collective-permute-start(f32[16,1024]{1,0:T(8,128)S(1)} %dynamic-slice_add_fusion.2), channel_id=1, source_target_pairs={{0,2},{1,3},{2,0},{3,1},{4,6},{5,7},{6,4},{7,5},{8,10},{9,11},{10,... | collective-permute-start | bytes 196616 | tf_op jit(solution)/shard_map/ppermute | solution.py:68
  36.1 4.3 %collective-permute-start.9 = (f32[16,1024]{1,0:T(8,128)S(1)}, f32[16,1024]{1,0:T(8,128)S(1)}, u32[]{:S(2)}, u32[]{:S(2)}) collective-permute-start(f32[16,1024]{1,0:T(8,128)S(1)} %add_add_fusion.1), channel_id=1, source_target_pairs={{0,8},{1,9},{2,10},{3,11},{4,12},{5,13},{6,14},{7,15},{8,0},{9,1},... | collective-permute-start | bytes 196616 | tf_op jit(solution)/shard_map/ppermute | solution.py:68
  40.4 5.2 %collective-permute-start.10 = (f32[16,1024]{1,0:T(8,128)S(1)}, f32[16,1024]{1,0:T(8,128)S(1)}, u32[]{:S(2)}, u32[]{:S(2)}) collective-permute-start(f32[16,1024]{1,0:T(8,128)S(1)} %add.157), channel_id=1, source_target_pairs={{0,16},{1,17},{2,18},{3,19},{4,20},{5,21},{6,22},{7,23},{8,24},{9,... | collective-permute-start | bytes 196616 | tf_op jit(solution)/shard_map/ppermute | solution.py:68
  45.7 1.3 %collective-permute-start.11 = (f32[16,1024]{1,0:T(8,128)S(1)}, f32[16,1024]{1,0:T(8,128)S(1)}, u32[]{:S(2)}, u32[]{:S(2)}) collective-permute-start(f32[16,1024]{1,0:T(8,128)S(1)} %get-tuple-element.18), channel_id=1, source_target_pairs={{0,1},{1,0},{2,3},{3,2},{4,5},{5,4},{6,7},{7,6},{8,9},{9,8},{10,11... | collective-permute-start | bytes 196616 | tf_op jit(solution)/shard_map/ppermute | solution.py:68
  54.8 4.2 %collective-permute-start.12 = (f32[32,384]{1,0:T(8,128)S(1)}, f32[32,384]{1,0:T(8,128)S(1)}, u32[]{:S(2)}, u32[]{:S(2)}) collective-permute-start(f32[32,384]{1,0:T(8,128)S(1)} %fusion.56), channel_id=1, source_target_pairs={{0,8},{8,0},{16,24},{24,16},{1,9},{9,1},{17,25},{25,17},{2,10},{10... | collective-permute-start | bytes 147464 | tf_op jit(solution)/shard_map/ppermute | solution.py:25
  59.0 5.9 %collective-permute-start.13 = (f32[32,384]{1,0:T(8,128)S(1)}, f32[32,384]{1,0:T(8,128)S(1)}, u32[]{:S(2)}, u32[]{:S(2)}) collective-permute-start(f32[32,384]{1,0:T(8,128)S(1)} %add.159), channel_id=1, source_target_pairs={{0,16},{8,24},{16,0},{24,8},{1,17},{9,25},{17,1},{25,9},{2,18},{10... | collective-permute-start | bytes 147464 | tf_op jit(solution)/shard_map/ppermute | solution.py:25
  65.7 2.2 %collective-permute-start.14 = (f32[16,1024]{1,0:T(8,128)S(1)}, f32[16,1024]{1,0:T(8,128)S(1)}, u32[]{:S(2)}, u32[]{:S(2)}) collective-permute-start(f32[16,1024]{1,0:T(8,128)S(1)} %constant_dynamic-slice_fusion.1), channel_id=1, source_target_pairs={{0,1},{1,0},{2,3},{3,2},{4,5},{5,4},{6,7},{7,6},{8,9},{9,8},{10,11... | collective-permute-start | bytes 196616 | tf_op jit(solution)/shard_map/ppermute | solution.py:68
  65.8 15.6 %collective-permute-start.23 = (f32[2,400,128]{2,1,0:T(8,128)S(1)}, f32[2,400,128]{2,1,0:T(8,128)}, u32[]{:S(2)}, u32[]{:S(2)}) collective-permute-start(f32[2,400,128]{2,1,0:T(8,128)S(1)} %dynamic-slice_bitcast_fusion), channel_id=1, source_target_pairs={{0,8},{8,0},{16,24},{24,16},{1,9},{9,1},{17,25},{25,17},{2,10},{10... | collective-permute-start | bytes 1228808 | tf_op jit(solution)/shard_map/ppermute | solution.py:114
  67.9 4.3 %collective-permute-start.16 = (f32[16,1024]{1,0:T(8,128)S(1)}, f32[16,1024]{1,0:T(8,128)S(1)}, u32[]{:S(2)}, u32[]{:S(2)}) collective-permute-start(f32[16,1024]{1,0:T(8,128)S(1)} %dynamic-slice_add_fusion.1), channel_id=1, source_target_pairs={{0,4},{1,5},{2,6},{3,7},{4,0},{5,1},{6,2},{7,3},{8,12},{9,13},{10,... | collective-permute-start | bytes 196616 | tf_op jit(solution)/shard_map/ppermute | solution.py:68
  68.9 5.7 %collective-permute-start.17 = (f32[16,1024]{1,0:T(8,128)S(1)}, f32[16,1024]{1,0:T(8,128)S(1)}, u32[]{:S(2)}, u32[]{:S(2)}) collective-permute-start(f32[16,1024]{1,0:T(8,128)S(1)} %dynamic-slice_add_fusion.1), channel_id=1, source_target_pairs={{0,6},{1,7},{2,4},{3,5},{4,2},{5,3},{6,0},{7,1},{8,14},{9,15},{10,... | collective-permute-start | bytes 196616 | tf_op jit(solution)/shard_map/ppermute | solution.py:68
  70.7 4.3 %collective-permute-start.15 = (f32[16,1024]{1,0:T(8,128)S(1)}, f32[16,1024]{1,0:T(8,128)S(1)}, u32[]{:S(2)}, u32[]{:S(2)}) collective-permute-start(f32[16,1024]{1,0:T(8,128)S(1)} %dynamic-slice_add_fusion.1), channel_id=1, source_target_pairs={{0,2},{1,3},{2,0},{3,1},{4,6},{5,7},{6,4},{7,5},{8,10},{9,11},{10,... | collective-permute-start | bytes 196616 | tf_op jit(solution)/shard_map/ppermute | solution.py:68
  75.0 4.4 %collective-permute-start.18 = (f32[16,1024]{1,0:T(8,128)S(1)}, f32[16,1024]{1,0:T(8,128)S(1)}, u32[]{:S(2)}, u32[]{:S(2)}) collective-permute-start(f32[16,1024]{1,0:T(8,128)S(1)} %add_add_fusion), channel_id=1, source_target_pairs={{0,8},{1,9},{2,10},{3,11},{4,12},{5,13},{6,14},{7,15},{8,0},{9,1},... | collective-permute-start | bytes 196616 | tf_op jit(solution)/shard_map/ppermute | solution.py:68
  79.5 6.5 %collective-permute-start.19 = (f32[16,1024]{1,0:T(8,128)S(1)}, f32[16,1024]{1,0:T(8,128)S(1)}, u32[]{:S(2)}, u32[]{:S(2)}) collective-permute-start(f32[16,1024]{1,0:T(8,128)S(1)} %add.165), channel_id=1, source_target_pairs={{0,16},{1,17},{2,18},{3,19},{4,20},{5,21},{6,22},{7,23},{8,24},{9,... | collective-permute-start | bytes 196616 | tf_op jit(solution)/shard_map/ppermute | solution.py:68
  86.0 15.4 %copy-start.11 = (f32[400,128]{1,0:T(8,128)S(1)}, f32[400,128]{1,0:T(8,128)}, u32[]{:S(2)}) copy-start(f32[400,128]{1,0:T(8,128)} %param.22) | copy-start | bytes 614404
  86.1 1.3 %collective-permute-start.20 = (f32[16,1024]{1,0:T(8,128)S(1)}, f32[16,1024]{1,0:T(8,128)S(1)}, u32[]{:S(2)}, u32[]{:S(2)}) collective-permute-start(f32[16,1024]{1,0:T(8,128)S(1)} %get-tuple-element.16), channel_id=1, source_target_pairs={{0,1},{1,0},{2,3},{3,2},{4,5},{5,4},{6,7},{7,6},{8,9},{9,8},{10,11... | collective-permute-start | bytes 196616 | tf_op jit(solution)/shard_map/ppermute | solution.py:68
  86.2 15.2 %collective-permute-start.24 = (f32[1,400,128]{2,1,0:T(8,128)S(1)}, f32[1,400,128]{2,1,0:T(8,128)S(1)}, u32[]{:S(2)}, u32[]{:S(2)}) collective-permute-start(f32[1,400,128]{2,1,0:T(8,128)S(1)} %constant_dynamic-slice_fusion), channel_id=1, source_target_pairs={{0,16},{8,24},{16,0},{24,8},{1,17},{9,25},{17,1},{25,9},{2,18},{10... | collective-permute-start | bytes 614408 | tf_op jit(solution)/shard_map/ppermute | solution.py:114
  95.4 4.6 %collective-permute-start.21 = (f32[32,384]{1,0:T(8,128)S(1)}, f32[32,384]{1,0:T(8,128)S(1)}, u32[]{:S(2)}, u32[]{:S(2)}) collective-permute-start(f32[32,384]{1,0:T(8,128)S(1)} %fusion.57), channel_id=1, source_target_pairs={{0,8},{8,0},{16,24},{24,16},{1,9},{9,1},{17,25},{25,17},{2,10},{10... | collective-permute-start | bytes 147464 | tf_op jit(solution)/shard_map/ppermute | solution.py:25
  100.0 5.1 %collective-permute-start.22 = (f32[32,384]{1,0:T(8,128)S(1)}, f32[32,384]{1,0:T(8,128)S(1)}, u32[]{:S(2)}, u32[]{:S(2)}) collective-permute-start(f32[32,384]{1,0:T(8,128)S(1)} %add.167), channel_id=1, source_target_pairs={{0,16},{8,24},{16,0},{24,8},{1,17},{9,25},{17,1},{25,9},{2,18},{10... | collective-permute-start | bytes 147464 | tf_op jit(solution)/shard_map/ppermute | solution.py:25
  105.9 1.2 copy-start.9
  105.9 1.2 copy-start.10

commit v18 on v17

--- a/solution.py
+++ b/solution.py
@@ -73,9 +73,10 @@
     given = lax.dynamic_slice_in_dim(value, (1 - core) * half, half, 0)
     kept = kept + exchange(given, 1)
     stride = 2
-    if count >= 8:
-        kept = (kept + exchange(kept, 2)) + (exchange(kept, 4) + exchange(kept, 6))
-        stride = 8
+    while 4 * stride <= count:
+        low, high = stride, 2 * stride
+        kept = (kept + exchange(kept, low)) + (exchange(kept, high) + exchange(kept, low ^ high))
+        stride *= 4
     while stride < count:
         kept = kept + exchange(kept, stride)
         stride *= 2

time: 128 us -> 124 us (0.969)
  starting transfers between devices: 33.4 us -> 30.8 us
    ppermute x14 -> x16, waiting for transfers between devices: 22 us -> 17.6 us  [exchange(): return lax.ppermute(piece, axes, [(i, i ^ stride) for i in range(count)])]
    ppermute x4, waiting for transfers between devices: 7.38 us -> 9.97 us  [tree_sum(): value = value + lax.ppermute(value, axes, pairs)]
    ppermute x4, starting transfers between devices: 7.43 us -> 5 us  [tree_sum(): value = value + lax.ppermute(value, axes, pairs)]
    ppermute x14 -> x16, starting transfers between devices: 15.3 us -> 15.9 us  [exchange(): return lax.ppermute(piece, axes, [(i, i ^ stride) for i in range(count)])]
  transfers between devices with their start and end apart: 25 -> 27, of which waited for: 19 -> 23; matrix products, arithmetic and copies ran while one was open for 14% -> 14% of each run, Pallas kernels for 0% -> 0%
where the time goes in v18:
time: 124 us
  waiting for transfers between devices  40.6 us (33%)
  starting transfers between devices  30.8 us (25%)
  other arithmetic  19.3 us (16%)
  blocking collectives  17.9 us (14%)
  matrix products  10.6 us (9%)
  local copies, waits for them, and re-layouts  3.62 us (3%)
    all_gather x1, blocking collectives, shards(): lax.all_gather(master_new.astype(jnp.bfloat16), 'rep', axis=0, tiled=True)  17.9 us
    ppermute x16, waiting for transfers between devices, exchange(): return lax.ppermute(piece, axes, [(i, i ^ stride) for i in range(count)])  17.6 us
    ppermute x16, starting transfers between devices, exchange(): return lax.ppermute(piece, axes, [(i, i ^ stride) for i in range(count)])  15.9 us
    ppermute x5, waiting for transfers between devices, exchange(): return lax.ppermute(value, axis, [(i, i ^ stride) for i in range(count)])  12 us
    ppermute x4, waiting for transfers between devices, tree_sum(): value = value + lax.ppermute(value, axes, pairs)  9.97 us
    ppermute x5, starting transfers between devices, exchange(): return lax.ppermute(value, axis, [(i, i ^ stride) for i in range(count)])  7.91 us
    another operation x6, other arithmetic, shards(): factor_low = lax.linalg.cholesky(gram_matrix, symmetrize_input=False)  7.18 us
    another operation x4, other arithmetic, shards(): jax.scipy.linalg.solve_triangular(factor_low, left_rows, lower=True)  6.17 us
  transfers between devices with their start and end apart: 27, of which 23 were waited for; matrix products, arithmetic and copies ran while one was open for 14% of the time, Pallas kernels for 0%

profile of v18, /device:TPU:0, one launch (start us, length us, event | category | flops | bytes accessed | tf_op | source)
XLA Modules:
  0.0 123.8 jit_solution(10293157263565034509)
XLA Ops:
  0.7 3.0 %collective-permute-start = (bf16[192,1024]{1,0:T(8,128)(2,1)}, bf16[192,1024]{1,0:T(8,128)(2,1)S(1)}, u32[]{:S(2)}, u32[]{:S(2)}) collective-permute-start(bf16[192,1024]{1,0:T(8,128)(2,1)} %param.13), channel_id=1, source_target_pairs={{0,2},{1,3},{2,0},{3,1},{4,6},{5,7},{6,4},{7,5},{8,10},{9,11},{10,... | collective-permute-start | bytes 1179656 | tf_op jit(solution)/shard_map/ppermute | solution.py:40
  3.7 1.5 %collective-permute-start.1 = (bf16[192,1024]{1,0:T(8,128)(2,1)}, bf16[192,1024]{1,0:T(8,128)(2,1)S(1)}, u32[]{:S(2)}, u32[]{:S(2)}) collective-permute-start(bf16[192,1024]{1,0:T(8,128)(2,1)} %param.13), channel_id=1, source_target_pairs={{0,4},{1,5},{2,6},{3,7},{4,0},{5,1},{6,2},{7,3},{8,12},{9,13},{10,... | collective-permute-start | bytes 1179656 | tf_op jit(solution)/shard_map/ppermute | solution.py:40
  5.2 7.8 %collective-permute-done = bf16[192,1024]{1,0:T(8,128)(2,1)S(1)} collective-permute-done((bf16[192,1024]{1,0:T(8,128)(2,1)}, bf16[192,1024]{1,0:T(8,128)(2,1)S(1)}, u32[]{:S(2)}, u32[]{:S(2)}) %collective-permute-start) | collective-permute-done | bytes 393248 | tf_op jit(solution)/shard_map/ppermute | solution.py:40
  13.0 1.8 %collective-permute-start.3 = (bf16[96,1024]{1,0:T(8,128)(2,1)S(1)}, bf16[96,1024]{1,0:T(8,128)(2,1)S(1)}, u32[]{:S(2)}, u32[]{:S(2)}) collective-permute-start(bf16[96,1024]{1,0:T(8,128)(2,1)S(1)} %slice.15), channel_id=1, source_target_pairs={{0,4},{1,5},{2,6},{3,7},{4,0},{5,1},{6,2},{7,3},{8,12},{9,13},{10,... | collective-permute-start | bytes 589832 | tf_op jit(solution)/shard_map/ppermute | solution.py:40
  14.9 1.6 %collective-permute-start.2 = (bf16[96,1024]{1,0:T(8,128)(2,1)S(1)}, bf16[96,1024]{1,0:T(8,128)(2,1)S(1)}, u32[]{:S(2)}, u32[]{:S(2)}) collective-permute-start(bf16[96,1024]{1,0:T(8,128)(2,1)S(1)} %slice.14), channel_id=1, source_target_pairs={{0,2},{1,3},{2,0},{3,1},{4,6},{5,7},{6,4},{7,5},{8,10},{9,11},{10,... | collective-permute-start | bytes 589832 | tf_op jit(solution)/shard_map/ppermute | solution.py:40
  16.4 2.7 %collective-permute-done.3 = bf16[96,1024]{1,0:T(8,128)(2,1)S(1)} collective-permute-done((bf16[96,1024]{1,0:T(8,128)(2,1)S(1)}, bf16[96,1024]{1,0:T(8,128)(2,1)S(1)}, u32[]{:S(2)}, u32[]{:S(2)}) %collective-permute-start.3) | collective-permute-done | bytes 196640 | tf_op jit(solution)/shard_map/ppermute | solution.py:40
  19.2 1.4 %collective-permute-done.2 = bf16[96,1024]{1,0:T(8,128)(2,1)S(1)} collective-permute-done((bf16[96,1024]{1,0:T(8,128)(2,1)S(1)}, bf16[96,1024]{1,0:T(8,128)(2,1)S(1)}, u32[]{:S(2)}, u32[]{:S(2)}) %collective-permute-start.2) | collective-permute-done | bytes 196640 | tf_op jit(solution)/shard_map/ppermute | solution.py:40
  21.4 1.6 %constant_dynamic-slice_fusion.6 = (bf16[1,192,384]{2,1,0:T(8,128)(2,1)S(1)}, bf16[1,192,384]{2,1,0:T(8,128)(2,1)S(1)}, bf16[1,192,384]{2,1,0:T(8,128)(2,1)S(1)}...) fusion(bf16[8,192,384]{2,1,0:T(8,128)(2,1)} %bitcast.53, ...), kind=kLoop, calls=%fused_computation.81 | loop fusion | bytes 2359328 | tf_op jit(solution)/shard_map/dynamic_slice | solution.py:53
  23.5 1.0 convert_add_fusion
  25.3 1.0 bitcast_add_fusion
  27.8 0.9 collective-permute-done.5
  28.8 1.2 collective-permute-start.7
  29.9 1.8 %collective-permute-start.8 = (f32[16,1024]{1,0:T(8,128)S(1)}, f32[16,1024]{1,0:T(8,128)S(1)}, u32[]{:S(2)}, u32[]{:S(2)}) collective-permute-start(f32[16,1024]{1,0:T(8,128)S(1)} %dynamic-slice_add_fusion.2), channel_id=1, source_target_pairs={{0,6},{1,7},{2,4},{3,5},{4,2},{5,3},{6,0},{7,1},{8,14},{9,15},{10,... | collective-permute-start | bytes 196616 | tf_op jit(solution)/shard_map/ppermute | solution.py:68
  32.3 0.9 collective-permute-done.7
  33.2 2.4 %collective-permute-done.8 = f32[16,1024]{1,0:T(8,128)S(1)} collective-permute-done((f32[16,1024]{1,0:T(8,128)S(1)}, f32[16,1024]{1,0:T(8,128)S(1)}, u32[]{:S(2)}, u32[]{:S(2)}) %collective-permute-start.8) | collective-permute-done | bytes 65568 | tf_op jit(solution)/shard_map/ppermute | solution.py:68
  36.1 2.6 %collective-permute-start.10 = (f32[16,1024]{1,0:T(8,128)S(1)}, f32[16,1024]{1,0:T(8,128)S(1)}, u32[]{:S(2)}, u32[]{:S(2)}) collective-permute-start(f32[16,1024]{1,0:T(8,128)S(1)} %add_add_fusion.3), channel_id=1, source_target_pairs={{0,16},{1,17},{2,18},{3,19},{4,20},{5,21},{6,22},{7,23},{8,24},{9,... | collective-permute-start | bytes 196616 | tf_op jit(solution)/shard_map/ppermute | solution.py:68
  38.7 1.3 %collective-permute-start.11 = (f32[16,1024]{1,0:T(8,128)S(1)}, f32[16,1024]{1,0:T(8,128)S(1)}, u32[]{:S(2)}, u32[]{:S(2)}) collective-permute-start(f32[16,1024]{1,0:T(8,128)S(1)} %add_add_fusion.3), channel_id=1, source_target_pairs={{0,24},{1,25},{2,26},{3,27},{4,28},{5,29},{6,30},{7,31},{8,16},{9,... | collective-permute-start | bytes 196616 | tf_op jit(solution)/shard_map/ppermute | solution.py:68
  40.3 1.1 collective-permute-done.10
  41.4 3.6 %collective-permute-done.11 = f32[16,1024]{1,0:T(8,128)S(1)} collective-permute-done((f32[16,1024]{1,0:T(8,128)S(1)}, f32[16,1024]{1,0:T(8,128)S(1)}, u32[]{:S(2)}, u32[]{:S(2)}) %collective-permute-start.11) | collective-permute-done | bytes 65568 | tf_op jit(solution)/shard_map/ppermute | solution.py:68
  45.2 1.2 %collective-permute-done.12 = f32[16,1024]{1,0:T(8,128)S(1)} collective-permute-done((f32[16,1024]{1,0:T(8,128)S(1)}, f32[16,1024]{1,0:T(8,128)S(1)}, u32[]{:S(2)}, u32[]{:S(2)}) %collective-permute-start.12) | collective-permute-done | bytes 65568 | tf_op jit(solution)/shard_map/ppermute | solution.py:68
  46.6 2.9 %custom-call.8 = f32[32,32]{1,0:T(8,128)S(1)} custom-call(f32[32,32]{1,0:T(8,128)S(1)} %fusion.29), custom_call_target="Cholesky" | custom-call | tf_op jit(solution)/shard_map/cholesky/custom-call.1 | solution.py:188
  50.9 2.4 %custom-call.9 = f32[1,32,32]{1,2,0:T(8,128)S(1)} custom-call(f32[1,32,32]{2,1,0:T(8,128)S(1)} %fusion.41), custom_call_target="InvertDiagBlocksLowerTriangular" | custom-call | tf_op jit(solution)/shard_map/jit(_solve_triangular)/triangular_solve | solution.py:189
  54.5 1.1 select_reduce_fusion
  55.6 2.8 %collective-permute-done.13 = f32[32,384]{1,0:T(8,128)S(1)} collective-permute-done((f32[32,384]{1,0:T(8,128)S(1)}, f32[32,384]{1,0:T(8,128)S(1)}, u32[]{:S(2)}, u32[]{:S(2)}) %collective-permute-start.13) | collective-permute-done | bytes 49184 | tf_op jit(solution)/shard_map/ppermute | solution.py:25
  58.4 2.2 %collective-permute-start.14 = (f32[32,384]{1,0:T(8,128)S(1)}, f32[32,384]{1,0:T(8,128)S(1)}, u32[]{:S(2)}, u32[]{:S(2)}) collective-permute-start(f32[32,384]{1,0:T(8,128)S(1)} %add.166), channel_id=1, source_target_pairs={{0,16},{8,24},{16,0},{24,8},{1,17},{9,25},{17,1},{25,9},{2,18},{10... | collective-permute-start | bytes 147464 | tf_op jit(solution)/shard_map/ppermute | solution.py:25
  60.6 3.1 %fusion = f32[1600,128]{1,0:T(8,128)S(1)} fusion(bf16[1536,128]{1,0:T(8,128)(2,1)S(1)} %copy-done, s32[1536]{0:T(1024)S(1)} %select_reduce_fusion), kind=kOutput, calls=%fused_computation.1 | convolution fusion | flops 631603200 | bytes 1218560 | tf_op jit(solution)/shard_map/dot_general | solution.py:103
  64.6 0.9 collective-permute-start.25
  66.7 1.8 %collective-permute-start.18 = (f32[16,1024]{1,0:T(8,128)S(1)}, f32[16,1024]{1,0:T(8,128)S(1)}, u32[]{:S(2)}, u32[]{:S(2)}) collective-permute-start(f32[16,1024]{1,0:T(8,128)S(1)} %dynamic-slice_add_fusion.1), channel_id=1, source_target_pairs={{0,6},{1,7},{2,4},{3,5},{4,2},{5,3},{6,0},{7,1},{8,14},{9,15},{10,... | collective-permute-start | bytes 196616 | tf_op jit(solution)/shard_map/ppermute | solution.py:68
  68.5 0.9 collective-permute-start.16
  69.4 1.5 %collective-permute-done.17 = f32[16,1024]{1,0:T(8,128)S(1)} collective-permute-done((f32[16,1024]{1,0:T(8,128)S(1)}, f32[16,1024]{1,0:T(8,128)S(1)}, u32[]{:S(2)}, u32[]{:S(2)}) %collective-permute-start.17) | collective-permute-done | bytes 65568 | tf_op jit(solution)/shard_map/ppermute | solution.py:68
  70.9 1.5 %collective-permute-done.18 = f32[16,1024]{1,0:T(8,128)S(1)} collective-permute-done((f32[16,1024]{1,0:T(8,128)S(1)}, f32[16,1024]{1,0:T(8,128)S(1)}, u32[]{:S(2)}, u32[]{:S(2)}) %collective-permute-start.18) | collective-permute-done | bytes 65568 | tf_op jit(solution)/shard_map/ppermute | solution.py:68
  72.8 1.9 %collective-permute-start.20 = (f32[16,1024]{1,0:T(8,128)S(1)}, f32[16,1024]{1,0:T(8,128)S(1)}, u32[]{:S(2)}, u32[]{:S(2)}) collective-permute-start(f32[16,1024]{1,0:T(8,128)S(1)} %add_add_fusion.1), channel_id=1, source_target_pairs={{0,16},{1,17},{2,18},{3,19},{4,20},{5,21},{6,22},{7,23},{8,24},{9,... | collective-permute-start | bytes 196616 | tf_op jit(solution)/shard_map/ppermute | solution.py:68
  74.7 1.4 %collective-permute-start.21 = (f32[16,1024]{1,0:T(8,128)S(1)}, f32[16,1024]{1,0:T(8,128)S(1)}, u32[]{:S(2)}, u32[]{:S(2)}) collective-permute-start(f32[16,1024]{1,0:T(8,128)S(1)} %add_add_fusion.1), channel_id=1, source_target_pairs={{0,24},{1,25},{2,26},{3,27},{4,28},{5,29},{6,30},{7,31},{8,16},{9,... | collective-permute-start | bytes 196616 | tf_op jit(solution)/shard_map/ppermute | solution.py:68
  76.4 1.0 collective-permute-done.25
  77.4 1.0 bitcast_add_fusion.1
  78.4 2.0 %collective-permute-done.20 = f32[16,1024]{1,0:T(8,128)S(1)} collective-permute-done((f32[16,1024]{1,0:T(8,128)S(1)}, f32[16,1024]{1,0:T(8,128)S(1)}, u32[]{:S(2)}, u32[]{:S(2)}) %collective-permute-start.20) | collective-permute-done | bytes 65568 | tf_op jit(solution)/shard_map/ppermute | solution.py:68
  80.4 1.0 collective-permute-done.21
  82.0 1.1 collective-permute-start.26
  83.4 2.9 %custom-call.10 = f32[32,32]{1,0:T(8,128)S(1)} custom-call(f32[32,32]{1,0:T(8,128)S(1)} %fusion.25), custom_call_target="Cholesky" | custom-call | tf_op jit(solution)/shard_map/cholesky/custom-call.1 | solution.py:188
  87.7 2.4 %custom-call.11 = f32[1,32,32]{1,2,0:T(8,128)S(1)} custom-call(f32[1,32,32]{2,1,0:T(8,128)S(1)} %fusion.42), custom_call_target="InvertDiagBlocksLowerTriangular" | custom-call | tf_op jit(solution)/shard_map/jit(_solve_triangular)/triangular_solve | solution.py:189
  91.0 1.4 %collective-permute-start.23 = (f32[32,384]{1,0:T(8,128)S(1)}, f32[32,384]{1,0:T(8,128)S(1)}, u32[]{:S(2)}, u32[]{:S(2)}) collective-permute-start(f32[32,384]{1,0:T(8,128)S(1)} %fusion.57), channel_id=1, source_target_pairs={{0,8},{8,0},{16,24},{24,16},{1,9},{9,1},{17,25},{25,17},{2,10},{10... | collective-permute-start | bytes 147464 | tf_op jit(solution)/shard_map/ppermute | solution.py:25
  92.4 3.5 %collective-permute-done.23 = f32[32,384]{1,0:T(8,128)S(1)} collective-permute-done((f32[32,384]{1,0:T(8,128)S(1)}, f32[32,384]{1,0:T(8,128)S(1)}, u32[]{:S(2)}, u32[]{:S(2)}) %collective-permute-start.23) | collective-permute-done | bytes 49184 | tf_op jit(solution)/shard_map/ppermute | solution.py:25
  95.9 1.1 collective-permute-start.24
  97.7 3.7 %collective-permute-done.24 = f32[32,384]{1,0:T(8,128)S(1)} collective-permute-done((f32[32,384]{1,0:T(8,128)S(1)}, f32[32,384]{1,0:T(8,128)S(1)}, u32[]{:S(2)}, u32[]{:S(2)}) %collective-permute-start.24) | collective-permute-done | bytes 49184 | tf_op jit(solution)/shard_map/ppermute | solution.py:25
  102.3 1.1 fusion.7
  103.4 1.0 fusion.55
  104.4 17.9 %all_gather.3 = bf16[1024,384]{1,0:T(8,128)(2,1)S(1)} all-gather(bf16[256,384]{1,0:T(8,128)(2,1)S(1)} %get-tuple-element.12), channel_id=1, replica_groups=mesh['rep'=4,'tp'=8] {'rep'}, dimensions={0}, use_global_device_ids=true | all-gather | bytes 983040 | tf_op jit(solution)/shard_map/all_gather | solution.py:203
  122.9 0.9 copy.21
  (91 shorter events, 15.4 us)
Async XLA Ops:
  0.6 59.9 %copy-start = (bf16[1536,128]{1,0:T(8,128)(2,1)S(1)}, bf16[1536,128]{1,0:T(8,128)(2,1)}, u32[]{:S(2)}) copy-start(bf16[1536,128]{1,0:T(8,128)(2,1)} %param.19) | copy-start | bytes 1179652
  0.6 20.0 %copy-start.7 = (bf16[192,1024]{1,0:T(8,128)(2,1)S(1)}, bf16[192,1024]{1,0:T(8,128)(2,1)}, u32[]{:S(2)}) copy-start(bf16[192,1024]{1,0:T(8,128)(2,1)} %param.13) | copy-start | bytes 1179652
  0.7 12.3 %collective-permute-start = (bf16[192,1024]{1,0:T(8,128)(2,1)}, bf16[192,1024]{1,0:T(8,128)(2,1)S(1)}, u32[]{:S(2)}, u32[]{:S(2)}) collective-permute-start(bf16[192,1024]{1,0:T(8,128)(2,1)} %param.13), channel_id=1, source_target_pairs={{0,2},{1,3},{2,0},{3,1},{4,6},{5,7},{6,4},{7,5},{8,10},{9,11},{10,... | collective-permute-start | bytes 1179656 | tf_op jit(solution)/shard_map/ppermute | solution.py:40
  3.7 11.2 %collective-permute-start.1 = (bf16[192,1024]{1,0:T(8,128)(2,1)}, bf16[192,1024]{1,0:T(8,128)(2,1)S(1)}, u32[]{:S(2)}, u32[]{:S(2)}) collective-permute-start(bf16[192,1024]{1,0:T(8,128)(2,1)} %param.13), channel_id=1, source_target_pairs={{0,4},{1,5},{2,6},{3,7},{4,0},{5,1},{6,2},{7,3},{8,12},{9,13},{10,... | collective-permute-start | bytes 1179656 | tf_op jit(solution)/shard_map/ppermute | solution.py:40
  13.0 7.9 %copy-start.3 = (bf16[192,1024]{1,0:T(8,128)(2,1)}, bf16[192,1024]{1,0:T(8,128)(2,1)S(1)}, u32[]{:S(2)}) copy-start(bf16[192,1024]{1,0:T(8,128)(2,1)S(1)} %collective-permute-done) | copy-start | bytes 1179652
  13.0 6.2 %collective-permute-start.3 = (bf16[96,1024]{1,0:T(8,128)(2,1)S(1)}, bf16[96,1024]{1,0:T(8,128)(2,1)S(1)}, u32[]{:S(2)}, u32[]{:S(2)}) collective-permute-start(bf16[96,1024]{1,0:T(8,128)(2,1)S(1)} %slice.15), channel_id=1, source_target_pairs={{0,4},{1,5},{2,6},{3,7},{4,0},{5,1},{6,2},{7,3},{8,12},{9,13},{10,... | collective-permute-start | bytes 589832 | tf_op jit(solution)/shard_map/ppermute | solution.py:40
  14.8 6.0 %copy-start.5 = (bf16[192,1024]{1,0:T(8,128)(2,1)}, bf16[192,1024]{1,0:T(8,128)(2,1)S(1)}, u32[]{:S(2)}) copy-start(bf16[192,1024]{1,0:T(8,128)(2,1)S(1)} %collective-permute-done.1) | copy-start | bytes 1179652
  14.9 5.7 %collective-permute-start.2 = (bf16[96,1024]{1,0:T(8,128)(2,1)S(1)}, bf16[96,1024]{1,0:T(8,128)(2,1)S(1)}, u32[]{:S(2)}, u32[]{:S(2)}) collective-permute-start(bf16[96,1024]{1,0:T(8,128)(2,1)S(1)} %slice.14), channel_id=1, source_target_pairs={{0,2},{1,3},{2,0},{3,1},{4,6},{5,7},{6,4},{7,5},{8,10},{9,11},{10,... | collective-permute-start | bytes 589832 | tf_op jit(solution)/shard_map/ppermute | solution.py:40
  20.6 0.7 copy-start.1
  21.4 4.0 %collective-permute-start.4 = (bf16[4,192,1024]{2,1,0:T(8,128)(2,1)S(1)}, bf16[4,192,1024]{2,1,0:T(8,128)(2,1)S(1)}, u32[]{:S(2)}, u32[]{:S(2)}) collective-permute-start(bf16[4,192,1024]{2,1,0:T(8,128)(2,1)S(1)} %pad_maximum_fusion), channel_id=1, source_target_pairs={{0,1},{1,0},{2,3},{3,2},{4,5},{5,4},{6,7},{7,6},{8,9},{9,8},{10,11... | collective-permute-start | bytes 4718600 | tf_op jit(solution)/shard_map/ppermute | solution.py:40
  21.4 1.7 %copy-start.2 = (bf16[1,192,1024]{2,1,0:T(8,128)(2,1)S(1)}, bf16[1,192,1024]{2,1,0:T(8,128)(2,1)}, u32[]{:S(2)}) copy-start(bf16[1,192,1024]{2,1,0:T(8,128)(2,1)} %copy-done.1) | copy-start | bytes 1179652
  21.4 1.7 %copy-start.4 = (bf16[192,1024]{1,0:T(8,128)(2,1)S(1)}, bf16[192,1024]{1,0:T(8,128)(2,1)}, u32[]{:S(2)}) copy-start(bf16[192,1024]{1,0:T(8,128)(2,1)} %copy-done.3) | copy-start | bytes 1179652
  21.4 1.7 %copy-start.6 = (bf16[192,1024]{1,0:T(8,128)(2,1)S(1)}, bf16[192,1024]{1,0:T(8,128)(2,1)}, u32[]{:S(2)}) copy-start(bf16[192,1024]{1,0:T(8,128)(2,1)} %copy-done.5) | copy-start | bytes 1179652
  21.4 1.8 %copy-start.8 = (bf16[192,1024]{1,0:T(8,128)(2,1)S(1)}, bf16[192,1024]{1,0:T(8,128)(2,1)}, u32[]{:S(2)}) copy-start(bf16[192,1024]{1,0:T(8,128)(2,1)} %param.13) | copy-start | bytes 1179652
  21.4 2.1 %copy-start.13 = (bf16[1,1024,384]{2,1,0:T(8,128)(2,1)S(1)}, bf16[1,1024,384]{2,1,0:T(8,128)(2,1)}, u32[]{:S(2)}) copy-start(bf16[1,1024,384]{2,1,0:T(8,128)(2,1)} %param.15) | copy-start | bytes 2359300
  23.5 1.0 copy-start.12
  27.3 1.5 %collective-permute-start.5 = (f32[16,1024]{1,0:T(8,128)S(1)}, f32[16,1024]{1,0:T(8,128)S(1)}, u32[]{:S(2)}, u32[]{:S(2)}) collective-permute-start(f32[16,1024]{1,0:T(8,128)S(1)} %constant_dynamic-slice_fusion.2), channel_id=1, source_target_pairs={{0,1},{1,0},{2,3},{3,2},{4,5},{5,4},{6,7},{7,6},{8,9},{9,8},{10,11... | collective-permute-start | bytes 196616 | tf_op jit(solution)/shard_map/ppermute | solution.py:68
  28.7 25.7 %copy-start.14 = (s32[1600]{0:T(1024)S(1)}, s32[1600]{0:T(1024)}, u32[]{:S(2)}) copy-start(s32[1600]{0:T(1024)} %param.21) | copy-start | bytes 19204
  28.7 25.7 %copy-start.15 = (s32[1536]{0:T(1024)S(1)}, s32[1536]{0:T(1024)}, u32[]{:S(2)}) copy-start(s32[1536]{0:T(1024)} %param.20) | copy-start | bytes 18436
  28.8 4.4 %collective-permute-start.7 = (f32[16,1024]{1,0:T(8,128)S(1)}, f32[16,1024]{1,0:T(8,128)S(1)}, u32[]{:S(2)}, u32[]{:S(2)}) collective-permute-start(f32[16,1024]{1,0:T(8,128)S(1)} %dynamic-slice_add_fusion.2), channel_id=1, source_target_pairs={{0,4},{1,5},{2,6},{3,7},{4,0},{5,1},{6,2},{7,3},{8,12},{9,13},{10,... | collective-permute-start | bytes 196616 | tf_op jit(solution)/shard_map/ppermute | solution.py:68
  29.9 5.7 %collective-permute-start.8 = (f32[16,1024]{1,0:T(8,128)S(1)}, f32[16,1024]{1,0:T(8,128)S(1)}, u32[]{:S(2)}, u32[]{:S(2)}) collective-permute-start(f32[16,1024]{1,0:T(8,128)S(1)} %dynamic-slice_add_fusion.2), channel_id=1, source_target_pairs={{0,6},{1,7},{2,4},{3,5},{4,2},{5,3},{6,0},{7,1},{8,14},{9,15},{10,... | collective-permute-start | bytes 196616 | tf_op jit(solution)/shard_map/ppermute | solution.py:68
  31.8 4.3 %collective-permute-start.6 = (f32[16,1024]{1,0:T(8,128)S(1)}, f32[16,1024]{1,0:T(8,128)S(1)}, u32[]{:S(2)}, u32[]{:S(2)}) collective-permute-start(f32[16,1024]{1,0:T(8,128)S(1)} %dynamic-slice_add_fusion.2), channel_id=1, source_target_pairs={{0,2},{1,3},{2,0},{3,1},{4,6},{5,7},{6,4},{7,5},{8,10},{9,11},{10,... | collective-permute-start | bytes 196616 | tf_op jit(solution)/shard_map/ppermute | solution.py:68
  36.1 5.3 %collective-permute-start.10 = (f32[16,1024]{1,0:T(8,128)S(1)}, f32[16,1024]{1,0:T(8,128)S(1)}, u32[]{:S(2)}, u32[]{:S(2)}) collective-permute-start(f32[16,1024]{1,0:T(8,128)S(1)} %add_add_fusion.3), channel_id=1, source_target_pairs={{0,16},{1,17},{2,18},{3,19},{4,20},{5,21},{6,22},{7,23},{8,24},{9,... | collective-permute-start | bytes 196616 | tf_op jit(solution)/shard_map/ppermute | solution.py:68
  38.7 6.2 %collective-permute-start.11 = (f32[16,1024]{1,0:T(8,128)S(1)}, f32[16,1024]{1,0:T(8,128)S(1)}, u32[]{:S(2)}, u32[]{:S(2)}) collective-permute-start(f32[16,1024]{1,0:T(8,128)S(1)} %add_add_fusion.3), channel_id=1, source_target_pairs={{0,24},{1,25},{2,26},{3,27},{4,28},{5,29},{6,30},{7,31},{8,16},{9,... | collective-permute-start | bytes 196616 | tf_op jit(solution)/shard_map/ppermute | solution.py:68
  40.1 5.0 %collective-permute-start.9 = (f32[16,1024]{1,0:T(8,128)S(1)}, f32[16,1024]{1,0:T(8,128)S(1)}, u32[]{:S(2)}, u32[]{:S(2)}) collective-permute-start(f32[16,1024]{1,0:T(8,128)S(1)} %add_add_fusion.3), channel_id=1, source_target_pairs={{0,8},{1,9},{2,10},{3,11},{4,12},{5,13},{6,14},{7,15},{8,0},{9,1},... | collective-permute-start | bytes 196616 | tf_op jit(solution)/shard_map/ppermute | solution.py:68
  45.1 1.3 %collective-permute-start.12 = (f32[16,1024]{1,0:T(8,128)S(1)}, f32[16,1024]{1,0:T(8,128)S(1)}, u32[]{:S(2)}, u32[]{:S(2)}) collective-permute-start(f32[16,1024]{1,0:T(8,128)S(1)} %get-tuple-element.18), channel_id=1, source_target_pairs={{0,1},{1,0},{2,3},{3,2},{4,5},{5,4},{6,7},{7,6},{8,9},{9,8},{10,11... | collective-permute-start | bytes 196616 | tf_op jit(solution)/shard_map/ppermute | solution.py:68
  54.2 4.2 %collective-permute-start.13 = (f32[32,384]{1,0:T(8,128)S(1)}, f32[32,384]{1,0:T(8,128)S(1)}, u32[]{:S(2)}, u32[]{:S(2)}) collective-permute-start(f32[32,384]{1,0:T(8,128)S(1)} %fusion.56), channel_id=1, source_target_pairs={{0,8},{8,0},{16,24},{24,16},{1,9},{9,1},{17,25},{25,17},{2,10},{10... | collective-permute-start | bytes 147464 | tf_op jit(solution)/shard_map/ppermute | solution.py:25
  58.4 5.3 %collective-permute-start.14 = (f32[32,384]{1,0:T(8,128)S(1)}, f32[32,384]{1,0:T(8,128)S(1)}, u32[]{:S(2)}, u32[]{:S(2)}) collective-permute-start(f32[32,384]{1,0:T(8,128)S(1)} %add.166), channel_id=1, source_target_pairs={{0,16},{8,24},{16,0},{24,8},{1,17},{9,25},{17,1},{25,9},{2,18},{10... | collective-permute-start | bytes 147464 | tf_op jit(solution)/shard_map/ppermute | solution.py:25
  64.5 1.3 %collective-permute-start.15 = (f32[16,1024]{1,0:T(8,128)S(1)}, f32[16,1024]{1,0:T(8,128)S(1)}, u32[]{:S(2)}, u32[]{:S(2)}) collective-permute-start(f32[16,1024]{1,0:T(8,128)S(1)} %constant_dynamic-slice_fusion.1), channel_id=1, source_target_pairs={{0,1},{1,0},{2,3},{3,2},{4,5},{5,4},{6,7},{7,6},{8,9},{9,8},{10,11... | collective-permute-start | bytes 196616 | tf_op jit(solution)/shard_map/ppermute | solution.py:68
  64.6 12.7 %collective-permute-start.25 = (f32[2,400,128]{2,1,0:T(8,128)S(1)}, f32[2,400,128]{2,1,0:T(8,128)}, u32[]{:S(2)}, u32[]{:S(2)}) collective-permute-start(f32[2,400,128]{2,1,0:T(8,128)S(1)} %dynamic-slice_bitcast_fusion), channel_id=1, source_target_pairs={{0,8},{8,0},{16,24},{24,16},{1,9},{9,1},{17,25},{25,17},{2,10},{10... | collective-permute-start | bytes 1228808 | tf_op jit(solution)/shard_map/ppermute | solution.py:115
  65.8 5.0 %collective-permute-start.17 = (f32[16,1024]{1,0:T(8,128)S(1)}, f32[16,1024]{1,0:T(8,128)S(1)}, u32[]{:S(2)}, u32[]{:S(2)}) collective-permute-start(f32[16,1024]{1,0:T(8,128)S(1)} %dynamic-slice_add_fusion.1), channel_id=1, source_target_pairs={{0,4},{1,5},{2,6},{3,7},{4,0},{5,1},{6,2},{7,3},{8,12},{9,13},{10,... | collective-permute-start | bytes 196616 | tf_op jit(solution)/shard_map/ppermute | solution.py:68
  66.7 5.7 %collective-permute-start.18 = (f32[16,1024]{1,0:T(8,128)S(1)}, f32[16,1024]{1,0:T(8,128)S(1)}, u32[]{:S(2)}, u32[]{:S(2)}) collective-permute-start(f32[16,1024]{1,0:T(8,128)S(1)} %dynamic-slice_add_fusion.1), channel_id=1, source_target_pairs={{0,6},{1,7},{2,4},{3,5},{4,2},{5,3},{6,0},{7,1},{8,14},{9,15},{10,... | collective-permute-start | bytes 196616 | tf_op jit(solution)/shard_map/ppermute | solution.py:68
  68.5 4.3 %collective-permute-start.16 = (f32[16,1024]{1,0:T(8,128)S(1)}, f32[16,1024]{1,0:T(8,128)S(1)}, u32[]{:S(2)}, u32[]{:S(2)}) collective-permute-start(f32[16,1024]{1,0:T(8,128)S(1)} %dynamic-slice_add_fusion.1), channel_id=1, source_target_pairs={{0,2},{1,3},{2,0},{3,1},{4,6},{5,7},{6,4},{7,5},{8,10},{9,11},{10,... | collective-permute-start | bytes 196616 | tf_op jit(solution)/shard_map/ppermute | solution.py:68
  72.8 7.6 %collective-permute-start.20 = (f32[16,1024]{1,0:T(8,128)S(1)}, f32[16,1024]{1,0:T(8,128)S(1)}, u32[]{:S(2)}, u32[]{:S(2)}) collective-permute-start(f32[16,1024]{1,0:T(8,128)S(1)} %add_add_fusion.1), channel_id=1, source_target_pairs={{0,16},{1,17},{2,18},{3,19},{4,20},{5,21},{6,22},{7,23},{8,24},{9,... | collective-permute-start | bytes 196616 | tf_op jit(solution)/shard_map/ppermute | solution.py:68
  74.7 6.7 %collective-permute-start.21 = (f32[16,1024]{1,0:T(8,128)S(1)}, f32[16,1024]{1,0:T(8,128)S(1)}, u32[]{:S(2)}, u32[]{:S(2)}) collective-permute-start(f32[16,1024]{1,0:T(8,128)S(1)} %add_add_fusion.1), channel_id=1, source_target_pairs={{0,24},{1,25},{2,26},{3,27},{4,28},{5,29},{6,30},{7,31},{8,16},{9,... | collective-permute-start | bytes 196616 | tf_op jit(solution)/shard_map/ppermute | solution.py:68
  76.2 5.5 %collective-permute-start.19 = (f32[16,1024]{1,0:T(8,128)S(1)}, f32[16,1024]{1,0:T(8,128)S(1)}, u32[]{:S(2)}, u32[]{:S(2)}) collective-permute-start(f32[16,1024]{1,0:T(8,128)S(1)} %add_add_fusion.1), channel_id=1, source_target_pairs={{0,8},{1,9},{2,10},{3,11},{4,12},{5,13},{6,14},{7,15},{8,0},{9,1},... | collective-permute-start | bytes 196616 | tf_op jit(solution)/shard_map/ppermute | solution.py:68
  81.6 15.4 %copy-start.11 = (f32[400,128]{1,0:T(8,128)S(1)}, f32[400,128]{1,0:T(8,128)}, u32[]{:S(2)}) copy-start(f32[400,128]{1,0:T(8,128)} %param.22) | copy-start | bytes 614404
  81.7 1.5 %collective-permute-start.22 = (f32[16,1024]{1,0:T(8,128)S(1)}, f32[16,1024]{1,0:T(8,128)S(1)}, u32[]{:S(2)}, u32[]{:S(2)}) collective-permute-start(f32[16,1024]{1,0:T(8,128)S(1)} %get-tuple-element.16), channel_id=1, source_target_pairs={{0,1},{1,0},{2,3},{3,2},{4,5},{5,4},{6,7},{7,6},{8,9},{9,8},{10,11... | collective-permute-start | bytes 196616 | tf_op jit(solution)/shard_map/ppermute | solution.py:68
  82.0 15.0 %collective-permute-start.26 = (f32[1,400,128]{2,1,0:T(8,128)S(1)}, f32[1,400,128]{2,1,0:T(8,128)S(1)}, u32[]{:S(2)}, u32[]{:S(2)}) collective-permute-start(f32[1,400,128]{2,1,0:T(8,128)S(1)} %constant_dynamic-slice_fusion), channel_id=1, source_target_pairs={{0,16},{8,24},{16,0},{24,8},{1,17},{9,25},{17,1},{25,9},{2,18},{10... | collective-permute-start | bytes 614408 | tf_op jit(solution)/shard_map/ppermute | solution.py:115
  91.0 4.9 %collective-permute-start.23 = (f32[32,384]{1,0:T(8,128)S(1)}, f32[32,384]{1,0:T(8,128)S(1)}, u32[]{:S(2)}, u32[]{:S(2)}) collective-permute-start(f32[32,384]{1,0:T(8,128)S(1)} %fusion.57), channel_id=1, source_target_pairs={{0,8},{8,0},{16,24},{24,16},{1,9},{9,1},{17,25},{25,17},{2,10},{10... | collective-permute-start | bytes 147464 | tf_op jit(solution)/shard_map/ppermute | solution.py:25
  95.9 5.6 %collective-permute-start.24 = (f32[32,384]{1,0:T(8,128)S(1)}, f32[32,384]{1,0:T(8,128)S(1)}, u32[]{:S(2)}, u32[]{:S(2)}) collective-permute-start(f32[32,384]{1,0:T(8,128)S(1)} %add.175), channel_id=1, source_target_pairs={{0,16},{8,24},{16,0},{24,8},{1,17},{9,25},{17,1},{25,9},{2,18},{10... | collective-permute-start | bytes 147464 | tf_op jit(solution)/shard_map/ppermute | solution.py:25
  102.3 1.2 copy-start.9
  102.3 1.2 copy-start.10

commit v19 on v18

--- a/solution.py
+++ b/solution.py
@@ -19,11 +19,17 @@
         count *= lax.axis_size(axis)
     if count & (count - 1):
         return lax.psum(value, axes)
+    def exchange(stride):
+        return lax.ppermute(value, axes, [(i, i ^ stride) for i in range(count)])
+
     stride = 1
+    if (count.bit_length() - 1) % 2:
+        value = value + exchange(1)
+        stride = 2
     while stride < count:
-        pairs = [(i, i ^ stride) for i in range(count)]
-        value = value + lax.ppermute(value, axes, pairs)
-        stride *= 2
+        low, high = stride, 2 * stride
+        value = (value + exchange(low)) + (exchange(high) + exchange(low ^ high))
+        stride *= 4
     return value
 
 

time: 124 us -> 121 us (0.976)
  waiting for transfers between devices: 40.6 us -> 34.8 us
  starting transfers between devices: 30.8 us -> 32.8 us
    ppermute x4 -> x6, waiting for transfers between devices: 9.97 us -> 5.51 us  [exchange(): return lax.ppermute(value, axes, [(i, i ^ stride) for i in range(count)])]
    ppermute x16, waiting for transfers between devices: 17.6 us -> 14.9 us  [exchange(): return lax.ppermute(piece, axes, [(i, i ^ stride) for i in range(count)])]
    ppermute x4 -> x6, starting transfers between devices: 5 us -> 7.33 us  [exchange(): return lax.ppermute(value, axes, [(i, i ^ stride) for i in range(count)])]
    ppermute x2, waiting for transfers between devices: 1 us -> 2.36 us  [word_update_dense(): blocks = kept + lax.ppermute(sent, 'rep', pairs)]
  transfers between devices with their start and end apart: 27 -> 29, of which waited for: 23 -> 21; matrix products, arithmetic and copies ran while one was open for 14% -> 15% of each run, Pallas kernels for 0% -> 0%
where the time goes in v19:
time: 121 us; the launch traced here: 120 us
  waiting for transfers between devices  34.8 us (29%)
  starting transfers between devices  32.8 us (27%)
  other arithmetic  18.7 us (15%)
  blocking collectives  18 us (15%)
  matrix products  10.6 us (9%)
  local copies, waits for them, and re-layouts  4.38 us (4%)
  between operations  1.3 us (1%)
    all_gather x1, blocking collectives, shards(): lax.all_gather(master_new.astype(jnp.bfloat16), 'rep', axis=0, tiled=True)  18 us
    ppermute x16, starting transfers between devices, exchange(): return lax.ppermute(piece, axes, [(i, i ^ stride) for i in range(count)])  16.2 us
    ppermute x16, waiting for transfers between devices, exchange(): return lax.ppermute(piece, axes, [(i, i ^ stride) for i in range(count)])  14.9 us
    ppermute x5, waiting for transfers between devices, exchange(): return lax.ppermute(value, axis, [(i, i ^ stride) for i in range(count)])  12 us
    ppermute x5, starting transfers between devices, exchange(): return lax.ppermute(value, axis, [(i, i ^ stride) for i in range(count)])  7.91 us
    ppermute x6, starting transfers between devices, exchange(): return lax.ppermute(value, axes, [(i, i ^ stride) for i in range(count)])  7.33 us
    another operation x6, other arithmetic, shards(): factor_low = lax.linalg.cholesky(gram_matrix, symmetrize_input=False)  7.18 us
    another operation x4, other arithmetic, shards(): jax.scipy.linalg.solve_triangular(factor_low, left_rows, lower=True)  6.17 us
  transfers between devices with their start and end apart: 29, of which 21 were waited for; matrix products, arithmetic and copies ran while one was open for 15% of the time, Pallas kernels for 0%

profile of v19, /device:TPU:0, one launch (start us, length us, event | category | flops | bytes accessed | tf_op | source)
XLA Modules:
  0.0 120.5 jit_solution(3590382023239552967)
XLA Ops:
  0.7 3.0 %collective-permute-start = (bf16[192,1024]{1,0:T(8,128)(2,1)}, bf16[192,1024]{1,0:T(8,128)(2,1)S(1)}, u32[]{:S(2)}, u32[]{:S(2)}) collective-permute-start(bf16[192,1024]{1,0:T(8,128)(2,1)} %param.13), channel_id=1, source_target_pairs={{0,2},{1,3},{2,0},{3,1},{4,6},{5,7},{6,4},{7,5},{8,10},{9,11},{10,... | collective-permute-start | bytes 1179656 | tf_op jit(solution)/shard_map/ppermute | solution.py:46
  3.7 1.5 %collective-permute-start.1 = (bf16[192,1024]{1,0:T(8,128)(2,1)}, bf16[192,1024]{1,0:T(8,128)(2,1)S(1)}, u32[]{:S(2)}, u32[]{:S(2)}) collective-permute-start(bf16[192,1024]{1,0:T(8,128)(2,1)} %param.13), channel_id=1, source_target_pairs={{0,4},{1,5},{2,6},{3,7},{4,0},{5,1},{6,2},{7,3},{8,12},{9,13},{10,... | collective-permute-start | bytes 1179656 | tf_op jit(solution)/shard_map/ppermute | solution.py:46
  5.2 7.8 %collective-permute-done = bf16[192,1024]{1,0:T(8,128)(2,1)S(1)} collective-permute-done((bf16[192,1024]{1,0:T(8,128)(2,1)}, bf16[192,1024]{1,0:T(8,128)(2,1)S(1)}, u32[]{:S(2)}, u32[]{:S(2)}) %collective-permute-start) | collective-permute-done | bytes 393248 | tf_op jit(solution)/shard_map/ppermute | solution.py:46
  13.0 1.8 %collective-permute-start.3 = (bf16[96,1024]{1,0:T(8,128)(2,1)S(1)}, bf16[96,1024]{1,0:T(8,128)(2,1)S(1)}, u32[]{:S(2)}, u32[]{:S(2)}) collective-permute-start(bf16[96,1024]{1,0:T(8,128)(2,1)S(1)} %slice.15), channel_id=1, source_target_pairs={{0,4},{1,5},{2,6},{3,7},{4,0},{5,1},{6,2},{7,3},{8,12},{9,13},{10,... | collective-permute-start | bytes 589832 | tf_op jit(solution)/shard_map/ppermute | solution.py:46
  14.9 1.6 %collective-permute-start.2 = (bf16[96,1024]{1,0:T(8,128)(2,1)S(1)}, bf16[96,1024]{1,0:T(8,128)(2,1)S(1)}, u32[]{:S(2)}, u32[]{:S(2)}) collective-permute-start(bf16[96,1024]{1,0:T(8,128)(2,1)S(1)} %slice.14), channel_id=1, source_target_pairs={{0,2},{1,3},{2,0},{3,1},{4,6},{5,7},{6,4},{7,5},{8,10},{9,11},{10,... | collective-permute-start | bytes 589832 | tf_op jit(solution)/shard_map/ppermute | solution.py:46
  16.4 2.7 %collective-permute-done.3 = bf16[96,1024]{1,0:T(8,128)(2,1)S(1)} collective-permute-done((bf16[96,1024]{1,0:T(8,128)(2,1)S(1)}, bf16[96,1024]{1,0:T(8,128)(2,1)S(1)}, u32[]{:S(2)}, u32[]{:S(2)}) %collective-permute-start.3) | collective-permute-done | bytes 196640 | tf_op jit(solution)/shard_map/ppermute | solution.py:46
  19.2 1.4 %collective-permute-done.2 = bf16[96,1024]{1,0:T(8,128)(2,1)S(1)} collective-permute-done((bf16[96,1024]{1,0:T(8,128)(2,1)S(1)}, bf16[96,1024]{1,0:T(8,128)(2,1)S(1)}, u32[]{:S(2)}, u32[]{:S(2)}) %collective-permute-start.2) | collective-permute-done | bytes 196640 | tf_op jit(solution)/shard_map/ppermute | solution.py:46
  21.4 1.6 %constant_dynamic-slice_fusion.6 = (bf16[1,192,384]{2,1,0:T(8,128)(2,1)S(1)}, bf16[1,192,384]{2,1,0:T(8,128)(2,1)S(1)}, bf16[1,192,384]{2,1,0:T(8,128)(2,1)S(1)}...) fusion(bf16[8,192,384]{2,1,0:T(8,128)(2,1)} %bitcast.53, ...), kind=kLoop, calls=%fused_computation.81 | loop fusion | bytes 2359328 | tf_op jit(solution)/shard_map/dynamic_slice | solution.py:59
  23.5 1.0 convert_add_fusion
  24.5 0.8 convolution_bitcast_fusion
  25.3 1.0 bitcast_add_fusion
  26.4 0.8 fusion.4
  27.8 0.9 collective-permute-done.5
  28.8 1.2 collective-permute-start.7
  29.9 1.8 %collective-permute-start.8 = (f32[16,1024]{1,0:T(8,128)S(1)}, f32[16,1024]{1,0:T(8,128)S(1)}, u32[]{:S(2)}, u32[]{:S(2)}) collective-permute-start(f32[16,1024]{1,0:T(8,128)S(1)} %dynamic-slice_add_fusion.2), channel_id=1, source_target_pairs={{0,6},{1,7},{2,4},{3,5},{4,2},{5,3},{6,0},{7,1},{8,14},{9,15},{10,... | collective-permute-start | bytes 196616 | tf_op jit(solution)/shard_map/ppermute | solution.py:74
  32.3 0.9 collective-permute-done.7
  33.2 2.4 %collective-permute-done.8 = f32[16,1024]{1,0:T(8,128)S(1)} collective-permute-done((f32[16,1024]{1,0:T(8,128)S(1)}, f32[16,1024]{1,0:T(8,128)S(1)}, u32[]{:S(2)}, u32[]{:S(2)}) %collective-permute-start.8) | collective-permute-done | bytes 65568 | tf_op jit(solution)/shard_map/ppermute | solution.py:74
  36.1 2.7 %collective-permute-start.10 = (f32[16,1024]{1,0:T(8,128)S(1)}, f32[16,1024]{1,0:T(8,128)S(1)}, u32[]{:S(2)}, u32[]{:S(2)}) collective-permute-start(f32[16,1024]{1,0:T(8,128)S(1)} %add_add_fusion.3), channel_id=1, source_target_pairs={{0,16},{1,17},{2,18},{3,19},{4,20},{5,21},{6,22},{7,23},{8,24},{9,... | collective-permute-start | bytes 196616 | tf_op jit(solution)/shard_map/ppermute | solution.py:74
  38.7 1.3 %collective-permute-start.11 = (f32[16,1024]{1,0:T(8,128)S(1)}, f32[16,1024]{1,0:T(8,128)S(1)}, u32[]{:S(2)}, u32[]{:S(2)}) collective-permute-start(f32[16,1024]{1,0:T(8,128)S(1)} %add_add_fusion.3), channel_id=1, source_target_pairs={{0,24},{1,25},{2,26},{3,27},{4,28},{5,29},{6,30},{7,31},{8,16},{9,... | collective-permute-start | bytes 196616 | tf_op jit(solution)/shard_map/ppermute | solution.py:74
  40.3 1.1 collective-permute-done.10
  41.4 3.6 %collective-permute-done.11 = f32[16,1024]{1,0:T(8,128)S(1)} collective-permute-done((f32[16,1024]{1,0:T(8,128)S(1)}, f32[16,1024]{1,0:T(8,128)S(1)}, u32[]{:S(2)}, u32[]{:S(2)}) %collective-permute-start.11) | collective-permute-done | bytes 65568 | tf_op jit(solution)/shard_map/ppermute | solution.py:74
  45.2 1.1 select_reduce_fusion
  46.6 2.9 %custom-call.8 = f32[32,32]{1,0:T(8,128)S(1)} custom-call(f32[32,32]{1,0:T(8,128)S(1)} %fusion.29), custom_call_target="Cholesky" | custom-call | tf_op jit(solution)/shard_map/cholesky/custom-call.1 | solution.py:194
  50.9 2.4 %custom-call.9 = f32[1,32,32]{1,2,0:T(8,128)S(1)} custom-call(f32[1,32,32]{2,1,0:T(8,128)S(1)} %fusion.41), custom_call_target="InvertDiagBlocksLowerTriangular" | custom-call | tf_op jit(solution)/shard_map/jit(_solve_triangular)/triangular_solve | solution.py:195
  54.2 2.2 %collective-permute-start.14 = (f32[32,384]{1,0:T(8,128)S(1)}, f32[32,384]{1,0:T(8,128)S(1)}, u32[]{:S(2)}, u32[]{:S(2)}) collective-permute-start(f32[32,384]{1,0:T(8,128)S(1)} %fusion.55), channel_id=1, source_target_pairs={{0,16},{8,24},{16,0},{24,8},{1,17},{9,25},{17,1},{25,9},{2,18},{10... | collective-permute-start | bytes 147464 | tf_op jit(solution)/shard_map/ppermute | solution.py:23
  56.9 0.9 collective-permute-start.13
  57.8 3.1 %fusion = f32[1600,128]{1,0:T(8,128)S(1)} fusion(bf16[1536,128]{1,0:T(8,128)(2,1)S(1)} %copy-done, s32[1536]{0:T(1024)S(1)} %select_reduce_fusion), kind=kOutput, calls=%fused_computation.1 | convolution fusion | flops 631603200 | bytes 1218560 | tf_op jit(solution)/shard_map/dot_general | solution.py:109
  60.9 1.6 %collective-permute-done.15 = f32[32,384]{1,0:T(8,128)S(1)} collective-permute-done((f32[32,384]{1,0:T(8,128)S(1)}, f32[32,384]{1,0:T(8,128)S(1)}, u32[]{:S(2)}, u32[]{:S(2)}) %collective-permute-start.15) | collective-permute-done | bytes 49184 | tf_op jit(solution)/shard_map/ppermute | solution.py:23
  65.5 1.8 %collective-permute-start.19 = (f32[16,1024]{1,0:T(8,128)S(1)}, f32[16,1024]{1,0:T(8,128)S(1)}, u32[]{:S(2)}, u32[]{:S(2)}) collective-permute-start(f32[16,1024]{1,0:T(8,128)S(1)} %dynamic-slice_add_fusion.1), channel_id=1, source_target_pairs={{0,6},{1,7},{2,4},{3,5},{4,2},{5,3},{6,0},{7,1},{8,14},{9,15},{10,... | collective-permute-start | bytes 196616 | tf_op jit(solution)/shard_map/ppermute | solution.py:74
  67.3 0.9 collective-permute-start.17
  68.2 1.5 %collective-permute-done.18 = f32[16,1024]{1,0:T(8,128)S(1)} collective-permute-done((f32[16,1024]{1,0:T(8,128)S(1)}, f32[16,1024]{1,0:T(8,128)S(1)}, u32[]{:S(2)}, u32[]{:S(2)}) %collective-permute-start.18) | collective-permute-done | bytes 65568 | tf_op jit(solution)/shard_map/ppermute | solution.py:74
  69.7 1.5 %collective-permute-done.19 = f32[16,1024]{1,0:T(8,128)S(1)} collective-permute-done((f32[16,1024]{1,0:T(8,128)S(1)}, f32[16,1024]{1,0:T(8,128)S(1)}, u32[]{:S(2)}, u32[]{:S(2)}) %collective-permute-start.19) | collective-permute-done | bytes 65568 | tf_op jit(solution)/shard_map/ppermute | solution.py:74
  71.6 2.5 %collective-permute-start.21 = (f32[16,1024]{1,0:T(8,128)S(1)}, f32[16,1024]{1,0:T(8,128)S(1)}, u32[]{:S(2)}, u32[]{:S(2)}) collective-permute-start(f32[16,1024]{1,0:T(8,128)S(1)} %add_add_fusion.1), channel_id=1, source_target_pairs={{0,16},{1,17},{2,18},{3,19},{4,20},{5,21},{6,22},{7,23},{8,24},{9,... | collective-permute-start | bytes 196616 | tf_op jit(solution)/shard_map/ppermute | solution.py:74
  74.1 1.5 %collective-permute-start.22 = (f32[16,1024]{1,0:T(8,128)S(1)}, f32[16,1024]{1,0:T(8,128)S(1)}, u32[]{:S(2)}, u32[]{:S(2)}) collective-permute-start(f32[16,1024]{1,0:T(8,128)S(1)} %add_add_fusion.1), channel_id=1, source_target_pairs={{0,24},{1,25},{2,26},{3,27},{4,28},{5,29},{6,30},{7,31},{8,16},{9,... | collective-permute-start | bytes 196616 | tf_op jit(solution)/shard_map/ppermute | solution.py:74
  75.7 2.4 %collective-permute-done.27 = f32[2,400,128]{2,1,0:T(8,128)} collective-permute-done((f32[2,400,128]{2,1,0:T(8,128)}, f32[2,400,128]{2,1,0:T(8,128)}, u32[]{:S(2)}, u32[]{:S(2)}) %collective-permute-start.27) | collective-permute-done | bytes 409632 | tf_op jit(solution)/shard_map/ppermute | solution.py:121
  78.0 1.0 bitcast_add_fusion.1
  79.1 1.7 %collective-permute-done.22 = f32[16,1024]{1,0:T(8,128)S(1)} collective-permute-done((f32[16,1024]{1,0:T(8,128)S(1)}, f32[16,1024]{1,0:T(8,128)S(1)}, u32[]{:S(2)}, u32[]{:S(2)}) %collective-permute-start.22) | collective-permute-done | bytes 65568 | tf_op jit(solution)/shard_map/ppermute | solution.py:74
  81.1 1.3 %collective-permute-start.28 = (f32[1,400,128]{2,1,0:T(8,128)S(1)}, f32[1,400,128]{2,1,0:T(8,128)S(1)}, u32[]{:S(2)}, u32[]{:S(2)}) collective-permute-start(f32[1,400,128]{2,1,0:T(8,128)S(1)} %constant_dynamic-slice_fusion), channel_id=1, source_target_pairs={{0,16},{8,24},{16,0},{24,8},{1,17},{9,25},{17,1},{25,9},{2,18},{10... | collective-permute-start | bytes 614408 | tf_op jit(solution)/shard_map/ppermute | solution.py:121
  82.6 2.9 %custom-call.10 = f32[32,32]{1,0:T(8,128)S(1)} custom-call(f32[32,32]{1,0:T(8,128)S(1)} %fusion.25), custom_call_target="Cholesky" | custom-call | tf_op jit(solution)/shard_map/cholesky/custom-call.1 | solution.py:194
  86.9 2.4 %custom-call.11 = f32[1,32,32]{1,2,0:T(8,128)S(1)} custom-call(f32[1,32,32]{2,1,0:T(8,128)S(1)} %fusion.42), custom_call_target="InvertDiagBlocksLowerTriangular" | custom-call | tf_op jit(solution)/shard_map/jit(_solve_triangular)/triangular_solve | solution.py:195
  90.2 1.8 %collective-permute-start.25 = (f32[32,384]{1,0:T(8,128)S(1)}, f32[32,384]{1,0:T(8,128)S(1)}, u32[]{:S(2)}, u32[]{:S(2)}) collective-permute-start(f32[32,384]{1,0:T(8,128)S(1)} %fusion.56), channel_id=1, source_target_pairs={{0,16},{8,24},{16,0},{24,8},{1,17},{9,25},{17,1},{25,9},{2,18},{10... | collective-permute-start | bytes 147464 | tf_op jit(solution)/shard_map/ppermute | solution.py:23
  92.0 2.0 %collective-permute-start.26 = (f32[32,384]{1,0:T(8,128)S(1)}, f32[32,384]{1,0:T(8,128)S(1)}, u32[]{:S(2)}, u32[]{:S(2)}) collective-permute-start(f32[32,384]{1,0:T(8,128)S(1)} %fusion.56), channel_id=1, source_target_pairs={{0,24},{8,16},{16,8},{24,0},{1,25},{9,17},{17,9},{25,1},{2,26},{10... | collective-permute-start | bytes 147464 | tf_op jit(solution)/shard_map/ppermute | solution.py:23
  94.7 2.6 %collective-permute-done.25 = f32[32,384]{1,0:T(8,128)S(1)} collective-permute-done((f32[32,384]{1,0:T(8,128)S(1)}, f32[32,384]{1,0:T(8,128)S(1)}, u32[]{:S(2)}, u32[]{:S(2)}) %collective-permute-start.25) | collective-permute-done | bytes 49184 | tf_op jit(solution)/shard_map/ppermute | solution.py:23
  98.6 0.8 fusion.57
  99.5 1.1 fusion.7
  100.6 1.0 fusion.54
  101.6 18.0 %all_gather.3 = bf16[1024,384]{1,0:T(8,128)(2,1)S(1)} all-gather(bf16[256,384]{1,0:T(8,128)(2,1)S(1)} %get-tuple-element.12), channel_id=1, replica_groups=mesh['rep'=4,'tp'=8] {'rep'}, dimensions={0}, use_global_device_ids=true | all-gather | bytes 983040 | tf_op jit(solution)/shard_map/all_gather | solution.py:209
  119.6 0.9 copy.21
  (95 shorter events, 14.3 us)
Async XLA Ops:
  0.6 57.1 %copy-start = (bf16[1536,128]{1,0:T(8,128)(2,1)S(1)}, bf16[1536,128]{1,0:T(8,128)(2,1)}, u32[]{:S(2)}) copy-start(bf16[1536,128]{1,0:T(8,128)(2,1)} %param.19) | copy-start | bytes 1179652
  0.6 20.0 %copy-start.7 = (bf16[192,1024]{1,0:T(8,128)(2,1)S(1)}, bf16[192,1024]{1,0:T(8,128)(2,1)}, u32[]{:S(2)}) copy-start(bf16[192,1024]{1,0:T(8,128)(2,1)} %param.13) | copy-start | bytes 1179652
  0.7 12.3 %collective-permute-start = (bf16[192,1024]{1,0:T(8,128)(2,1)}, bf16[192,1024]{1,0:T(8,128)(2,1)S(1)}, u32[]{:S(2)}, u32[]{:S(2)}) collective-permute-start(bf16[192,1024]{1,0:T(8,128)(2,1)} %param.13), channel_id=1, source_target_pairs={{0,2},{1,3},{2,0},{3,1},{4,6},{5,7},{6,4},{7,5},{8,10},{9,11},{10,... | collective-permute-start | bytes 1179656 | tf_op jit(solution)/shard_map/ppermute | solution.py:46
  3.7 11.2 %collective-permute-start.1 = (bf16[192,1024]{1,0:T(8,128)(2,1)}, bf16[192,1024]{1,0:T(8,128)(2,1)S(1)}, u32[]{:S(2)}, u32[]{:S(2)}) collective-permute-start(bf16[192,1024]{1,0:T(8,128)(2,1)} %param.13), channel_id=1, source_target_pairs={{0,4},{1,5},{2,6},{3,7},{4,0},{5,1},{6,2},{7,3},{8,12},{9,13},{10,... | collective-permute-start | bytes 1179656 | tf_op jit(solution)/shard_map/ppermute | solution.py:46
  13.0 7.9 %copy-start.3 = (bf16[192,1024]{1,0:T(8,128)(2,1)}, bf16[192,1024]{1,0:T(8,128)(2,1)S(1)}, u32[]{:S(2)}) copy-start(bf16[192,1024]{1,0:T(8,128)(2,1)S(1)} %collective-permute-done) | copy-start | bytes 1179652
  13.0 6.2 %collective-permute-start.3 = (bf16[96,1024]{1,0:T(8,128)(2,1)S(1)}, bf16[96,1024]{1,0:T(8,128)(2,1)S(1)}, u32[]{:S(2)}, u32[]{:S(2)}) collective-permute-start(bf16[96,1024]{1,0:T(8,128)(2,1)S(1)} %slice.15), channel_id=1, source_target_pairs={{0,4},{1,5},{2,6},{3,7},{4,0},{5,1},{6,2},{7,3},{8,12},{9,13},{10,... | collective-permute-start | bytes 589832 | tf_op jit(solution)/shard_map/ppermute | solution.py:46
  14.8 6.0 %copy-start.5 = (bf16[192,1024]{1,0:T(8,128)(2,1)}, bf16[192,1024]{1,0:T(8,128)(2,1)S(1)}, u32[]{:S(2)}) copy-start(bf16[192,1024]{1,0:T(8,128)(2,1)S(1)} %collective-permute-done.1) | copy-start | bytes 1179652
  14.9 5.7 %collective-permute-start.2 = (bf16[96,1024]{1,0:T(8,128)(2,1)S(1)}, bf16[96,1024]{1,0:T(8,128)(2,1)S(1)}, u32[]{:S(2)}, u32[]{:S(2)}) collective-permute-start(bf16[96,1024]{1,0:T(8,128)(2,1)S(1)} %slice.14), channel_id=1, source_target_pairs={{0,2},{1,3},{2,0},{3,1},{4,6},{5,7},{6,4},{7,5},{8,10},{9,11},{10,... | collective-permute-start | bytes 589832 | tf_op jit(solution)/shard_map/ppermute | solution.py:46
  20.6 0.7 copy-start.1
  21.4 4.0 %collective-permute-start.4 = (bf16[4,192,1024]{2,1,0:T(8,128)(2,1)S(1)}, bf16[4,192,1024]{2,1,0:T(8,128)(2,1)S(1)}, u32[]{:S(2)}, u32[]{:S(2)}) collective-permute-start(bf16[4,192,1024]{2,1,0:T(8,128)(2,1)S(1)} %pad_maximum_fusion), channel_id=1, source_target_pairs={{0,1},{1,0},{2,3},{3,2},{4,5},{5,4},{6,7},{7,6},{8,9},{9,8},{10,11... | collective-permute-start | bytes 4718600 | tf_op jit(solution)/shard_map/ppermute | solution.py:46
  21.4 1.7 %copy-start.2 = (bf16[1,192,1024]{2,1,0:T(8,128)(2,1)S(1)}, bf16[1,192,1024]{2,1,0:T(8,128)(2,1)}, u32[]{:S(2)}) copy-start(bf16[1,192,1024]{2,1,0:T(8,128)(2,1)} %copy-done.1) | copy-start | bytes 1179652
  21.4 1.7 %copy-start.4 = (bf16[192,1024]{1,0:T(8,128)(2,1)S(1)}, bf16[192,1024]{1,0:T(8,128)(2,1)}, u32[]{:S(2)}) copy-start(bf16[192,1024]{1,0:T(8,128)(2,1)} %copy-done.3) | copy-start | bytes 1179652
  21.4 1.7 %copy-start.6 = (bf16[192,1024]{1,0:T(8,128)(2,1)S(1)}, bf16[192,1024]{1,0:T(8,128)(2,1)}, u32[]{:S(2)}) copy-start(bf16[192,1024]{1,0:T(8,128)(2,1)} %copy-done.5) | copy-start | bytes 1179652
  21.4 1.8 %copy-start.8 = (bf16[192,1024]{1,0:T(8,128)(2,1)S(1)}, bf16[192,1024]{1,0:T(8,128)(2,1)}, u32[]{:S(2)}) copy-start(bf16[192,1024]{1,0:T(8,128)(2,1)} %param.13) | copy-start | bytes 1179652
  21.4 2.1 %copy-start.14 = (bf16[1,1024,384]{2,1,0:T(8,128)(2,1)S(1)}, bf16[1,1024,384]{2,1,0:T(8,128)(2,1)}, u32[]{:S(2)}) copy-start(bf16[1,1024,384]{2,1,0:T(8,128)(2,1)} %param.15) | copy-start | bytes 2359300
  23.5 1.0 copy-start.12
  26.4 18.8 %copy-start.15 = (s32[1600]{0:T(1024)S(1)}, s32[1600]{0:T(1024)}, u32[]{:S(2)}) copy-start(s32[1600]{0:T(1024)} %param.21) | copy-start | bytes 19204
  26.4 18.8 %copy-start.16 = (s32[1536]{0:T(1024)S(1)}, s32[1536]{0:T(1024)}, u32[]{:S(2)}) copy-start(s32[1536]{0:T(1024)} %param.20) | copy-start | bytes 18436
  27.3 1.5 %collective-permute-start.5 = (f32[16,1024]{1,0:T(8,128)S(1)}, f32[16,1024]{1,0:T(8,128)S(1)}, u32[]{:S(2)}, u32[]{:S(2)}) collective-permute-start(f32[16,1024]{1,0:T(8,128)S(1)} %constant_dynamic-slice_fusion.2), channel_id=1, source_target_pairs={{0,1},{1,0},{2,3},{3,2},{4,5},{5,4},{6,7},{7,6},{8,9},{9,8},{10,11... | collective-permute-start | bytes 196616 | tf_op jit(solution)/shard_map/ppermute | solution.py:74
  28.8 4.4 %collective-permute-start.7 = (f32[16,1024]{1,0:T(8,128)S(1)}, f32[16,1024]{1,0:T(8,128)S(1)}, u32[]{:S(2)}, u32[]{:S(2)}) collective-permute-start(f32[16,1024]{1,0:T(8,128)S(1)} %dynamic-slice_add_fusion.2), channel_id=1, source_target_pairs={{0,4},{1,5},{2,6},{3,7},{4,0},{5,1},{6,2},{7,3},{8,12},{9,13},{10,... | collective-permute-start | bytes 196616 | tf_op jit(solution)/shard_map/ppermute | solution.py:74
  29.9 5.7 %collective-permute-start.8 = (f32[16,1024]{1,0:T(8,128)S(1)}, f32[16,1024]{1,0:T(8,128)S(1)}, u32[]{:S(2)}, u32[]{:S(2)}) collective-permute-start(f32[16,1024]{1,0:T(8,128)S(1)} %dynamic-slice_add_fusion.2), channel_id=1, source_target_pairs={{0,6},{1,7},{2,4},{3,5},{4,2},{5,3},{6,0},{7,1},{8,14},{9,15},{10,... | collective-permute-start | bytes 196616 | tf_op jit(solution)/shard_map/ppermute | solution.py:74
  31.8 4.3 %collective-permute-start.6 = (f32[16,1024]{1,0:T(8,128)S(1)}, f32[16,1024]{1,0:T(8,128)S(1)}, u32[]{:S(2)}, u32[]{:S(2)}) collective-permute-start(f32[16,1024]{1,0:T(8,128)S(1)} %dynamic-slice_add_fusion.2), channel_id=1, source_target_pairs={{0,2},{1,3},{2,0},{3,1},{4,6},{5,7},{6,4},{7,5},{8,10},{9,11},{10,... | collective-permute-start | bytes 196616 | tf_op jit(solution)/shard_map/ppermute | solution.py:74
  36.1 5.3 %collective-permute-start.10 = (f32[16,1024]{1,0:T(8,128)S(1)}, f32[16,1024]{1,0:T(8,128)S(1)}, u32[]{:S(2)}, u32[]{:S(2)}) collective-permute-start(f32[16,1024]{1,0:T(8,128)S(1)} %add_add_fusion.3), channel_id=1, source_target_pairs={{0,16},{1,17},{2,18},{3,19},{4,20},{5,21},{6,22},{7,23},{8,24},{9,... | collective-permute-start | bytes 196616 | tf_op jit(solution)/shard_map/ppermute | solution.py:74
  38.7 6.2 %collective-permute-start.11 = (f32[16,1024]{1,0:T(8,128)S(1)}, f32[16,1024]{1,0:T(8,128)S(1)}, u32[]{:S(2)}, u32[]{:S(2)}) collective-permute-start(f32[16,1024]{1,0:T(8,128)S(1)} %add_add_fusion.3), channel_id=1, source_target_pairs={{0,24},{1,25},{2,26},{3,27},{4,28},{5,29},{6,30},{7,31},{8,16},{9,... | collective-permute-start | bytes 196616 | tf_op jit(solution)/shard_map/ppermute | solution.py:74
  40.1 5.0 %collective-permute-start.9 = (f32[16,1024]{1,0:T(8,128)S(1)}, f32[16,1024]{1,0:T(8,128)S(1)}, u32[]{:S(2)}, u32[]{:S(2)}) collective-permute-start(f32[16,1024]{1,0:T(8,128)S(1)} %add_add_fusion.3), channel_id=1, source_target_pairs={{0,8},{1,9},{2,10},{3,11},{4,12},{5,13},{6,14},{7,15},{8,0},{9,1},... | collective-permute-start | bytes 196616 | tf_op jit(solution)/shard_map/ppermute | solution.py:74
  45.1 1.3 %collective-permute-start.12 = (f32[16,1024]{1,0:T(8,128)S(1)}, f32[16,1024]{1,0:T(8,128)S(1)}, u32[]{:S(2)}, u32[]{:S(2)}) collective-permute-start(f32[16,1024]{1,0:T(8,128)S(1)} %get-tuple-element.18), channel_id=1, source_target_pairs={{0,1},{1,0},{2,3},{3,2},{4,5},{5,4},{6,7},{7,6},{8,9},{9,8},{10,11... | collective-permute-start | bytes 196616 | tf_op jit(solution)/shard_map/ppermute | solution.py:74
  54.2 6.7 %collective-permute-start.14 = (f32[32,384]{1,0:T(8,128)S(1)}, f32[32,384]{1,0:T(8,128)S(1)}, u32[]{:S(2)}, u32[]{:S(2)}) collective-permute-start(f32[32,384]{1,0:T(8,128)S(1)} %fusion.55), channel_id=1, source_target_pairs={{0,16},{8,24},{16,0},{24,8},{1,17},{9,25},{17,1},{25,9},{2,18},{10... | collective-permute-start | bytes 147464 | tf_op jit(solution)/shard_map/ppermute | solution.py:23
  56.4 6.1 %collective-permute-start.15 = (f32[32,384]{1,0:T(8,128)S(1)}, f32[32,384]{1,0:T(8,128)S(1)}, u32[]{:S(2)}, u32[]{:S(2)}) collective-permute-start(f32[32,384]{1,0:T(8,128)S(1)} %fusion.55), channel_id=1, source_target_pairs={{0,24},{8,16},{16,8},{24,0},{1,25},{9,17},{17,9},{25,1},{2,26},{10... | collective-permute-start | bytes 147464 | tf_op jit(solution)/shard_map/ppermute | solution.py:23
  56.9 5.6 %collective-permute-start.13 = (f32[32,384]{1,0:T(8,128)S(1)}, f32[32,384]{1,0:T(8,128)S(1)}, u32[]{:S(2)}, u32[]{:S(2)}) collective-permute-start(f32[32,384]{1,0:T(8,128)S(1)} %fusion.55), channel_id=1, source_target_pairs={{0,8},{8,0},{16,24},{24,16},{1,9},{9,1},{17,25},{25,17},{2,10},{10... | collective-permute-start | bytes 147464 | tf_op jit(solution)/shard_map/ppermute | solution.py:23
  63.3 1.3 %collective-permute-start.16 = (f32[16,1024]{1,0:T(8,128)S(1)}, f32[16,1024]{1,0:T(8,128)S(1)}, u32[]{:S(2)}, u32[]{:S(2)}) collective-permute-start(f32[16,1024]{1,0:T(8,128)S(1)} %constant_dynamic-slice_fusion.1), channel_id=1, source_target_pairs={{0,1},{1,0},{2,3},{3,2},{4,5},{5,4},{6,7},{7,6},{8,9},{9,8},{10,11... | collective-permute-start | bytes 196616 | tf_op jit(solution)/shard_map/ppermute | solution.py:74
  64.2 13.8 %collective-permute-start.27 = (f32[2,400,128]{2,1,0:T(8,128)}, f32[2,400,128]{2,1,0:T(8,128)}, u32[]{:S(2)}, u32[]{:S(2)}) collective-permute-start(f32[2,400,128]{2,1,0:T(8,128)} %dynamic-slice_bitcast_fusion), channel_id=1, source_target_pairs={{0,8},{8,0},{16,24},{24,16},{1,9},{9,1},{17,25},{25,17},{2,10},{10... | collective-permute-start | bytes 1228808 | tf_op jit(solution)/shard_map/ppermute | solution.py:121
  64.6 5.0 %collective-permute-start.18 = (f32[16,1024]{1,0:T(8,128)S(1)}, f32[16,1024]{1,0:T(8,128)S(1)}, u32[]{:S(2)}, u32[]{:S(2)}) collective-permute-start(f32[16,1024]{1,0:T(8,128)S(1)} %dynamic-slice_add_fusion.1), channel_id=1, source_target_pairs={{0,4},{1,5},{2,6},{3,7},{4,0},{5,1},{6,2},{7,3},{8,12},{9,13},{10,... | collective-permute-start | bytes 196616 | tf_op jit(solution)/shard_map/ppermute | solution.py:74
  65.5 5.7 %collective-permute-start.19 = (f32[16,1024]{1,0:T(8,128)S(1)}, f32[16,1024]{1,0:T(8,128)S(1)}, u32[]{:S(2)}, u32[]{:S(2)}) collective-permute-start(f32[16,1024]{1,0:T(8,128)S(1)} %dynamic-slice_add_fusion.1), channel_id=1, source_target_pairs={{0,6},{1,7},{2,4},{3,5},{4,2},{5,3},{6,0},{7,1},{8,14},{9,15},{10,... | collective-permute-start | bytes 196616 | tf_op jit(solution)/shard_map/ppermute | solution.py:74
  67.3 4.3 %collective-permute-start.17 = (f32[16,1024]{1,0:T(8,128)S(1)}, f32[16,1024]{1,0:T(8,128)S(1)}, u32[]{:S(2)}, u32[]{:S(2)}) collective-permute-start(f32[16,1024]{1,0:T(8,128)S(1)} %dynamic-slice_add_fusion.1), channel_id=1, source_target_pairs={{0,2},{1,3},{2,0},{3,1},{4,6},{5,7},{6,4},{7,5},{8,10},{9,11},{10,... | collective-permute-start | bytes 196616 | tf_op jit(solution)/shard_map/ppermute | solution.py:74
  71.6 7.5 %collective-permute-start.21 = (f32[16,1024]{1,0:T(8,128)S(1)}, f32[16,1024]{1,0:T(8,128)S(1)}, u32[]{:S(2)}, u32[]{:S(2)}) collective-permute-start(f32[16,1024]{1,0:T(8,128)S(1)} %add_add_fusion.1), channel_id=1, source_target_pairs={{0,16},{1,17},{2,18},{3,19},{4,20},{5,21},{6,22},{7,23},{8,24},{9,... | collective-permute-start | bytes 196616 | tf_op jit(solution)/shard_map/ppermute | solution.py:74
  74.1 6.6 %collective-permute-start.22 = (f32[16,1024]{1,0:T(8,128)S(1)}, f32[16,1024]{1,0:T(8,128)S(1)}, u32[]{:S(2)}, u32[]{:S(2)}) collective-permute-start(f32[16,1024]{1,0:T(8,128)S(1)} %add_add_fusion.1), channel_id=1, source_target_pairs={{0,24},{1,25},{2,26},{3,27},{4,28},{5,29},{6,30},{7,31},{8,16},{9,... | collective-permute-start | bytes 196616 | tf_op jit(solution)/shard_map/ppermute | solution.py:74
  75.7 5.1 %collective-permute-start.20 = (f32[16,1024]{1,0:T(8,128)S(1)}, f32[16,1024]{1,0:T(8,128)S(1)}, u32[]{:S(2)}, u32[]{:S(2)}) collective-permute-start(f32[16,1024]{1,0:T(8,128)S(1)} %add_add_fusion.1), channel_id=1, source_target_pairs={{0,8},{1,9},{2,10},{3,11},{4,12},{5,13},{6,14},{7,15},{8,0},{9,1},... | collective-permute-start | bytes 196616 | tf_op jit(solution)/shard_map/ppermute | solution.py:74
  81.0 13.0 %copy-start.11 = (f32[400,128]{1,0:T(8,128)S(1)}, f32[400,128]{1,0:T(8,128)}, u32[]{:S(2)}) copy-start(f32[400,128]{1,0:T(8,128)} %param.22) | copy-start | bytes 614404
  81.0 1.4 %collective-permute-start.23 = (f32[16,1024]{1,0:T(8,128)S(1)}, f32[16,1024]{1,0:T(8,128)S(1)}, u32[]{:S(2)}, u32[]{:S(2)}) collective-permute-start(f32[16,1024]{1,0:T(8,128)S(1)} %get-tuple-element.16), channel_id=1, source_target_pairs={{0,1},{1,0},{2,3},{3,2},{4,5},{5,4},{6,7},{7,6},{8,9},{9,8},{10,11... | collective-permute-start | bytes 196616 | tf_op jit(solution)/shard_map/ppermute | solution.py:74
  81.1 12.8 %collective-permute-start.28 = (f32[1,400,128]{2,1,0:T(8,128)S(1)}, f32[1,400,128]{2,1,0:T(8,128)S(1)}, u32[]{:S(2)}, u32[]{:S(2)}) collective-permute-start(f32[1,400,128]{2,1,0:T(8,128)S(1)} %constant_dynamic-slice_fusion), channel_id=1, source_target_pairs={{0,16},{8,24},{16,0},{24,8},{1,17},{9,25},{17,1},{25,9},{2,18},{10... | collective-permute-start | bytes 614408 | tf_op jit(solution)/shard_map/ppermute | solution.py:121
  90.2 7.1 %collective-permute-start.25 = (f32[32,384]{1,0:T(8,128)S(1)}, f32[32,384]{1,0:T(8,128)S(1)}, u32[]{:S(2)}, u32[]{:S(2)}) collective-permute-start(f32[32,384]{1,0:T(8,128)S(1)} %fusion.56), channel_id=1, source_target_pairs={{0,16},{8,24},{16,0},{24,8},{1,17},{9,25},{17,1},{25,9},{2,18},{10... | collective-permute-start | bytes 147464 | tf_op jit(solution)/shard_map/ppermute | solution.py:23
  92.0 6.1 %collective-permute-start.26 = (f32[32,384]{1,0:T(8,128)S(1)}, f32[32,384]{1,0:T(8,128)S(1)}, u32[]{:S(2)}, u32[]{:S(2)}) collective-permute-start(f32[32,384]{1,0:T(8,128)S(1)} %fusion.56), channel_id=1, source_target_pairs={{0,24},{8,16},{16,8},{24,0},{1,25},{9,17},{17,9},{25,1},{2,26},{10... | collective-permute-start | bytes 147464 | tf_op jit(solution)/shard_map/ppermute | solution.py:23
  93.9 4.7 %collective-permute-start.24 = (f32[32,384]{1,0:T(8,128)S(1)}, f32[32,384]{1,0:T(8,128)S(1)}, u32[]{:S(2)}, u32[]{:S(2)}) collective-permute-start(f32[32,384]{1,0:T(8,128)S(1)} %fusion.56), channel_id=1, source_target_pairs={{0,8},{8,0},{16,24},{24,16},{1,9},{9,1},{17,25},{25,17},{2,10},{10... | collective-permute-start | bytes 147464 | tf_op jit(solution)/shard_map/ppermute | solution.py:23
  98.6 2.0 %copy-start.13 = (f32[32,384]{1,0:T(8,128)}, f32[32,384]{1,0:T(8,128)S(1)}, u32[]{:S(2)}) copy-start(f32[32,384]{1,0:T(8,128)S(1)} %add_multiply_fusion) | copy-start | bytes 147460
  99.5 1.2 copy-start.9
  99.5 1.2 copy-start.10

commit v20 on v19

--- a/solution.py
+++ b/solution.py
@@ -47,18 +47,22 @@
 
     from_x = exchange(block, 2)
     from_y = exchange(block, 4)
+    partner = exchange(block, 1)
     half = block.shape[0] // 2
     diagonal = jnp.concatenate(
         [exchange(from_y[:half], 2), exchange(from_x[half:], 4)], axis=0
     )
     mine = jnp.stack([block, from_x, from_y, diagonal])
-    other = exchange(mine, 1)
+    other = exchange(jnp.stack([from_x, from_y, diagonal]), 1)
     rows = block.shape[0]
     grads = out_grads.reshape(count, rows, out_grads.shape[1])
     even = jnp.stack([grads[me ^ offset] for offset in (0, 2, 4, 6)])
-    odd = jnp.stack([grads[me ^ offset] for offset in (1, 3, 5, 7)])
+    odd = jnp.stack([grads[me ^ offset] for offset in (3, 5, 7)])
     contract = (((0, 1), (0, 1)), ((), ()))
     first = lax.dot_general(mine, even, contract, preferred_element_type=jnp.float32)
+    first = first + lax.dot_general(
+        partner, grads[me ^ 1], (((0,), (0,)), ((), ())), preferred_element_type=jnp.float32
+    )
     return first, (other, odd)
 
 

time: 121 us -> 123 us (1.017)
  matrix products: 10.6 us -> 14.4 us
  local copies, waits for them, and re-layouts: 4.38 us -> 2.83 us
    dynamic_slice x1, local copies, waits for them, and re-layouts: 1.61 us -> 0.11 us  [replica_product(): odd = jnp.stack([grads[me ^ offset] for offset in (3, 5, 7)])]
    dot_general x0 -> x1, matrix products: none -> 1.49 us  [replica_product(): lax.dot_general(partner, grads[me ^ 1], (((0,), (0,)), ((), ())), preferr...]
    ppermute x5 -> x6, starting transfers between devices: 7.91 us -> 8.48 us  [exchange(): return lax.ppermute(value, axis, [(i, i ^ stride) for i in range(count)])]
    ppermute x5 -> x6, waiting for transfers between devices: 12 us -> 12 us  [exchange(): return lax.ppermute(value, axis, [(i, i ^ stride) for i in range(count)])]
  transfers between devices with their start and end apart: 29 -> 30, of which waited for: 21 -> 22; matrix products, arithmetic and copies ran while one was open for 15% -> 16% of each run, Pallas kernels for 0% -> 0%
where the time goes in v20:
time: 123 us
  waiting for transfers between devices  35 us (28%)
  starting transfers between devices  33 us (27%)
  other arithmetic  18.6 us (15%)
  blocking collectives  18 us (15%)
  matrix products  14.4 us (12%)
  local copies, waits for them, and re-layouts  2.83 us (2%)
    all_gather x1, blocking collectives, shards(): lax.all_gather(master_new.astype(jnp.bfloat16), 'rep', axis=0, tiled=True)  18 us
    ppermute x16, starting transfers between devices, exchange(): return lax.ppermute(piece, axes, [(i, i ^ stride) for i in range(count)])  15.8 us
    ppermute x16, waiting for transfers between devices, exchange(): return lax.ppermute(piece, axes, [(i, i ^ stride) for i in range(count)])  14.9 us
    ppermute x6, waiting for transfers between devices, exchange(): return lax.ppermute(value, axis, [(i, i ^ stride) for i in range(count)])  12 us
    ppermute x6, starting transfers between devices, exchange(): return lax.ppermute(value, axis, [(i, i ^ stride) for i in range(count)])  8.48 us
    ppermute x6, starting transfers between devices, exchange(): return lax.ppermute(value, axes, [(i, i ^ stride) for i in range(count)])  7.36 us
    another operation x6, other arithmetic, shards(): factor_low = lax.linalg.cholesky(gram_matrix, symmetrize_input=False)  7.18 us
    another operation x4, other arithmetic, shards(): jax.scipy.linalg.solve_triangular(factor_low, left_rows, lower=True)  6.17 us
  transfers between devices with their start and end apart: 30, of which 22 were waited for; matrix products, arithmetic and copies ran while one was open for 16% of the time, Pallas kernels for 0%

profile of v20, /device:TPU:0, one launch (start us, length us, event | category | flops | bytes accessed | tf_op | source)
XLA Modules:
  0.0 122.9 jit_solution(10224354819074034631)
XLA Ops:
  0.6 3.0 %collective-permute-start = (bf16[192,1024]{1,0:T(8,128)(2,1)}, bf16[192,1024]{1,0:T(8,128)(2,1)S(1)}, u32[]{:S(2)}, u32[]{:S(2)}) collective-permute-start(bf16[192,1024]{1,0:T(8,128)(2,1)} %param.13), channel_id=1, source_target_pairs={{0,2},{1,3},{2,0},{3,1},{4,6},{5,7},{6,4},{7,5},{8,10},{9,11},{10,... | collective-permute-start | bytes 1179656 | tf_op jit(solution)/shard_map/ppermute | solution.py:46
  3.7 1.5 %collective-permute-start.1 = (bf16[192,1024]{1,0:T(8,128)(2,1)}, bf16[192,1024]{1,0:T(8,128)(2,1)S(1)}, u32[]{:S(2)}, u32[]{:S(2)}) collective-permute-start(bf16[192,1024]{1,0:T(8,128)(2,1)} %param.13), channel_id=1, source_target_pairs={{0,4},{1,5},{2,6},{3,7},{4,0},{5,1},{6,2},{7,3},{8,12},{9,13},{10,... | collective-permute-start | bytes 1179656 | tf_op jit(solution)/shard_map/ppermute | solution.py:46
  5.2 7.8 %collective-permute-done = bf16[192,1024]{1,0:T(8,128)(2,1)S(1)} collective-permute-done((bf16[192,1024]{1,0:T(8,128)(2,1)}, bf16[192,1024]{1,0:T(8,128)(2,1)S(1)}, u32[]{:S(2)}, u32[]{:S(2)}) %collective-permute-start) | collective-permute-done | bytes 393248 | tf_op jit(solution)/shard_map/ppermute | solution.py:46
  13.0 1.8 %collective-permute-start.3 = (bf16[96,1024]{1,0:T(8,128)(2,1)S(1)}, bf16[96,1024]{1,0:T(8,128)(2,1)S(1)}, u32[]{:S(2)}, u32[]{:S(2)}) collective-permute-start(bf16[96,1024]{1,0:T(8,128)(2,1)S(1)} %slice.15), channel_id=1, source_target_pairs={{0,4},{1,5},{2,6},{3,7},{4,0},{5,1},{6,2},{7,3},{8,12},{9,13},{10,... | collective-permute-start | bytes 589832 | tf_op jit(solution)/shard_map/ppermute | solution.py:46
  14.9 1.6 %collective-permute-start.2 = (bf16[96,1024]{1,0:T(8,128)(2,1)S(1)}, bf16[96,1024]{1,0:T(8,128)(2,1)S(1)}, u32[]{:S(2)}, u32[]{:S(2)}) collective-permute-start(bf16[96,1024]{1,0:T(8,128)(2,1)S(1)} %slice.14), channel_id=1, source_target_pairs={{0,2},{1,3},{2,0},{3,1},{4,6},{5,7},{6,4},{7,5},{8,10},{9,11},{10,... | collective-permute-start | bytes 589832 | tf_op jit(solution)/shard_map/ppermute | solution.py:46
  16.4 2.7 %collective-permute-done.3 = bf16[96,1024]{1,0:T(8,128)(2,1)S(1)} collective-permute-done((bf16[96,1024]{1,0:T(8,128)(2,1)S(1)}, bf16[96,1024]{1,0:T(8,128)(2,1)S(1)}, u32[]{:S(2)}, u32[]{:S(2)}) %collective-permute-start.3) | collective-permute-done | bytes 196640 | tf_op jit(solution)/shard_map/ppermute | solution.py:46
  19.1 1.4 %collective-permute-done.2 = bf16[96,1024]{1,0:T(8,128)(2,1)S(1)} collective-permute-done((bf16[96,1024]{1,0:T(8,128)(2,1)S(1)}, bf16[96,1024]{1,0:T(8,128)(2,1)S(1)}, u32[]{:S(2)}, u32[]{:S(2)}) %collective-permute-start.2) | collective-permute-done | bytes 196640 | tf_op jit(solution)/shard_map/ppermute | solution.py:46
  21.5 0.9 copy-done.3
  22.4 2.1 %fusion.2 = f32[1024,384,1]{1,0,2:T(8,128)S(1)} fusion(bf16[1,192,1024]{2,1,0:T(8,128)(2,1)S(1)} %maximum_bitcast_fusion, bf16[1,192,1024]{2,1,0:T(8,128)(2,1)S(1)} %bitcast.66, bf16[1,192,1024]{2,1,0:T(8,128)(2,1)S(1)} %bitcast.64, bf16[1,192,1024]{2,1,0:T(8,128)(2,1)} %bitcast, bf16[1,192,384]{2,1,0:T(8,128)(2,1)S(1)} %get-tuple-element.22, ...), kind=kOutput, calls=%fused_computation.5 | convolution fusion | flops 607223808 | bytes 3735552 | tf_op jit(solution)/shard_map/dot_general | solution.py:62
  24.5 1.5 %convert_add_fusion = f32[1024,384]{1,0:T(8,128)S(1)} fusion(f32[1024,384,1]{1,0,2:T(8,128)S(1)} %fusion.2, bf16[192,1024]{1,0:T(8,128)(2,1)} %collective-permute-done.4, bf16[1,1024,384]{2,1,0:T(8,128)(2,1)S(1)} %copy-done.4, bf16[8,192,384]{2,1,0:T(8,128)(2,1)S(1)} %bitcast.62, s32[]{:T(128)S(6)} %select_n.89), kind=kOutput, calls=%fused_computation.13 | convolution fusion | flops 152174592 | bytes 4472836 | tf_op jit(solution)/shard_map/dot_general | solution.py:63
  26.0 0.8 convolution_bitcast_fusion
  26.8 2.2 %bitcast_add_fusion = (f32[1024,384]{1,0:T(8,128)S(1)}, f32[1024,384,1]{1,0,2:T(8,128)S(1)}) fusion(f32[1024,384]{1,0:T(8,128)S(1)} %convert_add_fusion, bf16[3,192,1024]{2,1,0:T(8,128)(2,1)} %collective-permute-done.5, bf16[1,192,384]{2,1,0:T(8,128)(2,1)S(1)} %get-tuple-element.20, bf16[1,192,384]{2,1,0:T(8,128)(2,1)S(1)} %get-tuple-element.21, ...), kind=kOutput, calls=%fused_computation.16 | convolution fusion | flops 453820416 | bytes 6340608 | tf_op jit(solution)/shard_map/dot_general | solution.py:190
  29.1 0.8 fusion.12
  30.2 1.2 collective-permute-done.6
  31.3 1.2 collective-permute-start.8
  32.5 1.8 %collective-permute-start.9 = (f32[16,1024]{1,0:T(8,128)S(1)}, f32[16,1024]{1,0:T(8,128)S(1)}, u32[]{:S(2)}, u32[]{:S(2)}) collective-permute-start(f32[16,1024]{1,0:T(8,128)S(1)} %dynamic-slice_add_fusion.2), channel_id=1, source_target_pairs={{0,6},{1,7},{2,4},{3,5},{4,2},{5,3},{6,0},{7,1},{8,14},{9,15},{10,... | collective-permute-start | bytes 196616 | tf_op jit(solution)/shard_map/ppermute | solution.py:78
  35.7 2.3 %collective-permute-done.9 = f32[16,1024]{1,0:T(8,128)S(1)} collective-permute-done((f32[16,1024]{1,0:T(8,128)S(1)}, f32[16,1024]{1,0:T(8,128)S(1)}, u32[]{:S(2)}, u32[]{:S(2)}) %collective-permute-start.9) | collective-permute-done | bytes 65568 | tf_op jit(solution)/shard_map/ppermute | solution.py:78
  38.6 2.7 %collective-permute-start.11 = (f32[16,1024]{1,0:T(8,128)S(1)}, f32[16,1024]{1,0:T(8,128)S(1)}, u32[]{:S(2)}, u32[]{:S(2)}) collective-permute-start(f32[16,1024]{1,0:T(8,128)S(1)} %add_add_fusion.3), channel_id=1, source_target_pairs={{0,16},{1,17},{2,18},{3,19},{4,20},{5,21},{6,22},{7,23},{8,24},{9,... | collective-permute-start | bytes 196616 | tf_op jit(solution)/shard_map/ppermute | solution.py:78
  41.3 1.4 %collective-permute-start.12 = (f32[16,1024]{1,0:T(8,128)S(1)}, f32[16,1024]{1,0:T(8,128)S(1)}, u32[]{:S(2)}, u32[]{:S(2)}) collective-permute-start(f32[16,1024]{1,0:T(8,128)S(1)} %add_add_fusion.3), channel_id=1, source_target_pairs={{0,24},{1,25},{2,26},{3,27},{4,28},{5,29},{6,30},{7,31},{8,16},{9,... | collective-permute-start | bytes 196616 | tf_op jit(solution)/shard_map/ppermute | solution.py:78
  42.9 1.1 collective-permute-done.11
  43.9 3.6 %collective-permute-done.12 = f32[16,1024]{1,0:T(8,128)S(1)} collective-permute-done((f32[16,1024]{1,0:T(8,128)S(1)}, f32[16,1024]{1,0:T(8,128)S(1)}, u32[]{:S(2)}, u32[]{:S(2)}) %collective-permute-start.12) | collective-permute-done | bytes 65568 | tf_op jit(solution)/shard_map/ppermute | solution.py:78
  47.8 1.1 select_reduce_fusion
  49.2 2.9 %custom-call.8 = f32[32,32]{1,0:T(8,128)S(1)} custom-call(f32[32,32]{1,0:T(8,128)S(1)} %fusion.37), custom_call_target="Cholesky" | custom-call | tf_op jit(solution)/shard_map/cholesky/custom-call.1 | solution.py:198
  53.4 2.4 %custom-call.9 = f32[1,32,32]{1,2,0:T(8,128)S(1)} custom-call(f32[1,32,32]{2,1,0:T(8,128)S(1)} %fusion.49), custom_call_target="InvertDiagBlocksLowerTriangular" | custom-call | tf_op jit(solution)/shard_map/jit(_solve_triangular)/triangular_solve | solution.py:199
  56.8 2.2 %collective-permute-start.15 = (f32[32,384]{1,0:T(8,128)S(1)}, f32[32,384]{1,0:T(8,128)S(1)}, u32[]{:S(2)}, u32[]{:S(2)}) collective-permute-start(f32[32,384]{1,0:T(8,128)S(1)} %fusion.64), channel_id=1, source_target_pairs={{0,16},{8,24},{16,0},{24,8},{1,17},{9,25},{17,1},{25,9},{2,18},{10... | collective-permute-start | bytes 147464 | tf_op jit(solution)/shard_map/ppermute | solution.py:23
  59.4 0.9 collective-permute-start.14
  60.4 3.1 %fusion = f32[1600,128]{1,0:T(8,128)S(1)} fusion(bf16[1536,128]{1,0:T(8,128)(2,1)S(1)} %copy-done, s32[1536]{0:T(1024)S(1)} %select_reduce_fusion), kind=kOutput, calls=%fused_computation.1 | convolution fusion | flops 631603200 | bytes 1218560 | tf_op jit(solution)/shard_map/dot_general | solution.py:113
  63.5 1.6 %collective-permute-done.16 = f32[32,384]{1,0:T(8,128)S(1)} collective-permute-done((f32[32,384]{1,0:T(8,128)S(1)}, f32[32,384]{1,0:T(8,128)S(1)}, u32[]{:S(2)}, u32[]{:S(2)}) %collective-permute-start.16) | collective-permute-done | bytes 49184 | tf_op jit(solution)/shard_map/ppermute | solution.py:23
  67.6 1.8 %collective-permute-start.20 = (f32[16,1024]{1,0:T(8,128)S(1)}, f32[16,1024]{1,0:T(8,128)S(1)}, u32[]{:S(2)}, u32[]{:S(2)}) collective-permute-start(f32[16,1024]{1,0:T(8,128)S(1)} %dynamic-slice_add_fusion.1), channel_id=1, source_target_pairs={{0,6},{1,7},{2,4},{3,5},{4,2},{5,3},{6,0},{7,1},{8,14},{9,15},{10,... | collective-permute-start | bytes 196616 | tf_op jit(solution)/shard_map/ppermute | solution.py:78
  69.4 1.3 %collective-permute-start.18 = (f32[16,1024]{1,0:T(8,128)S(1)}, f32[16,1024]{1,0:T(8,128)S(1)}, u32[]{:S(2)}, u32[]{:S(2)}) collective-permute-start(f32[16,1024]{1,0:T(8,128)S(1)} %dynamic-slice_add_fusion.1), channel_id=1, source_target_pairs={{0,2},{1,3},{2,0},{3,1},{4,6},{5,7},{6,4},{7,5},{8,10},{9,11},{10,... | collective-permute-start | bytes 196616 | tf_op jit(solution)/shard_map/ppermute | solution.py:78
  70.8 1.6 %collective-permute-done.19 = f32[16,1024]{1,0:T(8,128)S(1)} collective-permute-done((f32[16,1024]{1,0:T(8,128)S(1)}, f32[16,1024]{1,0:T(8,128)S(1)}, u32[]{:S(2)}, u32[]{:S(2)}) %collective-permute-start.19) | collective-permute-done | bytes 65568 | tf_op jit(solution)/shard_map/ppermute | solution.py:78
  73.1 0.9 collective-permute-done.18
  74.0 2.5 %collective-permute-start.22 = (f32[16,1024]{1,0:T(8,128)S(1)}, f32[16,1024]{1,0:T(8,128)S(1)}, u32[]{:S(2)}, u32[]{:S(2)}) collective-permute-start(f32[16,1024]{1,0:T(8,128)S(1)} %add_add_fusion.1), channel_id=1, source_target_pairs={{0,16},{1,17},{2,18},{3,19},{4,20},{5,21},{6,22},{7,23},{8,24},{9,... | collective-permute-start | bytes 196616 | tf_op jit(solution)/shard_map/ppermute | solution.py:78
  76.6 1.5 %collective-permute-start.23 = (f32[16,1024]{1,0:T(8,128)S(1)}, f32[16,1024]{1,0:T(8,128)S(1)}, u32[]{:S(2)}, u32[]{:S(2)}) collective-permute-start(f32[16,1024]{1,0:T(8,128)S(1)} %add_add_fusion.1), channel_id=1, source_target_pairs={{0,24},{1,25},{2,26},{3,27},{4,28},{5,29},{6,30},{7,31},{8,16},{9,... | collective-permute-start | bytes 196616 | tf_op jit(solution)/shard_map/ppermute | solution.py:78
  78.1 2.6 %collective-permute-done.28 = f32[2,400,128]{2,1,0:T(8,128)} collective-permute-done((f32[2,400,128]{2,1,0:T(8,128)}, f32[2,400,128]{2,1,0:T(8,128)}, u32[]{:S(2)}, u32[]{:S(2)}) %collective-permute-start.28) | collective-permute-done | bytes 409632 | tf_op jit(solution)/shard_map/ppermute | solution.py:125
  80.7 1.0 bitcast_add_fusion.2
  81.8 1.5 %collective-permute-done.23 = f32[16,1024]{1,0:T(8,128)S(1)} collective-permute-done((f32[16,1024]{1,0:T(8,128)S(1)}, f32[16,1024]{1,0:T(8,128)S(1)}, u32[]{:S(2)}, u32[]{:S(2)}) %collective-permute-start.23) | collective-permute-done | bytes 65568 | tf_op jit(solution)/shard_map/ppermute | solution.py:78
  83.5 1.2 %collective-permute-start.29 = (f32[1,400,128]{2,1,0:T(8,128)S(1)}, f32[1,400,128]{2,1,0:T(8,128)S(1)}, u32[]{:S(2)}, u32[]{:S(2)}) collective-permute-start(f32[1,400,128]{2,1,0:T(8,128)S(1)} %constant_dynamic-slice_fusion), channel_id=1, source_target_pairs={{0,16},{8,24},{16,0},{24,8},{1,17},{9,25},{17,1},{25,9},{2,18},{10... | collective-permute-start | bytes 614408 | tf_op jit(solution)/shard_map/ppermute | solution.py:125
  85.0 2.9 %custom-call.10 = f32[32,32]{1,0:T(8,128)S(1)} custom-call(f32[32,32]{1,0:T(8,128)S(1)} %fusion.33), custom_call_target="Cholesky" | custom-call | tf_op jit(solution)/shard_map/cholesky/custom-call.1 | solution.py:198
  89.2 2.4 %custom-call.11 = f32[1,32,32]{1,2,0:T(8,128)S(1)} custom-call(f32[1,32,32]{2,1,0:T(8,128)S(1)} %fusion.50), custom_call_target="InvertDiagBlocksLowerTriangular" | custom-call | tf_op jit(solution)/shard_map/jit(_solve_triangular)/triangular_solve | solution.py:199
  92.5 1.8 %collective-permute-start.26 = (f32[32,384]{1,0:T(8,128)S(1)}, f32[32,384]{1,0:T(8,128)S(1)}, u32[]{:S(2)}, u32[]{:S(2)}) collective-permute-start(f32[32,384]{1,0:T(8,128)S(1)} %fusion.65), channel_id=1, source_target_pairs={{0,16},{8,24},{16,0},{24,8},{1,17},{9,25},{17,1},{25,9},{2,18},{10... | collective-permute-start | bytes 147464 | tf_op jit(solution)/shard_map/ppermute | solution.py:23
  94.4 2.0 %collective-permute-start.27 = (f32[32,384]{1,0:T(8,128)S(1)}, f32[32,384]{1,0:T(8,128)S(1)}, u32[]{:S(2)}, u32[]{:S(2)}) collective-permute-start(f32[32,384]{1,0:T(8,128)S(1)} %fusion.65), channel_id=1, source_target_pairs={{0,24},{8,16},{16,8},{24,0},{1,25},{9,17},{17,9},{25,1},{2,26},{10... | collective-permute-start | bytes 147464 | tf_op jit(solution)/shard_map/ppermute | solution.py:23
  97.1 2.6 %collective-permute-done.26 = f32[32,384]{1,0:T(8,128)S(1)} collective-permute-done((f32[32,384]{1,0:T(8,128)S(1)}, f32[32,384]{1,0:T(8,128)S(1)}, u32[]{:S(2)}, u32[]{:S(2)}) %collective-permute-start.26) | collective-permute-done | bytes 49184 | tf_op jit(solution)/shard_map/ppermute | solution.py:23
  101.0 0.8 fusion.66
  101.9 1.1 fusion.15
  103.0 1.0 fusion.63
  104.0 18.0 %all_gather.3 = bf16[1024,384]{1,0:T(8,128)(2,1)S(1)} all-gather(bf16[256,384]{1,0:T(8,128)(2,1)S(1)} %get-tuple-element.12), channel_id=1, replica_groups=mesh['rep'=4,'tp'=8] {'rep'}, dimensions={0}, use_global_device_ids=true | all-gather | bytes 983040 | tf_op jit(solution)/shard_map/all_gather | solution.py:213
  122.0 0.9 copy.24
  (88 shorter events, 14.4 us)
Async XLA Ops:
  0.6 59.7 %copy-start = (bf16[1536,128]{1,0:T(8,128)(2,1)S(1)}, bf16[1536,128]{1,0:T(8,128)(2,1)}, u32[]{:S(2)}) copy-start(bf16[1536,128]{1,0:T(8,128)(2,1)} %param.19) | copy-start | bytes 1179652
  0.6 12.3 %collective-permute-start = (bf16[192,1024]{1,0:T(8,128)(2,1)}, bf16[192,1024]{1,0:T(8,128)(2,1)S(1)}, u32[]{:S(2)}, u32[]{:S(2)}) collective-permute-start(bf16[192,1024]{1,0:T(8,128)(2,1)} %param.13), channel_id=1, source_target_pairs={{0,2},{1,3},{2,0},{3,1},{4,6},{5,7},{6,4},{7,5},{8,10},{9,11},{10,... | collective-permute-start | bytes 1179656 | tf_op jit(solution)/shard_map/ppermute | solution.py:46
  3.7 11.2 %collective-permute-start.1 = (bf16[192,1024]{1,0:T(8,128)(2,1)}, bf16[192,1024]{1,0:T(8,128)(2,1)S(1)}, u32[]{:S(2)}, u32[]{:S(2)}) collective-permute-start(bf16[192,1024]{1,0:T(8,128)(2,1)} %param.13), channel_id=1, source_target_pairs={{0,4},{1,5},{2,6},{3,7},{4,0},{5,1},{6,2},{7,3},{8,12},{9,13},{10,... | collective-permute-start | bytes 1179656 | tf_op jit(solution)/shard_map/ppermute | solution.py:46
  13.0 6.2 %collective-permute-start.3 = (bf16[96,1024]{1,0:T(8,128)(2,1)S(1)}, bf16[96,1024]{1,0:T(8,128)(2,1)S(1)}, u32[]{:S(2)}, u32[]{:S(2)}) collective-permute-start(bf16[96,1024]{1,0:T(8,128)(2,1)S(1)} %slice.15), channel_id=1, source_target_pairs={{0,4},{1,5},{2,6},{3,7},{4,0},{5,1},{6,2},{7,3},{8,12},{9,13},{10,... | collective-permute-start | bytes 589832 | tf_op jit(solution)/shard_map/ppermute | solution.py:46
  14.8 5.9 %copy-start.2 = (bf16[192,1024]{1,0:T(8,128)(2,1)}, bf16[192,1024]{1,0:T(8,128)(2,1)S(1)}, u32[]{:S(2)}) copy-start(bf16[192,1024]{1,0:T(8,128)(2,1)S(1)} %collective-permute-done.1) | copy-start | bytes 1179652
  14.9 6.5 %copy-start.1 = (bf16[1536,384]{1,0:T(8,128)(2,1)S(1)}, bf16[1536,384]{1,0:T(8,128)(2,1)}, u32[]{:S(2)}) copy-start(bf16[1536,384]{1,0:T(8,128)(2,1)} %param.14) | copy-start | bytes 3538948
  14.9 5.7 %collective-permute-start.2 = (bf16[96,1024]{1,0:T(8,128)(2,1)S(1)}, bf16[96,1024]{1,0:T(8,128)(2,1)S(1)}, u32[]{:S(2)}, u32[]{:S(2)}) collective-permute-start(bf16[96,1024]{1,0:T(8,128)(2,1)S(1)} %slice.14), channel_id=1, source_target_pairs={{0,2},{1,3},{2,0},{3,1},{4,6},{5,7},{6,4},{7,5},{8,10},{9,11},{10,... | collective-permute-start | bytes 589832 | tf_op jit(solution)/shard_map/ppermute | solution.py:46
  20.8 6.1 %collective-permute-start.5 = (bf16[3,192,1024]{2,1,0:T(8,128)(2,1)S(1)}, bf16[3,192,1024]{2,1,0:T(8,128)(2,1)}, u32[]{:S(2)}, u32[]{:S(2)}) collective-permute-start(bf16[3,192,1024]{2,1,0:T(8,128)(2,1)S(1)} %pad_maximum_fusion), channel_id=1, source_target_pairs={{0,1},{1,0},{2,3},{3,2},{4,5},{5,4},{6,7},{7,6},{8,9},{9,8},{10,11... | collective-permute-start | bytes 3538952 | tf_op jit(solution)/shard_map/ppermute | solution.py:46
  20.9 3.6 %collective-permute-start.4 = (bf16[192,1024]{1,0:T(8,128)(2,1)}, bf16[192,1024]{1,0:T(8,128)(2,1)}, u32[]{:S(2)}, u32[]{:S(2)}) collective-permute-start(bf16[192,1024]{1,0:T(8,128)(2,1)} %param.13), channel_id=1, source_target_pairs={{0,1},{1,0},{2,3},{3,2},{4,5},{5,4},{6,7},{7,6},{8,9},{9,8},{10,11... | collective-permute-start | bytes 1179656 | tf_op jit(solution)/shard_map/ppermute | solution.py:46
  21.4 1.0 copy-start.3
  22.4 2.1 %copy-start.4 = (bf16[1,1024,384]{2,1,0:T(8,128)(2,1)S(1)}, bf16[1,1024,384]{2,1,0:T(8,128)(2,1)}, u32[]{:S(2)}) copy-start(bf16[1,1024,384]{2,1,0:T(8,128)(2,1)} %param.15) | copy-start | bytes 2359300
  24.5 1.5 %copy-start.8 = (f32[384,32]{0,1:T(8,128)S(1)}, f32[384,32]{0,1:T(8,128)}, u32[]{:S(2)}) copy-start(f32[384,32]{0,1:T(8,128)} %param.16) | copy-start | bytes 147460
  29.1 18.6 %copy-start.10 = (s32[1600]{0:T(1024)S(1)}, s32[1600]{0:T(1024)}, u32[]{:S(2)}) copy-start(s32[1600]{0:T(1024)} %param.21) | copy-start | bytes 19204
  29.1 18.6 %copy-start.11 = (s32[1536]{0:T(1024)S(1)}, s32[1536]{0:T(1024)}, u32[]{:S(2)}) copy-start(s32[1536]{0:T(1024)} %param.20) | copy-start | bytes 18436
  30.0 1.3 %collective-permute-start.6 = (f32[16,1024]{1,0:T(8,128)S(1)}, f32[16,1024]{1,0:T(8,128)S(1)}, u32[]{:S(2)}, u32[]{:S(2)}) collective-permute-start(f32[16,1024]{1,0:T(8,128)S(1)} %constant_dynamic-slice_fusion.2), channel_id=1, source_target_pairs={{0,1},{1,0},{2,3},{3,2},{4,5},{5,4},{6,7},{7,6},{8,9},{9,8},{10,11... | collective-permute-start | bytes 196616 | tf_op jit(solution)/shard_map/ppermute | solution.py:78
  31.3 4.3 %collective-permute-start.8 = (f32[16,1024]{1,0:T(8,128)S(1)}, f32[16,1024]{1,0:T(8,128)S(1)}, u32[]{:S(2)}, u32[]{:S(2)}) collective-permute-start(f32[16,1024]{1,0:T(8,128)S(1)} %dynamic-slice_add_fusion.2), channel_id=1, source_target_pairs={{0,4},{1,5},{2,6},{3,7},{4,0},{5,1},{6,2},{7,3},{8,12},{9,13},{10,... | collective-permute-start | bytes 196616 | tf_op jit(solution)/shard_map/ppermute | solution.py:78
  32.5 5.5 %collective-permute-start.9 = (f32[16,1024]{1,0:T(8,128)S(1)}, f32[16,1024]{1,0:T(8,128)S(1)}, u32[]{:S(2)}, u32[]{:S(2)}) collective-permute-start(f32[16,1024]{1,0:T(8,128)S(1)} %dynamic-slice_add_fusion.2), channel_id=1, source_target_pairs={{0,6},{1,7},{2,4},{3,5},{4,2},{5,3},{6,0},{7,1},{8,14},{9,15},{10,... | collective-permute-start | bytes 196616 | tf_op jit(solution)/shard_map/ppermute | solution.py:78
  34.4 4.3 %collective-permute-start.7 = (f32[16,1024]{1,0:T(8,128)S(1)}, f32[16,1024]{1,0:T(8,128)S(1)}, u32[]{:S(2)}, u32[]{:S(2)}) collective-permute-start(f32[16,1024]{1,0:T(8,128)S(1)} %dynamic-slice_add_fusion.2), channel_id=1, source_target_pairs={{0,2},{1,3},{2,0},{3,1},{4,6},{5,7},{6,4},{7,5},{8,10},{9,11},{10,... | collective-permute-start | bytes 196616 | tf_op jit(solution)/shard_map/ppermute | solution.py:78
  38.6 5.3 %collective-permute-start.11 = (f32[16,1024]{1,0:T(8,128)S(1)}, f32[16,1024]{1,0:T(8,128)S(1)}, u32[]{:S(2)}, u32[]{:S(2)}) collective-permute-start(f32[16,1024]{1,0:T(8,128)S(1)} %add_add_fusion.3), channel_id=1, source_target_pairs={{0,16},{1,17},{2,18},{3,19},{4,20},{5,21},{6,22},{7,23},{8,24},{9,... | collective-permute-start | bytes 196616 | tf_op jit(solution)/shard_map/ppermute | solution.py:78
  41.3 6.2 %collective-permute-start.12 = (f32[16,1024]{1,0:T(8,128)S(1)}, f32[16,1024]{1,0:T(8,128)S(1)}, u32[]{:S(2)}, u32[]{:S(2)}) collective-permute-start(f32[16,1024]{1,0:T(8,128)S(1)} %add_add_fusion.3), channel_id=1, source_target_pairs={{0,24},{1,25},{2,26},{3,27},{4,28},{5,29},{6,30},{7,31},{8,16},{9,... | collective-permute-start | bytes 196616 | tf_op jit(solution)/shard_map/ppermute | solution.py:78
  42.6 5.0 %collective-permute-start.10 = (f32[16,1024]{1,0:T(8,128)S(1)}, f32[16,1024]{1,0:T(8,128)S(1)}, u32[]{:S(2)}, u32[]{:S(2)}) collective-permute-start(f32[16,1024]{1,0:T(8,128)S(1)} %add_add_fusion.3), channel_id=1, source_target_pairs={{0,8},{1,9},{2,10},{3,11},{4,12},{5,13},{6,14},{7,15},{8,0},{9,1},... | collective-permute-start | bytes 196616 | tf_op jit(solution)/shard_map/ppermute | solution.py:78
  47.7 1.3 %collective-permute-start.13 = (f32[16,1024]{1,0:T(8,128)S(1)}, f32[16,1024]{1,0:T(8,128)S(1)}, u32[]{:S(2)}, u32[]{:S(2)}) collective-permute-start(f32[16,1024]{1,0:T(8,128)S(1)} %get-tuple-element.18), channel_id=1, source_target_pairs={{0,1},{1,0},{2,3},{3,2},{4,5},{5,4},{6,7},{7,6},{8,9},{9,8},{10,11... | collective-permute-start | bytes 196616 | tf_op jit(solution)/shard_map/ppermute | solution.py:78
  56.8 6.7 %collective-permute-start.15 = (f32[32,384]{1,0:T(8,128)S(1)}, f32[32,384]{1,0:T(8,128)S(1)}, u32[]{:S(2)}, u32[]{:S(2)}) collective-permute-start(f32[32,384]{1,0:T(8,128)S(1)} %fusion.64), channel_id=1, source_target_pairs={{0,16},{8,24},{16,0},{24,8},{1,17},{9,25},{17,1},{25,9},{2,18},{10... | collective-permute-start | bytes 147464 | tf_op jit(solution)/shard_map/ppermute | solution.py:23
  59.0 6.1 %collective-permute-start.16 = (f32[32,384]{1,0:T(8,128)S(1)}, f32[32,384]{1,0:T(8,128)S(1)}, u32[]{:S(2)}, u32[]{:S(2)}) collective-permute-start(f32[32,384]{1,0:T(8,128)S(1)} %fusion.64), channel_id=1, source_target_pairs={{0,24},{8,16},{16,8},{24,0},{1,25},{9,17},{17,9},{25,1},{2,26},{10... | collective-permute-start | bytes 147464 | tf_op jit(solution)/shard_map/ppermute | solution.py:23
  59.4 5.6 %collective-permute-start.14 = (f32[32,384]{1,0:T(8,128)S(1)}, f32[32,384]{1,0:T(8,128)S(1)}, u32[]{:S(2)}, u32[]{:S(2)}) collective-permute-start(f32[32,384]{1,0:T(8,128)S(1)} %fusion.64), channel_id=1, source_target_pairs={{0,8},{8,0},{16,24},{24,16},{1,9},{9,1},{17,25},{25,17},{2,10},{10... | collective-permute-start | bytes 147464 | tf_op jit(solution)/shard_map/ppermute | solution.py:23
  65.9 1.3 %collective-permute-start.17 = (f32[16,1024]{1,0:T(8,128)S(1)}, f32[16,1024]{1,0:T(8,128)S(1)}, u32[]{:S(2)}, u32[]{:S(2)}) collective-permute-start(f32[16,1024]{1,0:T(8,128)S(1)} %constant_dynamic-slice_fusion.1), channel_id=1, source_target_pairs={{0,1},{1,0},{2,3},{3,2},{4,5},{5,4},{6,7},{7,6},{8,9},{9,8},{10,11... | collective-permute-start | bytes 196616 | tf_op jit(solution)/shard_map/ppermute | solution.py:78
  66.8 14.0 %collective-permute-start.28 = (f32[2,400,128]{2,1,0:T(8,128)}, f32[2,400,128]{2,1,0:T(8,128)}, u32[]{:S(2)}, u32[]{:S(2)}) collective-permute-start(f32[2,400,128]{2,1,0:T(8,128)} %dynamic-slice_bitcast_fusion), channel_id=1, source_target_pairs={{0,8},{8,0},{16,24},{24,16},{1,9},{9,1},{17,25},{25,17},{2,10},{10... | collective-permute-start | bytes 1228808 | tf_op jit(solution)/shard_map/ppermute | solution.py:125
  67.2 5.2 %collective-permute-start.19 = (f32[16,1024]{1,0:T(8,128)S(1)}, f32[16,1024]{1,0:T(8,128)S(1)}, u32[]{:S(2)}, u32[]{:S(2)}) collective-permute-start(f32[16,1024]{1,0:T(8,128)S(1)} %dynamic-slice_add_fusion.1), channel_id=1, source_target_pairs={{0,4},{1,5},{2,6},{3,7},{4,0},{5,1},{6,2},{7,3},{8,12},{9,13},{10,... | collective-permute-start | bytes 196616 | tf_op jit(solution)/shard_map/ppermute | solution.py:78
  67.6 5.5 %collective-permute-start.20 = (f32[16,1024]{1,0:T(8,128)S(1)}, f32[16,1024]{1,0:T(8,128)S(1)}, u32[]{:S(2)}, u32[]{:S(2)}) collective-permute-start(f32[16,1024]{1,0:T(8,128)S(1)} %dynamic-slice_add_fusion.1), channel_id=1, source_target_pairs={{0,6},{1,7},{2,4},{3,5},{4,2},{5,3},{6,0},{7,1},{8,14},{9,15},{10,... | collective-permute-start | bytes 196616 | tf_op jit(solution)/shard_map/ppermute | solution.py:78
  69.4 4.6 %collective-permute-start.18 = (f32[16,1024]{1,0:T(8,128)S(1)}, f32[16,1024]{1,0:T(8,128)S(1)}, u32[]{:S(2)}, u32[]{:S(2)}) collective-permute-start(f32[16,1024]{1,0:T(8,128)S(1)} %dynamic-slice_add_fusion.1), channel_id=1, source_target_pairs={{0,2},{1,3},{2,0},{3,1},{4,6},{5,7},{6,4},{7,5},{8,10},{9,11},{10,... | collective-permute-start | bytes 196616 | tf_op jit(solution)/shard_map/ppermute | solution.py:78
  74.0 7.7 %collective-permute-start.22 = (f32[16,1024]{1,0:T(8,128)S(1)}, f32[16,1024]{1,0:T(8,128)S(1)}, u32[]{:S(2)}, u32[]{:S(2)}) collective-permute-start(f32[16,1024]{1,0:T(8,128)S(1)} %add_add_fusion.1), channel_id=1, source_target_pairs={{0,16},{1,17},{2,18},{3,19},{4,20},{5,21},{6,22},{7,23},{8,24},{9,... | collective-permute-start | bytes 196616 | tf_op jit(solution)/shard_map/ppermute | solution.py:78
  76.6 6.7 %collective-permute-start.23 = (f32[16,1024]{1,0:T(8,128)S(1)}, f32[16,1024]{1,0:T(8,128)S(1)}, u32[]{:S(2)}, u32[]{:S(2)}) collective-permute-start(f32[16,1024]{1,0:T(8,128)S(1)} %add_add_fusion.1), channel_id=1, source_target_pairs={{0,24},{1,25},{2,26},{3,27},{4,28},{5,29},{6,30},{7,31},{8,16},{9,... | collective-permute-start | bytes 196616 | tf_op jit(solution)/shard_map/ppermute | solution.py:78
  78.1 5.2 %collective-permute-start.21 = (f32[16,1024]{1,0:T(8,128)S(1)}, f32[16,1024]{1,0:T(8,128)S(1)}, u32[]{:S(2)}, u32[]{:S(2)}) collective-permute-start(f32[16,1024]{1,0:T(8,128)S(1)} %add_add_fusion.1), channel_id=1, source_target_pairs={{0,8},{1,9},{2,10},{3,11},{4,12},{5,13},{6,14},{7,15},{8,0},{9,1},... | collective-permute-start | bytes 196616 | tf_op jit(solution)/shard_map/ppermute | solution.py:78
  83.3 13.0 %copy-start.7 = (f32[400,128]{1,0:T(8,128)S(1)}, f32[400,128]{1,0:T(8,128)}, u32[]{:S(2)}) copy-start(f32[400,128]{1,0:T(8,128)} %param.22) | copy-start | bytes 614404
  83.4 1.4 %collective-permute-start.24 = (f32[16,1024]{1,0:T(8,128)S(1)}, f32[16,1024]{1,0:T(8,128)S(1)}, u32[]{:S(2)}, u32[]{:S(2)}) collective-permute-start(f32[16,1024]{1,0:T(8,128)S(1)} %get-tuple-element.16), channel_id=1, source_target_pairs={{0,1},{1,0},{2,3},{3,2},{4,5},{5,4},{6,7},{7,6},{8,9},{9,8},{10,11... | collective-permute-start | bytes 196616 | tf_op jit(solution)/shard_map/ppermute | solution.py:78
  83.5 12.8 %collective-permute-start.29 = (f32[1,400,128]{2,1,0:T(8,128)S(1)}, f32[1,400,128]{2,1,0:T(8,128)S(1)}, u32[]{:S(2)}, u32[]{:S(2)}) collective-permute-start(f32[1,400,128]{2,1,0:T(8,128)S(1)} %constant_dynamic-slice_fusion), channel_id=1, source_target_pairs={{0,16},{8,24},{16,0},{24,8},{1,17},{9,25},{17,1},{25,9},{2,18},{10... | collective-permute-start | bytes 614408 | tf_op jit(solution)/shard_map/ppermute | solution.py:125
  92.5 7.1 %collective-permute-start.26 = (f32[32,384]{1,0:T(8,128)S(1)}, f32[32,384]{1,0:T(8,128)S(1)}, u32[]{:S(2)}, u32[]{:S(2)}) collective-permute-start(f32[32,384]{1,0:T(8,128)S(1)} %fusion.65), channel_id=1, source_target_pairs={{0,16},{8,24},{16,0},{24,8},{1,17},{9,25},{17,1},{25,9},{2,18},{10... | collective-permute-start | bytes 147464 | tf_op jit(solution)/shard_map/ppermute | solution.py:23
  94.4 6.0 %collective-permute-start.27 = (f32[32,384]{1,0:T(8,128)S(1)}, f32[32,384]{1,0:T(8,128)S(1)}, u32[]{:S(2)}, u32[]{:S(2)}) collective-permute-start(f32[32,384]{1,0:T(8,128)S(1)} %fusion.65), channel_id=1, source_target_pairs={{0,24},{8,16},{16,8},{24,0},{1,25},{9,17},{17,9},{25,1},{2,26},{10... | collective-permute-start | bytes 147464 | tf_op jit(solution)/shard_map/ppermute | solution.py:23
  96.3 4.7 %collective-permute-start.25 = (f32[32,384]{1,0:T(8,128)S(1)}, f32[32,384]{1,0:T(8,128)S(1)}, u32[]{:S(2)}, u32[]{:S(2)}) collective-permute-start(f32[32,384]{1,0:T(8,128)S(1)} %fusion.65), channel_id=1, source_target_pairs={{0,8},{8,0},{16,24},{24,16},{1,9},{9,1},{17,25},{25,17},{2,10},{10... | collective-permute-start | bytes 147464 | tf_op jit(solution)/shard_map/ppermute | solution.py:23
  101.0 2.0 %copy-start.9 = (f32[32,384]{1,0:T(8,128)}, f32[32,384]{1,0:T(8,128)S(1)}, u32[]{:S(2)}) copy-start(f32[32,384]{1,0:T(8,128)S(1)} %add_multiply_fusion) | copy-start | bytes 147460
  101.8 1.2 copy-start.5
  101.9 1.2 copy-start.6

commit v21 on v19

--- a/solution.py
+++ b/solution.py
@@ -87,9 +87,9 @@
         kept = kept + exchange(kept, stride)
         stride *= 2
     other = exchange(kept, 1)
-    total = jnp.zeros(value.shape, value.dtype)
-    total = lax.dynamic_update_slice_in_dim(total, kept, core * half, 0)
-    return lax.dynamic_update_slice_in_dim(total, other, (1 - core) * half, 0)
+    low_first = jnp.concatenate([kept, other], axis=0)
+    high_first = jnp.concatenate([other, kept], axis=0)
+    return jnp.where(core == 0, low_first, high_first)
 
 
 def orthonormal(left_basis, gram_matrix):

time: 121 us -> 120 us (level)
    ppermute x16, waiting for transfers between devices: 14.9 us -> 17.2 us  [exchange(): return lax.ppermute(piece, axes, [(i, i ^ stride) for i in range(count)])]
    ppermute x2, waiting for transfers between devices: 2.36 us -> 1.13 us  [word_update_dense(): blocks = kept + lax.ppermute(sent, 'rep', pairs)]
  transfers between devices with their start and end apart: 29 -> 29, of which waited for: 21 -> 25; matrix products, arithmetic and copies ran while one was open for 15% -> 14% of each run, Pallas kernels for 0% -> 0%
where the time goes in v21:
time: 120 us
  waiting for transfers between devices  35.7 us (30%)
  starting transfers between devices  32.3 us (27%)
  other arithmetic  18.6 us (16%)
  blocking collectives  18 us (15%)
  matrix products  10.6 us (9%)
  local copies, waits for them, and re-layouts  3.59 us (3%)
    all_gather x1, blocking collectives, shards(): lax.all_gather(master_new.astype(jnp.bfloat16), 'rep', axis=0, tiled=True)  18 us
    ppermute x16, waiting for transfers between devices, exchange(): return lax.ppermute(piece, axes, [(i, i ^ stride) for i in range(count)])  17.2 us
    ppermute x16, starting transfers between devices, exchange(): return lax.ppermute(piece, axes, [(i, i ^ stride) for i in range(count)])  15.9 us
    ppermute x5, waiting for transfers between devices, exchange(): return lax.ppermute(value, axis, [(i, i ^ stride) for i in range(count)])  12 us
    ppermute x5, starting transfers between devices, exchange(): return lax.ppermute(value, axis, [(i, i ^ stride) for i in range(count)])  7.91 us
    ppermute x6, starting transfers between devices, exchange(): return lax.ppermute(value, axes, [(i, i ^ stride) for i in range(count)])  7.32 us
    another operation x6, other arithmetic, shards(): factor_low = lax.linalg.cholesky(gram_matrix, symmetrize_input=False)  7.18 us
    another operation x4, other arithmetic, shards(): jax.scipy.linalg.solve_triangular(factor_low, left_rows, lower=True)  6.17 us
  transfers between devices with their start and end apart: 29, of which 25 were waited for; matrix products, arithmetic and copies ran while one was open for 14% of the time, Pallas kernels for 0%

profile of v21, /device:TPU:0, one launch (start us, length us, event | category | flops | bytes accessed | tf_op | source)
XLA Modules:
  0.0 120.0 jit_solution(6773193045836561908)
XLA Ops:
  0.7 3.0 %collective-permute-start = (bf16[192,1024]{1,0:T(8,128)(2,1)}, bf16[192,1024]{1,0:T(8,128)(2,1)S(1)}, u32[]{:S(2)}, u32[]{:S(2)}) collective-permute-start(bf16[192,1024]{1,0:T(8,128)(2,1)} %param.13), channel_id=1, source_target_pairs={{0,2},{1,3},{2,0},{3,1},{4,6},{5,7},{6,4},{7,5},{8,10},{9,11},{10,... | collective-permute-start | bytes 1179656 | tf_op jit(solution)/shard_map/ppermute | solution.py:46
  3.7 1.5 %collective-permute-start.1 = (bf16[192,1024]{1,0:T(8,128)(2,1)}, bf16[192,1024]{1,0:T(8,128)(2,1)S(1)}, u32[]{:S(2)}, u32[]{:S(2)}) collective-permute-start(bf16[192,1024]{1,0:T(8,128)(2,1)} %param.13), channel_id=1, source_target_pairs={{0,4},{1,5},{2,6},{3,7},{4,0},{5,1},{6,2},{7,3},{8,12},{9,13},{10,... | collective-permute-start | bytes 1179656 | tf_op jit(solution)/shard_map/ppermute | solution.py:46
  5.2 7.8 %collective-permute-done = bf16[192,1024]{1,0:T(8,128)(2,1)S(1)} collective-permute-done((bf16[192,1024]{1,0:T(8,128)(2,1)}, bf16[192,1024]{1,0:T(8,128)(2,1)S(1)}, u32[]{:S(2)}, u32[]{:S(2)}) %collective-permute-start) | collective-permute-done | bytes 393248 | tf_op jit(solution)/shard_map/ppermute | solution.py:46
  13.0 1.8 %collective-permute-start.3 = (bf16[96,1024]{1,0:T(8,128)(2,1)S(1)}, bf16[96,1024]{1,0:T(8,128)(2,1)S(1)}, u32[]{:S(2)}, u32[]{:S(2)}) collective-permute-start(bf16[96,1024]{1,0:T(8,128)(2,1)S(1)} %slice.15), channel_id=1, source_target_pairs={{0,4},{1,5},{2,6},{3,7},{4,0},{5,1},{6,2},{7,3},{8,12},{9,13},{10,... | collective-permute-start | bytes 589832 | tf_op jit(solution)/shard_map/ppermute | solution.py:46
  14.9 1.6 %collective-permute-start.2 = (bf16[96,1024]{1,0:T(8,128)(2,1)S(1)}, bf16[96,1024]{1,0:T(8,128)(2,1)S(1)}, u32[]{:S(2)}, u32[]{:S(2)}) collective-permute-start(bf16[96,1024]{1,0:T(8,128)(2,1)S(1)} %slice.14), channel_id=1, source_target_pairs={{0,2},{1,3},{2,0},{3,1},{4,6},{5,7},{6,4},{7,5},{8,10},{9,11},{10,... | collective-permute-start | bytes 589832 | tf_op jit(solution)/shard_map/ppermute | solution.py:46
  16.4 2.7 %collective-permute-done.3 = bf16[96,1024]{1,0:T(8,128)(2,1)S(1)} collective-permute-done((bf16[96,1024]{1,0:T(8,128)(2,1)S(1)}, bf16[96,1024]{1,0:T(8,128)(2,1)S(1)}, u32[]{:S(2)}, u32[]{:S(2)}) %collective-permute-start.3) | collective-permute-done | bytes 196640 | tf_op jit(solution)/shard_map/ppermute | solution.py:46
  19.2 1.4 %collective-permute-done.2 = bf16[96,1024]{1,0:T(8,128)(2,1)S(1)} collective-permute-done((bf16[96,1024]{1,0:T(8,128)(2,1)S(1)}, bf16[96,1024]{1,0:T(8,128)(2,1)S(1)}, u32[]{:S(2)}, u32[]{:S(2)}) %collective-permute-start.2) | collective-permute-done | bytes 196640 | tf_op jit(solution)/shard_map/ppermute | solution.py:46
  21.4 1.6 %constant_dynamic-slice_fusion.6 = (bf16[1,192,384]{2,1,0:T(8,128)(2,1)S(1)}, bf16[1,192,384]{2,1,0:T(8,128)(2,1)S(1)}, bf16[1,192,384]{2,1,0:T(8,128)(2,1)S(1)}...) fusion(bf16[8,192,384]{2,1,0:T(8,128)(2,1)} %bitcast.53, ...), kind=kLoop, calls=%fused_computation.81 | loop fusion | bytes 2359328 | tf_op jit(solution)/shard_map/dynamic_slice | solution.py:59
  23.5 1.0 convert_add_fusion
  25.3 1.0 bitcast_add_fusion
  27.8 0.9 collective-permute-done.5
  28.8 1.2 collective-permute-start.7
  29.9 1.8 %collective-permute-start.8 = (f32[16,1024]{1,0:T(8,128)S(1)}, f32[16,1024]{1,0:T(8,128)S(1)}, u32[]{:S(2)}, u32[]{:S(2)}) collective-permute-start(f32[16,1024]{1,0:T(8,128)S(1)} %dynamic-slice_add_fusion.2), channel_id=1, source_target_pairs={{0,6},{1,7},{2,4},{3,5},{4,2},{5,3},{6,0},{7,1},{8,14},{9,15},{10,... | collective-permute-start | bytes 196616 | tf_op jit(solution)/shard_map/ppermute | solution.py:74
  32.3 0.9 collective-permute-done.7
  33.2 2.4 %collective-permute-done.8 = f32[16,1024]{1,0:T(8,128)S(1)} collective-permute-done((f32[16,1024]{1,0:T(8,128)S(1)}, f32[16,1024]{1,0:T(8,128)S(1)}, u32[]{:S(2)}, u32[]{:S(2)}) %collective-permute-start.8) | collective-permute-done | bytes 65568 | tf_op jit(solution)/shard_map/ppermute | solution.py:74
  36.1 2.7 %collective-permute-start.10 = (f32[16,1024]{1,0:T(8,128)S(1)}, f32[16,1024]{1,0:T(8,128)S(1)}, u32[]{:S(2)}, u32[]{:S(2)}) collective-permute-start(f32[16,1024]{1,0:T(8,128)S(1)} %add_add_fusion.3), channel_id=1, source_target_pairs={{0,16},{1,17},{2,18},{3,19},{4,20},{5,21},{6,22},{7,23},{8,24},{9,... | collective-permute-start | bytes 196616 | tf_op jit(solution)/shard_map/ppermute | solution.py:74
  38.7 1.3 %collective-permute-start.11 = (f32[16,1024]{1,0:T(8,128)S(1)}, f32[16,1024]{1,0:T(8,128)S(1)}, u32[]{:S(2)}, u32[]{:S(2)}) collective-permute-start(f32[16,1024]{1,0:T(8,128)S(1)} %add_add_fusion.3), channel_id=1, source_target_pairs={{0,24},{1,25},{2,26},{3,27},{4,28},{5,29},{6,30},{7,31},{8,16},{9,... | collective-permute-start | bytes 196616 | tf_op jit(solution)/shard_map/ppermute | solution.py:74
  40.3 1.1 collective-permute-done.10
  41.4 3.6 %collective-permute-done.11 = f32[16,1024]{1,0:T(8,128)S(1)} collective-permute-done((f32[16,1024]{1,0:T(8,128)S(1)}, f32[16,1024]{1,0:T(8,128)S(1)}, u32[]{:S(2)}, u32[]{:S(2)}) %collective-permute-start.11) | collective-permute-done | bytes 65568 | tf_op jit(solution)/shard_map/ppermute | solution.py:74
  45.2 1.1 select_reduce_fusion
  46.6 2.9 %custom-call.8 = f32[32,32]{1,0:T(8,128)S(1)} custom-call(f32[32,32]{1,0:T(8,128)S(1)} %fusion.31), custom_call_target="Cholesky" | custom-call | tf_op jit(solution)/shard_map/cholesky/custom-call.1 | solution.py:194
  50.8 2.4 %custom-call.9 = f32[1,32,32]{1,2,0:T(8,128)S(1)} custom-call(f32[1,32,32]{2,1,0:T(8,128)S(1)} %fusion.47), custom_call_target="InvertDiagBlocksLowerTriangular" | custom-call | tf_op jit(solution)/shard_map/jit(_solve_triangular)/triangular_solve | solution.py:195
  54.2 2.2 %collective-permute-start.14 = (f32[32,384]{1,0:T(8,128)S(1)}, f32[32,384]{1,0:T(8,128)S(1)}, u32[]{:S(2)}, u32[]{:S(2)}) collective-permute-start(f32[32,384]{1,0:T(8,128)S(1)} %fusion.65), channel_id=1, source_target_pairs={{0,16},{8,24},{16,0},{24,8},{1,17},{9,25},{17,1},{25,9},{2,18},{10... | collective-permute-start | bytes 147464 | tf_op jit(solution)/shard_map/ppermute | solution.py:23
  56.8 0.9 collective-permute-start.13
  57.7 3.1 %fusion = f32[1600,128]{1,0:T(8,128)S(1)} fusion(bf16[1536,128]{1,0:T(8,128)(2,1)S(1)} %copy-done, s32[1536]{0:T(1024)S(1)} %select_reduce_fusion), kind=kOutput, calls=%fused_computation.1 | convolution fusion | flops 631603200 | bytes 1218560 | tf_op jit(solution)/shard_map/dot_general | solution.py:109
  60.9 1.6 %collective-permute-done.15 = f32[32,384]{1,0:T(8,128)S(1)} collective-permute-done((f32[32,384]{1,0:T(8,128)S(1)}, f32[32,384]{1,0:T(8,128)S(1)}, u32[]{:S(2)}, u32[]{:S(2)}) %collective-permute-start.15) | collective-permute-done | bytes 49184 | tf_op jit(solution)/shard_map/ppermute | solution.py:23
  63.6 1.0 collective-permute-done.16
  65.4 1.8 %collective-permute-start.19 = (f32[16,1024]{1,0:T(8,128)S(1)}, f32[16,1024]{1,0:T(8,128)S(1)}, u32[]{:S(2)}, u32[]{:S(2)}) collective-permute-start(f32[16,1024]{1,0:T(8,128)S(1)} %dynamic-slice_add_fusion.1), channel_id=1, source_target_pairs={{0,6},{1,7},{2,4},{3,5},{4,2},{5,3},{6,0},{7,1},{8,14},{9,15},{10,... | collective-permute-start | bytes 196616 | tf_op jit(solution)/shard_map/ppermute | solution.py:74
  67.3 0.9 collective-permute-start.17
  68.2 1.5 %collective-permute-done.18 = f32[16,1024]{1,0:T(8,128)S(1)} collective-permute-done((f32[16,1024]{1,0:T(8,128)S(1)}, f32[16,1024]{1,0:T(8,128)S(1)}, u32[]{:S(2)}, u32[]{:S(2)}) %collective-permute-start.18) | collective-permute-done | bytes 65568 | tf_op jit(solution)/shard_map/ppermute | solution.py:74
  69.6 1.5 %collective-permute-done.19 = f32[16,1024]{1,0:T(8,128)S(1)} collective-permute-done((f32[16,1024]{1,0:T(8,128)S(1)}, f32[16,1024]{1,0:T(8,128)S(1)}, u32[]{:S(2)}, u32[]{:S(2)}) %collective-permute-start.19) | collective-permute-done | bytes 65568 | tf_op jit(solution)/shard_map/ppermute | solution.py:74
  71.6 1.8 %collective-permute-start.21 = (f32[16,1024]{1,0:T(8,128)S(1)}, f32[16,1024]{1,0:T(8,128)S(1)}, u32[]{:S(2)}, u32[]{:S(2)}) collective-permute-start(f32[16,1024]{1,0:T(8,128)S(1)} %add_add_fusion.1), channel_id=1, source_target_pairs={{0,16},{1,17},{2,18},{3,19},{4,20},{5,21},{6,22},{7,23},{8,24},{9,... | collective-permute-start | bytes 196616 | tf_op jit(solution)/shard_map/ppermute | solution.py:74
  73.4 1.5 %collective-permute-start.22 = (f32[16,1024]{1,0:T(8,128)S(1)}, f32[16,1024]{1,0:T(8,128)S(1)}, u32[]{:S(2)}, u32[]{:S(2)}) collective-permute-start(f32[16,1024]{1,0:T(8,128)S(1)} %add_add_fusion.1), channel_id=1, source_target_pairs={{0,24},{1,25},{2,26},{3,27},{4,28},{5,29},{6,30},{7,31},{8,16},{9,... | collective-permute-start | bytes 196616 | tf_op jit(solution)/shard_map/ppermute | solution.py:74
  75.1 1.0 collective-permute-done.27
  76.1 1.0 bitcast_add_fusion.1
  77.2 2.1 %collective-permute-done.21 = f32[16,1024]{1,0:T(8,128)S(1)} collective-permute-done((f32[16,1024]{1,0:T(8,128)S(1)}, f32[16,1024]{1,0:T(8,128)S(1)}, u32[]{:S(2)}, u32[]{:S(2)}) %collective-permute-start.21) | collective-permute-done | bytes 65568 | tf_op jit(solution)/shard_map/ppermute | solution.py:74
  80.7 1.1 collective-permute-start.28
  82.1 2.9 %custom-call.10 = f32[32,32]{1,0:T(8,128)S(1)} custom-call(f32[32,32]{1,0:T(8,128)S(1)} %fusion.27), custom_call_target="Cholesky" | custom-call | tf_op jit(solution)/shard_map/cholesky/custom-call.1 | solution.py:194
  86.3 2.4 %custom-call.11 = f32[1,32,32]{1,2,0:T(8,128)S(1)} custom-call(f32[1,32,32]{2,1,0:T(8,128)S(1)} %fusion.48), custom_call_target="InvertDiagBlocksLowerTriangular" | custom-call | tf_op jit(solution)/shard_map/jit(_solve_triangular)/triangular_solve | solution.py:195
  89.7 1.8 %collective-permute-start.25 = (f32[32,384]{1,0:T(8,128)S(1)}, f32[32,384]{1,0:T(8,128)S(1)}, u32[]{:S(2)}, u32[]{:S(2)}) collective-permute-start(f32[32,384]{1,0:T(8,128)S(1)} %fusion.66), channel_id=1, source_target_pairs={{0,16},{8,24},{16,0},{24,8},{1,17},{9,25},{17,1},{25,9},{2,18},{10... | collective-permute-start | bytes 147464 | tf_op jit(solution)/shard_map/ppermute | solution.py:23
  91.5 1.9 %collective-permute-start.26 = (f32[32,384]{1,0:T(8,128)S(1)}, f32[32,384]{1,0:T(8,128)S(1)}, u32[]{:S(2)}, u32[]{:S(2)}) collective-permute-start(f32[32,384]{1,0:T(8,128)S(1)} %fusion.66), channel_id=1, source_target_pairs={{0,24},{8,16},{16,8},{24,0},{1,25},{9,17},{17,9},{25,1},{2,26},{10... | collective-permute-start | bytes 147464 | tf_op jit(solution)/shard_map/ppermute | solution.py:23
  94.2 2.5 %collective-permute-done.25 = f32[32,384]{1,0:T(8,128)S(1)} collective-permute-done((f32[32,384]{1,0:T(8,128)S(1)}, f32[32,384]{1,0:T(8,128)S(1)}, u32[]{:S(2)}, u32[]{:S(2)}) %collective-permute-start.25) | collective-permute-done | bytes 49184 | tf_op jit(solution)/shard_map/ppermute | solution.py:23
  96.7 0.8 collective-permute-done.26
  98.1 0.8 fusion.67
  99.0 1.1 fusion.7
  100.1 1.0 fusion.64
  101.1 18.0 %all_gather.3 = bf16[1024,384]{1,0:T(8,128)(2,1)S(1)} all-gather(bf16[256,384]{1,0:T(8,128)(2,1)S(1)} %get-tuple-element.12), channel_id=1, replica_groups=mesh['rep'=4,'tp'=8] {'rep'}, dimensions={0}, use_global_device_ids=true | all-gather | bytes 983040 | tf_op jit(solution)/shard_map/all_gather | solution.py:209
  119.1 0.9 copy.17
  (91 shorter events, 15.7 us)
Async XLA Ops:
  0.6 57.1 %copy-start = (bf16[1536,128]{1,0:T(8,128)(2,1)S(1)}, bf16[1536,128]{1,0:T(8,128)(2,1)}, u32[]{:S(2)}) copy-start(bf16[1536,128]{1,0:T(8,128)(2,1)} %param.19) | copy-start | bytes 1179652
  0.6 20.0 %copy-start.7 = (bf16[192,1024]{1,0:T(8,128)(2,1)S(1)}, bf16[192,1024]{1,0:T(8,128)(2,1)}, u32[]{:S(2)}) copy-start(bf16[192,1024]{1,0:T(8,128)(2,1)} %param.13) | copy-start | bytes 1179652
  0.7 12.3 %collective-permute-start = (bf16[192,1024]{1,0:T(8,128)(2,1)}, bf16[192,1024]{1,0:T(8,128)(2,1)S(1)}, u32[]{:S(2)}, u32[]{:S(2)}) collective-permute-start(bf16[192,1024]{1,0:T(8,128)(2,1)} %param.13), channel_id=1, source_target_pairs={{0,2},{1,3},{2,0},{3,1},{4,6},{5,7},{6,4},{7,5},{8,10},{9,11},{10,... | collective-permute-start | bytes 1179656 | tf_op jit(solution)/shard_map/ppermute | solution.py:46
  3.7 11.2 %collective-permute-start.1 = (bf16[192,1024]{1,0:T(8,128)(2,1)}, bf16[192,1024]{1,0:T(8,128)(2,1)S(1)}, u32[]{:S(2)}, u32[]{:S(2)}) collective-permute-start(bf16[192,1024]{1,0:T(8,128)(2,1)} %param.13), channel_id=1, source_target_pairs={{0,4},{1,5},{2,6},{3,7},{4,0},{5,1},{6,2},{7,3},{8,12},{9,13},{10,... | collective-permute-start | bytes 1179656 | tf_op jit(solution)/shard_map/ppermute | solution.py:46
  13.0 7.9 %copy-start.3 = (bf16[192,1024]{1,0:T(8,128)(2,1)}, bf16[192,1024]{1,0:T(8,128)(2,1)S(1)}, u32[]{:S(2)}) copy-start(bf16[192,1024]{1,0:T(8,128)(2,1)S(1)} %collective-permute-done) | copy-start | bytes 1179652
  13.0 6.2 %collective-permute-start.3 = (bf16[96,1024]{1,0:T(8,128)(2,1)S(1)}, bf16[96,1024]{1,0:T(8,128)(2,1)S(1)}, u32[]{:S(2)}, u32[]{:S(2)}) collective-permute-start(bf16[96,1024]{1,0:T(8,128)(2,1)S(1)} %slice.15), channel_id=1, source_target_pairs={{0,4},{1,5},{2,6},{3,7},{4,0},{5,1},{6,2},{7,3},{8,12},{9,13},{10,... | collective-permute-start | bytes 589832 | tf_op jit(solution)/shard_map/ppermute | solution.py:46
  14.8 6.0 %copy-start.5 = (bf16[192,1024]{1,0:T(8,128)(2,1)}, bf16[192,1024]{1,0:T(8,128)(2,1)S(1)}, u32[]{:S(2)}) copy-start(bf16[192,1024]{1,0:T(8,128)(2,1)S(1)} %collective-permute-done.1) | copy-start | bytes 1179652
  14.9 5.7 %collective-permute-start.2 = (bf16[96,1024]{1,0:T(8,128)(2,1)S(1)}, bf16[96,1024]{1,0:T(8,128)(2,1)S(1)}, u32[]{:S(2)}, u32[]{:S(2)}) collective-permute-start(bf16[96,1024]{1,0:T(8,128)(2,1)S(1)} %slice.14), channel_id=1, source_target_pairs={{0,2},{1,3},{2,0},{3,1},{4,6},{5,7},{6,4},{7,5},{8,10},{9,11},{10,... | collective-permute-start | bytes 589832 | tf_op jit(solution)/shard_map/ppermute | solution.py:46
  20.6 0.7 copy-start.1
  21.4 4.0 %collective-permute-start.4 = (bf16[4,192,1024]{2,1,0:T(8,128)(2,1)S(1)}, bf16[4,192,1024]{2,1,0:T(8,128)(2,1)S(1)}, u32[]{:S(2)}, u32[]{:S(2)}) collective-permute-start(bf16[4,192,1024]{2,1,0:T(8,128)(2,1)S(1)} %pad_maximum_fusion), channel_id=1, source_target_pairs={{0,1},{1,0},{2,3},{3,2},{4,5},{5,4},{6,7},{7,6},{8,9},{9,8},{10,11... | collective-permute-start | bytes 4718600 | tf_op jit(solution)/shard_map/ppermute | solution.py:46
  21.4 1.7 %copy-start.2 = (bf16[1,192,1024]{2,1,0:T(8,128)(2,1)S(1)}, bf16[1,192,1024]{2,1,0:T(8,128)(2,1)}, u32[]{:S(2)}) copy-start(bf16[1,192,1024]{2,1,0:T(8,128)(2,1)} %copy-done.1) | copy-start | bytes 1179652
  21.4 1.7 %copy-start.4 = (bf16[192,1024]{1,0:T(8,128)(2,1)S(1)}, bf16[192,1024]{1,0:T(8,128)(2,1)}, u32[]{:S(2)}) copy-start(bf16[192,1024]{1,0:T(8,128)(2,1)} %copy-done.3) | copy-start | bytes 1179652
  21.4 1.7 %copy-start.6 = (bf16[192,1024]{1,0:T(8,128)(2,1)S(1)}, bf16[192,1024]{1,0:T(8,128)(2,1)}, u32[]{:S(2)}) copy-start(bf16[192,1024]{1,0:T(8,128)(2,1)} %copy-done.5) | copy-start | bytes 1179652
  21.4 1.8 %copy-start.8 = (bf16[192,1024]{1,0:T(8,128)(2,1)S(1)}, bf16[192,1024]{1,0:T(8,128)(2,1)}, u32[]{:S(2)}) copy-start(bf16[192,1024]{1,0:T(8,128)(2,1)} %param.13) | copy-start | bytes 1179652
  21.4 2.1 %copy-start.14 = (bf16[1,1024,384]{2,1,0:T(8,128)(2,1)S(1)}, bf16[1,1024,384]{2,1,0:T(8,128)(2,1)}, u32[]{:S(2)}) copy-start(bf16[1,1024,384]{2,1,0:T(8,128)(2,1)} %param.15) | copy-start | bytes 2359300
  23.5 1.0 copy-start.12
  26.4 18.8 %copy-start.15 = (s32[1600]{0:T(1024)S(1)}, s32[1600]{0:T(1024)}, u32[]{:S(2)}) copy-start(s32[1600]{0:T(1024)} %param.21) | copy-start | bytes 19204
  26.4 18.8 %copy-start.16 = (s32[1536]{0:T(1024)S(1)}, s32[1536]{0:T(1024)}, u32[]{:S(2)}) copy-start(s32[1536]{0:T(1024)} %param.20) | copy-start | bytes 18436
  27.3 1.5 %collective-permute-start.5 = (f32[16,1024]{1,0:T(8,128)S(1)}, f32[16,1024]{1,0:T(8,128)S(1)}, u32[]{:S(2)}, u32[]{:S(2)}) collective-permute-start(f32[16,1024]{1,0:T(8,128)S(1)} %constant_dynamic-slice_fusion.2), channel_id=1, source_target_pairs={{0,1},{1,0},{2,3},{3,2},{4,5},{5,4},{6,7},{7,6},{8,9},{9,8},{10,11... | collective-permute-start | bytes 196616 | tf_op jit(solution)/shard_map/ppermute | solution.py:74
  28.8 4.4 %collective-permute-start.7 = (f32[16,1024]{1,0:T(8,128)S(1)}, f32[16,1024]{1,0:T(8,128)S(1)}, u32[]{:S(2)}, u32[]{:S(2)}) collective-permute-start(f32[16,1024]{1,0:T(8,128)S(1)} %dynamic-slice_add_fusion.2), channel_id=1, source_target_pairs={{0,4},{1,5},{2,6},{3,7},{4,0},{5,1},{6,2},{7,3},{8,12},{9,13},{10,... | collective-permute-start | bytes 196616 | tf_op jit(solution)/shard_map/ppermute | solution.py:74
  29.9 5.7 %collective-permute-start.8 = (f32[16,1024]{1,0:T(8,128)S(1)}, f32[16,1024]{1,0:T(8,128)S(1)}, u32[]{:S(2)}, u32[]{:S(2)}) collective-permute-start(f32[16,1024]{1,0:T(8,128)S(1)} %dynamic-slice_add_fusion.2), channel_id=1, source_target_pairs={{0,6},{1,7},{2,4},{3,5},{4,2},{5,3},{6,0},{7,1},{8,14},{9,15},{10,... | collective-permute-start | bytes 196616 | tf_op jit(solution)/shard_map/ppermute | solution.py:74
  31.8 4.3 %collective-permute-start.6 = (f32[16,1024]{1,0:T(8,128)S(1)}, f32[16,1024]{1,0:T(8,128)S(1)}, u32[]{:S(2)}, u32[]{:S(2)}) collective-permute-start(f32[16,1024]{1,0:T(8,128)S(1)} %dynamic-slice_add_fusion.2), channel_id=1, source_target_pairs={{0,2},{1,3},{2,0},{3,1},{4,6},{5,7},{6,4},{7,5},{8,10},{9,11},{10,... | collective-permute-start | bytes 196616 | tf_op jit(solution)/shard_map/ppermute | solution.py:74
  36.1 5.3 %collective-permute-start.10 = (f32[16,1024]{1,0:T(8,128)S(1)}, f32[16,1024]{1,0:T(8,128)S(1)}, u32[]{:S(2)}, u32[]{:S(2)}) collective-permute-start(f32[16,1024]{1,0:T(8,128)S(1)} %add_add_fusion.3), channel_id=1, source_target_pairs={{0,16},{1,17},{2,18},{3,19},{4,20},{5,21},{6,22},{7,23},{8,24},{9,... | collective-permute-start | bytes 196616 | tf_op jit(solution)/shard_map/ppermute | solution.py:74
  38.7 6.2 %collective-permute-start.11 = (f32[16,1024]{1,0:T(8,128)S(1)}, f32[16,1024]{1,0:T(8,128)S(1)}, u32[]{:S(2)}, u32[]{:S(2)}) collective-permute-start(f32[16,1024]{1,0:T(8,128)S(1)} %add_add_fusion.3), channel_id=1, source_target_pairs={{0,24},{1,25},{2,26},{3,27},{4,28},{5,29},{6,30},{7,31},{8,16},{9,... | collective-permute-start | bytes 196616 | tf_op jit(solution)/shard_map/ppermute | solution.py:74
  40.1 5.0 %collective-permute-start.9 = (f32[16,1024]{1,0:T(8,128)S(1)}, f32[16,1024]{1,0:T(8,128)S(1)}, u32[]{:S(2)}, u32[]{:S(2)}) collective-permute-start(f32[16,1024]{1,0:T(8,128)S(1)} %add_add_fusion.3), channel_id=1, source_target_pairs={{0,8},{1,9},{2,10},{3,11},{4,12},{5,13},{6,14},{7,15},{8,0},{9,1},... | collective-permute-start | bytes 196616 | tf_op jit(solution)/shard_map/ppermute | solution.py:74
  45.1 1.3 %collective-permute-start.12 = (f32[16,1024]{1,0:T(8,128)S(1)}, f32[16,1024]{1,0:T(8,128)S(1)}, u32[]{:S(2)}, u32[]{:S(2)}) collective-permute-start(f32[16,1024]{1,0:T(8,128)S(1)} %add_add_fusion.2), channel_id=1, source_target_pairs={{0,1},{1,0},{2,3},{3,2},{4,5},{5,4},{6,7},{7,6},{8,9},{9,8},{10,11... | collective-permute-start | bytes 196616 | tf_op jit(solution)/shard_map/ppermute | solution.py:74
  54.2 6.7 %collective-permute-start.14 = (f32[32,384]{1,0:T(8,128)S(1)}, f32[32,384]{1,0:T(8,128)S(1)}, u32[]{:S(2)}, u32[]{:S(2)}) collective-permute-start(f32[32,384]{1,0:T(8,128)S(1)} %fusion.65), channel_id=1, source_target_pairs={{0,16},{8,24},{16,0},{24,8},{1,17},{9,25},{17,1},{25,9},{2,18},{10... | collective-permute-start | bytes 147464 | tf_op jit(solution)/shard_map/ppermute | solution.py:23
  56.4 6.1 %collective-permute-start.15 = (f32[32,384]{1,0:T(8,128)S(1)}, f32[32,384]{1,0:T(8,128)S(1)}, u32[]{:S(2)}, u32[]{:S(2)}) collective-permute-start(f32[32,384]{1,0:T(8,128)S(1)} %fusion.65), channel_id=1, source_target_pairs={{0,24},{8,16},{16,8},{24,0},{1,25},{9,17},{17,9},{25,1},{2,26},{10... | collective-permute-start | bytes 147464 | tf_op jit(solution)/shard_map/ppermute | solution.py:23
  56.8 5.6 %collective-permute-start.13 = (f32[32,384]{1,0:T(8,128)S(1)}, f32[32,384]{1,0:T(8,128)S(1)}, u32[]{:S(2)}, u32[]{:S(2)}) collective-permute-start(f32[32,384]{1,0:T(8,128)S(1)} %fusion.65), channel_id=1, source_target_pairs={{0,8},{8,0},{16,24},{24,16},{1,9},{9,1},{17,25},{25,17},{2,10},{10... | collective-permute-start | bytes 147464 | tf_op jit(solution)/shard_map/ppermute | solution.py:23
  63.3 1.3 %collective-permute-start.16 = (f32[16,1024]{1,0:T(8,128)S(1)}, f32[16,1024]{1,0:T(8,128)S(1)}, u32[]{:S(2)}, u32[]{:S(2)}) collective-permute-start(f32[16,1024]{1,0:T(8,128)S(1)} %constant_dynamic-slice_fusion.1), channel_id=1, source_target_pairs={{0,1},{1,0},{2,3},{3,2},{4,5},{5,4},{6,7},{7,6},{8,9},{9,8},{10,11... | collective-permute-start | bytes 196616 | tf_op jit(solution)/shard_map/ppermute | solution.py:74
  63.4 12.7 %collective-permute-start.27 = (f32[2,400,128]{2,1,0:T(8,128)S(1)}, f32[2,400,128]{2,1,0:T(8,128)}, u32[]{:S(2)}, u32[]{:S(2)}) collective-permute-start(f32[2,400,128]{2,1,0:T(8,128)S(1)} %dynamic-slice_bitcast_fusion), channel_id=1, source_target_pairs={{0,8},{8,0},{16,24},{24,16},{1,9},{9,1},{17,25},{25,17},{2,10},{10... | collective-permute-start | bytes 1228808 | tf_op jit(solution)/shard_map/ppermute | solution.py:121
  64.6 5.0 %collective-permute-start.18 = (f32[16,1024]{1,0:T(8,128)S(1)}, f32[16,1024]{1,0:T(8,128)S(1)}, u32[]{:S(2)}, u32[]{:S(2)}) collective-permute-start(f32[16,1024]{1,0:T(8,128)S(1)} %dynamic-slice_add_fusion.1), channel_id=1, source_target_pairs={{0,4},{1,5},{2,6},{3,7},{4,0},{5,1},{6,2},{7,3},{8,12},{9,13},{10,... | collective-permute-start | bytes 196616 | tf_op jit(solution)/shard_map/ppermute | solution.py:74
  65.4 5.7 %collective-permute-start.19 = (f32[16,1024]{1,0:T(8,128)S(1)}, f32[16,1024]{1,0:T(8,128)S(1)}, u32[]{:S(2)}, u32[]{:S(2)}) collective-permute-start(f32[16,1024]{1,0:T(8,128)S(1)} %dynamic-slice_add_fusion.1), channel_id=1, source_target_pairs={{0,6},{1,7},{2,4},{3,5},{4,2},{5,3},{6,0},{7,1},{8,14},{9,15},{10,... | collective-permute-start | bytes 196616 | tf_op jit(solution)/shard_map/ppermute | solution.py:74
  67.3 4.3 %collective-permute-start.17 = (f32[16,1024]{1,0:T(8,128)S(1)}, f32[16,1024]{1,0:T(8,128)S(1)}, u32[]{:S(2)}, u32[]{:S(2)}) collective-permute-start(f32[16,1024]{1,0:T(8,128)S(1)} %dynamic-slice_add_fusion.1), channel_id=1, source_target_pairs={{0,2},{1,3},{2,0},{3,1},{4,6},{5,7},{6,4},{7,5},{8,10},{9,11},{10,... | collective-permute-start | bytes 196616 | tf_op jit(solution)/shard_map/ppermute | solution.py:74
  71.6 7.7 %collective-permute-start.21 = (f32[16,1024]{1,0:T(8,128)S(1)}, f32[16,1024]{1,0:T(8,128)S(1)}, u32[]{:S(2)}, u32[]{:S(2)}) collective-permute-start(f32[16,1024]{1,0:T(8,128)S(1)} %add_add_fusion.1), channel_id=1, source_target_pairs={{0,16},{1,17},{2,18},{3,19},{4,20},{5,21},{6,22},{7,23},{8,24},{9,... | collective-permute-start | bytes 196616 | tf_op jit(solution)/shard_map/ppermute | solution.py:74
  73.4 6.5 %collective-permute-start.22 = (f32[16,1024]{1,0:T(8,128)S(1)}, f32[16,1024]{1,0:T(8,128)S(1)}, u32[]{:S(2)}, u32[]{:S(2)}) collective-permute-start(f32[16,1024]{1,0:T(8,128)S(1)} %add_add_fusion.1), channel_id=1, source_target_pairs={{0,24},{1,25},{2,26},{3,27},{4,28},{5,29},{6,30},{7,31},{8,16},{9,... | collective-permute-start | bytes 196616 | tf_op jit(solution)/shard_map/ppermute | solution.py:74
  74.9 5.4 %collective-permute-start.20 = (f32[16,1024]{1,0:T(8,128)S(1)}, f32[16,1024]{1,0:T(8,128)S(1)}, u32[]{:S(2)}, u32[]{:S(2)}) collective-permute-start(f32[16,1024]{1,0:T(8,128)S(1)} %add_add_fusion.1), channel_id=1, source_target_pairs={{0,8},{1,9},{2,10},{3,11},{4,12},{5,13},{6,14},{7,15},{8,0},{9,1},... | collective-permute-start | bytes 196616 | tf_op jit(solution)/shard_map/ppermute | solution.py:74
  77.2 16.4 %copy-start.11 = (f32[400,128]{1,0:T(8,128)S(1)}, f32[400,128]{1,0:T(8,128)}, u32[]{:S(2)}) copy-start(f32[400,128]{1,0:T(8,128)} %param.22) | copy-start | bytes 614404
  80.4 1.5 %collective-permute-start.23 = (f32[16,1024]{1,0:T(8,128)S(1)}, f32[16,1024]{1,0:T(8,128)S(1)}, u32[]{:S(2)}, u32[]{:S(2)}) collective-permute-start(f32[16,1024]{1,0:T(8,128)S(1)} %add_add_fusion), channel_id=1, source_target_pairs={{0,1},{1,0},{2,3},{3,2},{4,5},{5,4},{6,7},{7,6},{8,9},{9,8},{10,11... | collective-permute-start | bytes 196616 | tf_op jit(solution)/shard_map/ppermute | solution.py:74
  80.7 12.9 %collective-permute-start.28 = (f32[1,400,128]{2,1,0:T(8,128)S(1)}, f32[1,400,128]{2,1,0:T(8,128)S(1)}, u32[]{:S(2)}, u32[]{:S(2)}) collective-permute-start(f32[1,400,128]{2,1,0:T(8,128)S(1)} %constant_dynamic-slice_fusion), channel_id=1, source_target_pairs={{0,16},{8,24},{16,0},{24,8},{1,17},{9,25},{17,1},{25,9},{2,18},{10... | collective-permute-start | bytes 614408 | tf_op jit(solution)/shard_map/ppermute | solution.py:121
  89.7 7.1 %collective-permute-start.25 = (f32[32,384]{1,0:T(8,128)S(1)}, f32[32,384]{1,0:T(8,128)S(1)}, u32[]{:S(2)}, u32[]{:S(2)}) collective-permute-start(f32[32,384]{1,0:T(8,128)S(1)} %fusion.66), channel_id=1, source_target_pairs={{0,16},{8,24},{16,0},{24,8},{1,17},{9,25},{17,1},{25,9},{2,18},{10... | collective-permute-start | bytes 147464 | tf_op jit(solution)/shard_map/ppermute | solution.py:23
  91.5 6.1 %collective-permute-start.26 = (f32[32,384]{1,0:T(8,128)S(1)}, f32[32,384]{1,0:T(8,128)S(1)}, u32[]{:S(2)}, u32[]{:S(2)}) collective-permute-start(f32[32,384]{1,0:T(8,128)S(1)} %fusion.66), channel_id=1, source_target_pairs={{0,24},{8,16},{16,8},{24,0},{1,25},{9,17},{17,9},{25,1},{2,26},{10... | collective-permute-start | bytes 147464 | tf_op jit(solution)/shard_map/ppermute | solution.py:23
  93.4 4.7 %collective-permute-start.24 = (f32[32,384]{1,0:T(8,128)S(1)}, f32[32,384]{1,0:T(8,128)S(1)}, u32[]{:S(2)}, u32[]{:S(2)}) collective-permute-start(f32[32,384]{1,0:T(8,128)S(1)} %fusion.66), channel_id=1, source_target_pairs={{0,8},{8,0},{16,24},{24,16},{1,9},{9,1},{17,25},{25,17},{2,10},{10... | collective-permute-start | bytes 147464 | tf_op jit(solution)/shard_map/ppermute | solution.py:23
  98.1 2.0 %copy-start.13 = (f32[32,384]{1,0:T(8,128)}, f32[32,384]{1,0:T(8,128)S(1)}, u32[]{:S(2)}) copy-start(f32[32,384]{1,0:T(8,128)S(1)} %add_multiply_fusion) | copy-start | bytes 147460
  98.9 1.2 copy-start.9
  99.0 1.2 copy-start.10
